TPU v7x, 32 devices: a whole 2x2x4 slice. The times are simulated.
32 devices in a mesh: lat: 8 (over z, core), lon: 4 (over y, x).
Axes of the slice: x: 2, y: 2, z: 4, core: 2. Of those that a mesh axis runs over, the one named last changes fastest.
Arguments:
- elem_codes: int32 [128, 32, 256], P('lat', 'lon'), may hold values from 32 to 207, as said below
- block_exps: int32 [128, 32, 8], P('lat', 'lon'), may hold values from -2 to 1
- up_kernel: bfloat16 [4, 4, 256, 128], replicated, may hold values from -0.1875 to 0.1875
- up_bias: float32 [128], replicated, may hold values from -3 to 3
- mix_kernel: bfloat16 [3, 3, 128, 128], replicated, may hold values from -0.1875 to 0.1875
- cotangent: bfloat16 [256, 64, 128], P('lat', 'lon'), may hold values from -6 to 6
Outputs:
- section_out: bfloat16 [256, 64, 128], P('lat', 'lon')
- input_grad: float32 [128, 32, 256], P('lat', 'lon')
- up_grad: float32 [4, 4, 256, 128], P(None, None, 'lon')
- mix_grad: float32 [3, 3, 128, 128], P(None, None, 'lon')
Inputs may be any that keep to these rules, and one draw needn't show every extreme that they name: `elem_codes`: every code has a sign bit of weight 128, a four-bit exponent field from 4 to 9 and a three-bit mantissa.
All inputs are finite; a program needn't handle non-finite values.
Results may differ from a plain program's by a relative error of at most 0.012.
Values may be sent and summed in bfloat16 or wider, within the bound.
No kernel may reach another device: no remote copies, remote signals or barrier semaphores. Data moves between devices by JAX's collectives and lax.ppermute only.
A program may use at most 64 MiB of HBM per device.

v0:
```python
import math

import jax
import jax.numpy as jnp
from jax import lax
from jax.sharding import PartitionSpec as P

CIN = 256
COUT = 128
BLOCK = 32


row_taps = (((1, 0), (3, -1)), ((0, 1), (2, 0)))


def padded_2(array, sides, width, wrap):
    for axis, dim in sides:
        size, length = (lax.axis_size(axis), array.shape[dim])
        up = [(i, (i + 1) % size) for i in range(size if wrap else size - 1)]
        down = [(j, i) for i, j in up]
        last = lax.slice_in_dim(array, length - width, length, axis=dim)
        leading = lax.slice_in_dim(array, 0, width, axis=dim)
        before = lax.ppermute(last, axis, up)
        after = lax.ppermute(leading, axis, down)
        array = jnp.concatenate([before, array, after], axis=dim)
    return array


def decode(elem_codes, block_exps):
    sign_bit = elem_codes // 128
    exponent = elem_codes // 8 % 16
    mantissa = elem_codes % 8
    magnitude = jnp.exp2((exponent - 7).astype(jnp.float32)) * (
        1.0 + mantissa.astype(jnp.float32) / 8.0
    )
    signed = jnp.where(sign_bit == 1, -magnitude, magnitude)
    factor = jnp.repeat(jnp.exp2(block_exps.astype(jnp.float32)), BLOCK, axis=2)
    return (signed * factor).astype(jnp.bfloat16)


def extend(field, margin):
    widened = padded_2(field, (("lon", 1),), margin, True)
    return padded_2(widened, (("lat", 0),), margin, False)


def slope(pre_act):
    plain = pre_act.astype(jnp.float32)
    sigmoid_v = jax.nn.sigmoid(plain)
    return sigmoid_v * (1.0 + plain * (1.0 - sigmoid_v))


def upsample(padded, up_kernel, row_count, col_count):
    halves = []
    for row_par in range(2):
        lane_list = []
        for col_par in range(2):
            pieces = []
            kernels = []
            for row_tap, row_off in row_taps[row_par]:
                for col_tap, col_off in row_taps[col_par]:
                    pieces.append(
                        padded[
                            1 + row_off : 1 + row_off + row_count,
                            1 + col_off : 1 + col_off + col_count,
                        ]
                    )
                    kernels.append(up_kernel[row_tap, col_tap])
            stacked = jnp.concatenate(pieces, axis=2)
            kernel = jnp.concatenate(kernels, axis=0)
            lane_list.append(
                jnp.einsum("rck,kn->rcn", stacked, kernel, preferred_element_type=jnp.float32)
            )
        halves.append(jnp.stack(lane_list, axis=2))
    merged = jnp.stack(halves, axis=1)
    return merged.reshape(2 * row_count, 2 * col_count, merged.shape[-1])


def neighbours(padded, row_count, col_count, flipped):
    pieces = []
    for row_tap in range(3):
        for col_tap in range(3):
            row_at = 2 - row_tap if flipped else row_tap
            col_at = 2 - col_tap if flipped else col_tap
            pieces.append(padded[row_at : row_at + row_count, col_at : col_at + col_count])
    return jnp.concatenate(pieces, axis=2)


def strided(padded, row_count, col_count):
    pieces = []
    for row_tap in range(4):
        for col_tap in range(4):
            pieces.append(
                padded[row_tap : row_tap + 2 * row_count : 2, col_tap : col_tap + 2 * col_count : 2]
            )
    return jnp.concatenate(pieces, axis=2)


def shards(elem_codes, block_exps, up_kernel, up_bias, mix_kernel, cotangent):
    inputs = decode(elem_codes, block_exps)
    in_rows, in_cols = (inputs.shape[0], inputs.shape[1])
    out_rows, out_cols = (2 * in_rows, 2 * in_cols)
    lat_count = lax.axis_size("lat")
    lon_count = lax.axis_size("lon")
    back_mix = mix_kernel.transpose(0, 1, 3, 2).reshape(9 * COUT, COUT)
    padded_in = extend(inputs, 1)
    raw = upsample(padded_in, up_kernel, in_rows, in_cols)
    pre_act = (raw + up_bias).astype(jnp.bfloat16)
    act_pad = extend(jax.nn.silu(pre_act.astype(jnp.float32)).astype(jnp.bfloat16), 1)
    grad_pad = extend(cotangent, 1)
    act_grad = jnp.einsum(
        "rck,kn->rcn",
        neighbours(grad_pad, out_rows, out_cols, True),
        back_mix,
        preferred_element_type=jnp.float32,
    )
    pre_grad_pad = extend((act_grad * slope(pre_act)).astype(jnp.bfloat16), 1)
    patches = neighbours(act_pad, out_rows, out_cols, False)
    mix_flat = mix_kernel.reshape(9 * COUT, COUT)
    section_out = jnp.einsum(
        "rck,kn->rcn", patches, mix_flat, preferred_element_type=jnp.float32
    ).astype(jnp.bfloat16)
    grad_scale = 1.0 / math.sqrt(out_rows * lat_count * out_cols * lon_count)
    mix_grad = (
        jnp.einsum("rck,rcn->kn", patches, cotangent, preferred_element_type=jnp.float32).reshape(
            3, 3, COUT, COUT
        )
        * grad_scale
    )
    grad_patches = strided(pre_grad_pad, in_rows, in_cols)
    back_up = up_kernel.transpose(0, 1, 3, 2).reshape(16 * COUT, CIN)
    input_grad = jnp.einsum(
        "rck,kn->rcn", grad_patches, back_up, preferred_element_type=jnp.float32
    )
    up_flat = jnp.einsum("rcm,rck->mk", inputs, grad_patches, preferred_element_type=jnp.float32)
    up_grad = up_flat.reshape(CIN, 4, 4, COUT).transpose(1, 2, 0, 3) * grad_scale
    summed = lax.psum((up_grad, mix_grad), ("lat", "lon"))
    lon_index = lax.axis_index("lon")
    up_span = CIN // lon_count
    mix_span = COUT // lon_count
    up_part = lax.dynamic_slice_in_dim(summed[0], lon_index * up_span, up_span, 2)
    mix_part = lax.dynamic_slice_in_dim(summed[1], lon_index * mix_span, mix_span, 2)
    return (section_out, input_grad, up_part, mix_part)


def solution(mesh):
    placed = (P("lat", "lon", None), P("lat", "lon", None), P(), P(), P(), P("lat", "lon", None))
    return jax.shard_map(
        shards,
        mesh=mesh,
        in_specs=placed,
        out_specs=(
            P("lat", "lon", None),
            P("lat", "lon", None),
            P(None, None, "lon", None),
            P(None, None, "lon", None),
        ),
        check_vma=False,
    )
```

profile of v0, /device:TPU:0, one launch (start us, length us, event | category | flops | bytes accessed | tf_op | source)
XLA Modules:
  0.0 213.7 jit_solution(17069438167955486399)
XLA Ops:
  7.2 0.9 multiply_exponential_fusion
  8.6 0.3 fusion.77
  8.9 3.0 %collective-permute-start = (bf16[16,1,256]{2,1,0:T(2,128)(2,1)S(1)}, bf16[16,1,256]{2,1,0:T(2,128)(2,1)S(1)}, u32[]{:S(2)}, u32[]{:S(2)}) collective-permute-start(bf16[16,1,256]{2,1,0:T(2,128)(2,1)S(1)} %get-tuple-element.50), channel_id=1, source_target_pairs={{0,1},{1,2},{2,3},{3,0},{4,5},{5,6},{6,7},{7,4},{8,9},{9,10},{10,1... | collective-permute-start | bytes 24584 | tf_op jit(solution)/shard_map/ppermute | solution.py:23
  11.9 1.0 collective-permute-start.1
  13.0 2.0 collective-permute-start.9
  15.7 1.3 collective-permute-start.2
  17.0 1.3 collective-permute-start.3
  18.3 1.3 collective-permute-done.8
  19.6 3.7 %collective-permute-start.11 = (bf16[1,18,128]{2,1,0:T(8,128)(2,1)S(1)}, bf16[1,18,128]{2,1,0:T(8,128)(2,1)S(1)}, u32[]{:S(2)}, u32[]{:S(2)}) collective-permute-start(bf16[1,18,128]{2,1,0:T(8,128)(2,1)S(1)} %get-tuple-element.26), channel_id=1, source_target_pairs={{0,4},{4,8},{8,12},{12,16},{16,20},{20,24},{24,28},{1,5},{5,9},{9,... | collective-permute-start | bytes 13832 | tf_op jit(solution)/shard_map/ppermute | solution.py:23
  23.3 1.3 collective-permute-start.10
  24.7 2.9 %collective-permute-done.10 = bf16[1,18,128]{2,1,0:T(8,128)(2,1)S(1)} collective-permute-done((bf16[1,18,128]{2,1,0:T(8,128)(2,1)S(1)}, bf16[1,18,128]{2,1,0:T(8,128)(2,1)S(1)}, u32[]{:S(2)}, u32[]{:S(2)}) %collective-permute-start.10) | collective-permute-done | bytes 4640 | tf_op jit(solution)/shard_map/ppermute | solution.py:24
  30.0 0.5 fusion.2
  30.5 2.5 %collective-permute-start.13 = (bf16[32,1,128]{2,1,0:T(2,128)(2,1)S(1)}, bf16[32,1,128]{2,1,0:T(2,128)(2,1)S(1)}, u32[]{:S(2)}, u32[]{:S(2)}) collective-permute-start(bf16[32,1,128]{2,1,0:T(2,128)(2,1)S(1)} %get-tuple-element.39), channel_id=1, source_target_pairs={{1,0},{2,1},{3,2},{0,3},{5,4},{6,5},{7,6},{4,7},{9,8},{10,9},{11,1... | collective-permute-start | bytes 24584 | tf_op jit(solution)/shard_map/ppermute | solution.py:24
  33.1 0.3 slice.305
  33.4 3.0 %collective-permute-start.5 = (bf16[32,1,128]{2,1,0:T(2,128)(2,1)S(1)}, bf16[32,1,128]{2,1,0:T(2,128)(2,1)S(1)}, u32[]{:S(2)}, u32[]{:S(2)}) collective-permute-start(bf16[32,1,128]{2,1,0:T(2,128)(2,1)S(1)} %get-tuple-element.43), channel_id=1, source_target_pairs={{1,0},{2,1},{3,2},{0,3},{5,4},{6,5},{7,6},{4,7},{9,8},{10,9},{11,1... | collective-permute-start | bytes 24584 | tf_op jit(solution)/shard_map/ppermute | solution.py:24
  36.4 1.3 collective-permute-done.12
  37.8 1.3 collective-permute-start.15
  39.1 3.5 %collective-permute-start.14 = (bf16[1,18,128]{2,1,0:T(8,128)(2,1)S(1)}, bf16[1,18,128]{2,1,0:T(8,128)(2,1)S(1)}, u32[]{:S(2)}, u32[]{:S(2)}) collective-permute-start(bf16[1,18,128]{2,1,0:T(8,128)(2,1)S(1)} %get-tuple-element.22), channel_id=1, source_target_pairs={{0,4},{4,8},{8,12},{12,16},{16,20},{20,24},{24,28},{1,5},{5,9},{9,... | collective-permute-start | bytes 13832 | tf_op jit(solution)/shard_map/ppermute | solution.py:23
  42.6 0.3 slice.304
  42.9 0.4 slice.306
  43.3 0.4 slice.307
  43.7 1.3 collective-permute-start.7
  45.0 4.3 %collective-permute-start.6 = (bf16[1,18,128]{2,1,0:T(8,128)(2,1)S(1)}, bf16[1,18,128]{2,1,0:T(8,128)(2,1)S(1)}, u32[]{:S(2)}, u32[]{:S(2)}) collective-permute-start(bf16[1,18,128]{2,1,0:T(8,128)(2,1)S(1)} %get-tuple-element.31), channel_id=1, source_target_pairs={{0,4},{4,8},{8,12},{12,16},{16,20},{20,24},{24,28},{1,5},{5,9},{9,... | collective-permute-start | bytes 13832 | tf_op jit(solution)/shard_map/ppermute | solution.py:23
  49.4 0.3 slice.300
  49.7 0.3 slice.301
  50.1 0.4 slice.302
  50.5 0.4 slice.303
  50.8 0.3 slice.308
  51.2 0.3 slice.309
  51.5 0.4 slice.310
  51.9 0.4 slice.311
  52.3 0.6 slice.312
  52.9 0.6 slice.313
  53.5 0.7 slice.314
  54.3 0.7 slice.315
  55.8 1.1 copy-done.2
  57.2 0.8 copy-done.6
  58.0 1.8 fusion
  59.8 2.7 %mul.54 = f32[256,4,4,128]{3,2,1,0:T(4,128)S(1)} reshape(f32[256,2048]{1,0:T(8,128)} %fusion) | data formatting | bytes 4194304 | tf_op jit(solution)/shard_map/mul | solution.py:135
  62.5 2.0 copy.30
  64.5 1.4 fusion.1
  65.8 0.5 copy.19
  66.4 0.7 copy-done.4
  67.1 2.1 convolution_convert_fusion
  69.2 1.0 fusion.91
  70.2 133.2 %all-reduce.3.cloned.1.call-done = (f32[4,4,256,128]{3,2,1,0:T(8,128)}, f32[3,3,128,128]{3,2,1,0:T(8,128)}) async-done(((f32[4,4,256,128]{3,2,1,0:T(8,128)}, f32[3,3,128,128]{3,2,1,0:T(8,128)}), (f32[4,4,256,128]{3,2,1,0:T(8,128)}, f32[3,3,128,128]{3,2,1,0:T(8,128)})) %all-reduce.3.cloned.1.call-update) | async-done | bytes 2686992 | tf_op jit(solution)/shard_map/psum | solution.py:136
  203.4 1.9 constant_dynamic-slice_fusion.1
  205.3 1.6 constant_dynamic-slice_fusion
  (98 shorter events, 4.9 us)
Async XLA Ops:
  7.2 1.4 copy-start.8
  7.2 5.8 %copy-start.1 = (bf16[32,16,128]{2,1,0:T(8,128)(2,1)S(1)}, bf16[32,16,128]{2,1,0:T(8,128)(2,1)}, u32[]{:S(2)}) copy-start(bf16[32,16,128]{2,1,0:T(8,128)(2,1)} %param.11) | copy-start | bytes 393220
  7.2 7.9 %copy-start = (bf16[4,4,256,128]{3,2,1,0:T(8,128)(2,1)S(1)}, bf16[4,4,256,128]{3,2,1,0:T(8,128)(2,1)}, u32[]{:S(2)}) copy-start(bf16[4,4,256,128]{3,2,1,0:T(8,128)(2,1)} %param.8) | copy-start | bytes 3145732
  7.2 196.2 %all-reduce.3.cloned.1.call-start = ((), (), s32[]{:S(2)}) async-start(), calls=%async_computation | async-start | bytes 5373952 | tf_op jit(solution)/shard_map/psum | solution.py:136
  8.9 6.3 %copy-start.5 = (bf16[3,3,128,128]{3,2,1,0:T(8,128)(2,1)S(1)}, bf16[3,3,128,128]{3,2,1,0:T(8,128)(2,1)}, u32[]{:S(2)}) copy-start(bf16[3,3,128,128]{3,2,1,0:T(8,128)(2,1)} %param.10) | copy-start | bytes 884740
  8.9 6.4 %collective-permute-start = (bf16[16,1,256]{2,1,0:T(2,128)(2,1)S(1)}, bf16[16,1,256]{2,1,0:T(2,128)(2,1)S(1)}, u32[]{:S(2)}, u32[]{:S(2)}) collective-permute-start(bf16[16,1,256]{2,1,0:T(2,128)(2,1)S(1)} %get-tuple-element.50), channel_id=1, source_target_pairs={{0,1},{1,2},{2,3},{3,0},{4,5},{5,6},{6,7},{7,4},{8,9},{9,10},{10,1... | collective-permute-start | bytes 24584 | tf_op jit(solution)/shard_map/ppermute | solution.py:23
  11.9 3.7 %collective-permute-start.1 = (bf16[16,1,256]{2,1,0:T(2,128)(2,1)S(1)}, bf16[16,1,256]{2,1,0:T(2,128)(2,1)S(1)}, u32[]{:S(2)}, u32[]{:S(2)}) collective-permute-start(bf16[16,1,256]{2,1,0:T(2,128)(2,1)S(1)} %get-tuple-element.51), channel_id=1, source_target_pairs={{1,0},{2,1},{3,2},{0,3},{5,4},{6,5},{7,6},{4,7},{9,8},{10,9},{11,1... | collective-permute-start | bytes 24584 | tf_op jit(solution)/shard_map/ppermute | solution.py:24
  13.0 5.3 %collective-permute-start.9 = (bf16[32,1,128]{2,1,0:T(2,128)(2,1)S(1)}, bf16[32,1,128]{2,1,0:T(2,128)(2,1)S(1)}, u32[]{:S(2)}, u32[]{:S(2)}) collective-permute-start(bf16[32,1,128]{2,1,0:T(2,128)(2,1)S(1)} %get-tuple-element.41), channel_id=1, source_target_pairs={{1,0},{2,1},{3,2},{0,3},{5,4},{6,5},{7,6},{4,7},{9,8},{10,9},{11,1... | collective-permute-start | bytes 24584 | tf_op jit(solution)/shard_map/ppermute | solution.py:24
  15.0 4.6 %collective-permute-start.8 = (bf16[32,1,128]{2,1,0:T(2,128)(2,1)S(1)}, bf16[32,1,128]{2,1,0:T(2,128)(2,1)S(1)}, u32[]{:S(2)}, u32[]{:S(2)}) collective-permute-start(bf16[32,1,128]{2,1,0:T(2,128)(2,1)S(1)} %get-tuple-element.40), channel_id=1, source_target_pairs={{0,1},{1,2},{2,3},{3,0},{4,5},{5,6},{6,7},{7,4},{8,9},{9,10},{10,1... | collective-permute-start | bytes 24584 | tf_op jit(solution)/shard_map/ppermute | solution.py:23
  15.7 12.6 %collective-permute-start.2 = (bf16[1,10,256]{2,1,0:T(8,128)(2,1)S(1)}, bf16[1,10,256]{2,1,0:T(8,128)(2,1)S(1)}, u32[]{:S(2)}, u32[]{:S(2)}) collective-permute-start(bf16[1,10,256]{2,1,0:T(8,128)(2,1)S(1)} %get-tuple-element.46), channel_id=1, source_target_pairs={{0,4},{4,8},{8,12},{12,16},{16,20},{20,24},{24,28},{1,5},{5,9},{9,... | collective-permute-start | bytes 15368 | tf_op jit(solution)/shard_map/ppermute | solution.py:23
  17.0 11.3 %collective-permute-start.3 = (bf16[1,10,256]{2,1,0:T(8,128)(2,1)S(1)}, bf16[1,10,256]{2,1,0:T(8,128)(2,1)S(1)}, u32[]{:S(2)}, u32[]{:S(2)}) collective-permute-start(bf16[1,10,256]{2,1,0:T(8,128)(2,1)S(1)} %get-tuple-element.47), channel_id=1, source_target_pairs={{4,0},{8,4},{12,8},{16,12},{20,16},{24,20},{28,24},{5,1},{9,5},{13... | collective-permute-start | bytes 15368 | tf_op jit(solution)/shard_map/ppermute | solution.py:24
  19.6 5.0 %collective-permute-start.11 = (bf16[1,18,128]{2,1,0:T(8,128)(2,1)S(1)}, bf16[1,18,128]{2,1,0:T(8,128)(2,1)S(1)}, u32[]{:S(2)}, u32[]{:S(2)}) collective-permute-start(bf16[1,18,128]{2,1,0:T(8,128)(2,1)S(1)} %get-tuple-element.26), channel_id=1, source_target_pairs={{0,4},{4,8},{8,12},{12,16},{16,20},{20,24},{24,28},{1,5},{5,9},{9,... | collective-permute-start | bytes 13832 | tf_op jit(solution)/shard_map/ppermute | solution.py:23
  23.3 4.3 %collective-permute-start.10 = (bf16[1,18,128]{2,1,0:T(8,128)(2,1)S(1)}, bf16[1,18,128]{2,1,0:T(8,128)(2,1)S(1)}, u32[]{:S(2)}, u32[]{:S(2)}) collective-permute-start(bf16[1,18,128]{2,1,0:T(8,128)(2,1)S(1)} %get-tuple-element.27), channel_id=1, source_target_pairs={{4,0},{8,4},{12,8},{16,12},{20,16},{24,20},{28,24},{5,1},{9,5},{13... | collective-permute-start | bytes 13832 | tf_op jit(solution)/shard_map/ppermute | solution.py:24
  29.2 0.7 copy-start.9
  30.5 5.9 %collective-permute-start.13 = (bf16[32,1,128]{2,1,0:T(2,128)(2,1)S(1)}, bf16[32,1,128]{2,1,0:T(2,128)(2,1)S(1)}, u32[]{:S(2)}, u32[]{:S(2)}) collective-permute-start(bf16[32,1,128]{2,1,0:T(2,128)(2,1)S(1)} %get-tuple-element.39), channel_id=1, source_target_pairs={{1,0},{2,1},{3,2},{0,3},{5,4},{6,5},{7,6},{4,7},{9,8},{10,9},{11,1... | collective-permute-start | bytes 24584 | tf_op jit(solution)/shard_map/ppermute | solution.py:24
  33.0 4.6 %collective-permute-start.12 = (bf16[32,1,128]{2,1,0:T(2,128)(2,1)S(1)}, bf16[32,1,128]{2,1,0:T(2,128)(2,1)S(1)}, u32[]{:S(2)}, u32[]{:S(2)}) collective-permute-start(bf16[32,1,128]{2,1,0:T(2,128)(2,1)S(1)} %get-tuple-element.38), channel_id=1, source_target_pairs={{0,1},{1,2},{2,3},{3,0},{4,5},{5,6},{6,7},{7,4},{8,9},{9,10},{10,1... | collective-permute-start | bytes 24584 | tf_op jit(solution)/shard_map/ppermute | solution.py:23
  33.4 9.2 %collective-permute-start.5 = (bf16[32,1,128]{2,1,0:T(2,128)(2,1)S(1)}, bf16[32,1,128]{2,1,0:T(2,128)(2,1)S(1)}, u32[]{:S(2)}, u32[]{:S(2)}) collective-permute-start(bf16[32,1,128]{2,1,0:T(2,128)(2,1)S(1)} %get-tuple-element.43), channel_id=1, source_target_pairs={{1,0},{2,1},{3,2},{0,3},{5,4},{6,5},{7,6},{4,7},{9,8},{10,9},{11,1... | collective-permute-start | bytes 24584 | tf_op jit(solution)/shard_map/ppermute | solution.py:24
  36.4 6.2 %collective-permute-start.4 = (bf16[32,1,128]{2,1,0:T(2,128)(2,1)S(1)}, bf16[32,1,128]{2,1,0:T(2,128)(2,1)S(1)}, u32[]{:S(2)}, u32[]{:S(2)}) collective-permute-start(bf16[32,1,128]{2,1,0:T(2,128)(2,1)S(1)} %get-tuple-element.42), channel_id=1, source_target_pairs={{0,1},{1,2},{2,3},{3,0},{4,5},{5,6},{6,7},{7,4},{8,9},{9,10},{10,1... | collective-permute-start | bytes 24584 | tf_op jit(solution)/shard_map/ppermute | solution.py:23
  37.8 11.5 %collective-permute-start.15 = (bf16[1,18,128]{2,1,0:T(8,128)(2,1)S(1)}, bf16[1,18,128]{2,1,0:T(8,128)(2,1)S(1)}, u32[]{:S(2)}, u32[]{:S(2)}) collective-permute-start(bf16[1,18,128]{2,1,0:T(8,128)(2,1)S(1)} %get-tuple-element.23), channel_id=1, source_target_pairs={{4,0},{8,4},{12,8},{16,12},{20,16},{24,20},{28,24},{5,1},{9,5},{13... | collective-permute-start | bytes 13832 | tf_op jit(solution)/shard_map/ppermute | solution.py:24
  39.1 10.2 %collective-permute-start.14 = (bf16[1,18,128]{2,1,0:T(8,128)(2,1)S(1)}, bf16[1,18,128]{2,1,0:T(8,128)(2,1)S(1)}, u32[]{:S(2)}, u32[]{:S(2)}) collective-permute-start(bf16[1,18,128]{2,1,0:T(8,128)(2,1)S(1)} %get-tuple-element.22), channel_id=1, source_target_pairs={{0,4},{4,8},{8,12},{12,16},{16,20},{20,24},{24,28},{1,5},{5,9},{9,... | collective-permute-start | bytes 13832 | tf_op jit(solution)/shard_map/ppermute | solution.py:23
  43.7 11.3 %collective-permute-start.7 = (bf16[1,18,128]{2,1,0:T(8,128)(2,1)S(1)}, bf16[1,18,128]{2,1,0:T(8,128)(2,1)S(1)}, u32[]{:S(2)}, u32[]{:S(2)}) collective-permute-start(bf16[1,18,128]{2,1,0:T(8,128)(2,1)S(1)} %get-tuple-element.30), channel_id=1, source_target_pairs={{4,0},{8,4},{12,8},{16,12},{20,16},{24,20},{28,24},{5,1},{9,5},{13... | collective-permute-start | bytes 13832 | tf_op jit(solution)/shard_map/ppermute | solution.py:24
  45.0 10.0 %collective-permute-start.6 = (bf16[1,18,128]{2,1,0:T(8,128)(2,1)S(1)}, bf16[1,18,128]{2,1,0:T(8,128)(2,1)S(1)}, u32[]{:S(2)}, u32[]{:S(2)}) collective-permute-start(bf16[1,18,128]{2,1,0:T(8,128)(2,1)S(1)} %get-tuple-element.31), channel_id=1, source_target_pairs={{0,4},{4,8},{8,12},{12,16},{16,20},{20,24},{24,28},{1,5},{5,9},{9,... | collective-permute-start | bytes 13832 | tf_op jit(solution)/shard_map/ppermute | solution.py:23
  55.8 1.1 copy-start.2
  57.2 0.8 copy-start.6
  62.5 2.0 copy-start.3
  65.8 1.3 copy-start.4
  66.4 2.8 %copy-start.7 = (bf16[16,8,2048]{2,1,0:T(8,128)(2,1)S(1)}, bf16[16,8,2048]{2,1,0:T(8,128)(2,1)}, u32[]{:S(2)}) copy-start(bf16[16,8,2048]{2,1,0:T(8,128)(2,1)} %copy-done.6) | copy-start | bytes 1572868
Sparse Core Ops, SparseCore 0:
  66.0 137.3 all-reduce.2
where the time goes:
time: 214 us
  waiting for transfers between devices  139 us (65%)
  starting transfers between devices  29.5 us (14%)
  local copies, waits for them, and re-layouts  20.3 us (9%)
  between operations  14.7 us (7%)
  matrix products  7.63 us (4%)
  other arithmetic  2.46 us (1%)
    psum x1, waiting for transfers between devices, shards(): summed = lax.psum((up_grad, mix_grad), ('lat', 'lon'))  133 us
    ppermute x8, starting transfers between devices, padded_2(): before = lax.ppermute(last, axis, up)  15.8 us
    ppermute x8, starting transfers between devices, padded_2(): after = lax.ppermute(leading, axis, down)  13.7 us
    slice x16, local copies, waits for them, and re-layouts, strided(): padded[row_tap:row_tap + 2 * row_count:2, col_tap:col_tap + 2 * col_count:2]  6.91 us
    mul x2, local copies, waits for them, and re-layouts, shards(): up_flat.reshape(CIN, 4, 4, COUT).transpose(1, 2, 0, 3) * grad_scale  4.64 us
  transfers between devices with their start and end apart: 17, of which 5 were waited for; matrix products, arithmetic and copies ran while one was open for 6% of the time, Pallas kernels for 0%

commit v1 on v0

--- a/solution.py
+++ b/solution.py
@@ -120,11 +120,11 @@
         "rck,kn->rcn", patches, mix_flat, preferred_element_type=jnp.float32
     ).astype(jnp.bfloat16)
     grad_scale = 1.0 / math.sqrt(out_rows * lat_count * out_cols * lon_count)
-    mix_grad = (
-        jnp.einsum("rck,rcn->kn", patches, cotangent, preferred_element_type=jnp.float32).reshape(
-            3, 3, COUT, COUT
-        )
-        * grad_scale
+    mix_flat_grad = jnp.einsum(
+        "rctm,rcn->mtn",
+        patches.reshape(out_rows, out_cols, 9, COUT),
+        cotangent,
+        preferred_element_type=jnp.float32,
     )
     grad_patches = strided(pre_grad_pad, in_rows, in_cols)
     back_up = up_kernel.transpose(0, 1, 3, 2).reshape(16 * COUT, CIN)
@@ -132,14 +132,78 @@
         "rck,kn->rcn", grad_patches, back_up, preferred_element_type=jnp.float32
     )
     up_flat = jnp.einsum("rcm,rck->mk", inputs, grad_patches, preferred_element_type=jnp.float32)
-    up_grad = up_flat.reshape(CIN, 4, 4, COUT).transpose(1, 2, 0, 3) * grad_scale
-    summed = lax.psum((up_grad, mix_grad), ("lat", "lon"))
-    lon_index = lax.axis_index("lon")
     up_span = CIN // lon_count
     mix_span = COUT // lon_count
-    up_part = lax.dynamic_slice_in_dim(summed[0], lon_index * up_span, up_span, 2)
-    mix_part = lax.dynamic_slice_in_dim(summed[1], lon_index * mix_span, mix_span, 2)
+    up_size = up_span * 16 * COUT
+    terms = jnp.concatenate(
+        [up_flat.reshape(lon_count, up_size), mix_flat_grad.reshape(lon_count, -1)], axis=1
+    )
+    summed = reduce_terms(terms) * grad_scale
+    up_part = summed[:up_size].reshape(up_span, 4, 4, COUT).transpose(1, 2, 0, 3)
+    mix_part = summed[up_size:].reshape(mix_span, 3, 3, COUT).transpose(1, 2, 0, 3)
     return (section_out, input_grad, up_part, mix_part)
+
+
+def exchange(part, axis, step):
+    size = lax.axis_size(axis)
+    return lax.ppermute(part, axis, [(i, i ^ step) for i in range(size)])
+
+
+def halve(buffer, axis, step, dim):
+    own = lax.axis_index(axis) // step % 2
+    keep = lax.dynamic_index_in_dim(buffer, own, dim, keepdims=False)
+    send = lax.dynamic_index_in_dim(buffer, 1 - own, dim, keepdims=False)
+    return keep + exchange(send, axis, step)
+
+
+def double(part, axis, step):
+    own = lax.axis_index(axis) // step % 2
+    got = exchange(part, axis, step)
+    low = jnp.where(own == 0, part, got)
+    high = jnp.where(own == 0, got, part)
+    return jnp.concatenate([low, high])
+
+
+def steps_of(size):
+    count = size.bit_length() - 1
+    return [1 << k for k in range(count)] if size == 1 << count else None
+
+
+def scatter_lon(rows, order):
+    lon_count = rows.shape[0]
+    steps = steps_of(lon_count)
+    width = len(steps)
+    grid = rows.reshape((2,) * width + rows.shape[1:])
+    held = list(reversed(steps))
+    for step in order:
+        dim = held.index(step)
+        grid = halve(grid, "lon", step, dim)
+        held.pop(dim)
+    return grid
+
+
+def reduce_lat(flat):
+    steps = steps_of(lax.axis_size("lat"))
+    if steps is None or flat.shape[0] % (1 << len(steps)):
+        return lax.psum(flat, "lat")
+    for step in steps:
+        flat = halve(flat.reshape(2, -1), "lat", step, 0)
+    for step in reversed(steps):
+        flat = double(flat, "lat", step)
+    return flat
+
+
+def reduce_terms(rows):
+    lon_count = rows.shape[0]
+    steps = steps_of(lon_count)
+    if steps is None or rows.shape[1] % 2:
+        own = lax.axis_index("lon")
+        mine = lax.dynamic_index_in_dim(lax.psum(rows, "lon"), own, 0, keepdims=False)
+        return reduce_lat(mine)
+    half = rows.shape[1] // 2
+    first = scatter_lon(rows[:, :half], steps)
+    second = scatter_lon(rows[:, half:], list(reversed(steps)))
+    return jnp.concatenate([reduce_lat(first), reduce_lat(second)])
 
 
 def solution(mesh):

time: 214 us -> 134 us (0.63)
  waiting for transfers between devices: 139 us -> 38.2 us
  starting transfers between devices: 29.5 us -> 45.7 us
  between operations: 14.7 us -> 1.82 us
  local copies, waits for them, and re-layouts: 20.3 us -> 29.9 us
  other arithmetic: 2.46 us -> 9.19 us
    psum x1 -> x0, waiting for transfers between devices: 133 us -> none  [shards(): summed = lax.psum((up_grad, mix_grad), ('lat', 'lon'))]
    ppermute x0 -> x16, waiting for transfers between devices: none -> 32.5 us  [exchange(): return lax.ppermute(part, axis, [(i, i ^ step) for i in range(size)])]
    ppermute x0 -> x16, starting transfers between devices: none -> 16.2 us  [exchange(): return lax.ppermute(part, axis, [(i, i ^ step) for i in range(size)])]
    reshape x0 -> x11, local copies, waits for them, and re-layouts: none -> 8.27 us  [the longest x2 3.4 us: scatter_lon(): grid = rows.reshape((2,) * width + rows.shape[1:])]
    mul x2 -> x0, local copies, waits for them, and re-layouts: 4.64 us -> none  [shards(): up_flat.reshape(CIN, 4, 4, COUT).transpose(1, 2, 0, 3) * grad_scale]
    unnamed x48 -> x53, local copies, waits for them, and re-layouts: 4.25 us -> 7.76 us
    slice x0 -> x1, other arithmetic: none -> 2.52 us  [reduce_terms(): first = scatter_lon(rows[:, :half], steps)]
    dynamic_slice x2 -> x9, local copies, waits for them, and re-layouts: 3.47 us -> 4.55 us  [the longest x8 3.39 us: halve(): send = lax.dynamic_index_in_dim(buffer, 1 - own, dim, keepdims=False)]
  transfers between devices with their start and end apart: 17 -> 32, of which waited for: 5 -> 14; matrix products, arithmetic and copies ran while one was open for 6% -> 16% of each run, Pallas kernels for 0% -> 0%
where the time goes in v1:
time: 134 us; the launch traced here: 133 us
  starting transfers between devices  45.7 us (34%)
  waiting for transfers between devices  38.2 us (29%)
  local copies, waits for them, and re-layouts  29.9 us (22%)
  other arithmetic  9.19 us (7%)
  matrix products  8.34 us (6%)
  between operations  1.82 us (1%)
    ppermute x16, waiting for transfers between devices, exchange(): return lax.ppermute(part, axis, [(i, i ^ step) for i in range(size)])  32.5 us
    ppermute x16, starting transfers between devices, exchange(): return lax.ppermute(part, axis, [(i, i ^ step) for i in range(size)])  16.2 us
    ppermute x8, starting transfers between devices, padded_2(): before = lax.ppermute(last, axis, up)  15.9 us
    ppermute x8, starting transfers between devices, padded_2(): after = lax.ppermute(leading, axis, down)  13.7 us
    unnamed x53, local copies, waits for them, and re-layouts  7.76 us
    slice x16, local copies, waits for them, and re-layouts, strided(): padded[row_tap:row_tap + 2 * row_count:2, col_tap:col_tap + 2 * col_count:2]  7.09 us
    reshape x2, local copies, waits for them, and re-layouts, scatter_lon(): grid = rows.reshape((2,) * width + rows.shape[1:])  3.4 us
    dynamic_slice x8, local copies, waits for them, and re-layouts, halve(): send = lax.dynamic_index_in_dim(buffer, 1 - own, dim, keepdims=False)  3.39 us
  transfers between devices with their start and end apart: 32, of which 14 were waited for; matrix products, arithmetic and copies ran while one was open for 16% of the time, Pallas kernels for 0%

profile of v1, /device:TPU:0, one launch (start us, length us, event | category | flops | bytes accessed | tf_op | source)
XLA Modules:
  0.0 133.2 jit_solution(16522022143993892866)
XLA Ops:
  0.7 0.9 multiply_exponential_fusion
  2.4 3.0 %collective-permute-start = (bf16[16,1,256]{2,1,0:T(2,128)(2,1)S(1)}, bf16[16,1,256]{2,1,0:T(2,128)(2,1)S(1)}, u32[]{:S(2)}, u32[]{:S(2)}) collective-permute-start(bf16[16,1,256]{2,1,0:T(2,128)(2,1)S(1)} %get-tuple-element.84), channel_id=1, source_target_pairs={{0,1},{1,2},{2,3},{3,0},{4,5},{5,6},{6,7},{7,4},{8,9},{9,10},{10,1... | collective-permute-start | bytes 24584 | tf_op jit(solution)/shard_map/ppermute | solution.py:23
  5.3 1.0 collective-permute-start.1
  6.4 2.0 %collective-permute-start.9 = (bf16[32,1,128]{2,1,0:T(2,128)(2,1)S(1)}, bf16[32,1,128]{2,1,0:T(2,128)(2,1)S(1)}, u32[]{:S(2)}, u32[]{:S(2)}) collective-permute-start(bf16[32,1,128]{2,1,0:T(2,128)(2,1)S(1)} %get-tuple-element.71), channel_id=1, source_target_pairs={{1,0},{2,1},{3,2},{0,3},{5,4},{6,5},{7,6},{4,7},{9,8},{10,9},{11,1... | collective-permute-start | bytes 24584 | tf_op jit(solution)/shard_map/ppermute | solution.py:24
  9.1 1.3 collective-permute-start.2
  10.4 1.3 collective-permute-start.3
  11.7 1.3 %collective-permute-done.8 = bf16[32,1,128]{2,1,0:T(2,128)(2,1)S(1)} collective-permute-done((bf16[32,1,128]{2,1,0:T(2,128)(2,1)S(1)}, bf16[32,1,128]{2,1,0:T(2,128)(2,1)S(1)}, u32[]{:S(2)}, u32[]{:S(2)}) %collective-permute-start.8) | collective-permute-done | bytes 8224 | tf_op jit(solution)/shard_map/ppermute | solution.py:23
  13.1 3.8 %collective-permute-start.11 = (bf16[1,18,128]{2,1,0:T(8,128)(2,1)S(1)}, bf16[1,18,128]{2,1,0:T(8,128)(2,1)S(1)}, u32[]{:S(2)}, u32[]{:S(2)}) collective-permute-start(bf16[1,18,128]{2,1,0:T(8,128)(2,1)S(1)} %get-tuple-element.56), channel_id=1, source_target_pairs={{0,4},{4,8},{8,12},{12,16},{16,20},{20,24},{24,28},{1,5},{5,9},{9,... | collective-permute-start | bytes 13832 | tf_op jit(solution)/shard_map/ppermute | solution.py:23
  16.8 1.3 collective-permute-start.10
  18.2 2.9 %collective-permute-done.10 = bf16[1,18,128]{2,1,0:T(8,128)(2,1)S(1)} collective-permute-done((bf16[1,18,128]{2,1,0:T(8,128)(2,1)S(1)}, bf16[1,18,128]{2,1,0:T(8,128)(2,1)S(1)}, u32[]{:S(2)}, u32[]{:S(2)}) %collective-permute-start.10) | collective-permute-done | bytes 4640 | tf_op jit(solution)/shard_map/ppermute | solution.py:24
  24.0 2.5 %collective-permute-start.13 = (bf16[32,1,128]{2,1,0:T(2,128)(2,1)S(1)}, bf16[32,1,128]{2,1,0:T(2,128)(2,1)S(1)}, u32[]{:S(2)}, u32[]{:S(2)}) collective-permute-start(bf16[32,1,128]{2,1,0:T(2,128)(2,1)S(1)} %get-tuple-element.69), channel_id=1, source_target_pairs={{1,0},{2,1},{3,2},{0,3},{5,4},{6,5},{7,6},{4,7},{9,8},{10,9},{11,1... | collective-permute-start | bytes 24584 | tf_op jit(solution)/shard_map/ppermute | solution.py:24
  26.9 3.0 %collective-permute-start.5 = (bf16[32,1,128]{2,1,0:T(2,128)(2,1)S(1)}, bf16[32,1,128]{2,1,0:T(2,128)(2,1)S(1)}, u32[]{:S(2)}, u32[]{:S(2)}) collective-permute-start(bf16[32,1,128]{2,1,0:T(2,128)(2,1)S(1)} %get-tuple-element.73), channel_id=1, source_target_pairs={{1,0},{2,1},{3,2},{0,3},{5,4},{6,5},{7,6},{4,7},{9,8},{10,9},{11,1... | collective-permute-start | bytes 24584 | tf_op jit(solution)/shard_map/ppermute | solution.py:24
  29.9 1.3 collective-permute-done.12
  31.3 1.3 collective-permute-start.15
  32.6 3.5 %collective-permute-start.14 = (bf16[1,18,128]{2,1,0:T(8,128)(2,1)S(1)}, bf16[1,18,128]{2,1,0:T(8,128)(2,1)S(1)}, u32[]{:S(2)}, u32[]{:S(2)}) collective-permute-start(bf16[1,18,128]{2,1,0:T(8,128)(2,1)S(1)} %get-tuple-element.48), channel_id=1, source_target_pairs={{0,4},{4,8},{8,12},{12,16},{16,20},{20,24},{24,28},{1,5},{5,9},{9,... | collective-permute-start | bytes 13832 | tf_op jit(solution)/shard_map/ppermute | solution.py:23
  37.2 1.3 collective-permute-start.7
  38.5 4.3 %collective-permute-start.6 = (bf16[1,18,128]{2,1,0:T(8,128)(2,1)S(1)}, bf16[1,18,128]{2,1,0:T(8,128)(2,1)S(1)}, u32[]{:S(2)}, u32[]{:S(2)}) collective-permute-start(bf16[1,18,128]{2,1,0:T(8,128)(2,1)S(1)} %get-tuple-element.61), channel_id=1, source_target_pairs={{0,4},{4,8},{8,12},{12,16},{16,20},{20,24},{24,28},{1,5},{5,9},{9,... | collective-permute-start | bytes 13832 | tf_op jit(solution)/shard_map/ppermute | solution.py:23
  47.0 0.7 slice.330
  47.8 0.9 slice.331
  51.8 0.8 constant_dynamic-update-slice_fusion
  55.7 0.8 copy-done.7
  56.5 1.8 %convolution_bitcast_fusion = f32[256,2048]{1,0:T(8,128)} fusion(bf16[16,8,256]{2,1,0:T(8,128)(2,1)S(1)} %fusion.78, bf16[16,8,2048]{2,1,0:T(8,128)(2,1)S(1)} %constant_dynamic-update-slice_fusion.2), kind=kOutput, calls=%fused_computation | convolution fusion | flops 134217728 | bytes 2686976 | tf_op jit(solution)/shard_map/rcm,rck->mk/dot_general | solution.py:134
  58.3 3.0 %reshape.71 = f32[4,131072]{1,0:T(4,128)S(1)} reshape(f32[256,2048]{1,0:T(8,128)} %convolution_bitcast_fusion) | data formatting | bytes 4194304 | tf_op jit(solution)/shard_map/reshape | solution.py:139
  61.3 1.8 %convolution_bitcast_fusion.1 = f32[128,9,128]{2,0,1:T(8,128)S(1)} fusion(bf16[32,16,128]{2,1,0:T(8,128)(2,1)S(1)} %copy-done.4, bf16[32,16,1152]{2,1,0:T(8,128)(2,1)} %slice_dynamic-update-slice_fusion.6), kind=kOutput, calls=%fused_computation.2 | convolution fusion | flops 150994944 | bytes 1900544 | tf_op jit(solution)/shard_map/rctm,rcn->mtn/dot_general | solution.py:123
  63.5 1.1 reshape.77
  64.6 2.5 %fusion.85 = (f32[4,83968]{1,0:T(4,128)S(1)}, f32[4,83968]{1,0:T(4,128)}) fusion(f32[4,131072]{1,0:T(4,128)S(1)} %reshape.71, f32[4,36864]{1,0:T(4,128)} %reshape.77), kind=kLoop, calls=%fused_computation.227 | loop fusion | flops 335872 | bytes 6717440 | tf_op jit(solution)/shard_map/slice | solution.py:204
  67.1 2.4 %reshape.78 = f32[2,2,83968]{2,1,0:T(2,128)S(1)} reshape(f32[4,83968]{1,0:T(4,128)} %get-tuple-element.17) | data formatting | bytes 2686976 | tf_op jit(solution)/shard_map/reshape | solution.py:176
  69.5 1.3 collective-permute-start.24
  70.8 1.0 reshape.72
  71.8 1.2 constant_dynamic-slice_fusion.9
  73.3 1.5 %collective-permute-start.16 = (f32[2,83968]{1,0:T(2,128)S(1)}, f32[2,83968]{1,0:T(2,128)S(1)}, u32[]{:S(2)}, u32[]{:S(2)}) collective-permute-start(f32[2,83968]{1,0:T(2,128)S(1)} %bitcast.127), channel_id=1, source_target_pairs={{0,1},{1,0},{2,3},{3,2},{4,5},{5,4},{6,7},{7,6},{8,9},{9,8},{10,11... | collective-permute-start | bytes 2015240 | tf_op jit(solution)/shard_map/ppermute | solution.py:149
  74.9 12.0 %collective-permute-done.24 = f32[2,83968]{1,0:T(2,128)} collective-permute-done((f32[2,83968]{1,0:T(2,128)S(1)}, f32[2,83968]{1,0:T(2,128)}, u32[]{:S(2)}, u32[]{:S(2)}) %collective-permute-start.24) | collective-permute-done | bytes 671776 | tf_op jit(solution)/shard_map/ppermute | solution.py:149
  86.9 1.4 %bitcast_add_fusion.1 = f32[2,83968]{1,0:T(2,128)S(1)} fusion(f32[2,83968]{1,0:T(2,128)} %collective-permute-done.24, f32[2,2,83968]{2,1,0:T(2,128)S(1)} %copy-done.1, s32[]{:T(128)S(6)} %select_n.214), kind=kLoop, calls=%fused_computation.15 | loop fusion | flops 167936 | bytes 2015236 | tf_op jit(solution)/shard_map/add | solution.py:156
  88.9 1.7 %collective-permute-start.25 = (f32[83968]{0:T(1024)S(1)}, f32[83968]{0:T(1024)S(1)}, u32[]{:S(2)}, u32[]{:S(2)}) collective-permute-start(f32[83968]{0:T(1024)S(1)} %bitcast.130), channel_id=1, source_target_pairs={{0,1},{1,0},{2,3},{3,2},{4,5},{5,4},{6,7},{7,6},{8,9},{9,8},{10,11... | collective-permute-start | bytes 1007624 | tf_op jit(solution)/shard_map/ppermute | solution.py:149
  91.9 0.8 collective-permute-start.17
  92.7 6.8 %collective-permute-done.25 = f32[83968]{0:T(1024)S(1)} collective-permute-done((f32[83968]{0:T(1024)S(1)}, f32[83968]{0:T(1024)S(1)}, u32[]{:S(2)}, u32[]{:S(2)}) %collective-permute-start.25) | collective-permute-done | bytes 335904 | tf_op jit(solution)/shard_map/ppermute | solution.py:149
  100.2 1.9 %collective-permute-done.17 = f32[83968]{0:T(1024)S(1)} collective-permute-done((f32[83968]{0:T(1024)S(1)}, f32[83968]{0:T(1024)S(1)}, u32[]{:S(2)}, u32[]{:S(2)}) %collective-permute-start.17) | collective-permute-done | bytes 335904 | tf_op jit(solution)/shard_map/ppermute | solution.py:149
  103.6 1.8 %collective-permute-start.27 = (f32[20992]{0:T(1024)S(1)}, f32[20992]{0:T(1024)S(1)}, u32[]{:S(2)}, u32[]{:S(2)}) collective-permute-start(f32[20992]{0:T(1024)S(1)} %get-tuple-element.10), channel_id=1, source_target_pairs={{0,8},{4,12},{8,0},{12,4},{16,24},{20,28},{24,16},{28,20},{1,9},{5... | collective-permute-start | bytes 251912 | tf_op jit(solution)/shard_map/ppermute | solution.py:149
  107.0 1.6 %collective-permute-done.27 = f32[20992]{0:T(1024)S(1)} collective-permute-done((f32[20992]{0:T(1024)S(1)}, f32[20992]{0:T(1024)S(1)}, u32[]{:S(2)}, u32[]{:S(2)}) %collective-permute-start.27) | collective-permute-done | bytes 84000 | tf_op jit(solution)/shard_map/ppermute | solution.py:149
  108.9 3.3 %collective-permute-start.28 = (f32[10496]{0:T(1024)S(1)}, f32[10496]{0:T(1024)S(1)}, u32[]{:S(2)}, u32[]{:S(2)}) collective-permute-start(f32[10496]{0:T(1024)S(1)} %get-tuple-element.14), channel_id=1, source_target_pairs={{0,16},{4,20},{8,24},{12,28},{16,0},{20,4},{24,8},{28,12},{1,17},{... | collective-permute-start | bytes 125960 | tf_op jit(solution)/shard_map/ppermute | solution.py:149
  112.2 1.0 fusion.93
  114.2 3.5 %collective-permute-start.29 = (f32[10496]{0:T(1024)S(1)}, f32[10496]{0:T(1024)S(1)}, u32[]{:S(2)}, u32[]{:S(2)}) collective-permute-start(f32[10496]{0:T(1024)S(1)} %add.180), channel_id=1, source_target_pairs={{0,16},{4,20},{8,24},{12,28},{16,0},{20,4},{24,8},{28,12},{1,17},{... | collective-permute-start | bytes 125960 | tf_op jit(solution)/shard_map/ppermute | solution.py:149
  117.7 2.4 %convolution_convert_fusion = bf16[32,16,128]{2,1,0:T(8,128)(2,1)} fusion(bf16[32,16,1152]{2,1,0:T(8,128)(2,1)} %slice_dynamic-update-slice_fusion.6, bf16[1152,128,1]{1,0,2:T(8,128)(2,1)S(1)} %bitcast.125), kind=kOutput, calls=%fused_computation.7 | convolution fusion | flops 151060480 | bytes 1605632 | tf_op jit(solution)/shard_map/rck,kn->rcn/dot_general | solution.py:119
  120.2 1.4 %collective-permute-start.30 = (f32[20992]{0:T(1024)S(1)}, f32[20992]{0:T(1024)S(1)}, u32[]{:S(2)}, u32[]{:S(2)}) collective-permute-start(f32[20992]{0:T(1024)S(1)} %pad_maximum_fusion.14), channel_id=1, source_target_pairs={{0,8},{4,12},{8,0},{12,4},{16,24},{20,28},{24,16},{28,20},{1,9},{5... | collective-permute-start | bytes 251912 | tf_op jit(solution)/shard_map/ppermute | solution.py:149
  121.7 3.6 %collective-permute-done.21 = f32[10496]{0:T(1024)S(1)} collective-permute-done((f32[10496]{0:T(1024)S(1)}, f32[10496]{0:T(1024)S(1)}, u32[]{:S(2)}, u32[]{:S(2)}) %collective-permute-start.21) | collective-permute-done | bytes 42016 | tf_op jit(solution)/shard_map/ppermute | solution.py:149
  125.8 4.0 %collective-permute-done.22 = f32[20992]{0:T(1024)S(1)} collective-permute-done((f32[20992]{0:T(1024)S(1)}, f32[20992]{0:T(1024)S(1)}, u32[]{:S(2)}, u32[]{:S(2)}) %collective-permute-start.22) | collective-permute-done | bytes 84000 | tf_op jit(solution)/shard_map/ppermute | solution.py:149
  130.0 1.3 %collective-permute-done.23 = f32[41984]{0:T(1024)S(1)} collective-permute-done((f32[41984]{0:T(1024)S(1)}, f32[41984]{0:T(1024)S(1)}, u32[]{:S(2)}, u32[]{:S(2)}) %collective-permute-start.23) | collective-permute-done | bytes 167968 | tf_op jit(solution)/shard_map/ppermute | solution.py:149
  131.5 1.0 copy.24
  (174 shorter events, 25.1 us)
Async XLA Ops:
  0.6 1.4 %copy-start.9 = (s32[16,8,256]{2,1,0:T(8,128)S(1)}, s32[16,8,256]{2,1,0:T(8,128)}, u32[]{:S(2)}) copy-start(s32[16,8,256]{2,1,0:T(8,128)} %param.6) | copy-start | bytes 393220
  0.6 5.7 %copy-start.4 = (bf16[32,16,128]{2,1,0:T(8,128)(2,1)S(1)}, bf16[32,16,128]{2,1,0:T(8,128)(2,1)}, u32[]{:S(2)}) copy-start(bf16[32,16,128]{2,1,0:T(8,128)(2,1)} %param.11) | copy-start | bytes 393220
  0.7 7.8 %copy-start.2 = (bf16[4,4,256,128]{3,2,1,0:T(8,128)(2,1)S(1)}, bf16[4,4,256,128]{3,2,1,0:T(8,128)(2,1)}, u32[]{:S(2)}) copy-start(bf16[4,4,256,128]{3,2,1,0:T(8,128)(2,1)} %param.8) | copy-start | bytes 3145732
  2.3 6.3 %copy-start.5 = (bf16[3,3,128,128]{3,2,1,0:T(8,128)(2,1)S(1)}, bf16[3,3,128,128]{3,2,1,0:T(8,128)(2,1)}, u32[]{:S(2)}) copy-start(bf16[3,3,128,128]{3,2,1,0:T(8,128)(2,1)} %param.10) | copy-start | bytes 884740
  2.4 6.5 %collective-permute-start = (bf16[16,1,256]{2,1,0:T(2,128)(2,1)S(1)}, bf16[16,1,256]{2,1,0:T(2,128)(2,1)S(1)}, u32[]{:S(2)}, u32[]{:S(2)}) collective-permute-start(bf16[16,1,256]{2,1,0:T(2,128)(2,1)S(1)} %get-tuple-element.84), channel_id=1, source_target_pairs={{0,1},{1,2},{2,3},{3,0},{4,5},{5,6},{6,7},{7,4},{8,9},{9,10},{10,1... | collective-permute-start | bytes 24584 | tf_op jit(solution)/shard_map/ppermute | solution.py:23
  5.3 3.7 %collective-permute-start.1 = (bf16[16,1,256]{2,1,0:T(2,128)(2,1)S(1)}, bf16[16,1,256]{2,1,0:T(2,128)(2,1)S(1)}, u32[]{:S(2)}, u32[]{:S(2)}) collective-permute-start(bf16[16,1,256]{2,1,0:T(2,128)(2,1)S(1)} %get-tuple-element.85), channel_id=1, source_target_pairs={{1,0},{2,1},{3,2},{0,3},{5,4},{6,5},{7,6},{4,7},{9,8},{10,9},{11,1... | collective-permute-start | bytes 24584 | tf_op jit(solution)/shard_map/ppermute | solution.py:24
  6.4 5.3 %collective-permute-start.9 = (bf16[32,1,128]{2,1,0:T(2,128)(2,1)S(1)}, bf16[32,1,128]{2,1,0:T(2,128)(2,1)S(1)}, u32[]{:S(2)}, u32[]{:S(2)}) collective-permute-start(bf16[32,1,128]{2,1,0:T(2,128)(2,1)S(1)} %get-tuple-element.71), channel_id=1, source_target_pairs={{1,0},{2,1},{3,2},{0,3},{5,4},{6,5},{7,6},{4,7},{9,8},{10,9},{11,1... | collective-permute-start | bytes 24584 | tf_op jit(solution)/shard_map/ppermute | solution.py:24
  8.4 4.6 %collective-permute-start.8 = (bf16[32,1,128]{2,1,0:T(2,128)(2,1)S(1)}, bf16[32,1,128]{2,1,0:T(2,128)(2,1)S(1)}, u32[]{:S(2)}, u32[]{:S(2)}) collective-permute-start(bf16[32,1,128]{2,1,0:T(2,128)(2,1)S(1)} %get-tuple-element.70), channel_id=1, source_target_pairs={{0,1},{1,2},{2,3},{3,0},{4,5},{5,6},{6,7},{7,4},{8,9},{9,10},{10,1... | collective-permute-start | bytes 24584 | tf_op jit(solution)/shard_map/ppermute | solution.py:23
  9.1 12.7 %collective-permute-start.2 = (bf16[1,10,256]{2,1,0:T(8,128)(2,1)S(1)}, bf16[1,10,256]{2,1,0:T(8,128)(2,1)S(1)}, u32[]{:S(2)}, u32[]{:S(2)}) collective-permute-start(bf16[1,10,256]{2,1,0:T(8,128)(2,1)S(1)} %get-tuple-element.76), channel_id=1, source_target_pairs={{0,4},{4,8},{8,12},{12,16},{16,20},{20,24},{24,28},{1,5},{5,9},{9,... | collective-permute-start | bytes 15368 | tf_op jit(solution)/shard_map/ppermute | solution.py:23
  10.4 11.4 %collective-permute-start.3 = (bf16[1,10,256]{2,1,0:T(8,128)(2,1)S(1)}, bf16[1,10,256]{2,1,0:T(8,128)(2,1)S(1)}, u32[]{:S(2)}, u32[]{:S(2)}) collective-permute-start(bf16[1,10,256]{2,1,0:T(8,128)(2,1)S(1)} %get-tuple-element.77), channel_id=1, source_target_pairs={{4,0},{8,4},{12,8},{16,12},{20,16},{24,20},{28,24},{5,1},{9,5},{13... | collective-permute-start | bytes 15368 | tf_op jit(solution)/shard_map/ppermute | solution.py:24
  13.1 5.2 %collective-permute-start.11 = (bf16[1,18,128]{2,1,0:T(8,128)(2,1)S(1)}, bf16[1,18,128]{2,1,0:T(8,128)(2,1)S(1)}, u32[]{:S(2)}, u32[]{:S(2)}) collective-permute-start(bf16[1,18,128]{2,1,0:T(8,128)(2,1)S(1)} %get-tuple-element.56), channel_id=1, source_target_pairs={{0,4},{4,8},{8,12},{12,16},{16,20},{20,24},{24,28},{1,5},{5,9},{9,... | collective-permute-start | bytes 13832 | tf_op jit(solution)/shard_map/ppermute | solution.py:23
  16.8 4.3 %collective-permute-start.10 = (bf16[1,18,128]{2,1,0:T(8,128)(2,1)S(1)}, bf16[1,18,128]{2,1,0:T(8,128)(2,1)S(1)}, u32[]{:S(2)}, u32[]{:S(2)}) collective-permute-start(bf16[1,18,128]{2,1,0:T(8,128)(2,1)S(1)} %get-tuple-element.57), channel_id=1, source_target_pairs={{4,0},{8,4},{12,8},{16,12},{20,16},{24,20},{28,24},{5,1},{9,5},{13... | collective-permute-start | bytes 13832 | tf_op jit(solution)/shard_map/ppermute | solution.py:24
  22.8 0.7 copy-start.10
  24.0 5.9 %collective-permute-start.13 = (bf16[32,1,128]{2,1,0:T(2,128)(2,1)S(1)}, bf16[32,1,128]{2,1,0:T(2,128)(2,1)S(1)}, u32[]{:S(2)}, u32[]{:S(2)}) collective-permute-start(bf16[32,1,128]{2,1,0:T(2,128)(2,1)S(1)} %get-tuple-element.69), channel_id=1, source_target_pairs={{1,0},{2,1},{3,2},{0,3},{5,4},{6,5},{7,6},{4,7},{9,8},{10,9},{11,1... | collective-permute-start | bytes 24584 | tf_op jit(solution)/shard_map/ppermute | solution.py:24
  26.5 4.6 %collective-permute-start.12 = (bf16[32,1,128]{2,1,0:T(2,128)(2,1)S(1)}, bf16[32,1,128]{2,1,0:T(2,128)(2,1)S(1)}, u32[]{:S(2)}, u32[]{:S(2)}) collective-permute-start(bf16[32,1,128]{2,1,0:T(2,128)(2,1)S(1)} %get-tuple-element.68), channel_id=1, source_target_pairs={{0,1},{1,2},{2,3},{3,0},{4,5},{5,6},{6,7},{7,4},{8,9},{9,10},{10,1... | collective-permute-start | bytes 24584 | tf_op jit(solution)/shard_map/ppermute | solution.py:23
  26.9 9.2 %collective-permute-start.5 = (bf16[32,1,128]{2,1,0:T(2,128)(2,1)S(1)}, bf16[32,1,128]{2,1,0:T(2,128)(2,1)S(1)}, u32[]{:S(2)}, u32[]{:S(2)}) collective-permute-start(bf16[32,1,128]{2,1,0:T(2,128)(2,1)S(1)} %get-tuple-element.73), channel_id=1, source_target_pairs={{1,0},{2,1},{3,2},{0,3},{5,4},{6,5},{7,6},{4,7},{9,8},{10,9},{11,1... | collective-permute-start | bytes 24584 | tf_op jit(solution)/shard_map/ppermute | solution.py:24
  29.9 6.2 %collective-permute-start.4 = (bf16[32,1,128]{2,1,0:T(2,128)(2,1)S(1)}, bf16[32,1,128]{2,1,0:T(2,128)(2,1)S(1)}, u32[]{:S(2)}, u32[]{:S(2)}) collective-permute-start(bf16[32,1,128]{2,1,0:T(2,128)(2,1)S(1)} %get-tuple-element.72), channel_id=1, source_target_pairs={{0,1},{1,2},{2,3},{3,0},{4,5},{5,6},{6,7},{7,4},{8,9},{9,10},{10,1... | collective-permute-start | bytes 24584 | tf_op jit(solution)/shard_map/ppermute | solution.py:23
  31.3 11.5 %collective-permute-start.15 = (bf16[1,18,128]{2,1,0:T(8,128)(2,1)S(1)}, bf16[1,18,128]{2,1,0:T(8,128)(2,1)S(1)}, u32[]{:S(2)}, u32[]{:S(2)}) collective-permute-start(bf16[1,18,128]{2,1,0:T(8,128)(2,1)S(1)} %get-tuple-element.49), channel_id=1, source_target_pairs={{4,0},{8,4},{12,8},{16,12},{20,16},{24,20},{28,24},{5,1},{9,5},{13... | collective-permute-start | bytes 13832 | tf_op jit(solution)/shard_map/ppermute | solution.py:24
  32.6 10.2 %collective-permute-start.14 = (bf16[1,18,128]{2,1,0:T(8,128)(2,1)S(1)}, bf16[1,18,128]{2,1,0:T(8,128)(2,1)S(1)}, u32[]{:S(2)}, u32[]{:S(2)}) collective-permute-start(bf16[1,18,128]{2,1,0:T(8,128)(2,1)S(1)} %get-tuple-element.48), channel_id=1, source_target_pairs={{0,4},{4,8},{8,12},{12,16},{16,20},{20,24},{24,28},{1,5},{5,9},{9,... | collective-permute-start | bytes 13832 | tf_op jit(solution)/shard_map/ppermute | solution.py:23
  37.2 11.5 %collective-permute-start.7 = (bf16[1,18,128]{2,1,0:T(8,128)(2,1)S(1)}, bf16[1,18,128]{2,1,0:T(8,128)(2,1)S(1)}, u32[]{:S(2)}, u32[]{:S(2)}) collective-permute-start(bf16[1,18,128]{2,1,0:T(8,128)(2,1)S(1)} %get-tuple-element.60), channel_id=1, source_target_pairs={{4,0},{8,4},{12,8},{16,12},{20,16},{24,20},{28,24},{5,1},{9,5},{13... | collective-permute-start | bytes 13832 | tf_op jit(solution)/shard_map/ppermute | solution.py:24
  38.5 10.2 %collective-permute-start.6 = (bf16[1,18,128]{2,1,0:T(8,128)(2,1)S(1)}, bf16[1,18,128]{2,1,0:T(8,128)(2,1)S(1)}, u32[]{:S(2)}, u32[]{:S(2)}) collective-permute-start(bf16[1,18,128]{2,1,0:T(8,128)(2,1)S(1)} %get-tuple-element.61), channel_id=1, source_target_pairs={{0,4},{4,8},{8,12},{12,16},{16,20},{20,24},{24,28},{1,5},{5,9},{9,... | collective-permute-start | bytes 13832 | tf_op jit(solution)/shard_map/ppermute | solution.py:23
  55.7 0.8 copy-start.7
  69.4 1.3 copy-start
  69.5 17.4 %collective-permute-start.24 = (f32[2,83968]{1,0:T(2,128)S(1)}, f32[2,83968]{1,0:T(2,128)}, u32[]{:S(2)}, u32[]{:S(2)}) collective-permute-start(f32[2,83968]{1,0:T(2,128)S(1)} %dynamic-slice_bitcast_fusion), channel_id=1, source_target_pairs={{0,2},{1,3},{2,0},{3,1},{4,6},{5,7},{6,4},{7,5},{8,10},{9,11},{10,... | collective-permute-start | bytes 2015240 | tf_op jit(solution)/shard_map/ppermute | solution.py:149
  73.0 13.9 %copy-start.1 = (f32[2,2,83968]{2,1,0:T(2,128)S(1)}, f32[2,2,83968]{2,1,0:T(2,128)}, u32[]{:S(2)}) copy-start(f32[2,2,83968]{2,1,0:T(2,128)} %copy-done) | copy-start | bytes 4030468
  73.3 17.5 %collective-permute-start.16 = (f32[2,83968]{1,0:T(2,128)S(1)}, f32[2,83968]{1,0:T(2,128)S(1)}, u32[]{:S(2)}, u32[]{:S(2)}) collective-permute-start(f32[2,83968]{1,0:T(2,128)S(1)} %bitcast.127), channel_id=1, source_target_pairs={{0,1},{1,0},{2,3},{3,2},{4,5},{5,4},{6,7},{7,6},{8,9},{9,8},{10,11... | collective-permute-start | bytes 2015240 | tf_op jit(solution)/shard_map/ppermute | solution.py:149
  88.9 10.6 %collective-permute-start.25 = (f32[83968]{0:T(1024)S(1)}, f32[83968]{0:T(1024)S(1)}, u32[]{:S(2)}, u32[]{:S(2)}) collective-permute-start(f32[83968]{0:T(1024)S(1)} %bitcast.130), channel_id=1, source_target_pairs={{0,1},{1,0},{2,3},{3,2},{4,5},{5,4},{6,7},{7,6},{8,9},{9,8},{10,11... | collective-permute-start | bytes 1007624 | tf_op jit(solution)/shard_map/ppermute | solution.py:149
  91.9 10.2 %collective-permute-start.17 = (f32[83968]{0:T(1024)S(1)}, f32[83968]{0:T(1024)S(1)}, u32[]{:S(2)}, u32[]{:S(2)}) collective-permute-start(f32[83968]{0:T(1024)S(1)} %bitcast.131), channel_id=1, source_target_pairs={{0,2},{1,3},{2,0},{3,1},{4,6},{5,7},{6,4},{7,5},{8,10},{9,11},{10,... | collective-permute-start | bytes 1007624 | tf_op jit(solution)/shard_map/ppermute | solution.py:149
  100.1 2.7 %collective-permute-start.26 = (f32[41984]{0:T(1024)S(1)}, f32[41984]{0:T(1024)S(1)}, u32[]{:S(2)}, u32[]{:S(2)}) collective-permute-start(f32[41984]{0:T(1024)S(1)} %bitcast.134), channel_id=1, source_target_pairs={{0,4},{4,0},{8,12},{12,8},{16,20},{20,16},{24,28},{28,24},{1,5},{5... | collective-permute-start | bytes 503816 | tf_op jit(solution)/shard_map/ppermute | solution.py:149
  102.1 3.3 %copy-start.3 = (bf16[4,4,256,128]{3,2,1,0:T(8,128)(2,1)S(1)}, bf16[4,4,256,128]{3,2,1,0:T(8,128)(2,1)}, u32[]{:S(2)}) copy-start(bf16[4,4,256,128]{3,2,1,0:T(8,128)(2,1)} %param.8) | copy-start | bytes 3145732
  102.7 3.3 %collective-permute-start.18 = (f32[41984]{0:T(1024)S(1)}, f32[41984]{0:T(1024)S(1)}, u32[]{:S(2)}, u32[]{:S(2)}) collective-permute-start(f32[41984]{0:T(1024)S(1)} %bitcast.133), channel_id=1, source_target_pairs={{0,4},{4,0},{8,12},{12,8},{16,20},{20,16},{24,28},{28,24},{1,5},{5... | collective-permute-start | bytes 503816 | tf_op jit(solution)/shard_map/ppermute | solution.py:149
  103.6 4.9 %collective-permute-start.27 = (f32[20992]{0:T(1024)S(1)}, f32[20992]{0:T(1024)S(1)}, u32[]{:S(2)}, u32[]{:S(2)}) collective-permute-start(f32[20992]{0:T(1024)S(1)} %get-tuple-element.10), channel_id=1, source_target_pairs={{0,8},{4,12},{8,0},{12,4},{16,24},{20,28},{24,16},{28,20},{1,9},{5... | collective-permute-start | bytes 251912 | tf_op jit(solution)/shard_map/ppermute | solution.py:149
  105.9 6.2 %copy-start.8 = (bf16[16,8,2048]{2,1,0:T(8,128)(2,1)S(1)}, bf16[16,8,2048]{2,1,0:T(8,128)(2,1)}, u32[]{:S(2)}) copy-start(bf16[16,8,2048]{2,1,0:T(8,128)(2,1)} %copy-done.7) | copy-start | bytes 1572868
  106.6 6.5 %collective-permute-start.19 = (f32[20992]{0:T(1024)S(1)}, f32[20992]{0:T(1024)S(1)}, u32[]{:S(2)}, u32[]{:S(2)}) collective-permute-start(f32[20992]{0:T(1024)S(1)} %get-tuple-element.8), channel_id=1, source_target_pairs={{0,8},{4,12},{8,0},{12,4},{16,24},{20,28},{24,16},{28,20},{1,9},{5... | collective-permute-start | bytes 251912 | tf_op jit(solution)/shard_map/ppermute | solution.py:149
  108.9 5.3 %collective-permute-start.28 = (f32[10496]{0:T(1024)S(1)}, f32[10496]{0:T(1024)S(1)}, u32[]{:S(2)}, u32[]{:S(2)}) collective-permute-start(f32[10496]{0:T(1024)S(1)} %get-tuple-element.14), channel_id=1, source_target_pairs={{0,16},{4,20},{8,24},{12,28},{16,0},{20,4},{24,8},{28,12},{1,17},{... | collective-permute-start | bytes 125960 | tf_op jit(solution)/shard_map/ppermute | solution.py:149
  112.2 5.5 %copy-start.6 = (bf16[3,3,128,128]{3,2,1,0:T(8,128)(2,1)S(1)}, bf16[3,3,128,128]{3,2,1,0:T(8,128)(2,1)}, u32[]{:S(2)}) copy-start(bf16[3,3,128,128]{3,2,1,0:T(8,128)(2,1)} %param.10) | copy-start | bytes 884740
  113.5 6.6 %collective-permute-start.20 = (f32[10496]{0:T(1024)S(1)}, f32[10496]{0:T(1024)S(1)}, u32[]{:S(2)}, u32[]{:S(2)}) collective-permute-start(f32[10496]{0:T(1024)S(1)} %get-tuple-element.12), channel_id=1, source_target_pairs={{0,16},{4,20},{8,24},{12,28},{16,0},{20,4},{24,8},{28,12},{1,17},{... | collective-permute-start | bytes 125960 | tf_op jit(solution)/shard_map/ppermute | solution.py:149
  114.2 6.0 %collective-permute-start.29 = (f32[10496]{0:T(1024)S(1)}, f32[10496]{0:T(1024)S(1)}, u32[]{:S(2)}, u32[]{:S(2)}) collective-permute-start(f32[10496]{0:T(1024)S(1)} %add.180), channel_id=1, source_target_pairs={{0,16},{4,20},{8,24},{12,28},{16,0},{20,4},{24,8},{28,12},{1,17},{... | collective-permute-start | bytes 125960 | tf_op jit(solution)/shard_map/ppermute | solution.py:149
  120.1 5.1 %collective-permute-start.21 = (f32[10496]{0:T(1024)S(1)}, f32[10496]{0:T(1024)S(1)}, u32[]{:S(2)}, u32[]{:S(2)}) collective-permute-start(f32[10496]{0:T(1024)S(1)} %add.175), channel_id=1, source_target_pairs={{0,16},{4,20},{8,24},{12,28},{16,0},{20,4},{24,8},{28,12},{1,17},{... | collective-permute-start | bytes 125960 | tf_op jit(solution)/shard_map/ppermute | solution.py:149
  120.2 5.4 %collective-permute-start.30 = (f32[20992]{0:T(1024)S(1)}, f32[20992]{0:T(1024)S(1)}, u32[]{:S(2)}, u32[]{:S(2)}) collective-permute-start(f32[20992]{0:T(1024)S(1)} %pad_maximum_fusion.14), channel_id=1, source_target_pairs={{0,8},{4,12},{8,0},{12,4},{16,24},{20,28},{24,16},{28,20},{1,9},{5... | collective-permute-start | bytes 251912 | tf_op jit(solution)/shard_map/ppermute | solution.py:149
  125.3 4.6 %collective-permute-start.22 = (f32[20992]{0:T(1024)S(1)}, f32[20992]{0:T(1024)S(1)}, u32[]{:S(2)}, u32[]{:S(2)}) collective-permute-start(f32[20992]{0:T(1024)S(1)} %pad_maximum_fusion.13), channel_id=1, source_target_pairs={{0,8},{4,12},{8,0},{12,4},{16,24},{20,28},{24,16},{28,20},{1,9},{5... | collective-permute-start | bytes 251912 | tf_op jit(solution)/shard_map/ppermute | solution.py:149
  125.7 4.2 %collective-permute-start.31 = (f32[41984]{0:T(1024)S(1)}, f32[41984]{0:T(1024)S(1)}, u32[]{:S(2)}, u32[]{:S(2)}) collective-permute-start(f32[41984]{0:T(1024)S(1)} %pad_maximum_fusion.7), channel_id=1, source_target_pairs={{0,4},{4,0},{8,12},{12,8},{16,20},{20,16},{24,28},{28,24},{1,5},{5... | collective-permute-start | bytes 503816 | tf_op jit(solution)/shard_map/ppermute | solution.py:149
  129.9 1.5 %collective-permute-start.23 = (f32[41984]{0:T(1024)S(1)}, f32[41984]{0:T(1024)S(1)}, u32[]{:S(2)}, u32[]{:S(2)}) collective-permute-start(f32[41984]{0:T(1024)S(1)} %pad_maximum_fusion.6), channel_id=1, source_target_pairs={{0,4},{4,0},{8,12},{12,8},{16,20},{20,16},{24,28},{28,24},{1,5},{5... | collective-permute-start | bytes 503816 | tf_op jit(solution)/shard_map/ppermute | solution.py:149

commit v2 on v1

--- a/solution.py
+++ b/solution.py
@@ -13,17 +13,30 @@
 row_taps = (((1, 0), (3, -1)), ((0, 1), (2, 0)))
 
 
-def padded_2(array, sides, width, wrap):
-    for axis, dim in sides:
-        size, length = (lax.axis_size(axis), array.shape[dim])
-        up = [(i, (i + 1) % size) for i in range(size if wrap else size - 1)]
-        down = [(j, i) for i, j in up]
-        last = lax.slice_in_dim(array, length - width, length, axis=dim)
-        leading = lax.slice_in_dim(array, 0, width, axis=dim)
-        before = lax.ppermute(last, axis, up)
-        after = lax.ppermute(leading, axis, down)
-        array = jnp.concatenate([before, array, after], axis=dim)
-    return array
+def swap_edges(fields, margins, axis, dim, wrap):
+    size = lax.axis_size(axis)
+    up = [(i, (i + 1) % size) for i in range(size if wrap else size - 1)]
+    down = [(j, i) for i, j in up]
+    lasts, leads = [], []
+    for field, width in zip(fields, margins):
+        length = field.shape[dim]
+        lasts.append(lax.slice_in_dim(field, length - width, length, axis=dim))
+        leads.append(lax.slice_in_dim(field, 0, width, axis=dim))
+    before = lax.ppermute(jnp.concatenate([p.reshape(-1) for p in lasts]), axis, up)
+    after = lax.ppermute(jnp.concatenate([p.reshape(-1) for p in leads]), axis, down)
+    joined, at = [], 0
+    for field, last, lead in zip(fields, lasts, leads):
+        count = last.size
+        head = before[at : at + count].reshape(last.shape)
+        tail = after[at : at + count].reshape(lead.shape)
+        joined.append(jnp.concatenate([head, field, tail], axis=dim))
+        at += count
+    return joined
+
+
+def extend_all(fields, margins):
+    widened = swap_edges(fields, margins, "lon", 1, True)
+    return swap_edges(widened, margins, "lat", 0, False)
 
 
 def decode(elem_codes, block_exps):
@@ -38,11 +51,6 @@
     return (signed * factor).astype(jnp.bfloat16)
 
 
-def extend(field, margin):
-    widened = padded_2(field, (("lon", 1),), margin, True)
-    return padded_2(widened, (("lat", 0),), margin, False)
-
-
 def slope(pre_act):
     plain = pre_act.astype(jnp.float32)
     sigmoid_v = jax.nn.sigmoid(plain)
@@ -51,18 +59,17 @@
 
 def upsample(padded, up_kernel, row_count, col_count):
     halves = []
-    for row_par in range(2):
+    for row_par in (1, 0):
         lane_list = []
-        for col_par in range(2):
+        for col_par in (1, 0):
             pieces = []
             kernels = []
             for row_tap, row_off in row_taps[row_par]:
                 for col_tap, col_off in row_taps[col_par]:
+                    row_at = 1 + row_off - row_par
+                    col_at = 1 + col_off - col_par
                     pieces.append(
-                        padded[
-                            1 + row_off : 1 + row_off + row_count,
-                            1 + col_off : 1 + col_off + col_count,
-                        ]
+                        padded[row_at : row_at + row_count + 1, col_at : col_at + col_count + 1]
                     )
                     kernels.append(up_kernel[row_tap, col_tap])
             stacked = jnp.concatenate(pieces, axis=2)
@@ -72,7 +79,7 @@
             )
         halves.append(jnp.stack(lane_list, axis=2))
     merged = jnp.stack(halves, axis=1)
-    return merged.reshape(2 * row_count, 2 * col_count, merged.shape[-1])
+    return merged.reshape(2 * row_count + 2, 2 * col_count + 2, merged.shape[-1])
 
 
 def neighbours(padded, row_count, col_count, flipped):
@@ -102,18 +109,21 @@
     lat_count = lax.axis_size("lat")
     lon_count = lax.axis_size("lon")
     back_mix = mix_kernel.transpose(0, 1, 3, 2).reshape(9 * COUT, COUT)
-    padded_in = extend(inputs, 1)
+    padded_in, grad_pad = extend_all((inputs, cotangent), (1, 2))
     raw = upsample(padded_in, up_kernel, in_rows, in_cols)
     pre_act = (raw + up_bias).astype(jnp.bfloat16)
-    act_pad = extend(jax.nn.silu(pre_act.astype(jnp.float32)).astype(jnp.bfloat16), 1)
-    grad_pad = extend(cotangent, 1)
+    row_at = lax.axis_index("lat") * out_rows - 1 + lax.broadcasted_iota(jnp.int32, (out_rows + 2, 1, 1), 0)
+    inside = (row_at >= 0) & (row_at < out_rows * lat_count)
+    activated = jax.nn.silu(pre_act.astype(jnp.float32)).astype(jnp.bfloat16)
+    act_pad = jnp.where(inside, activated, jnp.zeros_like(activated))
     act_grad = jnp.einsum(
         "rck,kn->rcn",
-        neighbours(grad_pad, out_rows, out_cols, True),
+        neighbours(grad_pad, out_rows + 2, out_cols + 2, True),
         back_mix,
         preferred_element_type=jnp.float32,
     )
-    pre_grad_pad = extend((act_grad * slope(pre_act)).astype(jnp.bfloat16), 1)
+    pre_grad = (act_grad * slope(pre_act)).astype(jnp.bfloat16)
+    pre_grad_pad = jnp.where(inside, pre_grad, jnp.zeros_like(pre_grad))
     patches = neighbours(act_pad, out_rows, out_cols, False)
     mix_flat = mix_kernel.reshape(9 * COUT, COUT)
     section_out = jnp.einsum(

time: 134 us -> 105 us (0.78)
  starting transfers between devices: 45.7 us -> 22.9 us
  waiting for transfers between devices: 38.2 us -> 35.9 us
  other arithmetic: 9.19 us -> 7.66 us
    ppermute x16 -> x4, starting transfers between devices: 29.6 us -> 8.35 us  [the longest x2 6.02 us: swap_edges(): lax.ppermute(jnp.concatenate([p.reshape(-1) for p in lasts]), axis, up)]
    ppermute x16 -> x4, waiting for transfers between devices: 5.75 us -> 2.37 us  [the longest x2 1.31 us: swap_edges(): lax.ppermute(jnp.concatenate([p.reshape(-1) for p in lasts]), axis, up)]
    unnamed x53 -> x66, local copies, waits for them, and re-layouts: 7.76 us -> 5.5 us
    unnamed x5, other arithmetic: 2.38 us -> 0.32 us
    ppermute x16, starting transfers between devices: 16.2 us -> 14.5 us  [exchange(): return lax.ppermute(part, axis, [(i, i ^ step) for i in range(size)])]
  transfers between devices with their start and end apart: 32 -> 20, of which waited for: 14 -> 13; matrix products, arithmetic and copies ran while one was open for 16% -> 13% of each run, Pallas kernels for 0% -> 0%
where the time goes in v2:
time: 105 us; the launch traced here: 104 us
  waiting for transfers between devices  35.9 us (34%)
  local copies, waits for them, and re-layouts  29 us (28%)
  starting transfers between devices  22.9 us (22%)
  other arithmetic  7.66 us (7%)
  matrix products  7.22 us (7%)
  between operations  1.84 us (2%)
    ppermute x16, waiting for transfers between devices, exchange(): return lax.ppermute(part, axis, [(i, i ^ step) for i in range(size)])  33.5 us
    ppermute x16, starting transfers between devices, exchange(): return lax.ppermute(part, axis, [(i, i ^ step) for i in range(size)])  14.5 us
    slice x16, local copies, waits for them, and re-layouts, strided(): padded[row_tap:row_tap + 2 * row_count:2, col_tap:col_tap + 2 * col_count:2]  7.14 us
    ppermute x2, starting transfers between devices, swap_edges(): lax.ppermute(jnp.concatenate([p.reshape(-1) for p in lasts]), axis, up)  6.02 us
    unnamed x66, local copies, waits for them, and re-layouts  5.5 us
    reshape x2, local copies, waits for them, and re-layouts, scatter_lon(): grid = rows.reshape((2,) * width + rows.shape[1:])  3.4 us
    dynamic_slice x8, local copies, waits for them, and re-layouts, halve(): send = lax.dynamic_index_in_dim(buffer, 1 - own, dim, keepdims=False)  3.39 us
    reshape x1, local copies, waits for them, and re-layouts, shards(): up_flat.reshape(lon_count, up_size)  3.12 us
  transfers between devices with their start and end apart: 20, of which 13 were waited for; matrix products, arithmetic and copies ran while one was open for 13% of the time, Pallas kernels for 0%

profile of v2, /device:TPU:0, one launch (start us, length us, event | category | flops | bytes accessed | tf_op | source)
XLA Modules:
  0.0 104.4 jit_solution(11569890004929608185)
XLA Ops:
  0.7 1.0 fusion.69
  1.7 0.8 multiply_exponential_fusion
  3.3 3.0 %collective-permute-start = (bf16[12288]{0:T(1024)(128)(2,1)S(1)}, bf16[12288]{0:T(1024)(128)(2,1)S(1)}, u32[]{:S(2)}, u32[]{:S(2)}) collective-permute-start(bf16[12288]{0:T(1024)(128)(2,1)S(1)} %pad_maximum_fusion.11), channel_id=1, source_target_pairs={{0,1},{1,2},{2,3},{3,0},{4,5},{5,6},{6,7},{7,4},{8,9},{9,10},{10,1... | collective-permute-start | bytes 73736 | tf_op jit(solution)/shard_map/ppermute | solution.py:25
  6.3 1.0 collective-permute-start.1
  7.3 0.7 slice_bitcast_fusion.15
  8.3 0.7 collective-permute-done
  9.1 1.1 %collective-permute-done.1 = bf16[12288]{0:T(1024)(128)(2,1)S(1)} collective-permute-done((bf16[12288]{0:T(1024)(128)(2,1)S(1)}, bf16[12288]{0:T(1024)(128)(2,1)S(1)}, u32[]{:S(2)}, u32[]{:S(2)}) %collective-permute-start.1) | collective-permute-done | bytes 24608 | tf_op jit(solution)/shard_map/ppermute | solution.py:26
  10.4 1.3 %collective-permute-start.2 = (bf16[7680]{0:T(1024)(128)(2,1)S(1)}, bf16[7680]{0:T(1024)(128)(2,1)S(1)}, u32[]{:S(2)}, u32[]{:S(2)}) collective-permute-start(bf16[7680]{0:T(1024)(128)(2,1)S(1)} %pad_maximum_fusion.13), channel_id=1, source_target_pairs={{4,0},{8,4},{12,8},{16,12},{20,16},{24,20},{28,24},{5,1},{9,5},{13... | collective-permute-start | bytes 46088 | tf_op jit(solution)/shard_map/ppermute | solution.py:26
  11.7 3.0 %collective-permute-start.3 = (bf16[7680]{0:T(1024)(128)(2,1)S(1)}, bf16[7680]{0:T(1024)(128)(2,1)S(1)}, u32[]{:S(2)}, u32[]{:S(2)}) collective-permute-start(bf16[7680]{0:T(1024)(128)(2,1)S(1)} %pad_maximum_fusion.14), channel_id=1, source_target_pairs={{0,4},{4,8},{8,12},{12,16},{16,20},{20,24},{24,28},{1,5},{5,9},{9,... | collective-permute-start | bytes 46088 | tf_op jit(solution)/shard_map/ppermute | solution.py:25
  15.0 0.6 collective-permute-done.3
  16.4 1.2 %convolution_bitcast_fusion.2 = f32[17,9,1,128]{3,0,1,2:T(8,128)S(1)} fusion(bf16[256,128]{1,0:T(8,128)(2,1)} %get-tuple-element.37, bf16[256,128]{1,0:T(8,128)(2,1)S(1)} %get-tuple-element.23, bf16[256,128]{1,0:T(8,128)(2,1)} %get-tuple-element.24, bf16[256,128]{1,0:T(8,128)(2,1)} %get-tuple-element.25, bf16[17,9,256]{2,0,1:T(8,128)(2,1)S(1)} %get-tuple-element.72, ...), kind=kOutput, calls=%fused_computation.6 | convolution fusion | flops 42409984 | bytes 653824 | tf_op jit(solution)/shard_map/rck,kn->rcn/dot_general | solution.py:78
  19.0 0.7 fusion.72
  25.5 0.7 slice.404
  26.3 0.9 slice.405
  27.7 1.0 copy-done.4
  29.0 0.8 copy-done.9
  29.8 1.9 %convolution_bitcast_fusion = f32[256,2048]{1,0:T(8,128)} fusion(bf16[16,8,256]{2,0,1:T(8,128)(2,1)S(1)} %fusion.59, bf16[16,8,2048]{2,1,0:T(8,128)(2,1)S(1)} %constant_dynamic-update-slice_fusion.2), kind=kOutput, calls=%fused_computation | convolution fusion | flops 134217728 | bytes 2686976 | tf_op jit(solution)/shard_map/rcm,rck->mk/dot_general | solution.py:144
  31.7 3.1 %reshape.186 = f32[4,131072]{1,0:T(4,128)S(1)} reshape(f32[256,2048]{1,0:T(8,128)} %convolution_bitcast_fusion) | data formatting | bytes 4194304 | tf_op jit(solution)/shard_map/reshape | solution.py:149
  35.7 1.1 %reshape.192 = f32[4,36864]{1,0:T(4,128)} reshape(f32[128,9,128]{2,1,0:T(8,128)S(1)} %copy.44) | data formatting | bytes 1179648 | tf_op jit(solution)/shard_map/reshape | solution.py:149
  36.8 2.5 %fusion.67 = (f32[4,83968]{1,0:T(4,128)S(1)}, f32[4,83968]{1,0:T(4,128)}) fusion(f32[4,131072]{1,0:T(4,128)S(1)} %reshape.186, f32[4,36864]{1,0:T(4,128)} %reshape.192), kind=kLoop, calls=%fused_computation.211 | loop fusion | flops 335872 | bytes 6717440 | tf_op jit(solution)/shard_map/slice | solution.py:214
  39.3 2.4 %reshape.193 = f32[2,2,83968]{2,1,0:T(2,128)S(1)} reshape(f32[4,83968]{1,0:T(4,128)} %get-tuple-element.19) | data formatting | bytes 2686976 | tf_op jit(solution)/shard_map/reshape | solution.py:186
  41.8 1.6 %collective-permute-start.12 = (f32[2,83968]{1,0:T(2,128)S(1)}, f32[2,83968]{1,0:T(2,128)}, u32[]{:S(2)}, u32[]{:S(2)}) collective-permute-start(f32[2,83968]{1,0:T(2,128)S(1)} %dynamic-slice_bitcast_fusion), channel_id=1, source_target_pairs={{0,2},{1,3},{2,0},{3,1},{4,6},{5,7},{6,4},{7,5},{8,10},{9,11},{10,... | collective-permute-start | bytes 2015240 | tf_op jit(solution)/shard_map/ppermute | solution.py:159
  43.4 1.0 reshape.187
  44.4 1.2 %constant_dynamic-slice_fusion.9 = (f32[2,1,83968]{2,1,0:T(1,128)S(1)}, f32[2,1,83968]{2,1,0:T(1,128)S(1)}) fusion(f32[2,2,83968]{2,1,0:T(2,128)S(1)} %reshape.187, s32[]{:T(128)S(6)} %select_n.219, s32[]{:T(128)S(6)} %select_n.220), kind=kLoop, calls=%fused_computation.205 | loop fusion | bytes 2686984 | tf_op jit(solution)/shard_map/jit(dynamic_index_in_dim)/dynamic_slice | solution.py:164
  45.9 1.9 %collective-permute-start.4 = (f32[2,83968]{1,0:T(2,128)S(1)}, f32[2,83968]{1,0:T(2,128)S(1)}, u32[]{:S(2)}, u32[]{:S(2)}) collective-permute-start(f32[2,83968]{1,0:T(2,128)S(1)} %bitcast.137), channel_id=1, source_target_pairs={{0,1},{1,0},{2,3},{3,2},{4,5},{5,4},{6,7},{7,6},{8,9},{9,8},{10,11... | collective-permute-start | bytes 2015240 | tf_op jit(solution)/shard_map/ppermute | solution.py:159
  47.8 11.8 %collective-permute-done.12 = f32[2,83968]{1,0:T(2,128)} collective-permute-done((f32[2,83968]{1,0:T(2,128)S(1)}, f32[2,83968]{1,0:T(2,128)}, u32[]{:S(2)}, u32[]{:S(2)}) %collective-permute-start.12) | collective-permute-done | bytes 671776 | tf_op jit(solution)/shard_map/ppermute | solution.py:159
  59.7 1.4 %bitcast_add_fusion.1 = f32[2,83968]{1,0:T(2,128)S(1)} fusion(f32[2,83968]{1,0:T(2,128)} %collective-permute-done.12, f32[2,2,83968]{2,1,0:T(2,128)S(1)} %copy-done.1, s32[]{:T(128)S(6)} %select_n.223), kind=kLoop, calls=%fused_computation.13 | loop fusion | flops 167936 | bytes 2015236 | tf_op jit(solution)/shard_map/add | solution.py:166
  61.7 2.5 %collective-permute-start.13 = (f32[83968]{0:T(1024)S(1)}, f32[83968]{0:T(1024)S(1)}, u32[]{:S(2)}, u32[]{:S(2)}) collective-permute-start(f32[83968]{0:T(1024)S(1)} %bitcast.140), channel_id=1, source_target_pairs={{0,1},{1,0},{2,3},{3,2},{4,5},{5,4},{6,7},{7,6},{8,9},{9,8},{10,11... | collective-permute-start | bytes 1007624 | tf_op jit(solution)/shard_map/ppermute | solution.py:159
  65.8 6.7 %collective-permute-done.13 = f32[83968]{0:T(1024)S(1)} collective-permute-done((f32[83968]{0:T(1024)S(1)}, f32[83968]{0:T(1024)S(1)}, u32[]{:S(2)}, u32[]{:S(2)}) %collective-permute-start.13) | collective-permute-done | bytes 335904 | tf_op jit(solution)/shard_map/ppermute | solution.py:159
  73.1 1.9 %collective-permute-done.5 = f32[83968]{0:T(1024)S(1)} collective-permute-done((f32[83968]{0:T(1024)S(1)}, f32[83968]{0:T(1024)S(1)}, u32[]{:S(2)}, u32[]{:S(2)}) %collective-permute-start.5) | collective-permute-done | bytes 335904 | tf_op jit(solution)/shard_map/ppermute | solution.py:159
  75.9 0.7 dynamic-slice_reduce_fusion
  78.2 1.8 %collective-permute-start.7 = (f32[20992]{0:T(1024)S(1)}, f32[20992]{0:T(1024)}, u32[]{:S(2)}, u32[]{:S(2)}) collective-permute-start(f32[20992]{0:T(1024)S(1)} %get-tuple-element.8), channel_id=1, source_target_pairs={{0,8},{4,12},{8,0},{12,4},{16,24},{20,28},{24,16},{28,20},{1,9},{5... | collective-permute-start | bytes 251912 | tf_op jit(solution)/shard_map/ppermute | solution.py:159
  79.9 2.0 %collective-permute-done.15 = f32[20992]{0:T(1024)S(1)} collective-permute-done((f32[20992]{0:T(1024)S(1)}, f32[20992]{0:T(1024)S(1)}, u32[]{:S(2)}, u32[]{:S(2)}) %collective-permute-start.15) | collective-permute-done | bytes 84000 | tf_op jit(solution)/shard_map/ppermute | solution.py:159
  82.3 1.1 %collective-permute-start.16 = (f32[10496]{0:T(1024)S(1)}, f32[10496]{0:T(1024)S(1)}, u32[]{:S(2)}, u32[]{:S(2)}) collective-permute-start(f32[10496]{0:T(1024)S(1)} %get-tuple-element.14), channel_id=1, source_target_pairs={{0,16},{4,20},{8,24},{12,28},{16,0},{20,4},{24,8},{28,12},{1,17},{... | collective-permute-start | bytes 125960 | tf_op jit(solution)/shard_map/ppermute | solution.py:159
  83.4 1.0 fusion.73
  84.4 0.9 add.186
  85.6 2.0 %collective-permute-start.8 = (f32[10496]{0:T(1024)S(1)}, f32[10496]{0:T(1024)S(1)}, u32[]{:S(2)}, u32[]{:S(2)}) collective-permute-start(f32[10496]{0:T(1024)S(1)} %get-tuple-element.12), channel_id=1, source_target_pairs={{0,16},{4,20},{8,24},{12,28},{16,0},{20,4},{24,8},{28,12},{1,17},{... | collective-permute-start | bytes 125960 | tf_op jit(solution)/shard_map/ppermute | solution.py:159
  87.6 1.1 %collective-permute-start.17 = (f32[10496]{0:T(1024)S(1)}, f32[10496]{0:T(1024)S(1)}, u32[]{:S(2)}, u32[]{:S(2)}) collective-permute-start(f32[10496]{0:T(1024)S(1)} %add.194), channel_id=1, source_target_pairs={{0,16},{4,20},{8,24},{12,28},{16,0},{20,4},{24,8},{28,12},{1,17},{... | collective-permute-start | bytes 125960 | tf_op jit(solution)/shard_map/ppermute | solution.py:159
  88.7 1.1 %convolution_convert_fusion = bf16[32,16,128]{2,1,0:T(8,128)(2,1)} fusion(bf16[32,16,1152]{2,1,0:T(8,128)(2,1)S(1)} %copy-done.6, bf16[1152,128,1]{1,0,2:T(8,128)(2,1)S(1)} %bitcast.135), kind=kOutput, calls=%fused_computation.5 | convolution fusion | flops 151060480 | bytes 1605632 | tf_op jit(solution)/shard_map/rck,kn->rcn/dot_general | solution.py:129
  89.8 1.7 %collective-permute-done.8 = f32[10496]{0:T(1024)S(1)} collective-permute-done((f32[10496]{0:T(1024)S(1)}, f32[10496]{0:T(1024)S(1)}, u32[]{:S(2)}, u32[]{:S(2)}) %collective-permute-start.8) | collective-permute-done | bytes 42016 | tf_op jit(solution)/shard_map/ppermute | solution.py:159
  91.5 1.1 %collective-permute-start.9 = (f32[10496]{0:T(1024)S(1)}, f32[10496]{0:T(1024)S(1)}, u32[]{:S(2)}, u32[]{:S(2)}) collective-permute-start(f32[10496]{0:T(1024)S(1)} %add.189), channel_id=1, source_target_pairs={{0,16},{4,20},{8,24},{12,28},{16,0},{20,4},{24,8},{28,12},{1,17},{... | collective-permute-start | bytes 125960 | tf_op jit(solution)/shard_map/ppermute | solution.py:159
  92.6 0.6 collective-permute-done.17
  93.5 3.0 %collective-permute-done.9 = f32[10496]{0:T(1024)S(1)} collective-permute-done((f32[10496]{0:T(1024)S(1)}, f32[10496]{0:T(1024)S(1)}, u32[]{:S(2)}, u32[]{:S(2)}) %collective-permute-start.9) | collective-permute-done | bytes 42016 | tf_op jit(solution)/shard_map/ppermute | solution.py:159
  96.6 1.7 %collective-permute-done.18 = f32[20992]{0:T(1024)S(1)} collective-permute-done((f32[20992]{0:T(1024)S(1)}, f32[20992]{0:T(1024)S(1)}, u32[]{:S(2)}, u32[]{:S(2)}) %collective-permute-start.18) | collective-permute-done | bytes 84000 | tf_op jit(solution)/shard_map/ppermute | solution.py:159
  98.4 2.7 %collective-permute-done.10 = f32[20992]{0:T(1024)S(1)} collective-permute-done((f32[20992]{0:T(1024)S(1)}, f32[20992]{0:T(1024)S(1)}, u32[]{:S(2)}, u32[]{:S(2)}) %collective-permute-start.10) | collective-permute-done | bytes 84000 | tf_op jit(solution)/shard_map/ppermute | solution.py:159
  101.3 1.3 %collective-permute-done.11 = f32[41984]{0:T(1024)S(1)} collective-permute-done((f32[41984]{0:T(1024)S(1)}, f32[41984]{0:T(1024)S(1)}, u32[]{:S(2)}, u32[]{:S(2)}) %collective-permute-start.11) | collective-permute-done | bytes 167968 | tf_op jit(solution)/shard_map/ppermute | solution.py:159
  102.8 1.0 copy.45
  103.8 0.7 copy.46
  (183 shorter events, 17.7 us)
Async XLA Ops:
  0.6 2.3 %copy-start.13 = (s32[16,8,256]{2,1,0:T(8,128)S(1)}, s32[16,8,256]{2,1,0:T(8,128)}, u32[]{:S(2)}) copy-start(s32[16,8,256]{2,1,0:T(8,128)} %param.6) | copy-start | bytes 393220
  0.6 6.7 %copy-start.2 = (bf16[4,4,256,128]{3,2,1,0:T(8,128)(2,1)S(1)}, bf16[4,4,256,128]{3,2,1,0:T(8,128)(2,1)}, u32[]{:S(2)}) copy-start(bf16[4,4,256,128]{3,2,1,0:T(8,128)(2,1)} %param.8) | copy-start | bytes 3145732
  2.9 5.1 %copy-start.7 = (bf16[3,3,128,128]{3,2,1,0:T(8,128)(2,1)S(1)}, bf16[3,3,128,128]{3,2,1,0:T(8,128)(2,1)}, u32[]{:S(2)}) copy-start(bf16[3,3,128,128]{3,2,1,0:T(8,128)(2,1)} %param.10) | copy-start | bytes 884740
  3.3 5.8 %collective-permute-start = (bf16[12288]{0:T(1024)(128)(2,1)S(1)}, bf16[12288]{0:T(1024)(128)(2,1)S(1)}, u32[]{:S(2)}, u32[]{:S(2)}) collective-permute-start(bf16[12288]{0:T(1024)(128)(2,1)S(1)} %pad_maximum_fusion.11), channel_id=1, source_target_pairs={{0,1},{1,2},{2,3},{3,0},{4,5},{5,6},{6,7},{7,4},{8,9},{9,10},{10,1... | collective-permute-start | bytes 73736 | tf_op jit(solution)/shard_map/ppermute | solution.py:25
  6.3 3.9 %collective-permute-start.1 = (bf16[12288]{0:T(1024)(128)(2,1)S(1)}, bf16[12288]{0:T(1024)(128)(2,1)S(1)}, u32[]{:S(2)}, u32[]{:S(2)}) collective-permute-start(bf16[12288]{0:T(1024)(128)(2,1)S(1)} %pad_maximum_fusion.12), channel_id=1, source_target_pairs={{1,0},{2,1},{3,2},{0,3},{5,4},{6,5},{7,6},{4,7},{9,8},{10,9},{11,1... | collective-permute-start | bytes 73736 | tf_op jit(solution)/shard_map/ppermute | solution.py:26
  7.3 1.7 %copy-start.11 = (bf16[32,16,128]{2,1,0:T(8,128)(2,1)S(1)}, bf16[32,16,128]{2,1,0:T(8,128)(2,1)}, u32[]{:S(2)}) copy-start(bf16[32,16,128]{2,1,0:T(8,128)(2,1)} %param.11) | copy-start | bytes 393220
  10.4 4.4 %collective-permute-start.2 = (bf16[7680]{0:T(1024)(128)(2,1)S(1)}, bf16[7680]{0:T(1024)(128)(2,1)S(1)}, u32[]{:S(2)}, u32[]{:S(2)}) collective-permute-start(bf16[7680]{0:T(1024)(128)(2,1)S(1)} %pad_maximum_fusion.13), channel_id=1, source_target_pairs={{4,0},{8,4},{12,8},{16,12},{20,16},{24,20},{28,24},{5,1},{9,5},{13... | collective-permute-start | bytes 46088 | tf_op jit(solution)/shard_map/ppermute | solution.py:26
  11.7 3.9 %collective-permute-start.3 = (bf16[7680]{0:T(1024)(128)(2,1)S(1)}, bf16[7680]{0:T(1024)(128)(2,1)S(1)}, u32[]{:S(2)}, u32[]{:S(2)}) collective-permute-start(bf16[7680]{0:T(1024)(128)(2,1)S(1)} %pad_maximum_fusion.14), channel_id=1, source_target_pairs={{0,4},{4,8},{8,12},{12,16},{16,20},{20,24},{24,28},{1,5},{5,9},{9,... | collective-permute-start | bytes 46088 | tf_op jit(solution)/shard_map/ppermute | solution.py:25
  19.0 0.7 copy-start.14
  27.7 1.0 copy-start.4
  29.0 0.8 copy-start.9
  31.7 3.1 %copy-start.5 = (bf16[32,16,1152]{2,1,0:T(8,128)(2,1)S(1)}, bf16[32,16,1152]{2,1,0:T(8,128)(2,1)}, u32[]{:S(2)}) copy-start(bf16[32,16,1152]{2,1,0:T(8,128)(2,1)} %copy-done.4) | copy-start | bytes 3538948
  31.7 3.1 %copy-start.12 = (bf16[32,16,128]{2,1,0:T(8,128)(2,1)S(1)}, bf16[32,16,128]{2,1,0:T(8,128)(2,1)}, u32[]{:S(2)}) copy-start(bf16[32,16,128]{2,1,0:T(8,128)(2,1)} %param.11) | copy-start | bytes 393220
  41.7 1.6 %copy-start = (f32[2,2,83968]{2,1,0:T(2,128)}, f32[2,2,83968]{2,1,0:T(2,128)S(1)}, u32[]{:S(2)}) copy-start(f32[2,2,83968]{2,1,0:T(2,128)S(1)} %reshape.193) | copy-start | bytes 4030468
  41.8 17.9 %collective-permute-start.12 = (f32[2,83968]{1,0:T(2,128)S(1)}, f32[2,83968]{1,0:T(2,128)}, u32[]{:S(2)}, u32[]{:S(2)}) collective-permute-start(f32[2,83968]{1,0:T(2,128)S(1)} %dynamic-slice_bitcast_fusion), channel_id=1, source_target_pairs={{0,2},{1,3},{2,0},{3,1},{4,6},{5,7},{6,4},{7,5},{8,10},{9,11},{10,... | collective-permute-start | bytes 2015240 | tf_op jit(solution)/shard_map/ppermute | solution.py:159
  45.6 14.1 %copy-start.1 = (f32[2,2,83968]{2,1,0:T(2,128)S(1)}, f32[2,2,83968]{2,1,0:T(2,128)}, u32[]{:S(2)}) copy-start(f32[2,2,83968]{2,1,0:T(2,128)} %copy-done) | copy-start | bytes 4030468
  45.9 18.2 %collective-permute-start.4 = (f32[2,83968]{1,0:T(2,128)S(1)}, f32[2,83968]{1,0:T(2,128)S(1)}, u32[]{:S(2)}, u32[]{:S(2)}) collective-permute-start(f32[2,83968]{1,0:T(2,128)S(1)} %bitcast.137), channel_id=1, source_target_pairs={{0,1},{1,0},{2,3},{3,2},{4,5},{5,4},{6,7},{7,6},{8,9},{9,8},{10,11... | collective-permute-start | bytes 2015240 | tf_op jit(solution)/shard_map/ppermute | solution.py:159
  61.7 10.8 %collective-permute-start.13 = (f32[83968]{0:T(1024)S(1)}, f32[83968]{0:T(1024)S(1)}, u32[]{:S(2)}, u32[]{:S(2)}) collective-permute-start(f32[83968]{0:T(1024)S(1)} %bitcast.140), channel_id=1, source_target_pairs={{0,1},{1,0},{2,3},{3,2},{4,5},{5,4},{6,7},{7,6},{8,9},{9,8},{10,11... | collective-permute-start | bytes 1007624 | tf_op jit(solution)/shard_map/ppermute | solution.py:159
  65.2 9.8 %collective-permute-start.5 = (f32[83968]{0:T(1024)S(1)}, f32[83968]{0:T(1024)S(1)}, u32[]{:S(2)}, u32[]{:S(2)}) collective-permute-start(f32[83968]{0:T(1024)S(1)} %bitcast.141), channel_id=1, source_target_pairs={{0,2},{1,3},{2,0},{3,1},{4,6},{5,7},{6,4},{7,5},{8,10},{9,11},{10,... | collective-permute-start | bytes 1007624 | tf_op jit(solution)/shard_map/ppermute | solution.py:159
  73.0 2.7 %collective-permute-start.14 = (f32[41984]{0:T(1024)S(1)}, f32[41984]{0:T(1024)S(1)}, u32[]{:S(2)}, u32[]{:S(2)}) collective-permute-start(f32[41984]{0:T(1024)S(1)} %bitcast.143), channel_id=1, source_target_pairs={{0,4},{4,0},{8,12},{12,8},{16,20},{20,16},{24,28},{28,24},{1,5},{5... | collective-permute-start | bytes 503816 | tf_op jit(solution)/shard_map/ppermute | solution.py:159
  75.1 1.9 %copy-start.3 = (bf16[4,4,256,128]{3,2,1,0:T(8,128)(2,1)S(1)}, bf16[4,4,256,128]{3,2,1,0:T(8,128)(2,1)}, u32[]{:S(2)}) copy-start(bf16[4,4,256,128]{3,2,1,0:T(8,128)(2,1)} %param.8) | copy-start | bytes 3145732
  75.6 1.9 %collective-permute-start.6 = (f32[41984]{0:T(1024)S(1)}, f32[41984]{0:T(1024)S(1)}, u32[]{:S(2)}, u32[]{:S(2)}) collective-permute-start(f32[41984]{0:T(1024)S(1)} %bitcast.142), channel_id=1, source_target_pairs={{0,4},{4,0},{8,12},{12,8},{16,20},{20,16},{24,28},{28,24},{1,5},{5... | collective-permute-start | bytes 503816 | tf_op jit(solution)/shard_map/ppermute | solution.py:159
  76.6 5.4 %collective-permute-start.15 = (f32[20992]{0:T(1024)S(1)}, f32[20992]{0:T(1024)S(1)}, u32[]{:S(2)}, u32[]{:S(2)}) collective-permute-start(f32[20992]{0:T(1024)S(1)} %get-tuple-element.10), channel_id=1, source_target_pairs={{0,8},{4,12},{8,0},{12,4},{16,24},{20,28},{24,16},{28,20},{1,9},{5... | collective-permute-start | bytes 251912 | tf_op jit(solution)/shard_map/ppermute | solution.py:159
  77.5 5.9 %copy-start.10 = (bf16[16,8,2048]{2,1,0:T(8,128)(2,1)S(1)}, bf16[16,8,2048]{2,1,0:T(8,128)(2,1)}, u32[]{:S(2)}) copy-start(bf16[16,8,2048]{2,1,0:T(8,128)(2,1)} %copy-done.9) | copy-start | bytes 1572868
  78.2 6.2 %collective-permute-start.7 = (f32[20992]{0:T(1024)S(1)}, f32[20992]{0:T(1024)}, u32[]{:S(2)}, u32[]{:S(2)}) collective-permute-start(f32[20992]{0:T(1024)S(1)} %get-tuple-element.8), channel_id=1, source_target_pairs={{0,8},{4,12},{8,0},{12,4},{16,24},{20,28},{24,16},{28,20},{1,9},{5... | collective-permute-start | bytes 251912 | tf_op jit(solution)/shard_map/ppermute | solution.py:159
  82.0 6.6 %copy-start.6 = (bf16[32,16,1152]{2,1,0:T(8,128)(2,1)S(1)}, bf16[32,16,1152]{2,1,0:T(8,128)(2,1)}, u32[]{:S(2)}) copy-start(bf16[32,16,1152]{2,1,0:T(8,128)(2,1)} %copy-done.4) | copy-start | bytes 3538948
  82.0 6.6 %copy-start.8 = (bf16[3,3,128,128]{3,2,1,0:T(8,128)(2,1)S(1)}, bf16[3,3,128,128]{3,2,1,0:T(8,128)(2,1)}, u32[]{:S(2)}) copy-start(bf16[3,3,128,128]{3,2,1,0:T(8,128)(2,1)} %param.10) | copy-start | bytes 884740
  82.3 5.2 %collective-permute-start.16 = (f32[10496]{0:T(1024)S(1)}, f32[10496]{0:T(1024)S(1)}, u32[]{:S(2)}, u32[]{:S(2)}) collective-permute-start(f32[10496]{0:T(1024)S(1)} %get-tuple-element.14), channel_id=1, source_target_pairs={{0,16},{4,20},{8,24},{12,28},{16,0},{20,4},{24,8},{28,12},{1,17},{... | collective-permute-start | bytes 125960 | tf_op jit(solution)/shard_map/ppermute | solution.py:159
  85.6 5.9 %collective-permute-start.8 = (f32[10496]{0:T(1024)S(1)}, f32[10496]{0:T(1024)S(1)}, u32[]{:S(2)}, u32[]{:S(2)}) collective-permute-start(f32[10496]{0:T(1024)S(1)} %get-tuple-element.12), channel_id=1, source_target_pairs={{0,16},{4,20},{8,24},{12,28},{16,0},{20,4},{24,8},{28,12},{1,17},{... | collective-permute-start | bytes 125960 | tf_op jit(solution)/shard_map/ppermute | solution.py:159
  87.6 5.6 %collective-permute-start.17 = (f32[10496]{0:T(1024)S(1)}, f32[10496]{0:T(1024)S(1)}, u32[]{:S(2)}, u32[]{:S(2)}) collective-permute-start(f32[10496]{0:T(1024)S(1)} %add.194), channel_id=1, source_target_pairs={{0,16},{4,20},{8,24},{12,28},{16,0},{20,4},{24,8},{28,12},{1,17},{... | collective-permute-start | bytes 125960 | tf_op jit(solution)/shard_map/ppermute | solution.py:159
  91.5 5.0 %collective-permute-start.9 = (f32[10496]{0:T(1024)S(1)}, f32[10496]{0:T(1024)S(1)}, u32[]{:S(2)}, u32[]{:S(2)}) collective-permute-start(f32[10496]{0:T(1024)S(1)} %add.189), channel_id=1, source_target_pairs={{0,16},{4,20},{8,24},{12,28},{16,0},{20,4},{24,8},{28,12},{1,17},{... | collective-permute-start | bytes 125960 | tf_op jit(solution)/shard_map/ppermute | solution.py:159
  93.2 5.1 %collective-permute-start.18 = (f32[20992]{0:T(1024)S(1)}, f32[20992]{0:T(1024)S(1)}, u32[]{:S(2)}, u32[]{:S(2)}) collective-permute-start(f32[20992]{0:T(1024)S(1)} %pad_maximum_fusion.10), channel_id=1, source_target_pairs={{0,8},{4,12},{8,0},{12,4},{16,24},{20,28},{24,16},{28,20},{1,9},{5... | collective-permute-start | bytes 251912 | tf_op jit(solution)/shard_map/ppermute | solution.py:159
  96.5 4.6 %collective-permute-start.10 = (f32[20992]{0:T(1024)S(1)}, f32[20992]{0:T(1024)S(1)}, u32[]{:S(2)}, u32[]{:S(2)}) collective-permute-start(f32[20992]{0:T(1024)S(1)} %pad_maximum_fusion.9), channel_id=1, source_target_pairs={{0,8},{4,12},{8,0},{12,4},{16,24},{20,28},{24,16},{28,20},{1,9},{5... | collective-permute-start | bytes 251912 | tf_op jit(solution)/shard_map/ppermute | solution.py:159
  98.4 2.9 %collective-permute-start.19 = (f32[41984]{0:T(1024)S(1)}, f32[41984]{0:T(1024)S(1)}, u32[]{:S(2)}, u32[]{:S(2)}) collective-permute-start(f32[41984]{0:T(1024)S(1)} %pad_maximum_fusion.7), channel_id=1, source_target_pairs={{0,4},{4,0},{8,12},{12,8},{16,20},{20,16},{24,28},{28,24},{1,5},{5... | collective-permute-start | bytes 503816 | tf_op jit(solution)/shard_map/ppermute | solution.py:159
  101.1 1.5 %collective-permute-start.11 = (f32[41984]{0:T(1024)S(1)}, f32[41984]{0:T(1024)S(1)}, u32[]{:S(2)}, u32[]{:S(2)}) collective-permute-start(f32[41984]{0:T(1024)S(1)} %pad_maximum_fusion.6), channel_id=1, source_target_pairs={{0,4},{4,0},{8,12},{12,8},{16,20},{20,16},{24,28},{28,24},{1,5},{5... | collective-permute-start | bytes 503816 | tf_op jit(solution)/shard_map/ppermute | solution.py:159

commit v3 on v2

--- a/solution.py
+++ b/solution.py
@@ -213,7 +213,7 @@
     half = rows.shape[1] // 2
     first = scatter_lon(rows[:, :half], steps)
     second = scatter_lon(rows[:, half:], list(reversed(steps)))
-    return jnp.concatenate([reduce_lat(first), reduce_lat(second)])
+    return reduce_lat(jnp.concatenate([first, second]))
 
 
 def solution(mesh):

time: 105 us -> 109 us (1.038)
  waiting for transfers between devices: 35.9 us -> 46.1 us
  starting transfers between devices: 22.9 us -> 17.3 us
    ppermute x16 -> x10, waiting for transfers between devices: 33.5 us -> 43.7 us  [exchange(): return lax.ppermute(part, axis, [(i, i ^ step) for i in range(size)])]
    ppermute x16 -> x10, starting transfers between devices: 14.5 us -> 8.95 us  [exchange(): return lax.ppermute(part, axis, [(i, i ^ step) for i in range(size)])]
    add x10 -> x7, other arithmetic: 2.94 us -> 2.07 us  [halve(): return keep + exchange(send, axis, step)]
    dynamic_slice x8 -> x5, local copies, waits for them, and re-layouts: 3.39 us -> 2.72 us  [halve(): send = lax.dynamic_index_in_dim(buffer, 1 - own, dim, keepdims=False)]
  transfers between devices with their start and end apart: 20 -> 14, of which waited for: 13 -> 11; matrix products, arithmetic and copies ran while one was open for 13% -> 9% of each run, Pallas kernels for 0% -> 0%
where the time goes in v3:
time: 109 us
  waiting for transfers between devices  46.1 us (42%)
  local copies, waits for them, and re-layouts  28.2 us (26%)
  starting transfers between devices  17.3 us (16%)
  other arithmetic  8.48 us (8%)
  matrix products  7.24 us (7%)
  between operations  1.65 us (2%)
    ppermute x10, waiting for transfers between devices, exchange(): return lax.ppermute(part, axis, [(i, i ^ step) for i in range(size)])  43.7 us
    ppermute x10, starting transfers between devices, exchange(): return lax.ppermute(part, axis, [(i, i ^ step) for i in range(size)])  8.95 us
    slice x16, local copies, waits for them, and re-layouts, strided(): padded[row_tap:row_tap + 2 * row_count:2, col_tap:col_tap + 2 * col_count:2]  7.14 us
    ppermute x2, starting transfers between devices, swap_edges(): lax.ppermute(jnp.concatenate([p.reshape(-1) for p in lasts]), axis, up)  6.02 us
    unnamed x66, local copies, waits for them, and re-layouts  5.51 us
    reshape x2, local copies, waits for them, and re-layouts, scatter_lon(): grid = rows.reshape((2,) * width + rows.shape[1:])  3.4 us
    reshape x1, local copies, waits for them, and re-layouts, shards(): up_flat.reshape(lon_count, up_size)  3.12 us
    dynamic_slice x5, local copies, waits for them, and re-layouts, halve(): send = lax.dynamic_index_in_dim(buffer, 1 - own, dim, keepdims=False)  2.72 us
  transfers between devices with their start and end apart: 14, of which 11 were waited for; matrix products, arithmetic and copies ran while one was open for 9% of the time, Pallas kernels for 0%

profile of v3, /device:TPU:0, one launch (start us, length us, event | category | flops | bytes accessed | tf_op | source)
XLA Modules:
  0.0 109.0 jit_solution(17213442707355699859)
XLA Ops:
  0.7 1.0 fusion.72
  1.7 0.8 multiply_exponential_fusion
  3.3 3.0 %collective-permute-start = (bf16[12288]{0:T(1024)(128)(2,1)S(1)}, bf16[12288]{0:T(1024)(128)(2,1)S(1)}, u32[]{:S(2)}, u32[]{:S(2)}) collective-permute-start(bf16[12288]{0:T(1024)(128)(2,1)S(1)} %pad_maximum_fusion.12), channel_id=1, source_target_pairs={{0,1},{1,2},{2,3},{3,0},{4,5},{5,6},{6,7},{7,4},{8,9},{9,10},{10,1... | collective-permute-start | bytes 73736 | tf_op jit(solution)/shard_map/ppermute | solution.py:25
  6.3 1.0 collective-permute-start.1
  7.3 0.7 slice_bitcast_fusion.15
  8.3 0.7 collective-permute-done
  9.1 1.1 collective-permute-done.1
  10.4 1.3 %collective-permute-start.2 = (bf16[7680]{0:T(1024)(128)(2,1)S(1)}, bf16[7680]{0:T(1024)(128)(2,1)S(1)}, u32[]{:S(2)}, u32[]{:S(2)}) collective-permute-start(bf16[7680]{0:T(1024)(128)(2,1)S(1)} %pad_maximum_fusion.14), channel_id=1, source_target_pairs={{4,0},{8,4},{12,8},{16,12},{20,16},{24,20},{28,24},{5,1},{9,5},{13... | collective-permute-start | bytes 46088 | tf_op jit(solution)/shard_map/ppermute | solution.py:26
  11.7 3.0 %collective-permute-start.3 = (bf16[7680]{0:T(1024)(128)(2,1)S(1)}, bf16[7680]{0:T(1024)(128)(2,1)S(1)}, u32[]{:S(2)}, u32[]{:S(2)}) collective-permute-start(bf16[7680]{0:T(1024)(128)(2,1)S(1)} %pad_maximum_fusion.15), channel_id=1, source_target_pairs={{0,4},{4,8},{8,12},{12,16},{16,20},{20,24},{24,28},{1,5},{5,9},{9,... | collective-permute-start | bytes 46088 | tf_op jit(solution)/shard_map/ppermute | solution.py:25
  15.0 0.6 collective-permute-done.3
  16.4 1.2 %convolution_bitcast_fusion.2 = f32[17,9,1,128]{3,0,1,2:T(8,128)S(1)} fusion(bf16[256,128]{1,0:T(8,128)(2,1)} %get-tuple-element.31, bf16[256,128]{1,0:T(8,128)(2,1)S(1)} %get-tuple-element.17, bf16[256,128]{1,0:T(8,128)(2,1)} %get-tuple-element.18, bf16[256,128]{1,0:T(8,128)(2,1)} %get-tuple-element.19, bf16[17,9,256]{2,0,1:T(8,128)(2,1)S(1)} %get-tuple-element.60, ...), kind=kOutput, calls=%fused_computation.6 | convolution fusion | flops 42409984 | bytes 653824 | tf_op jit(solution)/shard_map/rck,kn->rcn/dot_general | solution.py:78
  19.0 0.7 fusion.75
  24.3 0.6 slice.399
  24.9 0.6 slice.400
  25.5 0.7 slice.401
  26.3 0.9 slice.402
  27.7 1.0 copy-done.4
  29.0 0.8 copy-done.9
  29.8 1.9 %convolution_bitcast_fusion = f32[256,2048]{1,0:T(8,128)} fusion(bf16[16,8,256]{2,0,1:T(8,128)(2,1)S(1)} %fusion.62, bf16[16,8,2048]{2,1,0:T(8,128)(2,1)S(1)} %constant_dynamic-update-slice_fusion.2), kind=kOutput, calls=%fused_computation | convolution fusion | flops 134217728 | bytes 2686976 | tf_op jit(solution)/shard_map/rcm,rck->mk/dot_general | solution.py:144
  31.7 3.1 %reshape.175 = f32[4,131072]{1,0:T(4,128)S(1)} reshape(f32[256,2048]{1,0:T(8,128)} %convolution_bitcast_fusion) | data formatting | bytes 4194304 | tf_op jit(solution)/shard_map/reshape | solution.py:149
  35.7 1.1 %reshape.178 = f32[4,36864]{1,0:T(4,128)} reshape(f32[128,9,128]{2,1,0:T(8,128)S(1)} %copy.44) | data formatting | bytes 1179648 | tf_op jit(solution)/shard_map/reshape | solution.py:149
  36.8 2.5 %fusion.70 = (f32[4,83968]{1,0:T(4,128)S(1)}, f32[4,83968]{1,0:T(4,128)}) fusion(f32[4,131072]{1,0:T(4,128)S(1)} %reshape.175, f32[4,36864]{1,0:T(4,128)} %reshape.178), kind=kLoop, calls=%fused_computation.202 | loop fusion | flops 335872 | bytes 6717440 | tf_op jit(solution)/shard_map/slice | solution.py:214
  39.3 2.4 %reshape.179 = f32[2,2,83968]{2,1,0:T(2,128)S(1)} reshape(f32[4,83968]{1,0:T(4,128)} %get-tuple-element.13) | data formatting | bytes 2686976 | tf_op jit(solution)/shard_map/reshape | solution.py:186
  41.8 1.6 %collective-permute-start.6 = (f32[2,83968]{1,0:T(2,128)S(1)}, f32[2,83968]{1,0:T(2,128)}, u32[]{:S(2)}, u32[]{:S(2)}) collective-permute-start(f32[2,83968]{1,0:T(2,128)S(1)} %dynamic-slice_bitcast_fusion), channel_id=1, source_target_pairs={{0,2},{1,3},{2,0},{3,1},{4,6},{5,7},{6,4},{7,5},{8,10},{9,11},{10,... | collective-permute-start | bytes 2015240 | tf_op jit(solution)/shard_map/ppermute | solution.py:159
  43.3 1.0 reshape.176
  44.4 1.2 %constant_dynamic-slice_fusion.9 = (f32[2,1,83968]{2,1,0:T(1,128)S(1)}, f32[2,1,83968]{2,1,0:T(1,128)S(1)}) fusion(f32[2,2,83968]{2,1,0:T(2,128)S(1)} %reshape.176, s32[]{:T(128)S(6)} %select_n.170, s32[]{:T(128)S(6)} %select_n.171), kind=kLoop, calls=%fused_computation.196 | loop fusion | bytes 2686984 | tf_op jit(solution)/shard_map/jit(dynamic_index_in_dim)/dynamic_slice | solution.py:164
  45.9 1.9 %collective-permute-start.4 = (f32[2,83968]{1,0:T(2,128)S(1)}, f32[2,83968]{1,0:T(2,128)S(1)}, u32[]{:S(2)}, u32[]{:S(2)}) collective-permute-start(f32[2,83968]{1,0:T(2,128)S(1)} %bitcast.140), channel_id=1, source_target_pairs={{0,1},{1,0},{2,3},{3,2},{4,5},{5,4},{6,7},{7,6},{8,9},{9,8},{10,11... | collective-permute-start | bytes 2015240 | tf_op jit(solution)/shard_map/ppermute | solution.py:159
  47.8 11.8 %collective-permute-done.6 = f32[2,83968]{1,0:T(2,128)} collective-permute-done((f32[2,83968]{1,0:T(2,128)S(1)}, f32[2,83968]{1,0:T(2,128)}, u32[]{:S(2)}, u32[]{:S(2)}) %collective-permute-start.6) | collective-permute-done | bytes 671776 | tf_op jit(solution)/shard_map/ppermute | solution.py:159
  59.6 1.4 %bitcast_add_fusion.1 = f32[2,83968]{1,0:T(2,128)S(1)} fusion(f32[2,83968]{1,0:T(2,128)} %collective-permute-done.6, f32[2,2,83968]{2,1,0:T(2,128)S(1)} %copy-done.1, s32[]{:T(128)S(6)} %select_n.174), kind=kLoop, calls=%fused_computation.13 | loop fusion | flops 167936 | bytes 2015236 | tf_op jit(solution)/shard_map/add | solution.py:166
  61.1 0.6 constant_dynamic-slice_fusion.4
  61.7 2.5 %collective-permute-start.7 = (f32[83968]{0:T(1024)S(1)}, f32[83968]{0:T(1024)S(1)}, u32[]{:S(2)}, u32[]{:S(2)}) collective-permute-start(f32[83968]{0:T(1024)S(1)} %bitcast.143), channel_id=1, source_target_pairs={{0,1},{1,0},{2,3},{3,2},{4,5},{5,4},{6,7},{7,6},{8,9},{9,8},{10,11... | collective-permute-start | bytes 1007624 | tf_op jit(solution)/shard_map/ppermute | solution.py:159
  64.6 0.6 constant_dynamic-slice_fusion.6
  65.7 6.7 %collective-permute-done.7 = f32[83968]{0:T(1024)S(1)} collective-permute-done((f32[83968]{0:T(1024)S(1)}, f32[83968]{0:T(1024)S(1)}, u32[]{:S(2)}, u32[]{:S(2)}) %collective-permute-start.7) | collective-permute-done | bytes 335904 | tf_op jit(solution)/shard_map/ppermute | solution.py:159
  72.5 2.6 %collective-permute-done.5 = f32[83968]{0:T(1024)S(1)} collective-permute-done((f32[83968]{0:T(1024)S(1)}, f32[83968]{0:T(1024)S(1)}, u32[]{:S(2)}, u32[]{:S(2)}) %collective-permute-start.5) | collective-permute-done | bytes 335904 | tf_op jit(solution)/shard_map/ppermute | solution.py:159
  75.5 0.6 constant_dynamic-slice_fusion.2
  76.3 1.6 %collective-permute-done.8 = f32[83968]{0:T(1024)S(1)} collective-permute-done((f32[83968]{0:T(1024)S(1)}, f32[83968]{0:T(1024)S(1)}, u32[]{:S(2)}, u32[]{:S(2)}) %collective-permute-start.8) | collective-permute-done | bytes 335904 | tf_op jit(solution)/shard_map/ppermute | solution.py:159
  79.0 6.0 %collective-permute-done.9 = f32[41984]{0:T(1024)S(1)} collective-permute-done((f32[41984]{0:T(1024)S(1)}, f32[41984]{0:T(1024)S(1)}, u32[]{:S(2)}, u32[]{:S(2)}) %collective-permute-start.9) | collective-permute-done | bytes 167968 | tf_op jit(solution)/shard_map/ppermute | solution.py:159
  85.6 1.4 %collective-permute-start.10 = (f32[20992]{0:T(1024)S(1)}, f32[20992]{0:T(1024)S(1)}, u32[]{:S(2)}, u32[]{:S(2)}) collective-permute-start(f32[20992]{0:T(1024)S(1)} %get-tuple-element.8), channel_id=1, source_target_pairs={{0,16},{4,20},{8,24},{12,28},{16,0},{20,4},{24,8},{28,12},{1,17},{... | collective-permute-start | bytes 251912 | tf_op jit(solution)/shard_map/ppermute | solution.py:159
  87.0 4.9 %collective-permute-done.10 = f32[20992]{0:T(1024)S(1)} collective-permute-done((f32[20992]{0:T(1024)S(1)}, f32[20992]{0:T(1024)S(1)}, u32[]{:S(2)}, u32[]{:S(2)}) %collective-permute-start.10) | collective-permute-done | bytes 84000 | tf_op jit(solution)/shard_map/ppermute | solution.py:159
  91.9 0.6 collective-permute-start.11
  92.6 4.9 %collective-permute-done.11 = f32[20992]{0:T(1024)S(1)} collective-permute-done((f32[20992]{0:T(1024)S(1)}, f32[20992]{0:T(1024)S(1)}, u32[]{:S(2)}, u32[]{:S(2)}) %collective-permute-start.11) | collective-permute-done | bytes 84000 | tf_op jit(solution)/shard_map/ppermute | solution.py:159
  97.5 0.7 pad_maximum_fusion.9
  98.7 5.1 %collective-permute-done.12 = f32[41984]{0:T(1024)} collective-permute-done((f32[41984]{0:T(1024)}, f32[41984]{0:T(1024)}, u32[]{:S(2)}, u32[]{:S(2)}) %collective-permute-start.12) | collective-permute-done | bytes 167968 | tf_op jit(solution)/shard_map/ppermute | solution.py:159
  103.8 0.9 broadcast_select_fusion.4
  104.9 1.1 %convolution_convert_fusion = bf16[32,16,128]{2,1,0:T(8,128)(2,1)} fusion(bf16[32,16,1152]{2,1,0:T(8,128)(2,1)S(1)} %copy-done.6, bf16[1152,128,1]{1,0,2:T(8,128)(2,1)S(1)} %bitcast.138), kind=kOutput, calls=%fused_computation.5 | convolution fusion | flops 151060480 | bytes 1605632 | tf_op jit(solution)/shard_map/rck,kn->rcn/dot_general | solution.py:129
  106.1 1.0 fusion.76
  107.3 1.0 copy.45
  108.3 0.7 copy.46
  (157 shorter events, 14.3 us)
Async XLA Ops:
  0.6 2.3 %copy-start.13 = (s32[16,8,256]{2,1,0:T(8,128)S(1)}, s32[16,8,256]{2,1,0:T(8,128)}, u32[]{:S(2)}) copy-start(s32[16,8,256]{2,1,0:T(8,128)} %param.6) | copy-start | bytes 393220
  0.6 6.7 %copy-start.2 = (bf16[4,4,256,128]{3,2,1,0:T(8,128)(2,1)S(1)}, bf16[4,4,256,128]{3,2,1,0:T(8,128)(2,1)}, u32[]{:S(2)}) copy-start(bf16[4,4,256,128]{3,2,1,0:T(8,128)(2,1)} %param.8) | copy-start | bytes 3145732
  2.9 5.1 %copy-start.7 = (bf16[3,3,128,128]{3,2,1,0:T(8,128)(2,1)S(1)}, bf16[3,3,128,128]{3,2,1,0:T(8,128)(2,1)}, u32[]{:S(2)}) copy-start(bf16[3,3,128,128]{3,2,1,0:T(8,128)(2,1)} %param.10) | copy-start | bytes 884740
  3.3 5.8 %collective-permute-start = (bf16[12288]{0:T(1024)(128)(2,1)S(1)}, bf16[12288]{0:T(1024)(128)(2,1)S(1)}, u32[]{:S(2)}, u32[]{:S(2)}) collective-permute-start(bf16[12288]{0:T(1024)(128)(2,1)S(1)} %pad_maximum_fusion.12), channel_id=1, source_target_pairs={{0,1},{1,2},{2,3},{3,0},{4,5},{5,6},{6,7},{7,4},{8,9},{9,10},{10,1... | collective-permute-start | bytes 73736 | tf_op jit(solution)/shard_map/ppermute | solution.py:25
  6.3 3.9 %collective-permute-start.1 = (bf16[12288]{0:T(1024)(128)(2,1)S(1)}, bf16[12288]{0:T(1024)(128)(2,1)S(1)}, u32[]{:S(2)}, u32[]{:S(2)}) collective-permute-start(bf16[12288]{0:T(1024)(128)(2,1)S(1)} %pad_maximum_fusion.13), channel_id=1, source_target_pairs={{1,0},{2,1},{3,2},{0,3},{5,4},{6,5},{7,6},{4,7},{9,8},{10,9},{11,1... | collective-permute-start | bytes 73736 | tf_op jit(solution)/shard_map/ppermute | solution.py:26
  7.3 1.7 %copy-start.11 = (bf16[32,16,128]{2,1,0:T(8,128)(2,1)S(1)}, bf16[32,16,128]{2,1,0:T(8,128)(2,1)}, u32[]{:S(2)}) copy-start(bf16[32,16,128]{2,1,0:T(8,128)(2,1)} %param.11) | copy-start | bytes 393220
  10.4 4.4 %collective-permute-start.2 = (bf16[7680]{0:T(1024)(128)(2,1)S(1)}, bf16[7680]{0:T(1024)(128)(2,1)S(1)}, u32[]{:S(2)}, u32[]{:S(2)}) collective-permute-start(bf16[7680]{0:T(1024)(128)(2,1)S(1)} %pad_maximum_fusion.14), channel_id=1, source_target_pairs={{4,0},{8,4},{12,8},{16,12},{20,16},{24,20},{28,24},{5,1},{9,5},{13... | collective-permute-start | bytes 46088 | tf_op jit(solution)/shard_map/ppermute | solution.py:26
  11.7 3.9 %collective-permute-start.3 = (bf16[7680]{0:T(1024)(128)(2,1)S(1)}, bf16[7680]{0:T(1024)(128)(2,1)S(1)}, u32[]{:S(2)}, u32[]{:S(2)}) collective-permute-start(bf16[7680]{0:T(1024)(128)(2,1)S(1)} %pad_maximum_fusion.15), channel_id=1, source_target_pairs={{0,4},{4,8},{8,12},{12,16},{16,20},{20,24},{24,28},{1,5},{5,9},{9,... | collective-permute-start | bytes 46088 | tf_op jit(solution)/shard_map/ppermute | solution.py:25
  19.0 0.7 copy-start.14
  27.7 1.0 copy-start.4
  29.0 0.8 copy-start.9
  31.7 3.1 %copy-start.5 = (bf16[32,16,1152]{2,1,0:T(8,128)(2,1)S(1)}, bf16[32,16,1152]{2,1,0:T(8,128)(2,1)}, u32[]{:S(2)}) copy-start(bf16[32,16,1152]{2,1,0:T(8,128)(2,1)} %copy-done.4) | copy-start | bytes 3538948
  31.7 3.1 %copy-start.12 = (bf16[32,16,128]{2,1,0:T(8,128)(2,1)S(1)}, bf16[32,16,128]{2,1,0:T(8,128)(2,1)}, u32[]{:S(2)}) copy-start(bf16[32,16,128]{2,1,0:T(8,128)(2,1)} %param.11) | copy-start | bytes 393220
  41.7 1.6 %copy-start = (f32[2,2,83968]{2,1,0:T(2,128)}, f32[2,2,83968]{2,1,0:T(2,128)S(1)}, u32[]{:S(2)}) copy-start(f32[2,2,83968]{2,1,0:T(2,128)S(1)} %reshape.179) | copy-start | bytes 4030468
  41.8 17.9 %collective-permute-start.6 = (f32[2,83968]{1,0:T(2,128)S(1)}, f32[2,83968]{1,0:T(2,128)}, u32[]{:S(2)}, u32[]{:S(2)}) collective-permute-start(f32[2,83968]{1,0:T(2,128)S(1)} %dynamic-slice_bitcast_fusion), channel_id=1, source_target_pairs={{0,2},{1,3},{2,0},{3,1},{4,6},{5,7},{6,4},{7,5},{8,10},{9,11},{10,... | collective-permute-start | bytes 2015240 | tf_op jit(solution)/shard_map/ppermute | solution.py:159
  45.5 14.1 %copy-start.1 = (f32[2,2,83968]{2,1,0:T(2,128)S(1)}, f32[2,2,83968]{2,1,0:T(2,128)}, u32[]{:S(2)}) copy-start(f32[2,2,83968]{2,1,0:T(2,128)} %copy-done) | copy-start | bytes 4030468
  45.9 18.2 %collective-permute-start.4 = (f32[2,83968]{1,0:T(2,128)S(1)}, f32[2,83968]{1,0:T(2,128)S(1)}, u32[]{:S(2)}, u32[]{:S(2)}) collective-permute-start(f32[2,83968]{1,0:T(2,128)S(1)} %bitcast.140), channel_id=1, source_target_pairs={{0,1},{1,0},{2,3},{3,2},{4,5},{5,4},{6,7},{7,6},{8,9},{9,8},{10,11... | collective-permute-start | bytes 2015240 | tf_op jit(solution)/shard_map/ppermute | solution.py:159
  61.7 10.8 %collective-permute-start.7 = (f32[83968]{0:T(1024)S(1)}, f32[83968]{0:T(1024)S(1)}, u32[]{:S(2)}, u32[]{:S(2)}) collective-permute-start(f32[83968]{0:T(1024)S(1)} %bitcast.143), channel_id=1, source_target_pairs={{0,1},{1,0},{2,3},{3,2},{4,5},{5,4},{6,7},{7,6},{8,9},{9,8},{10,11... | collective-permute-start | bytes 1007624 | tf_op jit(solution)/shard_map/ppermute | solution.py:159
  65.2 9.8 %collective-permute-start.5 = (f32[83968]{0:T(1024)S(1)}, f32[83968]{0:T(1024)S(1)}, u32[]{:S(2)}, u32[]{:S(2)}) collective-permute-start(f32[83968]{0:T(1024)S(1)} %bitcast.144), channel_id=1, source_target_pairs={{0,2},{1,3},{2,0},{3,1},{4,6},{5,7},{6,4},{7,5},{8,10},{9,11},{10,... | collective-permute-start | bytes 1007624 | tf_op jit(solution)/shard_map/ppermute | solution.py:159
  76.1 1.7 %collective-permute-start.8 = (f32[83968]{0:T(1024)S(1)}, f32[83968]{0:T(1024)S(1)}, u32[]{:S(2)}, u32[]{:S(2)}) collective-permute-start(f32[83968]{0:T(1024)S(1)} %bitcast.142), channel_id=1, source_target_pairs={{0,4},{4,0},{8,12},{12,8},{16,20},{20,16},{24,28},{28,24},{1,5},{5... | collective-permute-start | bytes 1007624 | tf_op jit(solution)/shard_map/ppermute | solution.py:159
  78.1 20.1 %copy-start.3 = (bf16[4,4,256,128]{3,2,1,0:T(8,128)(2,1)S(1)}, bf16[4,4,256,128]{3,2,1,0:T(8,128)(2,1)}, u32[]{:S(2)}) copy-start(bf16[4,4,256,128]{3,2,1,0:T(8,128)(2,1)} %param.8) | copy-start | bytes 3145732
  78.6 6.4 %collective-permute-start.9 = (f32[41984]{0:T(1024)S(1)}, f32[41984]{0:T(1024)S(1)}, u32[]{:S(2)}, u32[]{:S(2)}) collective-permute-start(f32[41984]{0:T(1024)S(1)} %bitcast.145), channel_id=1, source_target_pairs={{0,8},{4,12},{8,0},{12,4},{16,24},{20,28},{24,16},{28,20},{1,9},{5... | collective-permute-start | bytes 503816 | tf_op jit(solution)/shard_map/ppermute | solution.py:159
  85.6 6.3 %collective-permute-start.10 = (f32[20992]{0:T(1024)S(1)}, f32[20992]{0:T(1024)S(1)}, u32[]{:S(2)}, u32[]{:S(2)}) collective-permute-start(f32[20992]{0:T(1024)S(1)} %get-tuple-element.8), channel_id=1, source_target_pairs={{0,16},{4,20},{8,24},{12,28},{16,0},{20,4},{24,8},{28,12},{1,17},{... | collective-permute-start | bytes 251912 | tf_op jit(solution)/shard_map/ppermute | solution.py:159
  91.9 5.5 %collective-permute-start.11 = (f32[20992]{0:T(1024)S(1)}, f32[20992]{0:T(1024)S(1)}, u32[]{:S(2)}, u32[]{:S(2)}) collective-permute-start(f32[20992]{0:T(1024)S(1)} %add.169), channel_id=1, source_target_pairs={{0,16},{4,20},{8,24},{12,28},{16,0},{20,4},{24,8},{28,12},{1,17},{... | collective-permute-start | bytes 251912 | tf_op jit(solution)/shard_map/ppermute | solution.py:159
  98.2 6.7 %copy-start.6 = (bf16[32,16,1152]{2,1,0:T(8,128)(2,1)S(1)}, bf16[32,16,1152]{2,1,0:T(8,128)(2,1)}, u32[]{:S(2)}) copy-start(bf16[32,16,1152]{2,1,0:T(8,128)(2,1)} %copy-done.4) | copy-start | bytes 3538948
  98.2 5.7 %collective-permute-start.12 = (f32[41984]{0:T(1024)}, f32[41984]{0:T(1024)}, u32[]{:S(2)}, u32[]{:S(2)}) collective-permute-start(f32[41984]{0:T(1024)} %pad_maximum_fusion.9), channel_id=1, source_target_pairs={{0,8},{4,12},{8,0},{12,4},{16,24},{20,28},{24,16},{28,20},{1,9},{5... | collective-permute-start | bytes 503816 | tf_op jit(solution)/shard_map/ppermute | solution.py:159
  98.7 6.2 %copy-start.8 = (bf16[3,3,128,128]{3,2,1,0:T(8,128)(2,1)S(1)}, bf16[3,3,128,128]{3,2,1,0:T(8,128)(2,1)}, u32[]{:S(2)}) copy-start(bf16[3,3,128,128]{3,2,1,0:T(8,128)(2,1)} %param.10) | copy-start | bytes 884740
  98.7 7.3 %copy-start.10 = (bf16[16,8,2048]{2,1,0:T(8,128)(2,1)S(1)}, bf16[16,8,2048]{2,1,0:T(8,128)(2,1)}, u32[]{:S(2)}) copy-start(bf16[16,8,2048]{2,1,0:T(8,128)(2,1)} %copy-done.9) | copy-start | bytes 1572868
  104.8 2.2 %collective-permute-start.13 = (f32[83968]{0:T(1024)S(1)}, f32[83968]{0:T(1024)S(1)}, u32[]{:S(2)}, u32[]{:S(2)}) collective-permute-start(f32[83968]{0:T(1024)S(1)} %pad_maximum_fusion.5), channel_id=1, source_target_pairs={{0,4},{4,0},{8,12},{12,8},{16,20},{20,16},{24,28},{28,24},{1,5},{5... | collective-permute-start | bytes 1007624 | tf_op jit(solution)/shard_map/ppermute | solution.py:159

commit v4 on v2

--- a/solution.py
+++ b/solution.py
@@ -163,7 +163,7 @@
     own = lax.axis_index(axis) // step % 2
     keep = lax.dynamic_index_in_dim(buffer, own, dim, keepdims=False)
     send = lax.dynamic_index_in_dim(buffer, 1 - own, dim, keepdims=False)
-    return keep + exchange(send, axis, step)
+    return keep + exchange(send.astype(jnp.bfloat16), axis, step).astype(keep.dtype)
 
 
 def double(part, axis, step):
@@ -198,9 +198,10 @@
         return lax.psum(flat, "lat")
     for step in steps:
         flat = halve(flat.reshape(2, -1), "lat", step, 0)
+    flat = flat.astype(jnp.bfloat16)
     for step in reversed(steps):
         flat = double(flat, "lat", step)
-    return flat
+    return flat.astype(jnp.float32)
 
 
 def reduce_terms(rows):

time: 105 us -> 94.3 us (0.90)
  waiting for transfers between devices: 35.9 us -> 18.1 us
  starting transfers between devices: 22.9 us -> 28.8 us
  local copies, waits for them, and re-layouts: 29 us -> 32.2 us
  other arithmetic: 7.66 us -> 5.91 us
    ppermute x16, waiting for transfers between devices: 33.5 us -> 17.1 us  [exchange(): return lax.ppermute(part, axis, [(i, i ^ step) for i in range(size)])]
    ppermute x16, starting transfers between devices: 14.5 us -> 20.4 us  [exchange(): return lax.ppermute(part, axis, [(i, i ^ step) for i in range(size)])]
    convert_element_type x0 -> x10, local copies, waits for them, and re-layouts: none -> 4.76 us  [halve(): send.astype(jnp.bfloat16)]
    dynamic_slice x8 -> x0, local copies, waits for them, and re-layouts: 3.39 us -> none  [halve(): send = lax.dynamic_index_in_dim(buffer, 1 - own, dim, keepdims=False)]
    add x10 -> x8, other arithmetic: 2.94 us -> 0.97 us  [halve(): keep + exchange(send.astype(jnp.bfloat16), axis, step).astype(keep.dtype)]
    dynamic_slice x1 -> x9, local copies, waits for them, and re-layouts: 1.16 us -> 2.31 us  [halve(): keep = lax.dynamic_index_in_dim(buffer, own, dim, keepdims=False)]
  transfers between devices with their start and end apart: 20 -> 20, of which waited for: 13 -> 13; matrix products, arithmetic and copies ran while one was open for 13% -> 16% of each run, Pallas kernels for 0% -> 0%
where the time goes in v4:
time: 94.3 us; the launch traced here: 93.9 us
  local copies, waits for them, and re-layouts  32.2 us (34%)
  starting transfers between devices  28.8 us (31%)
  waiting for transfers between devices  18.1 us (19%)
  matrix products  7.19 us (8%)
  other arithmetic  5.91 us (6%)
  between operations  1.8 us (2%)
    ppermute x16, starting transfers between devices, exchange(): return lax.ppermute(part, axis, [(i, i ^ step) for i in range(size)])  20.4 us
    ppermute x16, waiting for transfers between devices, exchange(): return lax.ppermute(part, axis, [(i, i ^ step) for i in range(size)])  17.1 us
    slice x16, local copies, waits for them, and re-layouts, strided(): padded[row_tap:row_tap + 2 * row_count:2, col_tap:col_tap + 2 * col_count:2]  7.14 us
    unnamed x66, local copies, waits for them, and re-layouts  6.28 us
    ppermute x2, starting transfers between devices, swap_edges(): lax.ppermute(jnp.concatenate([p.reshape(-1) for p in lasts]), axis, up)  6.02 us
    convert_element_type x10, local copies, waits for them, and re-layouts, halve(): send.astype(jnp.bfloat16)  4.76 us
    reshape x2, local copies, waits for them, and re-layouts, scatter_lon(): grid = rows.reshape((2,) * width + rows.shape[1:])  3.4 us
    reshape x1, local copies, waits for them, and re-layouts, shards(): up_flat.reshape(lon_count, up_size)  3.12 us
  transfers between devices with their start and end apart: 20, of which 13 were waited for; matrix products, arithmetic and copies ran while one was open for 16% of the time, Pallas kernels for 0%

profile of v4, /device:TPU:0, one launch (start us, length us, event | category | flops | bytes accessed | tf_op | source)
XLA Modules:
  0.0 93.9 jit_solution(18341165972184695919)
XLA Ops:
  0.7 1.0 %fusion.70 = (bf16[32,2,128]{2,1,0:T(2,128)(2,1)S(1)}, bf16[32,2,128]{2,1,0:T(2,128)(2,1)S(1)}) fusion(bf16[32,16,128]{2,1,0:T(8,128)(2,1)} %param.11), kind=kLoop, calls=%fused_computation.229 | loop fusion | bytes 65536 | tf_op jit(solution)/shard_map/slice | solution.py:23
  1.7 0.8 multiply_exponential_fusion
  3.2 3.0 %collective-permute-start = (bf16[12288]{0:T(1024)(128)(2,1)S(1)}, bf16[12288]{0:T(1024)(128)(2,1)S(1)}, u32[]{:S(2)}, u32[]{:S(2)}) collective-permute-start(bf16[12288]{0:T(1024)(128)(2,1)S(1)} %pad_maximum_fusion.17), channel_id=1, source_target_pairs={{0,1},{1,2},{2,3},{3,0},{4,5},{5,6},{6,7},{7,4},{8,9},{9,10},{10,1... | collective-permute-start | bytes 73736 | tf_op jit(solution)/shard_map/ppermute | solution.py:25
  6.3 1.0 %collective-permute-start.1 = (bf16[12288]{0:T(1024)(128)(2,1)S(1)}, bf16[12288]{0:T(1024)(128)(2,1)S(1)}, u32[]{:S(2)}, u32[]{:S(2)}) collective-permute-start(bf16[12288]{0:T(1024)(128)(2,1)S(1)} %pad_maximum_fusion.18), channel_id=1, source_target_pairs={{1,0},{2,1},{3,2},{0,3},{5,4},{6,5},{7,6},{4,7},{9,8},{10,9},{11,1... | collective-permute-start | bytes 73736 | tf_op jit(solution)/shard_map/ppermute | solution.py:26
  7.3 0.7 slice_bitcast_fusion.15
  8.0 1.3 %copy.67 = bf16[4,4,256,128]{2,3,1,0:T(8,128)(2,1)} copy(bf16[4,4,256,128]{3,2,1,0:T(8,128)(2,1)S(1)} %copy-done) | data formatting | bytes 2097152 | tf_op args[2]
  10.4 1.3 %collective-permute-start.2 = (bf16[7680]{0:T(1024)(128)(2,1)S(1)}, bf16[7680]{0:T(1024)(128)(2,1)S(1)}, u32[]{:S(2)}, u32[]{:S(2)}) collective-permute-start(bf16[7680]{0:T(1024)(128)(2,1)S(1)} %pad_maximum_fusion.19), channel_id=1, source_target_pairs={{4,0},{8,4},{12,8},{16,12},{20,16},{24,20},{28,24},{5,1},{9,5},{13... | collective-permute-start | bytes 46088 | tf_op jit(solution)/shard_map/ppermute | solution.py:26
  11.7 3.0 %collective-permute-start.3 = (bf16[7680]{0:T(1024)(128)(2,1)S(1)}, bf16[7680]{0:T(1024)(128)(2,1)S(1)}, u32[]{:S(2)}, u32[]{:S(2)}) collective-permute-start(bf16[7680]{0:T(1024)(128)(2,1)S(1)} %pad_maximum_fusion.20), channel_id=1, source_target_pairs={{0,4},{4,8},{8,12},{12,16},{16,20},{20,24},{24,28},{1,5},{5,9},{9,... | collective-permute-start | bytes 46088 | tf_op jit(solution)/shard_map/ppermute | solution.py:25
  15.0 0.6 collective-permute-done.3
  16.4 1.2 %convolution_bitcast_fusion.2 = f32[17,9,1,128]{3,0,1,2:T(8,128)S(1)} fusion(bf16[256,128]{1,0:T(8,128)(2,1)} %get-tuple-element.31, bf16[256,128]{1,0:T(8,128)(2,1)S(1)} %get-tuple-element.17, bf16[256,128]{1,0:T(8,128)(2,1)} %get-tuple-element.18, bf16[256,128]{1,0:T(8,128)(2,1)} %get-tuple-element.19, bf16[17,9,256]{2,0,1:T(8,128)(2,1)S(1)} %get-tuple-element.58, ...), kind=kOutput, calls=%fused_computation.6 | convolution fusion | flops 42409984 | bytes 653824 | tf_op jit(solution)/shard_map/rck,kn->rcn/dot_general | solution.py:78
  19.0 0.6 fusion.73
  24.2 0.6 slice.399
  25.5 0.7 slice.401
  26.2 0.9 slice.402
  27.7 1.0 %copy-done.4 = bf16[32,16,1152]{2,1,0:T(8,128)(2,1)} copy-done((bf16[32,16,1152]{2,1,0:T(8,128)(2,1)}, bf16[32,16,1152]{2,1,0:T(8,128)(2,1)S(1)}, u32[]{:S(2)}) %copy-start.4) | copy-done | bytes 1179672
  29.0 0.8 copy-done.9
  29.7 1.9 %convolution_bitcast_fusion = f32[256,2048]{1,0:T(8,128)} fusion(bf16[16,8,256]{2,0,1:T(8,128)(2,1)S(1)} %fusion.60, bf16[16,8,2048]{2,1,0:T(8,128)(2,1)S(1)} %constant_dynamic-update-slice_fusion.2), kind=kOutput, calls=%fused_computation | convolution fusion | flops 134217728 | bytes 2686976 | tf_op jit(solution)/shard_map/rcm,rck->mk/dot_general | solution.py:144
  31.6 3.1 %reshape.200 = f32[4,131072]{1,0:T(4,128)S(1)} reshape(f32[256,2048]{1,0:T(8,128)} %convolution_bitcast_fusion) | data formatting | bytes 4194304 | tf_op jit(solution)/shard_map/reshape | solution.py:149
  35.7 1.1 %reshape.206 = f32[4,36864]{1,0:T(4,128)} reshape(f32[128,9,128]{2,1,0:T(8,128)S(1)} %copy.70) | data formatting | bytes 1179648 | tf_op jit(solution)/shard_map/reshape | solution.py:149
  36.8 2.5 %fusion.68 = (f32[4,83968]{1,0:T(4,128)S(1)}, f32[4,83968]{1,0:T(4,128)}) fusion(f32[4,131072]{1,0:T(4,128)S(1)} %reshape.200, f32[4,36864]{1,0:T(4,128)} %reshape.206), kind=kLoop, calls=%fused_computation.227 | loop fusion | flops 335872 | bytes 6717440 | tf_op jit(solution)/shard_map/slice | solution.py:215
  39.3 2.4 %reshape.207 = f32[2,2,83968]{2,1,0:T(2,128)S(1)} reshape(f32[4,83968]{1,0:T(4,128)} %get-tuple-element.15) | data formatting | bytes 2686976 | tf_op jit(solution)/shard_map/reshape | solution.py:186
  41.9 1.7 %collective-permute-start.12 = (bf16[2,83968]{1,0:T(2,128)(2,1)S(1)}, bf16[2,83968]{1,0:T(2,128)(2,1)S(1)}, u32[]{:S(2)}, u32[]{:S(2)}) collective-permute-start(bf16[2,83968]{1,0:T(2,128)(2,1)S(1)} %fusion.11), channel_id=1, source_target_pairs={{0,2},{1,3},{2,0},{3,1},{4,6},{5,7},{6,4},{7,5},{8,10},{9,11},{10,... | collective-permute-start | bytes 1007624 | tf_op jit(solution)/shard_map/ppermute | solution.py:159
  43.6 1.0 %reshape.201 = f32[2,2,83968]{2,1,0:T(2,128)S(1)} reshape(f32[4,83968]{1,0:T(4,128)S(1)} %get-tuple-element.14) | data formatting | bytes 2686976 | tf_op jit(solution)/shard_map/reshape | solution.py:186
  44.7 0.7 constant_dynamic-slice_fusion.4
  45.4 0.6 dynamic-slice_convert_fusion.1
  46.1 1.1 %convolution_convert_fusion = bf16[32,16,128]{2,1,0:T(8,128)(2,1)} fusion(bf16[32,16,1152]{2,1,0:T(8,128)(2,1)S(1)} %copy-done.6, bf16[1152,128,1]{1,0,2:T(8,128)(2,1)S(1)} %bitcast.131), kind=kOutput, calls=%fused_computation.5 | convolution fusion | flops 151060480 | bytes 1605632 | tf_op jit(solution)/shard_map/rck,kn->rcn/dot_general | solution.py:129
  47.6 1.6 %collective-permute-start.4 = (bf16[2,83968]{1,0:T(2,128)(2,1)S(1)}, bf16[2,83968]{1,0:T(2,128)(2,1)S(1)}, u32[]{:S(2)}, u32[]{:S(2)}) collective-permute-start(bf16[2,83968]{1,0:T(2,128)(2,1)S(1)} %bitcast.137), channel_id=1, source_target_pairs={{0,1},{1,0},{2,3},{3,2},{4,5},{5,4},{6,7},{7,6},{8,9},{9,8},{10,11... | collective-permute-start | bytes 1007624 | tf_op jit(solution)/shard_map/ppermute | solution.py:159
  49.2 1.0 %fusion.74 = f32[16,8,256]{2,1,0:T(8,128)} fusion(bf16[16,8,2048]{2,1,0:T(8,128)(2,1)S(1)} %copy-done.10, bf16[2048,256,1]{1,0,2:T(8,128)(2,1)S(1)} %bitcast.127), kind=kOutput, calls=%fused_computation.233 | convolution fusion | flops 134217728 | bytes 1703936 | tf_op jit(solution)/shard_map/rck,kn->rcn/dot_general | solution.py:141
  50.1 2.3 %collective-permute-done.12 = bf16[2,83968]{1,0:T(2,128)(2,1)S(1)} collective-permute-done((bf16[2,83968]{1,0:T(2,128)(2,1)S(1)}, bf16[2,83968]{1,0:T(2,128)(2,1)S(1)}, u32[]{:S(2)}, u32[]{:S(2)}) %collective-permute-start.12) | collective-permute-done | bytes 335904 | tf_op jit(solution)/shard_map/ppermute | solution.py:159
  53.1 1.0 %convert_reduce_fusion = bf16[83968]{0:T(1024)(128)(2,1)S(1)} fusion(f32[2,83968]{1,0:T(2,128)S(1)} %bitcast_add_fusion.1, s32[]{:T(128)S(6)} %select_n.220), kind=kLoop, calls=%fused_computation.33 | loop fusion | bytes 335876 | tf_op jit(solution)/shard_map/convert_element_type | solution.py:166
  54.1 2.5 %collective-permute-start.13 = (bf16[83968]{0:T(1024)(128)(2,1)S(1)}, bf16[83968]{0:T(1024)(128)(2,1)S(1)}, u32[]{:S(2)}, u32[]{:S(2)}) collective-permute-start(bf16[83968]{0:T(1024)(128)(2,1)S(1)} %convert_reduce_fusion), channel_id=1, source_target_pairs={{0,1},{1,0},{2,3},{3,2},{4,5},{5,4},{6,7},{7,6},{8,9},{9,8},{10,11... | collective-permute-start | bytes 503816 | tf_op jit(solution)/shard_map/ppermute | solution.py:159
  56.6 1.7 %collective-permute-done.4 = bf16[2,83968]{1,0:T(2,128)(2,1)S(1)} collective-permute-done((bf16[2,83968]{1,0:T(2,128)(2,1)S(1)}, bf16[2,83968]{1,0:T(2,128)(2,1)S(1)}, u32[]{:S(2)}, u32[]{:S(2)}) %collective-permute-start.4) | collective-permute-done | bytes 335904 | tf_op jit(solution)/shard_map/ppermute | solution.py:159
  59.1 1.2 %convert_reduce_fusion.1 = bf16[83968]{0:T(1024)(128)(2,1)S(1)} fusion(f32[2,83968]{1,0:T(2,128)S(1)} %bitcast_add_fusion, s32[]{:T(128)S(6)} %select_n.224), kind=kLoop, calls=%fused_computation.35 | loop fusion | bytes 335876 | tf_op jit(solution)/shard_map/convert_element_type | solution.py:166
  60.3 0.6 collective-permute-start.5
  60.9 1.0 %collective-permute-done.13 = bf16[83968]{0:T(1024)(128)(2,1)S(1)} collective-permute-done((bf16[83968]{0:T(1024)(128)(2,1)S(1)}, bf16[83968]{0:T(1024)(128)(2,1)S(1)}, u32[]{:S(2)}, u32[]{:S(2)}) %collective-permute-start.13) | collective-permute-done | bytes 167968 | tf_op jit(solution)/shard_map/ppermute | solution.py:159
  63.0 3.8 %collective-permute-done.5 = bf16[83968]{0:T(1024)(128)(2,1)S(1)} collective-permute-done((bf16[83968]{0:T(1024)(128)(2,1)S(1)}, bf16[83968]{0:T(1024)(128)(2,1)S(1)}, u32[]{:S(2)}, u32[]{:S(2)}) %collective-permute-start.5) | collective-permute-done | bytes 167968 | tf_op jit(solution)/shard_map/ppermute | solution.py:159
  68.1 2.5 %collective-permute-start.15 = (bf16[20992]{0:T(1024)(128)(2,1)S(1)}, bf16[20992]{0:T(1024)(128)(2,1)S(1)}, u32[]{:S(2)}, u32[]{:S(2)}) collective-permute-start(bf16[20992]{0:T(1024)(128)(2,1)S(1)} %convert_reduce_fusion.4), channel_id=1, source_target_pairs={{0,8},{4,12},{8,0},{12,4},{16,24},{20,28},{24,16},{28,20},{1,9},{5... | collective-permute-start | bytes 125960 | tf_op jit(solution)/shard_map/ppermute | solution.py:159
  71.0 0.9 collective-permute-start.7
  73.1 3.0 %collective-permute-start.16 = (bf16[10496]{0:T(1024)(128)(2,1)S(1)}, bf16[10496]{0:T(1024)(128)(2,1)S(1)}, u32[]{:S(2)}, u32[]{:S(2)}) collective-permute-start(bf16[10496]{0:T(1024)(128)(2,1)S(1)} %convert_reduce_fusion.6), channel_id=1, source_target_pairs={{0,16},{4,20},{8,24},{12,28},{16,0},{20,4},{24,8},{28,12},{1,17},{... | collective-permute-start | bytes 62984 | tf_op jit(solution)/shard_map/ppermute | solution.py:159
  76.3 0.9 %collective-permute-start.8 = (bf16[10496]{0:T(1024)(128)(2,1)S(1)}, bf16[10496]{0:T(1024)(128)(2,1)S(1)}, u32[]{:S(2)}, u32[]{:S(2)}) collective-permute-start(bf16[10496]{0:T(1024)(128)(2,1)S(1)} %convert_reduce_fusion.7), channel_id=1, source_target_pairs={{0,16},{4,20},{8,24},{12,28},{16,0},{20,4},{24,8},{28,12},{1,17},{... | collective-permute-start | bytes 62984 | tf_op jit(solution)/shard_map/ppermute | solution.py:159
  77.9 3.0 %collective-permute-start.17 = (bf16[10496]{0:T(1024)(128)(2,1)S(1)}, bf16[10496]{0:T(1024)(128)(2,1)S(1)}, u32[]{:S(2)}, u32[]{:S(2)}) collective-permute-start(bf16[10496]{0:T(1024)(128)(2,1)S(1)} %add_convert_fusion.1), channel_id=1, source_target_pairs={{0,16},{4,20},{8,24},{12,28},{16,0},{20,4},{24,8},{28,12},{1,17},{... | collective-permute-start | bytes 62984 | tf_op jit(solution)/shard_map/ppermute | solution.py:159
  80.8 0.7 collective-permute-done.8
  82.7 2.3 %collective-permute-start.18 = (bf16[20992]{0:T(1024)(128)(2,1)S(1)}, bf16[20992]{0:T(1024)(128)(2,1)S(1)}, u32[]{:S(2)}, u32[]{:S(2)}) collective-permute-start(bf16[20992]{0:T(1024)(128)(2,1)S(1)} %pad_maximum_fusion.16), channel_id=1, source_target_pairs={{0,8},{4,12},{8,0},{12,4},{16,24},{20,28},{24,16},{28,20},{1,9},{5... | collective-permute-start | bytes 125960 | tf_op jit(solution)/shard_map/ppermute | solution.py:159
  84.9 1.6 %collective-permute-done.9 = bf16[10496]{0:T(1024)(128)(2,1)S(1)} collective-permute-done((bf16[10496]{0:T(1024)(128)(2,1)S(1)}, bf16[10496]{0:T(1024)(128)(2,1)S(1)}, u32[]{:S(2)}, u32[]{:S(2)}) %collective-permute-start.9) | collective-permute-done | bytes 21024 | tf_op jit(solution)/shard_map/ppermute | solution.py:159
  87.2 3.4 %collective-permute-done.10 = bf16[20992]{0:T(1024)(128)(2,1)S(1)} collective-permute-done((bf16[20992]{0:T(1024)(128)(2,1)S(1)}, bf16[20992]{0:T(1024)(128)(2,1)S(1)}, u32[]{:S(2)}, u32[]{:S(2)}) %collective-permute-start.10) | collective-permute-done | bytes 42016 | tf_op jit(solution)/shard_map/ppermute | solution.py:159
  90.8 1.2 %collective-permute-done.11 = bf16[41984]{0:T(1024)(128)(2,1)S(1)} collective-permute-done((bf16[41984]{0:T(1024)(128)(2,1)S(1)}, bf16[41984]{0:T(1024)(128)(2,1)S(1)}, u32[]{:S(2)}, u32[]{:S(2)}) %collective-permute-start.11) | collective-permute-done | bytes 84000 | tf_op jit(solution)/shard_map/ppermute | solution.py:159
  92.2 1.0 %copy.71 = f32[4,4,64,128]{3,2,1,0:T(8,128)} copy(f32[4,4,64,128]{3,1,0,2:T(4,128)S(1)} %multiply_bitcast_fusion) | data formatting | bytes 1048576
  93.3 0.7 copy.72
  (193 shorter events, 19.7 us)
Async XLA Ops:
  0.6 2.3 %copy-start.13 = (s32[16,8,256]{2,1,0:T(8,128)S(1)}, s32[16,8,256]{2,1,0:T(8,128)}, u32[]{:S(2)}) copy-start(s32[16,8,256]{2,1,0:T(8,128)} %param.6) | copy-start | bytes 393220
  0.6 6.7 %copy-start = (bf16[4,4,256,128]{3,2,1,0:T(8,128)(2,1)S(1)}, bf16[4,4,256,128]{3,2,1,0:T(8,128)(2,1)}, u32[]{:S(2)}) copy-start(bf16[4,4,256,128]{3,2,1,0:T(8,128)(2,1)} %param.8) | copy-start | bytes 3145732
  3.2 6.4 %collective-permute-start = (bf16[12288]{0:T(1024)(128)(2,1)S(1)}, bf16[12288]{0:T(1024)(128)(2,1)S(1)}, u32[]{:S(2)}, u32[]{:S(2)}) collective-permute-start(bf16[12288]{0:T(1024)(128)(2,1)S(1)} %pad_maximum_fusion.17), channel_id=1, source_target_pairs={{0,1},{1,2},{2,3},{3,0},{4,5},{5,6},{6,7},{7,4},{8,9},{9,10},{10,1... | collective-permute-start | bytes 73736 | tf_op jit(solution)/shard_map/ppermute | solution.py:25
  6.3 3.9 %collective-permute-start.1 = (bf16[12288]{0:T(1024)(128)(2,1)S(1)}, bf16[12288]{0:T(1024)(128)(2,1)S(1)}, u32[]{:S(2)}, u32[]{:S(2)}) collective-permute-start(bf16[12288]{0:T(1024)(128)(2,1)S(1)} %pad_maximum_fusion.18), channel_id=1, source_target_pairs={{1,0},{2,1},{3,2},{0,3},{5,4},{6,5},{7,6},{4,7},{9,8},{10,9},{11,1... | collective-permute-start | bytes 73736 | tf_op jit(solution)/shard_map/ppermute | solution.py:26
  8.0 1.4 %copy-start.7 = (bf16[3,3,128,128]{3,2,1,0:T(8,128)(2,1)S(1)}, bf16[3,3,128,128]{3,2,1,0:T(8,128)(2,1)}, u32[]{:S(2)}) copy-start(bf16[3,3,128,128]{3,2,1,0:T(8,128)(2,1)} %param.10) | copy-start | bytes 884740
  8.0 1.7 %copy-start.11 = (bf16[32,16,128]{2,1,0:T(8,128)(2,1)S(1)}, bf16[32,16,128]{2,1,0:T(8,128)(2,1)}, u32[]{:S(2)}) copy-start(bf16[32,16,128]{2,1,0:T(8,128)(2,1)} %param.11) | copy-start | bytes 393220
  10.4 4.4 %collective-permute-start.2 = (bf16[7680]{0:T(1024)(128)(2,1)S(1)}, bf16[7680]{0:T(1024)(128)(2,1)S(1)}, u32[]{:S(2)}, u32[]{:S(2)}) collective-permute-start(bf16[7680]{0:T(1024)(128)(2,1)S(1)} %pad_maximum_fusion.19), channel_id=1, source_target_pairs={{4,0},{8,4},{12,8},{16,12},{20,16},{24,20},{28,24},{5,1},{9,5},{13... | collective-permute-start | bytes 46088 | tf_op jit(solution)/shard_map/ppermute | solution.py:26
  11.7 3.9 %collective-permute-start.3 = (bf16[7680]{0:T(1024)(128)(2,1)S(1)}, bf16[7680]{0:T(1024)(128)(2,1)S(1)}, u32[]{:S(2)}, u32[]{:S(2)}) collective-permute-start(bf16[7680]{0:T(1024)(128)(2,1)S(1)} %pad_maximum_fusion.20), channel_id=1, source_target_pairs={{0,4},{4,8},{8,12},{12,16},{16,20},{20,24},{24,28},{1,5},{5,9},{9,... | collective-permute-start | bytes 46088 | tf_op jit(solution)/shard_map/ppermute | solution.py:25
  19.0 0.7 copy-start.14
  27.6 1.0 %copy-start.4 = (bf16[32,16,1152]{2,1,0:T(8,128)(2,1)}, bf16[32,16,1152]{2,1,0:T(8,128)(2,1)S(1)}, u32[]{:S(2)}) copy-start(bf16[32,16,1152]{2,1,0:T(8,128)(2,1)S(1)} %slice_dynamic-update-slice_fusion.3) | copy-start | bytes 3538948
  28.9 0.8 copy-start.9
  31.6 3.1 %copy-start.5 = (bf16[32,16,1152]{2,1,0:T(8,128)(2,1)S(1)}, bf16[32,16,1152]{2,1,0:T(8,128)(2,1)}, u32[]{:S(2)}) copy-start(bf16[32,16,1152]{2,1,0:T(8,128)(2,1)} %copy-done.4) | copy-start | bytes 3538948
  31.6 3.1 %copy-start.12 = (bf16[32,16,128]{2,1,0:T(8,128)(2,1)S(1)}, bf16[32,16,128]{2,1,0:T(8,128)(2,1)}, u32[]{:S(2)}) copy-start(bf16[32,16,128]{2,1,0:T(8,128)(2,1)} %param.11) | copy-start | bytes 393220
  41.7 2.0 %copy-start.2 = (f32[2,2,83968]{2,1,0:T(2,128)}, f32[2,2,83968]{2,1,0:T(2,128)S(1)}, u32[]{:S(2)}) copy-start(f32[2,2,83968]{2,1,0:T(2,128)S(1)} %reshape.207) | copy-start | bytes 4030468
  41.9 10.5 %collective-permute-start.12 = (bf16[2,83968]{1,0:T(2,128)(2,1)S(1)}, bf16[2,83968]{1,0:T(2,128)(2,1)S(1)}, u32[]{:S(2)}, u32[]{:S(2)}) collective-permute-start(bf16[2,83968]{1,0:T(2,128)(2,1)S(1)} %fusion.11), channel_id=1, source_target_pairs={{0,2},{1,3},{2,0},{3,1},{4,6},{5,7},{6,4},{7,5},{8,10},{9,11},{10,... | collective-permute-start | bytes 1007624 | tf_op jit(solution)/shard_map/ppermute | solution.py:159
  44.7 1.4 %copy-start.6 = (bf16[32,16,1152]{2,1,0:T(8,128)(2,1)S(1)}, bf16[32,16,1152]{2,1,0:T(8,128)(2,1)}, u32[]{:S(2)}) copy-start(bf16[32,16,1152]{2,1,0:T(8,128)(2,1)} %copy-done.4) | copy-start | bytes 3538948
  44.7 1.4 %copy-start.8 = (bf16[3,3,128,128]{3,2,1,0:T(8,128)(2,1)S(1)}, bf16[3,3,128,128]{3,2,1,0:T(8,128)(2,1)}, u32[]{:S(2)}) copy-start(bf16[3,3,128,128]{3,2,1,0:T(8,128)(2,1)} %param.10) | copy-start | bytes 884740
  46.0 3.1 %copy-start.1 = (bf16[4,4,256,128]{2,3,1,0:T(8,128)(2,1)S(1)}, bf16[4,4,256,128]{2,3,1,0:T(8,128)(2,1)}, u32[]{:S(2)}) copy-start(bf16[4,4,256,128]{2,3,1,0:T(8,128)(2,1)} %copy.67) | copy-start | bytes 3145732
  46.0 3.1 %copy-start.10 = (bf16[16,8,2048]{2,1,0:T(8,128)(2,1)S(1)}, bf16[16,8,2048]{2,1,0:T(8,128)(2,1)}, u32[]{:S(2)}) copy-start(bf16[16,8,2048]{2,1,0:T(8,128)(2,1)} %copy-done.9) | copy-start | bytes 1572868
  47.2 5.3 %copy-start.3 = (f32[2,2,83968]{2,1,0:T(2,128)S(1)}, f32[2,2,83968]{2,1,0:T(2,128)}, u32[]{:S(2)}) copy-start(f32[2,2,83968]{2,1,0:T(2,128)} %copy-done.2) | copy-start | bytes 4030468
  47.6 10.8 %collective-permute-start.4 = (bf16[2,83968]{1,0:T(2,128)(2,1)S(1)}, bf16[2,83968]{1,0:T(2,128)(2,1)S(1)}, u32[]{:S(2)}, u32[]{:S(2)}) collective-permute-start(bf16[2,83968]{1,0:T(2,128)(2,1)S(1)} %bitcast.137), channel_id=1, source_target_pairs={{0,1},{1,0},{2,3},{3,2},{4,5},{5,4},{6,7},{7,6},{8,9},{9,8},{10,11... | collective-permute-start | bytes 1007624 | tf_op jit(solution)/shard_map/ppermute | solution.py:159
  54.1 7.8 %collective-permute-start.13 = (bf16[83968]{0:T(1024)(128)(2,1)S(1)}, bf16[83968]{0:T(1024)(128)(2,1)S(1)}, u32[]{:S(2)}, u32[]{:S(2)}) collective-permute-start(bf16[83968]{0:T(1024)(128)(2,1)S(1)} %convert_reduce_fusion), channel_id=1, source_target_pairs={{0,1},{1,0},{2,3},{3,2},{4,5},{5,4},{6,7},{7,6},{8,9},{9,8},{10,11... | collective-permute-start | bytes 503816 | tf_op jit(solution)/shard_map/ppermute | solution.py:159
  60.3 6.5 %collective-permute-start.5 = (bf16[83968]{0:T(1024)(128)(2,1)S(1)}, bf16[83968]{0:T(1024)(128)(2,1)S(1)}, u32[]{:S(2)}, u32[]{:S(2)}) collective-permute-start(bf16[83968]{0:T(1024)(128)(2,1)S(1)} %convert_reduce_fusion.1), channel_id=1, source_target_pairs={{0,2},{1,3},{2,0},{3,1},{4,6},{5,7},{6,4},{7,5},{8,10},{9,11},{10,... | collective-permute-start | bytes 503816 | tf_op jit(solution)/shard_map/ppermute | solution.py:159
  62.8 4.9 %collective-permute-start.14 = (bf16[41984]{0:T(1024)(128)(2,1)S(1)}, bf16[41984]{0:T(1024)(128)(2,1)S(1)}, u32[]{:S(2)}, u32[]{:S(2)}) collective-permute-start(bf16[41984]{0:T(1024)(128)(2,1)S(1)} %convert_reduce_fusion.2), channel_id=1, source_target_pairs={{0,4},{4,0},{8,12},{12,8},{16,20},{20,16},{24,28},{28,24},{1,5},{5... | collective-permute-start | bytes 251912 | tf_op jit(solution)/shard_map/ppermute | solution.py:159
  67.7 3.0 %collective-permute-start.6 = (bf16[41984]{0:T(1024)(128)(2,1)S(1)}, bf16[41984]{0:T(1024)(128)(2,1)S(1)}, u32[]{:S(2)}, u32[]{:S(2)}) collective-permute-start(bf16[41984]{0:T(1024)(128)(2,1)S(1)} %convert_reduce_fusion.3), channel_id=1, source_target_pairs={{0,4},{4,0},{8,12},{12,8},{16,20},{20,16},{24,28},{28,24},{1,5},{5... | collective-permute-start | bytes 251912 | tf_op jit(solution)/shard_map/ppermute | solution.py:159
  68.1 4.8 %collective-permute-start.15 = (bf16[20992]{0:T(1024)(128)(2,1)S(1)}, bf16[20992]{0:T(1024)(128)(2,1)S(1)}, u32[]{:S(2)}, u32[]{:S(2)}) collective-permute-start(bf16[20992]{0:T(1024)(128)(2,1)S(1)} %convert_reduce_fusion.4), channel_id=1, source_target_pairs={{0,8},{4,12},{8,0},{12,4},{16,24},{20,28},{24,16},{28,20},{1,9},{5... | collective-permute-start | bytes 125960 | tf_op jit(solution)/shard_map/ppermute | solution.py:159
  71.0 5.0 %collective-permute-start.7 = (bf16[20992]{0:T(1024)(128)(2,1)S(1)}, bf16[20992]{0:T(1024)(128)(2,1)S(1)}, u32[]{:S(2)}, u32[]{:S(2)}) collective-permute-start(bf16[20992]{0:T(1024)(128)(2,1)S(1)} %convert_reduce_fusion.5), channel_id=1, source_target_pairs={{0,8},{4,12},{8,0},{12,4},{16,24},{20,28},{24,16},{28,20},{1,9},{5... | collective-permute-start | bytes 125960 | tf_op jit(solution)/shard_map/ppermute | solution.py:159
  73.1 4.8 %collective-permute-start.16 = (bf16[10496]{0:T(1024)(128)(2,1)S(1)}, bf16[10496]{0:T(1024)(128)(2,1)S(1)}, u32[]{:S(2)}, u32[]{:S(2)}) collective-permute-start(bf16[10496]{0:T(1024)(128)(2,1)S(1)} %convert_reduce_fusion.6), channel_id=1, source_target_pairs={{0,16},{4,20},{8,24},{12,28},{16,0},{20,4},{24,8},{28,12},{1,17},{... | collective-permute-start | bytes 62984 | tf_op jit(solution)/shard_map/ppermute | solution.py:159
  76.3 5.3 %collective-permute-start.8 = (bf16[10496]{0:T(1024)(128)(2,1)S(1)}, bf16[10496]{0:T(1024)(128)(2,1)S(1)}, u32[]{:S(2)}, u32[]{:S(2)}) collective-permute-start(bf16[10496]{0:T(1024)(128)(2,1)S(1)} %convert_reduce_fusion.7), channel_id=1, source_target_pairs={{0,16},{4,20},{8,24},{12,28},{16,0},{20,4},{24,8},{28,12},{1,17},{... | collective-permute-start | bytes 62984 | tf_op jit(solution)/shard_map/ppermute | solution.py:159
  77.9 4.8 %collective-permute-start.17 = (bf16[10496]{0:T(1024)(128)(2,1)S(1)}, bf16[10496]{0:T(1024)(128)(2,1)S(1)}, u32[]{:S(2)}, u32[]{:S(2)}) collective-permute-start(bf16[10496]{0:T(1024)(128)(2,1)S(1)} %add_convert_fusion.1), channel_id=1, source_target_pairs={{0,16},{4,20},{8,24},{12,28},{16,0},{20,4},{24,8},{28,12},{1,17},{... | collective-permute-start | bytes 62984 | tf_op jit(solution)/shard_map/ppermute | solution.py:159
  81.5 4.9 %collective-permute-start.9 = (bf16[10496]{0:T(1024)(128)(2,1)S(1)}, bf16[10496]{0:T(1024)(128)(2,1)S(1)}, u32[]{:S(2)}, u32[]{:S(2)}) collective-permute-start(bf16[10496]{0:T(1024)(128)(2,1)S(1)} %add_convert_fusion.2), channel_id=1, source_target_pairs={{0,16},{4,20},{8,24},{12,28},{16,0},{20,4},{24,8},{28,12},{1,17},{... | collective-permute-start | bytes 62984 | tf_op jit(solution)/shard_map/ppermute | solution.py:159
  82.7 4.4 %collective-permute-start.18 = (bf16[20992]{0:T(1024)(128)(2,1)S(1)}, bf16[20992]{0:T(1024)(128)(2,1)S(1)}, u32[]{:S(2)}, u32[]{:S(2)}) collective-permute-start(bf16[20992]{0:T(1024)(128)(2,1)S(1)} %pad_maximum_fusion.16), channel_id=1, source_target_pairs={{0,8},{4,12},{8,0},{12,4},{16,24},{20,28},{24,16},{28,20},{1,9},{5... | collective-permute-start | bytes 125960 | tf_op jit(solution)/shard_map/ppermute | solution.py:159
  86.5 4.1 %collective-permute-start.10 = (bf16[20992]{0:T(1024)(128)(2,1)S(1)}, bf16[20992]{0:T(1024)(128)(2,1)S(1)}, u32[]{:S(2)}, u32[]{:S(2)}) collective-permute-start(bf16[20992]{0:T(1024)(128)(2,1)S(1)} %pad_maximum_fusion.15), channel_id=1, source_target_pairs={{0,8},{4,12},{8,0},{12,4},{16,24},{20,28},{24,16},{28,20},{1,9},{5... | collective-permute-start | bytes 125960 | tf_op jit(solution)/shard_map/ppermute | solution.py:159
  87.1 3.6 %collective-permute-start.19 = (bf16[41984]{0:T(1024)(128)(2,1)S(1)}, bf16[41984]{0:T(1024)(128)(2,1)S(1)}, u32[]{:S(2)}, u32[]{:S(2)}) collective-permute-start(bf16[41984]{0:T(1024)(128)(2,1)S(1)} %pad_maximum_fusion.11), channel_id=1, source_target_pairs={{0,4},{4,0},{8,12},{12,8},{16,20},{20,16},{24,28},{28,24},{1,5},{5... | collective-permute-start | bytes 251912 | tf_op jit(solution)/shard_map/ppermute | solution.py:159
  90.7 1.3 %collective-permute-start.11 = (bf16[41984]{0:T(1024)(128)(2,1)S(1)}, bf16[41984]{0:T(1024)(128)(2,1)S(1)}, u32[]{:S(2)}, u32[]{:S(2)}) collective-permute-start(bf16[41984]{0:T(1024)(128)(2,1)S(1)} %pad_maximum_fusion.10), channel_id=1, source_target_pairs={{0,4},{4,0},{8,12},{12,8},{16,20},{20,16},{24,28},{28,24},{1,5},{5... | collective-permute-start | bytes 251912 | tf_op jit(solution)/shard_map/ppermute | solution.py:159

commit v5 on v4

--- a/solution.py
+++ b/solution.py
@@ -194,14 +194,13 @@
 
 def reduce_lat(flat):
     steps = steps_of(lax.axis_size("lat"))
-    if steps is None or flat.shape[0] % (1 << len(steps)):
+    if steps is None or flat.shape[0] % 2:
         return lax.psum(flat, "lat")
-    for step in steps:
-        flat = halve(flat.reshape(2, -1), "lat", step, 0)
-    flat = flat.astype(jnp.bfloat16)
-    for step in reversed(steps):
-        flat = double(flat, "lat", step)
-    return flat.astype(jnp.float32)
+    part = halve(flat.reshape(2, -1), "lat", steps[0], 0).astype(jnp.bfloat16)
+    for step in steps[1:]:
+        got = exchange(part, "lat", step)
+        part = (part.astype(jnp.float32) + got.astype(jnp.float32)).astype(jnp.bfloat16)
+    return double(part, "lat", steps[0]).astype(jnp.float32)
 
 
 def reduce_terms(rows):

time: 94.3 us -> 87.8 us (0.931)
  starting transfers between devices: 28.8 us -> 23.4 us
  local copies, waits for them, and re-layouts: 32.2 us -> 30.3 us
    ppermute x16 -> x12, starting transfers between devices: 20.4 us -> 15 us  [exchange(): return lax.ppermute(part, axis, [(i, i ^ step) for i in range(size)])]
    ppermute x16 -> x12, waiting for transfers between devices: 17.1 us -> 18 us  [exchange(): return lax.ppermute(part, axis, [(i, i ^ step) for i in range(size)])]
    convert_element_type x10 -> x6, local copies, waits for them, and re-layouts: 4.76 us -> 3.99 us  [halve(): send.astype(jnp.bfloat16)]
    dynamic_slice x9 -> x5, local copies, waits for them, and re-layouts: 2.31 us -> 1.58 us  [halve(): keep = lax.dynamic_index_in_dim(buffer, own, dim, keepdims=False)]
  transfers between devices with their start and end apart: 20 -> 16, of which waited for: 13 -> 10; matrix products, arithmetic and copies ran while one was open for 16% -> 15% of each run, Pallas kernels for 0% -> 0%
where the time goes in v5:
time: 87.8 us; the launch traced here: 87.4 us
  local copies, waits for them, and re-layouts  30.3 us (35%)
  starting transfers between devices  23.4 us (27%)
  waiting for transfers between devices  19 us (22%)
  matrix products  7.19 us (8%)
  other arithmetic  5.77 us (7%)
  between operations  1.68 us (2%)
    ppermute x12, waiting for transfers between devices, exchange(): return lax.ppermute(part, axis, [(i, i ^ step) for i in range(size)])  18 us
    ppermute x12, starting transfers between devices, exchange(): return lax.ppermute(part, axis, [(i, i ^ step) for i in range(size)])  15 us
    slice x16, local copies, waits for them, and re-layouts, strided(): padded[row_tap:row_tap + 2 * row_count:2, col_tap:col_tap + 2 * col_count:2]  7.14 us
    unnamed x66, local copies, waits for them, and re-layouts  6.27 us
    ppermute x2, starting transfers between devices, swap_edges(): lax.ppermute(jnp.concatenate([p.reshape(-1) for p in lasts]), axis, up)  6.02 us
    convert_element_type x6, local copies, waits for them, and re-layouts, halve(): send.astype(jnp.bfloat16)  3.99 us
    reshape x2, local copies, waits for them, and re-layouts, scatter_lon(): grid = rows.reshape((2,) * width + rows.shape[1:])  3.4 us
    reshape x1, local copies, waits for them, and re-layouts, shards(): up_flat.reshape(lon_count, up_size)  3.12 us
  transfers between devices with their start and end apart: 16, of which 10 were waited for; matrix products, arithmetic and copies ran while one was open for 15% of the time, Pallas kernels for 0%

profile of v5, /device:TPU:0, one launch (start us, length us, event | category | flops | bytes accessed | tf_op | source)
XLA Modules:
  0.0 87.4 jit_solution(16229724820446879805)
XLA Ops:
  0.7 1.0 %fusion.70 = (bf16[32,2,128]{2,1,0:T(2,128)(2,1)S(1)}, bf16[32,2,128]{2,1,0:T(2,128)(2,1)S(1)}) fusion(bf16[32,16,128]{2,1,0:T(8,128)(2,1)} %param.11), kind=kLoop, calls=%fused_computation.209 | loop fusion | bytes 65536 | tf_op jit(solution)/shard_map/slice | solution.py:23
  1.7 0.8 multiply_exponential_fusion
  3.2 3.0 %collective-permute-start = (bf16[12288]{0:T(1024)(128)(2,1)S(1)}, bf16[12288]{0:T(1024)(128)(2,1)S(1)}, u32[]{:S(2)}, u32[]{:S(2)}) collective-permute-start(bf16[12288]{0:T(1024)(128)(2,1)S(1)} %pad_maximum_fusion.13), channel_id=1, source_target_pairs={{0,1},{1,2},{2,3},{3,0},{4,5},{5,6},{6,7},{7,4},{8,9},{9,10},{10,1... | collective-permute-start | bytes 73736 | tf_op jit(solution)/shard_map/ppermute | solution.py:25
  6.3 1.0 %collective-permute-start.1 = (bf16[12288]{0:T(1024)(128)(2,1)S(1)}, bf16[12288]{0:T(1024)(128)(2,1)S(1)}, u32[]{:S(2)}, u32[]{:S(2)}) collective-permute-start(bf16[12288]{0:T(1024)(128)(2,1)S(1)} %pad_maximum_fusion.14), channel_id=1, source_target_pairs={{1,0},{2,1},{3,2},{0,3},{5,4},{6,5},{7,6},{4,7},{9,8},{10,9},{11,1... | collective-permute-start | bytes 73736 | tf_op jit(solution)/shard_map/ppermute | solution.py:26
  7.3 0.7 slice_bitcast_fusion.15
  8.0 1.3 %copy.67 = bf16[4,4,256,128]{2,3,1,0:T(8,128)(2,1)} copy(bf16[4,4,256,128]{3,2,1,0:T(8,128)(2,1)S(1)} %copy-done) | data formatting | bytes 2097152 | tf_op args[2]
  10.4 1.3 %collective-permute-start.2 = (bf16[7680]{0:T(1024)(128)(2,1)S(1)}, bf16[7680]{0:T(1024)(128)(2,1)S(1)}, u32[]{:S(2)}, u32[]{:S(2)}) collective-permute-start(bf16[7680]{0:T(1024)(128)(2,1)S(1)} %pad_maximum_fusion.15), channel_id=1, source_target_pairs={{4,0},{8,4},{12,8},{16,12},{20,16},{24,20},{28,24},{5,1},{9,5},{13... | collective-permute-start | bytes 46088 | tf_op jit(solution)/shard_map/ppermute | solution.py:26
  11.7 3.0 %collective-permute-start.3 = (bf16[7680]{0:T(1024)(128)(2,1)S(1)}, bf16[7680]{0:T(1024)(128)(2,1)S(1)}, u32[]{:S(2)}, u32[]{:S(2)}) collective-permute-start(bf16[7680]{0:T(1024)(128)(2,1)S(1)} %pad_maximum_fusion.16), channel_id=1, source_target_pairs={{0,4},{4,8},{8,12},{12,16},{16,20},{20,24},{24,28},{1,5},{5,9},{9,... | collective-permute-start | bytes 46088 | tf_op jit(solution)/shard_map/ppermute | solution.py:25
  15.0 0.6 collective-permute-done.3
  16.4 1.2 %convolution_bitcast_fusion.2 = f32[17,9,1,128]{3,0,1,2:T(8,128)S(1)} fusion(bf16[256,128]{1,0:T(8,128)(2,1)} %get-tuple-element.31, bf16[256,128]{1,0:T(8,128)(2,1)S(1)} %get-tuple-element.17, bf16[256,128]{1,0:T(8,128)(2,1)} %get-tuple-element.18, bf16[256,128]{1,0:T(8,128)(2,1)} %get-tuple-element.19, bf16[17,9,256]{2,0,1:T(8,128)(2,1)S(1)} %get-tuple-element.50, ...), kind=kOutput, calls=%fused_computation.6 | convolution fusion | flops 42409984 | bytes 653824 | tf_op jit(solution)/shard_map/rck,kn->rcn/dot_general | solution.py:78
  19.0 0.6 fusion.73
  24.2 0.6 slice.399
  24.9 0.6 slice.400
  25.5 0.7 slice.401
  26.2 0.9 %slice.402 = bf16[16,8,128]{2,1,0:T(8,128)(2,1)S(1)} slice(bf16[34,18,128]{2,1,0:T(8,128)(2,1)S(1)} %get-tuple-element.32), slice={[3:34:2], [3:18:2], [0:128:1]} | slice | bytes 65536 | tf_op jit(solution)/shard_map/slice | solution.py:100
  27.7 1.0 %copy-done.4 = bf16[32,16,1152]{2,1,0:T(8,128)(2,1)} copy-done((bf16[32,16,1152]{2,1,0:T(8,128)(2,1)}, bf16[32,16,1152]{2,1,0:T(8,128)(2,1)S(1)}, u32[]{:S(2)}) %copy-start.4) | copy-done | bytes 1179672
  29.0 0.8 copy-done.9
  29.7 1.9 %convolution_bitcast_fusion = f32[256,2048]{1,0:T(8,128)} fusion(bf16[16,8,256]{2,0,1:T(8,128)(2,1)S(1)} %fusion.60, bf16[16,8,2048]{2,1,0:T(8,128)(2,1)S(1)} %constant_dynamic-update-slice_fusion.2), kind=kOutput, calls=%fused_computation | convolution fusion | flops 134217728 | bytes 2686976 | tf_op jit(solution)/shard_map/rcm,rck->mk/dot_general | solution.py:144
  31.6 3.1 %reshape.184 = f32[4,131072]{1,0:T(4,128)S(1)} reshape(f32[256,2048]{1,0:T(8,128)} %convolution_bitcast_fusion) | data formatting | bytes 4194304 | tf_op jit(solution)/shard_map/reshape | solution.py:149
  34.8 0.5 convolution_bitcast_fusion.1
  35.7 1.1 %reshape.188 = f32[4,36864]{1,0:T(4,128)} reshape(f32[128,9,128]{2,1,0:T(8,128)S(1)} %copy.70) | data formatting | bytes 1179648 | tf_op jit(solution)/shard_map/reshape | solution.py:149
  36.8 2.5 %fusion.68 = (f32[4,83968]{1,0:T(4,128)S(1)}, f32[4,83968]{1,0:T(4,128)}) fusion(f32[4,131072]{1,0:T(4,128)S(1)} %reshape.184, f32[4,36864]{1,0:T(4,128)} %reshape.188), kind=kLoop, calls=%fused_computation.207 | loop fusion | flops 335872 | bytes 6717440 | tf_op jit(solution)/shard_map/slice | solution.py:214
  39.3 2.4 %reshape.189 = f32[2,2,83968]{2,1,0:T(2,128)S(1)} reshape(f32[4,83968]{1,0:T(4,128)} %get-tuple-element.15) | data formatting | bytes 2686976 | tf_op jit(solution)/shard_map/reshape | solution.py:186
  41.9 1.6 %collective-permute-start.10 = (bf16[2,83968]{1,0:T(2,128)(2,1)S(1)}, bf16[2,83968]{1,0:T(2,128)(2,1)S(1)}, u32[]{:S(2)}, u32[]{:S(2)}) collective-permute-start(bf16[2,83968]{1,0:T(2,128)(2,1)S(1)} %fusion.11), channel_id=1, source_target_pairs={{0,2},{1,3},{2,0},{3,1},{4,6},{5,7},{6,4},{7,5},{8,10},{9,11},{10,... | collective-permute-start | bytes 1007624 | tf_op jit(solution)/shard_map/ppermute | solution.py:159
  43.5 1.0 %reshape.185 = f32[2,2,83968]{2,1,0:T(2,128)S(1)} reshape(f32[4,83968]{1,0:T(4,128)S(1)} %get-tuple-element.14) | data formatting | bytes 2686976 | tf_op jit(solution)/shard_map/reshape | solution.py:186
  44.6 0.7 constant_dynamic-slice_fusion.4
  45.3 0.6 dynamic-slice_convert_fusion.1
  45.9 1.1 %convolution_convert_fusion = bf16[32,16,128]{2,1,0:T(8,128)(2,1)} fusion(bf16[32,16,1152]{2,1,0:T(8,128)(2,1)S(1)} %copy-done.6, bf16[1152,128,1]{1,0,2:T(8,128)(2,1)S(1)} %bitcast.131), kind=kOutput, calls=%fused_computation.5 | convolution fusion | flops 151060480 | bytes 1605632 | tf_op jit(solution)/shard_map/rck,kn->rcn/dot_general | solution.py:129
  47.4 1.6 %collective-permute-start.4 = (bf16[2,83968]{1,0:T(2,128)(2,1)S(1)}, bf16[2,83968]{1,0:T(2,128)(2,1)S(1)}, u32[]{:S(2)}, u32[]{:S(2)}) collective-permute-start(bf16[2,83968]{1,0:T(2,128)(2,1)S(1)} %bitcast.137), channel_id=1, source_target_pairs={{0,1},{1,0},{2,3},{3,2},{4,5},{5,4},{6,7},{7,6},{8,9},{9,8},{10,11... | collective-permute-start | bytes 1007624 | tf_op jit(solution)/shard_map/ppermute | solution.py:159
  49.1 1.0 %fusion.74 = f32[16,8,256]{2,1,0:T(8,128)} fusion(bf16[16,8,2048]{2,1,0:T(8,128)(2,1)S(1)} %copy-done.10, bf16[2048,256,1]{1,0,2:T(8,128)(2,1)S(1)} %bitcast.127), kind=kOutput, calls=%fused_computation.213 | convolution fusion | flops 134217728 | bytes 1703936 | tf_op jit(solution)/shard_map/rck,kn->rcn/dot_general | solution.py:141
  50.0 2.3 %collective-permute-done.10 = bf16[2,83968]{1,0:T(2,128)(2,1)S(1)} collective-permute-done((bf16[2,83968]{1,0:T(2,128)(2,1)S(1)}, bf16[2,83968]{1,0:T(2,128)(2,1)S(1)}, u32[]{:S(2)}, u32[]{:S(2)}) %collective-permute-start.10) | collective-permute-done | bytes 335904 | tf_op jit(solution)/shard_map/ppermute | solution.py:159
  53.1 1.0 %convert_reduce_fusion = bf16[83968]{0:T(1024)(128)(2,1)S(1)} fusion(f32[2,83968]{1,0:T(2,128)S(1)} %bitcast_add_fusion.1, s32[]{:T(128)S(6)} %select_n.124), kind=kLoop, calls=%fused_computation.33 | loop fusion | bytes 335876 | tf_op jit(solution)/shard_map/convert_element_type | solution.py:166
  54.0 2.5 %collective-permute-start.11 = (bf16[83968]{0:T(1024)(128)(2,1)S(1)}, bf16[83968]{0:T(1024)(128)(2,1)S(1)}, u32[]{:S(2)}, u32[]{:S(2)}) collective-permute-start(bf16[83968]{0:T(1024)(128)(2,1)S(1)} %convert_reduce_fusion), channel_id=1, source_target_pairs={{0,1},{1,0},{2,3},{3,2},{4,5},{5,4},{6,7},{7,6},{8,9},{9,8},{10,11... | collective-permute-start | bytes 503816 | tf_op jit(solution)/shard_map/ppermute | solution.py:159
  56.6 1.6 %collective-permute-done.4 = bf16[2,83968]{1,0:T(2,128)(2,1)S(1)} collective-permute-done((bf16[2,83968]{1,0:T(2,128)(2,1)S(1)}, bf16[2,83968]{1,0:T(2,128)(2,1)S(1)}, u32[]{:S(2)}, u32[]{:S(2)}) %collective-permute-start.4) | collective-permute-done | bytes 335904 | tf_op jit(solution)/shard_map/ppermute | solution.py:159
  58.9 1.2 %convert_reduce_fusion.1 = bf16[83968]{0:T(1024)(128)(2,1)S(1)} fusion(f32[2,83968]{1,0:T(2,128)S(1)} %bitcast_add_fusion, s32[]{:T(128)S(6)} %select_n.128), kind=kLoop, calls=%fused_computation.35 | loop fusion | bytes 335876 | tf_op jit(solution)/shard_map/convert_element_type | solution.py:166
  60.1 0.7 collective-permute-start.5
  60.8 0.9 %collective-permute-done.11 = bf16[83968]{0:T(1024)(128)(2,1)S(1)} collective-permute-done((bf16[83968]{0:T(1024)(128)(2,1)S(1)}, bf16[83968]{0:T(1024)(128)(2,1)S(1)}, u32[]{:S(2)}, u32[]{:S(2)}) %collective-permute-start.11) | collective-permute-done | bytes 167968 | tf_op jit(solution)/shard_map/ppermute | solution.py:159
  62.8 3.9 %collective-permute-done.5 = bf16[83968]{0:T(1024)(128)(2,1)S(1)} collective-permute-done((bf16[83968]{0:T(1024)(128)(2,1)S(1)}, bf16[83968]{0:T(1024)(128)(2,1)S(1)}, u32[]{:S(2)}, u32[]{:S(2)}) %collective-permute-start.5) | collective-permute-done | bytes 167968 | tf_op jit(solution)/shard_map/ppermute | solution.py:159
  67.7 2.5 %collective-permute-start.13 = (bf16[41984]{0:T(1024)(128)(2,1)S(1)}, bf16[41984]{0:T(1024)(128)(2,1)S(1)}, u32[]{:S(2)}, u32[]{:S(2)}) collective-permute-start(bf16[41984]{0:T(1024)(128)(2,1)S(1)} %add_convert_fusion.3), channel_id=1, source_target_pairs={{0,8},{4,12},{8,0},{12,4},{16,24},{20,28},{24,16},{28,20},{1,9},{5... | collective-permute-start | bytes 251912 | tf_op jit(solution)/shard_map/ppermute | solution.py:159
  70.2 1.2 %collective-permute-start.7 = (bf16[41984]{0:T(1024)(128)(2,1)S(1)}, bf16[41984]{0:T(1024)(128)(2,1)S(1)}, u32[]{:S(2)}, u32[]{:S(2)}) collective-permute-start(bf16[41984]{0:T(1024)(128)(2,1)S(1)} %add_convert_fusion.6), channel_id=1, source_target_pairs={{0,8},{4,12},{8,0},{12,4},{16,24},{20,28},{24,16},{28,20},{1,9},{5... | collective-permute-start | bytes 251912 | tf_op jit(solution)/shard_map/ppermute | solution.py:159
  71.5 2.1 %collective-permute-done.13 = bf16[41984]{0:T(1024)(128)(2,1)S(1)} collective-permute-done((bf16[41984]{0:T(1024)(128)(2,1)S(1)}, bf16[41984]{0:T(1024)(128)(2,1)S(1)}, u32[]{:S(2)}, u32[]{:S(2)}) %collective-permute-start.13) | collective-permute-done | bytes 84000 | tf_op jit(solution)/shard_map/ppermute | solution.py:159
  73.6 3.0 %collective-permute-start.14 = (bf16[41984]{0:T(1024)(128)(2,1)S(1)}, bf16[41984]{0:T(1024)(128)(2,1)S(1)}, u32[]{:S(2)}, u32[]{:S(2)}) collective-permute-start(bf16[41984]{0:T(1024)(128)(2,1)S(1)} %add_convert_fusion.2), channel_id=1, source_target_pairs={{0,16},{4,20},{8,24},{12,28},{16,0},{20,4},{24,8},{28,12},{1,17},{... | collective-permute-start | bytes 251912 | tf_op jit(solution)/shard_map/ppermute | solution.py:159
  76.6 1.4 %collective-permute-start.8 = (bf16[41984]{0:T(1024)(128)(2,1)S(1)}, bf16[41984]{0:T(1024)(128)(2,1)S(1)}, u32[]{:S(2)}, u32[]{:S(2)}) collective-permute-start(bf16[41984]{0:T(1024)(128)(2,1)S(1)} %add_convert_fusion.5), channel_id=1, source_target_pairs={{0,16},{4,20},{8,24},{12,28},{16,0},{20,4},{24,8},{28,12},{1,17},{... | collective-permute-start | bytes 251912 | tf_op jit(solution)/shard_map/ppermute | solution.py:159
  78.0 4.7 %collective-permute-done.14 = bf16[41984]{0:T(1024)(128)(2,1)S(1)} collective-permute-done((bf16[41984]{0:T(1024)(128)(2,1)S(1)}, bf16[41984]{0:T(1024)(128)(2,1)S(1)}, u32[]{:S(2)}, u32[]{:S(2)}) %collective-permute-start.14) | collective-permute-done | bytes 84000 | tf_op jit(solution)/shard_map/ppermute | solution.py:159
  82.8 1.3 %collective-permute-done.8 = bf16[41984]{0:T(1024)(128)(2,1)S(1)} collective-permute-done((bf16[41984]{0:T(1024)(128)(2,1)S(1)}, bf16[41984]{0:T(1024)(128)(2,1)S(1)}, u32[]{:S(2)}, u32[]{:S(2)}) %collective-permute-start.8) | collective-permute-done | bytes 84000 | tf_op jit(solution)/shard_map/ppermute | solution.py:159
  84.3 1.2 %collective-permute-done.9 = bf16[41984]{0:T(1024)(128)(2,1)S(1)} collective-permute-done((bf16[41984]{0:T(1024)(128)(2,1)S(1)}, bf16[41984]{0:T(1024)(128)(2,1)S(1)}, u32[]{:S(2)}, u32[]{:S(2)}) %collective-permute-start.9) | collective-permute-done | bytes 84000 | tf_op jit(solution)/shard_map/ppermute | solution.py:159
  85.7 1.0 %copy.71 = f32[4,4,64,128]{3,2,1,0:T(8,128)} copy(f32[4,4,64,128]{3,1,0,2:T(4,128)S(1)} %multiply_bitcast_fusion) | data formatting | bytes 1048576
  86.7 0.7 copy.72
  (165 shorter events, 14.1 us)
Async XLA Ops:
  0.6 2.3 %copy-start.13 = (s32[16,8,256]{2,1,0:T(8,128)S(1)}, s32[16,8,256]{2,1,0:T(8,128)}, u32[]{:S(2)}) copy-start(s32[16,8,256]{2,1,0:T(8,128)} %param.6) | copy-start | bytes 393220
  0.6 6.7 %copy-start = (bf16[4,4,256,128]{3,2,1,0:T(8,128)(2,1)S(1)}, bf16[4,4,256,128]{3,2,1,0:T(8,128)(2,1)}, u32[]{:S(2)}) copy-start(bf16[4,4,256,128]{3,2,1,0:T(8,128)(2,1)} %param.8) | copy-start | bytes 3145732
  3.2 6.4 %collective-permute-start = (bf16[12288]{0:T(1024)(128)(2,1)S(1)}, bf16[12288]{0:T(1024)(128)(2,1)S(1)}, u32[]{:S(2)}, u32[]{:S(2)}) collective-permute-start(bf16[12288]{0:T(1024)(128)(2,1)S(1)} %pad_maximum_fusion.13), channel_id=1, source_target_pairs={{0,1},{1,2},{2,3},{3,0},{4,5},{5,6},{6,7},{7,4},{8,9},{9,10},{10,1... | collective-permute-start | bytes 73736 | tf_op jit(solution)/shard_map/ppermute | solution.py:25
  6.3 3.9 %collective-permute-start.1 = (bf16[12288]{0:T(1024)(128)(2,1)S(1)}, bf16[12288]{0:T(1024)(128)(2,1)S(1)}, u32[]{:S(2)}, u32[]{:S(2)}) collective-permute-start(bf16[12288]{0:T(1024)(128)(2,1)S(1)} %pad_maximum_fusion.14), channel_id=1, source_target_pairs={{1,0},{2,1},{3,2},{0,3},{5,4},{6,5},{7,6},{4,7},{9,8},{10,9},{11,1... | collective-permute-start | bytes 73736 | tf_op jit(solution)/shard_map/ppermute | solution.py:26
  8.0 1.3 %copy-start.7 = (bf16[3,3,128,128]{3,2,1,0:T(8,128)(2,1)S(1)}, bf16[3,3,128,128]{3,2,1,0:T(8,128)(2,1)}, u32[]{:S(2)}) copy-start(bf16[3,3,128,128]{3,2,1,0:T(8,128)(2,1)} %param.10) | copy-start | bytes 884740
  8.0 1.6 %copy-start.11 = (bf16[32,16,128]{2,1,0:T(8,128)(2,1)S(1)}, bf16[32,16,128]{2,1,0:T(8,128)(2,1)}, u32[]{:S(2)}) copy-start(bf16[32,16,128]{2,1,0:T(8,128)(2,1)} %param.11) | copy-start | bytes 393220
  10.4 4.4 %collective-permute-start.2 = (bf16[7680]{0:T(1024)(128)(2,1)S(1)}, bf16[7680]{0:T(1024)(128)(2,1)S(1)}, u32[]{:S(2)}, u32[]{:S(2)}) collective-permute-start(bf16[7680]{0:T(1024)(128)(2,1)S(1)} %pad_maximum_fusion.15), channel_id=1, source_target_pairs={{4,0},{8,4},{12,8},{16,12},{20,16},{24,20},{28,24},{5,1},{9,5},{13... | collective-permute-start | bytes 46088 | tf_op jit(solution)/shard_map/ppermute | solution.py:26
  11.7 3.9 %collective-permute-start.3 = (bf16[7680]{0:T(1024)(128)(2,1)S(1)}, bf16[7680]{0:T(1024)(128)(2,1)S(1)}, u32[]{:S(2)}, u32[]{:S(2)}) collective-permute-start(bf16[7680]{0:T(1024)(128)(2,1)S(1)} %pad_maximum_fusion.16), channel_id=1, source_target_pairs={{0,4},{4,8},{8,12},{12,16},{16,20},{20,24},{24,28},{1,5},{5,9},{9,... | collective-permute-start | bytes 46088 | tf_op jit(solution)/shard_map/ppermute | solution.py:25
  19.0 0.7 copy-start.14
  27.6 1.0 %copy-start.4 = (bf16[32,16,1152]{2,1,0:T(8,128)(2,1)}, bf16[32,16,1152]{2,1,0:T(8,128)(2,1)S(1)}, u32[]{:S(2)}) copy-start(bf16[32,16,1152]{2,1,0:T(8,128)(2,1)S(1)} %slice_dynamic-update-slice_fusion.3) | copy-start | bytes 3538948
  29.0 0.8 copy-start.9
  31.6 3.1 %copy-start.5 = (bf16[32,16,1152]{2,1,0:T(8,128)(2,1)S(1)}, bf16[32,16,1152]{2,1,0:T(8,128)(2,1)}, u32[]{:S(2)}) copy-start(bf16[32,16,1152]{2,1,0:T(8,128)(2,1)} %copy-done.4) | copy-start | bytes 3538948
  31.6 3.1 %copy-start.12 = (bf16[32,16,128]{2,1,0:T(8,128)(2,1)S(1)}, bf16[32,16,128]{2,1,0:T(8,128)(2,1)}, u32[]{:S(2)}) copy-start(bf16[32,16,128]{2,1,0:T(8,128)(2,1)} %param.11) | copy-start | bytes 393220
  41.6 1.9 %copy-start.2 = (f32[2,2,83968]{2,1,0:T(2,128)}, f32[2,2,83968]{2,1,0:T(2,128)S(1)}, u32[]{:S(2)}) copy-start(f32[2,2,83968]{2,1,0:T(2,128)S(1)} %reshape.189) | copy-start | bytes 4030468
  41.9 10.5 %collective-permute-start.10 = (bf16[2,83968]{1,0:T(2,128)(2,1)S(1)}, bf16[2,83968]{1,0:T(2,128)(2,1)S(1)}, u32[]{:S(2)}, u32[]{:S(2)}) collective-permute-start(bf16[2,83968]{1,0:T(2,128)(2,1)S(1)} %fusion.11), channel_id=1, source_target_pairs={{0,2},{1,3},{2,0},{3,1},{4,6},{5,7},{6,4},{7,5},{8,10},{9,11},{10,... | collective-permute-start | bytes 1007624 | tf_op jit(solution)/shard_map/ppermute | solution.py:159
  44.6 1.4 %copy-start.6 = (bf16[32,16,1152]{2,1,0:T(8,128)(2,1)S(1)}, bf16[32,16,1152]{2,1,0:T(8,128)(2,1)}, u32[]{:S(2)}) copy-start(bf16[32,16,1152]{2,1,0:T(8,128)(2,1)} %copy-done.4) | copy-start | bytes 3538948
  44.6 1.4 %copy-start.8 = (bf16[3,3,128,128]{3,2,1,0:T(8,128)(2,1)S(1)}, bf16[3,3,128,128]{3,2,1,0:T(8,128)(2,1)}, u32[]{:S(2)}) copy-start(bf16[3,3,128,128]{3,2,1,0:T(8,128)(2,1)} %param.10) | copy-start | bytes 884740
  45.9 3.2 %copy-start.1 = (bf16[4,4,256,128]{2,3,1,0:T(8,128)(2,1)S(1)}, bf16[4,4,256,128]{2,3,1,0:T(8,128)(2,1)}, u32[]{:S(2)}) copy-start(bf16[4,4,256,128]{2,3,1,0:T(8,128)(2,1)} %copy.67) | copy-start | bytes 3145732
  45.9 3.2 %copy-start.10 = (bf16[16,8,2048]{2,1,0:T(8,128)(2,1)S(1)}, bf16[16,8,2048]{2,1,0:T(8,128)(2,1)}, u32[]{:S(2)}) copy-start(bf16[16,8,2048]{2,1,0:T(8,128)(2,1)} %copy-done.9) | copy-start | bytes 1572868
  47.1 5.3 %copy-start.3 = (f32[2,2,83968]{2,1,0:T(2,128)S(1)}, f32[2,2,83968]{2,1,0:T(2,128)}, u32[]{:S(2)}) copy-start(f32[2,2,83968]{2,1,0:T(2,128)} %copy-done.2) | copy-start | bytes 4030468
  47.4 10.7 %collective-permute-start.4 = (bf16[2,83968]{1,0:T(2,128)(2,1)S(1)}, bf16[2,83968]{1,0:T(2,128)(2,1)S(1)}, u32[]{:S(2)}, u32[]{:S(2)}) collective-permute-start(bf16[2,83968]{1,0:T(2,128)(2,1)S(1)} %bitcast.137), channel_id=1, source_target_pairs={{0,1},{1,0},{2,3},{3,2},{4,5},{5,4},{6,7},{7,6},{8,9},{9,8},{10,11... | collective-permute-start | bytes 1007624 | tf_op jit(solution)/shard_map/ppermute | solution.py:159
  54.0 7.7 %collective-permute-start.11 = (bf16[83968]{0:T(1024)(128)(2,1)S(1)}, bf16[83968]{0:T(1024)(128)(2,1)S(1)}, u32[]{:S(2)}, u32[]{:S(2)}) collective-permute-start(bf16[83968]{0:T(1024)(128)(2,1)S(1)} %convert_reduce_fusion), channel_id=1, source_target_pairs={{0,1},{1,0},{2,3},{3,2},{4,5},{5,4},{6,7},{7,6},{8,9},{9,8},{10,11... | collective-permute-start | bytes 503816 | tf_op jit(solution)/shard_map/ppermute | solution.py:159
  60.1 6.6 %collective-permute-start.5 = (bf16[83968]{0:T(1024)(128)(2,1)S(1)}, bf16[83968]{0:T(1024)(128)(2,1)S(1)}, u32[]{:S(2)}, u32[]{:S(2)}) collective-permute-start(bf16[83968]{0:T(1024)(128)(2,1)S(1)} %convert_reduce_fusion.1), channel_id=1, source_target_pairs={{0,2},{1,3},{2,0},{3,1},{4,6},{5,7},{6,4},{7,5},{8,10},{9,11},{10,... | collective-permute-start | bytes 503816 | tf_op jit(solution)/shard_map/ppermute | solution.py:159
  62.6 5.0 %collective-permute-start.12 = (bf16[41984]{0:T(1024)(128)(2,1)S(1)}, bf16[41984]{0:T(1024)(128)(2,1)S(1)}, u32[]{:S(2)}, u32[]{:S(2)}) collective-permute-start(bf16[41984]{0:T(1024)(128)(2,1)S(1)} %convert_reduce_fusion.2), channel_id=1, source_target_pairs={{0,4},{4,0},{8,12},{12,8},{16,20},{20,16},{24,28},{28,24},{1,5},{5... | collective-permute-start | bytes 251912 | tf_op jit(solution)/shard_map/ppermute | solution.py:159
  67.6 2.6 %collective-permute-start.6 = (bf16[41984]{0:T(1024)(128)(2,1)S(1)}, bf16[41984]{0:T(1024)(128)(2,1)S(1)}, u32[]{:S(2)}, u32[]{:S(2)}) collective-permute-start(bf16[41984]{0:T(1024)(128)(2,1)S(1)} %convert_reduce_fusion.3), channel_id=1, source_target_pairs={{0,4},{4,0},{8,12},{12,8},{16,20},{20,16},{24,28},{28,24},{1,5},{5... | collective-permute-start | bytes 251912 | tf_op jit(solution)/shard_map/ppermute | solution.py:159
  67.7 5.8 %collective-permute-start.13 = (bf16[41984]{0:T(1024)(128)(2,1)S(1)}, bf16[41984]{0:T(1024)(128)(2,1)S(1)}, u32[]{:S(2)}, u32[]{:S(2)}) collective-permute-start(bf16[41984]{0:T(1024)(128)(2,1)S(1)} %add_convert_fusion.3), channel_id=1, source_target_pairs={{0,8},{4,12},{8,0},{12,4},{16,24},{20,28},{24,16},{28,20},{1,9},{5... | collective-permute-start | bytes 251912 | tf_op jit(solution)/shard_map/ppermute | solution.py:159
  70.2 6.4 %collective-permute-start.7 = (bf16[41984]{0:T(1024)(128)(2,1)S(1)}, bf16[41984]{0:T(1024)(128)(2,1)S(1)}, u32[]{:S(2)}, u32[]{:S(2)}) collective-permute-start(bf16[41984]{0:T(1024)(128)(2,1)S(1)} %add_convert_fusion.6), channel_id=1, source_target_pairs={{0,8},{4,12},{8,0},{12,4},{16,24},{20,28},{24,16},{28,20},{1,9},{5... | collective-permute-start | bytes 251912 | tf_op jit(solution)/shard_map/ppermute | solution.py:159
  73.6 9.1 %collective-permute-start.14 = (bf16[41984]{0:T(1024)(128)(2,1)S(1)}, bf16[41984]{0:T(1024)(128)(2,1)S(1)}, u32[]{:S(2)}, u32[]{:S(2)}) collective-permute-start(bf16[41984]{0:T(1024)(128)(2,1)S(1)} %add_convert_fusion.2), channel_id=1, source_target_pairs={{0,16},{4,20},{8,24},{12,28},{16,0},{20,4},{24,8},{28,12},{1,17},{... | collective-permute-start | bytes 251912 | tf_op jit(solution)/shard_map/ppermute | solution.py:159
  76.6 7.5 %collective-permute-start.8 = (bf16[41984]{0:T(1024)(128)(2,1)S(1)}, bf16[41984]{0:T(1024)(128)(2,1)S(1)}, u32[]{:S(2)}, u32[]{:S(2)}) collective-permute-start(bf16[41984]{0:T(1024)(128)(2,1)S(1)} %add_convert_fusion.5), channel_id=1, source_target_pairs={{0,16},{4,20},{8,24},{12,28},{16,0},{20,4},{24,8},{28,12},{1,17},{... | collective-permute-start | bytes 251912 | tf_op jit(solution)/shard_map/ppermute | solution.py:159
  82.7 1.5 %collective-permute-start.15 = (bf16[41984]{0:T(1024)(128)(2,1)S(1)}, bf16[41984]{0:T(1024)(128)(2,1)S(1)}, u32[]{:S(2)}, u32[]{:S(2)}) collective-permute-start(bf16[41984]{0:T(1024)(128)(2,1)S(1)} %add_convert_fusion.1), channel_id=1, source_target_pairs={{0,4},{4,0},{8,12},{12,8},{16,20},{20,16},{24,28},{28,24},{1,5},{5... | collective-permute-start | bytes 251912 | tf_op jit(solution)/shard_map/ppermute | solution.py:159
  84.1 1.3 %collective-permute-start.9 = (bf16[41984]{0:T(1024)(128)(2,1)S(1)}, bf16[41984]{0:T(1024)(128)(2,1)S(1)}, u32[]{:S(2)}, u32[]{:S(2)}) collective-permute-start(bf16[41984]{0:T(1024)(128)(2,1)S(1)} %add_convert_fusion.4), channel_id=1, source_target_pairs={{0,4},{4,0},{8,12},{12,8},{16,20},{20,16},{24,28},{28,24},{1,5},{5... | collective-permute-start | bytes 251912 | tf_op jit(solution)/shard_map/ppermute | solution.py:159

commit v6 on v5

--- a/solution.py
+++ b/solution.py
@@ -130,8 +130,8 @@
         "rck,kn->rcn", patches, mix_flat, preferred_element_type=jnp.float32
     ).astype(jnp.bfloat16)
     grad_scale = 1.0 / math.sqrt(out_rows * lat_count * out_cols * lon_count)
-    mix_flat_grad = jnp.einsum(
-        "rctm,rcn->mtn",
+    mix_taps = jnp.einsum(
+        "rctm,rcn->tmn",
         patches.reshape(out_rows, out_cols, 9, COUT),
         cotangent,
         preferred_element_type=jnp.float32,
@@ -141,16 +141,23 @@
     input_grad = jnp.einsum(
         "rck,kn->rcn", grad_patches, back_up, preferred_element_type=jnp.float32
     )
-    up_flat = jnp.einsum("rcm,rck->mk", inputs, grad_patches, preferred_element_type=jnp.float32)
+    up_taps = jnp.einsum(
+        "rctn,rcm->tmn",
+        grad_patches.reshape(in_rows, in_cols, 16, COUT),
+        inputs,
+        preferred_element_type=jnp.float32,
+    )
     up_span = CIN // lon_count
     mix_span = COUT // lon_count
-    up_size = up_span * 16 * COUT
-    terms = jnp.concatenate(
-        [up_flat.reshape(lon_count, up_size), mix_flat_grad.reshape(lon_count, -1)], axis=1
-    )
+    up_rows = 16 * up_span
+    by_owner = [
+        up_taps.reshape(16, lon_count, up_span, COUT).transpose(1, 0, 2, 3),
+        mix_taps.reshape(9, lon_count, mix_span, COUT).transpose(1, 0, 2, 3),
+    ]
+    terms = jnp.concatenate([t.reshape(lon_count, -1, COUT) for t in by_owner], axis=1)
     summed = reduce_terms(terms) * grad_scale
-    up_part = summed[:up_size].reshape(up_span, 4, 4, COUT).transpose(1, 2, 0, 3)
-    mix_part = summed[up_size:].reshape(mix_span, 3, 3, COUT).transpose(1, 2, 0, 3)
+    up_part = summed[:up_rows].reshape(4, 4, up_span, COUT)
+    mix_part = summed[up_rows:].reshape(3, 3, mix_span, COUT)
     return (section_out, input_grad, up_part, mix_part)
 
 
@@ -196,7 +203,8 @@
     steps = steps_of(lax.axis_size("lat"))
     if steps is None or flat.shape[0] % 2:
         return lax.psum(flat, "lat")
-    part = halve(flat.reshape(2, -1), "lat", steps[0], 0).astype(jnp.bfloat16)
+    pair = flat.reshape((2, flat.shape[0] // 2) + flat.shape[1:])
+    part = halve(pair, "lat", steps[0], 0).astype(jnp.bfloat16)
     for step in steps[1:]:
         got = exchange(part, "lat", step)
         part = (part.astype(jnp.float32) + got.astype(jnp.float32)).astype(jnp.bfloat16)

time: 87.8 us -> 86.5 us (0.985)
  waiting for transfers between devices: 19 us -> 23 us
  local copies, waits for them, and re-layouts: 30.3 us -> 27.2 us
  starting transfers between devices: 23.4 us -> 20.8 us
  matrix products: 7.19 us -> 9.02 us
  other arithmetic: 5.77 us -> 4.1 us
    dot_general x0 -> x1, local copies, waits for them, and re-layouts: none -> 8.02 us  [shards(): jnp.einsum('rctm,rcn->tmn', patches.reshape(out_rows, out_cols, 9, COUT),...]
    reshape x7 -> x2, local copies, waits for them, and re-layouts: 8.08 us -> 1.93 us  [the longest x1 1.7 us: shards(): patches.reshape(out_rows, out_cols, 9, COUT)]
    ppermute x12, waiting for transfers between devices: 18 us -> 22.5 us  [exchange(): return lax.ppermute(part, axis, [(i, i ^ step) for i in range(size)])]
    convert_element_type x6, local copies, waits for them, and re-layouts: 3.99 us -> 0.19 us  [halve(): send.astype(jnp.bfloat16)]
    ppermute x12, starting transfers between devices: 15 us -> 11.8 us  [exchange(): return lax.ppermute(part, axis, [(i, i ^ step) for i in range(size)])]
    unnamed x66 -> x77, local copies, waits for them, and re-layouts: 6.27 us -> 3.43 us
    slice x1, other arithmetic: 2.49 us -> 0.18 us  [reduce_terms(): first = scatter_lon(rows[:, :half], steps)]
    dot_general x2, matrix products: 2.38 us -> 4.24 us  [the longest x1 3.71 us: shards(): jnp.einsum('rctm,rcn->tmn', patches.reshape(out_rows, out_cols, 9, COUT),...]
  transfers between devices with their start and end apart: 16 -> 16, of which waited for: 10 -> 9; matrix products, arithmetic and copies ran while one was open for 15% -> 5% of each run, Pallas kernels for 0% -> 0%
where the time goes in v6:
time: 86.5 us; the launch traced here: 85.8 us
  local copies, waits for them, and re-layouts  27.2 us (31%)
  waiting for transfers between devices  23 us (27%)
  starting transfers between devices  20.8 us (24%)
  matrix products  9.02 us (10%)
  other arithmetic  4.1 us (5%)
  between operations  1.71 us (2%)
    ppermute x12, waiting for transfers between devices, exchange(): return lax.ppermute(part, axis, [(i, i ^ step) for i in range(size)])  22.5 us
    ppermute x12, starting transfers between devices, exchange(): return lax.ppermute(part, axis, [(i, i ^ step) for i in range(size)])  11.8 us
    dot_general x1, local copies, waits for them, and re-layouts, shards(): jnp.einsum('rctm,rcn->tmn', patches.reshape(out_rows, out_cols, 9, COUT),...  8.02 us
    slice x16, local copies, waits for them, and re-layouts, strided(): padded[row_tap:row_tap + 2 * row_count:2, col_tap:col_tap + 2 * col_count:2]  6.96 us
    ppermute x2, starting transfers between devices, swap_edges(): lax.ppermute(jnp.concatenate([p.reshape(-1) for p in lasts]), axis, up)  6.63 us
    dot_general x1, matrix products, shards(): jnp.einsum('rctm,rcn->tmn', patches.reshape(out_rows, out_cols, 9, COUT),...  3.71 us
    unnamed x77, local copies, waits for them, and re-layouts  3.43 us
    ppermute x2, starting transfers between devices, swap_edges(): lax.ppermute(jnp.concatenate([p.reshape(-1) for p in leads]), axis, down)  2.33 us
  transfers between devices with their start and end apart: 16, of which 9 were waited for; matrix products, arithmetic and copies ran while one was open for 5% of the time, Pallas kernels for 0%

profile of v6, /device:TPU:0, one launch (start us, length us, event | category | flops | bytes accessed | tf_op | source)
XLA Modules:
  0.0 85.8 jit_solution(12628854437657194038)
XLA Ops:
  0.6 1.0 %fusion.82 = (bf16[32,2,128]{2,1,0:T(2,128)(2,1)S(1)}, bf16[32,2,128]{2,1,0:T(2,128)(2,1)S(1)}) fusion(bf16[32,16,128]{2,1,0:T(8,128)(2,1)} %param.11), kind=kLoop, calls=%fused_computation.204 | loop fusion | bytes 65536 | tf_op jit(solution)/shard_map/slice | solution.py:23
  1.6 0.8 multiply_exponential_fusion
  2.9 1.2 %fusion.69 = bf16[16,8,256]{2,0,1:T(8,128)(2,1)S(1)} fusion(f32[16,8,256]{2,0,1:T(8,128)S(1)} %reshape.172, s32[16,8,256]{2,1,0:T(8,128)} %param.6), kind=kLoop, calls=%fused_computation.140 | loop fusion | flops 1703936 | bytes 327680 | tf_op jit(solution)/shard_map/convert_element_type | solution.py:51
  4.1 3.0 %collective-permute-start = (bf16[12288]{0:T(1024)(128)(2,1)S(1)}, bf16[12288]{0:T(1024)(128)(2,1)S(1)}, u32[]{:S(2)}, u32[]{:S(2)}) collective-permute-start(bf16[12288]{0:T(1024)(128)(2,1)S(1)} %pad_maximum_fusion.7), channel_id=1, source_target_pairs={{0,1},{1,2},{2,3},{3,0},{4,5},{5,6},{6,7},{7,4},{8,9},{9,10},{10,1... | collective-permute-start | bytes 73736 | tf_op jit(solution)/shard_map/ppermute | solution.py:25
  7.1 1.0 %collective-permute-start.1 = (bf16[12288]{0:T(1024)(128)(2,1)S(1)}, bf16[12288]{0:T(1024)(128)(2,1)S(1)}, u32[]{:S(2)}, u32[]{:S(2)}) collective-permute-start(bf16[12288]{0:T(1024)(128)(2,1)S(1)} %pad_maximum_fusion.8), channel_id=1, source_target_pairs={{1,0},{2,1},{3,2},{0,3},{5,4},{6,5},{7,6},{4,7},{9,8},{10,9},{11,1... | collective-permute-start | bytes 73736 | tf_op jit(solution)/shard_map/ppermute | solution.py:26
  8.2 0.9 %slice_bitcast_fusion.15 = (bf16[256,128]{1,0:T(8,128)(2,1)S(1)}, bf16[256,128]{1,0:T(8,128)(2,1)S(1)}, bf16[256,128]{1,0:T(8,128)(2,1)S(1)}, bf16[256,128]{1,0:...) fusion(bf16[4,4,256,128]{3,2,1,0:T(8,128)(2,1)S(1)} %copy-done), kind=kLoop, calls=%fused_computation.185 | loop fusion | bytes 2097152 | tf_op jit(solution)/shard_map/squeeze | solution.py:74
  9.0 0.6 compare_and_fusion
  9.6 0.5 copy.39
  10.5 0.5 collective-permute-done.1
  11.2 1.3 %collective-permute-start.2 = (bf16[7680]{0:T(1024)(128)(2,1)S(1)}, bf16[7680]{0:T(1024)(128)(2,1)S(1)}, u32[]{:S(2)}, u32[]{:S(2)}) collective-permute-start(bf16[7680]{0:T(1024)(128)(2,1)S(1)} %pad_maximum_fusion.9), channel_id=1, source_target_pairs={{4,0},{8,4},{12,8},{16,12},{20,16},{24,20},{28,24},{5,1},{9,5},{13... | collective-permute-start | bytes 46088 | tf_op jit(solution)/shard_map/ppermute | solution.py:26
  12.6 3.6 %collective-permute-start.3 = (bf16[7680]{0:T(1024)(128)(2,1)S(1)}, bf16[7680]{0:T(1024)(128)(2,1)}, u32[]{:S(2)}, u32[]{:S(2)}) collective-permute-start(bf16[7680]{0:T(1024)(128)(2,1)S(1)} %pad_maximum_fusion.10), channel_id=1, source_target_pairs={{0,4},{4,8},{8,12},{12,16},{16,20},{20,24},{24,28},{1,5},{5,9},{9,... | collective-permute-start | bytes 46088 | tf_op jit(solution)/shard_map/ppermute | solution.py:25
  16.3 0.6 copy-done.19
  17.0 0.7 slice.436
  18.4 0.7 slice.419
  19.2 1.2 %convolution_bitcast_fusion = f32[17,9,1,128]{3,0,1,2:T(8,128)S(1)} fusion(bf16[256,128]{1,0:T(8,128)(2,1)} %get-tuple-element.23, bf16[256,128]{1,0:T(8,128)(2,1)S(1)} %get-tuple-element.9, bf16[256,128]{1,0:T(8,128)(2,1)S(1)} %get-tuple-element.10, bf16[256,128]{1,0:T(8,128)(2,1)S(1)} %get-tuple-element.11, bf16[17,9,256]{2,0,1:T(8,128)(2,1)S(1)} %get-tuple-element.42, ...), kind=kOutput, calls=%fused_computation.5 | convolution fusion | flops 42409984 | bytes 653824 | tf_op jit(solution)/shard_map/rck,kn->rcn/dot_general | solution.py:78
  20.8 0.4 copy-done.11
  22.3 1.0 %reshape.207 = f32[34,18,128]{2,1,0:T(8,128)} reshape(f32[17,2,9,2,128]{4,3,2,1,0:T(2,128)S(1)} %copy.50) | data formatting | bytes 626688 | tf_op jit(solution)/shard_map/reshape | solution.py:82
  23.2 0.7 fusion.85
  26.6 0.4 slice.392
  27.0 0.4 slice.393
  28.1 0.4 slice.396
  28.5 0.4 slice.397
  28.9 0.6 slice.398
  29.5 0.6 slice.399
  30.1 0.7 slice.400
  30.8 0.7 slice.401
  32.1 1.7 %reshape.190 = bf16[32,16,9,128]{3,2,1,0:T(8,128)(2,1)} reshape(bf16[32,16,1152]{2,1,0:T(8,128)(2,1)S(1)} %slice_dynamic-update-slice_fusion.3) | data formatting | bytes 2359296 | tf_op jit(solution)/shard_map/reshape | solution.py:135
  33.8 1.1 %convolution_convert_fusion = bf16[32,16,128]{2,1,0:T(8,128)(2,1)} fusion(bf16[32,16,1152]{2,1,0:T(8,128)(2,1)S(1)} %slice_dynamic-update-slice_fusion.3, bf16[1152,128,1]{1,0,2:T(8,128)(2,1)S(1)} %bitcast.160), kind=kOutput, calls=%fused_computation.4 | convolution fusion | flops 151060480 | bytes 1605632 | tf_op jit(solution)/shard_map/rck,kn->rcn/dot_general | solution.py:129
  35.2 0.5 fusion.5
  36.3 8.0 %reshape.208 = bf16[9,4,32,16,32]{2,1,0,3,4:T(4,128)(2,1)} reshape(bf16[9,128,16,32]{1,0,2,3:T(8,128)(2,1)} %bitcast.151) | data formatting | bytes 2359296 | tf_op jit(solution)/shard_map/rctm,rcn->tmn/dot_general | solution.py:133
  44.3 3.7 %fusion.2 = f32[4,9,32,128]{3,2,0,1:T(8,128)S(1)} fusion(bf16[9,4,32,16,32]{2,1,0,3,4:T(4,128)(2,1)} %reshape.208, bf16[32,16,128]{2,1,0:T(8,128)(2,1)S(1)} %copy-done.7), kind=kOutput, calls=%fused_computation.3 | convolution fusion | flops 150994944 | bytes 1900544 | tf_op jit(solution)/shard_map/rctm,rcn->tmn/dot_general | solution.py:133
  48.3 1.6 %collective-permute-start.10 = (bf16[2,656,128]{2,1,0:T(8,128)(2,1)S(1)}, bf16[2,656,128]{2,1,0:T(8,128)(2,1)S(1)}, u32[]{:S(2)}, u32[]{:S(2)}) collective-permute-start(bf16[2,656,128]{2,1,0:T(8,128)(2,1)S(1)} %fusion.16), channel_id=1, source_target_pairs={{0,2},{1,3},{2,0},{3,1},{4,6},{5,7},{6,4},{7,5},{8,10},{9,11},{10,... | collective-permute-start | bytes 1007624 | tf_op jit(solution)/shard_map/ppermute | solution.py:166
  49.9 1.0 %collective-permute-start.4 = (bf16[2,656,128]{2,1,0:T(8,128)(2,1)S(1)}, bf16[2,656,128]{2,1,0:T(8,128)(2,1)S(1)}, u32[]{:S(2)}, u32[]{:S(2)}) collective-permute-start(bf16[2,656,128]{2,1,0:T(8,128)(2,1)S(1)} %fusion.15), channel_id=1, source_target_pairs={{0,1},{1,0},{2,3},{3,2},{4,5},{5,4},{6,7},{7,6},{8,9},{9,8},{10,11... | collective-permute-start | bytes 1007624 | tf_op jit(solution)/shard_map/ppermute | solution.py:166
  50.9 1.0 %fusion.86 = f32[16,8,256]{2,1,0:T(8,128)} fusion(bf16[16,8,2048]{2,1,0:T(8,128)(2,1)S(1)} %copy-done.5, bf16[2048,256,1]{1,0,2:T(8,128)(2,1)S(1)} %bitcast.152), kind=kOutput, calls=%fused_computation.208 | convolution fusion | flops 134217728 | bytes 1703936 | tf_op jit(solution)/shard_map/rck,kn->rcn/dot_general | solution.py:141
  51.9 6.9 %collective-permute-done.10 = bf16[2,656,128]{2,1,0:T(8,128)(2,1)S(1)} collective-permute-done((bf16[2,656,128]{2,1,0:T(8,128)(2,1)S(1)}, bf16[2,656,128]{2,1,0:T(8,128)(2,1)S(1)}, u32[]{:S(2)}, u32[]{:S(2)}) %collective-permute-start.10) | collective-permute-done | bytes 335904 | tf_op jit(solution)/shard_map/ppermute | solution.py:166
  58.9 2.5 %collective-permute-start.11 = (bf16[656,128]{1,0:T(8,128)(2,1)S(1)}, bf16[656,128]{1,0:T(8,128)(2,1)S(1)}, u32[]{:S(2)}, u32[]{:S(2)}) collective-permute-start(bf16[656,128]{1,0:T(8,128)(2,1)S(1)} %fusion.53), channel_id=1, source_target_pairs={{0,1},{1,0},{2,3},{3,2},{4,5},{5,4},{6,7},{7,6},{8,9},{9,8},{10,11... | collective-permute-start | bytes 503816 | tf_op jit(solution)/shard_map/ppermute | solution.py:166
  61.8 3.8 %collective-permute-done.11 = bf16[656,128]{1,0:T(8,128)(2,1)S(1)} collective-permute-done((bf16[656,128]{1,0:T(8,128)(2,1)S(1)}, bf16[656,128]{1,0:T(8,128)(2,1)S(1)}, u32[]{:S(2)}, u32[]{:S(2)}) %collective-permute-start.11) | collective-permute-done | bytes 167968 | tf_op jit(solution)/shard_map/ppermute | solution.py:166
  65.8 1.5 %collective-permute-done.5 = bf16[656,128]{1,0:T(8,128)(2,1)S(1)} collective-permute-done((bf16[656,128]{1,0:T(8,128)(2,1)S(1)}, bf16[656,128]{1,0:T(8,128)(2,1)S(1)}, u32[]{:S(2)}, u32[]{:S(2)}) %collective-permute-start.5) | collective-permute-done | bytes 167968 | tf_op jit(solution)/shard_map/ppermute | solution.py:166
  67.4 1.3 %collective-permute-start.13 = (bf16[328,128]{1,0:T(8,128)(2,1)S(1)}, bf16[328,128]{1,0:T(8,128)(2,1)S(1)}, u32[]{:S(2)}, u32[]{:S(2)}) collective-permute-start(bf16[328,128]{1,0:T(8,128)(2,1)S(1)} %fusion.54), channel_id=1, source_target_pairs={{0,8},{4,12},{8,0},{12,4},{16,24},{20,28},{24,16},{28,20},{1,9},{5... | collective-permute-start | bytes 251912 | tf_op jit(solution)/shard_map/ppermute | solution.py:166
  68.8 1.2 %collective-permute-start.7 = (bf16[328,128]{1,0:T(8,128)(2,1)S(1)}, bf16[328,128]{1,0:T(8,128)(2,1)S(1)}, u32[]{:S(2)}, u32[]{:S(2)}) collective-permute-start(bf16[328,128]{1,0:T(8,128)(2,1)S(1)} %fusion.55), channel_id=1, source_target_pairs={{0,8},{4,12},{8,0},{12,4},{16,24},{20,28},{24,16},{28,20},{1,9},{5... | collective-permute-start | bytes 251912 | tf_op jit(solution)/shard_map/ppermute | solution.py:166
  70.0 2.8 %collective-permute-done.13 = bf16[328,128]{1,0:T(8,128)(2,1)S(1)} collective-permute-done((bf16[328,128]{1,0:T(8,128)(2,1)S(1)}, bf16[328,128]{1,0:T(8,128)(2,1)S(1)}, u32[]{:S(2)}, u32[]{:S(2)}) %collective-permute-start.13) | collective-permute-done | bytes 84000 | tf_op jit(solution)/shard_map/ppermute | solution.py:166
  72.8 2.3 %collective-permute-start.14 = (bf16[328,128]{1,0:T(8,128)(2,1)S(1)}, bf16[328,128]{1,0:T(8,128)(2,1)S(1)}, u32[]{:S(2)}, u32[]{:S(2)}) collective-permute-start(bf16[328,128]{1,0:T(8,128)(2,1)S(1)} %add_convert_fusion.2), channel_id=1, source_target_pairs={{0,16},{4,20},{8,24},{12,28},{16,0},{20,4},{24,8},{28,12},{1,17},{... | collective-permute-start | bytes 251912 | tf_op jit(solution)/shard_map/ppermute | solution.py:166
  75.2 1.4 %collective-permute-start.8 = (bf16[328,128]{1,0:T(8,128)(2,1)S(1)}, bf16[328,128]{1,0:T(8,128)(2,1)S(1)}, u32[]{:S(2)}, u32[]{:S(2)}) collective-permute-start(bf16[328,128]{1,0:T(8,128)(2,1)S(1)} %add_convert_fusion.4), channel_id=1, source_target_pairs={{0,16},{4,20},{8,24},{12,28},{16,0},{20,4},{24,8},{28,12},{1,17},{... | collective-permute-start | bytes 251912 | tf_op jit(solution)/shard_map/ppermute | solution.py:166
  76.5 5.2 %collective-permute-done.14 = bf16[328,128]{1,0:T(8,128)(2,1)S(1)} collective-permute-done((bf16[328,128]{1,0:T(8,128)(2,1)S(1)}, bf16[328,128]{1,0:T(8,128)(2,1)S(1)}, u32[]{:S(2)}, u32[]{:S(2)}) %collective-permute-start.14) | collective-permute-done | bytes 84000 | tf_op jit(solution)/shard_map/ppermute | solution.py:166
  81.8 1.1 %collective-permute-done.8 = bf16[328,128]{1,0:T(8,128)(2,1)S(1)} collective-permute-done((bf16[328,128]{1,0:T(8,128)(2,1)S(1)}, bf16[328,128]{1,0:T(8,128)(2,1)S(1)}, u32[]{:S(2)}, u32[]{:S(2)}) %collective-permute-start.8) | collective-permute-done | bytes 84000 | tf_op jit(solution)/shard_map/ppermute | solution.py:166
  83.1 1.1 %collective-permute-done.9 = bf16[328,128]{1,0:T(8,128)(2,1)S(1)} collective-permute-done((bf16[328,128]{1,0:T(8,128)(2,1)S(1)}, bf16[328,128]{1,0:T(8,128)(2,1)S(1)}, u32[]{:S(2)}, u32[]{:S(2)}) %collective-permute-start.9) | collective-permute-done | bytes 84000 | tf_op jit(solution)/shard_map/ppermute | solution.py:166
  84.3 0.8 slice.445
  85.2 0.7 slice.446
  (167 shorter events, 9.3 us)
Async XLA Ops:
  0.6 7.5 %copy-start = (bf16[4,4,256,128]{3,2,1,0:T(8,128)(2,1)S(1)}, bf16[4,4,256,128]{3,2,1,0:T(8,128)(2,1)}, u32[]{:S(2)}) copy-start(bf16[4,4,256,128]{3,2,1,0:T(8,128)(2,1)} %param.8) | copy-start | bytes 3145732
  4.1 6.3 %collective-permute-start = (bf16[12288]{0:T(1024)(128)(2,1)S(1)}, bf16[12288]{0:T(1024)(128)(2,1)S(1)}, u32[]{:S(2)}, u32[]{:S(2)}) collective-permute-start(bf16[12288]{0:T(1024)(128)(2,1)S(1)} %pad_maximum_fusion.7), channel_id=1, source_target_pairs={{0,1},{1,2},{2,3},{3,0},{4,5},{5,6},{6,7},{7,4},{8,9},{9,10},{10,1... | collective-permute-start | bytes 73736 | tf_op jit(solution)/shard_map/ppermute | solution.py:25
  7.1 3.9 %collective-permute-start.1 = (bf16[12288]{0:T(1024)(128)(2,1)S(1)}, bf16[12288]{0:T(1024)(128)(2,1)S(1)}, u32[]{:S(2)}, u32[]{:S(2)}) collective-permute-start(bf16[12288]{0:T(1024)(128)(2,1)S(1)} %pad_maximum_fusion.8), channel_id=1, source_target_pairs={{1,0},{2,1},{3,2},{0,3},{5,4},{6,5},{7,6},{4,7},{9,8},{10,9},{11,1... | collective-permute-start | bytes 73736 | tf_op jit(solution)/shard_map/ppermute | solution.py:26
  8.2 2.0 %copy-start.2 = (bf16[3,3,128,128]{3,2,1,0:T(8,128)(2,1)S(1)}, bf16[3,3,128,128]{3,2,1,0:T(8,128)(2,1)}, u32[]{:S(2)}) copy-start(bf16[3,3,128,128]{3,2,1,0:T(8,128)(2,1)} %param.10) | copy-start | bytes 884740
  9.0 1.4 %copy-start.6 = (bf16[32,16,128]{2,1,0:T(8,128)(2,1)S(1)}, bf16[32,16,128]{2,1,0:T(8,128)(2,1)}, u32[]{:S(2)}) copy-start(bf16[32,16,128]{2,1,0:T(8,128)(2,1)} %param.11) | copy-start | bytes 393220
  11.2 5.0 %collective-permute-start.2 = (bf16[7680]{0:T(1024)(128)(2,1)S(1)}, bf16[7680]{0:T(1024)(128)(2,1)S(1)}, u32[]{:S(2)}, u32[]{:S(2)}) collective-permute-start(bf16[7680]{0:T(1024)(128)(2,1)S(1)} %pad_maximum_fusion.9), channel_id=1, source_target_pairs={{4,0},{8,4},{12,8},{16,12},{20,16},{24,20},{28,24},{5,1},{9,5},{13... | collective-permute-start | bytes 46088 | tf_op jit(solution)/shard_map/ppermute | solution.py:26
  12.6 4.4 %collective-permute-start.3 = (bf16[7680]{0:T(1024)(128)(2,1)S(1)}, bf16[7680]{0:T(1024)(128)(2,1)}, u32[]{:S(2)}, u32[]{:S(2)}) collective-permute-start(bf16[7680]{0:T(1024)(128)(2,1)S(1)} %pad_maximum_fusion.10), channel_id=1, source_target_pairs={{0,4},{4,8},{8,12},{12,16},{16,20},{20,24},{24,28},{1,5},{5,9},{9,... | collective-permute-start | bytes 46088 | tf_op jit(solution)/shard_map/ppermute | solution.py:25
  16.2 0.6 copy-start.19
  16.9 1.5 %slice-start = ((bf16[7680]{0:T(1024)(128)(2,1)}), bf16[2560]{0:T(1024)(128)(2,1)S(1)}, s32[]{:S(2)}) async-start(bf16[7680]{0:T(1024)(128)(2,1)} %copy-done.19), calls=%async_computation | async-start | bytes 12288 | tf_op jit(solution)/shard_map/slice | solution.py:31
  19.2 1.3 %copy-start.15 = (bf16[256,128]{1,0:T(8,128)(2,1)S(1)}, bf16[256,128]{1,0:T(8,128)(2,1)}, u32[]{:S(2)}) copy-start(bf16[256,128]{1,0:T(8,128)(2,1)} %get-tuple-element.12) | copy-start | bytes 196612
  19.2 1.3 %copy-start.16 = (bf16[256,128]{1,0:T(8,128)(2,1)S(1)}, bf16[256,128]{1,0:T(8,128)(2,1)}, u32[]{:S(2)}) copy-start(bf16[256,128]{1,0:T(8,128)(2,1)} %get-tuple-element.13) | copy-start | bytes 196612
  19.2 1.3 %copy-start.17 = (bf16[256,128]{1,0:T(8,128)(2,1)S(1)}, bf16[256,128]{1,0:T(8,128)(2,1)}, u32[]{:S(2)}) copy-start(bf16[256,128]{1,0:T(8,128)(2,1)} %get-tuple-element.14) | copy-start | bytes 196612
  19.2 1.3 %copy-start.18 = (bf16[256,128]{1,0:T(8,128)(2,1)S(1)}, bf16[256,128]{1,0:T(8,128)(2,1)}, u32[]{:S(2)}) copy-start(bf16[256,128]{1,0:T(8,128)(2,1)} %get-tuple-element.15) | copy-start | bytes 196612
  20.4 0.8 copy-start.11
  20.4 0.9 %copy-start.12 = (bf16[256,128]{1,0:T(8,128)(2,1)S(1)}, bf16[256,128]{1,0:T(8,128)(2,1)}, u32[]{:S(2)}) copy-start(bf16[256,128]{1,0:T(8,128)(2,1)} %get-tuple-element.17) | copy-start | bytes 196612
  20.4 0.9 %copy-start.13 = (bf16[256,128]{1,0:T(8,128)(2,1)S(1)}, bf16[256,128]{1,0:T(8,128)(2,1)}, u32[]{:S(2)}) copy-start(bf16[256,128]{1,0:T(8,128)(2,1)} %get-tuple-element.18) | copy-start | bytes 196612
  20.4 0.9 %copy-start.14 = (bf16[256,128]{1,0:T(8,128)(2,1)S(1)}, bf16[256,128]{1,0:T(8,128)(2,1)}, u32[]{:S(2)}) copy-start(bf16[256,128]{1,0:T(8,128)(2,1)} %get-tuple-element.19) | copy-start | bytes 196612
  20.8 0.9 %copy-start.8 = (bf16[256,128]{1,0:T(8,128)(2,1)S(1)}, bf16[256,128]{1,0:T(8,128)(2,1)}, u32[]{:S(2)}) copy-start(bf16[256,128]{1,0:T(8,128)(2,1)} %get-tuple-element.20) | copy-start | bytes 196612
  20.8 0.9 %copy-start.9 = (bf16[256,128]{1,0:T(8,128)(2,1)S(1)}, bf16[256,128]{1,0:T(8,128)(2,1)}, u32[]{:S(2)}) copy-start(bf16[256,128]{1,0:T(8,128)(2,1)} %get-tuple-element.21) | copy-start | bytes 196612
  20.8 0.9 %copy-start.10 = (bf16[256,128]{1,0:T(8,128)(2,1)S(1)}, bf16[256,128]{1,0:T(8,128)(2,1)}, u32[]{:S(2)}) copy-start(bf16[256,128]{1,0:T(8,128)(2,1)} %get-tuple-element.22) | copy-start | bytes 196612
  22.3 1.7 %copy-start.20 = (f32[128]{0:T(128)S(1)}, f32[128]{0:T(128)}, u32[]{:S(2)}) copy-start(f32[128]{0:T(128)} %param.9) | copy-start | bytes 1540
  22.3 1.7 %copy-start.21 = (pred[34]{0:T(512)(128)(4,1)S(1)}, pred[34]{0:T(512)(128)(4,1)}, u32[]{:S(2)}) copy-start(pred[34]{0:T(512)(128)(4,1)} %compare_and_fusion) | copy-start | bytes 106
  23.2 1.0 %copy-start.1 = (f32[34,18,128]{2,1,0:T(8,128)S(1)}, f32[34,18,128]{2,1,0:T(8,128)}, u32[]{:S(2)}) copy-start(f32[34,18,128]{2,1,0:T(8,128)} %reshape.207) | copy-start | bytes 940036
  32.1 1.7 %copy-start.3 = (bf16[3,3,128,128]{3,2,1,0:T(8,128)(2,1)S(1)}, bf16[3,3,128,128]{3,2,1,0:T(8,128)(2,1)}, u32[]{:S(2)}) copy-start(bf16[3,3,128,128]{3,2,1,0:T(8,128)(2,1)} %param.10) | copy-start | bytes 884740
  35.2 0.8 copy-start.4
  36.3 8.0 %copy-start.7 = (bf16[32,16,128]{2,1,0:T(8,128)(2,1)S(1)}, bf16[32,16,128]{2,1,0:T(8,128)(2,1)}, u32[]{:S(2)}) copy-start(bf16[32,16,128]{2,1,0:T(8,128)(2,1)} %param.11) | copy-start | bytes 393220
  48.1 2.9 %copy-start.5 = (bf16[16,8,2048]{2,1,0:T(8,128)(2,1)S(1)}, bf16[16,8,2048]{2,1,0:T(8,128)(2,1)}, u32[]{:S(2)}) copy-start(bf16[16,8,2048]{2,1,0:T(8,128)(2,1)} %copy-done.4) | copy-start | bytes 1572868
  48.3 10.5 %collective-permute-start.10 = (bf16[2,656,128]{2,1,0:T(8,128)(2,1)S(1)}, bf16[2,656,128]{2,1,0:T(8,128)(2,1)S(1)}, u32[]{:S(2)}, u32[]{:S(2)}) collective-permute-start(bf16[2,656,128]{2,1,0:T(8,128)(2,1)S(1)} %fusion.16), channel_id=1, source_target_pairs={{0,2},{1,3},{2,0},{3,1},{4,6},{5,7},{6,4},{7,5},{8,10},{9,11},{10,... | collective-permute-start | bytes 1007624 | tf_op jit(solution)/shard_map/ppermute | solution.py:166
  49.9 11.4 %collective-permute-start.4 = (bf16[2,656,128]{2,1,0:T(8,128)(2,1)S(1)}, bf16[2,656,128]{2,1,0:T(8,128)(2,1)S(1)}, u32[]{:S(2)}, u32[]{:S(2)}) collective-permute-start(bf16[2,656,128]{2,1,0:T(8,128)(2,1)S(1)} %fusion.15), channel_id=1, source_target_pairs={{0,1},{1,0},{2,3},{3,2},{4,5},{5,4},{6,7},{7,6},{8,9},{9,8},{10,11... | collective-permute-start | bytes 1007624 | tf_op jit(solution)/shard_map/ppermute | solution.py:166
  58.9 6.7 %collective-permute-start.11 = (bf16[656,128]{1,0:T(8,128)(2,1)S(1)}, bf16[656,128]{1,0:T(8,128)(2,1)S(1)}, u32[]{:S(2)}, u32[]{:S(2)}) collective-permute-start(bf16[656,128]{1,0:T(8,128)(2,1)S(1)} %fusion.53), channel_id=1, source_target_pairs={{0,1},{1,0},{2,3},{3,2},{4,5},{5,4},{6,7},{7,6},{8,9},{9,8},{10,11... | collective-permute-start | bytes 503816 | tf_op jit(solution)/shard_map/ppermute | solution.py:166
  61.5 5.8 %collective-permute-start.5 = (bf16[656,128]{1,0:T(8,128)(2,1)S(1)}, bf16[656,128]{1,0:T(8,128)(2,1)S(1)}, u32[]{:S(2)}, u32[]{:S(2)}) collective-permute-start(bf16[656,128]{1,0:T(8,128)(2,1)S(1)} %fusion.52), channel_id=1, source_target_pairs={{0,2},{1,3},{2,0},{3,1},{4,6},{5,7},{6,4},{7,5},{8,10},{9,11},{10,... | collective-permute-start | bytes 503816 | tf_op jit(solution)/shard_map/ppermute | solution.py:166
  65.7 1.7 %collective-permute-start.12 = (bf16[328,128]{1,0:T(8,128)(2,1)S(1)}, bf16[328,128]{1,0:T(8,128)(2,1)S(1)}, u32[]{:S(2)}, u32[]{:S(2)}) collective-permute-start(bf16[328,128]{1,0:T(8,128)(2,1)S(1)} %fusion.73), channel_id=1, source_target_pairs={{0,4},{4,0},{8,12},{12,8},{16,20},{20,16},{24,28},{28,24},{1,5},{5... | collective-permute-start | bytes 251912 | tf_op jit(solution)/shard_map/ppermute | solution.py:166
  67.3 1.4 %collective-permute-start.6 = (bf16[328,128]{1,0:T(8,128)(2,1)S(1)}, bf16[328,128]{1,0:T(8,128)(2,1)S(1)}, u32[]{:S(2)}, u32[]{:S(2)}) collective-permute-start(bf16[328,128]{1,0:T(8,128)(2,1)S(1)} %fusion.72), channel_id=1, source_target_pairs={{0,4},{4,0},{8,12},{12,8},{16,20},{20,16},{24,28},{28,24},{1,5},{5... | collective-permute-start | bytes 251912 | tf_op jit(solution)/shard_map/ppermute | solution.py:166
  67.4 5.4 %collective-permute-start.13 = (bf16[328,128]{1,0:T(8,128)(2,1)S(1)}, bf16[328,128]{1,0:T(8,128)(2,1)S(1)}, u32[]{:S(2)}, u32[]{:S(2)}) collective-permute-start(bf16[328,128]{1,0:T(8,128)(2,1)S(1)} %fusion.54), channel_id=1, source_target_pairs={{0,8},{4,12},{8,0},{12,4},{16,24},{20,28},{24,16},{28,20},{1,9},{5... | collective-permute-start | bytes 251912 | tf_op jit(solution)/shard_map/ppermute | solution.py:166
  68.8 6.4 %collective-permute-start.7 = (bf16[328,128]{1,0:T(8,128)(2,1)S(1)}, bf16[328,128]{1,0:T(8,128)(2,1)S(1)}, u32[]{:S(2)}, u32[]{:S(2)}) collective-permute-start(bf16[328,128]{1,0:T(8,128)(2,1)S(1)} %fusion.55), channel_id=1, source_target_pairs={{0,8},{4,12},{8,0},{12,4},{16,24},{20,28},{24,16},{28,20},{1,9},{5... | collective-permute-start | bytes 251912 | tf_op jit(solution)/shard_map/ppermute | solution.py:166
  72.8 8.9 %collective-permute-start.14 = (bf16[328,128]{1,0:T(8,128)(2,1)S(1)}, bf16[328,128]{1,0:T(8,128)(2,1)S(1)}, u32[]{:S(2)}, u32[]{:S(2)}) collective-permute-start(bf16[328,128]{1,0:T(8,128)(2,1)S(1)} %add_convert_fusion.2), channel_id=1, source_target_pairs={{0,16},{4,20},{8,24},{12,28},{16,0},{20,4},{24,8},{28,12},{1,17},{... | collective-permute-start | bytes 251912 | tf_op jit(solution)/shard_map/ppermute | solution.py:166
  75.2 7.7 %collective-permute-start.8 = (bf16[328,128]{1,0:T(8,128)(2,1)S(1)}, bf16[328,128]{1,0:T(8,128)(2,1)S(1)}, u32[]{:S(2)}, u32[]{:S(2)}) collective-permute-start(bf16[328,128]{1,0:T(8,128)(2,1)S(1)} %add_convert_fusion.4), channel_id=1, source_target_pairs={{0,16},{4,20},{8,24},{12,28},{16,0},{20,4},{24,8},{28,12},{1,17},{... | collective-permute-start | bytes 251912 | tf_op jit(solution)/shard_map/ppermute | solution.py:166
  81.7 1.3 %collective-permute-start.15 = (bf16[328,128]{1,0:T(8,128)(2,1)S(1)}, bf16[328,128]{1,0:T(8,128)(2,1)S(1)}, u32[]{:S(2)}, u32[]{:S(2)}) collective-permute-start(bf16[328,128]{1,0:T(8,128)(2,1)S(1)} %add_convert_fusion.1), channel_id=1, source_target_pairs={{0,4},{4,0},{8,12},{12,8},{16,20},{20,16},{24,28},{28,24},{1,5},{5... | collective-permute-start | bytes 251912 | tf_op jit(solution)/shard_map/ppermute | solution.py:166
  82.9 1.3 %collective-permute-start.9 = (bf16[328,128]{1,0:T(8,128)(2,1)S(1)}, bf16[328,128]{1,0:T(8,128)(2,1)S(1)}, u32[]{:S(2)}, u32[]{:S(2)}) collective-permute-start(bf16[328,128]{1,0:T(8,128)(2,1)S(1)} %add_convert_fusion.3), channel_id=1, source_target_pairs={{0,4},{4,0},{8,12},{12,8},{16,20},{20,16},{24,28},{28,24},{1,5},{5... | collective-permute-start | bytes 251912 | tf_op jit(solution)/shard_map/ppermute | solution.py:166

commit v7 on v6

--- a/solution.py
+++ b/solution.py
@@ -130,12 +130,13 @@
         "rck,kn->rcn", patches, mix_flat, preferred_element_type=jnp.float32
     ).astype(jnp.bfloat16)
     grad_scale = 1.0 / math.sqrt(out_rows * lat_count * out_cols * lon_count)
-    mix_taps = jnp.einsum(
-        "rctm,rcn->tmn",
+    mix_span = COUT // lon_count
+    mix_owned = jnp.einsum(
+        "rctm,rcn->mtn",
         patches.reshape(out_rows, out_cols, 9, COUT),
         cotangent,
         preferred_element_type=jnp.float32,
-    )
+    ).reshape(lon_count, mix_span, 9, COUT).transpose(0, 2, 1, 3)
     grad_patches = strided(pre_grad_pad, in_rows, in_cols)
     back_up = up_kernel.transpose(0, 1, 3, 2).reshape(16 * COUT, CIN)
     input_grad = jnp.einsum(
@@ -148,11 +149,10 @@
         preferred_element_type=jnp.float32,
     )
     up_span = CIN // lon_count
-    mix_span = COUT // lon_count
     up_rows = 16 * up_span
     by_owner = [
         up_taps.reshape(16, lon_count, up_span, COUT).transpose(1, 0, 2, 3),
-        mix_taps.reshape(9, lon_count, mix_span, COUT).transpose(1, 0, 2, 3),
+        mix_owned,
     ]
     terms = jnp.concatenate([t.reshape(lon_count, -1, COUT) for t in by_owner], axis=1)
     summed = reduce_terms(terms) * grad_scale

time: 86.5 us -> 79.2 us (0.916)
  local copies, waits for them, and re-layouts: 27.2 us -> 19.2 us
  other arithmetic: 4.1 us -> 7.88 us
  matrix products: 9.02 us -> 6.41 us
    dot_general x1 -> x0, local copies, waits for them, and re-layouts: 8.02 us -> none  [shards(): jnp.einsum('rctm,rcn->tmn', patches.reshape(out_rows, out_cols, 9, COUT),...]
    unnamed x5, other arithmetic: 0.31 us -> 3.67 us
    dot_general x1, matrix products: 3.71 us -> 0.51 us  [shards(): jnp.einsum('rctm,rcn->mtn', patches.reshape(out_rows, out_cols, 9, COUT),...]
    reshape x1, local copies, waits for them, and re-layouts: 1.7 us -> 0.04 us  [shards(): mix_owned = jnp.einsum('rctm,rcn->mtn', patches.reshape(out_rows, out_col...]
    dot_general x1, matrix products: 0.67 us -> 2.1 us  [shards(): jnp.einsum('rck,kn->rcn', neighbours(grad_pad, out_rows + 2, out_cols + 2...]
    slice x9 -> x8, local copies, waits for them, and re-layouts: 0.06 us -> 1.48 us  [swap_edges(): tail = after[at:at + count].reshape(lead.shape)]
    unnamed x77 -> x55, local copies, waits for them, and re-layouts: 3.43 us -> 4.57 us
    ppermute x12, starting transfers between devices: 11.8 us -> 12.9 us  [exchange(): return lax.ppermute(part, axis, [(i, i ^ step) for i in range(size)])]
  transfers between devices with their start and end apart: 16 -> 16, of which waited for: 9 -> 8; matrix products, arithmetic and copies ran while one was open for 5% -> 8% of each run, Pallas kernels for 0% -> 0%
where the time goes in v7:
time: 79.2 us; the launch traced here: 78.7 us
  waiting for transfers between devices  22.6 us (29%)
  starting transfers between devices  21.1 us (27%)
  local copies, waits for them, and re-layouts  19.2 us (24%)
  other arithmetic  7.88 us (10%)
  matrix products  6.41 us (8%)
  between operations  1.55 us (2%)
    ppermute x12, waiting for transfers between devices, exchange(): return lax.ppermute(part, axis, [(i, i ^ step) for i in range(size)])  22.2 us
    ppermute x12, starting transfers between devices, exchange(): return lax.ppermute(part, axis, [(i, i ^ step) for i in range(size)])  12.9 us
    slice x16, local copies, waits for them, and re-layouts, strided(): padded[row_tap:row_tap + 2 * row_count:2, col_tap:col_tap + 2 * col_count:2]  6.96 us
    ppermute x2, starting transfers between devices, swap_edges(): lax.ppermute(jnp.concatenate([p.reshape(-1) for p in lasts]), axis, up)  5.97 us
    unnamed x55, local copies, waits for them, and re-layouts  4.57 us
    unnamed x5, other arithmetic  3.67 us
    ppermute x2, starting transfers between devices, swap_edges(): lax.ppermute(jnp.concatenate([p.reshape(-1) for p in leads]), axis, down)  2.25 us
    dot_general x1, matrix products, shards(): jnp.einsum('rck,kn->rcn', neighbours(grad_pad, out_rows + 2, out_cols + 2...  2.1 us
  transfers between devices with their start and end apart: 16, of which 8 were waited for; matrix products, arithmetic and copies ran while one was open for 8% of the time, Pallas kernels for 0%

profile of v7, /device:TPU:0, one launch (start us, length us, event | category | flops | bytes accessed | tf_op | source)
XLA Modules:
  0.0 78.7 jit_solution(15413211786073808091)
XLA Ops:
  0.7 1.0 %fusion.80 = (bf16[32,2,128]{2,1,0:T(2,128)(2,1)S(1)}, bf16[32,2,128]{2,1,0:T(2,128)(2,1)S(1)}) fusion(bf16[32,16,128]{2,1,0:T(8,128)(2,1)} %param.11), kind=kLoop, calls=%fused_computation.204 | loop fusion | bytes 65536 | tf_op jit(solution)/shard_map/slice | solution.py:23
  1.7 0.8 multiply_exponential_fusion
  3.2 0.6 pad_maximum_fusion.7
  3.8 2.9 %collective-permute-start = (bf16[12288]{0:T(1024)(128)(2,1)}, bf16[12288]{0:T(1024)(128)(2,1)}, u32[]{:S(2)}, u32[]{:S(2)}) collective-permute-start(bf16[12288]{0:T(1024)(128)(2,1)} %pad_maximum_fusion.7), channel_id=1, source_target_pairs={{0,1},{1,2},{2,3},{3,0},{4,5},{5,6},{6,7},{7,4},{8,9},{9,10},{10,1... | collective-permute-start | bytes 73736 | tf_op jit(solution)/shard_map/ppermute | solution.py:25
  6.8 0.6 pad_maximum_fusion.8
  7.4 1.0 %collective-permute-start.1 = (bf16[12288]{0:T(1024)(128)(2,1)}, bf16[12288]{0:T(1024)(128)(2,1)}, u32[]{:S(2)}, u32[]{:S(2)}) collective-permute-start(bf16[12288]{0:T(1024)(128)(2,1)} %pad_maximum_fusion.8), channel_id=1, source_target_pairs={{1,0},{2,1},{3,2},{0,3},{5,4},{6,5},{7,6},{4,7},{9,8},{10,9},{11,1... | collective-permute-start | bytes 73736 | tf_op jit(solution)/shard_map/ppermute | solution.py:26
  8.4 0.8 slice_bitcast_fusion.15
  9.2 0.5 copy.40
  10.4 0.7 slice.412
  11.5 0.7 slice.413
  12.3 0.7 slice.411
  13.0 0.7 slice.409
  13.8 1.3 %collective-permute-start.2 = (bf16[7680]{0:T(1024)(128)(2,1)S(1)}, bf16[7680]{0:T(1024)(128)(2,1)S(1)}, u32[]{:S(2)}, u32[]{:S(2)}) collective-permute-start(bf16[7680]{0:T(1024)(128)(2,1)S(1)} %pad_maximum_fusion.9), channel_id=1, source_target_pairs={{4,0},{8,4},{12,8},{16,12},{20,16},{24,20},{28,24},{5,1},{9,5},{13... | collective-permute-start | bytes 46088 | tf_op jit(solution)/shard_map/ppermute | solution.py:26
  15.2 3.0 %collective-permute-start.3 = (bf16[7680]{0:T(1024)(128)(2,1)S(1)}, bf16[7680]{0:T(1024)(128)(2,1)S(1)}, u32[]{:S(2)}, u32[]{:S(2)}) collective-permute-start(bf16[7680]{0:T(1024)(128)(2,1)S(1)} %pad_maximum_fusion.10), channel_id=1, source_target_pairs={{0,4},{4,8},{8,12},{12,16},{16,20},{20,24},{24,28},{1,5},{5,9},{9,... | collective-permute-start | bytes 46088 | tf_op jit(solution)/shard_map/ppermute | solution.py:25
  18.3 0.7 fusion.47
  19.0 0.7 fusion.45
  19.7 0.7 fusion.49
  20.6 0.7 slice_dynamic-update-slice_fusion.2
  21.4 0.7 slice_dynamic-update-slice_fusion.1
  22.1 0.8 slice_dynamic-update-slice_fusion
  22.9 0.8 fusion.43
  23.6 0.7 fusion.41
  24.4 0.8 fusion.48
  27.5 2.1 %fusion.83 = f32[34,18,128]{2,0,1:T(8,128)S(1)} fusion(bf16[34,18,1152]{2,0,1:T(8,128)(2,1)} %fusion.48, bf16[1152,128,1]{1,0,2:T(8,128)(2,1)S(1)} %bitcast.165), kind=kOutput, calls=%fused_computation.207 | convolution fusion | flops 180486144 | bytes 2018304 | tf_op jit(solution)/shard_map/rck,kn->rcn/dot_general | solution.py:119
  34.3 0.6 slice.398
  34.9 0.6 slice.399
  35.5 0.7 slice.400
  36.2 0.7 slice.401
  37.5 0.5 fusion
  38.0 1.1 %convolution_convert_fusion = bf16[32,16,128]{2,1,0:T(8,128)(2,1)} fusion(bf16[32,16,1152]{2,1,0:T(8,128)(2,1)S(1)} %slice_dynamic-update-slice_fusion.3, bf16[1152,128,1]{1,0,2:T(8,128)(2,1)S(1)} %bitcast.166), kind=kOutput, calls=%fused_computation.4 | convolution fusion | flops 151060480 | bytes 1605632 | tf_op jit(solution)/shard_map/rck,kn->rcn/dot_general | solution.py:129
  39.4 0.5 fusion.3
  40.4 1.7 %collective-permute-start.10 = (bf16[2,656,128]{2,1,0:T(8,128)(2,1)S(1)}, bf16[2,656,128]{2,1,0:T(8,128)(2,1)S(1)}, u32[]{:S(2)}, u32[]{:S(2)}) collective-permute-start(bf16[2,656,128]{2,1,0:T(8,128)(2,1)S(1)} %fusion.14), channel_id=1, source_target_pairs={{0,2},{1,3},{2,0},{3,1},{4,6},{5,7},{6,4},{7,5},{8,10},{9,11},{10,... | collective-permute-start | bytes 1007624 | tf_op jit(solution)/shard_map/ppermute | solution.py:166
  42.1 0.9 %collective-permute-start.4 = (bf16[2,656,128]{2,1,0:T(8,128)(2,1)S(1)}, bf16[2,656,128]{2,1,0:T(8,128)(2,1)S(1)}, u32[]{:S(2)}, u32[]{:S(2)}) collective-permute-start(bf16[2,656,128]{2,1,0:T(8,128)(2,1)S(1)} %fusion.13), channel_id=1, source_target_pairs={{0,1},{1,0},{2,3},{3,2},{4,5},{5,4},{6,7},{7,6},{8,9},{9,8},{10,11... | collective-permute-start | bytes 1007624 | tf_op jit(solution)/shard_map/ppermute | solution.py:166
  43.0 1.0 %fusion.84 = f32[16,8,256]{2,1,0:T(8,128)} fusion(bf16[16,8,2048]{2,1,0:T(8,128)(2,1)S(1)} %constant_dynamic-update-slice_fusion.2, bf16[2048,256,1]{1,0,2:T(8,128)(2,1)S(1)} %bitcast.158), kind=kOutput, calls=%fused_computation.208 | convolution fusion | flops 134217728 | bytes 1703936 | tf_op jit(solution)/shard_map/rck,kn->rcn/dot_general | solution.py:142
  44.0 7.0 %collective-permute-done.10 = bf16[2,656,128]{2,1,0:T(8,128)(2,1)S(1)} collective-permute-done((bf16[2,656,128]{2,1,0:T(8,128)(2,1)S(1)}, bf16[2,656,128]{2,1,0:T(8,128)(2,1)S(1)}, u32[]{:S(2)}, u32[]{:S(2)}) %collective-permute-start.10) | collective-permute-done | bytes 335904 | tf_op jit(solution)/shard_map/ppermute | solution.py:166
  51.0 2.5 %collective-permute-start.11 = (bf16[656,128]{1,0:T(8,128)(2,1)S(1)}, bf16[656,128]{1,0:T(8,128)(2,1)S(1)}, u32[]{:S(2)}, u32[]{:S(2)}) collective-permute-start(bf16[656,128]{1,0:T(8,128)(2,1)S(1)} %fusion.51), channel_id=1, source_target_pairs={{0,1},{1,0},{2,3},{3,2},{4,5},{5,4},{6,7},{7,6},{8,9},{9,8},{10,11... | collective-permute-start | bytes 503816 | tf_op jit(solution)/shard_map/ppermute | solution.py:166
  53.8 4.4 %collective-permute-done.11 = bf16[656,128]{1,0:T(8,128)(2,1)S(1)} collective-permute-done((bf16[656,128]{1,0:T(8,128)(2,1)S(1)}, bf16[656,128]{1,0:T(8,128)(2,1)S(1)}, u32[]{:S(2)}, u32[]{:S(2)}) %collective-permute-start.11) | collective-permute-done | bytes 167968 | tf_op jit(solution)/shard_map/ppermute | solution.py:166
  58.3 1.5 %collective-permute-done.5 = bf16[656,128]{1,0:T(8,128)(2,1)S(1)} collective-permute-done((bf16[656,128]{1,0:T(8,128)(2,1)S(1)}, bf16[656,128]{1,0:T(8,128)(2,1)S(1)}, u32[]{:S(2)}, u32[]{:S(2)}) %collective-permute-start.5) | collective-permute-done | bytes 167968 | tf_op jit(solution)/shard_map/ppermute | solution.py:166
  60.0 1.8 %collective-permute-start.13 = (bf16[328,128]{1,0:T(8,128)(2,1)S(1)}, bf16[328,128]{1,0:T(8,128)(2,1)S(1)}, u32[]{:S(2)}, u32[]{:S(2)}) collective-permute-start(bf16[328,128]{1,0:T(8,128)(2,1)S(1)} %fusion.52), channel_id=1, source_target_pairs={{0,8},{4,12},{8,0},{12,4},{16,24},{20,28},{24,16},{28,20},{1,9},{5... | collective-permute-start | bytes 251912 | tf_op jit(solution)/shard_map/ppermute | solution.py:166
  61.8 1.2 %collective-permute-start.7 = (bf16[328,128]{1,0:T(8,128)(2,1)S(1)}, bf16[328,128]{1,0:T(8,128)(2,1)S(1)}, u32[]{:S(2)}, u32[]{:S(2)}) collective-permute-start(bf16[328,128]{1,0:T(8,128)(2,1)S(1)} %fusion.53), channel_id=1, source_target_pairs={{0,8},{4,12},{8,0},{12,4},{16,24},{20,28},{24,16},{28,20},{1,9},{5... | collective-permute-start | bytes 251912 | tf_op jit(solution)/shard_map/ppermute | solution.py:166
  63.1 2.1 %collective-permute-done.13 = bf16[328,128]{1,0:T(8,128)(2,1)S(1)} collective-permute-done((bf16[328,128]{1,0:T(8,128)(2,1)S(1)}, bf16[328,128]{1,0:T(8,128)(2,1)S(1)}, u32[]{:S(2)}, u32[]{:S(2)}) %collective-permute-start.13) | collective-permute-done | bytes 84000 | tf_op jit(solution)/shard_map/ppermute | solution.py:166
  65.2 3.0 %collective-permute-start.14 = (bf16[328,128]{1,0:T(8,128)(2,1)S(1)}, bf16[328,128]{1,0:T(8,128)(2,1)S(1)}, u32[]{:S(2)}, u32[]{:S(2)}) collective-permute-start(bf16[328,128]{1,0:T(8,128)(2,1)S(1)} %add_convert_fusion.2), channel_id=1, source_target_pairs={{0,16},{4,20},{8,24},{12,28},{16,0},{20,4},{24,8},{28,12},{1,17},{... | collective-permute-start | bytes 251912 | tf_op jit(solution)/shard_map/ppermute | solution.py:166
  68.3 1.4 %collective-permute-start.8 = (bf16[328,128]{1,0:T(8,128)(2,1)S(1)}, bf16[328,128]{1,0:T(8,128)(2,1)S(1)}, u32[]{:S(2)}, u32[]{:S(2)}) collective-permute-start(bf16[328,128]{1,0:T(8,128)(2,1)S(1)} %add_convert_fusion.4), channel_id=1, source_target_pairs={{0,16},{4,20},{8,24},{12,28},{16,0},{20,4},{24,8},{28,12},{1,17},{... | collective-permute-start | bytes 251912 | tf_op jit(solution)/shard_map/ppermute | solution.py:166
  69.6 4.7 %collective-permute-done.14 = bf16[328,128]{1,0:T(8,128)(2,1)S(1)} collective-permute-done((bf16[328,128]{1,0:T(8,128)(2,1)S(1)}, bf16[328,128]{1,0:T(8,128)(2,1)S(1)}, u32[]{:S(2)}, u32[]{:S(2)}) %collective-permute-start.14) | collective-permute-done | bytes 84000 | tf_op jit(solution)/shard_map/ppermute | solution.py:166
  74.4 1.3 %collective-permute-done.8 = bf16[328,128]{1,0:T(8,128)(2,1)S(1)} collective-permute-done((bf16[328,128]{1,0:T(8,128)(2,1)S(1)}, bf16[328,128]{1,0:T(8,128)(2,1)S(1)}, u32[]{:S(2)}, u32[]{:S(2)}) %collective-permute-start.8) | collective-permute-done | bytes 84000 | tf_op jit(solution)/shard_map/ppermute | solution.py:166
  75.9 1.2 %collective-permute-done.9 = bf16[328,128]{1,0:T(8,128)(2,1)S(1)} collective-permute-done((bf16[328,128]{1,0:T(8,128)(2,1)S(1)}, bf16[328,128]{1,0:T(8,128)(2,1)S(1)}, u32[]{:S(2)}, u32[]{:S(2)}) %collective-permute-start.9) | collective-permute-done | bytes 84000 | tf_op jit(solution)/shard_map/ppermute | solution.py:166
  77.2 0.8 %slice.445 = f32[1024,128]{1,0:T(8,128)} slice(f32[1312,128]{1,0:T(8,128)S(1)} %convert_multiply_fusion), slice={[0:1024], [0:128]} | slice | bytes 1048576 | tf_op jit(solution)/shard_map/slice | solution.py:159
  78.0 0.7 slice.446
  (142 shorter events, 11.0 us)
Async XLA Ops:
  0.6 2.3 %copy-start.3 = (s32[16,8,256]{2,1,0:T(8,128)S(1)}, s32[16,8,256]{2,1,0:T(8,128)}, u32[]{:S(2)}) copy-start(s32[16,8,256]{2,1,0:T(8,128)} %param.6) | copy-start | bytes 393220
  0.6 7.7 %copy-start = (bf16[4,4,256,128]{3,2,1,0:T(8,128)(2,1)S(1)}, bf16[4,4,256,128]{3,2,1,0:T(8,128)(2,1)}, u32[]{:S(2)}) copy-start(bf16[4,4,256,128]{3,2,1,0:T(8,128)(2,1)} %param.8) | copy-start | bytes 3145732
  3.8 6.5 %collective-permute-start = (bf16[12288]{0:T(1024)(128)(2,1)}, bf16[12288]{0:T(1024)(128)(2,1)}, u32[]{:S(2)}, u32[]{:S(2)}) collective-permute-start(bf16[12288]{0:T(1024)(128)(2,1)} %pad_maximum_fusion.7), channel_id=1, source_target_pairs={{0,1},{1,2},{2,3},{3,0},{4,5},{5,6},{6,7},{7,4},{8,9},{9,10},{10,1... | collective-permute-start | bytes 73736 | tf_op jit(solution)/shard_map/ppermute | solution.py:25
  7.4 4.1 %collective-permute-start.1 = (bf16[12288]{0:T(1024)(128)(2,1)}, bf16[12288]{0:T(1024)(128)(2,1)}, u32[]{:S(2)}, u32[]{:S(2)}) collective-permute-start(bf16[12288]{0:T(1024)(128)(2,1)} %pad_maximum_fusion.8), channel_id=1, source_target_pairs={{1,0},{2,1},{3,2},{0,3},{5,4},{6,5},{7,6},{4,7},{9,8},{10,9},{11,1... | collective-permute-start | bytes 73736 | tf_op jit(solution)/shard_map/ppermute | solution.py:26
  9.1 1.0 %copy-start.1 = (bf16[3,3,128,128]{3,2,1,0:T(8,128)(2,1)S(1)}, bf16[3,3,128,128]{3,2,1,0:T(8,128)(2,1)}, u32[]{:S(2)}) copy-start(bf16[3,3,128,128]{3,2,1,0:T(8,128)(2,1)} %param.10) | copy-start | bytes 884740
  9.1 1.9 %copy-start.2 = (bf16[32,16,128]{2,1,0:T(8,128)(2,1)S(1)}, bf16[32,16,128]{2,1,0:T(8,128)(2,1)}, u32[]{:S(2)}) copy-start(bf16[32,16,128]{2,1,0:T(8,128)(2,1)} %param.11) | copy-start | bytes 393220
  13.8 4.4 %collective-permute-start.2 = (bf16[7680]{0:T(1024)(128)(2,1)S(1)}, bf16[7680]{0:T(1024)(128)(2,1)S(1)}, u32[]{:S(2)}, u32[]{:S(2)}) collective-permute-start(bf16[7680]{0:T(1024)(128)(2,1)S(1)} %pad_maximum_fusion.9), channel_id=1, source_target_pairs={{4,0},{8,4},{12,8},{16,12},{20,16},{24,20},{28,24},{5,1},{9,5},{13... | collective-permute-start | bytes 46088 | tf_op jit(solution)/shard_map/ppermute | solution.py:26
  15.2 5.3 %collective-permute-start.3 = (bf16[7680]{0:T(1024)(128)(2,1)S(1)}, bf16[7680]{0:T(1024)(128)(2,1)S(1)}, u32[]{:S(2)}, u32[]{:S(2)}) collective-permute-start(bf16[7680]{0:T(1024)(128)(2,1)S(1)} %pad_maximum_fusion.10), channel_id=1, source_target_pairs={{0,4},{4,8},{8,12},{12,16},{16,20},{20,24},{24,28},{1,5},{5,9},{9,... | collective-permute-start | bytes 46088 | tf_op jit(solution)/shard_map/ppermute | solution.py:25
  22.1 3.2 %copy-start.6 = (bf16[256,128]{1,0:T(8,128)(2,1)S(1)}, bf16[256,128]{1,0:T(8,128)(2,1)}, u32[]{:S(2)}) copy-start(bf16[256,128]{1,0:T(8,128)(2,1)} %get-tuple-element.9) | copy-start | bytes 196612
  22.1 3.2 %copy-start.7 = (bf16[256,128]{1,0:T(8,128)(2,1)S(1)}, bf16[256,128]{1,0:T(8,128)(2,1)}, u32[]{:S(2)}) copy-start(bf16[256,128]{1,0:T(8,128)(2,1)} %get-tuple-element.10) | copy-start | bytes 196612
  22.1 3.2 %copy-start.8 = (bf16[256,128]{1,0:T(8,128)(2,1)S(1)}, bf16[256,128]{1,0:T(8,128)(2,1)}, u32[]{:S(2)}) copy-start(bf16[256,128]{1,0:T(8,128)(2,1)} %get-tuple-element.11) | copy-start | bytes 196612
  22.1 3.2 %copy-start.9 = (bf16[256,128]{1,0:T(8,128)(2,1)S(1)}, bf16[256,128]{1,0:T(8,128)(2,1)}, u32[]{:S(2)}) copy-start(bf16[256,128]{1,0:T(8,128)(2,1)} %get-tuple-element.23) | copy-start | bytes 196612
  25.3 0.8 %copy-start.4 = (bf16[256,128]{1,0:T(8,128)(2,1)S(1)}, bf16[256,128]{1,0:T(8,128)(2,1)}, u32[]{:S(2)}) copy-start(bf16[256,128]{1,0:T(8,128)(2,1)} %get-tuple-element.14) | copy-start | bytes 196612
  25.3 0.9 %copy-start.5 = (bf16[256,128]{1,0:T(8,128)(2,1)S(1)}, bf16[256,128]{1,0:T(8,128)(2,1)}, u32[]{:S(2)}) copy-start(bf16[256,128]{1,0:T(8,128)(2,1)} %get-tuple-element.15) | copy-start | bytes 196612
  27.5 2.1 %copy-start.10 = (f32[128]{0:T(128)S(1)}, f32[128]{0:T(128)}, u32[]{:S(2)}) copy-start(f32[128]{0:T(128)} %param.9) | copy-start | bytes 1540
  40.4 10.5 %collective-permute-start.10 = (bf16[2,656,128]{2,1,0:T(8,128)(2,1)S(1)}, bf16[2,656,128]{2,1,0:T(8,128)(2,1)S(1)}, u32[]{:S(2)}, u32[]{:S(2)}) collective-permute-start(bf16[2,656,128]{2,1,0:T(8,128)(2,1)S(1)} %fusion.14), channel_id=1, source_target_pairs={{0,2},{1,3},{2,0},{3,1},{4,6},{5,7},{6,4},{7,5},{8,10},{9,11},{10,... | collective-permute-start | bytes 1007624 | tf_op jit(solution)/shard_map/ppermute | solution.py:166
  42.1 11.5 %collective-permute-start.4 = (bf16[2,656,128]{2,1,0:T(8,128)(2,1)S(1)}, bf16[2,656,128]{2,1,0:T(8,128)(2,1)S(1)}, u32[]{:S(2)}, u32[]{:S(2)}) collective-permute-start(bf16[2,656,128]{2,1,0:T(8,128)(2,1)S(1)} %fusion.13), channel_id=1, source_target_pairs={{0,1},{1,0},{2,3},{3,2},{4,5},{5,4},{6,7},{7,6},{8,9},{9,8},{10,11... | collective-permute-start | bytes 1007624 | tf_op jit(solution)/shard_map/ppermute | solution.py:166
  51.0 7.1 %collective-permute-start.11 = (bf16[656,128]{1,0:T(8,128)(2,1)S(1)}, bf16[656,128]{1,0:T(8,128)(2,1)S(1)}, u32[]{:S(2)}, u32[]{:S(2)}) collective-permute-start(bf16[656,128]{1,0:T(8,128)(2,1)S(1)} %fusion.51), channel_id=1, source_target_pairs={{0,1},{1,0},{2,3},{3,2},{4,5},{5,4},{6,7},{7,6},{8,9},{9,8},{10,11... | collective-permute-start | bytes 503816 | tf_op jit(solution)/shard_map/ppermute | solution.py:166
  53.7 6.1 %collective-permute-start.5 = (bf16[656,128]{1,0:T(8,128)(2,1)S(1)}, bf16[656,128]{1,0:T(8,128)(2,1)S(1)}, u32[]{:S(2)}, u32[]{:S(2)}) collective-permute-start(bf16[656,128]{1,0:T(8,128)(2,1)S(1)} %fusion.50), channel_id=1, source_target_pairs={{0,2},{1,3},{2,0},{3,1},{4,6},{5,7},{6,4},{7,5},{8,10},{9,11},{10,... | collective-permute-start | bytes 503816 | tf_op jit(solution)/shard_map/ppermute | solution.py:166
  58.2 1.7 %collective-permute-start.12 = (bf16[328,128]{1,0:T(8,128)(2,1)S(1)}, bf16[328,128]{1,0:T(8,128)(2,1)S(1)}, u32[]{:S(2)}, u32[]{:S(2)}) collective-permute-start(bf16[328,128]{1,0:T(8,128)(2,1)S(1)} %fusion.71), channel_id=1, source_target_pairs={{0,4},{4,0},{8,12},{12,8},{16,20},{20,16},{24,28},{28,24},{1,5},{5... | collective-permute-start | bytes 251912 | tf_op jit(solution)/shard_map/ppermute | solution.py:166
  59.9 2.0 %collective-permute-start.6 = (bf16[328,128]{1,0:T(8,128)(2,1)S(1)}, bf16[328,128]{1,0:T(8,128)(2,1)S(1)}, u32[]{:S(2)}, u32[]{:S(2)}) collective-permute-start(bf16[328,128]{1,0:T(8,128)(2,1)S(1)} %fusion.70), channel_id=1, source_target_pairs={{0,4},{4,0},{8,12},{12,8},{16,20},{20,16},{24,28},{28,24},{1,5},{5... | collective-permute-start | bytes 251912 | tf_op jit(solution)/shard_map/ppermute | solution.py:166
  60.0 5.2 %collective-permute-start.13 = (bf16[328,128]{1,0:T(8,128)(2,1)S(1)}, bf16[328,128]{1,0:T(8,128)(2,1)S(1)}, u32[]{:S(2)}, u32[]{:S(2)}) collective-permute-start(bf16[328,128]{1,0:T(8,128)(2,1)S(1)} %fusion.52), channel_id=1, source_target_pairs={{0,8},{4,12},{8,0},{12,4},{16,24},{20,28},{24,16},{28,20},{1,9},{5... | collective-permute-start | bytes 251912 | tf_op jit(solution)/shard_map/ppermute | solution.py:166
  61.8 6.4 %collective-permute-start.7 = (bf16[328,128]{1,0:T(8,128)(2,1)S(1)}, bf16[328,128]{1,0:T(8,128)(2,1)S(1)}, u32[]{:S(2)}, u32[]{:S(2)}) collective-permute-start(bf16[328,128]{1,0:T(8,128)(2,1)S(1)} %fusion.53), channel_id=1, source_target_pairs={{0,8},{4,12},{8,0},{12,4},{16,24},{20,28},{24,16},{28,20},{1,9},{5... | collective-permute-start | bytes 251912 | tf_op jit(solution)/shard_map/ppermute | solution.py:166
  65.2 9.1 %collective-permute-start.14 = (bf16[328,128]{1,0:T(8,128)(2,1)S(1)}, bf16[328,128]{1,0:T(8,128)(2,1)S(1)}, u32[]{:S(2)}, u32[]{:S(2)}) collective-permute-start(bf16[328,128]{1,0:T(8,128)(2,1)S(1)} %add_convert_fusion.2), channel_id=1, source_target_pairs={{0,16},{4,20},{8,24},{12,28},{16,0},{20,4},{24,8},{28,12},{1,17},{... | collective-permute-start | bytes 251912 | tf_op jit(solution)/shard_map/ppermute | solution.py:166
  68.3 7.5 %collective-permute-start.8 = (bf16[328,128]{1,0:T(8,128)(2,1)S(1)}, bf16[328,128]{1,0:T(8,128)(2,1)S(1)}, u32[]{:S(2)}, u32[]{:S(2)}) collective-permute-start(bf16[328,128]{1,0:T(8,128)(2,1)S(1)} %add_convert_fusion.4), channel_id=1, source_target_pairs={{0,16},{4,20},{8,24},{12,28},{16,0},{20,4},{24,8},{28,12},{1,17},{... | collective-permute-start | bytes 251912 | tf_op jit(solution)/shard_map/ppermute | solution.py:166
  74.3 1.5 %collective-permute-start.15 = (bf16[328,128]{1,0:T(8,128)(2,1)S(1)}, bf16[328,128]{1,0:T(8,128)(2,1)S(1)}, u32[]{:S(2)}, u32[]{:S(2)}) collective-permute-start(bf16[328,128]{1,0:T(8,128)(2,1)S(1)} %add_convert_fusion.1), channel_id=1, source_target_pairs={{0,4},{4,0},{8,12},{12,8},{16,20},{20,16},{24,28},{28,24},{1,5},{5... | collective-permute-start | bytes 251912 | tf_op jit(solution)/shard_map/ppermute | solution.py:166
  75.7 1.3 %collective-permute-start.9 = (bf16[328,128]{1,0:T(8,128)(2,1)S(1)}, bf16[328,128]{1,0:T(8,128)(2,1)S(1)}, u32[]{:S(2)}, u32[]{:S(2)}) collective-permute-start(bf16[328,128]{1,0:T(8,128)(2,1)S(1)} %add_convert_fusion.3), channel_id=1, source_target_pairs={{0,4},{4,0},{8,12},{12,8},{16,20},{20,16},{24,28},{28,24},{1,5},{5... | collective-permute-start | bytes 251912 | tf_op jit(solution)/shard_map/ppermute | solution.py:166

commit v8 on v7

--- a/solution.py
+++ b/solution.py
@@ -93,11 +93,18 @@
 
 
 def strided(padded, row_count, col_count):
+    split = padded.reshape(row_count + 1, 2, col_count + 1, 2, padded.shape[-1])
     pieces = []
     for row_tap in range(4):
         for col_tap in range(4):
+            row_at, col_at = (row_tap // 2, col_tap // 2)
             pieces.append(
-                padded[row_tap : row_tap + 2 * row_count : 2, col_tap : col_tap + 2 * col_count : 2]
+                split[
+                    row_at : row_at + row_count,
+                    row_tap % 2,
+                    col_at : col_at + col_count,
+                    col_tap % 2,
+                ]
             )
     return jnp.concatenate(pieces, axis=2)
 

time: 79.2 us -> 73.3 us (0.926)
  local copies, waits for them, and re-layouts: 19.2 us -> 13.4 us
    slice x16 -> x1, local copies, waits for them, and re-layouts: 6.96 us -> 0.75 us  [strided(): split[row_at:row_at + row_count, row_tap % 2, col_at:col_at + col_count,...]
    unnamed x55 -> x70, local copies, waits for them, and re-layouts: 4.57 us -> 4.83 us
  transfers between devices with their start and end apart: 16 -> 16, of which waited for: 8 -> 8; matrix products, arithmetic and copies ran while one was open for 8% -> 9% of each run, Pallas kernels for 0% -> 0%
where the time goes in v8:
time: 73.3 us; the launch traced here: 72.8 us
  waiting for transfers between devices  22.6 us (31%)
  starting transfers between devices  21.1 us (29%)
  local copies, waits for them, and re-layouts  13.4 us (18%)
  other arithmetic  7.87 us (11%)
  matrix products  6.32 us (9%)
  between operations  1.53 us (2%)
    ppermute x12, waiting for transfers between devices, exchange(): return lax.ppermute(part, axis, [(i, i ^ step) for i in range(size)])  22.2 us
    ppermute x12, starting transfers between devices, exchange(): return lax.ppermute(part, axis, [(i, i ^ step) for i in range(size)])  12.9 us
    ppermute x2, starting transfers between devices, swap_edges(): lax.ppermute(jnp.concatenate([p.reshape(-1) for p in lasts]), axis, up)  5.97 us
    unnamed x70, local copies, waits for them, and re-layouts  4.83 us
    unnamed x5, other arithmetic  3.67 us
    ppermute x2, starting transfers between devices, swap_edges(): lax.ppermute(jnp.concatenate([p.reshape(-1) for p in leads]), axis, down)  2.25 us
    dot_general x1, matrix products, shards(): jnp.einsum('rck,kn->rcn', neighbours(grad_pad, out_rows + 2, out_cols + 2...  2.09 us
    slice x8, local copies, waits for them, and re-layouts, swap_edges(): tail = after[at:at + count].reshape(lead.shape)  1.48 us
  transfers between devices with their start and end apart: 16, of which 8 were waited for; matrix products, arithmetic and copies ran while one was open for 9% of the time, Pallas kernels for 0%

profile of v8, /device:TPU:0, one launch (start us, length us, event | category | flops | bytes accessed | tf_op | source)
XLA Modules:
  0.0 72.8 jit_solution(14324142143582567506)
XLA Ops:
  0.7 1.0 %fusion.81 = (bf16[32,2,128]{2,1,0:T(2,128)(2,1)S(1)}, bf16[32,2,128]{2,1,0:T(2,128)(2,1)S(1)}) fusion(bf16[32,16,128]{2,1,0:T(8,128)(2,1)} %param.11), kind=kLoop, calls=%fused_computation.221 | loop fusion | bytes 65536 | tf_op jit(solution)/shard_map/slice | solution.py:23
  1.7 0.8 %multiply_exponential_fusion = f32[16,8,8]{0,2,1:T(8,128)S(1)} fusion(s32[16,8,8]{0,2,1:T(8,128)} %param.7), kind=kLoop, calls=%fused_computation.202 | loop fusion | flops 2048 | bytes 8192 | tf_op jit(solution)/shard_map/exp2 | solution.py:50
  3.2 0.6 pad_maximum_fusion.7
  3.8 2.9 %collective-permute-start = (bf16[12288]{0:T(1024)(128)(2,1)}, bf16[12288]{0:T(1024)(128)(2,1)}, u32[]{:S(2)}, u32[]{:S(2)}) collective-permute-start(bf16[12288]{0:T(1024)(128)(2,1)} %pad_maximum_fusion.7), channel_id=1, source_target_pairs={{0,1},{1,2},{2,3},{3,0},{4,5},{5,6},{6,7},{7,4},{8,9},{9,10},{10,1... | collective-permute-start | bytes 73736 | tf_op jit(solution)/shard_map/ppermute | solution.py:25
  6.8 0.6 pad_maximum_fusion.8
  7.4 1.0 %collective-permute-start.1 = (bf16[12288]{0:T(1024)(128)(2,1)}, bf16[12288]{0:T(1024)(128)(2,1)}, u32[]{:S(2)}, u32[]{:S(2)}) collective-permute-start(bf16[12288]{0:T(1024)(128)(2,1)} %pad_maximum_fusion.8), channel_id=1, source_target_pairs={{1,0},{2,1},{3,2},{0,3},{5,4},{6,5},{7,6},{4,7},{9,8},{10,9},{11,1... | collective-permute-start | bytes 73736 | tf_op jit(solution)/shard_map/ppermute | solution.py:26
  8.4 0.8 %slice_bitcast_fusion.15 = (bf16[256,128]{1,0:T(8,128)(2,1)S(1)}, bf16[256,128]{1,0:T(8,128)(2,1)}, bf16[256,128]{1,0:T(8,128)(2,1)}, bf16[256,128]{1,0:T(8,128)...) fusion(bf16[4,4,256,128]{3,2,1,0:T(8,128)(2,1)S(1)} %copy-done), kind=kLoop, calls=%fused_computation.201 | loop fusion | bytes 2097152 | tf_op jit(solution)/shard_map/squeeze | solution.py:74
  9.1 0.5 copy.73
  9.7 0.3 copy-done.1
  10.3 0.7 slice.412
  11.1 0.4 collective-permute-done.1
  11.5 0.7 slice.413
  12.3 0.7 slice.411
  13.0 0.7 slice.409
  13.8 1.3 %collective-permute-start.2 = (bf16[7680]{0:T(1024)(128)(2,1)S(1)}, bf16[7680]{0:T(1024)(128)(2,1)S(1)}, u32[]{:S(2)}, u32[]{:S(2)}) collective-permute-start(bf16[7680]{0:T(1024)(128)(2,1)S(1)} %pad_maximum_fusion.9), channel_id=1, source_target_pairs={{4,0},{8,4},{12,8},{16,12},{20,16},{24,20},{28,24},{5,1},{9,5},{13... | collective-permute-start | bytes 46088 | tf_op jit(solution)/shard_map/ppermute | solution.py:26
  15.2 3.0 %collective-permute-start.3 = (bf16[7680]{0:T(1024)(128)(2,1)S(1)}, bf16[7680]{0:T(1024)(128)(2,1)S(1)}, u32[]{:S(2)}, u32[]{:S(2)}) collective-permute-start(bf16[7680]{0:T(1024)(128)(2,1)S(1)} %pad_maximum_fusion.10), channel_id=1, source_target_pairs={{0,4},{4,8},{8,12},{12,16},{16,20},{20,24},{24,28},{1,5},{5,9},{9,... | collective-permute-start | bytes 46088 | tf_op jit(solution)/shard_map/ppermute | solution.py:25
  18.3 0.7 fusion.47
  19.0 0.7 fusion.45
  19.7 0.7 fusion.49
  20.6 0.8 %slice_dynamic-update-slice_fusion.2 = bf16[34,18,1152]{2,0,1:T(8,128)(2,1)} fusion(bf16[34,18,1152]{2,0,1:T(8,128)(2,1)} %fusion.49, bf16[36,20,128]{2,0,1:T(8,128)(2,1)S(1)} %pad_maximum_fusion.3), kind=kLoop, calls=%fused_computation.101 | loop fusion | bytes 340992
  21.4 0.7 %slice_dynamic-update-slice_fusion.1 = bf16[34,18,1152]{2,0,1:T(8,128)(2,1)} fusion(bf16[34,18,1152]{2,0,1:T(8,128)(2,1)} %slice_dynamic-update-slice_fusion.2, bf16[36,20,128]{2,0,1:T(8,128)(2,1)S(1)} %pad_maximum_fusion.3), kind=kLoop, calls=%fused_computation.100 | loop fusion | bytes 340992
  22.1 0.7 %slice_dynamic-update-slice_fusion = bf16[34,18,1152]{2,0,1:T(8,128)(2,1)} fusion(bf16[34,18,1152]{2,0,1:T(8,128)(2,1)} %slice_dynamic-update-slice_fusion.1, bf16[36,20,128]{2,0,1:T(8,128)(2,1)S(1)} %pad_maximum_fusion.3), kind=kLoop, calls=%fused_computation.99 | loop fusion | bytes 340992
  22.8 0.8 %fusion.43 = bf16[34,18,1152]{2,0,1:T(8,128)(2,1)} fusion(bf16[34,18,1152]{2,0,1:T(8,128)(2,1)} %slice_dynamic-update-slice_fusion, bf16[32,20,128]{2,0,1:T(8,128)(2,1)S(1)} %constant_dynamic-update-slice_fusion, bf16[2,20,128]{2,0,1:T(2,128)(2,1)S(1)} %copy.51), kind=kLoop, calls=%fused_computation.92 | loop fusion | flops 313344 | bytes 358400
  23.6 0.8 %fusion.41 = bf16[34,18,1152]{2,0,1:T(8,128)(2,1)} fusion(bf16[34,18,1152]{2,0,1:T(8,128)(2,1)} %fusion.43, bf16[32,20,128]{2,0,1:T(8,128)(2,1)S(1)} %constant_dynamic-update-slice_fusion, bf16[2,20,128]{2,0,1:T(2,128)(2,1)S(1)} %copy.51), kind=kLoop, calls=%fused_computation.90 | loop fusion | flops 313344 | bytes 358400
  24.4 0.7 %fusion.48 = bf16[34,18,1152]{2,0,1:T(8,128)(2,1)} fusion(bf16[34,18,1152]{2,0,1:T(8,128)(2,1)} %fusion.41, bf16[32,20,128]{2,0,1:T(8,128)(2,1)S(1)} %constant_dynamic-update-slice_fusion, bf16[2,20,128]{2,0,1:T(2,128)(2,1)S(1)} %copy.51), kind=kLoop, calls=%fused_computation.98 | loop fusion | flops 313344 | bytes 358400 | tf_op jit(solution)/shard_map/concatenate | solution.py:92
  25.6 0.5 copy-done.4
  27.5 2.1 %fusion.84 = f32[34,18,128]{2,0,1:T(8,128)S(1)} fusion(bf16[34,18,1152]{2,0,1:T(8,128)(2,1)} %fusion.48, bf16[1152,128,1]{1,0,2:T(8,128)(2,1)S(1)} %bitcast.228), kind=kOutput, calls=%fused_computation.224 | convolution fusion | flops 180486144 | bytes 2018304 | tf_op jit(solution)/shard_map/rck,kn->rcn/dot_general | solution.py:126
  30.1 0.7 %fusion.80 = (bf16[16,1,8,1,128]{4,3,2,1,0:T(2,128)(2,1)S(1)}, bf16[16,1,8,1,128]{4,3,2,1,0:T(2,128)(2,1)S(1)}, bf16[16,1,8,1,128]{4,3,2,1,0:T(2,128)(2,1)S(1)},...) fusion(bf16[17,2,9,2,128]{4,3,2,1,0:T(2,128)(2,1)S(1)} %reshape.243), kind=kLoop, calls=%fused_computation.220 | loop fusion | bytes 1048576 | tf_op jit(solution)/shard_map/slice | solution.py:102
  31.3 0.5 fusion
  31.9 1.1 %convolution_convert_fusion = bf16[32,16,128]{2,1,0:T(8,128)(2,1)} fusion(bf16[32,16,1152]{2,1,0:T(8,128)(2,1)S(1)} %slice_dynamic-update-slice_fusion.3, bf16[1152,128,1]{1,0,2:T(8,128)(2,1)S(1)} %bitcast.229), kind=kOutput, calls=%fused_computation.4 | convolution fusion | flops 151060480 | bytes 1605632 | tf_op jit(solution)/shard_map/rck,kn->rcn/dot_general | solution.py:136
  33.6 0.5 fusion.3
  34.5 1.7 %collective-permute-start.10 = (bf16[2,656,128]{2,1,0:T(8,128)(2,1)S(1)}, bf16[2,656,128]{2,1,0:T(8,128)(2,1)S(1)}, u32[]{:S(2)}, u32[]{:S(2)}) collective-permute-start(bf16[2,656,128]{2,1,0:T(8,128)(2,1)S(1)} %fusion.14), channel_id=1, source_target_pairs={{0,2},{1,3},{2,0},{3,1},{4,6},{5,7},{6,4},{7,5},{8,10},{9,11},{10,... | collective-permute-start | bytes 1007624 | tf_op jit(solution)/shard_map/ppermute | solution.py:173
  36.2 0.9 %collective-permute-start.4 = (bf16[2,656,128]{2,1,0:T(8,128)(2,1)S(1)}, bf16[2,656,128]{2,1,0:T(8,128)(2,1)S(1)}, u32[]{:S(2)}, u32[]{:S(2)}) collective-permute-start(bf16[2,656,128]{2,1,0:T(8,128)(2,1)S(1)} %fusion.13), channel_id=1, source_target_pairs={{0,1},{1,0},{2,3},{3,2},{4,5},{5,4},{6,7},{7,6},{8,9},{9,8},{10,11... | collective-permute-start | bytes 1007624 | tf_op jit(solution)/shard_map/ppermute | solution.py:173
  37.1 1.0 %fusion.85 = f32[16,8,256]{2,1,0:T(8,128)} fusion(bf16[16,8,2048]{2,1,0:T(8,128)(2,1)S(1)} %constant_dynamic-update-slice_fusion.2, bf16[2048,256,1]{1,0,2:T(8,128)(2,1)S(1)} %bitcast.221), kind=kOutput, calls=%fused_computation.225 | convolution fusion | flops 134217728 | bytes 1703936 | tf_op jit(solution)/shard_map/rck,kn->rcn/dot_general | solution.py:149
  38.1 7.0 %collective-permute-done.10 = bf16[2,656,128]{2,1,0:T(8,128)(2,1)S(1)} collective-permute-done((bf16[2,656,128]{2,1,0:T(8,128)(2,1)S(1)}, bf16[2,656,128]{2,1,0:T(8,128)(2,1)S(1)}, u32[]{:S(2)}, u32[]{:S(2)}) %collective-permute-start.10) | collective-permute-done | bytes 335904 | tf_op jit(solution)/shard_map/ppermute | solution.py:173
  45.1 2.5 %collective-permute-start.11 = (bf16[656,128]{1,0:T(8,128)(2,1)S(1)}, bf16[656,128]{1,0:T(8,128)(2,1)S(1)}, u32[]{:S(2)}, u32[]{:S(2)}) collective-permute-start(bf16[656,128]{1,0:T(8,128)(2,1)S(1)} %fusion.51), channel_id=1, source_target_pairs={{0,1},{1,0},{2,3},{3,2},{4,5},{5,4},{6,7},{7,6},{8,9},{9,8},{10,11... | collective-permute-start | bytes 503816 | tf_op jit(solution)/shard_map/ppermute | solution.py:173
  47.9 4.4 %collective-permute-done.11 = bf16[656,128]{1,0:T(8,128)(2,1)S(1)} collective-permute-done((bf16[656,128]{1,0:T(8,128)(2,1)S(1)}, bf16[656,128]{1,0:T(8,128)(2,1)S(1)}, u32[]{:S(2)}, u32[]{:S(2)}) %collective-permute-start.11) | collective-permute-done | bytes 167968 | tf_op jit(solution)/shard_map/ppermute | solution.py:173
  52.4 1.5 %collective-permute-done.5 = bf16[656,128]{1,0:T(8,128)(2,1)S(1)} collective-permute-done((bf16[656,128]{1,0:T(8,128)(2,1)S(1)}, bf16[656,128]{1,0:T(8,128)(2,1)S(1)}, u32[]{:S(2)}, u32[]{:S(2)}) %collective-permute-start.5) | collective-permute-done | bytes 167968 | tf_op jit(solution)/shard_map/ppermute | solution.py:173
  54.1 1.8 %collective-permute-start.13 = (bf16[328,128]{1,0:T(8,128)(2,1)S(1)}, bf16[328,128]{1,0:T(8,128)(2,1)S(1)}, u32[]{:S(2)}, u32[]{:S(2)}) collective-permute-start(bf16[328,128]{1,0:T(8,128)(2,1)S(1)} %fusion.52), channel_id=1, source_target_pairs={{0,8},{4,12},{8,0},{12,4},{16,24},{20,28},{24,16},{28,20},{1,9},{5... | collective-permute-start | bytes 251912 | tf_op jit(solution)/shard_map/ppermute | solution.py:173
  55.9 1.2 %collective-permute-start.7 = (bf16[328,128]{1,0:T(8,128)(2,1)S(1)}, bf16[328,128]{1,0:T(8,128)(2,1)S(1)}, u32[]{:S(2)}, u32[]{:S(2)}) collective-permute-start(bf16[328,128]{1,0:T(8,128)(2,1)S(1)} %fusion.53), channel_id=1, source_target_pairs={{0,8},{4,12},{8,0},{12,4},{16,24},{20,28},{24,16},{28,20},{1,9},{5... | collective-permute-start | bytes 251912 | tf_op jit(solution)/shard_map/ppermute | solution.py:173
  57.2 2.1 %collective-permute-done.13 = bf16[328,128]{1,0:T(8,128)(2,1)S(1)} collective-permute-done((bf16[328,128]{1,0:T(8,128)(2,1)S(1)}, bf16[328,128]{1,0:T(8,128)(2,1)S(1)}, u32[]{:S(2)}, u32[]{:S(2)}) %collective-permute-start.13) | collective-permute-done | bytes 84000 | tf_op jit(solution)/shard_map/ppermute | solution.py:173
  59.3 3.0 %collective-permute-start.14 = (bf16[328,128]{1,0:T(8,128)(2,1)S(1)}, bf16[328,128]{1,0:T(8,128)(2,1)S(1)}, u32[]{:S(2)}, u32[]{:S(2)}) collective-permute-start(bf16[328,128]{1,0:T(8,128)(2,1)S(1)} %add_convert_fusion.2), channel_id=1, source_target_pairs={{0,16},{4,20},{8,24},{12,28},{16,0},{20,4},{24,8},{28,12},{1,17},{... | collective-permute-start | bytes 251912 | tf_op jit(solution)/shard_map/ppermute | solution.py:173
  62.4 1.4 %collective-permute-start.8 = (bf16[328,128]{1,0:T(8,128)(2,1)S(1)}, bf16[328,128]{1,0:T(8,128)(2,1)S(1)}, u32[]{:S(2)}, u32[]{:S(2)}) collective-permute-start(bf16[328,128]{1,0:T(8,128)(2,1)S(1)} %add_convert_fusion.4), channel_id=1, source_target_pairs={{0,16},{4,20},{8,24},{12,28},{16,0},{20,4},{24,8},{28,12},{1,17},{... | collective-permute-start | bytes 251912 | tf_op jit(solution)/shard_map/ppermute | solution.py:173
  63.7 4.7 %collective-permute-done.14 = bf16[328,128]{1,0:T(8,128)(2,1)S(1)} collective-permute-done((bf16[328,128]{1,0:T(8,128)(2,1)S(1)}, bf16[328,128]{1,0:T(8,128)(2,1)S(1)}, u32[]{:S(2)}, u32[]{:S(2)}) %collective-permute-start.14) | collective-permute-done | bytes 84000 | tf_op jit(solution)/shard_map/ppermute | solution.py:173
  68.5 1.3 %collective-permute-done.8 = bf16[328,128]{1,0:T(8,128)(2,1)S(1)} collective-permute-done((bf16[328,128]{1,0:T(8,128)(2,1)S(1)}, bf16[328,128]{1,0:T(8,128)(2,1)S(1)}, u32[]{:S(2)}, u32[]{:S(2)}) %collective-permute-start.8) | collective-permute-done | bytes 84000 | tf_op jit(solution)/shard_map/ppermute | solution.py:173
  70.0 1.2 %collective-permute-done.9 = bf16[328,128]{1,0:T(8,128)(2,1)S(1)} collective-permute-done((bf16[328,128]{1,0:T(8,128)(2,1)S(1)}, bf16[328,128]{1,0:T(8,128)(2,1)S(1)}, u32[]{:S(2)}, u32[]{:S(2)}) %collective-permute-start.9) | collective-permute-done | bytes 84000 | tf_op jit(solution)/shard_map/ppermute | solution.py:173
  71.3 0.8 %slice.461 = f32[1024,128]{1,0:T(8,128)} slice(f32[1312,128]{1,0:T(8,128)S(1)} %convert_multiply_fusion), slice={[0:1024], [0:128]} | slice | bytes 1048576 | tf_op jit(solution)/shard_map/slice | solution.py:166
  72.1 0.7 slice.462
  (144 shorter events, 5.9 us)
Async XLA Ops:
  0.6 2.3 %copy-start.3 = (s32[16,8,256]{2,1,0:T(8,128)S(1)}, s32[16,8,256]{2,1,0:T(8,128)}, u32[]{:S(2)}) copy-start(s32[16,8,256]{2,1,0:T(8,128)} %param.6) | copy-start | bytes 393220
  0.6 7.7 %copy-start = (bf16[4,4,256,128]{3,2,1,0:T(8,128)(2,1)S(1)}, bf16[4,4,256,128]{3,2,1,0:T(8,128)(2,1)}, u32[]{:S(2)}) copy-start(bf16[4,4,256,128]{3,2,1,0:T(8,128)(2,1)} %param.8) | copy-start | bytes 3145732
  3.8 6.5 %collective-permute-start = (bf16[12288]{0:T(1024)(128)(2,1)}, bf16[12288]{0:T(1024)(128)(2,1)}, u32[]{:S(2)}, u32[]{:S(2)}) collective-permute-start(bf16[12288]{0:T(1024)(128)(2,1)} %pad_maximum_fusion.7), channel_id=1, source_target_pairs={{0,1},{1,2},{2,3},{3,0},{4,5},{5,6},{6,7},{7,4},{8,9},{9,10},{10,1... | collective-permute-start | bytes 73736 | tf_op jit(solution)/shard_map/ppermute | solution.py:25
  7.4 4.1 %collective-permute-start.1 = (bf16[12288]{0:T(1024)(128)(2,1)}, bf16[12288]{0:T(1024)(128)(2,1)}, u32[]{:S(2)}, u32[]{:S(2)}) collective-permute-start(bf16[12288]{0:T(1024)(128)(2,1)} %pad_maximum_fusion.8), channel_id=1, source_target_pairs={{1,0},{2,1},{3,2},{0,3},{5,4},{6,5},{7,6},{4,7},{9,8},{10,9},{11,1... | collective-permute-start | bytes 73736 | tf_op jit(solution)/shard_map/ppermute | solution.py:26
  9.1 1.0 %copy-start.1 = (bf16[3,3,128,128]{3,2,1,0:T(8,128)(2,1)S(1)}, bf16[3,3,128,128]{3,2,1,0:T(8,128)(2,1)}, u32[]{:S(2)}) copy-start(bf16[3,3,128,128]{3,2,1,0:T(8,128)(2,1)} %param.10) | copy-start | bytes 884740
  9.1 1.9 %copy-start.2 = (bf16[32,16,128]{2,1,0:T(8,128)(2,1)S(1)}, bf16[32,16,128]{2,1,0:T(8,128)(2,1)}, u32[]{:S(2)}) copy-start(bf16[32,16,128]{2,1,0:T(8,128)(2,1)} %param.11) | copy-start | bytes 393220
  13.8 4.4 %collective-permute-start.2 = (bf16[7680]{0:T(1024)(128)(2,1)S(1)}, bf16[7680]{0:T(1024)(128)(2,1)S(1)}, u32[]{:S(2)}, u32[]{:S(2)}) collective-permute-start(bf16[7680]{0:T(1024)(128)(2,1)S(1)} %pad_maximum_fusion.9), channel_id=1, source_target_pairs={{4,0},{8,4},{12,8},{16,12},{20,16},{24,20},{28,24},{5,1},{9,5},{13... | collective-permute-start | bytes 46088 | tf_op jit(solution)/shard_map/ppermute | solution.py:26
  15.2 5.2 %collective-permute-start.3 = (bf16[7680]{0:T(1024)(128)(2,1)S(1)}, bf16[7680]{0:T(1024)(128)(2,1)S(1)}, u32[]{:S(2)}, u32[]{:S(2)}) collective-permute-start(bf16[7680]{0:T(1024)(128)(2,1)S(1)} %pad_maximum_fusion.10), channel_id=1, source_target_pairs={{0,4},{4,8},{8,12},{12,16},{16,20},{20,24},{24,28},{1,5},{5,9},{9,... | collective-permute-start | bytes 46088 | tf_op jit(solution)/shard_map/ppermute | solution.py:25
  22.1 3.2 %copy-start.6 = (bf16[256,128]{1,0:T(8,128)(2,1)S(1)}, bf16[256,128]{1,0:T(8,128)(2,1)}, u32[]{:S(2)}) copy-start(bf16[256,128]{1,0:T(8,128)(2,1)} %get-tuple-element.9) | copy-start | bytes 196612
  22.1 3.2 %copy-start.7 = (bf16[256,128]{1,0:T(8,128)(2,1)S(1)}, bf16[256,128]{1,0:T(8,128)(2,1)}, u32[]{:S(2)}) copy-start(bf16[256,128]{1,0:T(8,128)(2,1)} %get-tuple-element.10) | copy-start | bytes 196612
  22.1 3.2 %copy-start.8 = (bf16[256,128]{1,0:T(8,128)(2,1)S(1)}, bf16[256,128]{1,0:T(8,128)(2,1)}, u32[]{:S(2)}) copy-start(bf16[256,128]{1,0:T(8,128)(2,1)} %get-tuple-element.11) | copy-start | bytes 196612
  22.1 3.2 %copy-start.9 = (bf16[256,128]{1,0:T(8,128)(2,1)S(1)}, bf16[256,128]{1,0:T(8,128)(2,1)}, u32[]{:S(2)}) copy-start(bf16[256,128]{1,0:T(8,128)(2,1)} %get-tuple-element.23) | copy-start | bytes 196612
  25.3 0.8 %copy-start.4 = (bf16[256,128]{1,0:T(8,128)(2,1)S(1)}, bf16[256,128]{1,0:T(8,128)(2,1)}, u32[]{:S(2)}) copy-start(bf16[256,128]{1,0:T(8,128)(2,1)} %get-tuple-element.14) | copy-start | bytes 196612
  25.3 0.9 %copy-start.5 = (bf16[256,128]{1,0:T(8,128)(2,1)S(1)}, bf16[256,128]{1,0:T(8,128)(2,1)}, u32[]{:S(2)}) copy-start(bf16[256,128]{1,0:T(8,128)(2,1)} %get-tuple-element.15) | copy-start | bytes 196612
  27.5 2.1 %copy-start.10 = (f32[128]{0:T(128)S(1)}, f32[128]{0:T(128)}, u32[]{:S(2)}) copy-start(f32[128]{0:T(128)} %param.9) | copy-start | bytes 1540
  34.5 10.5 %collective-permute-start.10 = (bf16[2,656,128]{2,1,0:T(8,128)(2,1)S(1)}, bf16[2,656,128]{2,1,0:T(8,128)(2,1)S(1)}, u32[]{:S(2)}, u32[]{:S(2)}) collective-permute-start(bf16[2,656,128]{2,1,0:T(8,128)(2,1)S(1)} %fusion.14), channel_id=1, source_target_pairs={{0,2},{1,3},{2,0},{3,1},{4,6},{5,7},{6,4},{7,5},{8,10},{9,11},{10,... | collective-permute-start | bytes 1007624 | tf_op jit(solution)/shard_map/ppermute | solution.py:173
  36.2 11.5 %collective-permute-start.4 = (bf16[2,656,128]{2,1,0:T(8,128)(2,1)S(1)}, bf16[2,656,128]{2,1,0:T(8,128)(2,1)S(1)}, u32[]{:S(2)}, u32[]{:S(2)}) collective-permute-start(bf16[2,656,128]{2,1,0:T(8,128)(2,1)S(1)} %fusion.13), channel_id=1, source_target_pairs={{0,1},{1,0},{2,3},{3,2},{4,5},{5,4},{6,7},{7,6},{8,9},{9,8},{10,11... | collective-permute-start | bytes 1007624 | tf_op jit(solution)/shard_map/ppermute | solution.py:173
  45.1 7.1 %collective-permute-start.11 = (bf16[656,128]{1,0:T(8,128)(2,1)S(1)}, bf16[656,128]{1,0:T(8,128)(2,1)S(1)}, u32[]{:S(2)}, u32[]{:S(2)}) collective-permute-start(bf16[656,128]{1,0:T(8,128)(2,1)S(1)} %fusion.51), channel_id=1, source_target_pairs={{0,1},{1,0},{2,3},{3,2},{4,5},{5,4},{6,7},{7,6},{8,9},{9,8},{10,11... | collective-permute-start | bytes 503816 | tf_op jit(solution)/shard_map/ppermute | solution.py:173
  47.8 6.1 %collective-permute-start.5 = (bf16[656,128]{1,0:T(8,128)(2,1)S(1)}, bf16[656,128]{1,0:T(8,128)(2,1)S(1)}, u32[]{:S(2)}, u32[]{:S(2)}) collective-permute-start(bf16[656,128]{1,0:T(8,128)(2,1)S(1)} %fusion.50), channel_id=1, source_target_pairs={{0,2},{1,3},{2,0},{3,1},{4,6},{5,7},{6,4},{7,5},{8,10},{9,11},{10,... | collective-permute-start | bytes 503816 | tf_op jit(solution)/shard_map/ppermute | solution.py:173
  52.3 1.7 %collective-permute-start.12 = (bf16[328,128]{1,0:T(8,128)(2,1)S(1)}, bf16[328,128]{1,0:T(8,128)(2,1)S(1)}, u32[]{:S(2)}, u32[]{:S(2)}) collective-permute-start(bf16[328,128]{1,0:T(8,128)(2,1)S(1)} %fusion.71), channel_id=1, source_target_pairs={{0,4},{4,0},{8,12},{12,8},{16,20},{20,16},{24,28},{28,24},{1,5},{5... | collective-permute-start | bytes 251912 | tf_op jit(solution)/shard_map/ppermute | solution.py:173
  54.0 2.0 %collective-permute-start.6 = (bf16[328,128]{1,0:T(8,128)(2,1)S(1)}, bf16[328,128]{1,0:T(8,128)(2,1)S(1)}, u32[]{:S(2)}, u32[]{:S(2)}) collective-permute-start(bf16[328,128]{1,0:T(8,128)(2,1)S(1)} %fusion.70), channel_id=1, source_target_pairs={{0,4},{4,0},{8,12},{12,8},{16,20},{20,16},{24,28},{28,24},{1,5},{5... | collective-permute-start | bytes 251912 | tf_op jit(solution)/shard_map/ppermute | solution.py:173
  54.1 5.2 %collective-permute-start.13 = (bf16[328,128]{1,0:T(8,128)(2,1)S(1)}, bf16[328,128]{1,0:T(8,128)(2,1)S(1)}, u32[]{:S(2)}, u32[]{:S(2)}) collective-permute-start(bf16[328,128]{1,0:T(8,128)(2,1)S(1)} %fusion.52), channel_id=1, source_target_pairs={{0,8},{4,12},{8,0},{12,4},{16,24},{20,28},{24,16},{28,20},{1,9},{5... | collective-permute-start | bytes 251912 | tf_op jit(solution)/shard_map/ppermute | solution.py:173
  55.9 6.4 %collective-permute-start.7 = (bf16[328,128]{1,0:T(8,128)(2,1)S(1)}, bf16[328,128]{1,0:T(8,128)(2,1)S(1)}, u32[]{:S(2)}, u32[]{:S(2)}) collective-permute-start(bf16[328,128]{1,0:T(8,128)(2,1)S(1)} %fusion.53), channel_id=1, source_target_pairs={{0,8},{4,12},{8,0},{12,4},{16,24},{20,28},{24,16},{28,20},{1,9},{5... | collective-permute-start | bytes 251912 | tf_op jit(solution)/shard_map/ppermute | solution.py:173
  59.3 9.1 %collective-permute-start.14 = (bf16[328,128]{1,0:T(8,128)(2,1)S(1)}, bf16[328,128]{1,0:T(8,128)(2,1)S(1)}, u32[]{:S(2)}, u32[]{:S(2)}) collective-permute-start(bf16[328,128]{1,0:T(8,128)(2,1)S(1)} %add_convert_fusion.2), channel_id=1, source_target_pairs={{0,16},{4,20},{8,24},{12,28},{16,0},{20,4},{24,8},{28,12},{1,17},{... | collective-permute-start | bytes 251912 | tf_op jit(solution)/shard_map/ppermute | solution.py:173
  62.4 7.4 %collective-permute-start.8 = (bf16[328,128]{1,0:T(8,128)(2,1)S(1)}, bf16[328,128]{1,0:T(8,128)(2,1)S(1)}, u32[]{:S(2)}, u32[]{:S(2)}) collective-permute-start(bf16[328,128]{1,0:T(8,128)(2,1)S(1)} %add_convert_fusion.4), channel_id=1, source_target_pairs={{0,16},{4,20},{8,24},{12,28},{16,0},{20,4},{24,8},{28,12},{1,17},{... | collective-permute-start | bytes 251912 | tf_op jit(solution)/shard_map/ppermute | solution.py:173
  68.4 1.5 %collective-permute-start.15 = (bf16[328,128]{1,0:T(8,128)(2,1)S(1)}, bf16[328,128]{1,0:T(8,128)(2,1)S(1)}, u32[]{:S(2)}, u32[]{:S(2)}) collective-permute-start(bf16[328,128]{1,0:T(8,128)(2,1)S(1)} %add_convert_fusion.1), channel_id=1, source_target_pairs={{0,4},{4,0},{8,12},{12,8},{16,20},{20,16},{24,28},{28,24},{1,5},{5... | collective-permute-start | bytes 251912 | tf_op jit(solution)/shard_map/ppermute | solution.py:173
  69.8 1.3 %collective-permute-start.9 = (bf16[328,128]{1,0:T(8,128)(2,1)S(1)}, bf16[328,128]{1,0:T(8,128)(2,1)S(1)}, u32[]{:S(2)}, u32[]{:S(2)}) collective-permute-start(bf16[328,128]{1,0:T(8,128)(2,1)S(1)} %add_convert_fusion.3), channel_id=1, source_target_pairs={{0,4},{4,0},{8,12},{12,8},{16,20},{20,16},{24,28},{28,24},{1,5},{5... | collective-permute-start | bytes 251912 | tf_op jit(solution)/shard_map/ppermute | solution.py:173

commit v9 on v8

--- a/solution.py
+++ b/solution.py
@@ -115,7 +115,7 @@
     out_rows, out_cols = (2 * in_rows, 2 * in_cols)
     lat_count = lax.axis_size("lat")
     lon_count = lax.axis_size("lon")
-    back_mix = mix_kernel.transpose(0, 1, 3, 2).reshape(9 * COUT, COUT)
+    back_mix = mix_kernel[::-1, ::-1].transpose(0, 1, 3, 2)
     padded_in, grad_pad = extend_all((inputs, cotangent), (1, 2))
     raw = upsample(padded_in, up_kernel, in_rows, in_cols)
     pre_act = (raw + up_bias).astype(jnp.bfloat16)
@@ -123,12 +123,14 @@
     inside = (row_at >= 0) & (row_at < out_rows * lat_count)
     activated = jax.nn.silu(pre_act.astype(jnp.float32)).astype(jnp.bfloat16)
     act_pad = jnp.where(inside, activated, jnp.zeros_like(activated))
-    act_grad = jnp.einsum(
-        "rck,kn->rcn",
-        neighbours(grad_pad, out_rows + 2, out_cols + 2, True),
+    act_grad = lax.conv_general_dilated(
+        grad_pad[None],
         back_mix,
+        (1, 1),
+        "VALID",
+        dimension_numbers=("NHWC", "HWIO", "NHWC"),
         preferred_element_type=jnp.float32,
-    )
+    )[0]
     pre_grad = (act_grad * slope(pre_act)).astype(jnp.bfloat16)
     pre_grad_pad = jnp.where(inside, pre_grad, jnp.zeros_like(pre_grad))
     patches = neighbours(act_pad, out_rows, out_cols, False)

time: 73.3 us -> 63.3 us (0.86)
  waiting for transfers between devices: 22.6 us -> 29.3 us
  other arithmetic: 7.87 us -> 2.44 us
  starting transfers between devices: 21.1 us -> 16.2 us
  local copies, waits for them, and re-layouts: 13.4 us -> 9.27 us
  matrix products: 6.32 us -> 4.24 us
    ppermute x12, starting transfers between devices: 12.9 us -> 7.9 us  [exchange(): return lax.ppermute(part, axis, [(i, i ^ step) for i in range(size)])]
    unnamed x5 -> x0, other arithmetic: 3.67 us -> none
    ppermute x2, waiting for transfers between devices: 0.01 us -> 3.41 us  [swap_edges(): lax.ppermute(jnp.concatenate([p.reshape(-1) for p in lasts]), axis, up)]
    ppermute x12, waiting for transfers between devices: 22.2 us -> 25.2 us  [exchange(): return lax.ppermute(part, axis, [(i, i ^ step) for i in range(size)])]
    ppermute x2, starting transfers between devices: 2.25 us -> 5.24 us  [swap_edges(): lax.ppermute(jnp.concatenate([p.reshape(-1) for p in leads]), axis, down)]
    ppermute x2, starting transfers between devices: 5.97 us -> 3.09 us  [swap_edges(): lax.ppermute(jnp.concatenate([p.reshape(-1) for p in lasts]), axis, up)]
    dot_general x1 -> x0, matrix products: 2.09 us -> none  [shards(): jnp.einsum('rck,kn->rcn', neighbours(grad_pad, out_rows + 2, out_cols + 2...]
    unnamed x70 -> x65, local copies, waits for them, and re-layouts: 4.83 us -> 3.3 us
  transfers between devices with their start and end apart: 16 -> 16, of which waited for: 8 -> 13; matrix products, arithmetic and copies ran while one was open for 9% -> 5% of each run, Pallas kernels for 0% -> 0%
where the time goes in v9:
time: 63.3 us; the launch traced here: 62.9 us
  waiting for transfers between devices  29.3 us (46%)
  starting transfers between devices  16.2 us (26%)
  local copies, waits for them, and re-layouts  9.27 us (15%)
  matrix products  4.24 us (7%)
  other arithmetic  2.44 us (4%)
  between operations  1.5 us (2%)
    ppermute x12, waiting for transfers between devices, exchange(): return lax.ppermute(part, axis, [(i, i ^ step) for i in range(size)])  25.2 us
    ppermute x12, starting transfers between devices, exchange(): return lax.ppermute(part, axis, [(i, i ^ step) for i in range(size)])  7.9 us
    ppermute x2, starting transfers between devices, swap_edges(): lax.ppermute(jnp.concatenate([p.reshape(-1) for p in leads]), axis, down)  5.24 us
    ppermute x2, waiting for transfers between devices, swap_edges(): lax.ppermute(jnp.concatenate([p.reshape(-1) for p in lasts]), axis, up)  3.41 us
    unnamed x65, local copies, waits for them, and re-layouts  3.3 us
    ppermute x2, starting transfers between devices, swap_edges(): lax.ppermute(jnp.concatenate([p.reshape(-1) for p in lasts]), axis, up)  3.09 us
  transfers between devices with their start and end apart: 16, of which 13 were waited for; matrix products, arithmetic and copies ran while one was open for 5% of the time, Pallas kernels for 0%

profile of v9, /device:TPU:0, one launch (start us, length us, event | category | flops | bytes accessed | tf_op | source)
XLA Modules:
  0.0 62.9 jit_solution(1493749691797759530)
XLA Ops:
  0.7 1.0 %fusion.82 = (bf16[32,2,128]{2,1,0:T(2,128)(2,1)S(1)}, bf16[32,2,128]{2,1,0:T(2,128)(2,1)S(1)}) fusion(bf16[32,16,128]{2,1,0:T(8,128)(2,1)} %param.11), kind=kLoop, calls=%fused_computation.213 | loop fusion | bytes 65536 | tf_op jit(solution)/shard_map/slice | solution.py:23
  1.7 0.8 %multiply_exponential_fusion = f32[16,8,8]{0,2,1:T(8,128)S(1)} fusion(s32[16,8,8]{0,2,1:T(8,128)} %param.7), kind=kLoop, calls=%fused_computation.189 | loop fusion | flops 2048 | bytes 8192 | tf_op jit(solution)/shard_map/exp2 | solution.py:50
  2.5 0.2 broadcast_in_dim.21
  2.7 0.2 reshape.205
  2.9 0.3 fusion.66
  3.3 3.9 %collective-permute-start.1 = (bf16[12288]{0:T(1024)(128)(2,1)S(1)}, bf16[12288]{0:T(1024)(128)(2,1)S(1)}, u32[]{:S(2)}, u32[]{:S(2)}) collective-permute-start(bf16[12288]{0:T(1024)(128)(2,1)S(1)} %pad_maximum_fusion.5), channel_id=1, source_target_pairs={{1,0},{2,1},{3,2},{0,3},{5,4},{6,5},{7,6},{4,7},{9,8},{10,9},{11,1... | collective-permute-start | bytes 73736 | tf_op jit(solution)/shard_map/ppermute | solution.py:26
  7.3 0.7 %slice_bitcast_fusion.15 = (bf16[256,128]{1,0:T(8,128)(2,1)S(1)}, bf16[256,128]{1,0:T(8,128)(2,1)}, bf16[256,128]{1,0:T(8,128)(2,1)}, bf16[256,128]{1,0:T(8,128)...) fusion(bf16[4,4,256,128]{3,2,1,0:T(8,128)(2,1)S(1)} %copy-done.1), kind=kLoop, calls=%fused_computation.188 | loop fusion | bytes 2097152 | tf_op jit(solution)/shard_map/squeeze | solution.py:74
  8.1 0.7 %collective-permute-done.1 = bf16[12288]{0:T(1024)(128)(2,1)S(1)} collective-permute-done((bf16[12288]{0:T(1024)(128)(2,1)S(1)}, bf16[12288]{0:T(1024)(128)(2,1)S(1)}, u32[]{:S(2)}, u32[]{:S(2)}) %collective-permute-start.1) | collective-permute-done | bytes 24608 | tf_op jit(solution)/shard_map/ppermute | solution.py:26
  8.8 3.3 %collective-permute-done = bf16[12288]{0:T(1024)(128)(2,1)S(1)} collective-permute-done((bf16[12288]{0:T(1024)(128)(2,1)S(1)}, bf16[12288]{0:T(1024)(128)(2,1)S(1)}, u32[]{:S(2)}, u32[]{:S(2)}) %collective-permute-start) | collective-permute-done | bytes 24608 | tf_op jit(solution)/shard_map/ppermute | solution.py:25
  12.2 1.3 %collective-permute-start.2 = (bf16[7680]{0:T(1024)(128)(2,1)S(1)}, bf16[7680]{0:T(1024)(128)(2,1)S(1)}, u32[]{:S(2)}, u32[]{:S(2)}) collective-permute-start(bf16[7680]{0:T(1024)(128)(2,1)S(1)} %pad_maximum_fusion.6), channel_id=1, source_target_pairs={{4,0},{8,4},{12,8},{16,12},{20,16},{24,20},{28,24},{5,1},{9,5},{13... | collective-permute-start | bytes 46088 | tf_op jit(solution)/shard_map/ppermute | solution.py:26
  13.6 3.0 %collective-permute-start.3 = (bf16[7680]{0:T(1024)(128)(2,1)S(1)}, bf16[7680]{0:T(1024)(128)(2,1)S(1)}, u32[]{:S(2)}, u32[]{:S(2)}) collective-permute-start(bf16[7680]{0:T(1024)(128)(2,1)S(1)} %pad_maximum_fusion.7), channel_id=1, source_target_pairs={{0,4},{4,8},{8,12},{12,16},{16,20},{20,24},{24,28},{1,5},{5,9},{9,... | collective-permute-start | bytes 46088 | tf_op jit(solution)/shard_map/ppermute | solution.py:25
  16.6 0.5 copy.32
  17.8 0.7 %convolution_select_fusion = f32[34,8,3,128]{3,1,2,0:T(8,128)S(1)} fusion(bf16[3,3,128,128]{3,2,1,0:T(8,128)(2,1)S(1)} %copy-done, bf16[36,1,7,2,128]{4,2,3,0,1:T(8,128)(2,1)S(1)} %slice.391, bf16[36,1,8,3,128]{4,2,3,0,1:T(8,128)(2,1)S(1)} %copy.29, pred[8,3]{0,1:T(4,128)(4,1)S(1)} %copy-done.10), kind=kOutput, calls=%fused_computation.1 | convolution fusion | flops 241858560 | bytes 1062936 | tf_op jit(solution)/shard_map/conv_general_dilated | solution.py:126
  18.7 0.2 squeeze.143
  18.9 0.5 copy-done.7
  19.5 0.3 convolution_bitcast_fusion
  19.8 0.5 copy-done.4
  20.4 0.3 convolution_bitcast_fusion.1
  20.7 0.3 convolution_bitcast_fusion.2
  21.0 0.3 convolution_bitcast_fusion.3
  21.4 0.6 copy-done.9
  22.0 0.2 broadcast_select_fusion
  22.4 0.2 reshape.252
  23.6 0.3 fusion.85
  23.9 0.7 %copy.39 = f32[16,8,256]{2,1,0:T(8,128)} copy(f32[16,8,256]{2,0,1:T(8,128)S(1)} %fusion.85) | data formatting | bytes 262144 | tf_op jit(solution)/shard_map/rck,kn->rcn/dot_general | solution.py:151
  25.0 0.5 fusion.71
  25.4 0.2 copy.34
  25.7 0.5 fusion
  26.5 0.6 collective-permute-start.10
  27.2 1.1 %convolution_convert_fusion = bf16[32,16,128]{2,1,0:T(8,128)(2,1)} fusion(bf16[32,16,1152]{2,1,0:T(8,128)(2,1)S(1)} %slice_dynamic-update-slice_fusion, bf16[1152,128,1]{1,0,2:T(8,128)(2,1)S(1)} %bitcast.224), kind=kOutput, calls=%fused_computation.5 | convolution fusion | flops 151060480 | bytes 1605632 | tf_op jit(solution)/shard_map/rck,kn->rcn/dot_general | solution.py:138
  28.3 8.8 %collective-permute-done.10 = bf16[2,656,128]{2,1,0:T(8,128)(2,1)S(1)} collective-permute-done((bf16[2,656,128]{2,1,0:T(8,128)(2,1)S(1)}, bf16[2,656,128]{2,1,0:T(8,128)(2,1)S(1)}, u32[]{:S(2)}, u32[]{:S(2)}) %collective-permute-start.10) | collective-permute-done | bytes 335904 | tf_op jit(solution)/shard_map/ppermute | solution.py:175
  37.3 0.6 collective-permute-done.4
  38.0 1.6 %collective-permute-start.5 = (bf16[656,128]{1,0:T(8,128)(2,1)S(1)}, bf16[656,128]{1,0:T(8,128)(2,1)S(1)}, u32[]{:S(2)}, u32[]{:S(2)}) collective-permute-start(bf16[656,128]{1,0:T(8,128)(2,1)S(1)} %fusion.49), channel_id=1, source_target_pairs={{0,2},{1,3},{2,0},{3,1},{4,6},{5,7},{6,4},{7,5},{8,10},{9,11},{10,... | collective-permute-start | bytes 503816 | tf_op jit(solution)/shard_map/ppermute | solution.py:175
  39.6 4.2 %collective-permute-done.11 = bf16[656,128]{1,0:T(8,128)(2,1)S(1)} collective-permute-done((bf16[656,128]{1,0:T(8,128)(2,1)S(1)}, bf16[656,128]{1,0:T(8,128)(2,1)S(1)}, u32[]{:S(2)}, u32[]{:S(2)}) %collective-permute-start.11) | collective-permute-done | bytes 167968 | tf_op jit(solution)/shard_map/ppermute | solution.py:175
  43.9 0.4 collective-permute-done.5
  44.4 0.2 collective-permute-start.6
  44.6 0.6 %collective-permute-done.12 = bf16[328,128]{1,0:T(8,128)(2,1)S(1)} collective-permute-done((bf16[328,128]{1,0:T(8,128)(2,1)S(1)}, bf16[328,128]{1,0:T(8,128)(2,1)S(1)}, u32[]{:S(2)}, u32[]{:S(2)}) %collective-permute-start.12) | collective-permute-done | bytes 84000 | tf_op jit(solution)/shard_map/ppermute | solution.py:175
  45.2 0.9 %collective-permute-start.13 = (bf16[328,128]{1,0:T(8,128)(2,1)S(1)}, bf16[328,128]{1,0:T(8,128)(2,1)S(1)}, u32[]{:S(2)}, u32[]{:S(2)}) collective-permute-start(bf16[328,128]{1,0:T(8,128)(2,1)S(1)} %fusion.51), channel_id=1, source_target_pairs={{0,8},{4,12},{8,0},{12,4},{16,24},{20,28},{24,16},{28,20},{1,9},{5... | collective-permute-start | bytes 251912 | tf_op jit(solution)/shard_map/ppermute | solution.py:175
  46.2 1.2 %collective-permute-start.7 = (bf16[328,128]{1,0:T(8,128)(2,1)S(1)}, bf16[328,128]{1,0:T(8,128)(2,1)S(1)}, u32[]{:S(2)}, u32[]{:S(2)}) collective-permute-start(bf16[328,128]{1,0:T(8,128)(2,1)S(1)} %fusion.52), channel_id=1, source_target_pairs={{0,8},{4,12},{8,0},{12,4},{16,24},{20,28},{24,16},{28,20},{1,9},{5... | collective-permute-start | bytes 251912 | tf_op jit(solution)/shard_map/ppermute | solution.py:175
  47.4 3.2 %collective-permute-done.13 = bf16[328,128]{1,0:T(8,128)(2,1)S(1)} collective-permute-done((bf16[328,128]{1,0:T(8,128)(2,1)S(1)}, bf16[328,128]{1,0:T(8,128)(2,1)S(1)}, u32[]{:S(2)}, u32[]{:S(2)}) %collective-permute-start.13) | collective-permute-done | bytes 84000 | tf_op jit(solution)/shard_map/ppermute | solution.py:175
  50.7 1.9 %collective-permute-start.14 = (bf16[328,128]{1,0:T(8,128)(2,1)S(1)}, bf16[328,128]{1,0:T(8,128)(2,1)S(1)}, u32[]{:S(2)}, u32[]{:S(2)}) collective-permute-start(bf16[328,128]{1,0:T(8,128)(2,1)S(1)} %add_convert_fusion.3), channel_id=1, source_target_pairs={{0,16},{4,20},{8,24},{12,28},{16,0},{20,4},{24,8},{28,12},{1,17},{... | collective-permute-start | bytes 251912 | tf_op jit(solution)/shard_map/ppermute | solution.py:175
  52.6 1.1 %collective-permute-start.8 = (bf16[328,128]{1,0:T(8,128)(2,1)S(1)}, bf16[328,128]{1,0:T(8,128)(2,1)S(1)}, u32[]{:S(2)}, u32[]{:S(2)}) collective-permute-start(bf16[328,128]{1,0:T(8,128)(2,1)S(1)} %add_convert_fusion.5), channel_id=1, source_target_pairs={{0,16},{4,20},{8,24},{12,28},{16,0},{20,4},{24,8},{28,12},{1,17},{... | collective-permute-start | bytes 251912 | tf_op jit(solution)/shard_map/ppermute | solution.py:175
  53.8 5.3 %collective-permute-done.14 = bf16[328,128]{1,0:T(8,128)(2,1)S(1)} collective-permute-done((bf16[328,128]{1,0:T(8,128)(2,1)S(1)}, bf16[328,128]{1,0:T(8,128)(2,1)S(1)}, u32[]{:S(2)}, u32[]{:S(2)}) %collective-permute-start.14) | collective-permute-done | bytes 84000 | tf_op jit(solution)/shard_map/ppermute | solution.py:175
  59.2 0.8 %collective-permute-done.8 = bf16[328,128]{1,0:T(8,128)(2,1)S(1)} collective-permute-done((bf16[328,128]{1,0:T(8,128)(2,1)S(1)}, bf16[328,128]{1,0:T(8,128)(2,1)S(1)}, u32[]{:S(2)}, u32[]{:S(2)}) %collective-permute-start.8) | collective-permute-done | bytes 84000 | tf_op jit(solution)/shard_map/ppermute | solution.py:175
  60.1 0.4 collective-permute-done.15
  60.5 0.9 %collective-permute-done.9 = bf16[328,128]{1,0:T(8,128)(2,1)S(1)} collective-permute-done((bf16[328,128]{1,0:T(8,128)(2,1)S(1)}, bf16[328,128]{1,0:T(8,128)(2,1)S(1)}, u32[]{:S(2)}, u32[]{:S(2)}) %collective-permute-start.9) | collective-permute-done | bytes 84000 | tf_op jit(solution)/shard_map/ppermute | solution.py:175
  61.4 0.8 %slice.410 = f32[1024,128]{1,0:T(8,128)} slice(f32[1312,128]{1,0:T(8,128)S(1)} %convert_multiply_fusion), slice={[0:1024], [0:128]} | slice | bytes 1048576 | tf_op jit(solution)/shard_map/slice | solution.py:168
  62.3 0.7 %slice.411 = f32[288,128]{1,0:T(8,128)} slice(f32[1312,128]{1,0:T(8,128)S(1)} %convert_multiply_fusion), slice={[1024:1312], [0:128]} | slice | bytes 294912 | tf_op jit(solution)/shard_map/slice | solution.py:169
  (135 shorter events, 3.8 us)
Async XLA Ops:
  0.6 17.2 %copy-start = (bf16[3,3,128,128]{3,2,1,0:T(8,128)(2,1)S(1)}, bf16[3,3,128,128]{3,2,1,0:T(8,128)(2,1)}, u32[]{:S(2)}) copy-start(bf16[3,3,128,128]{3,2,1,0:T(8,128)(2,1)} %param.10) | copy-start | bytes 884740
  0.6 2.3 %copy-start.3 = (s32[16,8,256]{2,1,0:T(8,128)S(1)}, s32[16,8,256]{2,1,0:T(8,128)}, u32[]{:S(2)}) copy-start(s32[16,8,256]{2,1,0:T(8,128)} %param.6) | copy-start | bytes 393220
  0.7 6.7 %copy-start.1 = (bf16[4,4,256,128]{3,2,1,0:T(8,128)(2,1)S(1)}, bf16[4,4,256,128]{3,2,1,0:T(8,128)(2,1)}, u32[]{:S(2)}) copy-start(bf16[4,4,256,128]{3,2,1,0:T(8,128)(2,1)} %param.8) | copy-start | bytes 3145732
  3.2 8.8 %copy-start.2 = (bf16[32,16,128]{2,1,0:T(8,128)(2,1)S(1)}, bf16[32,16,128]{2,1,0:T(8,128)(2,1)}, u32[]{:S(2)}) copy-start(bf16[32,16,128]{2,1,0:T(8,128)(2,1)} %param.11) | copy-start | bytes 393220
  3.3 5.5 %collective-permute-start.1 = (bf16[12288]{0:T(1024)(128)(2,1)S(1)}, bf16[12288]{0:T(1024)(128)(2,1)S(1)}, u32[]{:S(2)}, u32[]{:S(2)}) collective-permute-start(bf16[12288]{0:T(1024)(128)(2,1)S(1)} %pad_maximum_fusion.5), channel_id=1, source_target_pairs={{1,0},{2,1},{3,2},{0,3},{5,4},{6,5},{7,6},{4,7},{9,8},{10,9},{11,1... | collective-permute-start | bytes 73736 | tf_op jit(solution)/shard_map/ppermute | solution.py:26
  7.3 4.8 %collective-permute-start = (bf16[12288]{0:T(1024)(128)(2,1)S(1)}, bf16[12288]{0:T(1024)(128)(2,1)S(1)}, u32[]{:S(2)}, u32[]{:S(2)}) collective-permute-start(bf16[12288]{0:T(1024)(128)(2,1)S(1)} %pad_maximum_fusion.4), channel_id=1, source_target_pairs={{0,1},{1,2},{2,3},{3,0},{4,5},{5,6},{6,7},{7,4},{8,9},{9,10},{10,1... | collective-permute-start | bytes 73736 | tf_op jit(solution)/shard_map/ppermute | solution.py:25
  12.2 5.0 %collective-permute-start.2 = (bf16[7680]{0:T(1024)(128)(2,1)S(1)}, bf16[7680]{0:T(1024)(128)(2,1)S(1)}, u32[]{:S(2)}, u32[]{:S(2)}) collective-permute-start(bf16[7680]{0:T(1024)(128)(2,1)S(1)} %pad_maximum_fusion.6), channel_id=1, source_target_pairs={{4,0},{8,4},{12,8},{16,12},{20,16},{24,20},{28,24},{5,1},{9,5},{13... | collective-permute-start | bytes 46088 | tf_op jit(solution)/shard_map/ppermute | solution.py:26
  13.6 3.9 %collective-permute-start.3 = (bf16[7680]{0:T(1024)(128)(2,1)S(1)}, bf16[7680]{0:T(1024)(128)(2,1)S(1)}, u32[]{:S(2)}, u32[]{:S(2)}) collective-permute-start(bf16[7680]{0:T(1024)(128)(2,1)S(1)} %pad_maximum_fusion.7), channel_id=1, source_target_pairs={{0,4},{4,8},{8,12},{12,16},{16,20},{20,24},{24,28},{1,5},{5,9},{9,... | collective-permute-start | bytes 46088 | tf_op jit(solution)/shard_map/ppermute | solution.py:25
  17.2 0.7 %copy-start.10 = (pred[8,3]{0,1:T(4,128)(4,1)S(1)}, pred[8,3]{0,1:T(4,128)(4,1)}, u32[]{:S(2)}) copy-start(pred[8,3]{0,1:T(4,128)(4,1)} %constant.189) | copy-start | bytes 76
  18.6 0.8 %copy-start.7 = (bf16[256,128]{1,0:T(8,128)(2,1)S(1)}, bf16[256,128]{1,0:T(8,128)(2,1)}, u32[]{:S(2)}) copy-start(bf16[256,128]{1,0:T(8,128)(2,1)} %get-tuple-element.9) | copy-start | bytes 196612
  18.6 0.9 %copy-start.8 = (bf16[256,128]{1,0:T(8,128)(2,1)S(1)}, bf16[256,128]{1,0:T(8,128)(2,1)}, u32[]{:S(2)}) copy-start(bf16[256,128]{1,0:T(8,128)(2,1)} %get-tuple-element.10) | copy-start | bytes 196612
  19.5 0.8 %copy-start.4 = (bf16[256,128]{1,0:T(8,128)(2,1)S(1)}, bf16[256,128]{1,0:T(8,128)(2,1)}, u32[]{:S(2)}) copy-start(bf16[256,128]{1,0:T(8,128)(2,1)} %get-tuple-element.13) | copy-start | bytes 196612
  19.5 0.9 %copy-start.5 = (bf16[256,128]{1,0:T(8,128)(2,1)S(1)}, bf16[256,128]{1,0:T(8,128)(2,1)}, u32[]{:S(2)}) copy-start(bf16[256,128]{1,0:T(8,128)(2,1)} %get-tuple-element.14) | copy-start | bytes 196612
  19.5 0.9 %copy-start.6 = (bf16[256,128]{1,0:T(8,128)(2,1)S(1)}, bf16[256,128]{1,0:T(8,128)(2,1)}, u32[]{:S(2)}) copy-start(bf16[256,128]{1,0:T(8,128)(2,1)} %get-tuple-element.15) | copy-start | bytes 196612
  21.3 0.7 %copy-start.9 = (f32[128]{0:T(128)S(1)}, f32[128]{0:T(128)}, u32[]{:S(2)}) copy-start(f32[128]{0:T(128)} %param.9) | copy-start | bytes 1540
  26.5 10.6 %collective-permute-start.10 = (bf16[2,656,128]{2,1,0:T(8,128)(2,1)S(1)}, bf16[2,656,128]{2,1,0:T(8,128)(2,1)S(1)}, u32[]{:S(2)}, u32[]{:S(2)}) collective-permute-start(bf16[2,656,128]{2,1,0:T(8,128)(2,1)S(1)} %fusion.22), channel_id=1, source_target_pairs={{0,2},{1,3},{2,0},{3,1},{4,6},{5,7},{6,4},{7,5},{8,10},{9,11},{10,... | collective-permute-start | bytes 1007624 | tf_op jit(solution)/shard_map/ppermute | solution.py:175
  27.1 10.8 %collective-permute-start.4 = (bf16[2,656,128]{2,1,0:T(8,128)(2,1)S(1)}, bf16[2,656,128]{2,1,0:T(8,128)(2,1)S(1)}, u32[]{:S(2)}, u32[]{:S(2)}) collective-permute-start(bf16[2,656,128]{2,1,0:T(8,128)(2,1)S(1)} %fusion.21), channel_id=1, source_target_pairs={{0,1},{1,0},{2,3},{3,2},{4,5},{5,4},{6,7},{7,6},{8,9},{9,8},{10,11... | collective-permute-start | bytes 1007624 | tf_op jit(solution)/shard_map/ppermute | solution.py:175
  37.2 6.6 %collective-permute-start.11 = (bf16[656,128]{1,0:T(8,128)(2,1)S(1)}, bf16[656,128]{1,0:T(8,128)(2,1)S(1)}, u32[]{:S(2)}, u32[]{:S(2)}) collective-permute-start(bf16[656,128]{1,0:T(8,128)(2,1)S(1)} %fusion.50), channel_id=1, source_target_pairs={{0,1},{1,0},{2,3},{3,2},{4,5},{5,4},{6,7},{7,6},{8,9},{9,8},{10,11... | collective-permute-start | bytes 503816 | tf_op jit(solution)/shard_map/ppermute | solution.py:175
  38.0 6.3 %collective-permute-start.5 = (bf16[656,128]{1,0:T(8,128)(2,1)S(1)}, bf16[656,128]{1,0:T(8,128)(2,1)S(1)}, u32[]{:S(2)}, u32[]{:S(2)}) collective-permute-start(bf16[656,128]{1,0:T(8,128)(2,1)S(1)} %fusion.49), channel_id=1, source_target_pairs={{0,2},{1,3},{2,0},{3,1},{4,6},{5,7},{6,4},{7,5},{8,10},{9,11},{10,... | collective-permute-start | bytes 503816 | tf_op jit(solution)/shard_map/ppermute | solution.py:175
  43.9 1.3 %collective-permute-start.12 = (bf16[328,128]{1,0:T(8,128)(2,1)S(1)}, bf16[328,128]{1,0:T(8,128)(2,1)S(1)}, u32[]{:S(2)}, u32[]{:S(2)}) collective-permute-start(bf16[328,128]{1,0:T(8,128)(2,1)S(1)} %fusion.70), channel_id=1, source_target_pairs={{0,4},{4,0},{8,12},{12,8},{16,20},{20,16},{24,28},{28,24},{1,5},{5... | collective-permute-start | bytes 251912 | tf_op jit(solution)/shard_map/ppermute | solution.py:175
  44.4 1.8 %collective-permute-start.6 = (bf16[328,128]{1,0:T(8,128)(2,1)S(1)}, bf16[328,128]{1,0:T(8,128)(2,1)S(1)}, u32[]{:S(2)}, u32[]{:S(2)}) collective-permute-start(bf16[328,128]{1,0:T(8,128)(2,1)S(1)} %fusion.69), channel_id=1, source_target_pairs={{0,4},{4,0},{8,12},{12,8},{16,20},{20,16},{24,28},{28,24},{1,5},{5... | collective-permute-start | bytes 251912 | tf_op jit(solution)/shard_map/ppermute | solution.py:175
  45.2 5.4 %collective-permute-start.13 = (bf16[328,128]{1,0:T(8,128)(2,1)S(1)}, bf16[328,128]{1,0:T(8,128)(2,1)S(1)}, u32[]{:S(2)}, u32[]{:S(2)}) collective-permute-start(bf16[328,128]{1,0:T(8,128)(2,1)S(1)} %fusion.51), channel_id=1, source_target_pairs={{0,8},{4,12},{8,0},{12,4},{16,24},{20,28},{24,16},{28,20},{1,9},{5... | collective-permute-start | bytes 251912 | tf_op jit(solution)/shard_map/ppermute | solution.py:175
  46.2 6.4 %collective-permute-start.7 = (bf16[328,128]{1,0:T(8,128)(2,1)S(1)}, bf16[328,128]{1,0:T(8,128)(2,1)S(1)}, u32[]{:S(2)}, u32[]{:S(2)}) collective-permute-start(bf16[328,128]{1,0:T(8,128)(2,1)S(1)} %fusion.52), channel_id=1, source_target_pairs={{0,8},{4,12},{8,0},{12,4},{16,24},{20,28},{24,16},{28,20},{1,9},{5... | collective-permute-start | bytes 251912 | tf_op jit(solution)/shard_map/ppermute | solution.py:175
  50.7 8.4 %collective-permute-start.14 = (bf16[328,128]{1,0:T(8,128)(2,1)S(1)}, bf16[328,128]{1,0:T(8,128)(2,1)S(1)}, u32[]{:S(2)}, u32[]{:S(2)}) collective-permute-start(bf16[328,128]{1,0:T(8,128)(2,1)S(1)} %add_convert_fusion.3), channel_id=1, source_target_pairs={{0,16},{4,20},{8,24},{12,28},{16,0},{20,4},{24,8},{28,12},{1,17},{... | collective-permute-start | bytes 251912 | tf_op jit(solution)/shard_map/ppermute | solution.py:175
  52.6 7.3 %collective-permute-start.8 = (bf16[328,128]{1,0:T(8,128)(2,1)S(1)}, bf16[328,128]{1,0:T(8,128)(2,1)S(1)}, u32[]{:S(2)}, u32[]{:S(2)}) collective-permute-start(bf16[328,128]{1,0:T(8,128)(2,1)S(1)} %add_convert_fusion.5), channel_id=1, source_target_pairs={{0,16},{4,20},{8,24},{12,28},{16,0},{20,4},{24,8},{28,12},{1,17},{... | collective-permute-start | bytes 251912 | tf_op jit(solution)/shard_map/ppermute | solution.py:175
  59.1 1.3 %collective-permute-start.15 = (bf16[328,128]{1,0:T(8,128)(2,1)S(1)}, bf16[328,128]{1,0:T(8,128)(2,1)S(1)}, u32[]{:S(2)}, u32[]{:S(2)}) collective-permute-start(bf16[328,128]{1,0:T(8,128)(2,1)S(1)} %add_convert_fusion.2), channel_id=1, source_target_pairs={{0,4},{4,0},{8,12},{12,8},{16,20},{20,16},{24,28},{28,24},{1,5},{5... | collective-permute-start | bytes 251912 | tf_op jit(solution)/shard_map/ppermute | solution.py:175
  60.0 1.3 %collective-permute-start.9 = (bf16[328,128]{1,0:T(8,128)(2,1)S(1)}, bf16[328,128]{1,0:T(8,128)(2,1)S(1)}, u32[]{:S(2)}, u32[]{:S(2)}) collective-permute-start(bf16[328,128]{1,0:T(8,128)(2,1)S(1)} %add_convert_fusion.4), channel_id=1, source_target_pairs={{0,4},{4,0},{8,12},{12,8},{16,20},{20,16},{24,28},{28,24},{1,5},{5... | collective-permute-start | bytes 251912 | tf_op jit(solution)/shard_map/ppermute | solution.py:175

commit v10 on v9

--- a/solution.py
+++ b/solution.py
@@ -230,7 +230,7 @@
     half = rows.shape[1] // 2
     first = scatter_lon(rows[:, :half], steps)
     second = scatter_lon(rows[:, half:], list(reversed(steps)))
-    return jnp.concatenate([reduce_lat(first), reduce_lat(second)])
+    return reduce_lat(jnp.concatenate([first, second]))
 
 
 def solution(mesh):

time: 63.3 us -> 65.9 us (1.041)
  waiting for transfers between devices: 29.3 us -> 33.8 us
  starting transfers between devices: 16.2 us -> 13.3 us
  local copies, waits for them, and re-layouts: 9.27 us -> 10.3 us
    ppermute x12 -> x8, waiting for transfers between devices: 25.2 us -> 29.7 us  [exchange(): return lax.ppermute(part, axis, [(i, i ^ step) for i in range(size)])]
    ppermute x12 -> x8, starting transfers between devices: 7.9 us -> 4.94 us  [exchange(): return lax.ppermute(part, axis, [(i, i ^ step) for i in range(size)])]
    unnamed x65 -> x67, local copies, waits for them, and re-layouts: 3.3 us -> 4.34 us
  transfers between devices with their start and end apart: 16 -> 12, of which waited for: 13 -> 11; matrix products, arithmetic and copies ran while one was open for 5% -> 6% of each run, Pallas kernels for 0% -> 0%
where the time goes in v10:
time: 65.9 us; the launch traced here: 65.5 us
  waiting for transfers between devices  33.8 us (51%)
  starting transfers between devices  13.3 us (20%)
  local copies, waits for them, and re-layouts  10.3 us (16%)
  matrix products  4.22 us (6%)
  other arithmetic  2.43 us (4%)
  between operations  1.46 us (2%)
    ppermute x8, waiting for transfers between devices, exchange(): return lax.ppermute(part, axis, [(i, i ^ step) for i in range(size)])  29.7 us
    ppermute x2, starting transfers between devices, swap_edges(): lax.ppermute(jnp.concatenate([p.reshape(-1) for p in leads]), axis, down)  5.24 us
    ppermute x8, starting transfers between devices, exchange(): return lax.ppermute(part, axis, [(i, i ^ step) for i in range(size)])  4.94 us
    unnamed x67, local copies, waits for them, and re-layouts  4.34 us
    ppermute x2, waiting for transfers between devices, swap_edges(): lax.ppermute(jnp.concatenate([p.reshape(-1) for p in lasts]), axis, up)  3.41 us
    ppermute x2, starting transfers between devices, swap_edges(): lax.ppermute(jnp.concatenate([p.reshape(-1) for p in lasts]), axis, up)  3.09 us
  transfers between devices with their start and end apart: 12, of which 11 were waited for; matrix products, arithmetic and copies ran while one was open for 6% of the time, Pallas kernels for 0%

profile of v10, /device:TPU:0, one launch (start us, length us, event | category | flops | bytes accessed | tf_op | source)
XLA Modules:
  0.0 65.5 jit_solution(3860643441954962527)
XLA Ops:
  0.7 1.0 %fusion.80 = (bf16[32,2,128]{2,1,0:T(2,128)(2,1)S(1)}, bf16[32,2,128]{2,1,0:T(2,128)(2,1)S(1)}) fusion(bf16[32,16,128]{2,1,0:T(8,128)(2,1)} %param.11), kind=kLoop, calls=%fused_computation.206 | loop fusion | bytes 65536 | tf_op jit(solution)/shard_map/slice | solution.py:23
  1.7 0.8 %multiply_exponential_fusion = f32[16,8,8]{0,2,1:T(8,128)S(1)} fusion(s32[16,8,8]{0,2,1:T(8,128)} %param.7), kind=kLoop, calls=%fused_computation.182 | loop fusion | flops 2048 | bytes 8192 | tf_op jit(solution)/shard_map/exp2 | solution.py:50
  2.5 0.2 broadcast_in_dim.21
  2.7 0.2 reshape.201
  2.9 0.3 fusion.66
  3.3 3.9 %collective-permute-start.1 = (bf16[12288]{0:T(1024)(128)(2,1)S(1)}, bf16[12288]{0:T(1024)(128)(2,1)S(1)}, u32[]{:S(2)}, u32[]{:S(2)}) collective-permute-start(bf16[12288]{0:T(1024)(128)(2,1)S(1)} %pad_maximum_fusion.6), channel_id=1, source_target_pairs={{1,0},{2,1},{3,2},{0,3},{5,4},{6,5},{7,6},{4,7},{9,8},{10,9},{11,1... | collective-permute-start | bytes 73736 | tf_op jit(solution)/shard_map/ppermute | solution.py:26
  7.3 0.7 %slice_bitcast_fusion.15 = (bf16[256,128]{1,0:T(8,128)(2,1)S(1)}, bf16[256,128]{1,0:T(8,128)(2,1)}, bf16[256,128]{1,0:T(8,128)(2,1)}, bf16[256,128]{1,0:T(8,128)...) fusion(bf16[4,4,256,128]{3,2,1,0:T(8,128)(2,1)S(1)} %copy-done.1), kind=kLoop, calls=%fused_computation.181 | loop fusion | bytes 2097152 | tf_op jit(solution)/shard_map/squeeze | solution.py:74
  8.1 0.7 %collective-permute-done.1 = bf16[12288]{0:T(1024)(128)(2,1)S(1)} collective-permute-done((bf16[12288]{0:T(1024)(128)(2,1)S(1)}, bf16[12288]{0:T(1024)(128)(2,1)S(1)}, u32[]{:S(2)}, u32[]{:S(2)}) %collective-permute-start.1) | collective-permute-done | bytes 24608 | tf_op jit(solution)/shard_map/ppermute | solution.py:26
  8.8 3.3 %collective-permute-done = bf16[12288]{0:T(1024)(128)(2,1)S(1)} collective-permute-done((bf16[12288]{0:T(1024)(128)(2,1)S(1)}, bf16[12288]{0:T(1024)(128)(2,1)S(1)}, u32[]{:S(2)}, u32[]{:S(2)}) %collective-permute-start) | collective-permute-done | bytes 24608 | tf_op jit(solution)/shard_map/ppermute | solution.py:25
  12.2 1.3 %collective-permute-start.2 = (bf16[7680]{0:T(1024)(128)(2,1)S(1)}, bf16[7680]{0:T(1024)(128)(2,1)S(1)}, u32[]{:S(2)}, u32[]{:S(2)}) collective-permute-start(bf16[7680]{0:T(1024)(128)(2,1)S(1)} %pad_maximum_fusion.7), channel_id=1, source_target_pairs={{4,0},{8,4},{12,8},{16,12},{20,16},{24,20},{28,24},{5,1},{9,5},{13... | collective-permute-start | bytes 46088 | tf_op jit(solution)/shard_map/ppermute | solution.py:26
  13.6 3.0 %collective-permute-start.3 = (bf16[7680]{0:T(1024)(128)(2,1)S(1)}, bf16[7680]{0:T(1024)(128)(2,1)S(1)}, u32[]{:S(2)}, u32[]{:S(2)}) collective-permute-start(bf16[7680]{0:T(1024)(128)(2,1)S(1)} %pad_maximum_fusion.8), channel_id=1, source_target_pairs={{0,4},{4,8},{8,12},{12,16},{16,20},{20,24},{24,28},{1,5},{5,9},{9,... | collective-permute-start | bytes 46088 | tf_op jit(solution)/shard_map/ppermute | solution.py:25
  16.6 0.5 copy.32
  17.8 0.7 %convolution_select_fusion = f32[34,8,3,128]{3,1,2,0:T(8,128)S(1)} fusion(bf16[3,3,128,128]{3,2,1,0:T(8,128)(2,1)S(1)} %copy-done, bf16[36,1,7,2,128]{4,2,3,0,1:T(8,128)(2,1)S(1)} %slice.391, bf16[36,1,8,3,128]{4,2,3,0,1:T(8,128)(2,1)S(1)} %copy.29, pred[8,3]{0,1:T(4,128)(4,1)S(1)} %copy-done.11), kind=kOutput, calls=%fused_computation.1 | convolution fusion | flops 241858560 | bytes 1062936 | tf_op jit(solution)/shard_map/conv_general_dilated | solution.py:126
  18.7 0.2 squeeze.138
  18.9 0.5 copy-done.7
  19.5 0.3 convolution_bitcast_fusion
  19.8 0.5 copy-done.4
  20.4 0.3 convolution_bitcast_fusion.1
  20.7 0.3 convolution_bitcast_fusion.2
  21.0 0.3 convolution_bitcast_fusion.3
  21.4 0.6 copy-done.9
  22.0 0.2 broadcast_select_fusion
  22.2 0.6 constant_dynamic-update-slice_fusion.31
  22.8 0.2 copy.44
  23.0 0.2 reshape.247
  23.2 0.2 fusion.48
  24.1 0.4 copy-done.10
  24.9 0.5 fusion.69
  25.3 0.2 copy.34
  25.6 0.5 fusion
  26.1 0.2 fusion.79
  26.4 0.6 collective-permute-start.6
  27.1 9.9 %collective-permute-done.6 = bf16[2,656,128]{2,1,0:T(8,128)(2,1)S(1)} collective-permute-done((bf16[2,656,128]{2,1,0:T(8,128)(2,1)S(1)}, bf16[2,656,128]{2,1,0:T(8,128)(2,1)S(1)}, u32[]{:S(2)}, u32[]{:S(2)}) %collective-permute-start.6) | collective-permute-done | bytes 335904 | tf_op jit(solution)/shard_map/ppermute | solution.py:175
  37.2 0.6 collective-permute-done.4
  37.9 1.6 %collective-permute-start.5 = (bf16[656,128]{1,0:T(8,128)(2,1)S(1)}, bf16[656,128]{1,0:T(8,128)(2,1)S(1)}, u32[]{:S(2)}, u32[]{:S(2)}) collective-permute-start(bf16[656,128]{1,0:T(8,128)(2,1)S(1)} %fusion.50), channel_id=1, source_target_pairs={{0,2},{1,3},{2,0},{3,1},{4,6},{5,7},{6,4},{7,5},{8,10},{9,11},{10,... | collective-permute-start | bytes 503816 | tf_op jit(solution)/shard_map/ppermute | solution.py:175
  39.5 4.2 %collective-permute-done.7 = bf16[656,128]{1,0:T(8,128)(2,1)S(1)} collective-permute-done((bf16[656,128]{1,0:T(8,128)(2,1)S(1)}, bf16[656,128]{1,0:T(8,128)(2,1)S(1)}, u32[]{:S(2)}, u32[]{:S(2)}) %collective-permute-start.7) | collective-permute-done | bytes 167968 | tf_op jit(solution)/shard_map/ppermute | solution.py:175
  43.7 0.5 collective-permute-done.5
  44.5 1.4 %collective-permute-done.8 = bf16[656,128]{1,0:T(8,128)(2,1)S(1)} collective-permute-done((bf16[656,128]{1,0:T(8,128)(2,1)S(1)}, bf16[656,128]{1,0:T(8,128)(2,1)S(1)}, u32[]{:S(2)}, u32[]{:S(2)}) %collective-permute-start.8) | collective-permute-done | bytes 167968 | tf_op jit(solution)/shard_map/ppermute | solution.py:175
  45.9 0.7 %collective-permute-start.9 = (bf16[656,128]{1,0:T(8,128)(2,1)S(1)}, bf16[656,128]{1,0:T(8,128)(2,1)S(1)}, u32[]{:S(2)}, u32[]{:S(2)}) collective-permute-start(bf16[656,128]{1,0:T(8,128)(2,1)S(1)} %fusion.23), channel_id=1, source_target_pairs={{0,8},{4,12},{8,0},{12,4},{16,24},{20,28},{24,16},{28,20},{1,9},{5... | collective-permute-start | bytes 503816 | tf_op jit(solution)/shard_map/ppermute | solution.py:175
  46.6 5.6 %collective-permute-done.9 = bf16[656,128]{1,0:T(8,128)(2,1)S(1)} collective-permute-done((bf16[656,128]{1,0:T(8,128)(2,1)S(1)}, bf16[656,128]{1,0:T(8,128)(2,1)S(1)}, u32[]{:S(2)}, u32[]{:S(2)}) %collective-permute-start.9) | collective-permute-done | bytes 167968 | tf_op jit(solution)/shard_map/ppermute | solution.py:175
  52.3 1.8 %collective-permute-start.10 = (bf16[656,128]{1,0:T(8,128)(2,1)S(1)}, bf16[656,128]{1,0:T(8,128)(2,1)S(1)}, u32[]{:S(2)}, u32[]{:S(2)}) collective-permute-start(bf16[656,128]{1,0:T(8,128)(2,1)S(1)} %add_convert_fusion.3), channel_id=1, source_target_pairs={{0,16},{4,20},{8,24},{12,28},{16,0},{20,4},{24,8},{28,12},{1,17},{... | collective-permute-start | bytes 503816 | tf_op jit(solution)/shard_map/ppermute | solution.py:175
  54.1 0.3 fusion.83
  54.4 0.7 %copy.39 = f32[16,8,256]{2,1,0:T(8,128)} copy(f32[16,8,256]{2,0,1:T(8,128)S(1)} %fusion.83) | data formatting | bytes 262144 | tf_op jit(solution)/shard_map/rck,kn->rcn/dot_general | solution.py:151
  55.1 7.3 %collective-permute-done.10 = bf16[656,128]{1,0:T(8,128)(2,1)S(1)} collective-permute-done((bf16[656,128]{1,0:T(8,128)(2,1)S(1)}, bf16[656,128]{1,0:T(8,128)(2,1)S(1)}, u32[]{:S(2)}, u32[]{:S(2)}) %collective-permute-start.10) | collective-permute-done | bytes 167968 | tf_op jit(solution)/shard_map/ppermute | solution.py:175
  62.5 1.1 %convolution_convert_fusion = bf16[32,16,128]{2,1,0:T(8,128)(2,1)} fusion(bf16[32,16,1152]{2,1,0:T(8,128)(2,1)S(1)} %slice_dynamic-update-slice_fusion, bf16[1152,128,1]{1,0,2:T(8,128)(2,1)S(1)} %bitcast.217), kind=kOutput, calls=%fused_computation.5 | convolution fusion | flops 151060480 | bytes 1605632 | tf_op jit(solution)/shard_map/rck,kn->rcn/dot_general | solution.py:138
  63.6 0.2 collective-permute-done.11
  64.0 0.8 %slice.410 = f32[1024,128]{1,0:T(8,128)} slice(f32[1312,128]{1,0:T(8,128)S(1)} %convert_multiply_fusion), slice={[0:1024], [0:128]} | slice | bytes 1048576 | tf_op jit(solution)/shard_map/slice | solution.py:168
  64.8 0.7 %slice.411 = f32[288,128]{1,0:T(8,128)} slice(f32[1312,128]{1,0:T(8,128)S(1)} %convert_multiply_fusion), slice={[1024:1312], [0:128]} | slice | bytes 294912 | tf_op jit(solution)/shard_map/slice | solution.py:169
  (125 shorter events, 3.2 us)
Async XLA Ops:
  0.6 17.2 %copy-start = (bf16[3,3,128,128]{3,2,1,0:T(8,128)(2,1)S(1)}, bf16[3,3,128,128]{3,2,1,0:T(8,128)(2,1)}, u32[]{:S(2)}) copy-start(bf16[3,3,128,128]{3,2,1,0:T(8,128)(2,1)} %param.10) | copy-start | bytes 884740
  0.6 2.3 %copy-start.3 = (s32[16,8,256]{2,1,0:T(8,128)S(1)}, s32[16,8,256]{2,1,0:T(8,128)}, u32[]{:S(2)}) copy-start(s32[16,8,256]{2,1,0:T(8,128)} %param.6) | copy-start | bytes 393220
  0.7 6.7 %copy-start.1 = (bf16[4,4,256,128]{3,2,1,0:T(8,128)(2,1)S(1)}, bf16[4,4,256,128]{3,2,1,0:T(8,128)(2,1)}, u32[]{:S(2)}) copy-start(bf16[4,4,256,128]{3,2,1,0:T(8,128)(2,1)} %param.8) | copy-start | bytes 3145732
  3.2 8.8 %copy-start.2 = (bf16[32,16,128]{2,1,0:T(8,128)(2,1)S(1)}, bf16[32,16,128]{2,1,0:T(8,128)(2,1)}, u32[]{:S(2)}) copy-start(bf16[32,16,128]{2,1,0:T(8,128)(2,1)} %param.11) | copy-start | bytes 393220
  3.3 5.5 %collective-permute-start.1 = (bf16[12288]{0:T(1024)(128)(2,1)S(1)}, bf16[12288]{0:T(1024)(128)(2,1)S(1)}, u32[]{:S(2)}, u32[]{:S(2)}) collective-permute-start(bf16[12288]{0:T(1024)(128)(2,1)S(1)} %pad_maximum_fusion.6), channel_id=1, source_target_pairs={{1,0},{2,1},{3,2},{0,3},{5,4},{6,5},{7,6},{4,7},{9,8},{10,9},{11,1... | collective-permute-start | bytes 73736 | tf_op jit(solution)/shard_map/ppermute | solution.py:26
  7.3 4.8 %collective-permute-start = (bf16[12288]{0:T(1024)(128)(2,1)S(1)}, bf16[12288]{0:T(1024)(128)(2,1)S(1)}, u32[]{:S(2)}, u32[]{:S(2)}) collective-permute-start(bf16[12288]{0:T(1024)(128)(2,1)S(1)} %pad_maximum_fusion.5), channel_id=1, source_target_pairs={{0,1},{1,2},{2,3},{3,0},{4,5},{5,6},{6,7},{7,4},{8,9},{9,10},{10,1... | collective-permute-start | bytes 73736 | tf_op jit(solution)/shard_map/ppermute | solution.py:25
  12.2 5.0 %collective-permute-start.2 = (bf16[7680]{0:T(1024)(128)(2,1)S(1)}, bf16[7680]{0:T(1024)(128)(2,1)S(1)}, u32[]{:S(2)}, u32[]{:S(2)}) collective-permute-start(bf16[7680]{0:T(1024)(128)(2,1)S(1)} %pad_maximum_fusion.7), channel_id=1, source_target_pairs={{4,0},{8,4},{12,8},{16,12},{20,16},{24,20},{28,24},{5,1},{9,5},{13... | collective-permute-start | bytes 46088 | tf_op jit(solution)/shard_map/ppermute | solution.py:26
  13.6 3.9 %collective-permute-start.3 = (bf16[7680]{0:T(1024)(128)(2,1)S(1)}, bf16[7680]{0:T(1024)(128)(2,1)S(1)}, u32[]{:S(2)}, u32[]{:S(2)}) collective-permute-start(bf16[7680]{0:T(1024)(128)(2,1)S(1)} %pad_maximum_fusion.8), channel_id=1, source_target_pairs={{0,4},{4,8},{8,12},{12,16},{16,20},{20,24},{24,28},{1,5},{5,9},{9,... | collective-permute-start | bytes 46088 | tf_op jit(solution)/shard_map/ppermute | solution.py:25
  17.2 0.7 %copy-start.11 = (pred[8,3]{0,1:T(4,128)(4,1)S(1)}, pred[8,3]{0,1:T(4,128)(4,1)}, u32[]{:S(2)}) copy-start(pred[8,3]{0,1:T(4,128)(4,1)} %constant.175) | copy-start | bytes 76
  18.6 0.8 %copy-start.7 = (bf16[256,128]{1,0:T(8,128)(2,1)S(1)}, bf16[256,128]{1,0:T(8,128)(2,1)}, u32[]{:S(2)}) copy-start(bf16[256,128]{1,0:T(8,128)(2,1)} %get-tuple-element.9) | copy-start | bytes 196612
  18.6 0.9 %copy-start.8 = (bf16[256,128]{1,0:T(8,128)(2,1)S(1)}, bf16[256,128]{1,0:T(8,128)(2,1)}, u32[]{:S(2)}) copy-start(bf16[256,128]{1,0:T(8,128)(2,1)} %get-tuple-element.10) | copy-start | bytes 196612
  19.5 0.8 %copy-start.4 = (bf16[256,128]{1,0:T(8,128)(2,1)S(1)}, bf16[256,128]{1,0:T(8,128)(2,1)}, u32[]{:S(2)}) copy-start(bf16[256,128]{1,0:T(8,128)(2,1)} %get-tuple-element.13) | copy-start | bytes 196612
  19.5 0.9 %copy-start.5 = (bf16[256,128]{1,0:T(8,128)(2,1)S(1)}, bf16[256,128]{1,0:T(8,128)(2,1)}, u32[]{:S(2)}) copy-start(bf16[256,128]{1,0:T(8,128)(2,1)} %get-tuple-element.14) | copy-start | bytes 196612
  19.5 0.9 %copy-start.6 = (bf16[256,128]{1,0:T(8,128)(2,1)S(1)}, bf16[256,128]{1,0:T(8,128)(2,1)}, u32[]{:S(2)}) copy-start(bf16[256,128]{1,0:T(8,128)(2,1)} %get-tuple-element.15) | copy-start | bytes 196612
  21.3 0.7 %copy-start.9 = (f32[128]{0:T(128)S(1)}, f32[128]{0:T(128)}, u32[]{:S(2)}) copy-start(f32[128]{0:T(128)} %param.9) | copy-start | bytes 1540
  23.5 1.0 %copy-start.10 = (bf16[16,8,16,128]{3,0,1,2:T(8,128)(2,1)S(1)}, bf16[16,8,16,128]{3,0,1,2:T(8,128)(2,1)}, u32[]{:S(2)}) copy-start(bf16[16,8,16,128]{3,0,1,2:T(8,128)(2,1)} %constant_dynamic-update-slice_fusion.31) | copy-start | bytes 1572868
  26.4 10.6 %collective-permute-start.6 = (bf16[2,656,128]{2,1,0:T(8,128)(2,1)S(1)}, bf16[2,656,128]{2,1,0:T(8,128)(2,1)S(1)}, u32[]{:S(2)}, u32[]{:S(2)}) collective-permute-start(bf16[2,656,128]{2,1,0:T(8,128)(2,1)S(1)} %fusion.22), channel_id=1, source_target_pairs={{0,2},{1,3},{2,0},{3,1},{4,6},{5,7},{6,4},{7,5},{8,10},{9,11},{10,... | collective-permute-start | bytes 1007624 | tf_op jit(solution)/shard_map/ppermute | solution.py:175
  27.0 10.8 %collective-permute-start.4 = (bf16[2,656,128]{2,1,0:T(8,128)(2,1)S(1)}, bf16[2,656,128]{2,1,0:T(8,128)(2,1)S(1)}, u32[]{:S(2)}, u32[]{:S(2)}) collective-permute-start(bf16[2,656,128]{2,1,0:T(8,128)(2,1)S(1)} %fusion.21), channel_id=1, source_target_pairs={{0,1},{1,0},{2,3},{3,2},{4,5},{5,4},{6,7},{7,6},{8,9},{9,8},{10,11... | collective-permute-start | bytes 1007624 | tf_op jit(solution)/shard_map/ppermute | solution.py:175
  37.1 6.6 %collective-permute-start.7 = (bf16[656,128]{1,0:T(8,128)(2,1)S(1)}, bf16[656,128]{1,0:T(8,128)(2,1)S(1)}, u32[]{:S(2)}, u32[]{:S(2)}) collective-permute-start(bf16[656,128]{1,0:T(8,128)(2,1)S(1)} %fusion.51), channel_id=1, source_target_pairs={{0,1},{1,0},{2,3},{3,2},{4,5},{5,4},{6,7},{7,6},{8,9},{9,8},{10,11... | collective-permute-start | bytes 503816 | tf_op jit(solution)/shard_map/ppermute | solution.py:175
  37.9 6.3 %collective-permute-start.5 = (bf16[656,128]{1,0:T(8,128)(2,1)S(1)}, bf16[656,128]{1,0:T(8,128)(2,1)S(1)}, u32[]{:S(2)}, u32[]{:S(2)}) collective-permute-start(bf16[656,128]{1,0:T(8,128)(2,1)S(1)} %fusion.50), channel_id=1, source_target_pairs={{0,2},{1,3},{2,0},{3,1},{4,6},{5,7},{6,4},{7,5},{8,10},{9,11},{10,... | collective-permute-start | bytes 503816 | tf_op jit(solution)/shard_map/ppermute | solution.py:175
  44.3 1.5 %collective-permute-start.8 = (bf16[656,128]{1,0:T(8,128)(2,1)S(1)}, bf16[656,128]{1,0:T(8,128)(2,1)S(1)}, u32[]{:S(2)}, u32[]{:S(2)}) collective-permute-start(bf16[656,128]{1,0:T(8,128)(2,1)S(1)} %fusion.52), channel_id=1, source_target_pairs={{0,4},{4,0},{8,12},{12,8},{16,20},{20,16},{24,28},{28,24},{1,5},{5... | collective-permute-start | bytes 503816 | tf_op jit(solution)/shard_map/ppermute | solution.py:175
  45.9 6.4 %collective-permute-start.9 = (bf16[656,128]{1,0:T(8,128)(2,1)S(1)}, bf16[656,128]{1,0:T(8,128)(2,1)S(1)}, u32[]{:S(2)}, u32[]{:S(2)}) collective-permute-start(bf16[656,128]{1,0:T(8,128)(2,1)S(1)} %fusion.23), channel_id=1, source_target_pairs={{0,8},{4,12},{8,0},{12,4},{16,24},{20,28},{24,16},{28,20},{1,9},{5... | collective-permute-start | bytes 503816 | tf_op jit(solution)/shard_map/ppermute | solution.py:175
  52.3 10.1 %collective-permute-start.10 = (bf16[656,128]{1,0:T(8,128)(2,1)S(1)}, bf16[656,128]{1,0:T(8,128)(2,1)S(1)}, u32[]{:S(2)}, u32[]{:S(2)}) collective-permute-start(bf16[656,128]{1,0:T(8,128)(2,1)S(1)} %add_convert_fusion.3), channel_id=1, source_target_pairs={{0,16},{4,20},{8,24},{12,28},{16,0},{20,4},{24,8},{28,12},{1,17},{... | collective-permute-start | bytes 503816 | tf_op jit(solution)/shard_map/ppermute | solution.py:175
  62.4 1.5 %collective-permute-start.11 = (bf16[656,128]{1,0:T(8,128)(2,1)S(1)}, bf16[656,128]{1,0:T(8,128)(2,1)S(1)}, u32[]{:S(2)}, u32[]{:S(2)}) collective-permute-start(bf16[656,128]{1,0:T(8,128)(2,1)S(1)} %add_convert_fusion.2), channel_id=1, source_target_pairs={{0,4},{4,0},{8,12},{12,8},{16,20},{20,16},{24,28},{28,24},{1,5},{5... | collective-permute-start | bytes 503816 | tf_op jit(solution)/shard_map/ppermute | solution.py:175

commit v11 on v10

--- a/solution.py
+++ b/solution.py
@@ -220,17 +220,29 @@
     return double(part, "lat", steps[0]).astype(jnp.float32)
 
 
+def butterfly(part, steps):
+    part = part.astype(jnp.bfloat16)
+    for step in steps:
+        got = exchange(part, "lat", step)
+        part = (part.astype(jnp.float32) + got.astype(jnp.float32)).astype(jnp.bfloat16)
+    return part
+
+
 def reduce_terms(rows):
-    lon_count = rows.shape[0]
+    lon_count, count = rows.shape[:2]
     steps = steps_of(lon_count)
-    if steps is None or rows.shape[1] % 2:
+    lat_steps = steps_of(lax.axis_size("lat"))
+    if steps is None or lat_steps is None or count % 4:
         own = lax.axis_index("lon")
         mine = lax.dynamic_index_in_dim(lax.psum(rows, "lon"), own, 0, keepdims=False)
         return reduce_lat(mine)
-    half = rows.shape[1] // 2
-    first = scatter_lon(rows[:, :half], steps)
-    second = scatter_lon(rows[:, half:], list(reversed(steps)))
-    return reduce_lat(jnp.concatenate([first, second]))
+    pair = rows.reshape((lon_count, 2, count // 2) + rows.shape[2:])
+    part = halve(pair, "lat", lat_steps[0], 1)
+    half = count // 4
+    first = scatter_lon(part[:, :half], steps)
+    second = scatter_lon(part[:, half:], list(reversed(steps)))
+    joined = jnp.concatenate([butterfly(first, lat_steps[1:]), butterfly(second, lat_steps[1:])])
+    return double(joined, "lat", lat_steps[0]).astype(jnp.float32)
 
 
 def solution(mesh):

time: 65.9 us -> 59.9 us (0.909)
  waiting for transfers between devices: 33.8 us -> 19.8 us
  starting transfers between devices: 13.3 us -> 20.6 us
  local copies, waits for them, and re-layouts: 10.3 us -> 11 us
    ppermute x8 -> x10, waiting for transfers between devices: 29.7 us -> 15.7 us  [exchange(): return lax.ppermute(part, axis, [(i, i ^ step) for i in range(size)])]
    ppermute x8 -> x10, starting transfers between devices: 4.94 us -> 12.3 us  [exchange(): return lax.ppermute(part, axis, [(i, i ^ step) for i in range(size)])]
  transfers between devices with their start and end apart: 12 -> 14, of which waited for: 11 -> 11; matrix products, arithmetic and copies ran while one was open for 6% -> 6% of each run, Pallas kernels for 0% -> 0%
where the time goes in v11:
time: 59.9 us; the launch traced here: 59.5 us
  starting transfers between devices  20.6 us (34%)
  waiting for transfers between devices  19.8 us (33%)
  local copies, waits for them, and re-layouts  11 us (18%)
  matrix products  4.22 us (7%)
  other arithmetic  2.47 us (4%)
  between operations  1.47 us (2%)
    ppermute x10, waiting for transfers between devices, exchange(): return lax.ppermute(part, axis, [(i, i ^ step) for i in range(size)])  15.7 us
    ppermute x10, starting transfers between devices, exchange(): return lax.ppermute(part, axis, [(i, i ^ step) for i in range(size)])  12.3 us
    ppermute x2, starting transfers between devices, swap_edges(): lax.ppermute(jnp.concatenate([p.reshape(-1) for p in leads]), axis, down)  5.24 us
    unnamed x67, local copies, waits for them, and re-layouts  4.9 us
    ppermute x2, waiting for transfers between devices, swap_edges(): lax.ppermute(jnp.concatenate([p.reshape(-1) for p in lasts]), axis, up)  3.41 us
    ppermute x2, starting transfers between devices, swap_edges(): lax.ppermute(jnp.concatenate([p.reshape(-1) for p in lasts]), axis, up)  3.09 us
  transfers between devices with their start and end apart: 14, of which 11 were waited for; matrix products, arithmetic and copies ran while one was open for 6% of the time, Pallas kernels for 0%

profile of v11, /device:TPU:0, one launch (start us, length us, event | category | flops | bytes accessed | tf_op | source)
XLA Modules:
  0.0 59.5 jit_solution(12122181565863513830)
XLA Ops:
  0.7 1.0 %fusion.81 = (bf16[32,2,128]{2,1,0:T(2,128)(2,1)S(1)}, bf16[32,2,128]{2,1,0:T(2,128)(2,1)S(1)}) fusion(bf16[32,16,128]{2,1,0:T(8,128)(2,1)} %param.11), kind=kLoop, calls=%fused_computation.209 | loop fusion | bytes 65536 | tf_op jit(solution)/shard_map/slice | solution.py:23
  1.7 0.8 %multiply_exponential_fusion = f32[16,8,8]{0,2,1:T(8,128)S(1)} fusion(s32[16,8,8]{0,2,1:T(8,128)} %param.7), kind=kLoop, calls=%fused_computation.185 | loop fusion | flops 2048 | bytes 8192 | tf_op jit(solution)/shard_map/exp2 | solution.py:50
  2.5 0.2 broadcast_in_dim.21
  2.7 0.2 reshape.201
  2.9 0.3 fusion.65
  3.3 3.9 %collective-permute-start.1 = (bf16[12288]{0:T(1024)(128)(2,1)S(1)}, bf16[12288]{0:T(1024)(128)(2,1)S(1)}, u32[]{:S(2)}, u32[]{:S(2)}) collective-permute-start(bf16[12288]{0:T(1024)(128)(2,1)S(1)} %pad_maximum_fusion.6), channel_id=1, source_target_pairs={{1,0},{2,1},{3,2},{0,3},{5,4},{6,5},{7,6},{4,7},{9,8},{10,9},{11,1... | collective-permute-start | bytes 73736 | tf_op jit(solution)/shard_map/ppermute | solution.py:26
  7.3 0.7 %slice_bitcast_fusion.15 = (bf16[256,128]{1,0:T(8,128)(2,1)S(1)}, bf16[256,128]{1,0:T(8,128)(2,1)}, bf16[256,128]{1,0:T(8,128)(2,1)}, bf16[256,128]{1,0:T(8,128)...) fusion(bf16[4,4,256,128]{3,2,1,0:T(8,128)(2,1)S(1)} %copy-done.1), kind=kLoop, calls=%fused_computation.184 | loop fusion | bytes 2097152 | tf_op jit(solution)/shard_map/squeeze | solution.py:74
  8.1 0.7 %collective-permute-done.1 = bf16[12288]{0:T(1024)(128)(2,1)S(1)} collective-permute-done((bf16[12288]{0:T(1024)(128)(2,1)S(1)}, bf16[12288]{0:T(1024)(128)(2,1)S(1)}, u32[]{:S(2)}, u32[]{:S(2)}) %collective-permute-start.1) | collective-permute-done | bytes 24608 | tf_op jit(solution)/shard_map/ppermute | solution.py:26
  8.8 3.3 %collective-permute-done = bf16[12288]{0:T(1024)(128)(2,1)S(1)} collective-permute-done((bf16[12288]{0:T(1024)(128)(2,1)S(1)}, bf16[12288]{0:T(1024)(128)(2,1)S(1)}, u32[]{:S(2)}, u32[]{:S(2)}) %collective-permute-start) | collective-permute-done | bytes 24608 | tf_op jit(solution)/shard_map/ppermute | solution.py:25
  12.2 1.3 %collective-permute-start.2 = (bf16[7680]{0:T(1024)(128)(2,1)S(1)}, bf16[7680]{0:T(1024)(128)(2,1)S(1)}, u32[]{:S(2)}, u32[]{:S(2)}) collective-permute-start(bf16[7680]{0:T(1024)(128)(2,1)S(1)} %pad_maximum_fusion.7), channel_id=1, source_target_pairs={{4,0},{8,4},{12,8},{16,12},{20,16},{24,20},{28,24},{5,1},{9,5},{13... | collective-permute-start | bytes 46088 | tf_op jit(solution)/shard_map/ppermute | solution.py:26
  13.6 3.0 %collective-permute-start.3 = (bf16[7680]{0:T(1024)(128)(2,1)S(1)}, bf16[7680]{0:T(1024)(128)(2,1)S(1)}, u32[]{:S(2)}, u32[]{:S(2)}) collective-permute-start(bf16[7680]{0:T(1024)(128)(2,1)S(1)} %pad_maximum_fusion.8), channel_id=1, source_target_pairs={{0,4},{4,8},{8,12},{12,16},{16,20},{20,24},{24,28},{1,5},{5,9},{9,... | collective-permute-start | bytes 46088 | tf_op jit(solution)/shard_map/ppermute | solution.py:25
  16.6 0.5 copy.32
  17.8 0.7 %convolution_select_fusion = f32[34,8,3,128]{3,1,2,0:T(8,128)S(1)} fusion(bf16[3,3,128,128]{3,2,1,0:T(8,128)(2,1)S(1)} %copy-done, bf16[36,1,7,2,128]{4,2,3,0,1:T(8,128)(2,1)S(1)} %slice.391, bf16[36,1,8,3,128]{4,2,3,0,1:T(8,128)(2,1)S(1)} %copy.29, pred[8,3]{0,1:T(4,128)(4,1)S(1)} %copy-done.11), kind=kOutput, calls=%fused_computation.3 | convolution fusion | flops 241858560 | bytes 1062936 | tf_op jit(solution)/shard_map/conv_general_dilated | solution.py:126
  18.7 0.2 squeeze.139
  18.9 0.5 copy-done.7
  19.5 0.3 convolution_bitcast_fusion
  19.8 0.5 copy-done.4
  20.4 0.3 convolution_bitcast_fusion.1
  20.7 0.3 convolution_bitcast_fusion.2
  21.0 0.3 convolution_bitcast_fusion.3
  21.4 0.6 copy-done.9
  22.0 0.2 broadcast_select_fusion
  22.2 0.6 %constant_dynamic-update-slice_fusion.31 = bf16[16,8,16,128]{3,0,1,2:T(8,128)(2,1)} fusion(bf16[17,2,9,2,128]{4,0,2,3,1:T(8,128)(2,1)S(1)} %broadcast_select_fusion), kind=kLoop, calls=%fused_computation.164 | loop fusion | bytes 65536
  23.0 0.2 reshape.247
  24.1 0.5 fusion
  24.7 1.0 %copy-done.10 = bf16[16,8,16,128]{3,0,1,2:T(8,128)(2,1)S(1)} copy-done((bf16[16,8,16,128]{3,0,1,2:T(8,128)(2,1)S(1)}, bf16[16,8,16,128]{3,0,1,2:T(8,128)(2,1)}, u32[]{:S(2)}) %copy-start.10) | copy-done | bytes 524312
  26.0 0.5 fusion.70
  26.5 0.2 copy.34
  27.0 1.3 %collective-permute-start.4 = (bf16[4,656,128]{2,1,0:T(8,128)(2,1)S(1)}, bf16[4,656,128]{2,1,0:T(8,128)(2,1)S(1)}, u32[]{:S(2)}, u32[]{:S(2)}) collective-permute-start(bf16[4,656,128]{2,1,0:T(8,128)(2,1)S(1)} %fusion.4), channel_id=1, source_target_pairs={{0,4},{4,0},{8,12},{12,8},{16,20},{20,16},{24,28},{28,24},{1,5},{5... | collective-permute-start | bytes 2015240 | tf_op jit(solution)/shard_map/ppermute | solution.py:175
  28.3 1.7 %collective-permute-done.4 = bf16[4,656,128]{2,1,0:T(8,128)(2,1)S(1)} collective-permute-done((bf16[4,656,128]{2,1,0:T(8,128)(2,1)S(1)}, bf16[4,656,128]{2,1,0:T(8,128)(2,1)S(1)}, u32[]{:S(2)}, u32[]{:S(2)}) %collective-permute-start.4) | collective-permute-done | bytes 671776 | tf_op jit(solution)/shard_map/ppermute | solution.py:175
  30.3 0.6 collective-permute-start.9
  30.9 0.3 fusion.84
  31.2 0.7 %copy.39 = f32[16,8,256]{2,1,0:T(8,128)} copy(f32[16,8,256]{2,0,1:T(8,128)S(1)} %fusion.84) | data formatting | bytes 262144 | tf_op jit(solution)/shard_map/rck,kn->rcn/dot_general | solution.py:151
  32.0 4.9 %collective-permute-done.9 = bf16[2,328,128]{2,1,0:T(8,128)(2,1)S(1)} collective-permute-done((bf16[2,328,128]{2,1,0:T(8,128)(2,1)S(1)}, bf16[2,328,128]{2,1,0:T(8,128)(2,1)S(1)}, u32[]{:S(2)}, u32[]{:S(2)}) %collective-permute-start.9) | collective-permute-done | bytes 167968 | tf_op jit(solution)/shard_map/ppermute | solution.py:175
  37.0 1.2 %collective-permute-done.5 = bf16[2,328,128]{2,1,0:T(8,128)(2,1)S(1)} collective-permute-done((bf16[2,328,128]{2,1,0:T(8,128)(2,1)S(1)}, bf16[2,328,128]{2,1,0:T(8,128)(2,1)S(1)}, u32[]{:S(2)}, u32[]{:S(2)}) %collective-permute-start.5) | collective-permute-done | bytes 167968 | tf_op jit(solution)/shard_map/ppermute | solution.py:175
  38.3 1.6 %collective-permute-start.6 = (bf16[328,128]{1,0:T(8,128)(2,1)S(1)}, bf16[328,128]{1,0:T(8,128)(2,1)S(1)}, u32[]{:S(2)}, u32[]{:S(2)}) collective-permute-start(bf16[328,128]{1,0:T(8,128)(2,1)S(1)} %fusion.68), channel_id=1, source_target_pairs={{0,2},{1,3},{2,0},{3,1},{4,6},{5,7},{6,4},{7,5},{8,10},{9,11},{10,... | collective-permute-start | bytes 251912 | tf_op jit(solution)/shard_map/ppermute | solution.py:175
  40.0 1.5 %collective-permute-done.10 = bf16[328,128]{1,0:T(8,128)(2,1)S(1)} collective-permute-done((bf16[328,128]{1,0:T(8,128)(2,1)S(1)}, bf16[328,128]{1,0:T(8,128)(2,1)S(1)}, u32[]{:S(2)}, u32[]{:S(2)}) %collective-permute-start.10) | collective-permute-done | bytes 84000 | tf_op jit(solution)/shard_map/ppermute | solution.py:175
  41.5 2.4 %collective-permute-start.11 = (bf16[328,128]{1,0:T(8,128)(2,1)S(1)}, bf16[328,128]{1,0:T(8,128)(2,1)S(1)}, u32[]{:S(2)}, u32[]{:S(2)}) collective-permute-start(bf16[328,128]{1,0:T(8,128)(2,1)S(1)} %fusion.50), channel_id=1, source_target_pairs={{0,8},{4,12},{8,0},{12,4},{16,24},{20,28},{24,16},{28,20},{1,9},{5... | collective-permute-start | bytes 251912 | tf_op jit(solution)/shard_map/ppermute | solution.py:175
  43.9 1.3 %collective-permute-start.7 = (bf16[328,128]{1,0:T(8,128)(2,1)S(1)}, bf16[328,128]{1,0:T(8,128)(2,1)S(1)}, u32[]{:S(2)}, u32[]{:S(2)}) collective-permute-start(bf16[328,128]{1,0:T(8,128)(2,1)S(1)} %fusion.51), channel_id=1, source_target_pairs={{0,8},{4,12},{8,0},{12,4},{16,24},{20,28},{24,16},{28,20},{1,9},{5... | collective-permute-start | bytes 251912 | tf_op jit(solution)/shard_map/ppermute | solution.py:175
  45.3 1.1 %collective-permute-done.11 = bf16[328,128]{1,0:T(8,128)(2,1)S(1)} collective-permute-done((bf16[328,128]{1,0:T(8,128)(2,1)S(1)}, bf16[328,128]{1,0:T(8,128)(2,1)S(1)}, u32[]{:S(2)}, u32[]{:S(2)}) %collective-permute-start.11) | collective-permute-done | bytes 84000 | tf_op jit(solution)/shard_map/ppermute | solution.py:175
  46.4 3.6 %collective-permute-start.12 = (bf16[328,128]{1,0:T(8,128)(2,1)S(1)}, bf16[328,128]{1,0:T(8,128)(2,1)S(1)}, u32[]{:S(2)}, u32[]{:S(2)}) collective-permute-start(bf16[328,128]{1,0:T(8,128)(2,1)S(1)} %add_convert_fusion.3), channel_id=1, source_target_pairs={{0,16},{4,20},{8,24},{12,28},{16,0},{20,4},{24,8},{28,12},{1,17},{... | collective-permute-start | bytes 251912 | tf_op jit(solution)/shard_map/ppermute | solution.py:175
  50.0 1.2 %collective-permute-start.8 = (bf16[328,128]{1,0:T(8,128)(2,1)S(1)}, bf16[328,128]{1,0:T(8,128)(2,1)S(1)}, u32[]{:S(2)}, u32[]{:S(2)}) collective-permute-start(bf16[328,128]{1,0:T(8,128)(2,1)S(1)} %add_convert_fusion.5), channel_id=1, source_target_pairs={{0,16},{4,20},{8,24},{12,28},{16,0},{20,4},{24,8},{28,12},{1,17},{... | collective-permute-start | bytes 251912 | tf_op jit(solution)/shard_map/ppermute | solution.py:175
  51.3 2.2 %collective-permute-done.12 = bf16[328,128]{1,0:T(8,128)(2,1)S(1)} collective-permute-done((bf16[328,128]{1,0:T(8,128)(2,1)S(1)}, bf16[328,128]{1,0:T(8,128)(2,1)S(1)}, u32[]{:S(2)}, u32[]{:S(2)}) %collective-permute-start.12) | collective-permute-done | bytes 84000 | tf_op jit(solution)/shard_map/ppermute | solution.py:175
  53.5 2.9 %collective-permute-done.8 = bf16[328,128]{1,0:T(8,128)(2,1)S(1)} collective-permute-done((bf16[328,128]{1,0:T(8,128)(2,1)S(1)}, bf16[328,128]{1,0:T(8,128)(2,1)S(1)}, u32[]{:S(2)}, u32[]{:S(2)}) %collective-permute-start.8) | collective-permute-done | bytes 84000 | tf_op jit(solution)/shard_map/ppermute | solution.py:175
  56.5 1.1 %convolution_convert_fusion = bf16[32,16,128]{2,1,0:T(8,128)(2,1)} fusion(bf16[32,16,1152]{2,1,0:T(8,128)(2,1)S(1)} %slice_dynamic-update-slice_fusion, bf16[1152,128,1]{1,0,2:T(8,128)(2,1)S(1)} %bitcast.219), kind=kOutput, calls=%fused_computation.7 | convolution fusion | flops 151060480 | bytes 1605632 | tf_op jit(solution)/shard_map/rck,kn->rcn/dot_general | solution.py:138
  57.6 0.2 collective-permute-done.13
  58.0 0.8 %slice.411 = f32[1024,128]{1,0:T(8,128)} slice(f32[1312,128]{1,0:T(8,128)S(1)} %convert_multiply_fusion), slice={[0:1024], [0:128]} | slice | bytes 1048576 | tf_op jit(solution)/shard_map/slice | solution.py:168
  58.8 0.7 %slice.412 = f32[288,128]{1,0:T(8,128)} slice(f32[1312,128]{1,0:T(8,128)S(1)} %convert_multiply_fusion), slice={[1024:1312], [0:128]} | slice | bytes 294912 | tf_op jit(solution)/shard_map/slice | solution.py:169
  (132 shorter events, 3.8 us)
Async XLA Ops:
  0.6 17.2 %copy-start = (bf16[3,3,128,128]{3,2,1,0:T(8,128)(2,1)S(1)}, bf16[3,3,128,128]{3,2,1,0:T(8,128)(2,1)}, u32[]{:S(2)}) copy-start(bf16[3,3,128,128]{3,2,1,0:T(8,128)(2,1)} %param.10) | copy-start | bytes 884740
  0.6 2.3 %copy-start.3 = (s32[16,8,256]{2,1,0:T(8,128)S(1)}, s32[16,8,256]{2,1,0:T(8,128)}, u32[]{:S(2)}) copy-start(s32[16,8,256]{2,1,0:T(8,128)} %param.6) | copy-start | bytes 393220
  0.7 6.7 %copy-start.1 = (bf16[4,4,256,128]{3,2,1,0:T(8,128)(2,1)S(1)}, bf16[4,4,256,128]{3,2,1,0:T(8,128)(2,1)}, u32[]{:S(2)}) copy-start(bf16[4,4,256,128]{3,2,1,0:T(8,128)(2,1)} %param.8) | copy-start | bytes 3145732
  3.2 8.8 %copy-start.2 = (bf16[32,16,128]{2,1,0:T(8,128)(2,1)S(1)}, bf16[32,16,128]{2,1,0:T(8,128)(2,1)}, u32[]{:S(2)}) copy-start(bf16[32,16,128]{2,1,0:T(8,128)(2,1)} %param.11) | copy-start | bytes 393220
  3.3 5.5 %collective-permute-start.1 = (bf16[12288]{0:T(1024)(128)(2,1)S(1)}, bf16[12288]{0:T(1024)(128)(2,1)S(1)}, u32[]{:S(2)}, u32[]{:S(2)}) collective-permute-start(bf16[12288]{0:T(1024)(128)(2,1)S(1)} %pad_maximum_fusion.6), channel_id=1, source_target_pairs={{1,0},{2,1},{3,2},{0,3},{5,4},{6,5},{7,6},{4,7},{9,8},{10,9},{11,1... | collective-permute-start | bytes 73736 | tf_op jit(solution)/shard_map/ppermute | solution.py:26
  7.3 4.8 %collective-permute-start = (bf16[12288]{0:T(1024)(128)(2,1)S(1)}, bf16[12288]{0:T(1024)(128)(2,1)S(1)}, u32[]{:S(2)}, u32[]{:S(2)}) collective-permute-start(bf16[12288]{0:T(1024)(128)(2,1)S(1)} %pad_maximum_fusion.5), channel_id=1, source_target_pairs={{0,1},{1,2},{2,3},{3,0},{4,5},{5,6},{6,7},{7,4},{8,9},{9,10},{10,1... | collective-permute-start | bytes 73736 | tf_op jit(solution)/shard_map/ppermute | solution.py:25
  12.2 5.0 %collective-permute-start.2 = (bf16[7680]{0:T(1024)(128)(2,1)S(1)}, bf16[7680]{0:T(1024)(128)(2,1)S(1)}, u32[]{:S(2)}, u32[]{:S(2)}) collective-permute-start(bf16[7680]{0:T(1024)(128)(2,1)S(1)} %pad_maximum_fusion.7), channel_id=1, source_target_pairs={{4,0},{8,4},{12,8},{16,12},{20,16},{24,20},{28,24},{5,1},{9,5},{13... | collective-permute-start | bytes 46088 | tf_op jit(solution)/shard_map/ppermute | solution.py:26
  13.6 3.9 %collective-permute-start.3 = (bf16[7680]{0:T(1024)(128)(2,1)S(1)}, bf16[7680]{0:T(1024)(128)(2,1)S(1)}, u32[]{:S(2)}, u32[]{:S(2)}) collective-permute-start(bf16[7680]{0:T(1024)(128)(2,1)S(1)} %pad_maximum_fusion.8), channel_id=1, source_target_pairs={{0,4},{4,8},{8,12},{12,16},{16,20},{20,24},{24,28},{1,5},{5,9},{9,... | collective-permute-start | bytes 46088 | tf_op jit(solution)/shard_map/ppermute | solution.py:25
  17.2 0.7 %copy-start.11 = (pred[8,3]{0,1:T(4,128)(4,1)S(1)}, pred[8,3]{0,1:T(4,128)(4,1)}, u32[]{:S(2)}) copy-start(pred[8,3]{0,1:T(4,128)(4,1)} %constant.177) | copy-start | bytes 76
  18.6 0.8 %copy-start.7 = (bf16[256,128]{1,0:T(8,128)(2,1)S(1)}, bf16[256,128]{1,0:T(8,128)(2,1)}, u32[]{:S(2)}) copy-start(bf16[256,128]{1,0:T(8,128)(2,1)} %get-tuple-element.9) | copy-start | bytes 196612
  18.6 0.9 %copy-start.8 = (bf16[256,128]{1,0:T(8,128)(2,1)S(1)}, bf16[256,128]{1,0:T(8,128)(2,1)}, u32[]{:S(2)}) copy-start(bf16[256,128]{1,0:T(8,128)(2,1)} %get-tuple-element.10) | copy-start | bytes 196612
  19.5 0.8 %copy-start.4 = (bf16[256,128]{1,0:T(8,128)(2,1)S(1)}, bf16[256,128]{1,0:T(8,128)(2,1)}, u32[]{:S(2)}) copy-start(bf16[256,128]{1,0:T(8,128)(2,1)} %get-tuple-element.13) | copy-start | bytes 196612
  19.5 0.9 %copy-start.5 = (bf16[256,128]{1,0:T(8,128)(2,1)S(1)}, bf16[256,128]{1,0:T(8,128)(2,1)}, u32[]{:S(2)}) copy-start(bf16[256,128]{1,0:T(8,128)(2,1)} %get-tuple-element.14) | copy-start | bytes 196612
  19.5 0.9 %copy-start.6 = (bf16[256,128]{1,0:T(8,128)(2,1)S(1)}, bf16[256,128]{1,0:T(8,128)(2,1)}, u32[]{:S(2)}) copy-start(bf16[256,128]{1,0:T(8,128)(2,1)} %get-tuple-element.15) | copy-start | bytes 196612
  21.3 0.7 %copy-start.9 = (f32[128]{0:T(128)S(1)}, f32[128]{0:T(128)}, u32[]{:S(2)}) copy-start(f32[128]{0:T(128)} %param.9) | copy-start | bytes 1540
  24.7 1.0 %copy-start.10 = (bf16[16,8,16,128]{3,0,1,2:T(8,128)(2,1)S(1)}, bf16[16,8,16,128]{3,0,1,2:T(8,128)(2,1)}, u32[]{:S(2)}) copy-start(bf16[16,8,16,128]{3,0,1,2:T(8,128)(2,1)} %constant_dynamic-update-slice_fusion.31) | copy-start | bytes 1572868
  27.0 3.0 %collective-permute-start.4 = (bf16[4,656,128]{2,1,0:T(8,128)(2,1)S(1)}, bf16[4,656,128]{2,1,0:T(8,128)(2,1)S(1)}, u32[]{:S(2)}, u32[]{:S(2)}) collective-permute-start(bf16[4,656,128]{2,1,0:T(8,128)(2,1)S(1)} %fusion.4), channel_id=1, source_target_pairs={{0,4},{4,0},{8,12},{12,8},{16,20},{20,16},{24,28},{28,24},{1,5},{5... | collective-permute-start | bytes 2015240 | tf_op jit(solution)/shard_map/ppermute | solution.py:175
  30.3 6.6 %collective-permute-start.9 = (bf16[2,328,128]{2,1,0:T(8,128)(2,1)S(1)}, bf16[2,328,128]{2,1,0:T(8,128)(2,1)S(1)}, u32[]{:S(2)}, u32[]{:S(2)}) collective-permute-start(bf16[2,328,128]{2,1,0:T(8,128)(2,1)S(1)} %fusion.49), channel_id=1, source_target_pairs={{0,2},{1,3},{2,0},{3,1},{4,6},{5,7},{6,4},{7,5},{8,10},{9,11},{10,... | collective-permute-start | bytes 503816 | tf_op jit(solution)/shard_map/ppermute | solution.py:175
  31.9 6.3 %collective-permute-start.5 = (bf16[2,328,128]{2,1,0:T(8,128)(2,1)S(1)}, bf16[2,328,128]{2,1,0:T(8,128)(2,1)S(1)}, u32[]{:S(2)}, u32[]{:S(2)}) collective-permute-start(bf16[2,328,128]{2,1,0:T(8,128)(2,1)S(1)} %fusion.48), channel_id=1, source_target_pairs={{0,1},{1,0},{2,3},{3,2},{4,5},{5,4},{6,7},{7,6},{8,9},{9,8},{10,11... | collective-permute-start | bytes 503816 | tf_op jit(solution)/shard_map/ppermute | solution.py:175
  37.0 4.5 %collective-permute-start.10 = (bf16[328,128]{1,0:T(8,128)(2,1)S(1)}, bf16[328,128]{1,0:T(8,128)(2,1)S(1)}, u32[]{:S(2)}, u32[]{:S(2)}) collective-permute-start(bf16[328,128]{1,0:T(8,128)(2,1)S(1)} %fusion.69), channel_id=1, source_target_pairs={{0,1},{1,0},{2,3},{3,2},{4,5},{5,4},{6,7},{7,6},{8,9},{9,8},{10,11... | collective-permute-start | bytes 251912 | tf_op jit(solution)/shard_map/ppermute | solution.py:175
  38.3 5.6 %collective-permute-start.6 = (bf16[328,128]{1,0:T(8,128)(2,1)S(1)}, bf16[328,128]{1,0:T(8,128)(2,1)S(1)}, u32[]{:S(2)}, u32[]{:S(2)}) collective-permute-start(bf16[328,128]{1,0:T(8,128)(2,1)S(1)} %fusion.68), channel_id=1, source_target_pairs={{0,2},{1,3},{2,0},{3,1},{4,6},{5,7},{6,4},{7,5},{8,10},{9,11},{10,... | collective-permute-start | bytes 251912 | tf_op jit(solution)/shard_map/ppermute | solution.py:175
  41.5 4.8 %collective-permute-start.11 = (bf16[328,128]{1,0:T(8,128)(2,1)S(1)}, bf16[328,128]{1,0:T(8,128)(2,1)S(1)}, u32[]{:S(2)}, u32[]{:S(2)}) collective-permute-start(bf16[328,128]{1,0:T(8,128)(2,1)S(1)} %fusion.50), channel_id=1, source_target_pairs={{0,8},{4,12},{8,0},{12,4},{16,24},{20,28},{24,16},{28,20},{1,9},{5... | collective-permute-start | bytes 251912 | tf_op jit(solution)/shard_map/ppermute | solution.py:175
  43.9 6.1 %collective-permute-start.7 = (bf16[328,128]{1,0:T(8,128)(2,1)S(1)}, bf16[328,128]{1,0:T(8,128)(2,1)S(1)}, u32[]{:S(2)}, u32[]{:S(2)}) collective-permute-start(bf16[328,128]{1,0:T(8,128)(2,1)S(1)} %fusion.51), channel_id=1, source_target_pairs={{0,8},{4,12},{8,0},{12,4},{16,24},{20,28},{24,16},{28,20},{1,9},{5... | collective-permute-start | bytes 251912 | tf_op jit(solution)/shard_map/ppermute | solution.py:175
  46.4 7.1 %collective-permute-start.12 = (bf16[328,128]{1,0:T(8,128)(2,1)S(1)}, bf16[328,128]{1,0:T(8,128)(2,1)S(1)}, u32[]{:S(2)}, u32[]{:S(2)}) collective-permute-start(bf16[328,128]{1,0:T(8,128)(2,1)S(1)} %add_convert_fusion.3), channel_id=1, source_target_pairs={{0,16},{4,20},{8,24},{12,28},{16,0},{20,4},{24,8},{28,12},{1,17},{... | collective-permute-start | bytes 251912 | tf_op jit(solution)/shard_map/ppermute | solution.py:175
  50.0 6.3 %collective-permute-start.8 = (bf16[328,128]{1,0:T(8,128)(2,1)S(1)}, bf16[328,128]{1,0:T(8,128)(2,1)S(1)}, u32[]{:S(2)}, u32[]{:S(2)}) collective-permute-start(bf16[328,128]{1,0:T(8,128)(2,1)S(1)} %add_convert_fusion.5), channel_id=1, source_target_pairs={{0,16},{4,20},{8,24},{12,28},{16,0},{20,4},{24,8},{28,12},{1,17},{... | collective-permute-start | bytes 251912 | tf_op jit(solution)/shard_map/ppermute | solution.py:175
  56.4 1.5 %collective-permute-start.13 = (bf16[656,128]{1,0:T(8,128)(2,1)S(1)}, bf16[656,128]{1,0:T(8,128)(2,1)S(1)}, u32[]{:S(2)}, u32[]{:S(2)}) collective-permute-start(bf16[656,128]{1,0:T(8,128)(2,1)S(1)} %pad_maximum_fusion.3), channel_id=1, source_target_pairs={{0,4},{4,0},{8,12},{12,8},{16,20},{20,16},{24,28},{28,24},{1,5},{5... | collective-permute-start | bytes 503816 | tf_op jit(solution)/shard_map/ppermute | solution.py:175

commit v12 on v11

--- a/solution.py
+++ b/solution.py
@@ -241,7 +241,7 @@
     half = count // 4
     first = scatter_lon(part[:, :half], steps)
     second = scatter_lon(part[:, half:], list(reversed(steps)))
-    joined = jnp.concatenate([butterfly(first, lat_steps[1:]), butterfly(second, lat_steps[1:])])
+    joined = butterfly(jnp.concatenate([first, second]), lat_steps[1:])
     return double(joined, "lat", lat_steps[0]).astype(jnp.float32)
 
 

time: 59.9 us -> 59.9 us (level)
  waiting for transfers between devices: 19.8 us -> 22.4 us
  starting transfers between devices: 20.6 us -> 18.1 us
    ppermute x10 -> x8, waiting for transfers between devices: 15.7 us -> 18.3 us  [exchange(): return lax.ppermute(part, axis, [(i, i ^ step) for i in range(size)])]
    ppermute x10 -> x8, starting transfers between devices: 12.3 us -> 9.73 us  [exchange(): return lax.ppermute(part, axis, [(i, i ^ step) for i in range(size)])]
  transfers between devices with their start and end apart: 14 -> 12, of which waited for: 11 -> 11; matrix products, arithmetic and copies ran while one was open for 6% -> 6% of each run, Pallas kernels for 0% -> 0%
where the time goes in v12:
time: 59.9 us; the launch traced here: 59.6 us
  waiting for transfers between devices  22.4 us (37%)
  starting transfers between devices  18.1 us (30%)
  local copies, waits for them, and re-layouts  11 us (18%)
  matrix products  4.22 us (7%)
  other arithmetic  2.43 us (4%)
  between operations  1.46 us (2%)
    ppermute x8, waiting for transfers between devices, exchange(): return lax.ppermute(part, axis, [(i, i ^ step) for i in range(size)])  18.3 us
    ppermute x8, starting transfers between devices, exchange(): return lax.ppermute(part, axis, [(i, i ^ step) for i in range(size)])  9.73 us
    ppermute x2, starting transfers between devices, swap_edges(): lax.ppermute(jnp.concatenate([p.reshape(-1) for p in leads]), axis, down)  5.24 us
    unnamed x67, local copies, waits for them, and re-layouts  4.9 us
    ppermute x2, waiting for transfers between devices, swap_edges(): lax.ppermute(jnp.concatenate([p.reshape(-1) for p in lasts]), axis, up)  3.41 us
    ppermute x2, starting transfers between devices, swap_edges(): lax.ppermute(jnp.concatenate([p.reshape(-1) for p in lasts]), axis, up)  3.09 us
  transfers between devices with their start and end apart: 12, of which 11 were waited for; matrix products, arithmetic and copies ran while one was open for 6% of the time, Pallas kernels for 0%

profile of v12, /device:TPU:0, one launch (start us, length us, event | category | flops | bytes accessed | tf_op | source)
XLA Modules:
  0.0 59.6 jit_solution(10021662068380544323)
XLA Ops:
  0.7 1.0 %fusion.81 = (bf16[32,2,128]{2,1,0:T(2,128)(2,1)S(1)}, bf16[32,2,128]{2,1,0:T(2,128)(2,1)S(1)}) fusion(bf16[32,16,128]{2,1,0:T(8,128)(2,1)} %param.11), kind=kLoop, calls=%fused_computation.207 | loop fusion | bytes 65536 | tf_op jit(solution)/shard_map/slice | solution.py:23
  1.7 0.8 %multiply_exponential_fusion = f32[16,8,8]{0,2,1:T(8,128)S(1)} fusion(s32[16,8,8]{0,2,1:T(8,128)} %param.7), kind=kLoop, calls=%fused_computation.183 | loop fusion | flops 2048 | bytes 8192 | tf_op jit(solution)/shard_map/exp2 | solution.py:50
  2.5 0.2 broadcast_in_dim.21
  2.7 0.2 reshape.201
  2.9 0.3 fusion.65
  3.3 3.9 %collective-permute-start.1 = (bf16[12288]{0:T(1024)(128)(2,1)S(1)}, bf16[12288]{0:T(1024)(128)(2,1)S(1)}, u32[]{:S(2)}, u32[]{:S(2)}) collective-permute-start(bf16[12288]{0:T(1024)(128)(2,1)S(1)} %pad_maximum_fusion.6), channel_id=1, source_target_pairs={{1,0},{2,1},{3,2},{0,3},{5,4},{6,5},{7,6},{4,7},{9,8},{10,9},{11,1... | collective-permute-start | bytes 73736 | tf_op jit(solution)/shard_map/ppermute | solution.py:26
  7.3 0.7 %slice_bitcast_fusion.15 = (bf16[256,128]{1,0:T(8,128)(2,1)S(1)}, bf16[256,128]{1,0:T(8,128)(2,1)}, bf16[256,128]{1,0:T(8,128)(2,1)}, bf16[256,128]{1,0:T(8,128)...) fusion(bf16[4,4,256,128]{3,2,1,0:T(8,128)(2,1)S(1)} %copy-done.1), kind=kLoop, calls=%fused_computation.182 | loop fusion | bytes 2097152 | tf_op jit(solution)/shard_map/squeeze | solution.py:74
  8.1 0.7 %collective-permute-done.1 = bf16[12288]{0:T(1024)(128)(2,1)S(1)} collective-permute-done((bf16[12288]{0:T(1024)(128)(2,1)S(1)}, bf16[12288]{0:T(1024)(128)(2,1)S(1)}, u32[]{:S(2)}, u32[]{:S(2)}) %collective-permute-start.1) | collective-permute-done | bytes 24608 | tf_op jit(solution)/shard_map/ppermute | solution.py:26
  8.8 3.3 %collective-permute-done = bf16[12288]{0:T(1024)(128)(2,1)S(1)} collective-permute-done((bf16[12288]{0:T(1024)(128)(2,1)S(1)}, bf16[12288]{0:T(1024)(128)(2,1)S(1)}, u32[]{:S(2)}, u32[]{:S(2)}) %collective-permute-start) | collective-permute-done | bytes 24608 | tf_op jit(solution)/shard_map/ppermute | solution.py:25
  12.2 1.3 %collective-permute-start.2 = (bf16[7680]{0:T(1024)(128)(2,1)S(1)}, bf16[7680]{0:T(1024)(128)(2,1)S(1)}, u32[]{:S(2)}, u32[]{:S(2)}) collective-permute-start(bf16[7680]{0:T(1024)(128)(2,1)S(1)} %pad_maximum_fusion.7), channel_id=1, source_target_pairs={{4,0},{8,4},{12,8},{16,12},{20,16},{24,20},{28,24},{5,1},{9,5},{13... | collective-permute-start | bytes 46088 | tf_op jit(solution)/shard_map/ppermute | solution.py:26
  13.6 3.0 %collective-permute-start.3 = (bf16[7680]{0:T(1024)(128)(2,1)S(1)}, bf16[7680]{0:T(1024)(128)(2,1)S(1)}, u32[]{:S(2)}, u32[]{:S(2)}) collective-permute-start(bf16[7680]{0:T(1024)(128)(2,1)S(1)} %pad_maximum_fusion.8), channel_id=1, source_target_pairs={{0,4},{4,8},{8,12},{12,16},{16,20},{20,24},{24,28},{1,5},{5,9},{9,... | collective-permute-start | bytes 46088 | tf_op jit(solution)/shard_map/ppermute | solution.py:25
  16.6 0.5 copy.32
  17.8 0.7 %convolution_select_fusion = f32[34,8,3,128]{3,1,2,0:T(8,128)S(1)} fusion(bf16[3,3,128,128]{3,2,1,0:T(8,128)(2,1)S(1)} %copy-done, bf16[36,1,7,2,128]{4,2,3,0,1:T(8,128)(2,1)S(1)} %slice.391, bf16[36,1,8,3,128]{4,2,3,0,1:T(8,128)(2,1)S(1)} %copy.29, pred[8,3]{0,1:T(4,128)(4,1)S(1)} %copy-done.11), kind=kOutput, calls=%fused_computation.3 | convolution fusion | flops 241858560 | bytes 1062936 | tf_op jit(solution)/shard_map/conv_general_dilated | solution.py:126
  18.7 0.2 squeeze.139
  18.9 0.5 copy-done.7
  19.5 0.3 convolution_bitcast_fusion
  19.8 0.5 copy-done.4
  20.4 0.3 convolution_bitcast_fusion.1
  20.7 0.3 convolution_bitcast_fusion.2
  21.0 0.3 convolution_bitcast_fusion.3
  21.4 0.6 copy-done.9
  22.0 0.2 broadcast_select_fusion
  22.2 0.6 %constant_dynamic-update-slice_fusion.31 = bf16[16,8,16,128]{3,0,1,2:T(8,128)(2,1)} fusion(bf16[17,2,9,2,128]{4,0,2,3,1:T(8,128)(2,1)S(1)} %broadcast_select_fusion), kind=kLoop, calls=%fused_computation.162 | loop fusion | bytes 65536
  22.8 0.2 copy.44
  23.0 0.2 reshape.247
  24.1 0.5 fusion
  24.7 1.0 %copy-done.10 = bf16[16,8,16,128]{3,0,1,2:T(8,128)(2,1)S(1)} copy-done((bf16[16,8,16,128]{3,0,1,2:T(8,128)(2,1)S(1)}, bf16[16,8,16,128]{3,0,1,2:T(8,128)(2,1)}, u32[]{:S(2)}) %copy-start.10) | copy-done | bytes 524312
  25.9 0.5 fusion.70
  26.4 0.2 copy.34
  26.6 0.2 pad_maximum_fusion
  26.9 1.3 %collective-permute-start.4 = (bf16[4,656,128]{2,1,0:T(8,128)(2,1)S(1)}, bf16[4,656,128]{2,1,0:T(8,128)(2,1)S(1)}, u32[]{:S(2)}, u32[]{:S(2)}) collective-permute-start(bf16[4,656,128]{2,1,0:T(8,128)(2,1)S(1)} %fusion.4), channel_id=1, source_target_pairs={{0,4},{4,0},{8,12},{12,8},{16,20},{20,16},{24,28},{28,24},{1,5},{5... | collective-permute-start | bytes 2015240 | tf_op jit(solution)/shard_map/ppermute | solution.py:175
  28.3 1.7 %collective-permute-done.4 = bf16[4,656,128]{2,1,0:T(8,128)(2,1)S(1)} collective-permute-done((bf16[4,656,128]{2,1,0:T(8,128)(2,1)S(1)}, bf16[4,656,128]{2,1,0:T(8,128)(2,1)S(1)}, u32[]{:S(2)}, u32[]{:S(2)}) %collective-permute-start.4) | collective-permute-done | bytes 671776 | tf_op jit(solution)/shard_map/ppermute | solution.py:175
  30.2 0.6 collective-permute-start.7
  31.0 5.9 %collective-permute-done.7 = bf16[2,328,128]{2,1,0:T(8,128)(2,1)S(1)} collective-permute-done((bf16[2,328,128]{2,1,0:T(8,128)(2,1)S(1)}, bf16[2,328,128]{2,1,0:T(8,128)(2,1)S(1)}, u32[]{:S(2)}, u32[]{:S(2)}) %collective-permute-start.7) | collective-permute-done | bytes 167968 | tf_op jit(solution)/shard_map/ppermute | solution.py:175
  37.0 0.2 collective-permute-done.5
  37.3 1.6 %collective-permute-start.6 = (bf16[328,128]{1,0:T(8,128)(2,1)S(1)}, bf16[328,128]{1,0:T(8,128)(2,1)S(1)}, u32[]{:S(2)}, u32[]{:S(2)}) collective-permute-start(bf16[328,128]{1,0:T(8,128)(2,1)S(1)} %fusion.68), channel_id=1, source_target_pairs={{0,2},{1,3},{2,0},{3,1},{4,6},{5,7},{6,4},{7,5},{8,10},{9,11},{10,... | collective-permute-start | bytes 251912 | tf_op jit(solution)/shard_map/ppermute | solution.py:175
  38.8 2.6 %collective-permute-done.8 = bf16[328,128]{1,0:T(8,128)(2,1)S(1)} collective-permute-done((bf16[328,128]{1,0:T(8,128)(2,1)S(1)}, bf16[328,128]{1,0:T(8,128)(2,1)S(1)}, u32[]{:S(2)}, u32[]{:S(2)}) %collective-permute-start.8) | collective-permute-done | bytes 84000 | tf_op jit(solution)/shard_map/ppermute | solution.py:175
  41.5 0.3 collective-permute-done.6
  41.8 2.4 %collective-permute-start.9 = (bf16[656,128]{1,0:T(8,128)(2,1)S(1)}, bf16[656,128]{1,0:T(8,128)(2,1)S(1)}, u32[]{:S(2)}, u32[]{:S(2)}) collective-permute-start(bf16[656,128]{1,0:T(8,128)(2,1)S(1)} %pad_maximum_fusion.3), channel_id=1, source_target_pairs={{0,8},{4,12},{8,0},{12,4},{16,24},{20,28},{24,16},{28,20},{1,9},{5... | collective-permute-start | bytes 503816 | tf_op jit(solution)/shard_map/ppermute | solution.py:175
  44.2 3.3 %collective-permute-done.9 = bf16[656,128]{1,0:T(8,128)(2,1)S(1)} collective-permute-done((bf16[656,128]{1,0:T(8,128)(2,1)S(1)}, bf16[656,128]{1,0:T(8,128)(2,1)S(1)}, u32[]{:S(2)}, u32[]{:S(2)}) %collective-permute-start.9) | collective-permute-done | bytes 167968 | tf_op jit(solution)/shard_map/ppermute | solution.py:175
  47.6 3.7 %collective-permute-start.10 = (bf16[656,128]{1,0:T(8,128)(2,1)S(1)}, bf16[656,128]{1,0:T(8,128)(2,1)S(1)}, u32[]{:S(2)}, u32[]{:S(2)}) collective-permute-start(bf16[656,128]{1,0:T(8,128)(2,1)S(1)} %add_convert_fusion.3), channel_id=1, source_target_pairs={{0,16},{4,20},{8,24},{12,28},{16,0},{20,4},{24,8},{28,12},{1,17},{... | collective-permute-start | bytes 503816 | tf_op jit(solution)/shard_map/ppermute | solution.py:175
  51.3 0.3 fusion.84
  51.6 0.7 %copy.39 = f32[16,8,256]{2,1,0:T(8,128)} copy(f32[16,8,256]{2,0,1:T(8,128)S(1)} %fusion.84) | data formatting | bytes 262144 | tf_op jit(solution)/shard_map/rck,kn->rcn/dot_general | solution.py:151
  52.4 4.1 %collective-permute-done.10 = bf16[656,128]{1,0:T(8,128)(2,1)S(1)} collective-permute-done((bf16[656,128]{1,0:T(8,128)(2,1)S(1)}, bf16[656,128]{1,0:T(8,128)(2,1)S(1)}, u32[]{:S(2)}, u32[]{:S(2)}) %collective-permute-start.10) | collective-permute-done | bytes 167968 | tf_op jit(solution)/shard_map/ppermute | solution.py:175
  56.6 1.1 %convolution_convert_fusion = bf16[32,16,128]{2,1,0:T(8,128)(2,1)} fusion(bf16[32,16,1152]{2,1,0:T(8,128)(2,1)S(1)} %slice_dynamic-update-slice_fusion, bf16[1152,128,1]{1,0,2:T(8,128)(2,1)S(1)} %bitcast.219), kind=kOutput, calls=%fused_computation.7 | convolution fusion | flops 151060480 | bytes 1605632 | tf_op jit(solution)/shard_map/rck,kn->rcn/dot_general | solution.py:138
  57.7 0.2 collective-permute-done.11
  58.1 0.8 %slice.411 = f32[1024,128]{1,0:T(8,128)} slice(f32[1312,128]{1,0:T(8,128)S(1)} %convert_multiply_fusion), slice={[0:1024], [0:128]} | slice | bytes 1048576 | tf_op jit(solution)/shard_map/slice | solution.py:168
  58.9 0.7 %slice.412 = f32[288,128]{1,0:T(8,128)} slice(f32[1312,128]{1,0:T(8,128)S(1)} %convert_multiply_fusion), slice={[1024:1312], [0:128]} | slice | bytes 294912 | tf_op jit(solution)/shard_map/slice | solution.py:169
  (126 shorter events, 3.4 us)
Async XLA Ops:
  0.6 17.2 %copy-start = (bf16[3,3,128,128]{3,2,1,0:T(8,128)(2,1)S(1)}, bf16[3,3,128,128]{3,2,1,0:T(8,128)(2,1)}, u32[]{:S(2)}) copy-start(bf16[3,3,128,128]{3,2,1,0:T(8,128)(2,1)} %param.10) | copy-start | bytes 884740
  0.6 2.3 %copy-start.3 = (s32[16,8,256]{2,1,0:T(8,128)S(1)}, s32[16,8,256]{2,1,0:T(8,128)}, u32[]{:S(2)}) copy-start(s32[16,8,256]{2,1,0:T(8,128)} %param.6) | copy-start | bytes 393220
  0.7 6.7 %copy-start.1 = (bf16[4,4,256,128]{3,2,1,0:T(8,128)(2,1)S(1)}, bf16[4,4,256,128]{3,2,1,0:T(8,128)(2,1)}, u32[]{:S(2)}) copy-start(bf16[4,4,256,128]{3,2,1,0:T(8,128)(2,1)} %param.8) | copy-start | bytes 3145732
  3.2 8.8 %copy-start.2 = (bf16[32,16,128]{2,1,0:T(8,128)(2,1)S(1)}, bf16[32,16,128]{2,1,0:T(8,128)(2,1)}, u32[]{:S(2)}) copy-start(bf16[32,16,128]{2,1,0:T(8,128)(2,1)} %param.11) | copy-start | bytes 393220
  3.3 5.5 %collective-permute-start.1 = (bf16[12288]{0:T(1024)(128)(2,1)S(1)}, bf16[12288]{0:T(1024)(128)(2,1)S(1)}, u32[]{:S(2)}, u32[]{:S(2)}) collective-permute-start(bf16[12288]{0:T(1024)(128)(2,1)S(1)} %pad_maximum_fusion.6), channel_id=1, source_target_pairs={{1,0},{2,1},{3,2},{0,3},{5,4},{6,5},{7,6},{4,7},{9,8},{10,9},{11,1... | collective-permute-start | bytes 73736 | tf_op jit(solution)/shard_map/ppermute | solution.py:26
  7.3 4.8 %collective-permute-start = (bf16[12288]{0:T(1024)(128)(2,1)S(1)}, bf16[12288]{0:T(1024)(128)(2,1)S(1)}, u32[]{:S(2)}, u32[]{:S(2)}) collective-permute-start(bf16[12288]{0:T(1024)(128)(2,1)S(1)} %pad_maximum_fusion.5), channel_id=1, source_target_pairs={{0,1},{1,2},{2,3},{3,0},{4,5},{5,6},{6,7},{7,4},{8,9},{9,10},{10,1... | collective-permute-start | bytes 73736 | tf_op jit(solution)/shard_map/ppermute | solution.py:25
  12.2 5.0 %collective-permute-start.2 = (bf16[7680]{0:T(1024)(128)(2,1)S(1)}, bf16[7680]{0:T(1024)(128)(2,1)S(1)}, u32[]{:S(2)}, u32[]{:S(2)}) collective-permute-start(bf16[7680]{0:T(1024)(128)(2,1)S(1)} %pad_maximum_fusion.7), channel_id=1, source_target_pairs={{4,0},{8,4},{12,8},{16,12},{20,16},{24,20},{28,24},{5,1},{9,5},{13... | collective-permute-start | bytes 46088 | tf_op jit(solution)/shard_map/ppermute | solution.py:26
  13.6 3.9 %collective-permute-start.3 = (bf16[7680]{0:T(1024)(128)(2,1)S(1)}, bf16[7680]{0:T(1024)(128)(2,1)S(1)}, u32[]{:S(2)}, u32[]{:S(2)}) collective-permute-start(bf16[7680]{0:T(1024)(128)(2,1)S(1)} %pad_maximum_fusion.8), channel_id=1, source_target_pairs={{0,4},{4,8},{8,12},{12,16},{16,20},{20,24},{24,28},{1,5},{5,9},{9,... | collective-permute-start | bytes 46088 | tf_op jit(solution)/shard_map/ppermute | solution.py:25
  17.2 0.7 %copy-start.11 = (pred[8,3]{0,1:T(4,128)(4,1)S(1)}, pred[8,3]{0,1:T(4,128)(4,1)}, u32[]{:S(2)}) copy-start(pred[8,3]{0,1:T(4,128)(4,1)} %constant.177) | copy-start | bytes 76
  18.6 0.8 %copy-start.7 = (bf16[256,128]{1,0:T(8,128)(2,1)S(1)}, bf16[256,128]{1,0:T(8,128)(2,1)}, u32[]{:S(2)}) copy-start(bf16[256,128]{1,0:T(8,128)(2,1)} %get-tuple-element.9) | copy-start | bytes 196612
  18.6 0.9 %copy-start.8 = (bf16[256,128]{1,0:T(8,128)(2,1)S(1)}, bf16[256,128]{1,0:T(8,128)(2,1)}, u32[]{:S(2)}) copy-start(bf16[256,128]{1,0:T(8,128)(2,1)} %get-tuple-element.10) | copy-start | bytes 196612
  19.5 0.8 %copy-start.4 = (bf16[256,128]{1,0:T(8,128)(2,1)S(1)}, bf16[256,128]{1,0:T(8,128)(2,1)}, u32[]{:S(2)}) copy-start(bf16[256,128]{1,0:T(8,128)(2,1)} %get-tuple-element.13) | copy-start | bytes 196612
  19.5 0.9 %copy-start.5 = (bf16[256,128]{1,0:T(8,128)(2,1)S(1)}, bf16[256,128]{1,0:T(8,128)(2,1)}, u32[]{:S(2)}) copy-start(bf16[256,128]{1,0:T(8,128)(2,1)} %get-tuple-element.14) | copy-start | bytes 196612
  19.5 0.9 %copy-start.6 = (bf16[256,128]{1,0:T(8,128)(2,1)S(1)}, bf16[256,128]{1,0:T(8,128)(2,1)}, u32[]{:S(2)}) copy-start(bf16[256,128]{1,0:T(8,128)(2,1)} %get-tuple-element.15) | copy-start | bytes 196612
  21.3 0.7 %copy-start.9 = (f32[128]{0:T(128)S(1)}, f32[128]{0:T(128)}, u32[]{:S(2)}) copy-start(f32[128]{0:T(128)} %param.9) | copy-start | bytes 1540
  24.6 1.0 %copy-start.10 = (bf16[16,8,16,128]{3,0,1,2:T(8,128)(2,1)S(1)}, bf16[16,8,16,128]{3,0,1,2:T(8,128)(2,1)}, u32[]{:S(2)}) copy-start(bf16[16,8,16,128]{3,0,1,2:T(8,128)(2,1)} %constant_dynamic-update-slice_fusion.31) | copy-start | bytes 1572868
  26.9 3.0 %collective-permute-start.4 = (bf16[4,656,128]{2,1,0:T(8,128)(2,1)S(1)}, bf16[4,656,128]{2,1,0:T(8,128)(2,1)S(1)}, u32[]{:S(2)}, u32[]{:S(2)}) collective-permute-start(bf16[4,656,128]{2,1,0:T(8,128)(2,1)S(1)} %fusion.4), channel_id=1, source_target_pairs={{0,4},{4,0},{8,12},{12,8},{16,20},{20,16},{24,28},{28,24},{1,5},{5... | collective-permute-start | bytes 2015240 | tf_op jit(solution)/shard_map/ppermute | solution.py:175
  30.2 6.6 %collective-permute-start.7 = (bf16[2,328,128]{2,1,0:T(8,128)(2,1)S(1)}, bf16[2,328,128]{2,1,0:T(8,128)(2,1)S(1)}, u32[]{:S(2)}, u32[]{:S(2)}) collective-permute-start(bf16[2,328,128]{2,1,0:T(8,128)(2,1)S(1)} %fusion.49), channel_id=1, source_target_pairs={{0,2},{1,3},{2,0},{3,1},{4,6},{5,7},{6,4},{7,5},{8,10},{9,11},{10,... | collective-permute-start | bytes 503816 | tf_op jit(solution)/shard_map/ppermute | solution.py:175
  30.9 6.3 %collective-permute-start.5 = (bf16[2,328,128]{2,1,0:T(8,128)(2,1)S(1)}, bf16[2,328,128]{2,1,0:T(8,128)(2,1)S(1)}, u32[]{:S(2)}, u32[]{:S(2)}) collective-permute-start(bf16[2,328,128]{2,1,0:T(8,128)(2,1)S(1)} %fusion.48), channel_id=1, source_target_pairs={{0,1},{1,0},{2,3},{3,2},{4,5},{5,4},{6,7},{7,6},{8,9},{9,8},{10,11... | collective-permute-start | bytes 503816 | tf_op jit(solution)/shard_map/ppermute | solution.py:175
  36.9 4.5 %collective-permute-start.8 = (bf16[328,128]{1,0:T(8,128)(2,1)S(1)}, bf16[328,128]{1,0:T(8,128)(2,1)S(1)}, u32[]{:S(2)}, u32[]{:S(2)}) collective-permute-start(bf16[328,128]{1,0:T(8,128)(2,1)S(1)} %fusion.69), channel_id=1, source_target_pairs={{0,1},{1,0},{2,3},{3,2},{4,5},{5,4},{6,7},{7,6},{8,9},{9,8},{10,11... | collective-permute-start | bytes 251912 | tf_op jit(solution)/shard_map/ppermute | solution.py:175
  37.3 4.5 %collective-permute-start.6 = (bf16[328,128]{1,0:T(8,128)(2,1)S(1)}, bf16[328,128]{1,0:T(8,128)(2,1)S(1)}, u32[]{:S(2)}, u32[]{:S(2)}) collective-permute-start(bf16[328,128]{1,0:T(8,128)(2,1)S(1)} %fusion.68), channel_id=1, source_target_pairs={{0,2},{1,3},{2,0},{3,1},{4,6},{5,7},{6,4},{7,5},{8,10},{9,11},{10,... | collective-permute-start | bytes 251912 | tf_op jit(solution)/shard_map/ppermute | solution.py:175
  41.8 5.7 %collective-permute-start.9 = (bf16[656,128]{1,0:T(8,128)(2,1)S(1)}, bf16[656,128]{1,0:T(8,128)(2,1)S(1)}, u32[]{:S(2)}, u32[]{:S(2)}) collective-permute-start(bf16[656,128]{1,0:T(8,128)(2,1)S(1)} %pad_maximum_fusion.3), channel_id=1, source_target_pairs={{0,8},{4,12},{8,0},{12,4},{16,24},{20,28},{24,16},{28,20},{1,9},{5... | collective-permute-start | bytes 503816 | tf_op jit(solution)/shard_map/ppermute | solution.py:175
  47.6 8.8 %collective-permute-start.10 = (bf16[656,128]{1,0:T(8,128)(2,1)S(1)}, bf16[656,128]{1,0:T(8,128)(2,1)S(1)}, u32[]{:S(2)}, u32[]{:S(2)}) collective-permute-start(bf16[656,128]{1,0:T(8,128)(2,1)S(1)} %add_convert_fusion.3), channel_id=1, source_target_pairs={{0,16},{4,20},{8,24},{12,28},{16,0},{20,4},{24,8},{28,12},{1,17},{... | collective-permute-start | bytes 503816 | tf_op jit(solution)/shard_map/ppermute | solution.py:175
  56.5 1.5 %collective-permute-start.11 = (bf16[656,128]{1,0:T(8,128)(2,1)S(1)}, bf16[656,128]{1,0:T(8,128)(2,1)S(1)}, u32[]{:S(2)}, u32[]{:S(2)}) collective-permute-start(bf16[656,128]{1,0:T(8,128)(2,1)S(1)} %add_convert_fusion.2), channel_id=1, source_target_pairs={{0,4},{4,0},{8,12},{12,8},{16,20},{20,16},{24,28},{28,24},{1,5},{5... | collective-permute-start | bytes 503816 | tf_op jit(solution)/shard_map/ppermute | solution.py:175

commit v13 on v11

--- a/solution.py
+++ b/solution.py
@@ -34,9 +34,45 @@
     return joined
 
 
+def edge(field, width, dim, side):
+    if side == 0:
+        return field
+    length = field.shape[dim]
+    start = length - width if side == 1 else 0
+    return lax.slice_in_dim(field, start, start + width, axis=dim)
+
+
 def extend_all(fields, margins):
-    widened = swap_edges(fields, margins, "lon", 1, True)
-    return swap_edges(widened, margins, "lat", 0, False)
+    lat_count, lon_count = (lax.axis_size("lat"), lax.axis_size("lon"))
+    arrived = {}
+    for row_side in (1, 0, -1):
+        for col_side in (1, 0, -1):
+            if row_side == 0 and col_side == 0:
+                continue
+            pairs = [
+                (a * lon_count + o, (a + row_side) * lon_count + (o + col_side) % lon_count)
+                for a in range(lat_count)
+                for o in range(lon_count)
+                if 0 <= a + row_side < lat_count
+            ]
+            pieces = [
+                edge(edge(f, w, 0, row_side), w, 1, col_side) for f, w in zip(fields, margins)
+            ]
+            flat = jnp.concatenate([p.reshape(-1) for p in pieces])
+            got = lax.ppermute(flat, ("lat", "lon"), pairs)
+            at, parts = 0, []
+            for p in pieces:
+                parts.append(got[at : at + p.size].reshape(p.shape))
+                at += p.size
+            arrived[row_side, col_side] = parts
+    joined = []
+    for k, field in enumerate(fields):
+        bands = []
+        for row_side in (1, 0, -1):
+            row = [field if (row_side, s) == (0, 0) else arrived[row_side, s][k] for s in (1, 0, -1)]
+            bands.append(jnp.concatenate(row, axis=1))
+        joined.append(jnp.concatenate(bands, axis=0))
+    return joined
 
 
 def decode(elem_codes, block_exps):

time: 59.9 us -> 74.4 us (1.24)
  starting transfers between devices: 20.6 us -> 40.3 us
  waiting for transfers between devices: 19.8 us -> 13.9 us
    ppermute x4 -> x8, starting transfers between devices: 8.33 us -> 23.8 us  [extend_all(): got = lax.ppermute(flat, ('lat', 'lon'), pairs)]
    ppermute x10, waiting for transfers between devices: 15.7 us -> 11.5 us  [exchange(): return lax.ppermute(part, axis, [(i, i ^ step) for i in range(size)])]
    ppermute x10, starting transfers between devices: 12.3 us -> 16.4 us  [exchange(): return lax.ppermute(part, axis, [(i, i ^ step) for i in range(size)])]
    ppermute x4 -> x8, waiting for transfers between devices: 4.09 us -> 2.45 us  [extend_all(): got = lax.ppermute(flat, ('lat', 'lon'), pairs)]
    unnamed x67 -> x73, local copies, waits for them, and re-layouts: 4.9 us -> 5.42 us
  transfers between devices with their start and end apart: 14 -> 18, of which waited for: 11 -> 10; matrix products, arithmetic and copies ran while one was open for 6% -> 6% of each run, Pallas kernels for 0% -> 0%
where the time goes in v13:
time: 74.4 us; the launch traced here: 73.9 us
  starting transfers between devices  40.3 us (54%)
  waiting for transfers between devices  13.9 us (19%)
  local copies, waits for them, and re-layouts  11.4 us (15%)
  matrix products  4.22 us (6%)
  other arithmetic  2.42 us (3%)
  between operations  1.66 us (2%)
    ppermute x8, starting transfers between devices, extend_all(): got = lax.ppermute(flat, ('lat', 'lon'), pairs)  23.8 us
    ppermute x10, starting transfers between devices, exchange(): return lax.ppermute(part, axis, [(i, i ^ step) for i in range(size)])  16.4 us
    ppermute x10, waiting for transfers between devices, exchange(): return lax.ppermute(part, axis, [(i, i ^ step) for i in range(size)])  11.5 us
    unnamed x73, local copies, waits for them, and re-layouts  5.42 us
    ppermute x8, waiting for transfers between devices, extend_all(): got = lax.ppermute(flat, ('lat', 'lon'), pairs)  2.45 us
  transfers between devices with their start and end apart: 18, of which 10 were waited for; matrix products, arithmetic and copies ran while one was open for 6% of the time, Pallas kernels for 0%

profile of v13, /device:TPU:0, one launch (start us, length us, event | category | flops | bytes accessed | tf_op | source)
XLA Modules:
  0.0 73.9 jit_solution(6606722340593701932)
XLA Ops:
  0.7 0.9 %fusion.80 = (bf16[2,2,128]{2,1,0:T(2,128)(2,1)S(1)}, bf16[2,2,128]{2,1,0:T(2,128)(2,1)S(1)}, bf16[2,2,128]{2,1,0:T(2,128)(2,1)S(1)}, bf16[2,2,128]{2,1,0:T(2,128)(2,1)S(1)}) fusion(bf16[32,16,128]{2,1,0:T(8,128)(2,1)} %param.11), kind=kLoop, calls=%fused_computation.212 | loop fusion | bytes 8192 | tf_op jit(solution)/shard_map/slice | solution.py:42
  1.5 0.8 %multiply_exponential_fusion = f32[16,8,8]{0,2,1:T(8,128)S(1)} fusion(s32[16,8,8]{0,2,1:T(8,128)} %param.7), kind=kLoop, calls=%fused_computation.185 | loop fusion | flops 2048 | bytes 8192 | tf_op jit(solution)/shard_map/exp2 | solution.py:86
  2.8 0.3 fusion.65
  3.1 1.3 %collective-permute-start.4 = (bf16[768]{0:T(1024)(128)(2,1)S(1)}, bf16[768]{0:T(1024)(128)(2,1)S(1)}, u32[]{:S(2)}, u32[]{:S(2)}) collective-permute-start(bf16[768]{0:T(1024)(128)(2,1)S(1)} %pad_maximum_fusion.9), channel_id=1, source_target_pairs={{4,3},{5,0},{6,1},{7,2},{8,7},{9,4},{10,5},{11,6},{12,11},{13,8},{... | collective-permute-start | bytes 4616 | tf_op jit(solution)/shard_map/ppermute | solution.py:62
  4.5 1.3 %collective-permute-start.3 = (bf16[6144]{0:T(1024)(128)(2,1)S(1)}, bf16[6144]{0:T(1024)(128)(2,1)S(1)}, u32[]{:S(2)}, u32[]{:S(2)}) collective-permute-start(bf16[6144]{0:T(1024)(128)(2,1)S(1)} %pad_maximum_fusion.6), channel_id=1, source_target_pairs={{4,0},{5,1},{6,2},{7,3},{8,4},{9,5},{10,6},{11,7},{12,8},{13,9},{1... | collective-permute-start | bytes 36872 | tf_op jit(solution)/shard_map/ppermute | solution.py:62
  5.8 1.3 %collective-permute-start.2 = (bf16[768]{0:T(1024)(128)(2,1)S(1)}, bf16[768]{0:T(1024)(128)(2,1)S(1)}, u32[]{:S(2)}, u32[]{:S(2)}) collective-permute-start(bf16[768]{0:T(1024)(128)(2,1)S(1)} %pad_maximum_fusion.8), channel_id=1, source_target_pairs={{4,1},{5,2},{6,3},{7,0},{8,5},{9,6},{10,7},{11,4},{12,9},{13,10},{... | collective-permute-start | bytes 4616 | tf_op jit(solution)/shard_map/ppermute | solution.py:62
  7.2 3.9 %collective-permute-start.1 = (bf16[12288]{0:T(1024)(128)(2,1)S(1)}, bf16[12288]{0:T(1024)(128)(2,1)S(1)}, u32[]{:S(2)}, u32[]{:S(2)}) collective-permute-start(bf16[12288]{0:T(1024)(128)(2,1)S(1)} %pad_maximum_fusion.5), channel_id=1, source_target_pairs={{0,3},{1,0},{2,1},{3,2},{4,7},{5,4},{6,5},{7,6},{8,11},{9,8},{10,9... | collective-permute-start | bytes 73736 | tf_op jit(solution)/shard_map/ppermute | solution.py:62
  11.3 0.8 %slice_bitcast_fusion.15 = (bf16[256,128]{1,0:T(8,128)(2,1)S(1)}, bf16[256,128]{1,0:T(8,128)(2,1)}, bf16[256,128]{1,0:T(8,128)(2,1)}, bf16[256,128]{1,0:T(8,128)...) fusion(bf16[4,4,256,128]{3,2,1,0:T(8,128)(2,1)S(1)} %copy-done.1), kind=kLoop, calls=%fused_computation.184 | loop fusion | bytes 2097152 | tf_op jit(solution)/shard_map/squeeze | solution.py:110
  12.1 5.3 %collective-permute-start.6 = (bf16[6144]{0:T(1024)(128)(2,1)S(1)}, bf16[6144]{0:T(1024)(128)(2,1)S(1)}, u32[]{:S(2)}, u32[]{:S(2)}) collective-permute-start(bf16[6144]{0:T(1024)(128)(2,1)S(1)} %pad_maximum_fusion.7), channel_id=1, source_target_pairs={{0,4},{1,5},{2,6},{3,7},{4,8},{5,9},{6,10},{7,11},{8,12},{9,13},{1... | collective-permute-start | bytes 36872 | tf_op jit(solution)/shard_map/ppermute | solution.py:62
  17.5 0.5 copy.32
  18.0 7.1 %collective-permute-start.7 = (bf16[768]{0:T(1024)(128)(2,1)S(1)}, bf16[768]{0:T(1024)(128)(2,1)S(1)}, u32[]{:S(2)}, u32[]{:S(2)}) collective-permute-start(bf16[768]{0:T(1024)(128)(2,1)S(1)} %pad_maximum_fusion.11), channel_id=1, source_target_pairs={{0,7},{1,4},{2,5},{3,6},{4,11},{5,8},{6,9},{7,10},{8,15},{9,12},{1... | collective-permute-start | bytes 4616 | tf_op jit(solution)/shard_map/ppermute | solution.py:62
  25.2 1.3 %collective-permute-done.7 = bf16[768]{0:T(1024)(128)(2,1)S(1)} collective-permute-done((bf16[768]{0:T(1024)(128)(2,1)S(1)}, bf16[768]{0:T(1024)(128)(2,1)S(1)}, u32[]{:S(2)}, u32[]{:S(2)}) %collective-permute-start.7) | collective-permute-done | bytes 1568 | tf_op jit(solution)/shard_map/ppermute | solution.py:62
  26.4 3.5 %collective-permute-start.5 = (bf16[768]{0:T(1024)(128)(2,1)S(1)}, bf16[768]{0:T(1024)(128)(2,1)S(1)}, u32[]{:S(2)}, u32[]{:S(2)}) collective-permute-start(bf16[768]{0:T(1024)(128)(2,1)S(1)} %pad_maximum_fusion.10), channel_id=1, source_target_pairs={{0,5},{1,6},{2,7},{3,4},{4,9},{5,10},{6,11},{7,8},{8,13},{9,14},{1... | collective-permute-start | bytes 4616 | tf_op jit(solution)/shard_map/ppermute | solution.py:62
  30.1 1.2 %collective-permute-done.5 = bf16[768]{0:T(1024)(128)(2,1)S(1)} collective-permute-done((bf16[768]{0:T(1024)(128)(2,1)S(1)}, bf16[768]{0:T(1024)(128)(2,1)S(1)}, u32[]{:S(2)}, u32[]{:S(2)}) %collective-permute-start.5) | collective-permute-done | bytes 1568 | tf_op jit(solution)/shard_map/ppermute | solution.py:62
  31.8 0.7 convolution_select_fusion
  32.9 0.5 copy-done.9
  33.5 0.3 convolution_bitcast_fusion
  33.8 0.5 copy-done.5
  34.4 0.3 convolution_bitcast_fusion.1
  34.7 0.5 copy-done.4
  35.2 0.3 convolution_bitcast_fusion.2
  35.5 0.3 convolution_bitcast_fusion.3
  35.9 0.6 copy-done.11
  36.7 0.6 constant_dynamic-update-slice_fusion.31
  38.6 0.5 fusion
  39.2 1.0 %copy-done.12 = bf16[16,8,16,128]{3,0,1,2:T(8,128)(2,1)S(1)} copy-done((bf16[16,8,16,128]{3,0,1,2:T(8,128)(2,1)S(1)}, bf16[16,8,16,128]{3,0,1,2:T(8,128)(2,1)}, u32[]{:S(2)}) %copy-start.12) | copy-done | bytes 524312
  40.5 0.5 fusion.70
  41.5 0.4 collective-permute-start.8
  41.9 1.7 %collective-permute-done.8 = bf16[4,656,128]{2,1,0:T(8,128)(2,1)S(1)} collective-permute-done((bf16[4,656,128]{2,1,0:T(8,128)(2,1)S(1)}, bf16[4,656,128]{2,1,0:T(8,128)(2,1)S(1)}, u32[]{:S(2)}, u32[]{:S(2)}) %collective-permute-start.8) | collective-permute-done | bytes 671776 | tf_op jit(solution)/shard_map/ppermute | solution.py:211
  44.0 1.6 %collective-permute-start.13 = (bf16[2,328,128]{2,1,0:T(8,128)(2,1)S(1)}, bf16[2,328,128]{2,1,0:T(8,128)(2,1)S(1)}, u32[]{:S(2)}, u32[]{:S(2)}) collective-permute-start(bf16[2,328,128]{2,1,0:T(8,128)(2,1)S(1)} %fusion.49), channel_id=1, source_target_pairs={{0,2},{1,3},{2,0},{3,1},{4,6},{5,7},{6,4},{7,5},{8,10},{9,11},{10,... | collective-permute-start | bytes 503816 | tf_op jit(solution)/shard_map/ppermute | solution.py:211
  45.6 0.3 fusion.85
  45.9 0.7 copy.39
  46.6 1.8 %collective-permute-start.9 = (bf16[2,328,128]{2,1,0:T(8,128)(2,1)S(1)}, bf16[2,328,128]{2,1,0:T(8,128)(2,1)S(1)}, u32[]{:S(2)}, u32[]{:S(2)}) collective-permute-start(bf16[2,328,128]{2,1,0:T(8,128)(2,1)S(1)} %fusion.48), channel_id=1, source_target_pairs={{0,1},{1,0},{2,3},{3,2},{4,5},{5,4},{6,7},{7,6},{8,9},{9,8},{10,11... | collective-permute-start | bytes 503816 | tf_op jit(solution)/shard_map/ppermute | solution.py:211
  48.4 2.1 %collective-permute-done.13 = bf16[2,328,128]{2,1,0:T(8,128)(2,1)S(1)} collective-permute-done((bf16[2,328,128]{2,1,0:T(8,128)(2,1)S(1)}, bf16[2,328,128]{2,1,0:T(8,128)(2,1)S(1)}, u32[]{:S(2)}, u32[]{:S(2)}) %collective-permute-start.13) | collective-permute-done | bytes 167968 | tf_op jit(solution)/shard_map/ppermute | solution.py:211
  50.6 1.9 %collective-permute-start.14 = (bf16[328,128]{1,0:T(8,128)(2,1)S(1)}, bf16[328,128]{1,0:T(8,128)(2,1)S(1)}, u32[]{:S(2)}, u32[]{:S(2)}) collective-permute-start(bf16[328,128]{1,0:T(8,128)(2,1)S(1)} %fusion.69), channel_id=1, source_target_pairs={{0,1},{1,0},{2,3},{3,2},{4,5},{5,4},{6,7},{7,6},{8,9},{9,8},{10,11... | collective-permute-start | bytes 251912 | tf_op jit(solution)/shard_map/ppermute | solution.py:211
  52.4 0.6 collective-permute-done.9
  53.1 1.0 %collective-permute-start.10 = (bf16[328,128]{1,0:T(8,128)(2,1)S(1)}, bf16[328,128]{1,0:T(8,128)(2,1)S(1)}, u32[]{:S(2)}, u32[]{:S(2)}) collective-permute-start(bf16[328,128]{1,0:T(8,128)(2,1)S(1)} %fusion.68), channel_id=1, source_target_pairs={{0,2},{1,3},{2,0},{3,1},{4,6},{5,7},{6,4},{7,5},{8,10},{9,11},{10,... | collective-permute-start | bytes 251912 | tf_op jit(solution)/shard_map/ppermute | solution.py:211
  54.1 1.0 %collective-permute-done.14 = bf16[328,128]{1,0:T(8,128)(2,1)S(1)} collective-permute-done((bf16[328,128]{1,0:T(8,128)(2,1)S(1)}, bf16[328,128]{1,0:T(8,128)(2,1)S(1)}, u32[]{:S(2)}, u32[]{:S(2)}) %collective-permute-start.14) | collective-permute-done | bytes 84000 | tf_op jit(solution)/shard_map/ppermute | solution.py:211
  55.1 3.3 %collective-permute-start.15 = (bf16[328,128]{1,0:T(8,128)(2,1)S(1)}, bf16[328,128]{1,0:T(8,128)(2,1)S(1)}, u32[]{:S(2)}, u32[]{:S(2)}) collective-permute-start(bf16[328,128]{1,0:T(8,128)(2,1)S(1)} %fusion.50), channel_id=1, source_target_pairs={{0,8},{4,12},{8,0},{12,4},{16,24},{20,28},{24,16},{28,20},{1,9},{5... | collective-permute-start | bytes 251912 | tf_op jit(solution)/shard_map/ppermute | solution.py:211
  58.5 1.3 %collective-permute-start.11 = (bf16[328,128]{1,0:T(8,128)(2,1)S(1)}, bf16[328,128]{1,0:T(8,128)(2,1)S(1)}, u32[]{:S(2)}, u32[]{:S(2)}) collective-permute-start(bf16[328,128]{1,0:T(8,128)(2,1)S(1)} %fusion.51), channel_id=1, source_target_pairs={{0,8},{4,12},{8,0},{12,4},{16,24},{20,28},{24,16},{28,20},{1,9},{5... | collective-permute-start | bytes 251912 | tf_op jit(solution)/shard_map/ppermute | solution.py:211
  59.8 1.1 %collective-permute-done.15 = bf16[328,128]{1,0:T(8,128)(2,1)S(1)} collective-permute-done((bf16[328,128]{1,0:T(8,128)(2,1)S(1)}, bf16[328,128]{1,0:T(8,128)(2,1)S(1)}, u32[]{:S(2)}, u32[]{:S(2)}) %collective-permute-start.15) | collective-permute-done | bytes 84000 | tf_op jit(solution)/shard_map/ppermute | solution.py:211
  60.9 3.6 %collective-permute-start.16 = (bf16[328,128]{1,0:T(8,128)(2,1)S(1)}, bf16[328,128]{1,0:T(8,128)(2,1)S(1)}, u32[]{:S(2)}, u32[]{:S(2)}) collective-permute-start(bf16[328,128]{1,0:T(8,128)(2,1)S(1)} %add_convert_fusion.3), channel_id=1, source_target_pairs={{0,16},{4,20},{8,24},{12,28},{16,0},{20,4},{24,8},{28,12},{1,17},{... | collective-permute-start | bytes 251912 | tf_op jit(solution)/shard_map/ppermute | solution.py:211
  64.6 1.4 %collective-permute-start.12 = (bf16[328,128]{1,0:T(8,128)(2,1)S(1)}, bf16[328,128]{1,0:T(8,128)(2,1)S(1)}, u32[]{:S(2)}, u32[]{:S(2)}) collective-permute-start(bf16[328,128]{1,0:T(8,128)(2,1)S(1)} %add_convert_fusion.5), channel_id=1, source_target_pairs={{0,16},{4,20},{8,24},{12,28},{16,0},{20,4},{24,8},{28,12},{1,17},{... | collective-permute-start | bytes 251912 | tf_op jit(solution)/shard_map/ppermute | solution.py:211
  66.0 2.1 %collective-permute-done.16 = bf16[328,128]{1,0:T(8,128)(2,1)S(1)} collective-permute-done((bf16[328,128]{1,0:T(8,128)(2,1)S(1)}, bf16[328,128]{1,0:T(8,128)(2,1)S(1)}, u32[]{:S(2)}, u32[]{:S(2)}) %collective-permute-start.16) | collective-permute-done | bytes 84000 | tf_op jit(solution)/shard_map/ppermute | solution.py:211
  68.1 2.7 %collective-permute-done.12 = bf16[328,128]{1,0:T(8,128)(2,1)S(1)} collective-permute-done((bf16[328,128]{1,0:T(8,128)(2,1)S(1)}, bf16[328,128]{1,0:T(8,128)(2,1)S(1)}, u32[]{:S(2)}, u32[]{:S(2)}) %collective-permute-start.12) | collective-permute-done | bytes 84000 | tf_op jit(solution)/shard_map/ppermute | solution.py:211
  70.9 1.1 %convolution_convert_fusion = bf16[32,16,128]{2,1,0:T(8,128)(2,1)} fusion(bf16[32,16,1152]{2,1,0:T(8,128)(2,1)S(1)} %slice_dynamic-update-slice_fusion, bf16[1152,128,1]{1,0,2:T(8,128)(2,1)S(1)} %bitcast.235), kind=kOutput, calls=%fused_computation.7 | convolution fusion | flops 151060480 | bytes 1605632 | tf_op jit(solution)/shard_map/rck,kn->rcn/dot_general | solution.py:174
  72.4 0.8 %slice.541 = f32[1024,128]{1,0:T(8,128)} slice(f32[1312,128]{1,0:T(8,128)S(1)} %convert_multiply_fusion), slice={[0:1024], [0:128]} | slice | bytes 1048576 | tf_op jit(solution)/shard_map/slice | solution.py:204
  73.2 0.7 slice.542
  (158 shorter events, 5.0 us)
Async XLA Ops:
  0.6 31.1 %copy-start = (bf16[3,3,128,128]{3,2,1,0:T(8,128)(2,1)S(1)}, bf16[3,3,128,128]{3,2,1,0:T(8,128)(2,1)}, u32[]{:S(2)}) copy-start(bf16[3,3,128,128]{3,2,1,0:T(8,128)(2,1)} %param.10) | copy-start | bytes 884740
  0.6 3.8 %copy-start.2 = (bf16[32,16,128]{2,1,0:T(8,128)(2,1)S(1)}, bf16[32,16,128]{2,1,0:T(8,128)(2,1)}, u32[]{:S(2)}) copy-start(bf16[32,16,128]{2,1,0:T(8,128)(2,1)} %param.11) | copy-start | bytes 393220
  0.7 2.1 %copy-start.3 = (s32[16,8,256]{2,1,0:T(8,128)S(1)}, s32[16,8,256]{2,1,0:T(8,128)}, u32[]{:S(2)}) copy-start(s32[16,8,256]{2,1,0:T(8,128)} %param.6) | copy-start | bytes 393220
  0.7 10.6 %copy-start.1 = (bf16[4,4,256,128]{3,2,1,0:T(8,128)(2,1)S(1)}, bf16[4,4,256,128]{3,2,1,0:T(8,128)(2,1)}, u32[]{:S(2)}) copy-start(bf16[4,4,256,128]{3,2,1,0:T(8,128)(2,1)} %param.8) | copy-start | bytes 3145732
  3.1 9.0 %collective-permute-start.4 = (bf16[768]{0:T(1024)(128)(2,1)S(1)}, bf16[768]{0:T(1024)(128)(2,1)S(1)}, u32[]{:S(2)}, u32[]{:S(2)}) collective-permute-start(bf16[768]{0:T(1024)(128)(2,1)S(1)} %pad_maximum_fusion.9), channel_id=1, source_target_pairs={{4,3},{5,0},{6,1},{7,2},{8,7},{9,4},{10,5},{11,6},{12,11},{13,8},{... | collective-permute-start | bytes 4616 | tf_op jit(solution)/shard_map/ppermute | solution.py:62
  4.5 26.8 %collective-permute-start.3 = (bf16[6144]{0:T(1024)(128)(2,1)S(1)}, bf16[6144]{0:T(1024)(128)(2,1)S(1)}, u32[]{:S(2)}, u32[]{:S(2)}) collective-permute-start(bf16[6144]{0:T(1024)(128)(2,1)S(1)} %pad_maximum_fusion.6), channel_id=1, source_target_pairs={{4,0},{5,1},{6,2},{7,3},{8,4},{9,5},{10,6},{11,7},{12,8},{13,9},{1... | collective-permute-start | bytes 36872 | tf_op jit(solution)/shard_map/ppermute | solution.py:62
  5.8 12.2 %collective-permute-start.2 = (bf16[768]{0:T(1024)(128)(2,1)S(1)}, bf16[768]{0:T(1024)(128)(2,1)S(1)}, u32[]{:S(2)}, u32[]{:S(2)}) collective-permute-start(bf16[768]{0:T(1024)(128)(2,1)S(1)} %pad_maximum_fusion.8), channel_id=1, source_target_pairs={{4,1},{5,2},{6,3},{7,0},{8,5},{9,6},{10,7},{11,4},{12,9},{13,10},{... | collective-permute-start | bytes 4616 | tf_op jit(solution)/shard_map/ppermute | solution.py:62
  7.2 24.2 %collective-permute-start.1 = (bf16[12288]{0:T(1024)(128)(2,1)S(1)}, bf16[12288]{0:T(1024)(128)(2,1)S(1)}, u32[]{:S(2)}, u32[]{:S(2)}) collective-permute-start(bf16[12288]{0:T(1024)(128)(2,1)S(1)} %pad_maximum_fusion.5), channel_id=1, source_target_pairs={{0,3},{1,0},{2,1},{3,2},{4,7},{5,4},{6,5},{7,6},{8,11},{9,8},{10,9... | collective-permute-start | bytes 73736 | tf_op jit(solution)/shard_map/ppermute | solution.py:62
  11.2 20.2 %collective-permute-start = (bf16[12288]{0:T(1024)(128)(2,1)S(1)}, bf16[12288]{0:T(1024)(128)(2,1)S(1)}, u32[]{:S(2)}, u32[]{:S(2)}) collective-permute-start(bf16[12288]{0:T(1024)(128)(2,1)S(1)} %pad_maximum_fusion.4), channel_id=1, source_target_pairs={{0,1},{1,2},{2,3},{3,0},{4,5},{5,6},{6,7},{7,4},{8,9},{9,10},{10,1... | collective-permute-start | bytes 73736 | tf_op jit(solution)/shard_map/ppermute | solution.py:62
  12.1 19.2 %collective-permute-start.6 = (bf16[6144]{0:T(1024)(128)(2,1)S(1)}, bf16[6144]{0:T(1024)(128)(2,1)S(1)}, u32[]{:S(2)}, u32[]{:S(2)}) collective-permute-start(bf16[6144]{0:T(1024)(128)(2,1)S(1)} %pad_maximum_fusion.7), channel_id=1, source_target_pairs={{0,4},{1,5},{2,6},{3,7},{4,8},{5,9},{6,10},{7,11},{8,12},{9,13},{1... | collective-permute-start | bytes 36872 | tf_op jit(solution)/shard_map/ppermute | solution.py:62
  18.0 8.4 %collective-permute-start.7 = (bf16[768]{0:T(1024)(128)(2,1)S(1)}, bf16[768]{0:T(1024)(128)(2,1)S(1)}, u32[]{:S(2)}, u32[]{:S(2)}) collective-permute-start(bf16[768]{0:T(1024)(128)(2,1)S(1)} %pad_maximum_fusion.11), channel_id=1, source_target_pairs={{0,7},{1,4},{2,5},{3,6},{4,11},{5,8},{6,9},{7,10},{8,15},{9,12},{1... | collective-permute-start | bytes 4616 | tf_op jit(solution)/shard_map/ppermute | solution.py:62
  25.1 6.6 %copy-start.13 = (pred[8,3]{0,1:T(4,128)(4,1)S(1)}, pred[8,3]{0,1:T(4,128)(4,1)}, u32[]{:S(2)}) copy-start(pred[8,3]{0,1:T(4,128)(4,1)} %constant.177) | copy-start | bytes 76
  26.4 4.8 %collective-permute-start.5 = (bf16[768]{0:T(1024)(128)(2,1)S(1)}, bf16[768]{0:T(1024)(128)(2,1)S(1)}, u32[]{:S(2)}, u32[]{:S(2)}) collective-permute-start(bf16[768]{0:T(1024)(128)(2,1)S(1)} %pad_maximum_fusion.10), channel_id=1, source_target_pairs={{0,5},{1,6},{2,7},{3,4},{4,9},{5,10},{6,11},{7,8},{8,13},{9,14},{1... | collective-permute-start | bytes 4616 | tf_op jit(solution)/shard_map/ppermute | solution.py:62
  32.6 0.8 %copy-start.9 = (bf16[256,128]{1,0:T(8,128)(2,1)S(1)}, bf16[256,128]{1,0:T(8,128)(2,1)}, u32[]{:S(2)}) copy-start(bf16[256,128]{1,0:T(8,128)(2,1)} %get-tuple-element.13) | copy-start | bytes 196612
  32.6 0.9 %copy-start.10 = (bf16[256,128]{1,0:T(8,128)(2,1)S(1)}, bf16[256,128]{1,0:T(8,128)(2,1)}, u32[]{:S(2)}) copy-start(bf16[256,128]{1,0:T(8,128)(2,1)} %get-tuple-element.14) | copy-start | bytes 196612
  33.5 0.8 %copy-start.5 = (bf16[256,128]{1,0:T(8,128)(2,1)S(1)}, bf16[256,128]{1,0:T(8,128)(2,1)}, u32[]{:S(2)}) copy-start(bf16[256,128]{1,0:T(8,128)(2,1)} %get-tuple-element.16) | copy-start | bytes 196612
  33.5 0.9 %copy-start.6 = (bf16[256,128]{1,0:T(8,128)(2,1)S(1)}, bf16[256,128]{1,0:T(8,128)(2,1)}, u32[]{:S(2)}) copy-start(bf16[256,128]{1,0:T(8,128)(2,1)} %get-tuple-element.17) | copy-start | bytes 196612
  33.5 0.9 %copy-start.7 = (bf16[256,128]{1,0:T(8,128)(2,1)S(1)}, bf16[256,128]{1,0:T(8,128)(2,1)}, u32[]{:S(2)}) copy-start(bf16[256,128]{1,0:T(8,128)(2,1)} %get-tuple-element.18) | copy-start | bytes 196612
  33.5 0.9 %copy-start.8 = (bf16[256,128]{1,0:T(8,128)(2,1)S(1)}, bf16[256,128]{1,0:T(8,128)(2,1)}, u32[]{:S(2)}) copy-start(bf16[256,128]{1,0:T(8,128)(2,1)} %get-tuple-element.19) | copy-start | bytes 196612
  34.4 0.8 %copy-start.4 = (bf16[256,128]{1,0:T(8,128)(2,1)S(1)}, bf16[256,128]{1,0:T(8,128)(2,1)}, u32[]{:S(2)}) copy-start(bf16[256,128]{1,0:T(8,128)(2,1)} %get-tuple-element.23) | copy-start | bytes 196612
  35.8 0.7 copy-start.11
  39.1 1.0 %copy-start.12 = (bf16[16,8,16,128]{3,0,1,2:T(8,128)(2,1)S(1)}, bf16[16,8,16,128]{3,0,1,2:T(8,128)(2,1)}, u32[]{:S(2)}) copy-start(bf16[16,8,16,128]{3,0,1,2:T(8,128)(2,1)} %constant_dynamic-update-slice_fusion.31) | copy-start | bytes 1572868
  41.5 2.2 %collective-permute-start.8 = (bf16[4,656,128]{2,1,0:T(8,128)(2,1)S(1)}, bf16[4,656,128]{2,1,0:T(8,128)(2,1)S(1)}, u32[]{:S(2)}, u32[]{:S(2)}) collective-permute-start(bf16[4,656,128]{2,1,0:T(8,128)(2,1)S(1)} %fusion.4), channel_id=1, source_target_pairs={{0,4},{4,0},{8,12},{12,8},{16,20},{20,16},{24,28},{28,24},{1,5},{5... | collective-permute-start | bytes 2015240 | tf_op jit(solution)/shard_map/ppermute | solution.py:211
  44.0 6.5 %collective-permute-start.13 = (bf16[2,328,128]{2,1,0:T(8,128)(2,1)S(1)}, bf16[2,328,128]{2,1,0:T(8,128)(2,1)S(1)}, u32[]{:S(2)}, u32[]{:S(2)}) collective-permute-start(bf16[2,328,128]{2,1,0:T(8,128)(2,1)S(1)} %fusion.49), channel_id=1, source_target_pairs={{0,2},{1,3},{2,0},{3,1},{4,6},{5,7},{6,4},{7,5},{8,10},{9,11},{10,... | collective-permute-start | bytes 503816 | tf_op jit(solution)/shard_map/ppermute | solution.py:211
  46.6 6.4 %collective-permute-start.9 = (bf16[2,328,128]{2,1,0:T(8,128)(2,1)S(1)}, bf16[2,328,128]{2,1,0:T(8,128)(2,1)S(1)}, u32[]{:S(2)}, u32[]{:S(2)}) collective-permute-start(bf16[2,328,128]{2,1,0:T(8,128)(2,1)S(1)} %fusion.48), channel_id=1, source_target_pairs={{0,1},{1,0},{2,3},{3,2},{4,5},{5,4},{6,7},{7,6},{8,9},{9,8},{10,11... | collective-permute-start | bytes 503816 | tf_op jit(solution)/shard_map/ppermute | solution.py:211
  50.6 4.5 %collective-permute-start.14 = (bf16[328,128]{1,0:T(8,128)(2,1)S(1)}, bf16[328,128]{1,0:T(8,128)(2,1)S(1)}, u32[]{:S(2)}, u32[]{:S(2)}) collective-permute-start(bf16[328,128]{1,0:T(8,128)(2,1)S(1)} %fusion.69), channel_id=1, source_target_pairs={{0,1},{1,0},{2,3},{3,2},{4,5},{5,4},{6,7},{7,6},{8,9},{9,8},{10,11... | collective-permute-start | bytes 251912 | tf_op jit(solution)/shard_map/ppermute | solution.py:211
  53.1 5.4 %collective-permute-start.10 = (bf16[328,128]{1,0:T(8,128)(2,1)S(1)}, bf16[328,128]{1,0:T(8,128)(2,1)S(1)}, u32[]{:S(2)}, u32[]{:S(2)}) collective-permute-start(bf16[328,128]{1,0:T(8,128)(2,1)S(1)} %fusion.68), channel_id=1, source_target_pairs={{0,2},{1,3},{2,0},{3,1},{4,6},{5,7},{6,4},{7,5},{8,10},{9,11},{10,... | collective-permute-start | bytes 251912 | tf_op jit(solution)/shard_map/ppermute | solution.py:211
  55.1 5.8 %collective-permute-start.15 = (bf16[328,128]{1,0:T(8,128)(2,1)S(1)}, bf16[328,128]{1,0:T(8,128)(2,1)S(1)}, u32[]{:S(2)}, u32[]{:S(2)}) collective-permute-start(bf16[328,128]{1,0:T(8,128)(2,1)S(1)} %fusion.50), channel_id=1, source_target_pairs={{0,8},{4,12},{8,0},{12,4},{16,24},{20,28},{24,16},{28,20},{1,9},{5... | collective-permute-start | bytes 251912 | tf_op jit(solution)/shard_map/ppermute | solution.py:211
  58.5 6.1 %collective-permute-start.11 = (bf16[328,128]{1,0:T(8,128)(2,1)S(1)}, bf16[328,128]{1,0:T(8,128)(2,1)S(1)}, u32[]{:S(2)}, u32[]{:S(2)}) collective-permute-start(bf16[328,128]{1,0:T(8,128)(2,1)S(1)} %fusion.51), channel_id=1, source_target_pairs={{0,8},{4,12},{8,0},{12,4},{16,24},{20,28},{24,16},{28,20},{1,9},{5... | collective-permute-start | bytes 251912 | tf_op jit(solution)/shard_map/ppermute | solution.py:211
  60.9 7.1 %collective-permute-start.16 = (bf16[328,128]{1,0:T(8,128)(2,1)S(1)}, bf16[328,128]{1,0:T(8,128)(2,1)S(1)}, u32[]{:S(2)}, u32[]{:S(2)}) collective-permute-start(bf16[328,128]{1,0:T(8,128)(2,1)S(1)} %add_convert_fusion.3), channel_id=1, source_target_pairs={{0,16},{4,20},{8,24},{12,28},{16,0},{20,4},{24,8},{28,12},{1,17},{... | collective-permute-start | bytes 251912 | tf_op jit(solution)/shard_map/ppermute | solution.py:211
  64.6 6.2 %collective-permute-start.12 = (bf16[328,128]{1,0:T(8,128)(2,1)S(1)}, bf16[328,128]{1,0:T(8,128)(2,1)S(1)}, u32[]{:S(2)}, u32[]{:S(2)}) collective-permute-start(bf16[328,128]{1,0:T(8,128)(2,1)S(1)} %add_convert_fusion.5), channel_id=1, source_target_pairs={{0,16},{4,20},{8,24},{12,28},{16,0},{20,4},{24,8},{28,12},{1,17},{... | collective-permute-start | bytes 251912 | tf_op jit(solution)/shard_map/ppermute | solution.py:211
  70.8 1.5 %collective-permute-start.17 = (bf16[656,128]{1,0:T(8,128)(2,1)S(1)}, bf16[656,128]{1,0:T(8,128)(2,1)S(1)}, u32[]{:S(2)}, u32[]{:S(2)}) collective-permute-start(bf16[656,128]{1,0:T(8,128)(2,1)S(1)} %pad_maximum_fusion.3), channel_id=1, source_target_pairs={{0,4},{4,0},{8,12},{12,8},{16,20},{20,16},{24,28},{28,24},{1,5},{5... | collective-permute-start | bytes 503816 | tf_op jit(solution)/shard_map/ppermute | solution.py:211

commit v14 on v12

--- a/solution.py
+++ b/solution.py
@@ -238,11 +238,8 @@
         return reduce_lat(mine)
     pair = rows.reshape((lon_count, 2, count // 2) + rows.shape[2:])
     part = halve(pair, "lat", lat_steps[0], 1)
-    half = count // 4
-    first = scatter_lon(part[:, :half], steps)
-    second = scatter_lon(part[:, half:], list(reversed(steps)))
-    joined = butterfly(jnp.concatenate([first, second]), lat_steps[1:])
-    return double(joined, "lat", lat_steps[0]).astype(jnp.float32)
+    owned = butterfly(scatter_lon(part, steps), lat_steps[1:])
+    return double(owned, "lat", lat_steps[0]).astype(jnp.float32)
 
 
 def solution(mesh):

time: 59.9 us -> 62 us (1.035)
  waiting for transfers between devices: 22.4 us -> 28.7 us
  starting transfers between devices: 18.1 us -> 15.7 us
  local copies, waits for them, and re-layouts: 11 us -> 9.27 us
    ppermute x8 -> x6, waiting for transfers between devices: 18.3 us -> 24.6 us  [exchange(): return lax.ppermute(part, axis, [(i, i ^ step) for i in range(size)])]
    ppermute x8 -> x6, starting transfers between devices: 9.73 us -> 7.33 us  [exchange(): return lax.ppermute(part, axis, [(i, i ^ step) for i in range(size)])]
    unnamed x67 -> x65, local copies, waits for them, and re-layouts: 4.9 us -> 3.31 us
  transfers between devices with their start and end apart: 12 -> 10, of which waited for: 11 -> 9; matrix products, arithmetic and copies ran while one was open for 6% -> 6% of each run, Pallas kernels for 0% -> 0%
where the time goes in v14:
time: 62 us; the launch traced here: 61.7 us
  waiting for transfers between devices  28.7 us (46%)
  starting transfers between devices  15.7 us (25%)
  local copies, waits for them, and re-layouts  9.27 us (15%)
  matrix products  4.24 us (7%)
  other arithmetic  2.39 us (4%)
  between operations  1.44 us (2%)
    ppermute x6, waiting for transfers between devices, exchange(): return lax.ppermute(part, axis, [(i, i ^ step) for i in range(size)])  24.6 us
    ppermute x6, starting transfers between devices, exchange(): return lax.ppermute(part, axis, [(i, i ^ step) for i in range(size)])  7.33 us
    ppermute x2, starting transfers between devices, swap_edges(): lax.ppermute(jnp.concatenate([p.reshape(-1) for p in leads]), axis, down)  5.24 us
    ppermute x2, waiting for transfers between devices, swap_edges(): lax.ppermute(jnp.concatenate([p.reshape(-1) for p in lasts]), axis, up)  3.41 us
    unnamed x65, local copies, waits for them, and re-layouts  3.31 us
    ppermute x2, starting transfers between devices, swap_edges(): lax.ppermute(jnp.concatenate([p.reshape(-1) for p in lasts]), axis, up)  3.09 us
  transfers between devices with their start and end apart: 10, of which 9 were waited for; matrix products, arithmetic and copies ran while one was open for 6% of the time, Pallas kernels for 0%

profile of v14, /device:TPU:0, one launch (start us, length us, event | category | flops | bytes accessed | tf_op | source)
XLA Modules:
  0.0 61.7 jit_solution(11007692016979683494)
XLA Ops:
  0.7 1.0 %fusion.77 = (bf16[32,2,128]{2,1,0:T(2,128)(2,1)S(1)}, bf16[32,2,128]{2,1,0:T(2,128)(2,1)S(1)}) fusion(bf16[32,16,128]{2,1,0:T(8,128)(2,1)} %param.11), kind=kLoop, calls=%fused_computation.198 | loop fusion | bytes 65536 | tf_op jit(solution)/shard_map/slice | solution.py:23
  1.7 0.8 %multiply_exponential_fusion = f32[16,8,8]{0,2,1:T(8,128)S(1)} fusion(s32[16,8,8]{0,2,1:T(8,128)} %param.7), kind=kLoop, calls=%fused_computation.175 | loop fusion | flops 2048 | bytes 8192 | tf_op jit(solution)/shard_map/exp2 | solution.py:50
  2.5 0.2 broadcast_in_dim.21
  2.7 0.2 reshape.196
  2.9 0.3 fusion.64
  3.3 3.9 %collective-permute-start.1 = (bf16[12288]{0:T(1024)(128)(2,1)S(1)}, bf16[12288]{0:T(1024)(128)(2,1)S(1)}, u32[]{:S(2)}, u32[]{:S(2)}) collective-permute-start(bf16[12288]{0:T(1024)(128)(2,1)S(1)} %pad_maximum_fusion.5), channel_id=1, source_target_pairs={{1,0},{2,1},{3,2},{0,3},{5,4},{6,5},{7,6},{4,7},{9,8},{10,9},{11,1... | collective-permute-start | bytes 73736 | tf_op jit(solution)/shard_map/ppermute | solution.py:26
  7.3 0.7 %slice_bitcast_fusion.15 = (bf16[256,128]{1,0:T(8,128)(2,1)S(1)}, bf16[256,128]{1,0:T(8,128)(2,1)}, bf16[256,128]{1,0:T(8,128)(2,1)}, bf16[256,128]{1,0:T(8,128)...) fusion(bf16[4,4,256,128]{3,2,1,0:T(8,128)(2,1)S(1)} %copy-done.1), kind=kLoop, calls=%fused_computation.174 | loop fusion | bytes 2097152 | tf_op jit(solution)/shard_map/squeeze | solution.py:74
  8.1 0.7 %collective-permute-done.1 = bf16[12288]{0:T(1024)(128)(2,1)S(1)} collective-permute-done((bf16[12288]{0:T(1024)(128)(2,1)S(1)}, bf16[12288]{0:T(1024)(128)(2,1)S(1)}, u32[]{:S(2)}, u32[]{:S(2)}) %collective-permute-start.1) | collective-permute-done | bytes 24608 | tf_op jit(solution)/shard_map/ppermute | solution.py:26
  8.8 3.3 %collective-permute-done = bf16[12288]{0:T(1024)(128)(2,1)S(1)} collective-permute-done((bf16[12288]{0:T(1024)(128)(2,1)S(1)}, bf16[12288]{0:T(1024)(128)(2,1)S(1)}, u32[]{:S(2)}, u32[]{:S(2)}) %collective-permute-start) | collective-permute-done | bytes 24608 | tf_op jit(solution)/shard_map/ppermute | solution.py:25
  12.2 1.3 %collective-permute-start.2 = (bf16[7680]{0:T(1024)(128)(2,1)S(1)}, bf16[7680]{0:T(1024)(128)(2,1)S(1)}, u32[]{:S(2)}, u32[]{:S(2)}) collective-permute-start(bf16[7680]{0:T(1024)(128)(2,1)S(1)} %pad_maximum_fusion.6), channel_id=1, source_target_pairs={{4,0},{8,4},{12,8},{16,12},{20,16},{24,20},{28,24},{5,1},{9,5},{13... | collective-permute-start | bytes 46088 | tf_op jit(solution)/shard_map/ppermute | solution.py:26
  13.6 3.0 %collective-permute-start.3 = (bf16[7680]{0:T(1024)(128)(2,1)S(1)}, bf16[7680]{0:T(1024)(128)(2,1)S(1)}, u32[]{:S(2)}, u32[]{:S(2)}) collective-permute-start(bf16[7680]{0:T(1024)(128)(2,1)S(1)} %pad_maximum_fusion.7), channel_id=1, source_target_pairs={{0,4},{4,8},{8,12},{12,16},{16,20},{20,24},{24,28},{1,5},{5,9},{9,... | collective-permute-start | bytes 46088 | tf_op jit(solution)/shard_map/ppermute | solution.py:25
  16.6 0.5 copy.32
  17.3 0.1 collective-permute-done.3
  17.5 0.1 maximum_bitcast_fusion.10
  17.8 0.7 %convolution_select_fusion = f32[34,8,3,128]{3,1,2,0:T(8,128)S(1)} fusion(bf16[3,3,128,128]{3,2,1,0:T(8,128)(2,1)S(1)} %copy-done, bf16[36,1,7,2,128]{4,2,3,0,1:T(8,128)(2,1)S(1)} %slice.383, bf16[36,1,8,3,128]{4,2,3,0,1:T(8,128)(2,1)S(1)} %copy.29, pred[8,3]{0,1:T(4,128)(4,1)S(1)} %copy-done.10), kind=kOutput, calls=%fused_computation.3 | convolution fusion | flops 241858560 | bytes 1062936 | tf_op jit(solution)/shard_map/conv_general_dilated | solution.py:126
  18.7 0.2 squeeze.130
  18.9 0.5 copy-done.7
  19.5 0.3 convolution_bitcast_fusion
  19.8 0.5 copy-done.4
  20.4 0.3 convolution_bitcast_fusion.1
  20.7 0.3 convolution_bitcast_fusion.2
  21.0 0.3 convolution_bitcast_fusion.3
  21.4 0.6 copy-done.9
  22.0 0.2 broadcast_select_fusion
  22.2 0.2 copy.45
  22.4 0.2 reshape.241
  22.6 0.2 fusion.48
  23.4 0.5 fusion
  24.3 0.5 fusion.67
  24.8 0.2 copy.34
  25.0 0.2 pad_maximum_fusion
  25.2 0.1 fusion.4
  25.3 1.3 %collective-permute-start.4 = (bf16[4,656,128]{2,1,0:T(8,128)(2,1)S(1)}, bf16[4,656,128]{2,1,0:T(8,128)(2,1)S(1)}, u32[]{:S(2)}, u32[]{:S(2)}) collective-permute-start(bf16[4,656,128]{2,1,0:T(8,128)(2,1)S(1)} %fusion.4), channel_id=1, source_target_pairs={{0,4},{4,0},{8,12},{12,8},{16,20},{20,16},{24,28},{28,24},{1,5},{5... | collective-permute-start | bytes 2015240 | tf_op jit(solution)/shard_map/ppermute | solution.py:175
  26.7 1.7 %collective-permute-done.4 = bf16[4,656,128]{2,1,0:T(8,128)(2,1)S(1)} collective-permute-done((bf16[4,656,128]{2,1,0:T(8,128)(2,1)S(1)}, bf16[4,656,128]{2,1,0:T(8,128)(2,1)S(1)}, u32[]{:S(2)}, u32[]{:S(2)}) %collective-permute-start.4) | collective-permute-done | bytes 671776 | tf_op jit(solution)/shard_map/ppermute | solution.py:175
  28.3 0.1 bitcast_add_fusion
  28.7 10.1 %collective-permute-done.5 = bf16[2,656,128]{2,1,0:T(8,128)(2,1)S(1)} collective-permute-done((bf16[2,656,128]{2,1,0:T(8,128)(2,1)S(1)}, bf16[2,656,128]{2,1,0:T(8,128)(2,1)S(1)}, u32[]{:S(2)}, u32[]{:S(2)}) %collective-permute-start.5) | collective-permute-done | bytes 335904 | tf_op jit(solution)/shard_map/ppermute | solution.py:175
  38.8 0.6 collective-permute-start.6
  39.4 5.2 %collective-permute-done.6 = bf16[656,128]{1,0:T(8,128)(2,1)S(1)} collective-permute-done((bf16[656,128]{1,0:T(8,128)(2,1)S(1)}, bf16[656,128]{1,0:T(8,128)(2,1)S(1)}, u32[]{:S(2)}, u32[]{:S(2)}) %collective-permute-start.6) | collective-permute-done | bytes 167968 | tf_op jit(solution)/shard_map/ppermute | solution.py:175
  44.7 2.1 %collective-permute-start.7 = (bf16[656,128]{1,0:T(8,128)(2,1)S(1)}, bf16[656,128]{1,0:T(8,128)(2,1)S(1)}, u32[]{:S(2)}, u32[]{:S(2)}) collective-permute-start(bf16[656,128]{1,0:T(8,128)(2,1)S(1)} %fusion.23), channel_id=1, source_target_pairs={{0,8},{4,12},{8,0},{12,4},{16,24},{20,28},{24,16},{28,20},{1,9},{5... | collective-permute-start | bytes 503816 | tf_op jit(solution)/shard_map/ppermute | solution.py:175
  46.8 3.3 %collective-permute-done.7 = bf16[656,128]{1,0:T(8,128)(2,1)S(1)} collective-permute-done((bf16[656,128]{1,0:T(8,128)(2,1)S(1)}, bf16[656,128]{1,0:T(8,128)(2,1)S(1)}, u32[]{:S(2)}, u32[]{:S(2)}) %collective-permute-start.7) | collective-permute-done | bytes 167968 | tf_op jit(solution)/shard_map/ppermute | solution.py:175
  50.2 3.2 %collective-permute-start.8 = (bf16[656,128]{1,0:T(8,128)(2,1)S(1)}, bf16[656,128]{1,0:T(8,128)(2,1)S(1)}, u32[]{:S(2)}, u32[]{:S(2)}) collective-permute-start(bf16[656,128]{1,0:T(8,128)(2,1)S(1)} %add_convert_fusion.3), channel_id=1, source_target_pairs={{0,16},{4,20},{8,24},{12,28},{16,0},{20,4},{24,8},{28,12},{1,17},{... | collective-permute-start | bytes 503816 | tf_op jit(solution)/shard_map/ppermute | solution.py:175
  53.4 0.3 fusion.80
  53.7 0.7 %copy.40 = f32[16,8,256]{2,1,0:T(8,128)} copy(f32[16,8,256]{2,0,1:T(8,128)S(1)} %fusion.80) | data formatting | bytes 262144 | tf_op jit(solution)/shard_map/rck,kn->rcn/dot_general | solution.py:151
  54.5 4.1 %collective-permute-done.8 = bf16[656,128]{1,0:T(8,128)(2,1)S(1)} collective-permute-done((bf16[656,128]{1,0:T(8,128)(2,1)S(1)}, bf16[656,128]{1,0:T(8,128)(2,1)S(1)}, u32[]{:S(2)}, u32[]{:S(2)}) %collective-permute-start.8) | collective-permute-done | bytes 167968 | tf_op jit(solution)/shard_map/ppermute | solution.py:175
  58.7 1.1 %convolution_convert_fusion = bf16[32,16,128]{2,1,0:T(8,128)(2,1)} fusion(bf16[32,16,1152]{2,1,0:T(8,128)(2,1)S(1)} %slice_dynamic-update-slice_fusion, bf16[1152,128,1]{1,0,2:T(8,128)(2,1)S(1)} %bitcast.212), kind=kOutput, calls=%fused_computation.7 | convolution fusion | flops 151060480 | bytes 1605632 | tf_op jit(solution)/shard_map/rck,kn->rcn/dot_general | solution.py:138
  59.8 0.2 collective-permute-done.9
  60.2 0.8 %slice.401 = f32[1024,128]{1,0:T(8,128)} slice(f32[1312,128]{1,0:T(8,128)S(1)} %convert_multiply_fusion), slice={[0:1024], [0:128]} | slice | bytes 1048576 | tf_op jit(solution)/shard_map/slice | solution.py:168
  61.0 0.7 %slice.402 = f32[288,128]{1,0:T(8,128)} slice(f32[1312,128]{1,0:T(8,128)S(1)} %convert_multiply_fusion), slice={[1024:1312], [0:128]} | slice | bytes 294912 | tf_op jit(solution)/shard_map/slice | solution.py:169
  (114 shorter events, 2.6 us)
Async XLA Ops:
  0.6 17.2 %copy-start = (bf16[3,3,128,128]{3,2,1,0:T(8,128)(2,1)S(1)}, bf16[3,3,128,128]{3,2,1,0:T(8,128)(2,1)}, u32[]{:S(2)}) copy-start(bf16[3,3,128,128]{3,2,1,0:T(8,128)(2,1)} %param.10) | copy-start | bytes 884740
  0.6 2.3 %copy-start.3 = (s32[16,8,256]{2,1,0:T(8,128)S(1)}, s32[16,8,256]{2,1,0:T(8,128)}, u32[]{:S(2)}) copy-start(s32[16,8,256]{2,1,0:T(8,128)} %param.6) | copy-start | bytes 393220
  0.7 6.7 %copy-start.1 = (bf16[4,4,256,128]{3,2,1,0:T(8,128)(2,1)S(1)}, bf16[4,4,256,128]{3,2,1,0:T(8,128)(2,1)}, u32[]{:S(2)}) copy-start(bf16[4,4,256,128]{3,2,1,0:T(8,128)(2,1)} %param.8) | copy-start | bytes 3145732
  3.2 8.8 %copy-start.2 = (bf16[32,16,128]{2,1,0:T(8,128)(2,1)S(1)}, bf16[32,16,128]{2,1,0:T(8,128)(2,1)}, u32[]{:S(2)}) copy-start(bf16[32,16,128]{2,1,0:T(8,128)(2,1)} %param.11) | copy-start | bytes 393220
  3.3 5.5 %collective-permute-start.1 = (bf16[12288]{0:T(1024)(128)(2,1)S(1)}, bf16[12288]{0:T(1024)(128)(2,1)S(1)}, u32[]{:S(2)}, u32[]{:S(2)}) collective-permute-start(bf16[12288]{0:T(1024)(128)(2,1)S(1)} %pad_maximum_fusion.5), channel_id=1, source_target_pairs={{1,0},{2,1},{3,2},{0,3},{5,4},{6,5},{7,6},{4,7},{9,8},{10,9},{11,1... | collective-permute-start | bytes 73736 | tf_op jit(solution)/shard_map/ppermute | solution.py:26
  7.3 4.8 %collective-permute-start = (bf16[12288]{0:T(1024)(128)(2,1)S(1)}, bf16[12288]{0:T(1024)(128)(2,1)S(1)}, u32[]{:S(2)}, u32[]{:S(2)}) collective-permute-start(bf16[12288]{0:T(1024)(128)(2,1)S(1)} %pad_maximum_fusion.4), channel_id=1, source_target_pairs={{0,1},{1,2},{2,3},{3,0},{4,5},{5,6},{6,7},{7,4},{8,9},{9,10},{10,1... | collective-permute-start | bytes 73736 | tf_op jit(solution)/shard_map/ppermute | solution.py:25
  12.2 5.0 %collective-permute-start.2 = (bf16[7680]{0:T(1024)(128)(2,1)S(1)}, bf16[7680]{0:T(1024)(128)(2,1)S(1)}, u32[]{:S(2)}, u32[]{:S(2)}) collective-permute-start(bf16[7680]{0:T(1024)(128)(2,1)S(1)} %pad_maximum_fusion.6), channel_id=1, source_target_pairs={{4,0},{8,4},{12,8},{16,12},{20,16},{24,20},{28,24},{5,1},{9,5},{13... | collective-permute-start | bytes 46088 | tf_op jit(solution)/shard_map/ppermute | solution.py:26
  13.6 3.9 %collective-permute-start.3 = (bf16[7680]{0:T(1024)(128)(2,1)S(1)}, bf16[7680]{0:T(1024)(128)(2,1)S(1)}, u32[]{:S(2)}, u32[]{:S(2)}) collective-permute-start(bf16[7680]{0:T(1024)(128)(2,1)S(1)} %pad_maximum_fusion.7), channel_id=1, source_target_pairs={{0,4},{4,8},{8,12},{12,16},{16,20},{20,24},{24,28},{1,5},{5,9},{9,... | collective-permute-start | bytes 46088 | tf_op jit(solution)/shard_map/ppermute | solution.py:25
  17.2 0.7 %copy-start.10 = (pred[8,3]{0,1:T(4,128)(4,1)S(1)}, pred[8,3]{0,1:T(4,128)(4,1)}, u32[]{:S(2)}) copy-start(pred[8,3]{0,1:T(4,128)(4,1)} %constant.159) | copy-start | bytes 76
  18.6 0.8 %copy-start.7 = (bf16[256,128]{1,0:T(8,128)(2,1)S(1)}, bf16[256,128]{1,0:T(8,128)(2,1)}, u32[]{:S(2)}) copy-start(bf16[256,128]{1,0:T(8,128)(2,1)} %get-tuple-element.7) | copy-start | bytes 196612
  18.6 0.9 %copy-start.8 = (bf16[256,128]{1,0:T(8,128)(2,1)S(1)}, bf16[256,128]{1,0:T(8,128)(2,1)}, u32[]{:S(2)}) copy-start(bf16[256,128]{1,0:T(8,128)(2,1)} %get-tuple-element.8) | copy-start | bytes 196612
  19.5 0.8 %copy-start.4 = (bf16[256,128]{1,0:T(8,128)(2,1)S(1)}, bf16[256,128]{1,0:T(8,128)(2,1)}, u32[]{:S(2)}) copy-start(bf16[256,128]{1,0:T(8,128)(2,1)} %get-tuple-element.11) | copy-start | bytes 196612
  19.5 0.9 %copy-start.5 = (bf16[256,128]{1,0:T(8,128)(2,1)S(1)}, bf16[256,128]{1,0:T(8,128)(2,1)}, u32[]{:S(2)}) copy-start(bf16[256,128]{1,0:T(8,128)(2,1)} %get-tuple-element.12) | copy-start | bytes 196612
  19.5 0.9 %copy-start.6 = (bf16[256,128]{1,0:T(8,128)(2,1)S(1)}, bf16[256,128]{1,0:T(8,128)(2,1)}, u32[]{:S(2)}) copy-start(bf16[256,128]{1,0:T(8,128)(2,1)} %get-tuple-element.13) | copy-start | bytes 196612
  21.3 0.7 %copy-start.9 = (f32[128]{0:T(128)S(1)}, f32[128]{0:T(128)}, u32[]{:S(2)}) copy-start(f32[128]{0:T(128)} %param.9) | copy-start | bytes 1540
  25.3 3.0 %collective-permute-start.4 = (bf16[4,656,128]{2,1,0:T(8,128)(2,1)S(1)}, bf16[4,656,128]{2,1,0:T(8,128)(2,1)S(1)}, u32[]{:S(2)}, u32[]{:S(2)}) collective-permute-start(bf16[4,656,128]{2,1,0:T(8,128)(2,1)S(1)} %fusion.4), channel_id=1, source_target_pairs={{0,4},{4,0},{8,12},{12,8},{16,20},{20,16},{24,28},{28,24},{1,5},{5... | collective-permute-start | bytes 2015240 | tf_op jit(solution)/shard_map/ppermute | solution.py:175
  28.5 10.2 %collective-permute-start.5 = (bf16[2,656,128]{2,1,0:T(8,128)(2,1)S(1)}, bf16[2,656,128]{2,1,0:T(8,128)(2,1)S(1)}, u32[]{:S(2)}, u32[]{:S(2)}) collective-permute-start(bf16[2,656,128]{2,1,0:T(8,128)(2,1)S(1)} %fusion.22), channel_id=1, source_target_pairs={{0,1},{1,0},{2,3},{3,2},{4,5},{5,4},{6,7},{7,6},{8,9},{9,8},{10,11... | collective-permute-start | bytes 1007624 | tf_op jit(solution)/shard_map/ppermute | solution.py:175
  38.8 5.8 %collective-permute-start.6 = (bf16[656,128]{1,0:T(8,128)(2,1)S(1)}, bf16[656,128]{1,0:T(8,128)(2,1)S(1)}, u32[]{:S(2)}, u32[]{:S(2)}) collective-permute-start(bf16[656,128]{1,0:T(8,128)(2,1)S(1)} %fusion.50), channel_id=1, source_target_pairs={{0,2},{1,3},{2,0},{3,1},{4,6},{5,7},{6,4},{7,5},{8,10},{9,11},{10,... | collective-permute-start | bytes 503816 | tf_op jit(solution)/shard_map/ppermute | solution.py:175
  44.7 5.5 %collective-permute-start.7 = (bf16[656,128]{1,0:T(8,128)(2,1)S(1)}, bf16[656,128]{1,0:T(8,128)(2,1)S(1)}, u32[]{:S(2)}, u32[]{:S(2)}) collective-permute-start(bf16[656,128]{1,0:T(8,128)(2,1)S(1)} %fusion.23), channel_id=1, source_target_pairs={{0,8},{4,12},{8,0},{12,4},{16,24},{20,28},{24,16},{28,20},{1,9},{5... | collective-permute-start | bytes 503816 | tf_op jit(solution)/shard_map/ppermute | solution.py:175
  50.2 8.4 %collective-permute-start.8 = (bf16[656,128]{1,0:T(8,128)(2,1)S(1)}, bf16[656,128]{1,0:T(8,128)(2,1)S(1)}, u32[]{:S(2)}, u32[]{:S(2)}) collective-permute-start(bf16[656,128]{1,0:T(8,128)(2,1)S(1)} %add_convert_fusion.3), channel_id=1, source_target_pairs={{0,16},{4,20},{8,24},{12,28},{16,0},{20,4},{24,8},{28,12},{1,17},{... | collective-permute-start | bytes 503816 | tf_op jit(solution)/shard_map/ppermute | solution.py:175
  58.6 1.5 %collective-permute-start.9 = (bf16[656,128]{1,0:T(8,128)(2,1)S(1)}, bf16[656,128]{1,0:T(8,128)(2,1)S(1)}, u32[]{:S(2)}, u32[]{:S(2)}) collective-permute-start(bf16[656,128]{1,0:T(8,128)(2,1)S(1)} %add_convert_fusion.2), channel_id=1, source_target_pairs={{0,4},{4,0},{8,12},{12,8},{16,20},{20,16},{24,28},{28,24},{1,5},{5... | collective-permute-start | bytes 503816 | tf_op jit(solution)/shard_map/ppermute | solution.py:175

commit v15 on v11

--- a/solution.py
+++ b/solution.py
@@ -147,9 +147,11 @@
         preferred_element_type=jnp.float32,
     ).reshape(lon_count, mix_span, 9, COUT).transpose(0, 2, 1, 3)
     grad_patches = strided(pre_grad_pad, in_rows, in_cols)
-    back_up = up_kernel.transpose(0, 1, 3, 2).reshape(16 * COUT, CIN)
     input_grad = jnp.einsum(
-        "rck,kn->rcn", grad_patches, back_up, preferred_element_type=jnp.float32
+        "rctn,tmn->rcm",
+        grad_patches.reshape(in_rows, in_cols, 16, COUT),
+        up_kernel.reshape(16, CIN, COUT),
+        preferred_element_type=jnp.float32,
     )
     up_taps = jnp.einsum(
         "rctn,rcm->tmn",

time: 59.9 us -> 59 us (0.985)
  local copies, waits for them, and re-layouts: 11 us -> 7.81 us
  other arithmetic: 2.47 us -> 3.51 us
  waiting for transfers between devices: 19.8 us -> 20.6 us
    unnamed x67 -> x45, local copies, waits for them, and re-layouts: 4.9 us -> 1.67 us
    add x3, other arithmetic: 0.21 us -> 1.28 us  [halve(): keep + exchange(send.astype(jnp.bfloat16), axis, step).astype(keep.dtype)]
    convert_element_type x5, local copies, waits for them, and re-layouts: 0.19 us -> 1.04 us  [halve(): send.astype(jnp.bfloat16)]
    squeeze x1, local copies, waits for them, and re-layouts: 0.74 us -> 0.1 us  [upsample(): kernels.append(up_kernel[row_tap, col_tap])]
    ppermute x2, waiting for transfers between devices: 0.68 us -> 1.3 us  [swap_edges(): lax.ppermute(jnp.concatenate([p.reshape(-1) for p in leads]), axis, down)]
    ppermute x2, waiting for transfers between devices: 3.41 us -> 4.02 us  [swap_edges(): lax.ppermute(jnp.concatenate([p.reshape(-1) for p in lasts]), axis, up)]
  transfers between devices with their start and end apart: 14 -> 14, of which waited for: 11 -> 11; matrix products, arithmetic and copies ran while one was open for 6% -> 5% of each run, Pallas kernels for 0% -> 0%
where the time goes in v15:
time: 59 us; the launch traced here: 58.7 us
  starting transfers between devices  20.9 us (35%)
  waiting for transfers between devices  20.6 us (35%)
  local copies, waits for them, and re-layouts  7.81 us (13%)
  matrix products  4.4 us (7%)
  other arithmetic  3.51 us (6%)
  between operations  1.42 us (2%)
    ppermute x10, waiting for transfers between devices, exchange(): return lax.ppermute(part, axis, [(i, i ^ step) for i in range(size)])  15.3 us
    ppermute x10, starting transfers between devices, exchange(): return lax.ppermute(part, axis, [(i, i ^ step) for i in range(size)])  12.6 us
    ppermute x2, starting transfers between devices, swap_edges(): lax.ppermute(jnp.concatenate([p.reshape(-1) for p in leads]), axis, down)  5.24 us
    ppermute x2, waiting for transfers between devices, swap_edges(): lax.ppermute(jnp.concatenate([p.reshape(-1) for p in lasts]), axis, up)  4.02 us
    ppermute x2, starting transfers between devices, swap_edges(): lax.ppermute(jnp.concatenate([p.reshape(-1) for p in lasts]), axis, up)  3.09 us
    unnamed x45, local copies, waits for them, and re-layouts  1.67 us
    ppermute x2, waiting for transfers between devices, swap_edges(): lax.ppermute(jnp.concatenate([p.reshape(-1) for p in leads]), axis, down)  1.3 us
    add x3, other arithmetic, halve(): keep + exchange(send.astype(jnp.bfloat16), axis, step).astype(keep.dtype)  1.28 us
  transfers between devices with their start and end apart: 14, of which 11 were waited for; matrix products, arithmetic and copies ran while one was open for 5% of the time, Pallas kernels for 0%

profile of v15, /device:TPU:0, one launch (start us, length us, event | category | flops | bytes accessed | tf_op | source)
XLA Modules:
  0.0 58.7 jit_solution(11815713261334060847)
XLA Ops:
  0.7 1.0 %fusion.81 = (bf16[32,2,128]{2,1,0:T(2,128)(2,1)S(1)}, bf16[32,2,128]{2,1,0:T(2,128)(2,1)S(1)}) fusion(bf16[32,16,128]{2,1,0:T(8,128)(2,1)} %param.11), kind=kLoop, calls=%fused_computation.210 | loop fusion | bytes 65536 | tf_op jit(solution)/shard_map/slice | solution.py:23
  1.7 0.8 %multiply_exponential_fusion = f32[16,8,8]{0,2,1:T(8,128)S(1)} fusion(s32[16,8,8]{0,2,1:T(8,128)} %param.7), kind=kLoop, calls=%fused_computation.186 | loop fusion | flops 2048 | bytes 8192 | tf_op jit(solution)/shard_map/exp2 | solution.py:50
  2.5 0.2 broadcast_in_dim.21
  2.7 0.2 reshape.202
  2.9 0.3 fusion.65
  3.3 3.9 %collective-permute-start.1 = (bf16[12288]{0:T(1024)(128)(2,1)S(1)}, bf16[12288]{0:T(1024)(128)(2,1)S(1)}, u32[]{:S(2)}, u32[]{:S(2)}) collective-permute-start(bf16[12288]{0:T(1024)(128)(2,1)S(1)} %pad_maximum_fusion.6), channel_id=1, source_target_pairs={{1,0},{2,1},{3,2},{0,3},{5,4},{6,5},{7,6},{4,7},{9,8},{10,9},{11,1... | collective-permute-start | bytes 73736 | tf_op jit(solution)/shard_map/ppermute | solution.py:26
  7.5 1.3 %collective-permute-done.1 = bf16[12288]{0:T(1024)(128)(2,1)S(1)} collective-permute-done((bf16[12288]{0:T(1024)(128)(2,1)S(1)}, bf16[12288]{0:T(1024)(128)(2,1)S(1)}, u32[]{:S(2)}, u32[]{:S(2)}) %collective-permute-start.1) | collective-permute-done | bytes 24608 | tf_op jit(solution)/shard_map/ppermute | solution.py:26
  8.8 3.3 %collective-permute-done = bf16[12288]{0:T(1024)(128)(2,1)S(1)} collective-permute-done((bf16[12288]{0:T(1024)(128)(2,1)S(1)}, bf16[12288]{0:T(1024)(128)(2,1)S(1)}, u32[]{:S(2)}, u32[]{:S(2)}) %collective-permute-start) | collective-permute-done | bytes 24608 | tf_op jit(solution)/shard_map/ppermute | solution.py:25
  12.2 1.3 %collective-permute-start.2 = (bf16[7680]{0:T(1024)(128)(2,1)S(1)}, bf16[7680]{0:T(1024)(128)(2,1)S(1)}, u32[]{:S(2)}, u32[]{:S(2)}) collective-permute-start(bf16[7680]{0:T(1024)(128)(2,1)S(1)} %pad_maximum_fusion.7), channel_id=1, source_target_pairs={{4,0},{8,4},{12,8},{16,12},{20,16},{24,20},{28,24},{5,1},{9,5},{13... | collective-permute-start | bytes 46088 | tf_op jit(solution)/shard_map/ppermute | solution.py:26
  13.6 3.0 %collective-permute-start.3 = (bf16[7680]{0:T(1024)(128)(2,1)S(1)}, bf16[7680]{0:T(1024)(128)(2,1)S(1)}, u32[]{:S(2)}, u32[]{:S(2)}) collective-permute-start(bf16[7680]{0:T(1024)(128)(2,1)S(1)} %pad_maximum_fusion.8), channel_id=1, source_target_pairs={{0,4},{4,8},{8,12},{12,16},{16,20},{20,24},{24,28},{1,5},{5,9},{9,... | collective-permute-start | bytes 46088 | tf_op jit(solution)/shard_map/ppermute | solution.py:25
  16.7 0.8 %collective-permute-done.3 = bf16[7680]{0:T(1024)(128)(2,1)S(1)} collective-permute-done((bf16[7680]{0:T(1024)(128)(2,1)S(1)}, bf16[7680]{0:T(1024)(128)(2,1)S(1)}, u32[]{:S(2)}, u32[]{:S(2)}) %collective-permute-start.3) | collective-permute-done | bytes 15392 | tf_op jit(solution)/shard_map/ppermute | solution.py:25
  17.6 0.3 convolution_bitcast_fusion
  17.9 0.3 convolution_bitcast_fusion.1
  18.2 0.3 convolution_bitcast_fusion.2
  18.5 0.3 convolution_bitcast_fusion.3
  18.9 0.2 copy.44
  19.0 0.2 reshape.249
  19.2 0.2 copy-done.7
  20.5 0.2 copy-done.8
  20.7 0.7 %convolution_select_fusion = f32[34,8,3,128]{3,1,2,0:T(8,128)S(1)} fusion(bf16[3,3,128,128]{3,2,1,0:T(8,128)(2,1)S(1)} %copy-done, bf16[36,1,7,2,128]{4,2,3,0,1:T(8,128)(2,1)S(1)} %slice.391, bf16[36,1,8,3,128]{4,2,3,0,1:T(8,128)(2,1)S(1)} %copy.29, pred[8,3]{0,1:T(4,128)(4,1)S(1)} %copy-done.8), kind=kOutput, calls=%fused_computation.3 | convolution fusion | flops 241858560 | bytes 1062936 | tf_op jit(solution)/shard_map/conv_general_dilated | solution.py:126
  21.5 0.2 squeeze.107
  21.7 0.2 broadcast_select_fusion
  22.2 0.5 fusion
  22.8 0.5 fusion.70
  23.4 0.2 pad_maximum_fusion
  23.6 0.9 %fusion.4 = bf16[4,656,128]{2,1,0:T(8,128)(2,1)} fusion(f32[4,2,656,128]{3,2,1,0:T(8,128)S(1)} %bitcast.224, s32[]{:T(128)S(6)} %select_n.108), kind=kLoop, calls=%fused_computation.14 | loop fusion | bytes 1343492 | tf_op jit(solution)/shard_map/convert_element_type | solution.py:184
  24.5 1.2 %collective-permute-start.4 = (bf16[4,656,128]{2,1,0:T(8,128)(2,1)}, bf16[4,656,128]{2,1,0:T(8,128)(2,1)}, u32[]{:S(2)}, u32[]{:S(2)}) collective-permute-start(bf16[4,656,128]{2,1,0:T(8,128)(2,1)} %fusion.4), channel_id=1, source_target_pairs={{0,4},{4,0},{8,12},{12,8},{16,20},{20,16},{24,28},{28,24},{1,5},{5... | collective-permute-start | bytes 2015240 | tf_op jit(solution)/shard_map/ppermute | solution.py:177
  25.8 2.1 %collective-permute-done.4 = bf16[4,656,128]{2,1,0:T(8,128)(2,1)} collective-permute-done((bf16[4,656,128]{2,1,0:T(8,128)(2,1)}, bf16[4,656,128]{2,1,0:T(8,128)(2,1)}, u32[]{:S(2)}, u32[]{:S(2)}) %collective-permute-start.4) | collective-permute-done | bytes 671776 | tf_op jit(solution)/shard_map/ppermute | solution.py:177
  27.9 1.2 %bitcast_add_fusion = f32[4,656,128]{2,1,0:T(8,128)S(1)} fusion(bf16[4,656,128]{2,1,0:T(8,128)(2,1)} %collective-permute-done.4, f32[4,2,656,128]{3,2,1,0:T(8,128)S(1)} %bitcast.225, s32[]{:T(128)S(6)} %select_n.107), kind=kLoop, calls=%fused_computation.1 | loop fusion | flops 671744 | bytes 3358724 | tf_op jit(solution)/shard_map/add | solution.py:184
  29.2 0.6 collective-permute-start.9
  29.8 0.5 copy-done.2
  30.3 0.5 fusion.84
  30.8 0.7 %copy.61 = f32[16,8,256,1]{2,1,0,3:T(8,128)} copy(f32[16,8,256,1]{2,0,1,3:T(8,128)S(1)} %fusion.84) | data formatting | bytes 262144 | tf_op jit(solution)/shard_map/rctn,tmn->rcm/dot_general | solution.py:150
  31.6 4.3 %collective-permute-done.9 = bf16[2,328,128]{2,1,0:T(8,128)(2,1)S(1)} collective-permute-done((bf16[2,328,128]{2,1,0:T(8,128)(2,1)S(1)}, bf16[2,328,128]{2,1,0:T(8,128)(2,1)S(1)}, u32[]{:S(2)}, u32[]{:S(2)}) %collective-permute-start.9) | collective-permute-done | bytes 167968 | tf_op jit(solution)/shard_map/ppermute | solution.py:177
  36.0 2.2 %collective-permute-done.5 = bf16[2,328,128]{2,1,0:T(8,128)(2,1)S(1)} collective-permute-done((bf16[2,328,128]{2,1,0:T(8,128)(2,1)S(1)}, bf16[2,328,128]{2,1,0:T(8,128)(2,1)S(1)}, u32[]{:S(2)}, u32[]{:S(2)}) %collective-permute-start.5) | collective-permute-done | bytes 167968 | tf_op jit(solution)/shard_map/ppermute | solution.py:177
  38.3 0.9 %collective-permute-start.6 = (bf16[328,128]{1,0:T(8,128)(2,1)S(1)}, bf16[328,128]{1,0:T(8,128)(2,1)S(1)}, u32[]{:S(2)}, u32[]{:S(2)}) collective-permute-start(bf16[328,128]{1,0:T(8,128)(2,1)S(1)} %fusion.68), channel_id=1, source_target_pairs={{0,2},{1,3},{2,0},{3,1},{4,6},{5,7},{6,4},{7,5},{8,10},{9,11},{10,... | collective-permute-start | bytes 251912 | tf_op jit(solution)/shard_map/ppermute | solution.py:177
  39.2 1.3 %collective-permute-done.10 = bf16[328,128]{1,0:T(8,128)(2,1)S(1)} collective-permute-done((bf16[328,128]{1,0:T(8,128)(2,1)S(1)}, bf16[328,128]{1,0:T(8,128)(2,1)S(1)}, u32[]{:S(2)}, u32[]{:S(2)}) %collective-permute-start.10) | collective-permute-done | bytes 84000 | tf_op jit(solution)/shard_map/ppermute | solution.py:177
  40.5 2.4 %collective-permute-start.11 = (bf16[328,128]{1,0:T(8,128)(2,1)S(1)}, bf16[328,128]{1,0:T(8,128)(2,1)S(1)}, u32[]{:S(2)}, u32[]{:S(2)}) collective-permute-start(bf16[328,128]{1,0:T(8,128)(2,1)S(1)} %fusion.50), channel_id=1, source_target_pairs={{0,8},{4,12},{8,0},{12,4},{16,24},{20,28},{24,16},{28,20},{1,9},{5... | collective-permute-start | bytes 251912 | tf_op jit(solution)/shard_map/ppermute | solution.py:177
  42.9 2.5 %collective-permute-start.7 = (bf16[328,128]{1,0:T(8,128)(2,1)S(1)}, bf16[328,128]{1,0:T(8,128)(2,1)S(1)}, u32[]{:S(2)}, u32[]{:S(2)}) collective-permute-start(bf16[328,128]{1,0:T(8,128)(2,1)S(1)} %fusion.51), channel_id=1, source_target_pairs={{0,8},{4,12},{8,0},{12,4},{16,24},{20,28},{24,16},{28,20},{1,9},{5... | collective-permute-start | bytes 251912 | tf_op jit(solution)/shard_map/ppermute | solution.py:177
  45.4 0.7 %collective-permute-done.11 = bf16[328,128]{1,0:T(8,128)(2,1)S(1)} collective-permute-done((bf16[328,128]{1,0:T(8,128)(2,1)S(1)}, bf16[328,128]{1,0:T(8,128)(2,1)S(1)}, u32[]{:S(2)}, u32[]{:S(2)}) %collective-permute-start.11) | collective-permute-done | bytes 84000 | tf_op jit(solution)/shard_map/ppermute | solution.py:177
  46.1 3.1 %collective-permute-start.12 = (bf16[328,128]{1,0:T(8,128)(2,1)S(1)}, bf16[328,128]{1,0:T(8,128)(2,1)S(1)}, u32[]{:S(2)}, u32[]{:S(2)}) collective-permute-start(bf16[328,128]{1,0:T(8,128)(2,1)S(1)} %add_convert_fusion.3), channel_id=1, source_target_pairs={{0,16},{4,20},{8,24},{12,28},{16,0},{20,4},{24,8},{28,12},{1,17},{... | collective-permute-start | bytes 251912 | tf_op jit(solution)/shard_map/ppermute | solution.py:177
  49.2 1.8 %collective-permute-start.8 = (bf16[328,128]{1,0:T(8,128)(2,1)S(1)}, bf16[328,128]{1,0:T(8,128)(2,1)S(1)}, u32[]{:S(2)}, u32[]{:S(2)}) collective-permute-start(bf16[328,128]{1,0:T(8,128)(2,1)S(1)} %add_convert_fusion.5), channel_id=1, source_target_pairs={{0,16},{4,20},{8,24},{12,28},{16,0},{20,4},{24,8},{28,12},{1,17},{... | collective-permute-start | bytes 251912 | tf_op jit(solution)/shard_map/ppermute | solution.py:177
  50.9 2.3 %collective-permute-done.12 = bf16[328,128]{1,0:T(8,128)(2,1)S(1)} collective-permute-done((bf16[328,128]{1,0:T(8,128)(2,1)S(1)}, bf16[328,128]{1,0:T(8,128)(2,1)S(1)}, u32[]{:S(2)}, u32[]{:S(2)}) %collective-permute-start.12) | collective-permute-done | bytes 84000 | tf_op jit(solution)/shard_map/ppermute | solution.py:177
  53.3 2.3 %collective-permute-done.8 = bf16[328,128]{1,0:T(8,128)(2,1)S(1)} collective-permute-done((bf16[328,128]{1,0:T(8,128)(2,1)S(1)}, bf16[328,128]{1,0:T(8,128)(2,1)S(1)}, u32[]{:S(2)}, u32[]{:S(2)}) %collective-permute-start.8) | collective-permute-done | bytes 84000 | tf_op jit(solution)/shard_map/ppermute | solution.py:177
  55.7 1.1 %convolution_convert_fusion = bf16[32,16,128]{2,1,0:T(8,128)(2,1)} fusion(bf16[32,16,1152]{2,1,0:T(8,128)(2,1)S(1)} %copy-done.4, bf16[1152,128,1]{1,0,2:T(8,128)(2,1)S(1)} %bitcast.222), kind=kOutput, calls=%fused_computation.7 | convolution fusion | flops 151060480 | bytes 1605632 | tf_op jit(solution)/shard_map/rck,kn->rcn/dot_general | solution.py:138
  56.8 0.2 collective-permute-done.13
  57.2 0.8 %slice.411 = f32[1024,128]{1,0:T(8,128)} slice(f32[1312,128]{1,0:T(8,128)S(1)} %convert_multiply_fusion), slice={[0:1024], [0:128]} | slice | bytes 1048576 | tf_op jit(solution)/shard_map/slice | solution.py:170
  58.0 0.7 %slice.412 = f32[288,128]{1,0:T(8,128)} slice(f32[1312,128]{1,0:T(8,128)S(1)} %convert_multiply_fusion), slice={[1024:1312], [0:128]} | slice | bytes 294912 | tf_op jit(solution)/shard_map/slice | solution.py:171
  (109 shorter events, 2.9 us)
Async XLA Ops:
  0.6 19.8 %copy-start = (bf16[3,3,128,128]{3,2,1,0:T(8,128)(2,1)S(1)}, bf16[3,3,128,128]{3,2,1,0:T(8,128)(2,1)}, u32[]{:S(2)}) copy-start(bf16[3,3,128,128]{3,2,1,0:T(8,128)(2,1)} %param.10) | copy-start | bytes 884740
  0.6 2.3 %copy-start.6 = (s32[16,8,256]{2,1,0:T(8,128)S(1)}, s32[16,8,256]{2,1,0:T(8,128)}, u32[]{:S(2)}) copy-start(s32[16,8,256]{2,1,0:T(8,128)} %param.6) | copy-start | bytes 393220
  0.7 6.7 %copy-start.1 = (bf16[4,4,256,128]{3,2,1,0:T(8,128)(2,1)S(1)}, bf16[4,4,256,128]{3,2,1,0:T(8,128)(2,1)}, u32[]{:S(2)}) copy-start(bf16[4,4,256,128]{3,2,1,0:T(8,128)(2,1)} %param.8) | copy-start | bytes 3145732
  3.2 8.8 %copy-start.5 = (bf16[32,16,128]{2,1,0:T(8,128)(2,1)S(1)}, bf16[32,16,128]{2,1,0:T(8,128)(2,1)}, u32[]{:S(2)}) copy-start(bf16[32,16,128]{2,1,0:T(8,128)(2,1)} %param.11) | copy-start | bytes 393220
  3.3 5.5 %collective-permute-start.1 = (bf16[12288]{0:T(1024)(128)(2,1)S(1)}, bf16[12288]{0:T(1024)(128)(2,1)S(1)}, u32[]{:S(2)}, u32[]{:S(2)}) collective-permute-start(bf16[12288]{0:T(1024)(128)(2,1)S(1)} %pad_maximum_fusion.6), channel_id=1, source_target_pairs={{1,0},{2,1},{3,2},{0,3},{5,4},{6,5},{7,6},{4,7},{9,8},{10,9},{11,1... | collective-permute-start | bytes 73736 | tf_op jit(solution)/shard_map/ppermute | solution.py:26
  7.3 4.8 %collective-permute-start = (bf16[12288]{0:T(1024)(128)(2,1)S(1)}, bf16[12288]{0:T(1024)(128)(2,1)S(1)}, u32[]{:S(2)}, u32[]{:S(2)}) collective-permute-start(bf16[12288]{0:T(1024)(128)(2,1)S(1)} %pad_maximum_fusion.5), channel_id=1, source_target_pairs={{0,1},{1,2},{2,3},{3,0},{4,5},{5,6},{6,7},{7,4},{8,9},{9,10},{10,1... | collective-permute-start | bytes 73736 | tf_op jit(solution)/shard_map/ppermute | solution.py:25
  12.2 4.4 %collective-permute-start.2 = (bf16[7680]{0:T(1024)(128)(2,1)S(1)}, bf16[7680]{0:T(1024)(128)(2,1)S(1)}, u32[]{:S(2)}, u32[]{:S(2)}) collective-permute-start(bf16[7680]{0:T(1024)(128)(2,1)S(1)} %pad_maximum_fusion.7), channel_id=1, source_target_pairs={{4,0},{8,4},{12,8},{16,12},{20,16},{24,20},{28,24},{5,1},{9,5},{13... | collective-permute-start | bytes 46088 | tf_op jit(solution)/shard_map/ppermute | solution.py:26
  13.6 3.9 %collective-permute-start.3 = (bf16[7680]{0:T(1024)(128)(2,1)S(1)}, bf16[7680]{0:T(1024)(128)(2,1)S(1)}, u32[]{:S(2)}, u32[]{:S(2)}) collective-permute-start(bf16[7680]{0:T(1024)(128)(2,1)S(1)} %pad_maximum_fusion.8), channel_id=1, source_target_pairs={{0,4},{4,8},{8,12},{12,16},{16,20},{20,24},{24,28},{1,5},{5,9},{9,... | collective-permute-start | bytes 46088 | tf_op jit(solution)/shard_map/ppermute | solution.py:25
  18.8 0.7 %copy-start.7 = (f32[128]{0:T(128)S(1)}, f32[128]{0:T(128)}, u32[]{:S(2)}) copy-start(f32[128]{0:T(128)} %param.9) | copy-start | bytes 1540
  20.1 0.7 %copy-start.8 = (pred[8,3]{0,1:T(4,128)(4,1)S(1)}, pred[8,3]{0,1:T(4,128)(4,1)}, u32[]{:S(2)}) copy-start(pred[8,3]{0,1:T(4,128)(4,1)} %constant.177) | copy-start | bytes 76
  20.1 2.1 %copy-start.3 = (bf16[32,16,1152]{2,1,0:T(8,128)(2,1)}, bf16[32,16,1152]{2,1,0:T(8,128)(2,1)S(1)}, u32[]{:S(2)}) copy-start(bf16[32,16,1152]{2,1,0:T(8,128)(2,1)S(1)} %slice_dynamic-update-slice_fusion) | copy-start | bytes 3538948
  24.5 3.3 %collective-permute-start.4 = (bf16[4,656,128]{2,1,0:T(8,128)(2,1)}, bf16[4,656,128]{2,1,0:T(8,128)(2,1)}, u32[]{:S(2)}, u32[]{:S(2)}) collective-permute-start(bf16[4,656,128]{2,1,0:T(8,128)(2,1)} %fusion.4), channel_id=1, source_target_pairs={{0,4},{4,0},{8,12},{12,8},{16,20},{20,16},{24,28},{28,24},{1,5},{5... | collective-permute-start | bytes 2015240 | tf_op jit(solution)/shard_map/ppermute | solution.py:177
  29.1 1.2 %copy-start.2 = (bf16[4,4,256,128]{3,2,1,0:T(8,128)(2,1)S(1)}, bf16[4,4,256,128]{3,2,1,0:T(8,128)(2,1)}, u32[]{:S(2)}) copy-start(bf16[4,4,256,128]{3,2,1,0:T(8,128)(2,1)} %param.8) | copy-start | bytes 3145732
  29.2 6.7 %collective-permute-start.9 = (bf16[2,328,128]{2,1,0:T(8,128)(2,1)S(1)}, bf16[2,328,128]{2,1,0:T(8,128)(2,1)S(1)}, u32[]{:S(2)}, u32[]{:S(2)}) collective-permute-start(bf16[2,328,128]{2,1,0:T(8,128)(2,1)S(1)} %fusion.49), channel_id=1, source_target_pairs={{0,2},{1,3},{2,0},{3,1},{4,6},{5,7},{6,4},{7,5},{8,10},{9,11},{10,... | collective-permute-start | bytes 503816 | tf_op jit(solution)/shard_map/ppermute | solution.py:177
  31.5 6.7 %collective-permute-start.5 = (bf16[2,328,128]{2,1,0:T(8,128)(2,1)S(1)}, bf16[2,328,128]{2,1,0:T(8,128)(2,1)S(1)}, u32[]{:S(2)}, u32[]{:S(2)}) collective-permute-start(bf16[2,328,128]{2,1,0:T(8,128)(2,1)S(1)} %fusion.48), channel_id=1, source_target_pairs={{0,1},{1,0},{2,3},{3,2},{4,5},{5,4},{6,7},{7,6},{8,9},{9,8},{10,11... | collective-permute-start | bytes 503816 | tf_op jit(solution)/shard_map/ppermute | solution.py:177
  36.0 4.5 %collective-permute-start.10 = (bf16[328,128]{1,0:T(8,128)(2,1)S(1)}, bf16[328,128]{1,0:T(8,128)(2,1)S(1)}, u32[]{:S(2)}, u32[]{:S(2)}) collective-permute-start(bf16[328,128]{1,0:T(8,128)(2,1)S(1)} %fusion.69), channel_id=1, source_target_pairs={{0,1},{1,0},{2,3},{3,2},{4,5},{5,4},{6,7},{7,6},{8,9},{9,8},{10,11... | collective-permute-start | bytes 251912 | tf_op jit(solution)/shard_map/ppermute | solution.py:177
  38.3 17.4 %copy-start.4 = (bf16[32,16,1152]{2,1,0:T(8,128)(2,1)S(1)}, bf16[32,16,1152]{2,1,0:T(8,128)(2,1)}, u32[]{:S(2)}) copy-start(bf16[32,16,1152]{2,1,0:T(8,128)(2,1)} %copy-done.3) | copy-start | bytes 3538948
  38.3 4.6 %collective-permute-start.6 = (bf16[328,128]{1,0:T(8,128)(2,1)S(1)}, bf16[328,128]{1,0:T(8,128)(2,1)S(1)}, u32[]{:S(2)}, u32[]{:S(2)}) collective-permute-start(bf16[328,128]{1,0:T(8,128)(2,1)S(1)} %fusion.68), channel_id=1, source_target_pairs={{0,2},{1,3},{2,0},{3,1},{4,6},{5,7},{6,4},{7,5},{8,10},{9,11},{10,... | collective-permute-start | bytes 251912 | tf_op jit(solution)/shard_map/ppermute | solution.py:177
  40.5 5.5 %collective-permute-start.11 = (bf16[328,128]{1,0:T(8,128)(2,1)S(1)}, bf16[328,128]{1,0:T(8,128)(2,1)S(1)}, u32[]{:S(2)}, u32[]{:S(2)}) collective-permute-start(bf16[328,128]{1,0:T(8,128)(2,1)S(1)} %fusion.50), channel_id=1, source_target_pairs={{0,8},{4,12},{8,0},{12,4},{16,24},{20,28},{24,16},{28,20},{1,9},{5... | collective-permute-start | bytes 251912 | tf_op jit(solution)/shard_map/ppermute | solution.py:177
  42.9 6.3 %collective-permute-start.7 = (bf16[328,128]{1,0:T(8,128)(2,1)S(1)}, bf16[328,128]{1,0:T(8,128)(2,1)S(1)}, u32[]{:S(2)}, u32[]{:S(2)}) collective-permute-start(bf16[328,128]{1,0:T(8,128)(2,1)S(1)} %fusion.51), channel_id=1, source_target_pairs={{0,8},{4,12},{8,0},{12,4},{16,24},{20,28},{24,16},{28,20},{1,9},{5... | collective-permute-start | bytes 251912 | tf_op jit(solution)/shard_map/ppermute | solution.py:177
  46.1 7.2 %collective-permute-start.12 = (bf16[328,128]{1,0:T(8,128)(2,1)S(1)}, bf16[328,128]{1,0:T(8,128)(2,1)S(1)}, u32[]{:S(2)}, u32[]{:S(2)}) collective-permute-start(bf16[328,128]{1,0:T(8,128)(2,1)S(1)} %add_convert_fusion.3), channel_id=1, source_target_pairs={{0,16},{4,20},{8,24},{12,28},{16,0},{20,4},{24,8},{28,12},{1,17},{... | collective-permute-start | bytes 251912 | tf_op jit(solution)/shard_map/ppermute | solution.py:177
  49.2 6.3 %collective-permute-start.8 = (bf16[328,128]{1,0:T(8,128)(2,1)S(1)}, bf16[328,128]{1,0:T(8,128)(2,1)S(1)}, u32[]{:S(2)}, u32[]{:S(2)}) collective-permute-start(bf16[328,128]{1,0:T(8,128)(2,1)S(1)} %add_convert_fusion.5), channel_id=1, source_target_pairs={{0,16},{4,20},{8,24},{12,28},{16,0},{20,4},{24,8},{28,12},{1,17},{... | collective-permute-start | bytes 251912 | tf_op jit(solution)/shard_map/ppermute | solution.py:177
  55.6 1.5 %collective-permute-start.13 = (bf16[656,128]{1,0:T(8,128)(2,1)S(1)}, bf16[656,128]{1,0:T(8,128)(2,1)S(1)}, u32[]{:S(2)}, u32[]{:S(2)}) collective-permute-start(bf16[656,128]{1,0:T(8,128)(2,1)S(1)} %pad_maximum_fusion.3), channel_id=1, source_target_pairs={{0,4},{4,0},{8,12},{12,8},{16,20},{20,16},{24,28},{28,24},{1,5},{5... | collective-permute-start | bytes 503816 | tf_op jit(solution)/shard_map/ppermute | solution.py:177

commit v16 on v15

--- a/solution.py
+++ b/solution.py
@@ -35,8 +35,8 @@
 
 
 def extend_all(fields, margins):
-    widened = swap_edges(fields, margins, "lon", 1, True)
-    return swap_edges(widened, margins, "lat", 0, False)
+    widened = swap_edges(fields, margins, "lat", 0, False)
+    return swap_edges(widened, margins, "lon", 1, True)
 
 
 def decode(elem_codes, block_exps):

time: 59 us -> 59 us (level)
    unnamed x45 -> x44, local copies, waits for them, and re-layouts: 1.67 us -> 1.69 us
where the time goes in v16:
time: 59 us; the launch traced here: 58.6 us
  waiting for transfers between devices  20.9 us (35%)
  starting transfers between devices  20.8 us (35%)
  local copies, waits for them, and re-layouts  7.69 us (13%)
  matrix products  4.39 us (7%)
  other arithmetic  3.5 us (6%)
  between operations  1.38 us (2%)
    ppermute x10, waiting for transfers between devices, exchange(): return lax.ppermute(part, axis, [(i, i ^ step) for i in range(size)])  15.2 us
    ppermute x10, starting transfers between devices, exchange(): return lax.ppermute(part, axis, [(i, i ^ step) for i in range(size)])  12.4 us
    ppermute x2, starting transfers between devices, swap_edges(): lax.ppermute(jnp.concatenate([p.reshape(-1) for p in leads]), axis, down)  5.24 us
    ppermute x2, waiting for transfers between devices, swap_edges(): lax.ppermute(jnp.concatenate([p.reshape(-1) for p in lasts]), axis, up)  4.19 us
    ppermute x2, starting transfers between devices, swap_edges(): lax.ppermute(jnp.concatenate([p.reshape(-1) for p in lasts]), axis, up)  3.22 us
    unnamed x44, local copies, waits for them, and re-layouts  1.69 us
    ppermute x2, waiting for transfers between devices, swap_edges(): lax.ppermute(jnp.concatenate([p.reshape(-1) for p in leads]), axis, down)  1.43 us
    add x3, other arithmetic, halve(): keep + exchange(send.astype(jnp.bfloat16), axis, step).astype(keep.dtype)  1.28 us
  transfers between devices with their start and end apart: 14, of which 11 were waited for; matrix products, arithmetic and copies ran while one was open for 5% of the time, Pallas kernels for 0%

profile of v16, /device:TPU:0, one launch (start us, length us, event | category | flops | bytes accessed | tf_op | source)
XLA Modules:
  0.0 58.6 jit_solution(3448903523032724489)
XLA Ops:
  0.7 0.8 %fusion.80 = (bf16[2,16,128]{2,1,0:T(8,128)(2,1)S(1)}, bf16[2,16,128]{2,1,0:T(8,128)(2,1)S(1)}) fusion(bf16[32,16,128]{2,1,0:T(8,128)(2,1)} %param.11), kind=kLoop, calls=%fused_computation.209 | loop fusion | bytes 32768 | tf_op jit(solution)/shard_map/slice | solution.py:23
  1.5 0.8 %multiply_exponential_fusion = f32[16,8,8]{0,2,1:T(8,128)S(1)} fusion(s32[16,8,8]{0,2,1:T(8,128)} %param.7), kind=kLoop, calls=%fused_computation.186 | loop fusion | flops 2048 | bytes 8192 | tf_op jit(solution)/shard_map/exp2 | solution.py:50
  2.3 0.2 broadcast_in_dim.21
  2.6 0.2 reshape.202
  2.8 0.3 fusion.65
  3.1 1.3 %collective-permute-start.1 = (bf16[6144]{0:T(1024)(128)(2,1)S(1)}, bf16[6144]{0:T(1024)(128)(2,1)S(1)}, u32[]{:S(2)}, u32[]{:S(2)}) collective-permute-start(bf16[6144]{0:T(1024)(128)(2,1)S(1)} %pad_maximum_fusion.14), channel_id=1, source_target_pairs={{4,0},{8,4},{12,8},{16,12},{20,16},{24,20},{28,24},{5,1},{9,5},{13... | collective-permute-start | bytes 36872 | tf_op jit(solution)/shard_map/ppermute | solution.py:26
  4.5 3.2 %collective-permute-start = (bf16[6144]{0:T(1024)(128)(2,1)S(1)}, bf16[6144]{0:T(1024)(128)(2,1)S(1)}, u32[]{:S(2)}, u32[]{:S(2)}) collective-permute-start(bf16[6144]{0:T(1024)(128)(2,1)S(1)} %pad_maximum_fusion.13), channel_id=1, source_target_pairs={{0,4},{4,8},{8,12},{12,16},{16,20},{20,24},{24,28},{1,5},{5,9},{9,... | collective-permute-start | bytes 36872 | tf_op jit(solution)/shard_map/ppermute | solution.py:25
  7.8 0.7 %collective-permute-done = bf16[6144]{0:T(1024)(128)(2,1)S(1)} collective-permute-done((bf16[6144]{0:T(1024)(128)(2,1)S(1)}, bf16[6144]{0:T(1024)(128)(2,1)S(1)}, u32[]{:S(2)}, u32[]{:S(2)}) %collective-permute-start) | collective-permute-done | bytes 12320 | tf_op jit(solution)/shard_map/ppermute | solution.py:25
  8.6 3.9 %collective-permute-start.2 = (bf16[13824]{0:T(1024)(128)(2,1)S(1)}, bf16[13824]{0:T(1024)(128)(2,1)S(1)}, u32[]{:S(2)}, u32[]{:S(2)}) collective-permute-start(bf16[13824]{0:T(1024)(128)(2,1)S(1)} %pad_maximum_fusion.5), channel_id=1, source_target_pairs={{1,0},{2,1},{3,2},{0,3},{5,4},{6,5},{7,6},{4,7},{9,8},{10,9},{11,1... | collective-permute-start | bytes 82952 | tf_op jit(solution)/shard_map/ppermute | solution.py:26
  12.7 1.4 %collective-permute-done.2 = bf16[13824]{0:T(1024)(128)(2,1)S(1)} collective-permute-done((bf16[13824]{0:T(1024)(128)(2,1)S(1)}, bf16[13824]{0:T(1024)(128)(2,1)S(1)}, u32[]{:S(2)}, u32[]{:S(2)}) %collective-permute-start.2) | collective-permute-done | bytes 27680 | tf_op jit(solution)/shard_map/ppermute | solution.py:26
  14.1 3.5 %collective-permute-done.3 = bf16[13824]{0:T(1024)(128)(2,1)S(1)} collective-permute-done((bf16[13824]{0:T(1024)(128)(2,1)S(1)}, bf16[13824]{0:T(1024)(128)(2,1)S(1)}, u32[]{:S(2)}, u32[]{:S(2)}) %collective-permute-start.3) | collective-permute-done | bytes 27680 | tf_op jit(solution)/shard_map/ppermute | solution.py:25
  17.8 0.3 convolution_bitcast_fusion
  18.1 0.3 convolution_bitcast_fusion.1
  18.4 0.3 convolution_bitcast_fusion.2
  18.7 0.3 convolution_bitcast_fusion.3
  19.1 0.2 copy.44
  19.3 0.2 reshape.249
  19.5 0.2 copy-done.7
  19.7 0.1 fusion.46
  20.7 0.2 copy-done.8
  21.0 0.7 %convolution_select_fusion = f32[34,8,3,128]{3,1,2,0:T(8,128)S(1)} fusion(bf16[3,3,128,128]{3,2,1,0:T(8,128)(2,1)S(1)} %copy-done, bf16[36,1,7,2,128]{4,2,3,0,1:T(8,128)(2,1)S(1)} %slice.391, bf16[36,1,8,3,128]{4,2,3,0,1:T(8,128)(2,1)S(1)} %copy.29, pred[8,3]{0,1:T(4,128)(4,1)S(1)} %copy-done.8), kind=kOutput, calls=%fused_computation.3 | convolution fusion | flops 241858560 | bytes 1062936 | tf_op jit(solution)/shard_map/conv_general_dilated | solution.py:126
  21.8 0.2 squeeze.107
  22.0 0.2 broadcast_select_fusion
  22.5 0.5 fusion
  23.1 0.5 fusion.70
  23.7 0.2 pad_maximum_fusion
  23.9 0.9 %fusion.4 = bf16[4,656,128]{2,1,0:T(8,128)(2,1)} fusion(f32[4,2,656,128]{3,2,1,0:T(8,128)S(1)} %bitcast.228, s32[]{:T(128)S(6)} %select_n.108), kind=kLoop, calls=%fused_computation.14 | loop fusion | bytes 1343492 | tf_op jit(solution)/shard_map/convert_element_type | solution.py:184
  24.8 2.4 %collective-permute-done.4 = bf16[4,656,128]{2,1,0:T(8,128)(2,1)} collective-permute-done((bf16[4,656,128]{2,1,0:T(8,128)(2,1)}, bf16[4,656,128]{2,1,0:T(8,128)(2,1)}, u32[]{:S(2)}, u32[]{:S(2)}) %collective-permute-start.4) | collective-permute-done | bytes 671776 | tf_op jit(solution)/shard_map/ppermute | solution.py:177
  27.3 1.2 %bitcast_add_fusion = f32[4,656,128]{2,1,0:T(8,128)S(1)} fusion(bf16[4,656,128]{2,1,0:T(8,128)(2,1)} %collective-permute-done.4, f32[4,2,656,128]{3,2,1,0:T(8,128)S(1)} %bitcast.229, s32[]{:T(128)S(6)} %select_n.107), kind=kLoop, calls=%fused_computation.1 | loop fusion | flops 671744 | bytes 3358724 | tf_op jit(solution)/shard_map/add | solution.py:184
  28.6 0.6 collective-permute-start.9
  29.2 0.5 copy-done.2
  29.7 0.5 fusion.83
  30.2 0.7 %copy.61 = f32[16,8,256,1]{2,1,0,3:T(8,128)} copy(f32[16,8,256,1]{2,0,1,3:T(8,128)S(1)} %fusion.83) | data formatting | bytes 262144 | tf_op jit(solution)/shard_map/rctn,tmn->rcm/dot_general | solution.py:150
  31.0 4.0 %collective-permute-done.9 = bf16[2,328,128]{2,1,0:T(8,128)(2,1)S(1)} collective-permute-done((bf16[2,328,128]{2,1,0:T(8,128)(2,1)S(1)}, bf16[2,328,128]{2,1,0:T(8,128)(2,1)S(1)}, u32[]{:S(2)}, u32[]{:S(2)}) %collective-permute-start.9) | collective-permute-done | bytes 167968 | tf_op jit(solution)/shard_map/ppermute | solution.py:177
  35.2 2.4 %collective-permute-done.5 = bf16[2,328,128]{2,1,0:T(8,128)(2,1)S(1)} collective-permute-done((bf16[2,328,128]{2,1,0:T(8,128)(2,1)S(1)}, bf16[2,328,128]{2,1,0:T(8,128)(2,1)S(1)}, u32[]{:S(2)}, u32[]{:S(2)}) %collective-permute-start.5) | collective-permute-done | bytes 167968 | tf_op jit(solution)/shard_map/ppermute | solution.py:177
  37.6 1.0 %collective-permute-start.6 = (bf16[328,128]{1,0:T(8,128)(2,1)S(1)}, bf16[328,128]{1,0:T(8,128)(2,1)S(1)}, u32[]{:S(2)}, u32[]{:S(2)}) collective-permute-start(bf16[328,128]{1,0:T(8,128)(2,1)S(1)} %fusion.68), channel_id=1, source_target_pairs={{0,2},{1,3},{2,0},{3,1},{4,6},{5,7},{6,4},{7,5},{8,10},{9,11},{10,... | collective-permute-start | bytes 251912 | tf_op jit(solution)/shard_map/ppermute | solution.py:177
  38.6 1.0 %collective-permute-done.10 = bf16[328,128]{1,0:T(8,128)(2,1)S(1)} collective-permute-done((bf16[328,128]{1,0:T(8,128)(2,1)S(1)}, bf16[328,128]{1,0:T(8,128)(2,1)S(1)}, u32[]{:S(2)}, u32[]{:S(2)}) %collective-permute-start.10) | collective-permute-done | bytes 84000 | tf_op jit(solution)/shard_map/ppermute | solution.py:177
  39.7 3.2 %collective-permute-start.11 = (bf16[328,128]{1,0:T(8,128)(2,1)S(1)}, bf16[328,128]{1,0:T(8,128)(2,1)S(1)}, u32[]{:S(2)}, u32[]{:S(2)}) collective-permute-start(bf16[328,128]{1,0:T(8,128)(2,1)S(1)} %fusion.50), channel_id=1, source_target_pairs={{0,8},{4,12},{8,0},{12,4},{16,24},{20,28},{24,16},{28,20},{1,9},{5... | collective-permute-start | bytes 251912 | tf_op jit(solution)/shard_map/ppermute | solution.py:177
  42.9 2.5 %collective-permute-start.7 = (bf16[328,128]{1,0:T(8,128)(2,1)S(1)}, bf16[328,128]{1,0:T(8,128)(2,1)S(1)}, u32[]{:S(2)}, u32[]{:S(2)}) collective-permute-start(bf16[328,128]{1,0:T(8,128)(2,1)S(1)} %fusion.51), channel_id=1, source_target_pairs={{0,8},{4,12},{8,0},{12,4},{16,24},{20,28},{24,16},{28,20},{1,9},{5... | collective-permute-start | bytes 251912 | tf_op jit(solution)/shard_map/ppermute | solution.py:177
  45.4 0.7 %collective-permute-done.11 = bf16[328,128]{1,0:T(8,128)(2,1)S(1)} collective-permute-done((bf16[328,128]{1,0:T(8,128)(2,1)S(1)}, bf16[328,128]{1,0:T(8,128)(2,1)S(1)}, u32[]{:S(2)}, u32[]{:S(2)}) %collective-permute-start.11) | collective-permute-done | bytes 84000 | tf_op jit(solution)/shard_map/ppermute | solution.py:177
  46.0 3.1 %collective-permute-start.12 = (bf16[328,128]{1,0:T(8,128)(2,1)S(1)}, bf16[328,128]{1,0:T(8,128)(2,1)S(1)}, u32[]{:S(2)}, u32[]{:S(2)}) collective-permute-start(bf16[328,128]{1,0:T(8,128)(2,1)S(1)} %add_convert_fusion.3), channel_id=1, source_target_pairs={{0,16},{4,20},{8,24},{12,28},{16,0},{20,4},{24,8},{28,12},{1,17},{... | collective-permute-start | bytes 251912 | tf_op jit(solution)/shard_map/ppermute | solution.py:177
  49.2 1.8 %collective-permute-start.8 = (bf16[328,128]{1,0:T(8,128)(2,1)S(1)}, bf16[328,128]{1,0:T(8,128)(2,1)S(1)}, u32[]{:S(2)}, u32[]{:S(2)}) collective-permute-start(bf16[328,128]{1,0:T(8,128)(2,1)S(1)} %add_convert_fusion.5), channel_id=1, source_target_pairs={{0,16},{4,20},{8,24},{12,28},{16,0},{20,4},{24,8},{28,12},{1,17},{... | collective-permute-start | bytes 251912 | tf_op jit(solution)/shard_map/ppermute | solution.py:177
  50.9 2.3 %collective-permute-done.12 = bf16[328,128]{1,0:T(8,128)(2,1)S(1)} collective-permute-done((bf16[328,128]{1,0:T(8,128)(2,1)S(1)}, bf16[328,128]{1,0:T(8,128)(2,1)S(1)}, u32[]{:S(2)}, u32[]{:S(2)}) %collective-permute-start.12) | collective-permute-done | bytes 84000 | tf_op jit(solution)/shard_map/ppermute | solution.py:177
  53.2 2.3 %collective-permute-done.8 = bf16[328,128]{1,0:T(8,128)(2,1)S(1)} collective-permute-done((bf16[328,128]{1,0:T(8,128)(2,1)S(1)}, bf16[328,128]{1,0:T(8,128)(2,1)S(1)}, u32[]{:S(2)}, u32[]{:S(2)}) %collective-permute-start.8) | collective-permute-done | bytes 84000 | tf_op jit(solution)/shard_map/ppermute | solution.py:177
  55.6 1.1 %convolution_convert_fusion = bf16[32,16,128]{2,1,0:T(8,128)(2,1)} fusion(bf16[32,16,1152]{2,1,0:T(8,128)(2,1)S(1)} %copy-done.4, bf16[1152,128,1]{1,0,2:T(8,128)(2,1)S(1)} %bitcast.226), kind=kOutput, calls=%fused_computation.7 | convolution fusion | flops 151060480 | bytes 1605632 | tf_op jit(solution)/shard_map/rck,kn->rcn/dot_general | solution.py:138
  56.8 0.2 collective-permute-done.13
  57.1 0.8 %slice.411 = f32[1024,128]{1,0:T(8,128)} slice(f32[1312,128]{1,0:T(8,128)S(1)} %convert_multiply_fusion), slice={[0:1024], [0:128]} | slice | bytes 1048576 | tf_op jit(solution)/shard_map/slice | solution.py:170
  58.0 0.7 %slice.412 = f32[288,128]{1,0:T(8,128)} slice(f32[1312,128]{1,0:T(8,128)S(1)} %convert_multiply_fusion), slice={[1024:1312], [0:128]} | slice | bytes 294912 | tf_op jit(solution)/shard_map/slice | solution.py:171
  (105 shorter events, 2.8 us)
Async XLA Ops:
  0.6 20.1 %copy-start = (bf16[3,3,128,128]{3,2,1,0:T(8,128)(2,1)S(1)}, bf16[3,3,128,128]{3,2,1,0:T(8,128)(2,1)}, u32[]{:S(2)}) copy-start(bf16[3,3,128,128]{3,2,1,0:T(8,128)(2,1)} %param.10) | copy-start | bytes 884740
  0.6 2.1 %copy-start.6 = (s32[16,8,256]{2,1,0:T(8,128)S(1)}, s32[16,8,256]{2,1,0:T(8,128)}, u32[]{:S(2)}) copy-start(s32[16,8,256]{2,1,0:T(8,128)} %param.6) | copy-start | bytes 393220
  0.7 7.0 %copy-start.1 = (bf16[4,4,256,128]{3,2,1,0:T(8,128)(2,1)S(1)}, bf16[4,4,256,128]{3,2,1,0:T(8,128)(2,1)}, u32[]{:S(2)}) copy-start(bf16[4,4,256,128]{3,2,1,0:T(8,128)(2,1)} %param.8) | copy-start | bytes 3145732
  3.1 4.6 %collective-permute-start.1 = (bf16[6144]{0:T(1024)(128)(2,1)S(1)}, bf16[6144]{0:T(1024)(128)(2,1)S(1)}, u32[]{:S(2)}, u32[]{:S(2)}) collective-permute-start(bf16[6144]{0:T(1024)(128)(2,1)S(1)} %pad_maximum_fusion.14), channel_id=1, source_target_pairs={{4,0},{8,4},{12,8},{16,12},{20,16},{24,20},{28,24},{5,1},{9,5},{13... | collective-permute-start | bytes 36872 | tf_op jit(solution)/shard_map/ppermute | solution.py:26
  4.4 4.1 %copy-start.5 = (bf16[32,16,128]{2,1,0:T(8,128)(2,1)S(1)}, bf16[32,16,128]{2,1,0:T(8,128)(2,1)}, u32[]{:S(2)}) copy-start(bf16[32,16,128]{2,1,0:T(8,128)(2,1)} %param.11) | copy-start | bytes 393220
  4.5 4.0 %collective-permute-start = (bf16[6144]{0:T(1024)(128)(2,1)S(1)}, bf16[6144]{0:T(1024)(128)(2,1)S(1)}, u32[]{:S(2)}, u32[]{:S(2)}) collective-permute-start(bf16[6144]{0:T(1024)(128)(2,1)S(1)} %pad_maximum_fusion.13), channel_id=1, source_target_pairs={{0,4},{4,8},{8,12},{12,16},{16,20},{20,24},{24,28},{1,5},{5,9},{9,... | collective-permute-start | bytes 36872 | tf_op jit(solution)/shard_map/ppermute | solution.py:25
  8.6 5.5 %collective-permute-start.2 = (bf16[13824]{0:T(1024)(128)(2,1)S(1)}, bf16[13824]{0:T(1024)(128)(2,1)S(1)}, u32[]{:S(2)}, u32[]{:S(2)}) collective-permute-start(bf16[13824]{0:T(1024)(128)(2,1)S(1)} %pad_maximum_fusion.5), channel_id=1, source_target_pairs={{1,0},{2,1},{3,2},{0,3},{5,4},{6,5},{7,6},{4,7},{9,8},{10,9},{11,1... | collective-permute-start | bytes 82952 | tf_op jit(solution)/shard_map/ppermute | solution.py:26
  12.6 5.1 %collective-permute-start.3 = (bf16[13824]{0:T(1024)(128)(2,1)S(1)}, bf16[13824]{0:T(1024)(128)(2,1)S(1)}, u32[]{:S(2)}, u32[]{:S(2)}) collective-permute-start(bf16[13824]{0:T(1024)(128)(2,1)S(1)} %pad_maximum_fusion.6), channel_id=1, source_target_pairs={{0,1},{1,2},{2,3},{3,0},{4,5},{5,6},{6,7},{7,4},{8,9},{9,10},{10,1... | collective-permute-start | bytes 82952 | tf_op jit(solution)/shard_map/ppermute | solution.py:25
  19.1 0.7 %copy-start.7 = (f32[128]{0:T(128)S(1)}, f32[128]{0:T(128)}, u32[]{:S(2)}) copy-start(f32[128]{0:T(128)} %param.9) | copy-start | bytes 1540
  20.3 0.7 %copy-start.8 = (pred[8,3]{0,1:T(4,128)(4,1)S(1)}, pred[8,3]{0,1:T(4,128)(4,1)}, u32[]{:S(2)}) copy-start(pred[8,3]{0,1:T(4,128)(4,1)} %constant.177) | copy-start | bytes 76
  20.4 2.1 %copy-start.3 = (bf16[32,16,1152]{2,1,0:T(8,128)(2,1)}, bf16[32,16,1152]{2,1,0:T(8,128)(2,1)S(1)}, u32[]{:S(2)}) copy-start(bf16[32,16,1152]{2,1,0:T(8,128)(2,1)S(1)} %slice_dynamic-update-slice_fusion) | copy-start | bytes 3538948
  24.8 2.5 %collective-permute-start.4 = (bf16[4,656,128]{2,1,0:T(8,128)(2,1)}, bf16[4,656,128]{2,1,0:T(8,128)(2,1)}, u32[]{:S(2)}, u32[]{:S(2)}) collective-permute-start(bf16[4,656,128]{2,1,0:T(8,128)(2,1)} %fusion.4), channel_id=1, source_target_pairs={{0,4},{4,0},{8,12},{12,8},{16,20},{20,16},{24,28},{28,24},{1,5},{5... | collective-permute-start | bytes 2015240 | tf_op jit(solution)/shard_map/ppermute | solution.py:177
  28.5 1.2 %copy-start.2 = (bf16[4,4,256,128]{3,2,1,0:T(8,128)(2,1)S(1)}, bf16[4,4,256,128]{3,2,1,0:T(8,128)(2,1)}, u32[]{:S(2)}) copy-start(bf16[4,4,256,128]{3,2,1,0:T(8,128)(2,1)} %param.8) | copy-start | bytes 3145732
  28.6 6.4 %collective-permute-start.9 = (bf16[2,328,128]{2,1,0:T(8,128)(2,1)S(1)}, bf16[2,328,128]{2,1,0:T(8,128)(2,1)S(1)}, u32[]{:S(2)}, u32[]{:S(2)}) collective-permute-start(bf16[2,328,128]{2,1,0:T(8,128)(2,1)S(1)} %fusion.49), channel_id=1, source_target_pairs={{0,2},{1,3},{2,0},{3,1},{4,6},{5,7},{6,4},{7,5},{8,10},{9,11},{10,... | collective-permute-start | bytes 503816 | tf_op jit(solution)/shard_map/ppermute | solution.py:177
  30.9 6.6 %collective-permute-start.5 = (bf16[2,328,128]{2,1,0:T(8,128)(2,1)S(1)}, bf16[2,328,128]{2,1,0:T(8,128)(2,1)S(1)}, u32[]{:S(2)}, u32[]{:S(2)}) collective-permute-start(bf16[2,328,128]{2,1,0:T(8,128)(2,1)S(1)} %fusion.48), channel_id=1, source_target_pairs={{0,1},{1,0},{2,3},{3,2},{4,5},{5,4},{6,7},{7,6},{8,9},{9,8},{10,11... | collective-permute-start | bytes 503816 | tf_op jit(solution)/shard_map/ppermute | solution.py:177
  35.1 4.5 %collective-permute-start.10 = (bf16[328,128]{1,0:T(8,128)(2,1)S(1)}, bf16[328,128]{1,0:T(8,128)(2,1)S(1)}, u32[]{:S(2)}, u32[]{:S(2)}) collective-permute-start(bf16[328,128]{1,0:T(8,128)(2,1)S(1)} %fusion.69), channel_id=1, source_target_pairs={{0,1},{1,0},{2,3},{3,2},{4,5},{5,4},{6,7},{7,6},{8,9},{9,8},{10,11... | collective-permute-start | bytes 251912 | tf_op jit(solution)/shard_map/ppermute | solution.py:177
  37.6 18.0 %copy-start.4 = (bf16[32,16,1152]{2,1,0:T(8,128)(2,1)S(1)}, bf16[32,16,1152]{2,1,0:T(8,128)(2,1)}, u32[]{:S(2)}) copy-start(bf16[32,16,1152]{2,1,0:T(8,128)(2,1)} %copy-done.3) | copy-start | bytes 3538948
  37.6 5.2 %collective-permute-start.6 = (bf16[328,128]{1,0:T(8,128)(2,1)S(1)}, bf16[328,128]{1,0:T(8,128)(2,1)S(1)}, u32[]{:S(2)}, u32[]{:S(2)}) collective-permute-start(bf16[328,128]{1,0:T(8,128)(2,1)S(1)} %fusion.68), channel_id=1, source_target_pairs={{0,2},{1,3},{2,0},{3,1},{4,6},{5,7},{6,4},{7,5},{8,10},{9,11},{10,... | collective-permute-start | bytes 251912 | tf_op jit(solution)/shard_map/ppermute | solution.py:177
  39.7 6.4 %collective-permute-start.11 = (bf16[328,128]{1,0:T(8,128)(2,1)S(1)}, bf16[328,128]{1,0:T(8,128)(2,1)S(1)}, u32[]{:S(2)}, u32[]{:S(2)}) collective-permute-start(bf16[328,128]{1,0:T(8,128)(2,1)S(1)} %fusion.50), channel_id=1, source_target_pairs={{0,8},{4,12},{8,0},{12,4},{16,24},{20,28},{24,16},{28,20},{1,9},{5... | collective-permute-start | bytes 251912 | tf_op jit(solution)/shard_map/ppermute | solution.py:177
  42.9 6.3 %collective-permute-start.7 = (bf16[328,128]{1,0:T(8,128)(2,1)S(1)}, bf16[328,128]{1,0:T(8,128)(2,1)S(1)}, u32[]{:S(2)}, u32[]{:S(2)}) collective-permute-start(bf16[328,128]{1,0:T(8,128)(2,1)S(1)} %fusion.51), channel_id=1, source_target_pairs={{0,8},{4,12},{8,0},{12,4},{16,24},{20,28},{24,16},{28,20},{1,9},{5... | collective-permute-start | bytes 251912 | tf_op jit(solution)/shard_map/ppermute | solution.py:177
  46.0 7.2 %collective-permute-start.12 = (bf16[328,128]{1,0:T(8,128)(2,1)S(1)}, bf16[328,128]{1,0:T(8,128)(2,1)S(1)}, u32[]{:S(2)}, u32[]{:S(2)}) collective-permute-start(bf16[328,128]{1,0:T(8,128)(2,1)S(1)} %add_convert_fusion.3), channel_id=1, source_target_pairs={{0,16},{4,20},{8,24},{12,28},{16,0},{20,4},{24,8},{28,12},{1,17},{... | collective-permute-start | bytes 251912 | tf_op jit(solution)/shard_map/ppermute | solution.py:177
  49.2 6.3 %collective-permute-start.8 = (bf16[328,128]{1,0:T(8,128)(2,1)S(1)}, bf16[328,128]{1,0:T(8,128)(2,1)S(1)}, u32[]{:S(2)}, u32[]{:S(2)}) collective-permute-start(bf16[328,128]{1,0:T(8,128)(2,1)S(1)} %add_convert_fusion.5), channel_id=1, source_target_pairs={{0,16},{4,20},{8,24},{12,28},{16,0},{20,4},{24,8},{28,12},{1,17},{... | collective-permute-start | bytes 251912 | tf_op jit(solution)/shard_map/ppermute | solution.py:177
  55.6 1.5 %collective-permute-start.13 = (bf16[656,128]{1,0:T(8,128)(2,1)S(1)}, bf16[656,128]{1,0:T(8,128)(2,1)S(1)}, u32[]{:S(2)}, u32[]{:S(2)}) collective-permute-start(bf16[656,128]{1,0:T(8,128)(2,1)S(1)} %pad_maximum_fusion.3), channel_id=1, source_target_pairs={{0,4},{4,0},{8,12},{12,8},{16,20},{20,16},{24,28},{28,24},{1,5},{5... | collective-permute-start | bytes 503816 | tf_op jit(solution)/shard_map/ppermute | solution.py:177

commit v17 on v15

--- a/solution.py
+++ b/solution.py
@@ -240,7 +240,7 @@
         return reduce_lat(mine)
     pair = rows.reshape((lon_count, 2, count // 2) + rows.shape[2:])
     part = halve(pair, "lat", lat_steps[0], 1)
-    half = count // 4
+    half = count // 6 // 8 * 8
     first = scatter_lon(part[:, :half], steps)
     second = scatter_lon(part[:, half:], list(reversed(steps)))
     joined = jnp.concatenate([butterfly(first, lat_steps[1:]), butterfly(second, lat_steps[1:])])

time: 59 us -> 58.9 us (level)
  the two profiles are of different devices: /device:TPU:0 before, /device:TPU:3 now
where the time goes in v17:
time: 58.9 us; the launch traced here: 58.6 us
  starting transfers between devices  29 us (49%)
  waiting for transfers between devices  11.7 us (20%)
  local copies, waits for them, and re-layouts  7.29 us (12%)
  matrix products  5.62 us (10%)
  other arithmetic  3.53 us (6%)
  between operations  1.39 us (2%)
    ppermute x10, starting transfers between devices, exchange(): return lax.ppermute(part, axis, [(i, i ^ step) for i in range(size)])  19.7 us
    ppermute x10, waiting for transfers between devices, exchange(): return lax.ppermute(part, axis, [(i, i ^ step) for i in range(size)])  9.62 us
    ppermute x2, starting transfers between devices, swap_edges(): lax.ppermute(jnp.concatenate([p.reshape(-1) for p in lasts]), axis, up)  5.49 us
    ppermute x2, starting transfers between devices, swap_edges(): lax.ppermute(jnp.concatenate([p.reshape(-1) for p in leads]), axis, down)  3.79 us
    dot_general x1, matrix products, shards(): jnp.einsum('rctn,tmn->rcm', grad_patches.reshape(in_rows, in_cols, 16, CO...  1.69 us
    add x3, other arithmetic, halve(): keep + exchange(send.astype(jnp.bfloat16), axis, step).astype(keep.dtype)  1.3 us
  transfers between devices with their start and end apart: 14, of which 7 were waited for; matrix products, arithmetic and copies ran while one was open for 7% of the time, Pallas kernels for 0%

profile of v17, /device:TPU:3, one launch (start us, length us, event | category | flops | bytes accessed | tf_op | source)
XLA Modules:
  0.0 58.6 jit_solution(12691189948928698299)
XLA Ops:
  0.7 1.0 %fusion.80 = (bf16[32,2,128]{2,1,0:T(2,128)(2,1)S(1)}, bf16[32,2,128]{2,1,0:T(2,128)(2,1)S(1)}) fusion(bf16[32,16,128]{2,1,0:T(8,128)(2,1)} %param.11), kind=kLoop, calls=%fused_computation.209 | loop fusion | bytes 65536 | tf_op jit(solution)/shard_map/slice | solution.py:23
  1.7 0.8 %multiply_exponential_fusion = f32[16,8,8]{0,2,1:T(8,128)S(1)} fusion(s32[16,8,8]{0,2,1:T(8,128)} %param.7), kind=kLoop, calls=%fused_computation.186 | loop fusion | flops 2048 | bytes 8192 | tf_op jit(solution)/shard_map/exp2 | solution.py:50
  2.5 0.2 broadcast_in_dim.21
  2.7 0.2 reshape.202
  2.9 0.3 fusion.63
  3.4 2.4 %collective-permute-start = (bf16[12288]{0:T(1024)(128)(2,1)S(1)}, bf16[12288]{0:T(1024)(128)(2,1)S(1)}, u32[]{:S(2)}, u32[]{:S(2)}) collective-permute-start(bf16[12288]{0:T(1024)(128)(2,1)S(1)} %pad_maximum_fusion.5), channel_id=1, source_target_pairs={{0,1},{1,2},{2,3},{3,0},{4,5},{5,6},{6,7},{7,4},{8,9},{9,10},{10,1... | collective-permute-start | bytes 73736 | tf_op jit(solution)/shard_map/ppermute | solution.py:25
  5.9 1.0 %collective-permute-done.1 = bf16[12288]{0:T(1024)(128)(2,1)S(1)} collective-permute-done((bf16[12288]{0:T(1024)(128)(2,1)S(1)}, bf16[12288]{0:T(1024)(128)(2,1)S(1)}, u32[]{:S(2)}, u32[]{:S(2)}) %collective-permute-start.1) | collective-permute-done | bytes 24608 | tf_op jit(solution)/shard_map/ppermute | solution.py:26
  6.9 0.3 collective-permute-done
  7.4 3.7 %collective-permute-start.2 = (bf16[7680]{0:T(1024)(128)(2,1)S(1)}, bf16[7680]{0:T(1024)(128)(2,1)S(1)}, u32[]{:S(2)}, u32[]{:S(2)}) collective-permute-start(bf16[7680]{0:T(1024)(128)(2,1)S(1)} %pad_maximum_fusion.7), channel_id=1, source_target_pairs={{4,0},{8,4},{12,8},{16,12},{20,16},{24,20},{28,24},{5,1},{9,5},{13... | collective-permute-start | bytes 46088 | tf_op jit(solution)/shard_map/ppermute | solution.py:26
  11.2 3.1 %collective-permute-start.3 = (bf16[7680]{0:T(1024)(128)(2,1)S(1)}, bf16[7680]{0:T(1024)(128)(2,1)S(1)}, u32[]{:S(2)}, u32[]{:S(2)}) collective-permute-start(bf16[7680]{0:T(1024)(128)(2,1)S(1)} %pad_maximum_fusion.8), channel_id=1, source_target_pairs={{0,4},{4,8},{8,12},{12,16},{16,20},{20,24},{24,28},{1,5},{5,9},{9,... | collective-permute-start | bytes 46088 | tf_op jit(solution)/shard_map/ppermute | solution.py:25
  14.4 0.8 %collective-permute-done.3 = bf16[7680]{0:T(1024)(128)(2,1)S(1)} collective-permute-done((bf16[7680]{0:T(1024)(128)(2,1)S(1)}, bf16[7680]{0:T(1024)(128)(2,1)S(1)}, u32[]{:S(2)}, u32[]{:S(2)}) %collective-permute-start.3) | collective-permute-done | bytes 15392 | tf_op jit(solution)/shard_map/ppermute | solution.py:25
  15.3 0.3 convolution_bitcast_fusion
  15.6 0.3 convolution_bitcast_fusion.1
  15.9 0.3 convolution_bitcast_fusion.2
  16.2 0.3 convolution_bitcast_fusion.3
  16.6 0.2 copy.44
  16.8 0.2 reshape.249
  17.0 0.2 copy-done.6
  17.2 0.1 fusion.48
  17.9 0.1 maximum_bitcast_fusion.10
  18.2 0.2 copy-done.7
  18.5 0.7 %convolution_select_fusion = f32[34,8,3,128]{3,1,2,0:T(8,128)S(1)} fusion(bf16[3,3,128,128]{3,2,1,0:T(8,128)(2,1)S(1)} %copy-done, bf16[36,1,7,2,128]{4,2,3,0,1:T(8,128)(2,1)S(1)} %slice.391, bf16[36,1,8,3,128]{4,2,3,0,1:T(8,128)(2,1)S(1)} %copy.29, pred[8,3]{0,1:T(4,128)(4,1)S(1)} %copy-done.7), kind=kOutput, calls=%fused_computation.3 | convolution fusion | flops 241858560 | bytes 1062936 | tf_op jit(solution)/shard_map/conv_general_dilated | solution.py:126
  19.3 0.2 squeeze.108
  19.4 0.2 broadcast_select_fusion
  20.0 0.5 fusion
  20.6 0.5 fusion.69
  21.0 0.1 copy.33
  21.2 0.2 pad_maximum_fusion
  21.3 0.9 %fusion.4 = bf16[4,656,128]{2,1,0:T(8,128)(2,1)} fusion(f32[4,2,656,128]{3,2,1,0:T(8,128)S(1)} %bitcast.224, s32[]{:T(128)S(6)} %select_n.109), kind=kLoop, calls=%fused_computation.14 | loop fusion | bytes 1343492 | tf_op jit(solution)/shard_map/convert_element_type | solution.py:184
  22.3 1.7 %fusion.83 = f32[16,8,256,1]{2,0,1,3:T(8,128)S(1)} fusion(bf16[16,8,16,128]{3,0,1,2:T(8,128)(2,1)S(1)} %constant_dynamic-update-slice_fusion, bf16[16,256,128,1]{2,1,3,0:T(8,128)(2,1)} %bitcast.226), kind=kOutput, calls=%fused_computation.212 | convolution fusion | flops 134217728 | bytes 1703936 | tf_op jit(solution)/shard_map/rctn,tmn->rcm/dot_general | solution.py:150
  24.0 0.7 %copy.61 = f32[16,8,256,1]{2,1,0,3:T(8,128)} copy(f32[16,8,256,1]{2,0,1,3:T(8,128)S(1)} %fusion.83) | data formatting | bytes 262144 | tf_op jit(solution)/shard_map/rctn,tmn->rcm/dot_general | solution.py:150
  24.8 1.2 %bitcast_add_fusion = f32[4,656,128]{2,1,0:T(8,128)S(1)} fusion(bf16[4,656,128]{2,1,0:T(8,128)(2,1)} %collective-permute-done.4, f32[4,2,656,128]{3,2,1,0:T(8,128)S(1)} %bitcast.225, s32[]{:T(128)S(6)} %select_n.108), kind=kLoop, calls=%fused_computation.1 | loop fusion | flops 671744 | bytes 3358724 | tf_op jit(solution)/shard_map/add | solution.py:184
  26.1 2.5 %collective-permute-start.5 = (bf16[2,216,128]{2,1,0:T(8,128)(2,1)S(1)}, bf16[2,216,128]{2,1,0:T(8,128)(2,1)S(1)}, u32[]{:S(2)}, u32[]{:S(2)}) collective-permute-start(bf16[2,216,128]{2,1,0:T(8,128)(2,1)S(1)} %fusion.67), channel_id=1, source_target_pairs={{0,1},{1,0},{2,3},{3,2},{4,5},{5,4},{6,7},{7,6},{8,9},{9,8},{10,11... | collective-permute-start | bytes 331784 | tf_op jit(solution)/shard_map/ppermute | solution.py:177
  28.7 0.3 collective-permute-start.9
  29.0 2.7 %collective-permute-done.5 = bf16[2,216,128]{2,1,0:T(8,128)(2,1)S(1)} collective-permute-done((bf16[2,216,128]{2,1,0:T(8,128)(2,1)S(1)}, bf16[2,216,128]{2,1,0:T(8,128)(2,1)S(1)}, u32[]{:S(2)}, u32[]{:S(2)}) %collective-permute-start.5) | collective-permute-done | bytes 110624 | tf_op jit(solution)/shard_map/ppermute | solution.py:177
  31.7 0.3 collective-permute-start.6
  32.0 3.0 %collective-permute-done.9 = bf16[2,440,128]{2,1,0:T(8,128)(2,1)S(1)} collective-permute-done((bf16[2,440,128]{2,1,0:T(8,128)(2,1)S(1)}, bf16[2,440,128]{2,1,0:T(8,128)(2,1)S(1)}, u32[]{:S(2)}, u32[]{:S(2)}) %collective-permute-start.9) | collective-permute-done | bytes 225312 | tf_op jit(solution)/shard_map/ppermute | solution.py:177
  35.2 0.4 collective-permute-start.10
  35.6 0.7 %collective-permute-done.6 = bf16[216,128]{1,0:T(8,128)(2,1)S(1)} collective-permute-done((bf16[216,128]{1,0:T(8,128)(2,1)S(1)}, bf16[216,128]{1,0:T(8,128)(2,1)S(1)}, u32[]{:S(2)}, u32[]{:S(2)}) %collective-permute-start.6) | collective-permute-done | bytes 55328 | tf_op jit(solution)/shard_map/ppermute | solution.py:177
  36.3 3.0 %collective-permute-start.7 = (bf16[216,128]{1,0:T(8,128)(2,1)S(1)}, bf16[216,128]{1,0:T(8,128)(2,1)S(1)}, u32[]{:S(2)}, u32[]{:S(2)}) collective-permute-start(bf16[216,128]{1,0:T(8,128)(2,1)S(1)} %fusion.68), channel_id=1, source_target_pairs={{0,8},{4,12},{8,0},{12,4},{16,24},{20,28},{24,16},{28,20},{1,9},{5... | collective-permute-start | bytes 165896 | tf_op jit(solution)/shard_map/ppermute | solution.py:177
  39.3 2.6 %collective-permute-start.11 = (bf16[440,128]{1,0:T(8,128)(2,1)S(1)}, bf16[440,128]{1,0:T(8,128)(2,1)S(1)}, u32[]{:S(2)}, u32[]{:S(2)}) collective-permute-start(bf16[440,128]{1,0:T(8,128)(2,1)S(1)} %fusion.47), channel_id=1, source_target_pairs={{0,8},{4,12},{8,0},{12,4},{16,24},{20,28},{24,16},{28,20},{1,9},{5... | collective-permute-start | bytes 337928 | tf_op jit(solution)/shard_map/ppermute | solution.py:177
  41.9 2.4 %collective-permute-start.8 = (bf16[216,128]{1,0:T(8,128)(2,1)S(1)}, bf16[216,128]{1,0:T(8,128)(2,1)S(1)}, u32[]{:S(2)}, u32[]{:S(2)}) collective-permute-start(bf16[216,128]{1,0:T(8,128)(2,1)S(1)} %add_convert_fusion.5), channel_id=1, source_target_pairs={{0,16},{4,20},{8,24},{12,28},{16,0},{20,4},{24,8},{28,12},{1,17},{... | collective-permute-start | bytes 165896 | tf_op jit(solution)/shard_map/ppermute | solution.py:177
  44.3 2.3 %collective-permute-start.12 = (bf16[440,128]{1,0:T(8,128)(2,1)S(1)}, bf16[440,128]{1,0:T(8,128)(2,1)S(1)}, u32[]{:S(2)}, u32[]{:S(2)}) collective-permute-start(bf16[440,128]{1,0:T(8,128)(2,1)S(1)} %add_convert_fusion.3), channel_id=1, source_target_pairs={{0,16},{4,20},{8,24},{12,28},{16,0},{20,4},{24,8},{28,12},{1,17},{... | collective-permute-start | bytes 337928 | tf_op jit(solution)/shard_map/ppermute | solution.py:177
  46.6 3.1 %collective-permute-done.12 = bf16[440,128]{1,0:T(8,128)(2,1)S(1)} collective-permute-done((bf16[440,128]{1,0:T(8,128)(2,1)S(1)}, bf16[440,128]{1,0:T(8,128)(2,1)S(1)}, u32[]{:S(2)}, u32[]{:S(2)}) %collective-permute-start.12) | collective-permute-done | bytes 112672 | tf_op jit(solution)/shard_map/ppermute | solution.py:177
  49.8 6.0 %collective-permute-start.13 = (bf16[656,128]{1,0:T(8,128)(2,1)S(1)}, bf16[656,128]{1,0:T(8,128)(2,1)S(1)}, u32[]{:S(2)}, u32[]{:S(2)}) collective-permute-start(bf16[656,128]{1,0:T(8,128)(2,1)S(1)} %pad_maximum_fusion.3), channel_id=1, source_target_pairs={{0,4},{4,0},{8,12},{12,8},{16,20},{20,16},{24,28},{28,24},{1,5},{5... | collective-permute-start | bytes 503816 | tf_op jit(solution)/shard_map/ppermute | solution.py:177
  55.8 1.1 %convolution_convert_fusion = bf16[32,16,128]{2,1,0:T(8,128)(2,1)} fusion(bf16[32,16,1152]{2,1,0:T(8,128)(2,1)S(1)} %copy-done.3, bf16[1152,128,1]{1,0,2:T(8,128)(2,1)S(1)} %bitcast.222), kind=kOutput, calls=%fused_computation.7 | convolution fusion | flops 151060480 | bytes 1605632 | tf_op jit(solution)/shard_map/rck,kn->rcn/dot_general | solution.py:138
  57.1 0.8 %slice.411 = f32[1024,128]{1,0:T(8,128)} slice(f32[1312,128]{1,0:T(8,128)S(1)} %convert_multiply_fusion), slice={[0:1024], [0:128]} | slice | bytes 1048576 | tf_op jit(solution)/shard_map/slice | solution.py:170
  57.9 0.7 %slice.412 = f32[288,128]{1,0:T(8,128)} slice(f32[1312,128]{1,0:T(8,128)S(1)} %convert_multiply_fusion), slice={[1024:1312], [0:128]} | slice | bytes 294912 | tf_op jit(solution)/shard_map/slice | solution.py:171
  (108 shorter events, 2.3 us)
Async XLA Ops:
  0.6 17.6 %copy-start = (bf16[3,3,128,128]{3,2,1,0:T(8,128)(2,1)S(1)}, bf16[3,3,128,128]{3,2,1,0:T(8,128)(2,1)}, u32[]{:S(2)}) copy-start(bf16[3,3,128,128]{3,2,1,0:T(8,128)(2,1)} %param.10) | copy-start | bytes 884740
  0.6 2.3 %copy-start.5 = (s32[16,8,256]{2,1,0:T(8,128)S(1)}, s32[16,8,256]{2,1,0:T(8,128)}, u32[]{:S(2)}) copy-start(s32[16,8,256]{2,1,0:T(8,128)} %param.6) | copy-start | bytes 393220
  0.7 5.1 %copy-start.1 = (bf16[4,4,256,128]{3,2,1,0:T(8,128)(2,1)S(1)}, bf16[4,4,256,128]{3,2,1,0:T(8,128)(2,1)}, u32[]{:S(2)}) copy-start(bf16[4,4,256,128]{3,2,1,0:T(8,128)(2,1)} %param.8) | copy-start | bytes 3145732
  3.2 4.0 %copy-start.4 = (bf16[32,16,128]{2,1,0:T(8,128)(2,1)S(1)}, bf16[32,16,128]{2,1,0:T(8,128)(2,1)}, u32[]{:S(2)}) copy-start(bf16[32,16,128]{2,1,0:T(8,128)(2,1)} %param.11) | copy-start | bytes 393220
  3.3 3.6 %collective-permute-start.1 = (bf16[12288]{0:T(1024)(128)(2,1)S(1)}, bf16[12288]{0:T(1024)(128)(2,1)S(1)}, u32[]{:S(2)}, u32[]{:S(2)}) collective-permute-start(bf16[12288]{0:T(1024)(128)(2,1)S(1)} %pad_maximum_fusion.6), channel_id=1, source_target_pairs={{1,0},{2,1},{3,2},{0,3},{5,4},{6,5},{7,6},{4,7},{9,8},{10,9},{11,1... | collective-permute-start | bytes 73736 | tf_op jit(solution)/shard_map/ppermute | solution.py:26
  3.4 3.9 %collective-permute-start = (bf16[12288]{0:T(1024)(128)(2,1)S(1)}, bf16[12288]{0:T(1024)(128)(2,1)S(1)}, u32[]{:S(2)}, u32[]{:S(2)}) collective-permute-start(bf16[12288]{0:T(1024)(128)(2,1)S(1)} %pad_maximum_fusion.5), channel_id=1, source_target_pairs={{0,1},{1,2},{2,3},{3,0},{4,5},{5,6},{6,7},{7,4},{8,9},{9,10},{10,1... | collective-permute-start | bytes 73736 | tf_op jit(solution)/shard_map/ppermute | solution.py:25
  7.4 6.9 %collective-permute-start.2 = (bf16[7680]{0:T(1024)(128)(2,1)S(1)}, bf16[7680]{0:T(1024)(128)(2,1)S(1)}, u32[]{:S(2)}, u32[]{:S(2)}) collective-permute-start(bf16[7680]{0:T(1024)(128)(2,1)S(1)} %pad_maximum_fusion.7), channel_id=1, source_target_pairs={{4,0},{8,4},{12,8},{16,12},{20,16},{24,20},{28,24},{5,1},{9,5},{13... | collective-permute-start | bytes 46088 | tf_op jit(solution)/shard_map/ppermute | solution.py:26
  11.2 4.0 %collective-permute-start.3 = (bf16[7680]{0:T(1024)(128)(2,1)S(1)}, bf16[7680]{0:T(1024)(128)(2,1)S(1)}, u32[]{:S(2)}, u32[]{:S(2)}) collective-permute-start(bf16[7680]{0:T(1024)(128)(2,1)S(1)} %pad_maximum_fusion.8), channel_id=1, source_target_pairs={{0,4},{4,8},{8,12},{12,16},{16,20},{20,24},{24,28},{1,5},{5,9},{9,... | collective-permute-start | bytes 46088 | tf_op jit(solution)/shard_map/ppermute | solution.py:25
  16.5 0.7 %copy-start.6 = (f32[128]{0:T(128)S(1)}, f32[128]{0:T(128)}, u32[]{:S(2)}) copy-start(f32[128]{0:T(128)} %param.9) | copy-start | bytes 1540
  17.8 0.7 %copy-start.7 = (pred[8,3]{0,1:T(4,128)(4,1)S(1)}, pred[8,3]{0,1:T(4,128)(4,1)}, u32[]{:S(2)}) copy-start(pred[8,3]{0,1:T(4,128)(4,1)} %constant.179) | copy-start | bytes 76
  17.9 2.1 %copy-start.2 = (bf16[32,16,1152]{2,1,0:T(8,128)(2,1)}, bf16[32,16,1152]{2,1,0:T(8,128)(2,1)S(1)}, u32[]{:S(2)}) copy-start(bf16[32,16,1152]{2,1,0:T(8,128)(2,1)S(1)} %slice_dynamic-update-slice_fusion) | copy-start | bytes 3538948
  22.3 2.5 %collective-permute-start.4 = (bf16[4,656,128]{2,1,0:T(8,128)(2,1)}, bf16[4,656,128]{2,1,0:T(8,128)(2,1)}, u32[]{:S(2)}, u32[]{:S(2)}) collective-permute-start(bf16[4,656,128]{2,1,0:T(8,128)(2,1)} %fusion.4), channel_id=1, source_target_pairs={{0,4},{4,0},{8,12},{12,8},{16,20},{20,16},{24,28},{28,24},{1,5},{5... | collective-permute-start | bytes 2015240 | tf_op jit(solution)/shard_map/ppermute | solution.py:177
  26.1 5.6 %collective-permute-start.5 = (bf16[2,216,128]{2,1,0:T(8,128)(2,1)S(1)}, bf16[2,216,128]{2,1,0:T(8,128)(2,1)S(1)}, u32[]{:S(2)}, u32[]{:S(2)}) collective-permute-start(bf16[2,216,128]{2,1,0:T(8,128)(2,1)S(1)} %fusion.67), channel_id=1, source_target_pairs={{0,1},{1,0},{2,3},{3,2},{4,5},{5,4},{6,7},{7,6},{8,9},{9,8},{10,11... | collective-permute-start | bytes 331784 | tf_op jit(solution)/shard_map/ppermute | solution.py:177
  28.7 6.4 %collective-permute-start.9 = (bf16[2,440,128]{2,1,0:T(8,128)(2,1)S(1)}, bf16[2,440,128]{2,1,0:T(8,128)(2,1)S(1)}, u32[]{:S(2)}, u32[]{:S(2)}) collective-permute-start(bf16[2,440,128]{2,1,0:T(8,128)(2,1)S(1)} %fusion.46), channel_id=1, source_target_pairs={{0,2},{1,3},{2,0},{3,1},{4,6},{5,7},{6,4},{7,5},{8,10},{9,11},{10,... | collective-permute-start | bytes 675848 | tf_op jit(solution)/shard_map/ppermute | solution.py:177
  31.7 4.5 %collective-permute-start.6 = (bf16[216,128]{1,0:T(8,128)(2,1)S(1)}, bf16[216,128]{1,0:T(8,128)(2,1)S(1)}, u32[]{:S(2)}, u32[]{:S(2)}) collective-permute-start(bf16[216,128]{1,0:T(8,128)(2,1)S(1)} %fusion.71), channel_id=1, source_target_pairs={{0,2},{1,3},{2,0},{3,1},{4,6},{5,7},{6,4},{7,5},{8,10},{9,11},{10,... | collective-permute-start | bytes 165896 | tf_op jit(solution)/shard_map/ppermute | solution.py:177
  35.1 20.7 %copy-start.3 = (bf16[32,16,1152]{2,1,0:T(8,128)(2,1)S(1)}, bf16[32,16,1152]{2,1,0:T(8,128)(2,1)}, u32[]{:S(2)}) copy-start(bf16[32,16,1152]{2,1,0:T(8,128)(2,1)} %copy-done.2) | copy-start | bytes 3538948
  35.2 4.1 %collective-permute-start.10 = (bf16[440,128]{1,0:T(8,128)(2,1)S(1)}, bf16[440,128]{1,0:T(8,128)(2,1)S(1)}, u32[]{:S(2)}, u32[]{:S(2)}) collective-permute-start(bf16[440,128]{1,0:T(8,128)(2,1)S(1)} %fusion.66), channel_id=1, source_target_pairs={{0,1},{1,0},{2,3},{3,2},{4,5},{5,4},{6,7},{7,6},{8,9},{9,8},{10,11... | collective-permute-start | bytes 337928 | tf_op jit(solution)/shard_map/ppermute | solution.py:177
  36.3 5.6 %collective-permute-start.7 = (bf16[216,128]{1,0:T(8,128)(2,1)S(1)}, bf16[216,128]{1,0:T(8,128)(2,1)S(1)}, u32[]{:S(2)}, u32[]{:S(2)}) collective-permute-start(bf16[216,128]{1,0:T(8,128)(2,1)S(1)} %fusion.68), channel_id=1, source_target_pairs={{0,8},{4,12},{8,0},{12,4},{16,24},{20,28},{24,16},{28,20},{1,9},{5... | collective-permute-start | bytes 165896 | tf_op jit(solution)/shard_map/ppermute | solution.py:177
  39.3 5.0 %collective-permute-start.11 = (bf16[440,128]{1,0:T(8,128)(2,1)S(1)}, bf16[440,128]{1,0:T(8,128)(2,1)S(1)}, u32[]{:S(2)}, u32[]{:S(2)}) collective-permute-start(bf16[440,128]{1,0:T(8,128)(2,1)S(1)} %fusion.47), channel_id=1, source_target_pairs={{0,8},{4,12},{8,0},{12,4},{16,24},{20,28},{24,16},{28,20},{1,9},{5... | collective-permute-start | bytes 337928 | tf_op jit(solution)/shard_map/ppermute | solution.py:177
  41.9 4.7 %collective-permute-start.8 = (bf16[216,128]{1,0:T(8,128)(2,1)S(1)}, bf16[216,128]{1,0:T(8,128)(2,1)S(1)}, u32[]{:S(2)}, u32[]{:S(2)}) collective-permute-start(bf16[216,128]{1,0:T(8,128)(2,1)S(1)} %add_convert_fusion.5), channel_id=1, source_target_pairs={{0,16},{4,20},{8,24},{12,28},{16,0},{20,4},{24,8},{28,12},{1,17},{... | collective-permute-start | bytes 165896 | tf_op jit(solution)/shard_map/ppermute | solution.py:177
  44.3 5.4 %collective-permute-start.12 = (bf16[440,128]{1,0:T(8,128)(2,1)S(1)}, bf16[440,128]{1,0:T(8,128)(2,1)S(1)}, u32[]{:S(2)}, u32[]{:S(2)}) collective-permute-start(bf16[440,128]{1,0:T(8,128)(2,1)S(1)} %add_convert_fusion.3), channel_id=1, source_target_pairs={{0,16},{4,20},{8,24},{12,28},{16,0},{20,4},{24,8},{28,12},{1,17},{... | collective-permute-start | bytes 337928 | tf_op jit(solution)/shard_map/ppermute | solution.py:177
  49.8 7.2 %collective-permute-start.13 = (bf16[656,128]{1,0:T(8,128)(2,1)S(1)}, bf16[656,128]{1,0:T(8,128)(2,1)S(1)}, u32[]{:S(2)}, u32[]{:S(2)}) collective-permute-start(bf16[656,128]{1,0:T(8,128)(2,1)S(1)} %pad_maximum_fusion.3), channel_id=1, source_target_pairs={{0,4},{4,0},{8,12},{12,8},{16,20},{20,16},{24,28},{28,24},{1,5},{5... | collective-permute-start | bytes 503816 | tf_op jit(solution)/shard_map/ppermute | solution.py:177

commit v18 on v15

--- a/solution.py
+++ b/solution.py
@@ -223,10 +223,11 @@
 
 
 def butterfly(part, steps):
+    for step in steps:
+        part = halve(part.reshape((2, part.shape[0] // 2) + part.shape[1:]), "lat", step, 0)
     part = part.astype(jnp.bfloat16)
-    for step in steps:
-        got = exchange(part, "lat", step)
-        part = (part.astype(jnp.float32) + got.astype(jnp.float32)).astype(jnp.bfloat16)
+    for step in reversed(steps):
+        part = double(part, "lat", step)
     return part
 
 
@@ -234,7 +235,7 @@
     lon_count, count = rows.shape[:2]
     steps = steps_of(lon_count)
     lat_steps = steps_of(lax.axis_size("lat"))
-    if steps is None or lat_steps is None or count % 4:
+    if steps is None or lat_steps is None or count % (4 << len(lat_steps)):
         own = lax.axis_index("lon")
         mine = lax.dynamic_index_in_dim(lax.psum(rows, "lon"), own, 0, keepdims=False)
         return reduce_lat(mine)

time: 59 us -> 65.5 us (1.11)
  starting transfers between devices: 20.9 us -> 29.2 us
  waiting for transfers between devices: 20.6 us -> 18.5 us
    ppermute x10 -> x14, starting transfers between devices: 12.6 us -> 20.8 us  [exchange(): return lax.ppermute(part, axis, [(i, i ^ step) for i in range(size)])]
    ppermute x10 -> x14, waiting for transfers between devices: 15.3 us -> 13.2 us  [exchange(): return lax.ppermute(part, axis, [(i, i ^ step) for i in range(size)])]
    add x3 -> x7, other arithmetic: 1.28 us -> 1.33 us  [halve(): keep + exchange(send.astype(jnp.bfloat16), axis, step).astype(keep.dtype)]
  transfers between devices with their start and end apart: 14 -> 18, of which waited for: 11 -> 11; matrix products, arithmetic and copies ran while one was open for 5% -> 4% of each run, Pallas kernels for 0% -> 0%
where the time goes in v18:
time: 65.5 us; the launch traced here: 65.1 us
  starting transfers between devices  29.2 us (45%)
  waiting for transfers between devices  18.5 us (28%)
  local copies, waits for them, and re-layouts  7.93 us (12%)
  matrix products  4.4 us (7%)
  other arithmetic  3.57 us (5%)
  between operations  1.52 us (2%)
    ppermute x14, starting transfers between devices, exchange(): return lax.ppermute(part, axis, [(i, i ^ step) for i in range(size)])  20.8 us
    ppermute x14, waiting for transfers between devices, exchange(): return lax.ppermute(part, axis, [(i, i ^ step) for i in range(size)])  13.2 us
    ppermute x2, starting transfers between devices, swap_edges(): lax.ppermute(jnp.concatenate([p.reshape(-1) for p in leads]), axis, down)  5.24 us
    ppermute x2, waiting for transfers between devices, swap_edges(): lax.ppermute(jnp.concatenate([p.reshape(-1) for p in lasts]), axis, up)  4.02 us
    ppermute x2, starting transfers between devices, swap_edges(): lax.ppermute(jnp.concatenate([p.reshape(-1) for p in lasts]), axis, up)  3.09 us
    unnamed x45, local copies, waits for them, and re-layouts  1.67 us
    add x7, other arithmetic, halve(): keep + exchange(send.astype(jnp.bfloat16), axis, step).astype(keep.dtype)  1.33 us
  transfers between devices with their start and end apart: 18, of which 11 were waited for; matrix products, arithmetic and copies ran while one was open for 4% of the time, Pallas kernels for 0%

profile of v18, /device:TPU:0, one launch (start us, length us, event | category | flops | bytes accessed | tf_op | source)
XLA Modules:
  0.0 65.1 jit_solution(428086333955622119)
XLA Ops:
  0.7 1.0 %fusion.85 = (bf16[32,2,128]{2,1,0:T(2,128)(2,1)S(1)}, bf16[32,2,128]{2,1,0:T(2,128)(2,1)S(1)}) fusion(bf16[32,16,128]{2,1,0:T(8,128)(2,1)} %param.11), kind=kLoop, calls=%fused_computation.228 | loop fusion | bytes 65536 | tf_op jit(solution)/shard_map/slice | solution.py:23
  1.7 0.8 %multiply_exponential_fusion = f32[16,8,8]{0,2,1:T(8,128)S(1)} fusion(s32[16,8,8]{0,2,1:T(8,128)} %param.7), kind=kLoop, calls=%fused_computation.198 | loop fusion | flops 2048 | bytes 8192 | tf_op jit(solution)/shard_map/exp2 | solution.py:50
  2.5 0.2 broadcast_in_dim.21
  2.7 0.2 reshape.218
  2.9 0.3 fusion.63
  3.3 3.9 %collective-permute-start.1 = (bf16[12288]{0:T(1024)(128)(2,1)S(1)}, bf16[12288]{0:T(1024)(128)(2,1)S(1)}, u32[]{:S(2)}, u32[]{:S(2)}) collective-permute-start(bf16[12288]{0:T(1024)(128)(2,1)S(1)} %pad_maximum_fusion.8), channel_id=1, source_target_pairs={{1,0},{2,1},{3,2},{0,3},{5,4},{6,5},{7,6},{4,7},{9,8},{10,9},{11,1... | collective-permute-start | bytes 73736 | tf_op jit(solution)/shard_map/ppermute | solution.py:26
  7.5 1.3 %collective-permute-done.1 = bf16[12288]{0:T(1024)(128)(2,1)S(1)} collective-permute-done((bf16[12288]{0:T(1024)(128)(2,1)S(1)}, bf16[12288]{0:T(1024)(128)(2,1)S(1)}, u32[]{:S(2)}, u32[]{:S(2)}) %collective-permute-start.1) | collective-permute-done | bytes 24608 | tf_op jit(solution)/shard_map/ppermute | solution.py:26
  8.8 3.3 %collective-permute-done = bf16[12288]{0:T(1024)(128)(2,1)S(1)} collective-permute-done((bf16[12288]{0:T(1024)(128)(2,1)S(1)}, bf16[12288]{0:T(1024)(128)(2,1)S(1)}, u32[]{:S(2)}, u32[]{:S(2)}) %collective-permute-start) | collective-permute-done | bytes 24608 | tf_op jit(solution)/shard_map/ppermute | solution.py:25
  12.2 1.3 %collective-permute-start.2 = (bf16[7680]{0:T(1024)(128)(2,1)S(1)}, bf16[7680]{0:T(1024)(128)(2,1)S(1)}, u32[]{:S(2)}, u32[]{:S(2)}) collective-permute-start(bf16[7680]{0:T(1024)(128)(2,1)S(1)} %pad_maximum_fusion.9), channel_id=1, source_target_pairs={{4,0},{8,4},{12,8},{16,12},{20,16},{24,20},{28,24},{5,1},{9,5},{13... | collective-permute-start | bytes 46088 | tf_op jit(solution)/shard_map/ppermute | solution.py:26
  13.6 3.0 %collective-permute-start.3 = (bf16[7680]{0:T(1024)(128)(2,1)S(1)}, bf16[7680]{0:T(1024)(128)(2,1)S(1)}, u32[]{:S(2)}, u32[]{:S(2)}) collective-permute-start(bf16[7680]{0:T(1024)(128)(2,1)S(1)} %pad_maximum_fusion.10), channel_id=1, source_target_pairs={{0,4},{4,8},{8,12},{12,16},{16,20},{20,24},{24,28},{1,5},{5,9},{9,... | collective-permute-start | bytes 46088 | tf_op jit(solution)/shard_map/ppermute | solution.py:25
  16.7 0.7 %collective-permute-done.3 = bf16[7680]{0:T(1024)(128)(2,1)S(1)} collective-permute-done((bf16[7680]{0:T(1024)(128)(2,1)S(1)}, bf16[7680]{0:T(1024)(128)(2,1)S(1)}, u32[]{:S(2)}, u32[]{:S(2)}) %collective-permute-start.3) | collective-permute-done | bytes 15392 | tf_op jit(solution)/shard_map/ppermute | solution.py:25
  17.6 0.3 convolution_bitcast_fusion
  17.9 0.3 convolution_bitcast_fusion.1
  18.2 0.3 convolution_bitcast_fusion.2
  18.5 0.3 convolution_bitcast_fusion.3
  19.0 0.2 reshape.269
  19.2 0.2 copy-done.7
  20.5 0.2 copy-done.8
  20.7 0.7 %convolution_select_fusion = f32[34,8,3,128]{3,1,2,0:T(8,128)S(1)} fusion(bf16[3,3,128,128]{3,2,1,0:T(8,128)(2,1)S(1)} %copy-done, bf16[36,1,7,2,128]{4,2,3,0,1:T(8,128)(2,1)S(1)} %slice.391, bf16[36,1,8,3,128]{4,2,3,0,1:T(8,128)(2,1)S(1)} %copy.29, pred[8,3]{0,1:T(4,128)(4,1)S(1)} %copy-done.8), kind=kOutput, calls=%fused_computation.3 | convolution fusion | flops 241858560 | bytes 1062936 | tf_op jit(solution)/shard_map/conv_general_dilated | solution.py:126
  21.7 0.2 broadcast_select_fusion
  22.2 0.5 fusion
  22.8 0.5 fusion.68
  23.6 1.0 %fusion.4 = bf16[4,656,128]{2,1,0:T(8,128)(2,1)} fusion(f32[4,2,656,128]{3,2,1,0:T(8,128)S(1)} %bitcast.240, s32[]{:T(128)S(6)} %select_n.204), kind=kLoop, calls=%fused_computation.14 | loop fusion | bytes 1343492 | tf_op jit(solution)/shard_map/convert_element_type | solution.py:184
  24.6 1.2 %collective-permute-start.4 = (bf16[4,656,128]{2,1,0:T(8,128)(2,1)}, bf16[4,656,128]{2,1,0:T(8,128)(2,1)}, u32[]{:S(2)}, u32[]{:S(2)}) collective-permute-start(bf16[4,656,128]{2,1,0:T(8,128)(2,1)} %fusion.4), channel_id=1, source_target_pairs={{0,4},{4,0},{8,12},{12,8},{16,20},{20,16},{24,28},{28,24},{1,5},{5... | collective-permute-start | bytes 2015240 | tf_op jit(solution)/shard_map/ppermute | solution.py:177
  25.8 2.1 %collective-permute-done.4 = bf16[4,656,128]{2,1,0:T(8,128)(2,1)} collective-permute-done((bf16[4,656,128]{2,1,0:T(8,128)(2,1)}, bf16[4,656,128]{2,1,0:T(8,128)(2,1)}, u32[]{:S(2)}, u32[]{:S(2)}) %collective-permute-start.4) | collective-permute-done | bytes 671776 | tf_op jit(solution)/shard_map/ppermute | solution.py:177
  27.9 1.2 %bitcast_add_fusion = f32[4,656,128]{2,1,0:T(8,128)S(1)} fusion(bf16[4,656,128]{2,1,0:T(8,128)(2,1)} %collective-permute-done.4, f32[4,2,656,128]{3,2,1,0:T(8,128)S(1)} %bitcast.241, s32[]{:T(128)S(6)} %select_n.203), kind=kLoop, calls=%fused_computation.1 | loop fusion | flops 671744 | bytes 3358724 | tf_op jit(solution)/shard_map/add | solution.py:184
  29.2 0.6 collective-permute-start.11
  29.8 0.5 copy-done.2
  30.3 0.5 fusion.88
  30.8 0.7 %copy.61 = f32[16,8,256,1]{2,1,0,3:T(8,128)} copy(f32[16,8,256,1]{2,0,1,3:T(8,128)S(1)} %fusion.88) | data formatting | bytes 262144 | tf_op jit(solution)/shard_map/rctn,tmn->rcm/dot_general | solution.py:150
  31.6 4.3 %collective-permute-done.11 = bf16[2,328,128]{2,1,0:T(8,128)(2,1)S(1)} collective-permute-done((bf16[2,328,128]{2,1,0:T(8,128)(2,1)S(1)}, bf16[2,328,128]{2,1,0:T(8,128)(2,1)S(1)}, u32[]{:S(2)}, u32[]{:S(2)}) %collective-permute-start.11) | collective-permute-done | bytes 167968 | tf_op jit(solution)/shard_map/ppermute | solution.py:177
  36.1 2.2 %collective-permute-done.5 = bf16[2,328,128]{2,1,0:T(8,128)(2,1)S(1)} collective-permute-done((bf16[2,328,128]{2,1,0:T(8,128)(2,1)S(1)}, bf16[2,328,128]{2,1,0:T(8,128)(2,1)S(1)}, u32[]{:S(2)}, u32[]{:S(2)}) %collective-permute-start.5) | collective-permute-done | bytes 167968 | tf_op jit(solution)/shard_map/ppermute | solution.py:177
  38.3 0.9 %collective-permute-start.6 = (bf16[328,128]{1,0:T(8,128)(2,1)S(1)}, bf16[328,128]{1,0:T(8,128)(2,1)S(1)}, u32[]{:S(2)}, u32[]{:S(2)}) collective-permute-start(bf16[328,128]{1,0:T(8,128)(2,1)S(1)} %fusion.66), channel_id=1, source_target_pairs={{0,2},{1,3},{2,0},{3,1},{4,6},{5,7},{6,4},{7,5},{8,10},{9,11},{10,... | collective-permute-start | bytes 251912 | tf_op jit(solution)/shard_map/ppermute | solution.py:177
  39.2 1.3 %collective-permute-done.12 = bf16[328,128]{1,0:T(8,128)(2,1)S(1)} collective-permute-done((bf16[328,128]{1,0:T(8,128)(2,1)S(1)}, bf16[328,128]{1,0:T(8,128)(2,1)S(1)}, u32[]{:S(2)}, u32[]{:S(2)}) %collective-permute-start.12) | collective-permute-done | bytes 84000 | tf_op jit(solution)/shard_map/ppermute | solution.py:177
  40.6 2.4 %collective-permute-start.13 = (bf16[164,128]{1,0:T(8,128)(2,1)S(1)}, bf16[164,128]{1,0:T(8,128)(2,1)S(1)}, u32[]{:S(2)}, u32[]{:S(2)}) collective-permute-start(bf16[164,128]{1,0:T(8,128)(2,1)S(1)} %fusion.73), channel_id=1, source_target_pairs={{0,8},{4,12},{8,0},{12,4},{16,24},{20,28},{24,16},{28,20},{1,9},{5... | collective-permute-start | bytes 125960 | tf_op jit(solution)/shard_map/ppermute | solution.py:177
  43.0 2.4 %collective-permute-start.7 = (bf16[164,128]{1,0:T(8,128)(2,1)S(1)}, bf16[164,128]{1,0:T(8,128)(2,1)S(1)}, u32[]{:S(2)}, u32[]{:S(2)}) collective-permute-start(bf16[164,128]{1,0:T(8,128)(2,1)S(1)} %fusion.72), channel_id=1, source_target_pairs={{0,8},{4,12},{8,0},{12,4},{16,24},{20,28},{24,16},{28,20},{1,9},{5... | collective-permute-start | bytes 125960 | tf_op jit(solution)/shard_map/ppermute | solution.py:177
  45.5 2.7 %collective-permute-start.14 = (bf16[82,128]{1,0:T(8,128)(2,1)S(1)}, bf16[82,128]{1,0:T(8,128)(2,1)S(1)}, u32[]{:S(2)}, u32[]{:S(2)}) collective-permute-start(bf16[82,128]{1,0:T(8,128)(2,1)S(1)} %fusion.75), channel_id=1, source_target_pairs={{0,16},{4,20},{8,24},{12,28},{16,0},{20,4},{24,8},{28,12},{1,17},{... | collective-permute-start | bytes 62984 | tf_op jit(solution)/shard_map/ppermute | solution.py:177
  48.2 2.4 %collective-permute-start.8 = (bf16[82,128]{1,0:T(8,128)(2,1)S(1)}, bf16[82,128]{1,0:T(8,128)(2,1)S(1)}, u32[]{:S(2)}, u32[]{:S(2)}) collective-permute-start(bf16[82,128]{1,0:T(8,128)(2,1)S(1)} %fusion.74), channel_id=1, source_target_pairs={{0,16},{4,20},{8,24},{12,28},{16,0},{20,4},{24,8},{28,12},{1,17},{... | collective-permute-start | bytes 62984 | tf_op jit(solution)/shard_map/ppermute | solution.py:177
  50.6 2.3 %collective-permute-start.15 = (bf16[82,128]{1,0:T(8,128)(2,1)S(1)}, bf16[82,128]{1,0:T(8,128)(2,1)S(1)}, u32[]{:S(2)}, u32[]{:S(2)}) collective-permute-start(bf16[82,128]{1,0:T(8,128)(2,1)S(1)} %fusion.70), channel_id=1, source_target_pairs={{0,16},{4,20},{8,24},{12,28},{16,0},{20,4},{24,8},{28,12},{1,17},{... | collective-permute-start | bytes 62984 | tf_op jit(solution)/shard_map/ppermute | solution.py:177
  53.1 2.3 %collective-permute-start.9 = (bf16[82,128]{1,0:T(8,128)(2,1)S(1)}, bf16[82,128]{1,0:T(8,128)(2,1)S(1)}, u32[]{:S(2)}, u32[]{:S(2)}) collective-permute-start(bf16[82,128]{1,0:T(8,128)(2,1)S(1)} %fusion.71), channel_id=1, source_target_pairs={{0,16},{4,20},{8,24},{12,28},{16,0},{20,4},{24,8},{28,12},{1,17},{... | collective-permute-start | bytes 62984 | tf_op jit(solution)/shard_map/ppermute | solution.py:177
  55.4 1.8 %collective-permute-start.16 = (bf16[164,128]{1,0:T(8,128)(2,1)S(1)}, bf16[164,128]{1,0:T(8,128)(2,1)S(1)}, u32[]{:S(2)}, u32[]{:S(2)}) collective-permute-start(bf16[164,128]{1,0:T(8,128)(2,1)S(1)} %pad_maximum_fusion.6), channel_id=1, source_target_pairs={{0,8},{4,12},{8,0},{12,4},{16,24},{20,28},{24,16},{28,20},{1,9},{5... | collective-permute-start | bytes 125960 | tf_op jit(solution)/shard_map/ppermute | solution.py:177
  57.2 0.6 collective-permute-done.9
  57.9 1.7 %collective-permute-start.10 = (bf16[164,128]{1,0:T(8,128)(2,1)S(1)}, bf16[164,128]{1,0:T(8,128)(2,1)S(1)}, u32[]{:S(2)}, u32[]{:S(2)}) collective-permute-start(bf16[164,128]{1,0:T(8,128)(2,1)S(1)} %pad_maximum_fusion.5), channel_id=1, source_target_pairs={{0,8},{4,12},{8,0},{12,4},{16,24},{20,28},{24,16},{28,20},{1,9},{5... | collective-permute-start | bytes 125960 | tf_op jit(solution)/shard_map/ppermute | solution.py:177
  59.6 2.4 %collective-permute-done.10 = bf16[164,128]{1,0:T(8,128)(2,1)S(1)} collective-permute-done((bf16[164,128]{1,0:T(8,128)(2,1)S(1)}, bf16[164,128]{1,0:T(8,128)(2,1)S(1)}, u32[]{:S(2)}, u32[]{:S(2)}) %collective-permute-start.10) | collective-permute-done | bytes 42016 | tf_op jit(solution)/shard_map/ppermute | solution.py:177
  62.1 1.1 %convolution_convert_fusion = bf16[32,16,128]{2,1,0:T(8,128)(2,1)} fusion(bf16[32,16,1152]{2,1,0:T(8,128)(2,1)S(1)} %copy-done.4, bf16[1152,128,1]{1,0,2:T(8,128)(2,1)S(1)} %bitcast.238), kind=kOutput, calls=%fused_computation.7 | convolution fusion | flops 151060480 | bytes 1605632 | tf_op jit(solution)/shard_map/rck,kn->rcn/dot_general | solution.py:138
  63.3 0.2 collective-permute-done.17
  63.6 0.8 %slice.411 = f32[1024,128]{1,0:T(8,128)} slice(f32[1312,128]{1,0:T(8,128)S(1)} %convert_multiply_fusion), slice={[0:1024], [0:128]} | slice | bytes 1048576 | tf_op jit(solution)/shard_map/slice | solution.py:170
  64.5 0.7 %slice.412 = f32[288,128]{1,0:T(8,128)} slice(f32[1312,128]{1,0:T(8,128)S(1)} %convert_multiply_fusion), slice={[1024:1312], [0:128]} | slice | bytes 294912 | tf_op jit(solution)/shard_map/slice | solution.py:171
  (131 shorter events, 3.6 us)
Async XLA Ops:
  0.6 19.8 %copy-start = (bf16[3,3,128,128]{3,2,1,0:T(8,128)(2,1)S(1)}, bf16[3,3,128,128]{3,2,1,0:T(8,128)(2,1)}, u32[]{:S(2)}) copy-start(bf16[3,3,128,128]{3,2,1,0:T(8,128)(2,1)} %param.10) | copy-start | bytes 884740
  0.6 2.3 %copy-start.6 = (s32[16,8,256]{2,1,0:T(8,128)S(1)}, s32[16,8,256]{2,1,0:T(8,128)}, u32[]{:S(2)}) copy-start(s32[16,8,256]{2,1,0:T(8,128)} %param.6) | copy-start | bytes 393220
  0.7 6.7 %copy-start.1 = (bf16[4,4,256,128]{3,2,1,0:T(8,128)(2,1)S(1)}, bf16[4,4,256,128]{3,2,1,0:T(8,128)(2,1)}, u32[]{:S(2)}) copy-start(bf16[4,4,256,128]{3,2,1,0:T(8,128)(2,1)} %param.8) | copy-start | bytes 3145732
  3.2 8.8 %copy-start.5 = (bf16[32,16,128]{2,1,0:T(8,128)(2,1)S(1)}, bf16[32,16,128]{2,1,0:T(8,128)(2,1)}, u32[]{:S(2)}) copy-start(bf16[32,16,128]{2,1,0:T(8,128)(2,1)} %param.11) | copy-start | bytes 393220
  3.3 5.5 %collective-permute-start.1 = (bf16[12288]{0:T(1024)(128)(2,1)S(1)}, bf16[12288]{0:T(1024)(128)(2,1)S(1)}, u32[]{:S(2)}, u32[]{:S(2)}) collective-permute-start(bf16[12288]{0:T(1024)(128)(2,1)S(1)} %pad_maximum_fusion.8), channel_id=1, source_target_pairs={{1,0},{2,1},{3,2},{0,3},{5,4},{6,5},{7,6},{4,7},{9,8},{10,9},{11,1... | collective-permute-start | bytes 73736 | tf_op jit(solution)/shard_map/ppermute | solution.py:26
  7.3 4.8 %collective-permute-start = (bf16[12288]{0:T(1024)(128)(2,1)S(1)}, bf16[12288]{0:T(1024)(128)(2,1)S(1)}, u32[]{:S(2)}, u32[]{:S(2)}) collective-permute-start(bf16[12288]{0:T(1024)(128)(2,1)S(1)} %pad_maximum_fusion.7), channel_id=1, source_target_pairs={{0,1},{1,2},{2,3},{3,0},{4,5},{5,6},{6,7},{7,4},{8,9},{9,10},{10,1... | collective-permute-start | bytes 73736 | tf_op jit(solution)/shard_map/ppermute | solution.py:25
  12.2 4.4 %collective-permute-start.2 = (bf16[7680]{0:T(1024)(128)(2,1)S(1)}, bf16[7680]{0:T(1024)(128)(2,1)S(1)}, u32[]{:S(2)}, u32[]{:S(2)}) collective-permute-start(bf16[7680]{0:T(1024)(128)(2,1)S(1)} %pad_maximum_fusion.9), channel_id=1, source_target_pairs={{4,0},{8,4},{12,8},{16,12},{20,16},{24,20},{28,24},{5,1},{9,5},{13... | collective-permute-start | bytes 46088 | tf_op jit(solution)/shard_map/ppermute | solution.py:26
  13.6 3.9 %collective-permute-start.3 = (bf16[7680]{0:T(1024)(128)(2,1)S(1)}, bf16[7680]{0:T(1024)(128)(2,1)S(1)}, u32[]{:S(2)}, u32[]{:S(2)}) collective-permute-start(bf16[7680]{0:T(1024)(128)(2,1)S(1)} %pad_maximum_fusion.10), channel_id=1, source_target_pairs={{0,4},{4,8},{8,12},{12,16},{16,20},{20,24},{24,28},{1,5},{5,9},{9,... | collective-permute-start | bytes 46088 | tf_op jit(solution)/shard_map/ppermute | solution.py:25
  18.8 0.7 %copy-start.7 = (f32[128]{0:T(128)S(1)}, f32[128]{0:T(128)}, u32[]{:S(2)}) copy-start(f32[128]{0:T(128)} %param.9) | copy-start | bytes 1540
  20.1 0.7 %copy-start.8 = (pred[8,3]{0,1:T(4,128)(4,1)S(1)}, pred[8,3]{0,1:T(4,128)(4,1)}, u32[]{:S(2)}) copy-start(pred[8,3]{0,1:T(4,128)(4,1)} %constant.247) | copy-start | bytes 76
  20.1 2.1 %copy-start.3 = (bf16[32,16,1152]{2,1,0:T(8,128)(2,1)}, bf16[32,16,1152]{2,1,0:T(8,128)(2,1)S(1)}, u32[]{:S(2)}) copy-start(bf16[32,16,1152]{2,1,0:T(8,128)(2,1)S(1)} %slice_dynamic-update-slice_fusion) | copy-start | bytes 3538948
  24.6 3.3 %collective-permute-start.4 = (bf16[4,656,128]{2,1,0:T(8,128)(2,1)}, bf16[4,656,128]{2,1,0:T(8,128)(2,1)}, u32[]{:S(2)}, u32[]{:S(2)}) collective-permute-start(bf16[4,656,128]{2,1,0:T(8,128)(2,1)} %fusion.4), channel_id=1, source_target_pairs={{0,4},{4,0},{8,12},{12,8},{16,20},{20,16},{24,28},{28,24},{1,5},{5... | collective-permute-start | bytes 2015240 | tf_op jit(solution)/shard_map/ppermute | solution.py:177
  29.1 1.2 %copy-start.2 = (bf16[4,4,256,128]{3,2,1,0:T(8,128)(2,1)S(1)}, bf16[4,4,256,128]{3,2,1,0:T(8,128)(2,1)}, u32[]{:S(2)}) copy-start(bf16[4,4,256,128]{3,2,1,0:T(8,128)(2,1)} %param.8) | copy-start | bytes 3145732
  29.2 6.7 %collective-permute-start.11 = (bf16[2,328,128]{2,1,0:T(8,128)(2,1)S(1)}, bf16[2,328,128]{2,1,0:T(8,128)(2,1)S(1)}, u32[]{:S(2)}, u32[]{:S(2)}) collective-permute-start(bf16[2,328,128]{2,1,0:T(8,128)(2,1)S(1)} %fusion.49), channel_id=1, source_target_pairs={{0,2},{1,3},{2,0},{3,1},{4,6},{5,7},{6,4},{7,5},{8,10},{9,11},{10,... | collective-permute-start | bytes 503816 | tf_op jit(solution)/shard_map/ppermute | solution.py:177
  31.6 6.7 %collective-permute-start.5 = (bf16[2,328,128]{2,1,0:T(8,128)(2,1)S(1)}, bf16[2,328,128]{2,1,0:T(8,128)(2,1)S(1)}, u32[]{:S(2)}, u32[]{:S(2)}) collective-permute-start(bf16[2,328,128]{2,1,0:T(8,128)(2,1)S(1)} %fusion.48), channel_id=1, source_target_pairs={{0,1},{1,0},{2,3},{3,2},{4,5},{5,4},{6,7},{7,6},{8,9},{9,8},{10,11... | collective-permute-start | bytes 503816 | tf_op jit(solution)/shard_map/ppermute | solution.py:177
  36.0 4.5 %collective-permute-start.12 = (bf16[328,128]{1,0:T(8,128)(2,1)S(1)}, bf16[328,128]{1,0:T(8,128)(2,1)S(1)}, u32[]{:S(2)}, u32[]{:S(2)}) collective-permute-start(bf16[328,128]{1,0:T(8,128)(2,1)S(1)} %fusion.67), channel_id=1, source_target_pairs={{0,1},{1,0},{2,3},{3,2},{4,5},{5,4},{6,7},{7,6},{8,9},{9,8},{10,11... | collective-permute-start | bytes 251912 | tf_op jit(solution)/shard_map/ppermute | solution.py:177
  38.3 4.6 %collective-permute-start.6 = (bf16[328,128]{1,0:T(8,128)(2,1)S(1)}, bf16[328,128]{1,0:T(8,128)(2,1)S(1)}, u32[]{:S(2)}, u32[]{:S(2)}) collective-permute-start(bf16[328,128]{1,0:T(8,128)(2,1)S(1)} %fusion.66), channel_id=1, source_target_pairs={{0,2},{1,3},{2,0},{3,1},{4,6},{5,7},{6,4},{7,5},{8,10},{9,11},{10,... | collective-permute-start | bytes 251912 | tf_op jit(solution)/shard_map/ppermute | solution.py:177
  40.6 4.9 %collective-permute-start.13 = (bf16[164,128]{1,0:T(8,128)(2,1)S(1)}, bf16[164,128]{1,0:T(8,128)(2,1)S(1)}, u32[]{:S(2)}, u32[]{:S(2)}) collective-permute-start(bf16[164,128]{1,0:T(8,128)(2,1)S(1)} %fusion.73), channel_id=1, source_target_pairs={{0,8},{4,12},{8,0},{12,4},{16,24},{20,28},{24,16},{28,20},{1,9},{5... | collective-permute-start | bytes 125960 | tf_op jit(solution)/shard_map/ppermute | solution.py:177
  43.0 19.1 %copy-start.4 = (bf16[32,16,1152]{2,1,0:T(8,128)(2,1)S(1)}, bf16[32,16,1152]{2,1,0:T(8,128)(2,1)}, u32[]{:S(2)}) copy-start(bf16[32,16,1152]{2,1,0:T(8,128)(2,1)} %copy-done.3) | copy-start | bytes 3538948
  43.0 5.1 %collective-permute-start.7 = (bf16[164,128]{1,0:T(8,128)(2,1)S(1)}, bf16[164,128]{1,0:T(8,128)(2,1)S(1)}, u32[]{:S(2)}, u32[]{:S(2)}) collective-permute-start(bf16[164,128]{1,0:T(8,128)(2,1)S(1)} %fusion.72), channel_id=1, source_target_pairs={{0,8},{4,12},{8,0},{12,4},{16,24},{20,28},{24,16},{28,20},{1,9},{5... | collective-permute-start | bytes 125960 | tf_op jit(solution)/shard_map/ppermute | solution.py:177
  45.5 5.1 %collective-permute-start.14 = (bf16[82,128]{1,0:T(8,128)(2,1)S(1)}, bf16[82,128]{1,0:T(8,128)(2,1)S(1)}, u32[]{:S(2)}, u32[]{:S(2)}) collective-permute-start(bf16[82,128]{1,0:T(8,128)(2,1)S(1)} %fusion.75), channel_id=1, source_target_pairs={{0,16},{4,20},{8,24},{12,28},{16,0},{20,4},{24,8},{28,12},{1,17},{... | collective-permute-start | bytes 62984 | tf_op jit(solution)/shard_map/ppermute | solution.py:177
  48.2 4.8 %collective-permute-start.8 = (bf16[82,128]{1,0:T(8,128)(2,1)S(1)}, bf16[82,128]{1,0:T(8,128)(2,1)S(1)}, u32[]{:S(2)}, u32[]{:S(2)}) collective-permute-start(bf16[82,128]{1,0:T(8,128)(2,1)S(1)} %fusion.74), channel_id=1, source_target_pairs={{0,16},{4,20},{8,24},{12,28},{16,0},{20,4},{24,8},{28,12},{1,17},{... | collective-permute-start | bytes 62984 | tf_op jit(solution)/shard_map/ppermute | solution.py:177
  50.6 4.8 %collective-permute-start.15 = (bf16[82,128]{1,0:T(8,128)(2,1)S(1)}, bf16[82,128]{1,0:T(8,128)(2,1)S(1)}, u32[]{:S(2)}, u32[]{:S(2)}) collective-permute-start(bf16[82,128]{1,0:T(8,128)(2,1)S(1)} %fusion.70), channel_id=1, source_target_pairs={{0,16},{4,20},{8,24},{12,28},{16,0},{20,4},{24,8},{28,12},{1,17},{... | collective-permute-start | bytes 62984 | tf_op jit(solution)/shard_map/ppermute | solution.py:177
  53.1 4.8 %collective-permute-start.9 = (bf16[82,128]{1,0:T(8,128)(2,1)S(1)}, bf16[82,128]{1,0:T(8,128)(2,1)S(1)}, u32[]{:S(2)}, u32[]{:S(2)}) collective-permute-start(bf16[82,128]{1,0:T(8,128)(2,1)S(1)} %fusion.71), channel_id=1, source_target_pairs={{0,16},{4,20},{8,24},{12,28},{16,0},{20,4},{24,8},{28,12},{1,17},{... | collective-permute-start | bytes 62984 | tf_op jit(solution)/shard_map/ppermute | solution.py:177
  55.4 4.1 %collective-permute-start.16 = (bf16[164,128]{1,0:T(8,128)(2,1)S(1)}, bf16[164,128]{1,0:T(8,128)(2,1)S(1)}, u32[]{:S(2)}, u32[]{:S(2)}) collective-permute-start(bf16[164,128]{1,0:T(8,128)(2,1)S(1)} %pad_maximum_fusion.6), channel_id=1, source_target_pairs={{0,8},{4,12},{8,0},{12,4},{16,24},{20,28},{24,16},{28,20},{1,9},{5... | collective-permute-start | bytes 125960 | tf_op jit(solution)/shard_map/ppermute | solution.py:177
  57.9 4.1 %collective-permute-start.10 = (bf16[164,128]{1,0:T(8,128)(2,1)S(1)}, bf16[164,128]{1,0:T(8,128)(2,1)S(1)}, u32[]{:S(2)}, u32[]{:S(2)}) collective-permute-start(bf16[164,128]{1,0:T(8,128)(2,1)S(1)} %pad_maximum_fusion.5), channel_id=1, source_target_pairs={{0,8},{4,12},{8,0},{12,4},{16,24},{20,28},{24,16},{28,20},{1,9},{5... | collective-permute-start | bytes 125960 | tf_op jit(solution)/shard_map/ppermute | solution.py:177
  62.0 1.5 %collective-permute-start.17 = (bf16[656,128]{1,0:T(8,128)(2,1)S(1)}, bf16[656,128]{1,0:T(8,128)(2,1)S(1)}, u32[]{:S(2)}, u32[]{:S(2)}) collective-permute-start(bf16[656,128]{1,0:T(8,128)(2,1)S(1)} %pad_maximum_fusion.3), channel_id=1, source_target_pairs={{0,4},{4,0},{8,12},{12,8},{16,20},{20,16},{24,28},{28,24},{1,5},{5... | collective-permute-start | bytes 503816 | tf_op jit(solution)/shard_map/ppermute | solution.py:177

commit v19 on v15

--- a/solution.py
+++ b/solution.py
@@ -47,8 +47,9 @@
         1.0 + mantissa.astype(jnp.float32) / 8.0
     )
     signed = jnp.where(sign_bit == 1, -magnitude, magnitude)
-    factor = jnp.repeat(jnp.exp2(block_exps.astype(jnp.float32)), BLOCK, axis=2)
-    return (signed * factor).astype(jnp.bfloat16)
+    factor = jnp.exp2(block_exps.astype(jnp.float32))[..., None]
+    blocks = signed.reshape(block_exps.shape + (BLOCK,))
+    return (blocks * factor).reshape(signed.shape).astype(jnp.bfloat16)
 
 
 def slope(pre_act):

time: 59 us -> 59 us (level)
  no operation moved by 1% of the time
where the time goes in v19:
time: 59 us; the launch traced here: 58.7 us
  starting transfers between devices  20.9 us (35%)
  waiting for transfers between devices  20.6 us (35%)
  local copies, waits for them, and re-layouts  7.81 us (13%)
  matrix products  4.4 us (7%)
  other arithmetic  3.51 us (6%)
  between operations  1.42 us (2%)
    ppermute x10, waiting for transfers between devices, exchange(): return lax.ppermute(part, axis, [(i, i ^ step) for i in range(size)])  15.3 us
    ppermute x10, starting transfers between devices, exchange(): return lax.ppermute(part, axis, [(i, i ^ step) for i in range(size)])  12.6 us
    ppermute x2, starting transfers between devices, swap_edges(): lax.ppermute(jnp.concatenate([p.reshape(-1) for p in leads]), axis, down)  5.24 us
    ppermute x2, waiting for transfers between devices, swap_edges(): lax.ppermute(jnp.concatenate([p.reshape(-1) for p in lasts]), axis, up)  4.02 us
    ppermute x2, starting transfers between devices, swap_edges(): lax.ppermute(jnp.concatenate([p.reshape(-1) for p in lasts]), axis, up)  3.09 us
    unnamed x45, local copies, waits for them, and re-layouts  1.67 us
    ppermute x2, waiting for transfers between devices, swap_edges(): lax.ppermute(jnp.concatenate([p.reshape(-1) for p in leads]), axis, down)  1.3 us
    add x3, other arithmetic, halve(): keep + exchange(send.astype(jnp.bfloat16), axis, step).astype(keep.dtype)  1.28 us
  transfers between devices with their start and end apart: 14, of which 11 were waited for; matrix products, arithmetic and copies ran while one was open for 5% of the time, Pallas kernels for 0%

profile of v19, /device:TPU:0, one launch (start us, length us, event | category | flops | bytes accessed | tf_op | source)
XLA Modules:
  0.0 58.7 jit_solution(11815713261334060847)
XLA Ops:
  0.7 1.0 %fusion.81 = (bf16[32,2,128]{2,1,0:T(2,128)(2,1)S(1)}, bf16[32,2,128]{2,1,0:T(2,128)(2,1)S(1)}) fusion(bf16[32,16,128]{2,1,0:T(8,128)(2,1)} %param.11), kind=kLoop, calls=%fused_computation.210 | loop fusion | bytes 65536 | tf_op jit(solution)/shard_map/slice | solution.py:23
  1.7 0.8 %multiply_exponential_fusion = f32[16,8,8]{0,2,1:T(8,128)S(1)} fusion(s32[16,8,8]{0,2,1:T(8,128)} %param.7), kind=kLoop, calls=%fused_computation.186 | loop fusion | flops 2048 | bytes 8192 | tf_op jit(solution)/shard_map/exp2 | solution.py:50
  2.5 0.2 mul.41
  2.7 0.2 mul.42
  2.9 0.3 fusion.65
  3.3 3.9 %collective-permute-start.1 = (bf16[12288]{0:T(1024)(128)(2,1)S(1)}, bf16[12288]{0:T(1024)(128)(2,1)S(1)}, u32[]{:S(2)}, u32[]{:S(2)}) collective-permute-start(bf16[12288]{0:T(1024)(128)(2,1)S(1)} %pad_maximum_fusion.6), channel_id=1, source_target_pairs={{1,0},{2,1},{3,2},{0,3},{5,4},{6,5},{7,6},{4,7},{9,8},{10,9},{11,1... | collective-permute-start | bytes 73736 | tf_op jit(solution)/shard_map/ppermute | solution.py:26
  7.5 1.3 %collective-permute-done.1 = bf16[12288]{0:T(1024)(128)(2,1)S(1)} collective-permute-done((bf16[12288]{0:T(1024)(128)(2,1)S(1)}, bf16[12288]{0:T(1024)(128)(2,1)S(1)}, u32[]{:S(2)}, u32[]{:S(2)}) %collective-permute-start.1) | collective-permute-done | bytes 24608 | tf_op jit(solution)/shard_map/ppermute | solution.py:26
  8.8 3.3 %collective-permute-done = bf16[12288]{0:T(1024)(128)(2,1)S(1)} collective-permute-done((bf16[12288]{0:T(1024)(128)(2,1)S(1)}, bf16[12288]{0:T(1024)(128)(2,1)S(1)}, u32[]{:S(2)}, u32[]{:S(2)}) %collective-permute-start) | collective-permute-done | bytes 24608 | tf_op jit(solution)/shard_map/ppermute | solution.py:25
  12.2 1.3 %collective-permute-start.2 = (bf16[7680]{0:T(1024)(128)(2,1)S(1)}, bf16[7680]{0:T(1024)(128)(2,1)S(1)}, u32[]{:S(2)}, u32[]{:S(2)}) collective-permute-start(bf16[7680]{0:T(1024)(128)(2,1)S(1)} %pad_maximum_fusion.7), channel_id=1, source_target_pairs={{4,0},{8,4},{12,8},{16,12},{20,16},{24,20},{28,24},{5,1},{9,5},{13... | collective-permute-start | bytes 46088 | tf_op jit(solution)/shard_map/ppermute | solution.py:26
  13.6 3.0 %collective-permute-start.3 = (bf16[7680]{0:T(1024)(128)(2,1)S(1)}, bf16[7680]{0:T(1024)(128)(2,1)S(1)}, u32[]{:S(2)}, u32[]{:S(2)}) collective-permute-start(bf16[7680]{0:T(1024)(128)(2,1)S(1)} %pad_maximum_fusion.8), channel_id=1, source_target_pairs={{0,4},{4,8},{8,12},{12,16},{16,20},{20,24},{24,28},{1,5},{5,9},{9,... | collective-permute-start | bytes 46088 | tf_op jit(solution)/shard_map/ppermute | solution.py:25
  16.7 0.8 %collective-permute-done.3 = bf16[7680]{0:T(1024)(128)(2,1)S(1)} collective-permute-done((bf16[7680]{0:T(1024)(128)(2,1)S(1)}, bf16[7680]{0:T(1024)(128)(2,1)S(1)}, u32[]{:S(2)}, u32[]{:S(2)}) %collective-permute-start.3) | collective-permute-done | bytes 15392 | tf_op jit(solution)/shard_map/ppermute | solution.py:25
  17.6 0.3 convolution_bitcast_fusion
  17.9 0.3 convolution_bitcast_fusion.1
  18.2 0.3 convolution_bitcast_fusion.2
  18.5 0.3 convolution_bitcast_fusion.3
  18.9 0.2 copy.44
  19.0 0.2 reshape.249
  19.2 0.2 copy-done.7
  20.5 0.2 copy-done.8
  20.7 0.7 %convolution_select_fusion = f32[34,8,3,128]{3,1,2,0:T(8,128)S(1)} fusion(bf16[3,3,128,128]{3,2,1,0:T(8,128)(2,1)S(1)} %copy-done, bf16[36,1,7,2,128]{4,2,3,0,1:T(8,128)(2,1)S(1)} %slice.391, bf16[36,1,8,3,128]{4,2,3,0,1:T(8,128)(2,1)S(1)} %copy.29, pred[8,3]{0,1:T(4,128)(4,1)S(1)} %copy-done.8), kind=kOutput, calls=%fused_computation.3 | convolution fusion | flops 241858560 | bytes 1062936 | tf_op jit(solution)/shard_map/conv_general_dilated | solution.py:127
  21.5 0.2 squeeze.107
  21.7 0.2 broadcast_select_fusion
  22.2 0.5 fusion
  22.8 0.5 fusion.70
  23.4 0.2 pad_maximum_fusion
  23.6 0.9 %fusion.4 = bf16[4,656,128]{2,1,0:T(8,128)(2,1)} fusion(f32[4,2,656,128]{3,2,1,0:T(8,128)S(1)} %bitcast.224, s32[]{:T(128)S(6)} %select_n.108), kind=kLoop, calls=%fused_computation.14 | loop fusion | bytes 1343492 | tf_op jit(solution)/shard_map/convert_element_type | solution.py:185
  24.5 1.2 %collective-permute-start.4 = (bf16[4,656,128]{2,1,0:T(8,128)(2,1)}, bf16[4,656,128]{2,1,0:T(8,128)(2,1)}, u32[]{:S(2)}, u32[]{:S(2)}) collective-permute-start(bf16[4,656,128]{2,1,0:T(8,128)(2,1)} %fusion.4), channel_id=1, source_target_pairs={{0,4},{4,0},{8,12},{12,8},{16,20},{20,16},{24,28},{28,24},{1,5},{5... | collective-permute-start | bytes 2015240 | tf_op jit(solution)/shard_map/ppermute | solution.py:178
  25.8 2.1 %collective-permute-done.4 = bf16[4,656,128]{2,1,0:T(8,128)(2,1)} collective-permute-done((bf16[4,656,128]{2,1,0:T(8,128)(2,1)}, bf16[4,656,128]{2,1,0:T(8,128)(2,1)}, u32[]{:S(2)}, u32[]{:S(2)}) %collective-permute-start.4) | collective-permute-done | bytes 671776 | tf_op jit(solution)/shard_map/ppermute | solution.py:178
  27.9 1.2 %bitcast_add_fusion = f32[4,656,128]{2,1,0:T(8,128)S(1)} fusion(bf16[4,656,128]{2,1,0:T(8,128)(2,1)} %collective-permute-done.4, f32[4,2,656,128]{3,2,1,0:T(8,128)S(1)} %bitcast.225, s32[]{:T(128)S(6)} %select_n.107), kind=kLoop, calls=%fused_computation.1 | loop fusion | flops 671744 | bytes 3358724 | tf_op jit(solution)/shard_map/add | solution.py:185
  29.2 0.6 collective-permute-start.9
  29.8 0.5 copy-done.2
  30.3 0.5 fusion.84
  30.8 0.7 %copy.61 = f32[16,8,256,1]{2,1,0,3:T(8,128)} copy(f32[16,8,256,1]{2,0,1,3:T(8,128)S(1)} %fusion.84) | data formatting | bytes 262144 | tf_op jit(solution)/shard_map/rctn,tmn->rcm/dot_general | solution.py:151
  31.6 4.3 %collective-permute-done.9 = bf16[2,328,128]{2,1,0:T(8,128)(2,1)S(1)} collective-permute-done((bf16[2,328,128]{2,1,0:T(8,128)(2,1)S(1)}, bf16[2,328,128]{2,1,0:T(8,128)(2,1)S(1)}, u32[]{:S(2)}, u32[]{:S(2)}) %collective-permute-start.9) | collective-permute-done | bytes 167968 | tf_op jit(solution)/shard_map/ppermute | solution.py:178
  36.0 2.2 %collective-permute-done.5 = bf16[2,328,128]{2,1,0:T(8,128)(2,1)S(1)} collective-permute-done((bf16[2,328,128]{2,1,0:T(8,128)(2,1)S(1)}, bf16[2,328,128]{2,1,0:T(8,128)(2,1)S(1)}, u32[]{:S(2)}, u32[]{:S(2)}) %collective-permute-start.5) | collective-permute-done | bytes 167968 | tf_op jit(solution)/shard_map/ppermute | solution.py:178
  38.3 0.9 %collective-permute-start.6 = (bf16[328,128]{1,0:T(8,128)(2,1)S(1)}, bf16[328,128]{1,0:T(8,128)(2,1)S(1)}, u32[]{:S(2)}, u32[]{:S(2)}) collective-permute-start(bf16[328,128]{1,0:T(8,128)(2,1)S(1)} %fusion.68), channel_id=1, source_target_pairs={{0,2},{1,3},{2,0},{3,1},{4,6},{5,7},{6,4},{7,5},{8,10},{9,11},{10,... | collective-permute-start | bytes 251912 | tf_op jit(solution)/shard_map/ppermute | solution.py:178
  39.2 1.3 %collective-permute-done.10 = bf16[328,128]{1,0:T(8,128)(2,1)S(1)} collective-permute-done((bf16[328,128]{1,0:T(8,128)(2,1)S(1)}, bf16[328,128]{1,0:T(8,128)(2,1)S(1)}, u32[]{:S(2)}, u32[]{:S(2)}) %collective-permute-start.10) | collective-permute-done | bytes 84000 | tf_op jit(solution)/shard_map/ppermute | solution.py:178
  40.5 2.4 %collective-permute-start.11 = (bf16[328,128]{1,0:T(8,128)(2,1)S(1)}, bf16[328,128]{1,0:T(8,128)(2,1)S(1)}, u32[]{:S(2)}, u32[]{:S(2)}) collective-permute-start(bf16[328,128]{1,0:T(8,128)(2,1)S(1)} %fusion.50), channel_id=1, source_target_pairs={{0,8},{4,12},{8,0},{12,4},{16,24},{20,28},{24,16},{28,20},{1,9},{5... | collective-permute-start | bytes 251912 | tf_op jit(solution)/shard_map/ppermute | solution.py:178
  42.9 2.5 %collective-permute-start.7 = (bf16[328,128]{1,0:T(8,128)(2,1)S(1)}, bf16[328,128]{1,0:T(8,128)(2,1)S(1)}, u32[]{:S(2)}, u32[]{:S(2)}) collective-permute-start(bf16[328,128]{1,0:T(8,128)(2,1)S(1)} %fusion.51), channel_id=1, source_target_pairs={{0,8},{4,12},{8,0},{12,4},{16,24},{20,28},{24,16},{28,20},{1,9},{5... | collective-permute-start | bytes 251912 | tf_op jit(solution)/shard_map/ppermute | solution.py:178
  45.4 0.7 %collective-permute-done.11 = bf16[328,128]{1,0:T(8,128)(2,1)S(1)} collective-permute-done((bf16[328,128]{1,0:T(8,128)(2,1)S(1)}, bf16[328,128]{1,0:T(8,128)(2,1)S(1)}, u32[]{:S(2)}, u32[]{:S(2)}) %collective-permute-start.11) | collective-permute-done | bytes 84000 | tf_op jit(solution)/shard_map/ppermute | solution.py:178
  46.1 3.1 %collective-permute-start.12 = (bf16[328,128]{1,0:T(8,128)(2,1)S(1)}, bf16[328,128]{1,0:T(8,128)(2,1)S(1)}, u32[]{:S(2)}, u32[]{:S(2)}) collective-permute-start(bf16[328,128]{1,0:T(8,128)(2,1)S(1)} %add_convert_fusion.3), channel_id=1, source_target_pairs={{0,16},{4,20},{8,24},{12,28},{16,0},{20,4},{24,8},{28,12},{1,17},{... | collective-permute-start | bytes 251912 | tf_op jit(solution)/shard_map/ppermute | solution.py:178
  49.2 1.8 %collective-permute-start.8 = (bf16[328,128]{1,0:T(8,128)(2,1)S(1)}, bf16[328,128]{1,0:T(8,128)(2,1)S(1)}, u32[]{:S(2)}, u32[]{:S(2)}) collective-permute-start(bf16[328,128]{1,0:T(8,128)(2,1)S(1)} %add_convert_fusion.5), channel_id=1, source_target_pairs={{0,16},{4,20},{8,24},{12,28},{16,0},{20,4},{24,8},{28,12},{1,17},{... | collective-permute-start | bytes 251912 | tf_op jit(solution)/shard_map/ppermute | solution.py:178
  50.9 2.3 %collective-permute-done.12 = bf16[328,128]{1,0:T(8,128)(2,1)S(1)} collective-permute-done((bf16[328,128]{1,0:T(8,128)(2,1)S(1)}, bf16[328,128]{1,0:T(8,128)(2,1)S(1)}, u32[]{:S(2)}, u32[]{:S(2)}) %collective-permute-start.12) | collective-permute-done | bytes 84000 | tf_op jit(solution)/shard_map/ppermute | solution.py:178
  53.3 2.3 %collective-permute-done.8 = bf16[328,128]{1,0:T(8,128)(2,1)S(1)} collective-permute-done((bf16[328,128]{1,0:T(8,128)(2,1)S(1)}, bf16[328,128]{1,0:T(8,128)(2,1)S(1)}, u32[]{:S(2)}, u32[]{:S(2)}) %collective-permute-start.8) | collective-permute-done | bytes 84000 | tf_op jit(solution)/shard_map/ppermute | solution.py:178
  55.7 1.1 %convolution_convert_fusion = bf16[32,16,128]{2,1,0:T(8,128)(2,1)} fusion(bf16[32,16,1152]{2,1,0:T(8,128)(2,1)S(1)} %copy-done.4, bf16[1152,128,1]{1,0,2:T(8,128)(2,1)S(1)} %bitcast.222), kind=kOutput, calls=%fused_computation.7 | convolution fusion | flops 151060480 | bytes 1605632 | tf_op jit(solution)/shard_map/rck,kn->rcn/dot_general | solution.py:139
  56.8 0.2 collective-permute-done.13
  57.2 0.8 %slice.411 = f32[1024,128]{1,0:T(8,128)} slice(f32[1312,128]{1,0:T(8,128)S(1)} %convert_multiply_fusion), slice={[0:1024], [0:128]} | slice | bytes 1048576 | tf_op jit(solution)/shard_map/slice | solution.py:171
  58.0 0.7 %slice.412 = f32[288,128]{1,0:T(8,128)} slice(f32[1312,128]{1,0:T(8,128)S(1)} %convert_multiply_fusion), slice={[1024:1312], [0:128]} | slice | bytes 294912 | tf_op jit(solution)/shard_map/slice | solution.py:172
  (109 shorter events, 2.9 us)
Async XLA Ops:
  0.6 19.8 %copy-start = (bf16[3,3,128,128]{3,2,1,0:T(8,128)(2,1)S(1)}, bf16[3,3,128,128]{3,2,1,0:T(8,128)(2,1)}, u32[]{:S(2)}) copy-start(bf16[3,3,128,128]{3,2,1,0:T(8,128)(2,1)} %param.10) | copy-start | bytes 884740
  0.6 2.3 %copy-start.6 = (s32[16,8,256]{2,1,0:T(8,128)S(1)}, s32[16,8,256]{2,1,0:T(8,128)}, u32[]{:S(2)}) copy-start(s32[16,8,256]{2,1,0:T(8,128)} %param.6) | copy-start | bytes 393220
  0.7 6.7 %copy-start.1 = (bf16[4,4,256,128]{3,2,1,0:T(8,128)(2,1)S(1)}, bf16[4,4,256,128]{3,2,1,0:T(8,128)(2,1)}, u32[]{:S(2)}) copy-start(bf16[4,4,256,128]{3,2,1,0:T(8,128)(2,1)} %param.8) | copy-start | bytes 3145732
  3.2 8.8 %copy-start.5 = (bf16[32,16,128]{2,1,0:T(8,128)(2,1)S(1)}, bf16[32,16,128]{2,1,0:T(8,128)(2,1)}, u32[]{:S(2)}) copy-start(bf16[32,16,128]{2,1,0:T(8,128)(2,1)} %param.11) | copy-start | bytes 393220
  3.3 5.5 %collective-permute-start.1 = (bf16[12288]{0:T(1024)(128)(2,1)S(1)}, bf16[12288]{0:T(1024)(128)(2,1)S(1)}, u32[]{:S(2)}, u32[]{:S(2)}) collective-permute-start(bf16[12288]{0:T(1024)(128)(2,1)S(1)} %pad_maximum_fusion.6), channel_id=1, source_target_pairs={{1,0},{2,1},{3,2},{0,3},{5,4},{6,5},{7,6},{4,7},{9,8},{10,9},{11,1... | collective-permute-start | bytes 73736 | tf_op jit(solution)/shard_map/ppermute | solution.py:26
  7.3 4.8 %collective-permute-start = (bf16[12288]{0:T(1024)(128)(2,1)S(1)}, bf16[12288]{0:T(1024)(128)(2,1)S(1)}, u32[]{:S(2)}, u32[]{:S(2)}) collective-permute-start(bf16[12288]{0:T(1024)(128)(2,1)S(1)} %pad_maximum_fusion.5), channel_id=1, source_target_pairs={{0,1},{1,2},{2,3},{3,0},{4,5},{5,6},{6,7},{7,4},{8,9},{9,10},{10,1... | collective-permute-start | bytes 73736 | tf_op jit(solution)/shard_map/ppermute | solution.py:25
  12.2 4.4 %collective-permute-start.2 = (bf16[7680]{0:T(1024)(128)(2,1)S(1)}, bf16[7680]{0:T(1024)(128)(2,1)S(1)}, u32[]{:S(2)}, u32[]{:S(2)}) collective-permute-start(bf16[7680]{0:T(1024)(128)(2,1)S(1)} %pad_maximum_fusion.7), channel_id=1, source_target_pairs={{4,0},{8,4},{12,8},{16,12},{20,16},{24,20},{28,24},{5,1},{9,5},{13... | collective-permute-start | bytes 46088 | tf_op jit(solution)/shard_map/ppermute | solution.py:26
  13.6 3.9 %collective-permute-start.3 = (bf16[7680]{0:T(1024)(128)(2,1)S(1)}, bf16[7680]{0:T(1024)(128)(2,1)S(1)}, u32[]{:S(2)}, u32[]{:S(2)}) collective-permute-start(bf16[7680]{0:T(1024)(128)(2,1)S(1)} %pad_maximum_fusion.8), channel_id=1, source_target_pairs={{0,4},{4,8},{8,12},{12,16},{16,20},{20,24},{24,28},{1,5},{5,9},{9,... | collective-permute-start | bytes 46088 | tf_op jit(solution)/shard_map/ppermute | solution.py:25
  18.8 0.7 %copy-start.7 = (f32[128]{0:T(128)S(1)}, f32[128]{0:T(128)}, u32[]{:S(2)}) copy-start(f32[128]{0:T(128)} %param.9) | copy-start | bytes 1540
  20.1 0.7 %copy-start.8 = (pred[8,3]{0,1:T(4,128)(4,1)S(1)}, pred[8,3]{0,1:T(4,128)(4,1)}, u32[]{:S(2)}) copy-start(pred[8,3]{0,1:T(4,128)(4,1)} %constant.177) | copy-start | bytes 76
  20.1 2.1 %copy-start.3 = (bf16[32,16,1152]{2,1,0:T(8,128)(2,1)}, bf16[32,16,1152]{2,1,0:T(8,128)(2,1)S(1)}, u32[]{:S(2)}) copy-start(bf16[32,16,1152]{2,1,0:T(8,128)(2,1)S(1)} %slice_dynamic-update-slice_fusion) | copy-start | bytes 3538948
  24.5 3.3 %collective-permute-start.4 = (bf16[4,656,128]{2,1,0:T(8,128)(2,1)}, bf16[4,656,128]{2,1,0:T(8,128)(2,1)}, u32[]{:S(2)}, u32[]{:S(2)}) collective-permute-start(bf16[4,656,128]{2,1,0:T(8,128)(2,1)} %fusion.4), channel_id=1, source_target_pairs={{0,4},{4,0},{8,12},{12,8},{16,20},{20,16},{24,28},{28,24},{1,5},{5... | collective-permute-start | bytes 2015240 | tf_op jit(solution)/shard_map/ppermute | solution.py:178
  29.1 1.2 %copy-start.2 = (bf16[4,4,256,128]{3,2,1,0:T(8,128)(2,1)S(1)}, bf16[4,4,256,128]{3,2,1,0:T(8,128)(2,1)}, u32[]{:S(2)}) copy-start(bf16[4,4,256,128]{3,2,1,0:T(8,128)(2,1)} %param.8) | copy-start | bytes 3145732
  29.2 6.7 %collective-permute-start.9 = (bf16[2,328,128]{2,1,0:T(8,128)(2,1)S(1)}, bf16[2,328,128]{2,1,0:T(8,128)(2,1)S(1)}, u32[]{:S(2)}, u32[]{:S(2)}) collective-permute-start(bf16[2,328,128]{2,1,0:T(8,128)(2,1)S(1)} %fusion.49), channel_id=1, source_target_pairs={{0,2},{1,3},{2,0},{3,1},{4,6},{5,7},{6,4},{7,5},{8,10},{9,11},{10,... | collective-permute-start | bytes 503816 | tf_op jit(solution)/shard_map/ppermute | solution.py:178
  31.5 6.7 %collective-permute-start.5 = (bf16[2,328,128]{2,1,0:T(8,128)(2,1)S(1)}, bf16[2,328,128]{2,1,0:T(8,128)(2,1)S(1)}, u32[]{:S(2)}, u32[]{:S(2)}) collective-permute-start(bf16[2,328,128]{2,1,0:T(8,128)(2,1)S(1)} %fusion.48), channel_id=1, source_target_pairs={{0,1},{1,0},{2,3},{3,2},{4,5},{5,4},{6,7},{7,6},{8,9},{9,8},{10,11... | collective-permute-start | bytes 503816 | tf_op jit(solution)/shard_map/ppermute | solution.py:178
  36.0 4.5 %collective-permute-start.10 = (bf16[328,128]{1,0:T(8,128)(2,1)S(1)}, bf16[328,128]{1,0:T(8,128)(2,1)S(1)}, u32[]{:S(2)}, u32[]{:S(2)}) collective-permute-start(bf16[328,128]{1,0:T(8,128)(2,1)S(1)} %fusion.69), channel_id=1, source_target_pairs={{0,1},{1,0},{2,3},{3,2},{4,5},{5,4},{6,7},{7,6},{8,9},{9,8},{10,11... | collective-permute-start | bytes 251912 | tf_op jit(solution)/shard_map/ppermute | solution.py:178
  38.3 17.4 %copy-start.4 = (bf16[32,16,1152]{2,1,0:T(8,128)(2,1)S(1)}, bf16[32,16,1152]{2,1,0:T(8,128)(2,1)}, u32[]{:S(2)}) copy-start(bf16[32,16,1152]{2,1,0:T(8,128)(2,1)} %copy-done.3) | copy-start | bytes 3538948
  38.3 4.6 %collective-permute-start.6 = (bf16[328,128]{1,0:T(8,128)(2,1)S(1)}, bf16[328,128]{1,0:T(8,128)(2,1)S(1)}, u32[]{:S(2)}, u32[]{:S(2)}) collective-permute-start(bf16[328,128]{1,0:T(8,128)(2,1)S(1)} %fusion.68), channel_id=1, source_target_pairs={{0,2},{1,3},{2,0},{3,1},{4,6},{5,7},{6,4},{7,5},{8,10},{9,11},{10,... | collective-permute-start | bytes 251912 | tf_op jit(solution)/shard_map/ppermute | solution.py:178
  40.5 5.5 %collective-permute-start.11 = (bf16[328,128]{1,0:T(8,128)(2,1)S(1)}, bf16[328,128]{1,0:T(8,128)(2,1)S(1)}, u32[]{:S(2)}, u32[]{:S(2)}) collective-permute-start(bf16[328,128]{1,0:T(8,128)(2,1)S(1)} %fusion.50), channel_id=1, source_target_pairs={{0,8},{4,12},{8,0},{12,4},{16,24},{20,28},{24,16},{28,20},{1,9},{5... | collective-permute-start | bytes 251912 | tf_op jit(solution)/shard_map/ppermute | solution.py:178
  42.9 6.3 %collective-permute-start.7 = (bf16[328,128]{1,0:T(8,128)(2,1)S(1)}, bf16[328,128]{1,0:T(8,128)(2,1)S(1)}, u32[]{:S(2)}, u32[]{:S(2)}) collective-permute-start(bf16[328,128]{1,0:T(8,128)(2,1)S(1)} %fusion.51), channel_id=1, source_target_pairs={{0,8},{4,12},{8,0},{12,4},{16,24},{20,28},{24,16},{28,20},{1,9},{5... | collective-permute-start | bytes 251912 | tf_op jit(solution)/shard_map/ppermute | solution.py:178
  46.1 7.2 %collective-permute-start.12 = (bf16[328,128]{1,0:T(8,128)(2,1)S(1)}, bf16[328,128]{1,0:T(8,128)(2,1)S(1)}, u32[]{:S(2)}, u32[]{:S(2)}) collective-permute-start(bf16[328,128]{1,0:T(8,128)(2,1)S(1)} %add_convert_fusion.3), channel_id=1, source_target_pairs={{0,16},{4,20},{8,24},{12,28},{16,0},{20,4},{24,8},{28,12},{1,17},{... | collective-permute-start | bytes 251912 | tf_op jit(solution)/shard_map/ppermute | solution.py:178
  49.2 6.3 %collective-permute-start.8 = (bf16[328,128]{1,0:T(8,128)(2,1)S(1)}, bf16[328,128]{1,0:T(8,128)(2,1)S(1)}, u32[]{:S(2)}, u32[]{:S(2)}) collective-permute-start(bf16[328,128]{1,0:T(8,128)(2,1)S(1)} %add_convert_fusion.5), channel_id=1, source_target_pairs={{0,16},{4,20},{8,24},{12,28},{16,0},{20,4},{24,8},{28,12},{1,17},{... | collective-permute-start | bytes 251912 | tf_op jit(solution)/shard_map/ppermute | solution.py:178
  55.6 1.5 %collective-permute-start.13 = (bf16[656,128]{1,0:T(8,128)(2,1)S(1)}, bf16[656,128]{1,0:T(8,128)(2,1)S(1)}, u32[]{:S(2)}, u32[]{:S(2)}) collective-permute-start(bf16[656,128]{1,0:T(8,128)(2,1)S(1)} %pad_maximum_fusion.3), channel_id=1, source_target_pairs={{0,4},{4,0},{8,12},{12,8},{16,20},{20,16},{24,28},{28,24},{1,5},{5... | collective-permute-start | bytes 503816 | tf_op jit(solution)/shard_map/ppermute | solution.py:178

commit v20 on v15

--- a/solution.py
+++ b/solution.py
@@ -116,7 +116,10 @@
     lat_count = lax.axis_size("lat")
     lon_count = lax.axis_size("lon")
     back_mix = mix_kernel[::-1, ::-1].transpose(0, 1, 3, 2)
-    padded_in, grad_pad = extend_all((inputs, cotangent), (1, 2))
+    coded = (elem_codes.astype(jnp.bfloat16), block_exps.astype(jnp.bfloat16), cotangent)
+    codes_wide, exps_wide, grad_wide = swap_edges(coded, (1, 1, 2), "lon", 1, True)
+    inputs_wide = decode(codes_wide.astype(jnp.int32), exps_wide.astype(jnp.int32))
+    padded_in, grad_pad = swap_edges((inputs_wide, grad_wide), (1, 2), "lat", 0, False)
     raw = upsample(padded_in, up_kernel, in_rows, in_cols)
     pre_act = (raw + up_bias).astype(jnp.bfloat16)
     row_at = lax.axis_index("lat") * out_rows - 1 + lax.broadcasted_iota(jnp.int32, (out_rows + 2, 1, 1), 0)

time: 59 us -> 63.6 us (1.078)
  local copies, waits for them, and re-layouts: 7.81 us -> 11.1 us
  starting transfers between devices: 20.9 us -> 18.6 us
  other arithmetic: 3.51 us -> 5.26 us
  waiting for transfers between devices: 20.6 us -> 22.1 us
    ppermute x2, starting transfers between devices: 3.09 us -> 1.35 us  [swap_edges(): lax.ppermute(jnp.concatenate([p.reshape(-1) for p in lasts]), axis, up)]
    ppermute x2, waiting for transfers between devices: 1.3 us -> 3.03 us  [swap_edges(): lax.ppermute(jnp.concatenate([p.reshape(-1) for p in leads]), axis, down)]
    convert_element_type x0 -> x2, other arithmetic: none -> 1.71 us  [the longest x1 0.95 us: shards(): elem_codes.astype(jnp.bfloat16)]
    ppermute x2, waiting for transfers between devices: 4.02 us -> 2.39 us  [swap_edges(): lax.ppermute(jnp.concatenate([p.reshape(-1) for p in lasts]), axis, up)]
    ppermute x10, waiting for transfers between devices: 15.3 us -> 16.6 us  [exchange(): return lax.ppermute(part, axis, [(i, i ^ step) for i in range(size)])]
    squeeze x1, local copies, waits for them, and re-layouts: 0.1 us -> 1.33 us  [upsample(): kernels.append(up_kernel[row_tap, col_tap])]
    unnamed x45 -> x43, local copies, waits for them, and re-layouts: 1.67 us -> 2.51 us
  transfers between devices with their start and end apart: 14 -> 14, of which waited for: 11 -> 11; matrix products, arithmetic and copies ran while one was open for 5% -> 9% of each run, Pallas kernels for 0% -> 0%
where the time goes in v20:
time: 63.6 us; the launch traced here: 63.1 us
  waiting for transfers between devices  22.1 us (35%)
  starting transfers between devices  18.6 us (29%)
  local copies, waits for them, and re-layouts  11.1 us (17%)
  other arithmetic  5.26 us (8%)
  matrix products  4.62 us (7%)
  between operations  1.47 us (2%)
    ppermute x10, waiting for transfers between devices, exchange(): return lax.ppermute(part, axis, [(i, i ^ step) for i in range(size)])  16.6 us
    ppermute x10, starting transfers between devices, exchange(): return lax.ppermute(part, axis, [(i, i ^ step) for i in range(size)])  12 us
    ppermute x2, starting transfers between devices, swap_edges(): lax.ppermute(jnp.concatenate([p.reshape(-1) for p in leads]), axis, down)  5.24 us
    ppermute x2, waiting for transfers between devices, swap_edges(): lax.ppermute(jnp.concatenate([p.reshape(-1) for p in leads]), axis, down)  3.03 us
    unnamed x43, local copies, waits for them, and re-layouts  2.51 us
    ppermute x2, waiting for transfers between devices, swap_edges(): lax.ppermute(jnp.concatenate([p.reshape(-1) for p in lasts]), axis, up)  2.39 us
    ppermute x2, starting transfers between devices, swap_edges(): lax.ppermute(jnp.concatenate([p.reshape(-1) for p in lasts]), axis, up)  1.35 us
    squeeze x1, local copies, waits for them, and re-layouts, upsample(): kernels.append(up_kernel[row_tap, col_tap])  1.33 us
  transfers between devices with their start and end apart: 14, of which 11 were waited for; matrix products, arithmetic and copies ran while one was open for 9% of the time, Pallas kernels for 0%

profile of v20, /device:TPU:0, one launch (start us, length us, event | category | flops | bytes accessed | tf_op | source)
XLA Modules:
  0.0 63.1 jit_solution(5168061384263610558)
XLA Ops:
  0.6 0.9 %fusion.136 = (bf16[32,2,128]{2,1,0:T(2,128)(2,1)S(1)}, bf16[32,2,128]{2,1,0:T(2,128)(2,1)S(1)}) fusion(bf16[32,16,128]{2,1,0:T(8,128)(2,1)} %param.11), kind=kLoop, calls=%fused_computation.279 | loop fusion | bytes 65536 | tf_op jit(solution)/shard_map/slice | solution.py:23
  1.6 0.8 %convert_element_type.150 = bf16[16,8,8]{0,2,1:T(8,128)(2,1)S(1)} convert(s32[16,8,8]{0,2,1:T(8,128)} %param.7) | non-fusion elementwise | flops 1024 | bytes 6144 | tf_op jit(solution)/shard_map/convert_element_type | solution.py:119
  2.6 0.9 %copy_convert_fusion = bf16[16,8,256]{2,0,1:T(8,128)(2,1)S(1)} fusion(s32[16,8,256]{2,1,0:T(8,128)} %param.6), kind=kLoop, calls=%fused_computation.169 | loop fusion | flops 32768 | bytes 196608 | tf_op jit(solution)/shard_map/convert_element_type | solution.py:119
  3.5 3.9 %collective-permute-start.1 = (bf16[12416]{0:T(1024)(128)(2,1)S(1)}, bf16[12416]{0:T(1024)(128)(2,1)S(1)}, u32[]{:S(2)}, u32[]{:S(2)}) collective-permute-start(bf16[12416]{0:T(1024)(128)(2,1)S(1)} %pad_maximum_fusion.6), channel_id=1, source_target_pairs={{1,0},{2,1},{3,2},{0,3},{5,4},{6,5},{7,6},{4,7},{9,8},{10,9},{11,1... | collective-permute-start | bytes 74504 | tf_op jit(solution)/shard_map/ppermute | solution.py:26
  7.8 0.8 %multiply_exponential_fusion.1 = f32[16,8,8]{0,2,1:T(8,128)S(1)} fusion(s32[16,8,8]{0,2,1:T(8,128)} %param.7), kind=kLoop, calls=%fused_computation.244 | loop fusion | flops 2048 | bytes 8192 | tf_op jit(solution)/shard_map/exp2 | solution.py:50
  8.6 1.3 %slice_bitcast_fusion.15 = (bf16[256,128]{1,0:T(8,128)(2,1)S(1)}, bf16[256,128]{1,0:T(8,128)(2,1)S(1)}, bf16[256,128]{1,0:T(8,128)(2,1)S(1)}, bf16[256,128]{1,0:...) fusion(bf16[4,4,256,128]{3,2,1,0:T(8,128)(2,1)} %param.8), kind=kLoop, calls=%fused_computation.210 | loop fusion | bytes 2097152 | tf_op jit(solution)/shard_map/squeeze | solution.py:74
  10.1 2.4 %collective-permute-done = bf16[12416]{0:T(1024)(128)(2,1)S(1)} collective-permute-done((bf16[12416]{0:T(1024)(128)(2,1)S(1)}, bf16[12416]{0:T(1024)(128)(2,1)S(1)}, u32[]{:S(2)}, u32[]{:S(2)}) %collective-permute-start) | collective-permute-done | bytes 24864 | tf_op jit(solution)/shard_map/ppermute | solution.py:25
  12.8 0.2 broadcast_in_dim.24
  13.4 0.4 fusion.74
  13.9 1.3 %collective-permute-start.3 = (bf16[7680]{0:T(1024)(128)(2,1)S(1)}, bf16[7680]{0:T(1024)(128)(2,1)S(1)}, u32[]{:S(2)}, u32[]{:S(2)}) collective-permute-start(bf16[7680]{0:T(1024)(128)(2,1)S(1)} %pad_maximum_fusion.8), channel_id=1, source_target_pairs={{0,4},{4,8},{8,12},{12,16},{16,20},{20,24},{24,28},{1,5},{5,9},{9,... | collective-permute-start | bytes 46088 | tf_op jit(solution)/shard_map/ppermute | solution.py:25
  15.2 1.3 %collective-permute-start.2 = (bf16[7680]{0:T(1024)(128)(2,1)S(1)}, bf16[7680]{0:T(1024)(128)(2,1)S(1)}, u32[]{:S(2)}, u32[]{:S(2)}) collective-permute-start(bf16[7680]{0:T(1024)(128)(2,1)S(1)} %pad_maximum_fusion.7), channel_id=1, source_target_pairs={{4,0},{8,4},{12,8},{16,12},{20,16},{24,20},{28,24},{5,1},{9,5},{13... | collective-permute-start | bytes 46088 | tf_op jit(solution)/shard_map/ppermute | solution.py:26
  17.1 3.0 %collective-permute-done.2 = bf16[7680]{0:T(1024)(128)(2,1)S(1)} collective-permute-done((bf16[7680]{0:T(1024)(128)(2,1)S(1)}, bf16[7680]{0:T(1024)(128)(2,1)S(1)}, u32[]{:S(2)}, u32[]{:S(2)}) %collective-permute-start.2) | collective-permute-done | bytes 15392 | tf_op jit(solution)/shard_map/ppermute | solution.py:26
  20.2 0.3 convolution_bitcast_fusion.2
  20.5 0.3 convolution_bitcast_fusion.3
  20.8 0.3 convolution_bitcast_fusion
  21.0 0.3 convolution_bitcast_fusion.1
  21.6 0.2 reshape.265
  21.8 0.2 copy-done.6
  23.1 0.2 copy-done.7
  23.3 0.7 %convolution_select_fusion = f32[34,8,3,128]{3,1,2,0:T(8,128)S(1)} fusion(bf16[3,3,128,128]{3,2,1,0:T(8,128)(2,1)S(1)} %copy-done, bf16[36,1,7,2,128]{4,2,3,0,1:T(8,128)(2,1)S(1)} %slice.385, bf16[36,1,8,3,128]{4,2,3,0,1:T(8,128)(2,1)S(1)} %copy.33, pred[8,3]{0,1:T(4,128)(4,1)S(1)} %copy-done.7), kind=kOutput, calls=%fused_computation.3 | convolution fusion | flops 241858560 | bytes 1062936 | tf_op jit(solution)/shard_map/conv_general_dilated | solution.py:129
  24.3 0.2 broadcast_select_fusion
  24.8 0.5 fusion
  25.4 0.8 %copy-done.5 = s32[16,8,256]{2,1,0:T(8,128)S(1)} copy-done((s32[16,8,256]{2,1,0:T(8,128)S(1)}, s32[16,8,256]{2,1,0:T(8,128)}, u32[]{:S(2)}) %copy-start.5) | copy-done | bytes 131096
  26.2 0.7 %fusion.5 = f32[256,16,128,1]{2,0,3,1:T(8,128)S(1)} fusion(bf16[16,8,16,128]{3,0,1,2:T(8,128)(2,1)S(1)} %constant_dynamic-update-slice_fusion, f32[16,8,256]{2,1,0:T(8,128)S(1)} %reshape.229, s32[16,8,256]{2,1,0:T(8,128)S(1)} %copy-done.5), kind=kOutput, calls=%fused_computation.18 | convolution fusion | flops 135921664 | bytes 2883584 | tf_op jit(solution)/shard_map/rctn,rcm->tmn/dot_general | solution.py:159
  27.3 0.9 %fusion.4 = bf16[4,656,128]{2,1,0:T(8,128)(2,1)} fusion(f32[4,2,656,128]{3,2,1,0:T(8,128)S(1)} %bitcast.229, s32[]{:T(128)S(6)} %select_n.135), kind=kLoop, calls=%fused_computation.14 | loop fusion | bytes 1343492 | tf_op jit(solution)/shard_map/convert_element_type | solution.py:187
  28.2 2.5 %collective-permute-start.4 = (bf16[4,656,128]{2,1,0:T(8,128)(2,1)}, bf16[4,656,128]{2,1,0:T(8,128)(2,1)}, u32[]{:S(2)}, u32[]{:S(2)}) collective-permute-start(bf16[4,656,128]{2,1,0:T(8,128)(2,1)} %fusion.4), channel_id=1, source_target_pairs={{0,4},{4,0},{8,12},{12,8},{16,20},{20,16},{24,28},{28,24},{1,5},{5... | collective-permute-start | bytes 2015240 | tf_op jit(solution)/shard_map/ppermute | solution.py:180
  30.7 2.1 %collective-permute-done.4 = bf16[4,656,128]{2,1,0:T(8,128)(2,1)} collective-permute-done((bf16[4,656,128]{2,1,0:T(8,128)(2,1)}, bf16[4,656,128]{2,1,0:T(8,128)(2,1)}, u32[]{:S(2)}, u32[]{:S(2)}) %collective-permute-start.4) | collective-permute-done | bytes 671776 | tf_op jit(solution)/shard_map/ppermute | solution.py:180
  32.8 1.2 %bitcast_add_fusion = f32[4,656,128]{2,1,0:T(8,128)S(1)} fusion(bf16[4,656,128]{2,1,0:T(8,128)(2,1)} %collective-permute-done.4, f32[4,2,656,128]{3,2,1,0:T(8,128)S(1)} %bitcast.230, s32[]{:T(128)S(6)} %select_n.134), kind=kLoop, calls=%fused_computation.1 | loop fusion | flops 671744 | bytes 3358724 | tf_op jit(solution)/shard_map/add | solution.py:187
  34.2 0.6 collective-permute-start.9
  34.7 0.5 copy-done.1
  35.2 0.5 fusion.138
  35.7 0.7 %copy.72 = f32[16,8,256,1]{2,1,0,3:T(8,128)} copy(f32[16,8,256,1]{2,0,1,3:T(8,128)S(1)} %fusion.138) | data formatting | bytes 262144 | tf_op jit(solution)/shard_map/rctn,tmn->rcm/dot_general | solution.py:153
  36.6 4.2 %collective-permute-done.9 = bf16[2,328,128]{2,1,0:T(8,128)(2,1)S(1)} collective-permute-done((bf16[2,328,128]{2,1,0:T(8,128)(2,1)S(1)}, bf16[2,328,128]{2,1,0:T(8,128)(2,1)S(1)}, u32[]{:S(2)}, u32[]{:S(2)}) %collective-permute-start.9) | collective-permute-done | bytes 167968 | tf_op jit(solution)/shard_map/ppermute | solution.py:180
  41.0 2.2 %collective-permute-done.5 = bf16[2,328,128]{2,1,0:T(8,128)(2,1)S(1)} collective-permute-done((bf16[2,328,128]{2,1,0:T(8,128)(2,1)S(1)}, bf16[2,328,128]{2,1,0:T(8,128)(2,1)S(1)}, u32[]{:S(2)}, u32[]{:S(2)}) %collective-permute-start.5) | collective-permute-done | bytes 167968 | tf_op jit(solution)/shard_map/ppermute | solution.py:180
  43.2 0.9 %collective-permute-start.6 = (bf16[328,128]{1,0:T(8,128)(2,1)S(1)}, bf16[328,128]{1,0:T(8,128)(2,1)S(1)}, u32[]{:S(2)}, u32[]{:S(2)}) collective-permute-start(bf16[328,128]{1,0:T(8,128)(2,1)S(1)} %fusion.95), channel_id=1, source_target_pairs={{0,2},{1,3},{2,0},{3,1},{4,6},{5,7},{6,4},{7,5},{8,10},{9,11},{10,... | collective-permute-start | bytes 251912 | tf_op jit(solution)/shard_map/ppermute | solution.py:180
  44.2 1.3 %collective-permute-done.10 = bf16[328,128]{1,0:T(8,128)(2,1)S(1)} collective-permute-done((bf16[328,128]{1,0:T(8,128)(2,1)S(1)}, bf16[328,128]{1,0:T(8,128)(2,1)S(1)}, u32[]{:S(2)}, u32[]{:S(2)}) %collective-permute-start.10) | collective-permute-done | bytes 84000 | tf_op jit(solution)/shard_map/ppermute | solution.py:180
  45.5 1.6 %collective-permute-start.11 = (bf16[328,128]{1,0:T(8,128)(2,1)S(1)}, bf16[328,128]{1,0:T(8,128)(2,1)S(1)}, u32[]{:S(2)}, u32[]{:S(2)}) collective-permute-start(bf16[328,128]{1,0:T(8,128)(2,1)S(1)} %fusion.55), channel_id=1, source_target_pairs={{0,8},{4,12},{8,0},{12,4},{16,24},{20,28},{24,16},{28,20},{1,9},{5... | collective-permute-start | bytes 251912 | tf_op jit(solution)/shard_map/ppermute | solution.py:180
  47.1 0.7 %collective-permute-done.6 = bf16[328,128]{1,0:T(8,128)(2,1)S(1)} collective-permute-done((bf16[328,128]{1,0:T(8,128)(2,1)S(1)}, bf16[328,128]{1,0:T(8,128)(2,1)S(1)}, u32[]{:S(2)}, u32[]{:S(2)}) %collective-permute-start.6) | collective-permute-done | bytes 84000 | tf_op jit(solution)/shard_map/ppermute | solution.py:180
  47.8 1.6 %collective-permute-start.7 = (bf16[328,128]{1,0:T(8,128)(2,1)S(1)}, bf16[328,128]{1,0:T(8,128)(2,1)S(1)}, u32[]{:S(2)}, u32[]{:S(2)}) collective-permute-start(bf16[328,128]{1,0:T(8,128)(2,1)S(1)} %fusion.56), channel_id=1, source_target_pairs={{0,8},{4,12},{8,0},{12,4},{16,24},{20,28},{24,16},{28,20},{1,9},{5... | collective-permute-start | bytes 251912 | tf_op jit(solution)/shard_map/ppermute | solution.py:180
  49.4 1.3 %collective-permute-done.11 = bf16[328,128]{1,0:T(8,128)(2,1)S(1)} collective-permute-done((bf16[328,128]{1,0:T(8,128)(2,1)S(1)}, bf16[328,128]{1,0:T(8,128)(2,1)S(1)}, u32[]{:S(2)}, u32[]{:S(2)}) %collective-permute-start.11) | collective-permute-done | bytes 84000 | tf_op jit(solution)/shard_map/ppermute | solution.py:180
  50.8 2.8 %collective-permute-start.12 = (bf16[328,128]{1,0:T(8,128)(2,1)S(1)}, bf16[328,128]{1,0:T(8,128)(2,1)S(1)}, u32[]{:S(2)}, u32[]{:S(2)}) collective-permute-start(bf16[328,128]{1,0:T(8,128)(2,1)S(1)} %add_convert_fusion.3), channel_id=1, source_target_pairs={{0,16},{4,20},{8,24},{12,28},{16,0},{20,4},{24,8},{28,12},{1,17},{... | collective-permute-start | bytes 251912 | tf_op jit(solution)/shard_map/ppermute | solution.py:180
  53.6 1.6 %collective-permute-start.8 = (bf16[328,128]{1,0:T(8,128)(2,1)S(1)}, bf16[328,128]{1,0:T(8,128)(2,1)S(1)}, u32[]{:S(2)}, u32[]{:S(2)}) collective-permute-start(bf16[328,128]{1,0:T(8,128)(2,1)S(1)} %add_convert_fusion.5), channel_id=1, source_target_pairs={{0,16},{4,20},{8,24},{12,28},{16,0},{20,4},{24,8},{28,12},{1,17},{... | collective-permute-start | bytes 251912 | tf_op jit(solution)/shard_map/ppermute | solution.py:180
  55.2 2.8 %collective-permute-done.12 = bf16[328,128]{1,0:T(8,128)(2,1)S(1)} collective-permute-done((bf16[328,128]{1,0:T(8,128)(2,1)S(1)}, bf16[328,128]{1,0:T(8,128)(2,1)S(1)}, u32[]{:S(2)}, u32[]{:S(2)}) %collective-permute-start.12) | collective-permute-done | bytes 84000 | tf_op jit(solution)/shard_map/ppermute | solution.py:180
  58.0 1.9 %collective-permute-done.8 = bf16[328,128]{1,0:T(8,128)(2,1)S(1)} collective-permute-done((bf16[328,128]{1,0:T(8,128)(2,1)S(1)}, bf16[328,128]{1,0:T(8,128)(2,1)S(1)}, u32[]{:S(2)}, u32[]{:S(2)}) %collective-permute-start.8) | collective-permute-done | bytes 84000 | tf_op jit(solution)/shard_map/ppermute | solution.py:180
  60.1 1.1 %convolution_convert_fusion = bf16[32,16,128]{2,1,0:T(8,128)(2,1)} fusion(bf16[32,16,1152]{2,1,0:T(8,128)(2,1)S(1)} %copy-done.3, bf16[1152,128,1]{1,0,2:T(8,128)(2,1)S(1)} %bitcast.227), kind=kOutput, calls=%fused_computation.7 | convolution fusion | flops 151060480 | bytes 1605632 | tf_op jit(solution)/shard_map/rck,kn->rcn/dot_general | solution.py:141
  61.2 0.2 collective-permute-done.13
  61.6 0.8 %slice.405 = f32[1024,128]{1,0:T(8,128)} slice(f32[1312,128]{1,0:T(8,128)S(1)} %convert_multiply_fusion), slice={[0:1024], [0:128]} | slice | bytes 1048576 | tf_op jit(solution)/shard_map/slice | solution.py:173
  62.4 0.7 %slice.406 = f32[288,128]{1,0:T(8,128)} slice(f32[1312,128]{1,0:T(8,128)S(1)} %convert_multiply_fusion), slice={[1024:1312], [0:128]} | slice | bytes 294912 | tf_op jit(solution)/shard_map/slice | solution.py:174
  (122 shorter events, 4.8 us)
Async XLA Ops:
  0.6 22.4 %copy-start = (bf16[3,3,128,128]{3,2,1,0:T(8,128)(2,1)S(1)}, bf16[3,3,128,128]{3,2,1,0:T(8,128)(2,1)}, u32[]{:S(2)}) copy-start(bf16[3,3,128,128]{3,2,1,0:T(8,128)(2,1)} %param.10) | copy-start | bytes 884740
  3.5 6.4 %collective-permute-start.1 = (bf16[12416]{0:T(1024)(128)(2,1)S(1)}, bf16[12416]{0:T(1024)(128)(2,1)S(1)}, u32[]{:S(2)}, u32[]{:S(2)}) collective-permute-start(bf16[12416]{0:T(1024)(128)(2,1)S(1)} %pad_maximum_fusion.6), channel_id=1, source_target_pairs={{1,0},{2,1},{3,2},{0,3},{5,4},{6,5},{7,6},{4,7},{9,8},{10,9},{11,1... | collective-permute-start | bytes 74504 | tf_op jit(solution)/shard_map/ppermute | solution.py:26
  7.7 4.8 %collective-permute-start = (bf16[12416]{0:T(1024)(128)(2,1)S(1)}, bf16[12416]{0:T(1024)(128)(2,1)S(1)}, u32[]{:S(2)}, u32[]{:S(2)}) collective-permute-start(bf16[12416]{0:T(1024)(128)(2,1)S(1)} %pad_maximum_fusion.5), channel_id=1, source_target_pairs={{0,1},{1,2},{2,3},{3,0},{4,5},{5,6},{6,7},{7,4},{8,9},{9,10},{10,1... | collective-permute-start | bytes 74504 | tf_op jit(solution)/shard_map/ppermute | solution.py:25
  9.9 3.5 %copy-start.4 = (bf16[32,16,128]{2,1,0:T(8,128)(2,1)S(1)}, bf16[32,16,128]{2,1,0:T(8,128)(2,1)}, u32[]{:S(2)}) copy-start(bf16[32,16,128]{2,1,0:T(8,128)(2,1)} %param.11) | copy-start | bytes 393220
  13.9 3.2 %collective-permute-start.3 = (bf16[7680]{0:T(1024)(128)(2,1)S(1)}, bf16[7680]{0:T(1024)(128)(2,1)S(1)}, u32[]{:S(2)}, u32[]{:S(2)}) collective-permute-start(bf16[7680]{0:T(1024)(128)(2,1)S(1)} %pad_maximum_fusion.8), channel_id=1, source_target_pairs={{0,4},{4,8},{8,12},{12,16},{16,20},{20,24},{24,28},{1,5},{5,9},{9,... | collective-permute-start | bytes 46088 | tf_op jit(solution)/shard_map/ppermute | solution.py:25
  15.2 4.9 %collective-permute-start.2 = (bf16[7680]{0:T(1024)(128)(2,1)S(1)}, bf16[7680]{0:T(1024)(128)(2,1)S(1)}, u32[]{:S(2)}, u32[]{:S(2)}) collective-permute-start(bf16[7680]{0:T(1024)(128)(2,1)S(1)} %pad_maximum_fusion.7), channel_id=1, source_target_pairs={{4,0},{8,4},{12,8},{16,12},{20,16},{24,20},{28,24},{5,1},{9,5},{13... | collective-permute-start | bytes 46088 | tf_op jit(solution)/shard_map/ppermute | solution.py:26
  21.4 0.7 %copy-start.6 = (f32[128]{0:T(128)S(1)}, f32[128]{0:T(128)}, u32[]{:S(2)}) copy-start(f32[128]{0:T(128)} %param.9) | copy-start | bytes 1540
  22.6 0.7 %copy-start.7 = (pred[8,3]{0,1:T(4,128)(4,1)S(1)}, pred[8,3]{0,1:T(4,128)(4,1)}, u32[]{:S(2)}) copy-start(pred[8,3]{0,1:T(4,128)(4,1)} %constant.214) | copy-start | bytes 76
  22.7 2.1 %copy-start.2 = (bf16[32,16,1152]{2,1,0:T(8,128)(2,1)}, bf16[32,16,1152]{2,1,0:T(8,128)(2,1)S(1)}, u32[]{:S(2)}) copy-start(bf16[32,16,1152]{2,1,0:T(8,128)(2,1)S(1)} %slice_dynamic-update-slice_fusion) | copy-start | bytes 3538948
  25.3 0.9 %copy-start.5 = (s32[16,8,256]{2,1,0:T(8,128)S(1)}, s32[16,8,256]{2,1,0:T(8,128)}, u32[]{:S(2)}) copy-start(s32[16,8,256]{2,1,0:T(8,128)} %param.6) | copy-start | bytes 393220
  28.2 4.6 %collective-permute-start.4 = (bf16[4,656,128]{2,1,0:T(8,128)(2,1)}, bf16[4,656,128]{2,1,0:T(8,128)(2,1)}, u32[]{:S(2)}, u32[]{:S(2)}) collective-permute-start(bf16[4,656,128]{2,1,0:T(8,128)(2,1)} %fusion.4), channel_id=1, source_target_pairs={{0,4},{4,0},{8,12},{12,8},{16,20},{20,16},{24,28},{28,24},{1,5},{5... | collective-permute-start | bytes 2015240 | tf_op jit(solution)/shard_map/ppermute | solution.py:180
  34.0 1.2 %copy-start.1 = (bf16[4,4,256,128]{3,2,1,0:T(8,128)(2,1)S(1)}, bf16[4,4,256,128]{3,2,1,0:T(8,128)(2,1)}, u32[]{:S(2)}) copy-start(bf16[4,4,256,128]{3,2,1,0:T(8,128)(2,1)} %param.8) | copy-start | bytes 3145732
  34.2 6.7 %collective-permute-start.9 = (bf16[2,328,128]{2,1,0:T(8,128)(2,1)S(1)}, bf16[2,328,128]{2,1,0:T(8,128)(2,1)S(1)}, u32[]{:S(2)}, u32[]{:S(2)}) collective-permute-start(bf16[2,328,128]{2,1,0:T(8,128)(2,1)S(1)} %fusion.54), channel_id=1, source_target_pairs={{0,2},{1,3},{2,0},{3,1},{4,6},{5,7},{6,4},{7,5},{8,10},{9,11},{10,... | collective-permute-start | bytes 503816 | tf_op jit(solution)/shard_map/ppermute | solution.py:180
  36.5 6.7 %collective-permute-start.5 = (bf16[2,328,128]{2,1,0:T(8,128)(2,1)S(1)}, bf16[2,328,128]{2,1,0:T(8,128)(2,1)S(1)}, u32[]{:S(2)}, u32[]{:S(2)}) collective-permute-start(bf16[2,328,128]{2,1,0:T(8,128)(2,1)S(1)} %fusion.53), channel_id=1, source_target_pairs={{0,1},{1,0},{2,3},{3,2},{4,5},{5,4},{6,7},{7,6},{8,9},{9,8},{10,11... | collective-permute-start | bytes 503816 | tf_op jit(solution)/shard_map/ppermute | solution.py:180
  40.9 4.5 %collective-permute-start.10 = (bf16[328,128]{1,0:T(8,128)(2,1)S(1)}, bf16[328,128]{1,0:T(8,128)(2,1)S(1)}, u32[]{:S(2)}, u32[]{:S(2)}) collective-permute-start(bf16[328,128]{1,0:T(8,128)(2,1)S(1)} %fusion.96), channel_id=1, source_target_pairs={{0,1},{1,0},{2,3},{3,2},{4,5},{5,4},{6,7},{7,6},{8,9},{9,8},{10,11... | collective-permute-start | bytes 251912 | tf_op jit(solution)/shard_map/ppermute | solution.py:180
  43.2 16.9 %copy-start.3 = (bf16[32,16,1152]{2,1,0:T(8,128)(2,1)S(1)}, bf16[32,16,1152]{2,1,0:T(8,128)(2,1)}, u32[]{:S(2)}) copy-start(bf16[32,16,1152]{2,1,0:T(8,128)(2,1)} %copy-done.2) | copy-start | bytes 3538948
  43.2 4.5 %collective-permute-start.6 = (bf16[328,128]{1,0:T(8,128)(2,1)S(1)}, bf16[328,128]{1,0:T(8,128)(2,1)S(1)}, u32[]{:S(2)}, u32[]{:S(2)}) collective-permute-start(bf16[328,128]{1,0:T(8,128)(2,1)S(1)} %fusion.95), channel_id=1, source_target_pairs={{0,2},{1,3},{2,0},{3,1},{4,6},{5,7},{6,4},{7,5},{8,10},{9,11},{10,... | collective-permute-start | bytes 251912 | tf_op jit(solution)/shard_map/ppermute | solution.py:180
  45.5 5.3 %collective-permute-start.11 = (bf16[328,128]{1,0:T(8,128)(2,1)S(1)}, bf16[328,128]{1,0:T(8,128)(2,1)S(1)}, u32[]{:S(2)}, u32[]{:S(2)}) collective-permute-start(bf16[328,128]{1,0:T(8,128)(2,1)S(1)} %fusion.55), channel_id=1, source_target_pairs={{0,8},{4,12},{8,0},{12,4},{16,24},{20,28},{24,16},{28,20},{1,9},{5... | collective-permute-start | bytes 251912 | tf_op jit(solution)/shard_map/ppermute | solution.py:180
  47.8 5.8 %collective-permute-start.7 = (bf16[328,128]{1,0:T(8,128)(2,1)S(1)}, bf16[328,128]{1,0:T(8,128)(2,1)S(1)}, u32[]{:S(2)}, u32[]{:S(2)}) collective-permute-start(bf16[328,128]{1,0:T(8,128)(2,1)S(1)} %fusion.56), channel_id=1, source_target_pairs={{0,8},{4,12},{8,0},{12,4},{16,24},{20,28},{24,16},{28,20},{1,9},{5... | collective-permute-start | bytes 251912 | tf_op jit(solution)/shard_map/ppermute | solution.py:180
  50.8 7.2 %collective-permute-start.12 = (bf16[328,128]{1,0:T(8,128)(2,1)S(1)}, bf16[328,128]{1,0:T(8,128)(2,1)S(1)}, u32[]{:S(2)}, u32[]{:S(2)}) collective-permute-start(bf16[328,128]{1,0:T(8,128)(2,1)S(1)} %add_convert_fusion.3), channel_id=1, source_target_pairs={{0,16},{4,20},{8,24},{12,28},{16,0},{20,4},{24,8},{28,12},{1,17},{... | collective-permute-start | bytes 251912 | tf_op jit(solution)/shard_map/ppermute | solution.py:180
  53.6 6.3 %collective-permute-start.8 = (bf16[328,128]{1,0:T(8,128)(2,1)S(1)}, bf16[328,128]{1,0:T(8,128)(2,1)S(1)}, u32[]{:S(2)}, u32[]{:S(2)}) collective-permute-start(bf16[328,128]{1,0:T(8,128)(2,1)S(1)} %add_convert_fusion.5), channel_id=1, source_target_pairs={{0,16},{4,20},{8,24},{12,28},{16,0},{20,4},{24,8},{28,12},{1,17},{... | collective-permute-start | bytes 251912 | tf_op jit(solution)/shard_map/ppermute | solution.py:180
  60.0 1.5 %collective-permute-start.13 = (bf16[656,128]{1,0:T(8,128)(2,1)S(1)}, bf16[656,128]{1,0:T(8,128)(2,1)S(1)}, u32[]{:S(2)}, u32[]{:S(2)}) collective-permute-start(bf16[656,128]{1,0:T(8,128)(2,1)S(1)} %pad_maximum_fusion.4), channel_id=1, source_target_pairs={{0,4},{4,0},{8,12},{12,8},{16,20},{20,16},{24,28},{28,24},{1,5},{5... | collective-permute-start | bytes 503816 | tf_op jit(solution)/shard_map/ppermute | solution.py:180

commit v21 on v17

--- a/solution.py
+++ b/solution.py
@@ -160,15 +160,13 @@
         preferred_element_type=jnp.float32,
     )
     up_span = CIN // lon_count
-    up_rows = 16 * up_span
     by_owner = [
         up_taps.reshape(16, lon_count, up_span, COUT).transpose(1, 0, 2, 3),
         mix_owned,
     ]
-    terms = jnp.concatenate([t.reshape(lon_count, -1, COUT) for t in by_owner], axis=1)
-    summed = reduce_terms(terms) * grad_scale
-    up_part = summed[:up_rows].reshape(4, 4, up_span, COUT)
-    mix_part = summed[up_rows:].reshape(3, 3, mix_span, COUT)
+    up_sum, mix_sum = reduce_terms([t.reshape(lon_count, -1, COUT) for t in by_owner])
+    up_part = (up_sum * grad_scale).reshape(4, 4, up_span, COUT)
+    mix_part = (mix_sum * grad_scale).reshape(3, 3, mix_span, COUT)
     return (section_out, input_grad, up_part, mix_part)
 
 
@@ -230,21 +228,29 @@
     return part
 
 
-def reduce_terms(rows):
-    lon_count, count = rows.shape[:2]
+def reduce_terms(terms):
+    lon_count = terms[0].shape[0]
+    sizes = [t.shape[1] for t in terms]
     steps = steps_of(lon_count)
     lat_steps = steps_of(lax.axis_size("lat"))
-    if steps is None or lat_steps is None or count % 4:
+    if steps is None or lat_steps is None or any(n % 2 for n in sizes) or sum(sizes) % 32:
+        rows = jnp.concatenate(terms, axis=1)
         own = lax.axis_index("lon")
         mine = lax.dynamic_index_in_dim(lax.psum(rows, "lon"), own, 0, keepdims=False)
-        return reduce_lat(mine)
-    pair = rows.reshape((lon_count, 2, count // 2) + rows.shape[2:])
-    part = halve(pair, "lat", lat_steps[0], 1)
-    half = count // 6 // 8 * 8
+        summed = reduce_lat(mine)
+        return summed[: sizes[0]], summed[sizes[0] :]
+    kept = [
+        halve(t.reshape((lon_count, 2, t.shape[1] // 2) + t.shape[2:]), "lat", lat_steps[0], 1)
+        for t in terms
+    ]
+    part = jnp.concatenate(kept, axis=1)
+    half = part.shape[1] // 2
     first = scatter_lon(part[:, :half], steps)
     second = scatter_lon(part[:, half:], list(reversed(steps)))
     joined = jnp.concatenate([butterfly(first, lat_steps[1:]), butterfly(second, lat_steps[1:])])
-    return double(joined, "lat", lat_steps[0]).astype(jnp.float32)
+    low, high = jnp.split(double(joined, "lat", lat_steps[0]).astype(jnp.float32), 2)
+    cut = sizes[0] // 2
+    return (jnp.concatenate([low[:cut], high[:cut]]), jnp.concatenate([low[cut:], high[cut:]]))
 
 
 def solution(mesh):

time: 58.9 us -> 62 us (1.053)
  the two profiles are of different devices: /device:TPU:3 before, /device:TPU:0 now
where the time goes in v21:
time: 62 us; the launch traced here: 61.6 us
  waiting for transfers between devices  22.3 us (36%)
  starting transfers between devices  19.5 us (31%)
  local copies, waits for them, and re-layouts  7.89 us (13%)
  other arithmetic  6.04 us (10%)
  matrix products  4.4 us (7%)
  between operations  1.44 us (2%)
    ppermute x11, waiting for transfers between devices, exchange(): return lax.ppermute(part, axis, [(i, i ^ step) for i in range(size)])  14.3 us
    ppermute x11, starting transfers between devices, exchange(): return lax.ppermute(part, axis, [(i, i ^ step) for i in range(size)])  12.9 us
    ppermute x2, starting transfers between devices, swap_edges(): lax.ppermute(jnp.concatenate([p.reshape(-1) for p in leads]), axis, down)  5.24 us
    ppermute x2, waiting for transfers between devices, swap_edges(): lax.ppermute(jnp.concatenate([p.reshape(-1) for p in leads]), axis, down)  4.8 us
    ppermute x2, waiting for transfers between devices, swap_edges(): lax.ppermute(jnp.concatenate([p.reshape(-1) for p in lasts]), axis, up)  3.26 us
    unnamed x51, local copies, waits for them, and re-layouts  2.71 us
    add x4, other arithmetic, halve(): keep + exchange(send.astype(jnp.bfloat16), axis, step).astype(keep.dtype)  2.27 us
    convert_element_type x6, local copies, waits for them, and re-layouts, halve(): send.astype(jnp.bfloat16)  1.66 us
  transfers between devices with their start and end apart: 15, of which 12 were waited for; matrix products, arithmetic and copies ran while one was open for 8% of the time, Pallas kernels for 0%

profile of v21, /device:TPU:0, one launch (start us, length us, event | category | flops | bytes accessed | tf_op | source)
XLA Modules:
  0.0 61.6 jit_solution(12988082554346323662)
XLA Ops:
  0.7 0.9 %multiply_exponential_fusion = f32[16,8,8]{0,2,1:T(8,128)S(1)} fusion(s32[16,8,8]{0,2,1:T(8,128)} %param.7), kind=kLoop, calls=%fused_computation.193 | loop fusion | flops 2048 | bytes 8192 | tf_op jit(solution)/shard_map/exp2 | solution.py:50
  1.6 0.9 %fusion.83 = (bf16[32,2,128]{2,1,0:T(2,128)(2,1)S(1)}, bf16[32,2,128]{2,1,0:T(2,128)(2,1)S(1)}) fusion(bf16[32,16,128]{2,1,0:T(8,128)(2,1)} %param.11), kind=kLoop, calls=%fused_computation.218 | loop fusion | bytes 65536 | tf_op jit(solution)/shard_map/slice | solution.py:23
  2.9 0.3 fusion.66
  3.3 3.9 %collective-permute-start.1 = (bf16[12288]{0:T(1024)(128)(2,1)S(1)}, bf16[12288]{0:T(1024)(128)(2,1)S(1)}, u32[]{:S(2)}, u32[]{:S(2)}) collective-permute-start(bf16[12288]{0:T(1024)(128)(2,1)S(1)} %pad_maximum_fusion.6), channel_id=1, source_target_pairs={{1,0},{2,1},{3,2},{0,3},{5,4},{6,5},{7,6},{4,7},{9,8},{10,9},{11,1... | collective-permute-start | bytes 73736 | tf_op jit(solution)/shard_map/ppermute | solution.py:26
  7.4 1.3 %collective-permute-done.1 = bf16[12288]{0:T(1024)(128)(2,1)S(1)} collective-permute-done((bf16[12288]{0:T(1024)(128)(2,1)S(1)}, bf16[12288]{0:T(1024)(128)(2,1)S(1)}, u32[]{:S(2)}, u32[]{:S(2)}) %collective-permute-start.1) | collective-permute-done | bytes 24608 | tf_op jit(solution)/shard_map/ppermute | solution.py:26
  8.8 3.3 %collective-permute-done = bf16[12288]{0:T(1024)(128)(2,1)S(1)} collective-permute-done((bf16[12288]{0:T(1024)(128)(2,1)S(1)}, bf16[12288]{0:T(1024)(128)(2,1)S(1)}, u32[]{:S(2)}, u32[]{:S(2)}) %collective-permute-start) | collective-permute-done | bytes 24608 | tf_op jit(solution)/shard_map/ppermute | solution.py:25
  12.2 1.3 %collective-permute-start.3 = (bf16[7680]{0:T(1024)(128)(2,1)S(1)}, bf16[7680]{0:T(1024)(128)(2,1)S(1)}, u32[]{:S(2)}, u32[]{:S(2)}) collective-permute-start(bf16[7680]{0:T(1024)(128)(2,1)S(1)} %pad_maximum_fusion.8), channel_id=1, source_target_pairs={{0,4},{4,8},{8,12},{12,16},{16,20},{20,24},{24,28},{1,5},{5,9},{9,... | collective-permute-start | bytes 46088 | tf_op jit(solution)/shard_map/ppermute | solution.py:25
  13.6 1.3 %collective-permute-start.2 = (bf16[7680]{0:T(1024)(128)(2,1)S(1)}, bf16[7680]{0:T(1024)(128)(2,1)S(1)}, u32[]{:S(2)}, u32[]{:S(2)}) collective-permute-start(bf16[7680]{0:T(1024)(128)(2,1)S(1)} %pad_maximum_fusion.7), channel_id=1, source_target_pairs={{4,0},{8,4},{12,8},{16,12},{20,16},{24,20},{28,24},{5,1},{9,5},{13... | collective-permute-start | bytes 46088 | tf_op jit(solution)/shard_map/ppermute | solution.py:26
  15.0 3.5 %collective-permute-done.2 = bf16[7680]{0:T(1024)(128)(2,1)S(1)} collective-permute-done((bf16[7680]{0:T(1024)(128)(2,1)S(1)}, bf16[7680]{0:T(1024)(128)(2,1)S(1)}, u32[]{:S(2)}, u32[]{:S(2)}) %collective-permute-start.2) | collective-permute-done | bytes 15392 | tf_op jit(solution)/shard_map/ppermute | solution.py:26
  18.8 0.7 %convolution_select_fusion = f32[34,8,3,128]{3,1,2,0:T(8,128)S(1)} fusion(bf16[3,3,128,128]{3,2,1,0:T(8,128)(2,1)S(1)} %copy-done, bf16[36,1,7,2,128]{4,2,3,0,1:T(8,128)(2,1)S(1)} %slice.403, bf16[36,1,8,3,128]{4,2,3,0,1:T(8,128)(2,1)S(1)} %copy.29, pred[8,3]{0,1:T(4,128)(4,1)S(1)} %copy-done.11), kind=kOutput, calls=%fused_computation | convolution fusion | flops 241858560 | bytes 1062936 | tf_op jit(solution)/shard_map/conv_general_dilated | solution.py:126
  19.9 0.3 convolution_bitcast_fusion.3
  20.2 0.3 convolution_bitcast_fusion.2
  20.5 0.3 convolution_bitcast_fusion
  20.8 0.3 convolution_bitcast_fusion.1
  21.3 0.2 reshape.238
  21.6 0.2 copy-done.10
  21.8 0.2 broadcast_select_fusion
  23.1 0.5 fusion.71
  23.6 0.2 copy.33
  23.8 0.9 %fusion.4 = bf16[4,512,128]{2,1,0:T(8,128)(2,1)} fusion(f32[4,2,512,128]{3,2,1,0:T(8,128)S(1)} %bitcast.230, s32[]{:T(128)S(6)} %select_n.114), kind=kLoop, calls=%fused_computation.16 | loop fusion | bytes 1048580 | tf_op jit(solution)/shard_map/convert_element_type | solution.py:182
  24.7 2.5 %collective-permute-start.4 = (bf16[4,512,128]{2,1,0:T(8,128)(2,1)}, bf16[4,512,128]{2,1,0:T(8,128)(2,1)}, u32[]{:S(2)}, u32[]{:S(2)}) collective-permute-start(bf16[4,512,128]{2,1,0:T(8,128)(2,1)} %fusion.4), channel_id=1, source_target_pairs={{0,4},{4,0},{8,12},{12,8},{16,20},{20,16},{24,28},{28,24},{1,5},{5... | collective-permute-start | bytes 1572872 | tf_op jit(solution)/shard_map/ppermute | solution.py:175
  27.2 0.5 fusion
  27.8 0.8 %copy-done.2 = f32[4,32,9,128]{3,1,2,0:T(8,128)} copy-done((f32[4,32,9,128]{3,1,2,0:T(8,128)}, f32[4,32,9,128]{3,1,2,0:T(8,128)S(1)}, u32[]{:S(2)}) %copy-start.2) | copy-done | bytes 589848
  28.6 0.7 %fusion.52 = bf16[4,144,128]{2,1,0:T(8,128)(2,1)} fusion(f32[4,2,144,128]{3,2,1,0:T(8,128)S(1)} %bitcast.238, s32[]{:T(128)S(6)} %select_n.114), kind=kLoop, calls=%fused_computation.108 | loop fusion | bytes 294916 | tf_op jit(solution)/shard_map/convert_element_type | solution.py:182
  29.3 1.7 %collective-permute-done.9 = bf16[4,144,128]{2,1,0:T(8,128)(2,1)} collective-permute-done((bf16[4,144,128]{2,1,0:T(8,128)(2,1)}, bf16[4,144,128]{2,1,0:T(8,128)(2,1)}, u32[]{:S(2)}, u32[]{:S(2)}) %collective-permute-start.9) | collective-permute-done | bytes 147488 | tf_op jit(solution)/shard_map/ppermute | solution.py:175
  31.0 1.1 %bitcast_add_fusion.3 = f32[4,144,128]{2,1,0:T(8,128)S(1)} fusion(bf16[4,144,128]{2,1,0:T(8,128)(2,1)} %collective-permute-done.9, f32[4,2,144,128]{3,2,1,0:T(8,128)} %bitcast.239, s32[]{:T(128)S(6)} %select_n.113), kind=kLoop, calls=%fused_computation.46 | loop fusion | flops 147456 | bytes 737284 | tf_op jit(solution)/shard_map/add | solution.py:182
  32.1 1.1 %bitcast_add_fusion = f32[4,512,128]{2,1,0:T(8,128)S(1)} fusion(bf16[4,512,128]{2,1,0:T(8,128)(2,1)} %collective-permute-done.4, f32[4,2,512,128]{3,2,1,0:T(8,128)S(1)} %bitcast.231, s32[]{:T(128)S(6)} %select_n.113), kind=kLoop, calls=%fused_computation.9 | loop fusion | flops 524288 | bytes 2621444 | tf_op jit(solution)/shard_map/add | solution.py:182
  33.4 0.8 %copy-done.8 = bf16[16,8,16,128]{3,0,1,2:T(8,128)(2,1)S(1)} copy-done((bf16[16,8,16,128]{3,0,1,2:T(8,128)(2,1)S(1)}, bf16[16,8,16,128]{3,0,1,2:T(8,128)(2,1)}, u32[]{:S(2)}) %copy-start.8) | copy-done | bytes 524312
  34.3 0.5 fusion.86
  34.7 0.7 %copy.63 = f32[16,8,256,1]{2,1,0,3:T(8,128)} copy(f32[16,8,256,1]{2,0,1,3:T(8,128)S(1)} %fusion.86) | data formatting | bytes 262144 | tf_op jit(solution)/shard_map/rctn,tmn->rcm/dot_general | solution.py:150
  35.5 0.6 collective-permute-start.10
  36.1 3.7 %collective-permute-done.5 = bf16[2,328,128]{2,1,0:T(8,128)(2,1)S(1)} collective-permute-done((bf16[2,328,128]{2,1,0:T(8,128)(2,1)S(1)}, bf16[2,328,128]{2,1,0:T(8,128)(2,1)S(1)}, u32[]{:S(2)}, u32[]{:S(2)}) %collective-permute-start.5) | collective-permute-done | bytes 167968 | tf_op jit(solution)/shard_map/ppermute | solution.py:175
  39.8 0.6 collective-permute-start.6
  40.4 1.5 %collective-permute-done.10 = bf16[2,328,128]{2,1,0:T(8,128)(2,1)S(1)} collective-permute-done((bf16[2,328,128]{2,1,0:T(8,128)(2,1)S(1)}, bf16[2,328,128]{2,1,0:T(8,128)(2,1)S(1)}, u32[]{:S(2)}, u32[]{:S(2)}) %collective-permute-start.10) | collective-permute-done | bytes 167968 | tf_op jit(solution)/shard_map/ppermute | solution.py:175
  42.0 1.3 %collective-permute-start.11 = (bf16[328,128]{1,0:T(8,128)(2,1)S(1)}, bf16[328,128]{1,0:T(8,128)(2,1)S(1)}, u32[]{:S(2)}, u32[]{:S(2)}) collective-permute-start(bf16[328,128]{1,0:T(8,128)(2,1)S(1)} %fusion.70), channel_id=1, source_target_pairs={{0,1},{1,0},{2,3},{3,2},{4,5},{5,4},{6,7},{7,6},{8,9},{9,8},{10,11... | collective-permute-start | bytes 251912 | tf_op jit(solution)/shard_map/ppermute | solution.py:175
  43.3 1.0 %collective-permute-done.6 = bf16[328,128]{1,0:T(8,128)(2,1)S(1)} collective-permute-done((bf16[328,128]{1,0:T(8,128)(2,1)S(1)}, bf16[328,128]{1,0:T(8,128)(2,1)S(1)}, u32[]{:S(2)}, u32[]{:S(2)}) %collective-permute-start.6) | collective-permute-done | bytes 84000 | tf_op jit(solution)/shard_map/ppermute | solution.py:175
  44.4 1.6 %collective-permute-start.7 = (bf16[328,128]{1,0:T(8,128)(2,1)S(1)}, bf16[328,128]{1,0:T(8,128)(2,1)S(1)}, u32[]{:S(2)}, u32[]{:S(2)}) collective-permute-start(bf16[328,128]{1,0:T(8,128)(2,1)S(1)} %fusion.51), channel_id=1, source_target_pairs={{0,8},{4,12},{8,0},{12,4},{16,24},{20,28},{24,16},{28,20},{1,9},{5... | collective-permute-start | bytes 251912 | tf_op jit(solution)/shard_map/ppermute | solution.py:175
  46.0 0.5 collective-permute-done.11
  46.5 1.6 %collective-permute-start.12 = (bf16[328,128]{1,0:T(8,128)(2,1)S(1)}, bf16[328,128]{1,0:T(8,128)(2,1)S(1)}, u32[]{:S(2)}, u32[]{:S(2)}) collective-permute-start(bf16[328,128]{1,0:T(8,128)(2,1)S(1)} %fusion.50), channel_id=1, source_target_pairs={{0,8},{4,12},{8,0},{12,4},{16,24},{20,28},{24,16},{28,20},{1,9},{5... | collective-permute-start | bytes 251912 | tf_op jit(solution)/shard_map/ppermute | solution.py:175
  48.2 0.9 %collective-permute-done.7 = bf16[328,128]{1,0:T(8,128)(2,1)S(1)} collective-permute-done((bf16[328,128]{1,0:T(8,128)(2,1)S(1)}, bf16[328,128]{1,0:T(8,128)(2,1)S(1)}, u32[]{:S(2)}, u32[]{:S(2)}) %collective-permute-start.7) | collective-permute-done | bytes 84000 | tf_op jit(solution)/shard_map/ppermute | solution.py:175
  49.2 2.9 %collective-permute-start.8 = (bf16[328,128]{1,0:T(8,128)(2,1)S(1)}, bf16[328,128]{1,0:T(8,128)(2,1)S(1)}, u32[]{:S(2)}, u32[]{:S(2)}) collective-permute-start(bf16[328,128]{1,0:T(8,128)(2,1)S(1)} %add_convert_fusion.5), channel_id=1, source_target_pairs={{0,16},{4,20},{8,24},{12,28},{16,0},{20,4},{24,8},{28,12},{1,17},{... | collective-permute-start | bytes 251912 | tf_op jit(solution)/shard_map/ppermute | solution.py:175
  52.1 1.6 %collective-permute-start.13 = (bf16[328,128]{1,0:T(8,128)(2,1)S(1)}, bf16[328,128]{1,0:T(8,128)(2,1)S(1)}, u32[]{:S(2)}, u32[]{:S(2)}) collective-permute-start(bf16[328,128]{1,0:T(8,128)(2,1)S(1)} %add_convert_fusion.3), channel_id=1, source_target_pairs={{0,16},{4,20},{8,24},{12,28},{16,0},{20,4},{24,8},{28,12},{1,17},{... | collective-permute-start | bytes 251912 | tf_op jit(solution)/shard_map/ppermute | solution.py:175
  53.8 2.2 %collective-permute-done.8 = bf16[328,128]{1,0:T(8,128)(2,1)S(1)} collective-permute-done((bf16[328,128]{1,0:T(8,128)(2,1)S(1)}, bf16[328,128]{1,0:T(8,128)(2,1)S(1)}, u32[]{:S(2)}, u32[]{:S(2)}) %collective-permute-start.8) | collective-permute-done | bytes 84000 | tf_op jit(solution)/shard_map/ppermute | solution.py:175
  56.0 2.5 %collective-permute-done.13 = bf16[328,128]{1,0:T(8,128)(2,1)S(1)} collective-permute-done((bf16[328,128]{1,0:T(8,128)(2,1)S(1)}, bf16[328,128]{1,0:T(8,128)(2,1)S(1)}, u32[]{:S(2)}, u32[]{:S(2)}) %collective-permute-start.13) | collective-permute-done | bytes 84000 | tf_op jit(solution)/shard_map/ppermute | solution.py:175
  58.6 1.1 %convolution_convert_fusion = bf16[32,16,128]{2,1,0:T(8,128)(2,1)} fusion(bf16[32,16,1152]{2,1,0:T(8,128)(2,1)S(1)} %copy-done.4, bf16[1152,128,1]{1,0,2:T(8,128)(2,1)S(1)} %bitcast.229), kind=kOutput, calls=%fused_computation.4 | convolution fusion | flops 151060480 | bytes 1605632 | tf_op jit(solution)/shard_map/rck,kn->rcn/dot_general | solution.py:138
  59.7 0.2 collective-permute-done.14
  60.1 0.7 %maximum_multiply_fusion.1 = f32[288,128]{1,0:T(8,128)} fusion(f32[144,128]{1,0:T(8,128)S(1)} %get-tuple-element.27, f32[144,128]{1,0:T(8,128)S(1)} %get-tuple-element.26), kind=kLoop, calls=%fused_computation.109 | loop fusion | flops 73728 | bytes 294912 | tf_op jit(solution)/shard_map/mul | solution.py:169
  60.8 0.8 %maximum_multiply_fusion = f32[1024,128]{1,0:T(8,128)} fusion(f32[512,128]{1,0:T(8,128)S(1)} %get-tuple-element.25, f32[512,128]{1,0:T(8,128)S(1)} %get-tuple-element.24), kind=kLoop, calls=%fused_computation.17 | loop fusion | flops 262144 | bytes 1048576 | tf_op jit(solution)/shard_map/mul | solution.py:168
  (120 shorter events, 3.5 us)
Async XLA Ops:
  0.6 18.1 %copy-start = (bf16[3,3,128,128]{3,2,1,0:T(8,128)(2,1)S(1)}, bf16[3,3,128,128]{3,2,1,0:T(8,128)(2,1)}, u32[]{:S(2)}) copy-start(bf16[3,3,128,128]{3,2,1,0:T(8,128)(2,1)} %param.10) | copy-start | bytes 884740
  0.6 2.3 %copy-start.9 = (s32[16,8,256]{2,1,0:T(8,128)S(1)}, s32[16,8,256]{2,1,0:T(8,128)}, u32[]{:S(2)}) copy-start(s32[16,8,256]{2,1,0:T(8,128)} %param.6) | copy-start | bytes 393220
  0.7 6.7 %copy-start.1 = (bf16[4,4,256,128]{3,2,1,0:T(8,128)(2,1)S(1)}, bf16[4,4,256,128]{3,2,1,0:T(8,128)(2,1)}, u32[]{:S(2)}) copy-start(bf16[4,4,256,128]{3,2,1,0:T(8,128)(2,1)} %param.8) | copy-start | bytes 3145732
  3.3 5.5 %collective-permute-start.1 = (bf16[12288]{0:T(1024)(128)(2,1)S(1)}, bf16[12288]{0:T(1024)(128)(2,1)S(1)}, u32[]{:S(2)}, u32[]{:S(2)}) collective-permute-start(bf16[12288]{0:T(1024)(128)(2,1)S(1)} %pad_maximum_fusion.6), channel_id=1, source_target_pairs={{1,0},{2,1},{3,2},{0,3},{5,4},{6,5},{7,6},{4,7},{9,8},{10,9},{11,1... | collective-permute-start | bytes 73736 | tf_op jit(solution)/shard_map/ppermute | solution.py:26
  7.2 4.8 %collective-permute-start = (bf16[12288]{0:T(1024)(128)(2,1)S(1)}, bf16[12288]{0:T(1024)(128)(2,1)S(1)}, u32[]{:S(2)}, u32[]{:S(2)}) collective-permute-start(bf16[12288]{0:T(1024)(128)(2,1)S(1)} %pad_maximum_fusion.5), channel_id=1, source_target_pairs={{0,1},{1,2},{2,3},{3,0},{4,5},{5,6},{6,7},{7,4},{8,9},{9,10},{10,1... | collective-permute-start | bytes 73736 | tf_op jit(solution)/shard_map/ppermute | solution.py:25
  7.3 4.8 %copy-start.5 = (bf16[32,16,128]{2,1,0:T(8,128)(2,1)S(1)}, bf16[32,16,128]{2,1,0:T(8,128)(2,1)}, u32[]{:S(2)}) copy-start(bf16[32,16,128]{2,1,0:T(8,128)(2,1)} %param.11) | copy-start | bytes 393220
  12.2 6.6 %copy-start.11 = (pred[8,3]{0,1:T(4,128)(4,1)S(1)}, pred[8,3]{0,1:T(4,128)(4,1)}, u32[]{:S(2)}) copy-start(pred[8,3]{0,1:T(4,128)(4,1)} %constant.188) | copy-start | bytes 76
  12.2 2.6 %collective-permute-start.3 = (bf16[7680]{0:T(1024)(128)(2,1)S(1)}, bf16[7680]{0:T(1024)(128)(2,1)S(1)}, u32[]{:S(2)}, u32[]{:S(2)}) collective-permute-start(bf16[7680]{0:T(1024)(128)(2,1)S(1)} %pad_maximum_fusion.8), channel_id=1, source_target_pairs={{0,4},{4,8},{8,12},{12,16},{16,20},{20,24},{24,28},{1,5},{5,9},{9,... | collective-permute-start | bytes 46088 | tf_op jit(solution)/shard_map/ppermute | solution.py:25
  13.6 4.9 %collective-permute-start.2 = (bf16[7680]{0:T(1024)(128)(2,1)S(1)}, bf16[7680]{0:T(1024)(128)(2,1)S(1)}, u32[]{:S(2)}, u32[]{:S(2)}) collective-permute-start(bf16[7680]{0:T(1024)(128)(2,1)S(1)} %pad_maximum_fusion.7), channel_id=1, source_target_pairs={{4,0},{8,4},{12,8},{16,12},{20,16},{24,20},{28,24},{5,1},{9,5},{13... | collective-permute-start | bytes 46088 | tf_op jit(solution)/shard_map/ppermute | solution.py:26
  21.1 0.7 %copy-start.10 = (f32[128]{0:T(128)S(1)}, f32[128]{0:T(128)}, u32[]{:S(2)}) copy-start(f32[128]{0:T(128)} %param.9) | copy-start | bytes 1540
  22.3 0.8 %copy-start.7 = (bf16[16,8,16,128]{3,0,1,2:T(8,128)(2,1)}, bf16[16,8,16,128]{3,0,1,2:T(8,128)(2,1)S(1)}, u32[]{:S(2)}) copy-start(bf16[16,8,16,128]{3,0,1,2:T(8,128)(2,1)S(1)} %constant_dynamic-update-slice_fusion) | copy-start | bytes 1572868
  23.1 4.1 %copy-start.3 = (bf16[32,16,1152]{2,1,0:T(8,128)(2,1)}, bf16[32,16,1152]{2,1,0:T(8,128)(2,1)S(1)}, u32[]{:S(2)}) copy-start(bf16[32,16,1152]{2,1,0:T(8,128)(2,1)S(1)} %slice_dynamic-update-slice_fusion) | copy-start | bytes 3538948
  23.6 3.6 %copy-start.6 = (bf16[32,16,128]{2,1,0:T(8,128)(2,1)S(1)}, bf16[32,16,128]{2,1,0:T(8,128)(2,1)}, u32[]{:S(2)}) copy-start(bf16[32,16,128]{2,1,0:T(8,128)(2,1)} %param.11) | copy-start | bytes 393220
  24.7 7.3 %collective-permute-start.4 = (bf16[4,512,128]{2,1,0:T(8,128)(2,1)}, bf16[4,512,128]{2,1,0:T(8,128)(2,1)}, u32[]{:S(2)}, u32[]{:S(2)}) collective-permute-start(bf16[4,512,128]{2,1,0:T(8,128)(2,1)} %fusion.4), channel_id=1, source_target_pairs={{0,4},{4,0},{8,12},{12,8},{16,20},{20,16},{24,28},{28,24},{1,5},{5... | collective-permute-start | bytes 1572872 | tf_op jit(solution)/shard_map/ppermute | solution.py:175
  27.8 0.8 %copy-start.2 = (f32[4,32,9,128]{3,1,2,0:T(8,128)}, f32[4,32,9,128]{3,1,2,0:T(8,128)S(1)}, u32[]{:S(2)}) copy-start(f32[4,32,9,128]{3,1,2,0:T(8,128)S(1)} %copy.36) | copy-start | bytes 1769476
  29.3 1.7 %collective-permute-start.9 = (bf16[4,144,128]{2,1,0:T(8,128)(2,1)}, bf16[4,144,128]{2,1,0:T(8,128)(2,1)}, u32[]{:S(2)}, u32[]{:S(2)}) collective-permute-start(bf16[4,144,128]{2,1,0:T(8,128)(2,1)} %fusion.52), channel_id=1, source_target_pairs={{0,4},{4,0},{8,12},{12,8},{16,20},{20,16},{24,28},{28,24},{1,5},{5... | collective-permute-start | bytes 442376 | tf_op jit(solution)/shard_map/ppermute | solution.py:175
  33.2 1.0 %copy-start.8 = (bf16[16,8,16,128]{3,0,1,2:T(8,128)(2,1)S(1)}, bf16[16,8,16,128]{3,0,1,2:T(8,128)(2,1)}, u32[]{:S(2)}) copy-start(bf16[16,8,16,128]{3,0,1,2:T(8,128)(2,1)} %copy-done.7) | copy-start | bytes 1572868
  33.4 6.4 %collective-permute-start.5 = (bf16[2,328,128]{2,1,0:T(8,128)(2,1)S(1)}, bf16[2,328,128]{2,1,0:T(8,128)(2,1)S(1)}, u32[]{:S(2)}, u32[]{:S(2)}) collective-permute-start(bf16[2,328,128]{2,1,0:T(8,128)(2,1)S(1)} %fusion.48), channel_id=1, source_target_pairs={{0,1},{1,0},{2,3},{3,2},{4,5},{5,4},{6,7},{7,6},{8,9},{9,8},{10,11... | collective-permute-start | bytes 503816 | tf_op jit(solution)/shard_map/ppermute | solution.py:175
  35.5 6.4 %collective-permute-start.10 = (bf16[2,328,128]{2,1,0:T(8,128)(2,1)S(1)}, bf16[2,328,128]{2,1,0:T(8,128)(2,1)S(1)}, u32[]{:S(2)}, u32[]{:S(2)}) collective-permute-start(bf16[2,328,128]{2,1,0:T(8,128)(2,1)S(1)} %fusion.49), channel_id=1, source_target_pairs={{0,2},{1,3},{2,0},{3,1},{4,6},{5,7},{6,4},{7,5},{8,10},{9,11},{10,... | collective-permute-start | bytes 503816 | tf_op jit(solution)/shard_map/ppermute | solution.py:175
  39.8 4.5 %collective-permute-start.6 = (bf16[328,128]{1,0:T(8,128)(2,1)S(1)}, bf16[328,128]{1,0:T(8,128)(2,1)S(1)}, u32[]{:S(2)}, u32[]{:S(2)}) collective-permute-start(bf16[328,128]{1,0:T(8,128)(2,1)S(1)} %fusion.69), channel_id=1, source_target_pairs={{0,2},{1,3},{2,0},{3,1},{4,6},{5,7},{6,4},{7,5},{8,10},{9,11},{10,... | collective-permute-start | bytes 251912 | tf_op jit(solution)/shard_map/ppermute | solution.py:175
  42.0 16.6 %copy-start.4 = (bf16[32,16,1152]{2,1,0:T(8,128)(2,1)S(1)}, bf16[32,16,1152]{2,1,0:T(8,128)(2,1)}, u32[]{:S(2)}) copy-start(bf16[32,16,1152]{2,1,0:T(8,128)(2,1)} %copy-done.3) | copy-start | bytes 3538948
  42.0 4.5 %collective-permute-start.11 = (bf16[328,128]{1,0:T(8,128)(2,1)S(1)}, bf16[328,128]{1,0:T(8,128)(2,1)S(1)}, u32[]{:S(2)}, u32[]{:S(2)}) collective-permute-start(bf16[328,128]{1,0:T(8,128)(2,1)S(1)} %fusion.70), channel_id=1, source_target_pairs={{0,1},{1,0},{2,3},{3,2},{4,5},{5,4},{6,7},{7,6},{8,9},{9,8},{10,11... | collective-permute-start | bytes 251912 | tf_op jit(solution)/shard_map/ppermute | solution.py:175
  44.4 4.8 %collective-permute-start.7 = (bf16[328,128]{1,0:T(8,128)(2,1)S(1)}, bf16[328,128]{1,0:T(8,128)(2,1)S(1)}, u32[]{:S(2)}, u32[]{:S(2)}) collective-permute-start(bf16[328,128]{1,0:T(8,128)(2,1)S(1)} %fusion.51), channel_id=1, source_target_pairs={{0,8},{4,12},{8,0},{12,4},{16,24},{20,28},{24,16},{28,20},{1,9},{5... | collective-permute-start | bytes 251912 | tf_op jit(solution)/shard_map/ppermute | solution.py:175
  46.5 5.5 %collective-permute-start.12 = (bf16[328,128]{1,0:T(8,128)(2,1)S(1)}, bf16[328,128]{1,0:T(8,128)(2,1)S(1)}, u32[]{:S(2)}, u32[]{:S(2)}) collective-permute-start(bf16[328,128]{1,0:T(8,128)(2,1)S(1)} %fusion.50), channel_id=1, source_target_pairs={{0,8},{4,12},{8,0},{12,4},{16,24},{20,28},{24,16},{28,20},{1,9},{5... | collective-permute-start | bytes 251912 | tf_op jit(solution)/shard_map/ppermute | solution.py:175
  49.2 6.8 %collective-permute-start.8 = (bf16[328,128]{1,0:T(8,128)(2,1)S(1)}, bf16[328,128]{1,0:T(8,128)(2,1)S(1)}, u32[]{:S(2)}, u32[]{:S(2)}) collective-permute-start(bf16[328,128]{1,0:T(8,128)(2,1)S(1)} %add_convert_fusion.5), channel_id=1, source_target_pairs={{0,16},{4,20},{8,24},{12,28},{16,0},{20,4},{24,8},{28,12},{1,17},{... | collective-permute-start | bytes 251912 | tf_op jit(solution)/shard_map/ppermute | solution.py:175
  52.1 6.3 %collective-permute-start.13 = (bf16[328,128]{1,0:T(8,128)(2,1)S(1)}, bf16[328,128]{1,0:T(8,128)(2,1)S(1)}, u32[]{:S(2)}, u32[]{:S(2)}) collective-permute-start(bf16[328,128]{1,0:T(8,128)(2,1)S(1)} %add_convert_fusion.3), channel_id=1, source_target_pairs={{0,16},{4,20},{8,24},{12,28},{16,0},{20,4},{24,8},{28,12},{1,17},{... | collective-permute-start | bytes 251912 | tf_op jit(solution)/shard_map/ppermute | solution.py:175
  58.5 1.5 %collective-permute-start.14 = (bf16[656,128]{1,0:T(8,128)(2,1)S(1)}, bf16[656,128]{1,0:T(8,128)(2,1)S(1)}, u32[]{:S(2)}, u32[]{:S(2)}) collective-permute-start(bf16[656,128]{1,0:T(8,128)(2,1)S(1)} %pad_maximum_fusion.3), channel_id=1, source_target_pairs={{0,4},{4,0},{8,12},{12,8},{16,20},{20,16},{24,28},{28,24},{1,5},{5... | collective-permute-start | bytes 503816 | tf_op jit(solution)/shard_map/ppermute | solution.py:175

commit v22 on v15

--- a/solution.py
+++ b/solution.py
@@ -153,16 +153,16 @@
         up_kernel.reshape(16, CIN, COUT),
         preferred_element_type=jnp.float32,
     )
-    up_taps = jnp.einsum(
-        "rctn,rcm->tmn",
+    up_owned = jnp.einsum(
+        "rctn,rcom->otmn",
         grad_patches.reshape(in_rows, in_cols, 16, COUT),
-        inputs,
+        inputs.reshape(in_rows, in_cols, lon_count, CIN // lon_count),
         preferred_element_type=jnp.float32,
     )
     up_span = CIN // lon_count
     up_rows = 16 * up_span
     by_owner = [
-        up_taps.reshape(16, lon_count, up_span, COUT).transpose(1, 0, 2, 3),
+        up_owned,
         mix_owned,
     ]
     terms = jnp.concatenate([t.reshape(lon_count, -1, COUT) for t in by_owner], axis=1)

time: 59 us -> 58.9 us (level)
    dot_general x1 -> x0, local copies, waits for them, and re-layouts: 0.74 us -> none  [shards(): jnp.einsum('rctn,tmn->rcm', grad_patches.reshape(in_rows, in_cols, 16, CO...]
    unnamed x45 -> x46, local copies, waits for them, and re-layouts: 1.67 us -> 2.41 us
where the time goes in v22:
time: 58.9 us; the launch traced here: 58.5 us
  starting transfers between devices  21 us (36%)
  waiting for transfers between devices  20.5 us (35%)
  local copies, waits for them, and re-layouts  7.78 us (13%)
  matrix products  4.4 us (7%)
  other arithmetic  3.5 us (6%)
  between operations  1.42 us (2%)
    ppermute x10, waiting for transfers between devices, exchange(): return lax.ppermute(part, axis, [(i, i ^ step) for i in range(size)])  15.3 us
    ppermute x10, starting transfers between devices, exchange(): return lax.ppermute(part, axis, [(i, i ^ step) for i in range(size)])  12.6 us
    ppermute x2, starting transfers between devices, swap_edges(): lax.ppermute(jnp.concatenate([p.reshape(-1) for p in leads]), axis, down)  5.24 us
    ppermute x2, waiting for transfers between devices, swap_edges(): lax.ppermute(jnp.concatenate([p.reshape(-1) for p in lasts]), axis, up)  3.9 us
    ppermute x2, starting transfers between devices, swap_edges(): lax.ppermute(jnp.concatenate([p.reshape(-1) for p in lasts]), axis, up)  3.09 us
    unnamed x46, local copies, waits for them, and re-layouts  2.41 us
    ppermute x2, waiting for transfers between devices, swap_edges(): lax.ppermute(jnp.concatenate([p.reshape(-1) for p in leads]), axis, down)  1.31 us
    add x3, other arithmetic, halve(): keep + exchange(send.astype(jnp.bfloat16), axis, step).astype(keep.dtype)  1.27 us
  transfers between devices with their start and end apart: 14, of which 11 were waited for; matrix products, arithmetic and copies ran while one was open for 5% of the time, Pallas kernels for 0%

profile of v22, /device:TPU:0, one launch (start us, length us, event | category | flops | bytes accessed | tf_op | source)
XLA Modules:
  0.0 58.5 jit_solution(6406042740266805878)
XLA Ops:
  0.7 1.0 %fusion.82 = (bf16[32,2,128]{2,1,0:T(2,128)(2,1)S(1)}, bf16[32,2,128]{2,1,0:T(2,128)(2,1)S(1)}) fusion(bf16[32,16,128]{2,1,0:T(8,128)(2,1)} %param.11), kind=kLoop, calls=%fused_computation.211 | loop fusion | bytes 65536 | tf_op jit(solution)/shard_map/slice | solution.py:23
  1.7 0.8 %multiply_exponential_fusion = f32[16,8,8]{0,2,1:T(8,128)S(1)} fusion(s32[16,8,8]{0,2,1:T(8,128)} %param.7), kind=kLoop, calls=%fused_computation.187 | loop fusion | flops 2048 | bytes 8192 | tf_op jit(solution)/shard_map/exp2 | solution.py:50
  2.5 0.2 broadcast_in_dim.21
  2.7 0.2 reshape.202
  2.9 0.3 fusion.68
  3.3 3.9 %collective-permute-start.1 = (bf16[12288]{0:T(1024)(128)(2,1)S(1)}, bf16[12288]{0:T(1024)(128)(2,1)S(1)}, u32[]{:S(2)}, u32[]{:S(2)}) collective-permute-start(bf16[12288]{0:T(1024)(128)(2,1)S(1)} %pad_maximum_fusion.6), channel_id=1, source_target_pairs={{1,0},{2,1},{3,2},{0,3},{5,4},{6,5},{7,6},{4,7},{9,8},{10,9},{11,1... | collective-permute-start | bytes 73736 | tf_op jit(solution)/shard_map/ppermute | solution.py:26
  7.5 1.3 %collective-permute-done.1 = bf16[12288]{0:T(1024)(128)(2,1)S(1)} collective-permute-done((bf16[12288]{0:T(1024)(128)(2,1)S(1)}, bf16[12288]{0:T(1024)(128)(2,1)S(1)}, u32[]{:S(2)}, u32[]{:S(2)}) %collective-permute-start.1) | collective-permute-done | bytes 24608 | tf_op jit(solution)/shard_map/ppermute | solution.py:26
  8.8 3.3 %collective-permute-done = bf16[12288]{0:T(1024)(128)(2,1)S(1)} collective-permute-done((bf16[12288]{0:T(1024)(128)(2,1)S(1)}, bf16[12288]{0:T(1024)(128)(2,1)S(1)}, u32[]{:S(2)}, u32[]{:S(2)}) %collective-permute-start) | collective-permute-done | bytes 24608 | tf_op jit(solution)/shard_map/ppermute | solution.py:25
  12.2 1.3 %collective-permute-start.2 = (bf16[7680]{0:T(1024)(128)(2,1)S(1)}, bf16[7680]{0:T(1024)(128)(2,1)S(1)}, u32[]{:S(2)}, u32[]{:S(2)}) collective-permute-start(bf16[7680]{0:T(1024)(128)(2,1)S(1)} %pad_maximum_fusion.7), channel_id=1, source_target_pairs={{4,0},{8,4},{12,8},{16,12},{20,16},{24,20},{28,24},{5,1},{9,5},{13... | collective-permute-start | bytes 46088 | tf_op jit(solution)/shard_map/ppermute | solution.py:26
  13.6 3.0 %collective-permute-start.3 = (bf16[7680]{0:T(1024)(128)(2,1)S(1)}, bf16[7680]{0:T(1024)(128)(2,1)S(1)}, u32[]{:S(2)}, u32[]{:S(2)}) collective-permute-start(bf16[7680]{0:T(1024)(128)(2,1)S(1)} %pad_maximum_fusion.8), channel_id=1, source_target_pairs={{0,4},{4,8},{8,12},{12,16},{16,20},{20,24},{24,28},{1,5},{5,9},{9,... | collective-permute-start | bytes 46088 | tf_op jit(solution)/shard_map/ppermute | solution.py:25
  16.8 0.6 %collective-permute-done.3 = bf16[7680]{0:T(1024)(128)(2,1)S(1)} collective-permute-done((bf16[7680]{0:T(1024)(128)(2,1)S(1)}, bf16[7680]{0:T(1024)(128)(2,1)S(1)}, u32[]{:S(2)}, u32[]{:S(2)}) %collective-permute-start.3) | collective-permute-done | bytes 15392 | tf_op jit(solution)/shard_map/ppermute | solution.py:25
  17.6 0.3 convolution_bitcast_fusion.1
  17.8 0.3 convolution_bitcast_fusion.2
  18.2 0.3 convolution_bitcast_fusion.3
  18.5 0.3 convolution_bitcast_fusion.4
  18.8 0.2 copy.61
  19.0 0.2 reshape.250
  19.2 0.2 copy-done.7
  20.5 0.2 copy-done.8
  20.7 0.7 %convolution_select_fusion = f32[34,8,3,128]{3,1,2,0:T(8,128)S(1)} fusion(bf16[3,3,128,128]{3,2,1,0:T(8,128)(2,1)S(1)} %copy-done, bf16[36,1,7,2,128]{4,2,3,0,1:T(8,128)(2,1)S(1)} %slice.391, bf16[36,1,8,3,128]{4,2,3,0,1:T(8,128)(2,1)S(1)} %copy.50, pred[8,3]{0,1:T(4,128)(4,1)S(1)} %copy-done.8), kind=kOutput, calls=%fused_computation.3 | convolution fusion | flops 241858560 | bytes 1062936 | tf_op jit(solution)/shard_map/conv_general_dilated | solution.py:126
  21.5 0.2 squeeze.107
  21.7 0.2 broadcast_select_fusion
  22.2 0.5 fusion
  22.8 0.5 fusion.5
  23.3 0.2 pad_maximum_fusion
  23.4 0.9 %fusion.4 = bf16[4,656,128]{2,1,0:T(8,128)(2,1)} fusion(f32[4,2,656,128]{3,2,1,0:T(8,128)S(1)} %bitcast.222, s32[]{:T(128)S(6)} %select_n.108), kind=kLoop, calls=%fused_computation.15 | loop fusion | bytes 1343492 | tf_op jit(solution)/shard_map/convert_element_type | solution.py:184
  24.4 1.2 %collective-permute-start.4 = (bf16[4,656,128]{2,1,0:T(8,128)(2,1)}, bf16[4,656,128]{2,1,0:T(8,128)(2,1)}, u32[]{:S(2)}, u32[]{:S(2)}) collective-permute-start(bf16[4,656,128]{2,1,0:T(8,128)(2,1)} %fusion.4), channel_id=1, source_target_pairs={{0,4},{4,0},{8,12},{12,8},{16,20},{20,16},{24,28},{28,24},{1,5},{5... | collective-permute-start | bytes 2015240 | tf_op jit(solution)/shard_map/ppermute | solution.py:177
  25.6 2.1 %collective-permute-done.4 = bf16[4,656,128]{2,1,0:T(8,128)(2,1)} collective-permute-done((bf16[4,656,128]{2,1,0:T(8,128)(2,1)}, bf16[4,656,128]{2,1,0:T(8,128)(2,1)}, u32[]{:S(2)}, u32[]{:S(2)}) %collective-permute-start.4) | collective-permute-done | bytes 671776 | tf_op jit(solution)/shard_map/ppermute | solution.py:177
  27.7 1.2 %bitcast_add_fusion = f32[4,656,128]{2,1,0:T(8,128)S(1)} fusion(bf16[4,656,128]{2,1,0:T(8,128)(2,1)} %collective-permute-done.4, f32[4,2,656,128]{3,2,1,0:T(8,128)S(1)} %bitcast.223, s32[]{:T(128)S(6)} %select_n.107), kind=kLoop, calls=%fused_computation.1 | loop fusion | flops 671744 | bytes 3358724 | tf_op jit(solution)/shard_map/add | solution.py:184
  29.1 0.6 collective-permute-start.9
  29.6 0.5 copy-done.2
  30.1 0.5 convolution_bitcast_fusion
  30.6 0.7 %copy.56 = f32[16,8,256]{2,1,0:T(8,128)} copy(f32[16,8,256]{2,0,1:T(8,128)S(1)} %convolution_bitcast_fusion) | data formatting | bytes 262144
  31.5 4.3 %collective-permute-done.9 = bf16[2,328,128]{2,1,0:T(8,128)(2,1)S(1)} collective-permute-done((bf16[2,328,128]{2,1,0:T(8,128)(2,1)S(1)}, bf16[2,328,128]{2,1,0:T(8,128)(2,1)S(1)}, u32[]{:S(2)}, u32[]{:S(2)}) %collective-permute-start.9) | collective-permute-done | bytes 167968 | tf_op jit(solution)/shard_map/ppermute | solution.py:177
  35.9 2.2 %collective-permute-done.5 = bf16[2,328,128]{2,1,0:T(8,128)(2,1)S(1)} collective-permute-done((bf16[2,328,128]{2,1,0:T(8,128)(2,1)S(1)}, bf16[2,328,128]{2,1,0:T(8,128)(2,1)S(1)}, u32[]{:S(2)}, u32[]{:S(2)}) %collective-permute-start.5) | collective-permute-done | bytes 167968 | tf_op jit(solution)/shard_map/ppermute | solution.py:177
  38.1 0.9 %collective-permute-start.6 = (bf16[328,128]{1,0:T(8,128)(2,1)S(1)}, bf16[328,128]{1,0:T(8,128)(2,1)S(1)}, u32[]{:S(2)}, u32[]{:S(2)}) collective-permute-start(bf16[328,128]{1,0:T(8,128)(2,1)S(1)} %fusion.71), channel_id=1, source_target_pairs={{0,2},{1,3},{2,0},{3,1},{4,6},{5,7},{6,4},{7,5},{8,10},{9,11},{10,... | collective-permute-start | bytes 251912 | tf_op jit(solution)/shard_map/ppermute | solution.py:177
  39.1 1.3 %collective-permute-done.10 = bf16[328,128]{1,0:T(8,128)(2,1)S(1)} collective-permute-done((bf16[328,128]{1,0:T(8,128)(2,1)S(1)}, bf16[328,128]{1,0:T(8,128)(2,1)S(1)}, u32[]{:S(2)}, u32[]{:S(2)}) %collective-permute-start.10) | collective-permute-done | bytes 84000 | tf_op jit(solution)/shard_map/ppermute | solution.py:177
  40.4 2.4 %collective-permute-start.11 = (bf16[328,128]{1,0:T(8,128)(2,1)S(1)}, bf16[328,128]{1,0:T(8,128)(2,1)S(1)}, u32[]{:S(2)}, u32[]{:S(2)}) collective-permute-start(bf16[328,128]{1,0:T(8,128)(2,1)S(1)} %fusion.52), channel_id=1, source_target_pairs={{0,8},{4,12},{8,0},{12,4},{16,24},{20,28},{24,16},{28,20},{1,9},{5... | collective-permute-start | bytes 251912 | tf_op jit(solution)/shard_map/ppermute | solution.py:177
  42.7 2.5 %collective-permute-start.7 = (bf16[328,128]{1,0:T(8,128)(2,1)S(1)}, bf16[328,128]{1,0:T(8,128)(2,1)S(1)}, u32[]{:S(2)}, u32[]{:S(2)}) collective-permute-start(bf16[328,128]{1,0:T(8,128)(2,1)S(1)} %fusion.53), channel_id=1, source_target_pairs={{0,8},{4,12},{8,0},{12,4},{16,24},{20,28},{24,16},{28,20},{1,9},{5... | collective-permute-start | bytes 251912 | tf_op jit(solution)/shard_map/ppermute | solution.py:177
  45.2 0.7 %collective-permute-done.11 = bf16[328,128]{1,0:T(8,128)(2,1)S(1)} collective-permute-done((bf16[328,128]{1,0:T(8,128)(2,1)S(1)}, bf16[328,128]{1,0:T(8,128)(2,1)S(1)}, u32[]{:S(2)}, u32[]{:S(2)}) %collective-permute-start.11) | collective-permute-done | bytes 84000 | tf_op jit(solution)/shard_map/ppermute | solution.py:177
  45.9 3.1 %collective-permute-start.12 = (bf16[328,128]{1,0:T(8,128)(2,1)S(1)}, bf16[328,128]{1,0:T(8,128)(2,1)S(1)}, u32[]{:S(2)}, u32[]{:S(2)}) collective-permute-start(bf16[328,128]{1,0:T(8,128)(2,1)S(1)} %add_convert_fusion.3), channel_id=1, source_target_pairs={{0,16},{4,20},{8,24},{12,28},{16,0},{20,4},{24,8},{28,12},{1,17},{... | collective-permute-start | bytes 251912 | tf_op jit(solution)/shard_map/ppermute | solution.py:177
  49.1 1.7 %collective-permute-start.8 = (bf16[328,128]{1,0:T(8,128)(2,1)S(1)}, bf16[328,128]{1,0:T(8,128)(2,1)S(1)}, u32[]{:S(2)}, u32[]{:S(2)}) collective-permute-start(bf16[328,128]{1,0:T(8,128)(2,1)S(1)} %add_convert_fusion.5), channel_id=1, source_target_pairs={{0,16},{4,20},{8,24},{12,28},{16,0},{20,4},{24,8},{28,12},{1,17},{... | collective-permute-start | bytes 251912 | tf_op jit(solution)/shard_map/ppermute | solution.py:177
  50.8 2.3 %collective-permute-done.12 = bf16[328,128]{1,0:T(8,128)(2,1)S(1)} collective-permute-done((bf16[328,128]{1,0:T(8,128)(2,1)S(1)}, bf16[328,128]{1,0:T(8,128)(2,1)S(1)}, u32[]{:S(2)}, u32[]{:S(2)}) %collective-permute-start.12) | collective-permute-done | bytes 84000 | tf_op jit(solution)/shard_map/ppermute | solution.py:177
  53.2 2.2 %collective-permute-done.8 = bf16[328,128]{1,0:T(8,128)(2,1)S(1)} collective-permute-done((bf16[328,128]{1,0:T(8,128)(2,1)S(1)}, bf16[328,128]{1,0:T(8,128)(2,1)S(1)}, u32[]{:S(2)}, u32[]{:S(2)}) %collective-permute-start.8) | collective-permute-done | bytes 84000 | tf_op jit(solution)/shard_map/ppermute | solution.py:177
  55.5 1.1 %convolution_convert_fusion = bf16[32,16,128]{2,1,0:T(8,128)(2,1)} fusion(bf16[32,16,1152]{2,1,0:T(8,128)(2,1)S(1)} %copy-done.4, bf16[1152,128,1]{1,0,2:T(8,128)(2,1)S(1)} %bitcast.220), kind=kOutput, calls=%fused_computation.7 | convolution fusion | flops 151060480 | bytes 1605632 | tf_op jit(solution)/shard_map/rck,kn->rcn/dot_general | solution.py:138
  56.7 0.2 collective-permute-done.13
  57.0 0.8 %slice.411 = f32[1024,128]{1,0:T(8,128)} slice(f32[1312,128]{1,0:T(8,128)S(1)} %convert_multiply_fusion), slice={[0:1024], [0:128]} | slice | bytes 1048576 | tf_op jit(solution)/shard_map/slice | solution.py:170
  57.9 0.7 %slice.412 = f32[288,128]{1,0:T(8,128)} slice(f32[1312,128]{1,0:T(8,128)S(1)} %convert_multiply_fusion), slice={[1024:1312], [0:128]} | slice | bytes 294912 | tf_op jit(solution)/shard_map/slice | solution.py:171
  (109 shorter events, 2.8 us)
Async XLA Ops:
  0.6 19.8 %copy-start = (bf16[3,3,128,128]{3,2,1,0:T(8,128)(2,1)S(1)}, bf16[3,3,128,128]{3,2,1,0:T(8,128)(2,1)}, u32[]{:S(2)}) copy-start(bf16[3,3,128,128]{3,2,1,0:T(8,128)(2,1)} %param.10) | copy-start | bytes 884740
  0.6 2.3 %copy-start.6 = (s32[16,8,256]{2,1,0:T(8,128)S(1)}, s32[16,8,256]{2,1,0:T(8,128)}, u32[]{:S(2)}) copy-start(s32[16,8,256]{2,1,0:T(8,128)} %param.6) | copy-start | bytes 393220
  0.7 6.7 %copy-start.1 = (bf16[4,4,256,128]{3,2,1,0:T(8,128)(2,1)S(1)}, bf16[4,4,256,128]{3,2,1,0:T(8,128)(2,1)}, u32[]{:S(2)}) copy-start(bf16[4,4,256,128]{3,2,1,0:T(8,128)(2,1)} %param.8) | copy-start | bytes 3145732
  3.2 8.8 %copy-start.5 = (bf16[32,16,128]{2,1,0:T(8,128)(2,1)S(1)}, bf16[32,16,128]{2,1,0:T(8,128)(2,1)}, u32[]{:S(2)}) copy-start(bf16[32,16,128]{2,1,0:T(8,128)(2,1)} %param.11) | copy-start | bytes 393220
  3.3 5.5 %collective-permute-start.1 = (bf16[12288]{0:T(1024)(128)(2,1)S(1)}, bf16[12288]{0:T(1024)(128)(2,1)S(1)}, u32[]{:S(2)}, u32[]{:S(2)}) collective-permute-start(bf16[12288]{0:T(1024)(128)(2,1)S(1)} %pad_maximum_fusion.6), channel_id=1, source_target_pairs={{1,0},{2,1},{3,2},{0,3},{5,4},{6,5},{7,6},{4,7},{9,8},{10,9},{11,1... | collective-permute-start | bytes 73736 | tf_op jit(solution)/shard_map/ppermute | solution.py:26
  7.3 4.8 %collective-permute-start = (bf16[12288]{0:T(1024)(128)(2,1)S(1)}, bf16[12288]{0:T(1024)(128)(2,1)S(1)}, u32[]{:S(2)}, u32[]{:S(2)}) collective-permute-start(bf16[12288]{0:T(1024)(128)(2,1)S(1)} %pad_maximum_fusion.5), channel_id=1, source_target_pairs={{0,1},{1,2},{2,3},{3,0},{4,5},{5,6},{6,7},{7,4},{8,9},{9,10},{10,1... | collective-permute-start | bytes 73736 | tf_op jit(solution)/shard_map/ppermute | solution.py:25
  12.2 4.5 %collective-permute-start.2 = (bf16[7680]{0:T(1024)(128)(2,1)S(1)}, bf16[7680]{0:T(1024)(128)(2,1)S(1)}, u32[]{:S(2)}, u32[]{:S(2)}) collective-permute-start(bf16[7680]{0:T(1024)(128)(2,1)S(1)} %pad_maximum_fusion.7), channel_id=1, source_target_pairs={{4,0},{8,4},{12,8},{16,12},{20,16},{24,20},{28,24},{5,1},{9,5},{13... | collective-permute-start | bytes 46088 | tf_op jit(solution)/shard_map/ppermute | solution.py:26
  13.6 3.9 %collective-permute-start.3 = (bf16[7680]{0:T(1024)(128)(2,1)S(1)}, bf16[7680]{0:T(1024)(128)(2,1)S(1)}, u32[]{:S(2)}, u32[]{:S(2)}) collective-permute-start(bf16[7680]{0:T(1024)(128)(2,1)S(1)} %pad_maximum_fusion.8), channel_id=1, source_target_pairs={{0,4},{4,8},{8,12},{12,16},{16,20},{20,24},{24,28},{1,5},{5,9},{9,... | collective-permute-start | bytes 46088 | tf_op jit(solution)/shard_map/ppermute | solution.py:25
  18.8 0.7 %copy-start.7 = (f32[128]{0:T(128)S(1)}, f32[128]{0:T(128)}, u32[]{:S(2)}) copy-start(f32[128]{0:T(128)} %param.9) | copy-start | bytes 1540
  20.0 0.7 %copy-start.8 = (pred[8,3]{0,1:T(4,128)(4,1)S(1)}, pred[8,3]{0,1:T(4,128)(4,1)}, u32[]{:S(2)}) copy-start(pred[8,3]{0,1:T(4,128)(4,1)} %constant.177) | copy-start | bytes 76
  20.1 2.1 %copy-start.3 = (bf16[32,16,1152]{2,1,0:T(8,128)(2,1)}, bf16[32,16,1152]{2,1,0:T(8,128)(2,1)S(1)}, u32[]{:S(2)}) copy-start(bf16[32,16,1152]{2,1,0:T(8,128)(2,1)S(1)} %slice_dynamic-update-slice_fusion) | copy-start | bytes 3538948
  24.4 3.3 %collective-permute-start.4 = (bf16[4,656,128]{2,1,0:T(8,128)(2,1)}, bf16[4,656,128]{2,1,0:T(8,128)(2,1)}, u32[]{:S(2)}, u32[]{:S(2)}) collective-permute-start(bf16[4,656,128]{2,1,0:T(8,128)(2,1)} %fusion.4), channel_id=1, source_target_pairs={{0,4},{4,0},{8,12},{12,8},{16,20},{20,16},{24,28},{28,24},{1,5},{5... | collective-permute-start | bytes 2015240 | tf_op jit(solution)/shard_map/ppermute | solution.py:177
  28.9 1.2 %copy-start.2 = (bf16[4,4,256,128]{3,2,1,0:T(8,128)(2,1)S(1)}, bf16[4,4,256,128]{3,2,1,0:T(8,128)(2,1)}, u32[]{:S(2)}) copy-start(bf16[4,4,256,128]{3,2,1,0:T(8,128)(2,1)} %param.8) | copy-start | bytes 3145732
  29.1 6.7 %collective-permute-start.9 = (bf16[2,328,128]{2,1,0:T(8,128)(2,1)S(1)}, bf16[2,328,128]{2,1,0:T(8,128)(2,1)S(1)}, u32[]{:S(2)}, u32[]{:S(2)}) collective-permute-start(bf16[2,328,128]{2,1,0:T(8,128)(2,1)S(1)} %fusion.51), channel_id=1, source_target_pairs={{0,2},{1,3},{2,0},{3,1},{4,6},{5,7},{6,4},{7,5},{8,10},{9,11},{10,... | collective-permute-start | bytes 503816 | tf_op jit(solution)/shard_map/ppermute | solution.py:177
  31.4 6.7 %collective-permute-start.5 = (bf16[2,328,128]{2,1,0:T(8,128)(2,1)S(1)}, bf16[2,328,128]{2,1,0:T(8,128)(2,1)S(1)}, u32[]{:S(2)}, u32[]{:S(2)}) collective-permute-start(bf16[2,328,128]{2,1,0:T(8,128)(2,1)S(1)} %fusion.50), channel_id=1, source_target_pairs={{0,1},{1,0},{2,3},{3,2},{4,5},{5,4},{6,7},{7,6},{8,9},{9,8},{10,11... | collective-permute-start | bytes 503816 | tf_op jit(solution)/shard_map/ppermute | solution.py:177
  35.8 4.5 %collective-permute-start.10 = (bf16[328,128]{1,0:T(8,128)(2,1)S(1)}, bf16[328,128]{1,0:T(8,128)(2,1)S(1)}, u32[]{:S(2)}, u32[]{:S(2)}) collective-permute-start(bf16[328,128]{1,0:T(8,128)(2,1)S(1)} %fusion.72), channel_id=1, source_target_pairs={{0,1},{1,0},{2,3},{3,2},{4,5},{5,4},{6,7},{7,6},{8,9},{9,8},{10,11... | collective-permute-start | bytes 251912 | tf_op jit(solution)/shard_map/ppermute | solution.py:177
  38.1 17.4 %copy-start.4 = (bf16[32,16,1152]{2,1,0:T(8,128)(2,1)S(1)}, bf16[32,16,1152]{2,1,0:T(8,128)(2,1)}, u32[]{:S(2)}) copy-start(bf16[32,16,1152]{2,1,0:T(8,128)(2,1)} %copy-done.3) | copy-start | bytes 3538948
  38.1 4.6 %collective-permute-start.6 = (bf16[328,128]{1,0:T(8,128)(2,1)S(1)}, bf16[328,128]{1,0:T(8,128)(2,1)S(1)}, u32[]{:S(2)}, u32[]{:S(2)}) collective-permute-start(bf16[328,128]{1,0:T(8,128)(2,1)S(1)} %fusion.71), channel_id=1, source_target_pairs={{0,2},{1,3},{2,0},{3,1},{4,6},{5,7},{6,4},{7,5},{8,10},{9,11},{10,... | collective-permute-start | bytes 251912 | tf_op jit(solution)/shard_map/ppermute | solution.py:177
  40.4 5.5 %collective-permute-start.11 = (bf16[328,128]{1,0:T(8,128)(2,1)S(1)}, bf16[328,128]{1,0:T(8,128)(2,1)S(1)}, u32[]{:S(2)}, u32[]{:S(2)}) collective-permute-start(bf16[328,128]{1,0:T(8,128)(2,1)S(1)} %fusion.52), channel_id=1, source_target_pairs={{0,8},{4,12},{8,0},{12,4},{16,24},{20,28},{24,16},{28,20},{1,9},{5... | collective-permute-start | bytes 251912 | tf_op jit(solution)/shard_map/ppermute | solution.py:177
  42.7 6.3 %collective-permute-start.7 = (bf16[328,128]{1,0:T(8,128)(2,1)S(1)}, bf16[328,128]{1,0:T(8,128)(2,1)S(1)}, u32[]{:S(2)}, u32[]{:S(2)}) collective-permute-start(bf16[328,128]{1,0:T(8,128)(2,1)S(1)} %fusion.53), channel_id=1, source_target_pairs={{0,8},{4,12},{8,0},{12,4},{16,24},{20,28},{24,16},{28,20},{1,9},{5... | collective-permute-start | bytes 251912 | tf_op jit(solution)/shard_map/ppermute | solution.py:177
  45.9 7.2 %collective-permute-start.12 = (bf16[328,128]{1,0:T(8,128)(2,1)S(1)}, bf16[328,128]{1,0:T(8,128)(2,1)S(1)}, u32[]{:S(2)}, u32[]{:S(2)}) collective-permute-start(bf16[328,128]{1,0:T(8,128)(2,1)S(1)} %add_convert_fusion.3), channel_id=1, source_target_pairs={{0,16},{4,20},{8,24},{12,28},{16,0},{20,4},{24,8},{28,12},{1,17},{... | collective-permute-start | bytes 251912 | tf_op jit(solution)/shard_map/ppermute | solution.py:177
  49.1 6.3 %collective-permute-start.8 = (bf16[328,128]{1,0:T(8,128)(2,1)S(1)}, bf16[328,128]{1,0:T(8,128)(2,1)S(1)}, u32[]{:S(2)}, u32[]{:S(2)}) collective-permute-start(bf16[328,128]{1,0:T(8,128)(2,1)S(1)} %add_convert_fusion.5), channel_id=1, source_target_pairs={{0,16},{4,20},{8,24},{12,28},{16,0},{20,4},{24,8},{28,12},{1,17},{... | collective-permute-start | bytes 251912 | tf_op jit(solution)/shard_map/ppermute | solution.py:177
  55.5 1.5 %collective-permute-start.13 = (bf16[656,128]{1,0:T(8,128)(2,1)S(1)}, bf16[656,128]{1,0:T(8,128)(2,1)S(1)}, u32[]{:S(2)}, u32[]{:S(2)}) collective-permute-start(bf16[656,128]{1,0:T(8,128)(2,1)S(1)} %pad_maximum_fusion.3), channel_id=1, source_target_pairs={{0,4},{4,0},{8,12},{12,8},{16,20},{20,16},{24,28},{28,24},{1,5},{5... | collective-permute-start | bytes 503816 | tf_op jit(solution)/shard_map/ppermute | solution.py:177

commit v23 on v15

--- a/solution.py
+++ b/solution.py
@@ -243,7 +243,8 @@
     half = count // 4
     first = scatter_lon(part[:, :half], steps)
     second = scatter_lon(part[:, half:], list(reversed(steps)))
-    joined = jnp.concatenate([butterfly(first, lat_steps[1:]), butterfly(second, lat_steps[1:])])
+    order = list(reversed(lat_steps[1:]))
+    joined = jnp.concatenate([butterfly(first, order), butterfly(second, order)])
     return double(joined, "lat", lat_steps[0]).astype(jnp.float32)
 
 

time: 59 us -> 58.6 us (level)
  starting transfers between devices: 20.9 us -> 20 us
  waiting for transfers between devices: 20.6 us -> 21.2 us
    ppermute x10, starting transfers between devices: 12.6 us -> 11.6 us  [exchange(): return lax.ppermute(part, axis, [(i, i ^ step) for i in range(size)])]
    ppermute x10, waiting for transfers between devices: 15.3 us -> 15.9 us  [exchange(): return lax.ppermute(part, axis, [(i, i ^ step) for i in range(size)])]
where the time goes in v23:
time: 58.6 us; the launch traced here: 58.3 us
  waiting for transfers between devices  21.2 us (36%)
  starting transfers between devices  20 us (34%)
  local copies, waits for them, and re-layouts  7.81 us (13%)
  matrix products  4.4 us (8%)
  other arithmetic  3.51 us (6%)
  between operations  1.42 us (2%)
    ppermute x10, waiting for transfers between devices, exchange(): return lax.ppermute(part, axis, [(i, i ^ step) for i in range(size)])  15.9 us
    ppermute x10, starting transfers between devices, exchange(): return lax.ppermute(part, axis, [(i, i ^ step) for i in range(size)])  11.6 us
    ppermute x2, starting transfers between devices, swap_edges(): lax.ppermute(jnp.concatenate([p.reshape(-1) for p in leads]), axis, down)  5.24 us
    ppermute x2, waiting for transfers between devices, swap_edges(): lax.ppermute(jnp.concatenate([p.reshape(-1) for p in lasts]), axis, up)  4.02 us
    ppermute x2, starting transfers between devices, swap_edges(): lax.ppermute(jnp.concatenate([p.reshape(-1) for p in lasts]), axis, up)  3.09 us
    unnamed x45, local copies, waits for them, and re-layouts  1.67 us
    ppermute x2, waiting for transfers between devices, swap_edges(): lax.ppermute(jnp.concatenate([p.reshape(-1) for p in leads]), axis, down)  1.3 us
    add x3, other arithmetic, halve(): keep + exchange(send.astype(jnp.bfloat16), axis, step).astype(keep.dtype)  1.28 us
  transfers between devices with their start and end apart: 14, of which 11 were waited for; matrix products, arithmetic and copies ran while one was open for 5% of the time, Pallas kernels for 0%

profile of v23, /device:TPU:0, one launch (start us, length us, event | category | flops | bytes accessed | tf_op | source)
XLA Modules:
  0.0 58.3 jit_solution(14791718595382836141)
XLA Ops:
  0.7 1.0 %fusion.81 = (bf16[32,2,128]{2,1,0:T(2,128)(2,1)S(1)}, bf16[32,2,128]{2,1,0:T(2,128)(2,1)S(1)}) fusion(bf16[32,16,128]{2,1,0:T(8,128)(2,1)} %param.11), kind=kLoop, calls=%fused_computation.210 | loop fusion | bytes 65536 | tf_op jit(solution)/shard_map/slice | solution.py:23
  1.7 0.8 %multiply_exponential_fusion = f32[16,8,8]{0,2,1:T(8,128)S(1)} fusion(s32[16,8,8]{0,2,1:T(8,128)} %param.7), kind=kLoop, calls=%fused_computation.186 | loop fusion | flops 2048 | bytes 8192 | tf_op jit(solution)/shard_map/exp2 | solution.py:50
  2.5 0.2 broadcast_in_dim.21
  2.7 0.2 reshape.202
  2.9 0.3 fusion.65
  3.3 3.9 %collective-permute-start.1 = (bf16[12288]{0:T(1024)(128)(2,1)S(1)}, bf16[12288]{0:T(1024)(128)(2,1)S(1)}, u32[]{:S(2)}, u32[]{:S(2)}) collective-permute-start(bf16[12288]{0:T(1024)(128)(2,1)S(1)} %pad_maximum_fusion.6), channel_id=1, source_target_pairs={{1,0},{2,1},{3,2},{0,3},{5,4},{6,5},{7,6},{4,7},{9,8},{10,9},{11,1... | collective-permute-start | bytes 73736 | tf_op jit(solution)/shard_map/ppermute | solution.py:26
  7.5 1.3 %collective-permute-done.1 = bf16[12288]{0:T(1024)(128)(2,1)S(1)} collective-permute-done((bf16[12288]{0:T(1024)(128)(2,1)S(1)}, bf16[12288]{0:T(1024)(128)(2,1)S(1)}, u32[]{:S(2)}, u32[]{:S(2)}) %collective-permute-start.1) | collective-permute-done | bytes 24608 | tf_op jit(solution)/shard_map/ppermute | solution.py:26
  8.8 3.3 %collective-permute-done = bf16[12288]{0:T(1024)(128)(2,1)S(1)} collective-permute-done((bf16[12288]{0:T(1024)(128)(2,1)S(1)}, bf16[12288]{0:T(1024)(128)(2,1)S(1)}, u32[]{:S(2)}, u32[]{:S(2)}) %collective-permute-start) | collective-permute-done | bytes 24608 | tf_op jit(solution)/shard_map/ppermute | solution.py:25
  12.2 1.3 %collective-permute-start.2 = (bf16[7680]{0:T(1024)(128)(2,1)S(1)}, bf16[7680]{0:T(1024)(128)(2,1)S(1)}, u32[]{:S(2)}, u32[]{:S(2)}) collective-permute-start(bf16[7680]{0:T(1024)(128)(2,1)S(1)} %pad_maximum_fusion.7), channel_id=1, source_target_pairs={{4,0},{8,4},{12,8},{16,12},{20,16},{24,20},{28,24},{5,1},{9,5},{13... | collective-permute-start | bytes 46088 | tf_op jit(solution)/shard_map/ppermute | solution.py:26
  13.6 3.0 %collective-permute-start.3 = (bf16[7680]{0:T(1024)(128)(2,1)S(1)}, bf16[7680]{0:T(1024)(128)(2,1)S(1)}, u32[]{:S(2)}, u32[]{:S(2)}) collective-permute-start(bf16[7680]{0:T(1024)(128)(2,1)S(1)} %pad_maximum_fusion.8), channel_id=1, source_target_pairs={{0,4},{4,8},{8,12},{12,16},{16,20},{20,24},{24,28},{1,5},{5,9},{9,... | collective-permute-start | bytes 46088 | tf_op jit(solution)/shard_map/ppermute | solution.py:25
  16.7 0.8 %collective-permute-done.3 = bf16[7680]{0:T(1024)(128)(2,1)S(1)} collective-permute-done((bf16[7680]{0:T(1024)(128)(2,1)S(1)}, bf16[7680]{0:T(1024)(128)(2,1)S(1)}, u32[]{:S(2)}, u32[]{:S(2)}) %collective-permute-start.3) | collective-permute-done | bytes 15392 | tf_op jit(solution)/shard_map/ppermute | solution.py:25
  17.6 0.3 convolution_bitcast_fusion
  17.9 0.3 convolution_bitcast_fusion.1
  18.2 0.3 convolution_bitcast_fusion.2
  18.5 0.3 convolution_bitcast_fusion.3
  18.9 0.2 copy.44
  19.0 0.2 reshape.249
  19.2 0.2 copy-done.7
  20.5 0.2 copy-done.8
  20.7 0.7 %convolution_select_fusion = f32[34,8,3,128]{3,1,2,0:T(8,128)S(1)} fusion(bf16[3,3,128,128]{3,2,1,0:T(8,128)(2,1)S(1)} %copy-done, bf16[36,1,7,2,128]{4,2,3,0,1:T(8,128)(2,1)S(1)} %slice.391, bf16[36,1,8,3,128]{4,2,3,0,1:T(8,128)(2,1)S(1)} %copy.29, pred[8,3]{0,1:T(4,128)(4,1)S(1)} %copy-done.8), kind=kOutput, calls=%fused_computation.3 | convolution fusion | flops 241858560 | bytes 1062936 | tf_op jit(solution)/shard_map/conv_general_dilated | solution.py:126
  21.5 0.2 squeeze.107
  21.7 0.2 broadcast_select_fusion
  22.2 0.5 fusion
  22.8 0.5 fusion.70
  23.4 0.2 pad_maximum_fusion
  23.6 0.9 %fusion.4 = bf16[4,656,128]{2,1,0:T(8,128)(2,1)} fusion(f32[4,2,656,128]{3,2,1,0:T(8,128)S(1)} %bitcast.224, s32[]{:T(128)S(6)} %select_n.108), kind=kLoop, calls=%fused_computation.14 | loop fusion | bytes 1343492 | tf_op jit(solution)/shard_map/convert_element_type | solution.py:184
  24.5 1.2 %collective-permute-start.4 = (bf16[4,656,128]{2,1,0:T(8,128)(2,1)}, bf16[4,656,128]{2,1,0:T(8,128)(2,1)}, u32[]{:S(2)}, u32[]{:S(2)}) collective-permute-start(bf16[4,656,128]{2,1,0:T(8,128)(2,1)} %fusion.4), channel_id=1, source_target_pairs={{0,4},{4,0},{8,12},{12,8},{16,20},{20,16},{24,28},{28,24},{1,5},{5... | collective-permute-start | bytes 2015240 | tf_op jit(solution)/shard_map/ppermute | solution.py:177
  25.8 2.1 %collective-permute-done.4 = bf16[4,656,128]{2,1,0:T(8,128)(2,1)} collective-permute-done((bf16[4,656,128]{2,1,0:T(8,128)(2,1)}, bf16[4,656,128]{2,1,0:T(8,128)(2,1)}, u32[]{:S(2)}, u32[]{:S(2)}) %collective-permute-start.4) | collective-permute-done | bytes 671776 | tf_op jit(solution)/shard_map/ppermute | solution.py:177
  27.9 1.2 %bitcast_add_fusion = f32[4,656,128]{2,1,0:T(8,128)S(1)} fusion(bf16[4,656,128]{2,1,0:T(8,128)(2,1)} %collective-permute-done.4, f32[4,2,656,128]{3,2,1,0:T(8,128)S(1)} %bitcast.225, s32[]{:T(128)S(6)} %select_n.107), kind=kLoop, calls=%fused_computation.1 | loop fusion | flops 671744 | bytes 3358724 | tf_op jit(solution)/shard_map/add | solution.py:184
  29.2 0.6 collective-permute-start.9
  29.8 0.5 copy-done.2
  30.3 0.5 fusion.84
  30.8 0.7 %copy.61 = f32[16,8,256,1]{2,1,0,3:T(8,128)} copy(f32[16,8,256,1]{2,0,1,3:T(8,128)S(1)} %fusion.84) | data formatting | bytes 262144 | tf_op jit(solution)/shard_map/rctn,tmn->rcm/dot_general | solution.py:150
  31.6 4.3 %collective-permute-done.9 = bf16[2,328,128]{2,1,0:T(8,128)(2,1)S(1)} collective-permute-done((bf16[2,328,128]{2,1,0:T(8,128)(2,1)S(1)}, bf16[2,328,128]{2,1,0:T(8,128)(2,1)S(1)}, u32[]{:S(2)}, u32[]{:S(2)}) %collective-permute-start.9) | collective-permute-done | bytes 167968 | tf_op jit(solution)/shard_map/ppermute | solution.py:177
  36.0 2.2 %collective-permute-done.5 = bf16[2,328,128]{2,1,0:T(8,128)(2,1)S(1)} collective-permute-done((bf16[2,328,128]{2,1,0:T(8,128)(2,1)S(1)}, bf16[2,328,128]{2,1,0:T(8,128)(2,1)S(1)}, u32[]{:S(2)}, u32[]{:S(2)}) %collective-permute-start.5) | collective-permute-done | bytes 167968 | tf_op jit(solution)/shard_map/ppermute | solution.py:177
  38.3 0.9 %collective-permute-start.6 = (bf16[328,128]{1,0:T(8,128)(2,1)S(1)}, bf16[328,128]{1,0:T(8,128)(2,1)S(1)}, u32[]{:S(2)}, u32[]{:S(2)}) collective-permute-start(bf16[328,128]{1,0:T(8,128)(2,1)S(1)} %fusion.68), channel_id=1, source_target_pairs={{0,2},{1,3},{2,0},{3,1},{4,6},{5,7},{6,4},{7,5},{8,10},{9,11},{10,... | collective-permute-start | bytes 251912 | tf_op jit(solution)/shard_map/ppermute | solution.py:177
  39.2 1.3 %collective-permute-done.10 = bf16[328,128]{1,0:T(8,128)(2,1)S(1)} collective-permute-done((bf16[328,128]{1,0:T(8,128)(2,1)S(1)}, bf16[328,128]{1,0:T(8,128)(2,1)S(1)}, u32[]{:S(2)}, u32[]{:S(2)}) %collective-permute-start.10) | collective-permute-done | bytes 84000 | tf_op jit(solution)/shard_map/ppermute | solution.py:177
  40.5 3.4 %collective-permute-start.11 = (bf16[328,128]{1,0:T(8,128)(2,1)S(1)}, bf16[328,128]{1,0:T(8,128)(2,1)S(1)}, u32[]{:S(2)}, u32[]{:S(2)}) collective-permute-start(bf16[328,128]{1,0:T(8,128)(2,1)S(1)} %fusion.50), channel_id=1, source_target_pairs={{0,16},{4,20},{8,24},{12,28},{16,0},{20,4},{24,8},{28,12},{1,17},{... | collective-permute-start | bytes 251912 | tf_op jit(solution)/shard_map/ppermute | solution.py:177
  43.9 2.5 %collective-permute-start.7 = (bf16[328,128]{1,0:T(8,128)(2,1)S(1)}, bf16[328,128]{1,0:T(8,128)(2,1)S(1)}, u32[]{:S(2)}, u32[]{:S(2)}) collective-permute-start(bf16[328,128]{1,0:T(8,128)(2,1)S(1)} %fusion.51), channel_id=1, source_target_pairs={{0,16},{4,20},{8,24},{12,28},{16,0},{20,4},{24,8},{28,12},{1,17},{... | collective-permute-start | bytes 251912 | tf_op jit(solution)/shard_map/ppermute | solution.py:177
  46.4 2.4 %collective-permute-done.11 = bf16[328,128]{1,0:T(8,128)(2,1)S(1)} collective-permute-done((bf16[328,128]{1,0:T(8,128)(2,1)S(1)}, bf16[328,128]{1,0:T(8,128)(2,1)S(1)}, u32[]{:S(2)}, u32[]{:S(2)}) %collective-permute-start.11) | collective-permute-done | bytes 84000 | tf_op jit(solution)/shard_map/ppermute | solution.py:177
  48.9 1.8 %collective-permute-start.12 = (bf16[328,128]{1,0:T(8,128)(2,1)S(1)}, bf16[328,128]{1,0:T(8,128)(2,1)S(1)}, u32[]{:S(2)}, u32[]{:S(2)}) collective-permute-start(bf16[328,128]{1,0:T(8,128)(2,1)S(1)} %add_convert_fusion.3), channel_id=1, source_target_pairs={{0,8},{4,12},{8,0},{12,4},{16,24},{20,28},{24,16},{28,20},{1,9},{5... | collective-permute-start | bytes 251912 | tf_op jit(solution)/shard_map/ppermute | solution.py:177
  50.6 1.1 %collective-permute-start.8 = (bf16[328,128]{1,0:T(8,128)(2,1)S(1)}, bf16[328,128]{1,0:T(8,128)(2,1)S(1)}, u32[]{:S(2)}, u32[]{:S(2)}) collective-permute-start(bf16[328,128]{1,0:T(8,128)(2,1)S(1)} %add_convert_fusion.5), channel_id=1, source_target_pairs={{0,8},{4,12},{8,0},{12,4},{16,24},{20,28},{24,16},{28,20},{1,9},{5... | collective-permute-start | bytes 251912 | tf_op jit(solution)/shard_map/ppermute | solution.py:177
  51.7 2.1 %collective-permute-done.12 = bf16[328,128]{1,0:T(8,128)(2,1)S(1)} collective-permute-done((bf16[328,128]{1,0:T(8,128)(2,1)S(1)}, bf16[328,128]{1,0:T(8,128)(2,1)S(1)}, u32[]{:S(2)}, u32[]{:S(2)}) %collective-permute-start.12) | collective-permute-done | bytes 84000 | tf_op jit(solution)/shard_map/ppermute | solution.py:177
  53.9 1.3 %collective-permute-done.8 = bf16[328,128]{1,0:T(8,128)(2,1)S(1)} collective-permute-done((bf16[328,128]{1,0:T(8,128)(2,1)S(1)}, bf16[328,128]{1,0:T(8,128)(2,1)S(1)}, u32[]{:S(2)}, u32[]{:S(2)}) %collective-permute-start.8) | collective-permute-done | bytes 84000 | tf_op jit(solution)/shard_map/ppermute | solution.py:177
  55.3 1.1 %convolution_convert_fusion = bf16[32,16,128]{2,1,0:T(8,128)(2,1)} fusion(bf16[32,16,1152]{2,1,0:T(8,128)(2,1)S(1)} %copy-done.4, bf16[1152,128,1]{1,0,2:T(8,128)(2,1)S(1)} %bitcast.222), kind=kOutput, calls=%fused_computation.7 | convolution fusion | flops 151060480 | bytes 1605632 | tf_op jit(solution)/shard_map/rck,kn->rcn/dot_general | solution.py:138
  56.4 0.2 collective-permute-done.13
  56.8 0.8 %slice.411 = f32[1024,128]{1,0:T(8,128)} slice(f32[1312,128]{1,0:T(8,128)S(1)} %convert_multiply_fusion), slice={[0:1024], [0:128]} | slice | bytes 1048576 | tf_op jit(solution)/shard_map/slice | solution.py:170
  57.6 0.7 %slice.412 = f32[288,128]{1,0:T(8,128)} slice(f32[1312,128]{1,0:T(8,128)S(1)} %convert_multiply_fusion), slice={[1024:1312], [0:128]} | slice | bytes 294912 | tf_op jit(solution)/shard_map/slice | solution.py:171
  (109 shorter events, 2.9 us)
Async XLA Ops:
  0.6 19.8 %copy-start = (bf16[3,3,128,128]{3,2,1,0:T(8,128)(2,1)S(1)}, bf16[3,3,128,128]{3,2,1,0:T(8,128)(2,1)}, u32[]{:S(2)}) copy-start(bf16[3,3,128,128]{3,2,1,0:T(8,128)(2,1)} %param.10) | copy-start | bytes 884740
  0.6 2.3 %copy-start.6 = (s32[16,8,256]{2,1,0:T(8,128)S(1)}, s32[16,8,256]{2,1,0:T(8,128)}, u32[]{:S(2)}) copy-start(s32[16,8,256]{2,1,0:T(8,128)} %param.6) | copy-start | bytes 393220
  0.7 6.7 %copy-start.1 = (bf16[4,4,256,128]{3,2,1,0:T(8,128)(2,1)S(1)}, bf16[4,4,256,128]{3,2,1,0:T(8,128)(2,1)}, u32[]{:S(2)}) copy-start(bf16[4,4,256,128]{3,2,1,0:T(8,128)(2,1)} %param.8) | copy-start | bytes 3145732
  3.2 8.8 %copy-start.5 = (bf16[32,16,128]{2,1,0:T(8,128)(2,1)S(1)}, bf16[32,16,128]{2,1,0:T(8,128)(2,1)}, u32[]{:S(2)}) copy-start(bf16[32,16,128]{2,1,0:T(8,128)(2,1)} %param.11) | copy-start | bytes 393220
  3.3 5.5 %collective-permute-start.1 = (bf16[12288]{0:T(1024)(128)(2,1)S(1)}, bf16[12288]{0:T(1024)(128)(2,1)S(1)}, u32[]{:S(2)}, u32[]{:S(2)}) collective-permute-start(bf16[12288]{0:T(1024)(128)(2,1)S(1)} %pad_maximum_fusion.6), channel_id=1, source_target_pairs={{1,0},{2,1},{3,2},{0,3},{5,4},{6,5},{7,6},{4,7},{9,8},{10,9},{11,1... | collective-permute-start | bytes 73736 | tf_op jit(solution)/shard_map/ppermute | solution.py:26
  7.3 4.8 %collective-permute-start = (bf16[12288]{0:T(1024)(128)(2,1)S(1)}, bf16[12288]{0:T(1024)(128)(2,1)S(1)}, u32[]{:S(2)}, u32[]{:S(2)}) collective-permute-start(bf16[12288]{0:T(1024)(128)(2,1)S(1)} %pad_maximum_fusion.5), channel_id=1, source_target_pairs={{0,1},{1,2},{2,3},{3,0},{4,5},{5,6},{6,7},{7,4},{8,9},{9,10},{10,1... | collective-permute-start | bytes 73736 | tf_op jit(solution)/shard_map/ppermute | solution.py:25
  12.2 4.4 %collective-permute-start.2 = (bf16[7680]{0:T(1024)(128)(2,1)S(1)}, bf16[7680]{0:T(1024)(128)(2,1)S(1)}, u32[]{:S(2)}, u32[]{:S(2)}) collective-permute-start(bf16[7680]{0:T(1024)(128)(2,1)S(1)} %pad_maximum_fusion.7), channel_id=1, source_target_pairs={{4,0},{8,4},{12,8},{16,12},{20,16},{24,20},{28,24},{5,1},{9,5},{13... | collective-permute-start | bytes 46088 | tf_op jit(solution)/shard_map/ppermute | solution.py:26
  13.6 3.9 %collective-permute-start.3 = (bf16[7680]{0:T(1024)(128)(2,1)S(1)}, bf16[7680]{0:T(1024)(128)(2,1)S(1)}, u32[]{:S(2)}, u32[]{:S(2)}) collective-permute-start(bf16[7680]{0:T(1024)(128)(2,1)S(1)} %pad_maximum_fusion.8), channel_id=1, source_target_pairs={{0,4},{4,8},{8,12},{12,16},{16,20},{20,24},{24,28},{1,5},{5,9},{9,... | collective-permute-start | bytes 46088 | tf_op jit(solution)/shard_map/ppermute | solution.py:25
  18.8 0.7 %copy-start.7 = (f32[128]{0:T(128)S(1)}, f32[128]{0:T(128)}, u32[]{:S(2)}) copy-start(f32[128]{0:T(128)} %param.9) | copy-start | bytes 1540
  20.1 0.7 %copy-start.8 = (pred[8,3]{0,1:T(4,128)(4,1)S(1)}, pred[8,3]{0,1:T(4,128)(4,1)}, u32[]{:S(2)}) copy-start(pred[8,3]{0,1:T(4,128)(4,1)} %constant.177) | copy-start | bytes 76
  20.1 2.1 %copy-start.3 = (bf16[32,16,1152]{2,1,0:T(8,128)(2,1)}, bf16[32,16,1152]{2,1,0:T(8,128)(2,1)S(1)}, u32[]{:S(2)}) copy-start(bf16[32,16,1152]{2,1,0:T(8,128)(2,1)S(1)} %slice_dynamic-update-slice_fusion) | copy-start | bytes 3538948
  24.5 3.3 %collective-permute-start.4 = (bf16[4,656,128]{2,1,0:T(8,128)(2,1)}, bf16[4,656,128]{2,1,0:T(8,128)(2,1)}, u32[]{:S(2)}, u32[]{:S(2)}) collective-permute-start(bf16[4,656,128]{2,1,0:T(8,128)(2,1)} %fusion.4), channel_id=1, source_target_pairs={{0,4},{4,0},{8,12},{12,8},{16,20},{20,16},{24,28},{28,24},{1,5},{5... | collective-permute-start | bytes 2015240 | tf_op jit(solution)/shard_map/ppermute | solution.py:177
  29.1 1.2 %copy-start.2 = (bf16[4,4,256,128]{3,2,1,0:T(8,128)(2,1)S(1)}, bf16[4,4,256,128]{3,2,1,0:T(8,128)(2,1)}, u32[]{:S(2)}) copy-start(bf16[4,4,256,128]{3,2,1,0:T(8,128)(2,1)} %param.8) | copy-start | bytes 3145732
  29.2 6.7 %collective-permute-start.9 = (bf16[2,328,128]{2,1,0:T(8,128)(2,1)S(1)}, bf16[2,328,128]{2,1,0:T(8,128)(2,1)S(1)}, u32[]{:S(2)}, u32[]{:S(2)}) collective-permute-start(bf16[2,328,128]{2,1,0:T(8,128)(2,1)S(1)} %fusion.49), channel_id=1, source_target_pairs={{0,2},{1,3},{2,0},{3,1},{4,6},{5,7},{6,4},{7,5},{8,10},{9,11},{10,... | collective-permute-start | bytes 503816 | tf_op jit(solution)/shard_map/ppermute | solution.py:177
  31.5 6.7 %collective-permute-start.5 = (bf16[2,328,128]{2,1,0:T(8,128)(2,1)S(1)}, bf16[2,328,128]{2,1,0:T(8,128)(2,1)S(1)}, u32[]{:S(2)}, u32[]{:S(2)}) collective-permute-start(bf16[2,328,128]{2,1,0:T(8,128)(2,1)S(1)} %fusion.48), channel_id=1, source_target_pairs={{0,1},{1,0},{2,3},{3,2},{4,5},{5,4},{6,7},{7,6},{8,9},{9,8},{10,11... | collective-permute-start | bytes 503816 | tf_op jit(solution)/shard_map/ppermute | solution.py:177
  36.0 4.5 %collective-permute-start.10 = (bf16[328,128]{1,0:T(8,128)(2,1)S(1)}, bf16[328,128]{1,0:T(8,128)(2,1)S(1)}, u32[]{:S(2)}, u32[]{:S(2)}) collective-permute-start(bf16[328,128]{1,0:T(8,128)(2,1)S(1)} %fusion.69), channel_id=1, source_target_pairs={{0,1},{1,0},{2,3},{3,2},{4,5},{5,4},{6,7},{7,6},{8,9},{9,8},{10,11... | collective-permute-start | bytes 251912 | tf_op jit(solution)/shard_map/ppermute | solution.py:177
  38.3 17.0 %copy-start.4 = (bf16[32,16,1152]{2,1,0:T(8,128)(2,1)S(1)}, bf16[32,16,1152]{2,1,0:T(8,128)(2,1)}, u32[]{:S(2)}) copy-start(bf16[32,16,1152]{2,1,0:T(8,128)(2,1)} %copy-done.3) | copy-start | bytes 3538948
  38.3 5.6 %collective-permute-start.6 = (bf16[328,128]{1,0:T(8,128)(2,1)S(1)}, bf16[328,128]{1,0:T(8,128)(2,1)S(1)}, u32[]{:S(2)}, u32[]{:S(2)}) collective-permute-start(bf16[328,128]{1,0:T(8,128)(2,1)S(1)} %fusion.68), channel_id=1, source_target_pairs={{0,2},{1,3},{2,0},{3,1},{4,6},{5,7},{6,4},{7,5},{8,10},{9,11},{10,... | collective-permute-start | bytes 251912 | tf_op jit(solution)/shard_map/ppermute | solution.py:177
  40.5 8.3 %collective-permute-start.11 = (bf16[328,128]{1,0:T(8,128)(2,1)S(1)}, bf16[328,128]{1,0:T(8,128)(2,1)S(1)}, u32[]{:S(2)}, u32[]{:S(2)}) collective-permute-start(bf16[328,128]{1,0:T(8,128)(2,1)S(1)} %fusion.50), channel_id=1, source_target_pairs={{0,16},{4,20},{8,24},{12,28},{16,0},{20,4},{24,8},{28,12},{1,17},{... | collective-permute-start | bytes 251912 | tf_op jit(solution)/shard_map/ppermute | solution.py:177
  43.9 6.7 %collective-permute-start.7 = (bf16[328,128]{1,0:T(8,128)(2,1)S(1)}, bf16[328,128]{1,0:T(8,128)(2,1)S(1)}, u32[]{:S(2)}, u32[]{:S(2)}) collective-permute-start(bf16[328,128]{1,0:T(8,128)(2,1)S(1)} %fusion.51), channel_id=1, source_target_pairs={{0,16},{4,20},{8,24},{12,28},{16,0},{20,4},{24,8},{28,12},{1,17},{... | collective-permute-start | bytes 251912 | tf_op jit(solution)/shard_map/ppermute | solution.py:177
  48.9 5.0 %collective-permute-start.12 = (bf16[328,128]{1,0:T(8,128)(2,1)S(1)}, bf16[328,128]{1,0:T(8,128)(2,1)S(1)}, u32[]{:S(2)}, u32[]{:S(2)}) collective-permute-start(bf16[328,128]{1,0:T(8,128)(2,1)S(1)} %add_convert_fusion.3), channel_id=1, source_target_pairs={{0,8},{4,12},{8,0},{12,4},{16,24},{20,28},{24,16},{28,20},{1,9},{5... | collective-permute-start | bytes 251912 | tf_op jit(solution)/shard_map/ppermute | solution.py:177
  50.6 4.5 %collective-permute-start.8 = (bf16[328,128]{1,0:T(8,128)(2,1)S(1)}, bf16[328,128]{1,0:T(8,128)(2,1)S(1)}, u32[]{:S(2)}, u32[]{:S(2)}) collective-permute-start(bf16[328,128]{1,0:T(8,128)(2,1)S(1)} %add_convert_fusion.5), channel_id=1, source_target_pairs={{0,8},{4,12},{8,0},{12,4},{16,24},{20,28},{24,16},{28,20},{1,9},{5... | collective-permute-start | bytes 251912 | tf_op jit(solution)/shard_map/ppermute | solution.py:177
  55.2 1.5 %collective-permute-start.13 = (bf16[656,128]{1,0:T(8,128)(2,1)S(1)}, bf16[656,128]{1,0:T(8,128)(2,1)S(1)}, u32[]{:S(2)}, u32[]{:S(2)}) collective-permute-start(bf16[656,128]{1,0:T(8,128)(2,1)S(1)} %pad_maximum_fusion.3), channel_id=1, source_target_pairs={{0,4},{4,0},{8,12},{12,8},{16,20},{20,16},{24,28},{28,24},{1,5},{5... | collective-permute-start | bytes 503816 | tf_op jit(solution)/shard_map/ppermute | solution.py:177

commit v24 on v23

--- a/solution.py
+++ b/solution.py
@@ -244,7 +244,7 @@
     first = scatter_lon(part[:, :half], steps)
     second = scatter_lon(part[:, half:], list(reversed(steps)))
     order = list(reversed(lat_steps[1:]))
-    joined = jnp.concatenate([butterfly(first, order), butterfly(second, order)])
+    joined = jnp.concatenate([butterfly(first, order), butterfly(second, order[::-1])])
     return double(joined, "lat", lat_steps[0]).astype(jnp.float32)
 
 

time: 58.6 us -> 59.3 us (1.012)
  waiting for transfers between devices: 21.2 us -> 22.2 us
    ppermute x10, waiting for transfers between devices: 15.9 us -> 16.8 us  [exchange(): return lax.ppermute(part, axis, [(i, i ^ step) for i in range(size)])]
where the time goes in v24:
time: 59.3 us; the launch traced here: 59 us
  waiting for transfers between devices  22.2 us (37%)
  starting transfers between devices  19.7 us (33%)
  local copies, waits for them, and re-layouts  7.81 us (13%)
  matrix products  4.4 us (7%)
  other arithmetic  3.51 us (6%)
  between operations  1.42 us (2%)
    ppermute x10, waiting for transfers between devices, exchange(): return lax.ppermute(part, axis, [(i, i ^ step) for i in range(size)])  16.8 us
    ppermute x10, starting transfers between devices, exchange(): return lax.ppermute(part, axis, [(i, i ^ step) for i in range(size)])  11.4 us
    ppermute x2, starting transfers between devices, swap_edges(): lax.ppermute(jnp.concatenate([p.reshape(-1) for p in leads]), axis, down)  5.24 us
    ppermute x2, waiting for transfers between devices, swap_edges(): lax.ppermute(jnp.concatenate([p.reshape(-1) for p in lasts]), axis, up)  4.02 us
    ppermute x2, starting transfers between devices, swap_edges(): lax.ppermute(jnp.concatenate([p.reshape(-1) for p in lasts]), axis, up)  3.09 us
    unnamed x45, local copies, waits for them, and re-layouts  1.67 us
    ppermute x2, waiting for transfers between devices, swap_edges(): lax.ppermute(jnp.concatenate([p.reshape(-1) for p in leads]), axis, down)  1.3 us
    add x3, other arithmetic, halve(): keep + exchange(send.astype(jnp.bfloat16), axis, step).astype(keep.dtype)  1.28 us
  transfers between devices with their start and end apart: 14, of which 11 were waited for; matrix products, arithmetic and copies ran while one was open for 5% of the time, Pallas kernels for 0%

profile of v24, /device:TPU:0, one launch (start us, length us, event | category | flops | bytes accessed | tf_op | source)
XLA Modules:
  0.0 59.0 jit_solution(12039239001054811839)
XLA Ops:
  0.7 1.0 %fusion.81 = (bf16[32,2,128]{2,1,0:T(2,128)(2,1)S(1)}, bf16[32,2,128]{2,1,0:T(2,128)(2,1)S(1)}) fusion(bf16[32,16,128]{2,1,0:T(8,128)(2,1)} %param.11), kind=kLoop, calls=%fused_computation.210 | loop fusion | bytes 65536 | tf_op jit(solution)/shard_map/slice | solution.py:23
  1.7 0.8 %multiply_exponential_fusion = f32[16,8,8]{0,2,1:T(8,128)S(1)} fusion(s32[16,8,8]{0,2,1:T(8,128)} %param.7), kind=kLoop, calls=%fused_computation.186 | loop fusion | flops 2048 | bytes 8192 | tf_op jit(solution)/shard_map/exp2 | solution.py:50
  2.5 0.2 broadcast_in_dim.21
  2.7 0.2 reshape.202
  2.9 0.3 fusion.65
  3.3 3.9 %collective-permute-start.1 = (bf16[12288]{0:T(1024)(128)(2,1)S(1)}, bf16[12288]{0:T(1024)(128)(2,1)S(1)}, u32[]{:S(2)}, u32[]{:S(2)}) collective-permute-start(bf16[12288]{0:T(1024)(128)(2,1)S(1)} %pad_maximum_fusion.6), channel_id=1, source_target_pairs={{1,0},{2,1},{3,2},{0,3},{5,4},{6,5},{7,6},{4,7},{9,8},{10,9},{11,1... | collective-permute-start | bytes 73736 | tf_op jit(solution)/shard_map/ppermute | solution.py:26
  7.5 1.3 %collective-permute-done.1 = bf16[12288]{0:T(1024)(128)(2,1)S(1)} collective-permute-done((bf16[12288]{0:T(1024)(128)(2,1)S(1)}, bf16[12288]{0:T(1024)(128)(2,1)S(1)}, u32[]{:S(2)}, u32[]{:S(2)}) %collective-permute-start.1) | collective-permute-done | bytes 24608 | tf_op jit(solution)/shard_map/ppermute | solution.py:26
  8.8 3.3 %collective-permute-done = bf16[12288]{0:T(1024)(128)(2,1)S(1)} collective-permute-done((bf16[12288]{0:T(1024)(128)(2,1)S(1)}, bf16[12288]{0:T(1024)(128)(2,1)S(1)}, u32[]{:S(2)}, u32[]{:S(2)}) %collective-permute-start) | collective-permute-done | bytes 24608 | tf_op jit(solution)/shard_map/ppermute | solution.py:25
  12.2 1.3 %collective-permute-start.2 = (bf16[7680]{0:T(1024)(128)(2,1)S(1)}, bf16[7680]{0:T(1024)(128)(2,1)S(1)}, u32[]{:S(2)}, u32[]{:S(2)}) collective-permute-start(bf16[7680]{0:T(1024)(128)(2,1)S(1)} %pad_maximum_fusion.7), channel_id=1, source_target_pairs={{4,0},{8,4},{12,8},{16,12},{20,16},{24,20},{28,24},{5,1},{9,5},{13... | collective-permute-start | bytes 46088 | tf_op jit(solution)/shard_map/ppermute | solution.py:26
  13.6 3.0 %collective-permute-start.3 = (bf16[7680]{0:T(1024)(128)(2,1)S(1)}, bf16[7680]{0:T(1024)(128)(2,1)S(1)}, u32[]{:S(2)}, u32[]{:S(2)}) collective-permute-start(bf16[7680]{0:T(1024)(128)(2,1)S(1)} %pad_maximum_fusion.8), channel_id=1, source_target_pairs={{0,4},{4,8},{8,12},{12,16},{16,20},{20,24},{24,28},{1,5},{5,9},{9,... | collective-permute-start | bytes 46088 | tf_op jit(solution)/shard_map/ppermute | solution.py:25
  16.7 0.8 %collective-permute-done.3 = bf16[7680]{0:T(1024)(128)(2,1)S(1)} collective-permute-done((bf16[7680]{0:T(1024)(128)(2,1)S(1)}, bf16[7680]{0:T(1024)(128)(2,1)S(1)}, u32[]{:S(2)}, u32[]{:S(2)}) %collective-permute-start.3) | collective-permute-done | bytes 15392 | tf_op jit(solution)/shard_map/ppermute | solution.py:25
  17.6 0.3 convolution_bitcast_fusion
  17.9 0.3 convolution_bitcast_fusion.1
  18.2 0.3 convolution_bitcast_fusion.2
  18.5 0.3 convolution_bitcast_fusion.3
  18.9 0.2 copy.44
  19.0 0.2 reshape.249
  19.2 0.2 copy-done.7
  20.5 0.2 copy-done.8
  20.7 0.7 %convolution_select_fusion = f32[34,8,3,128]{3,1,2,0:T(8,128)S(1)} fusion(bf16[3,3,128,128]{3,2,1,0:T(8,128)(2,1)S(1)} %copy-done, bf16[36,1,7,2,128]{4,2,3,0,1:T(8,128)(2,1)S(1)} %slice.391, bf16[36,1,8,3,128]{4,2,3,0,1:T(8,128)(2,1)S(1)} %copy.29, pred[8,3]{0,1:T(4,128)(4,1)S(1)} %copy-done.8), kind=kOutput, calls=%fused_computation.3 | convolution fusion | flops 241858560 | bytes 1062936 | tf_op jit(solution)/shard_map/conv_general_dilated | solution.py:126
  21.5 0.2 squeeze.107
  21.7 0.2 broadcast_select_fusion
  22.2 0.5 fusion
  22.8 0.5 fusion.70
  23.4 0.2 pad_maximum_fusion
  23.6 0.9 %fusion.4 = bf16[4,656,128]{2,1,0:T(8,128)(2,1)} fusion(f32[4,2,656,128]{3,2,1,0:T(8,128)S(1)} %bitcast.224, s32[]{:T(128)S(6)} %select_n.108), kind=kLoop, calls=%fused_computation.14 | loop fusion | bytes 1343492 | tf_op jit(solution)/shard_map/convert_element_type | solution.py:184
  24.5 1.2 %collective-permute-start.4 = (bf16[4,656,128]{2,1,0:T(8,128)(2,1)}, bf16[4,656,128]{2,1,0:T(8,128)(2,1)}, u32[]{:S(2)}, u32[]{:S(2)}) collective-permute-start(bf16[4,656,128]{2,1,0:T(8,128)(2,1)} %fusion.4), channel_id=1, source_target_pairs={{0,4},{4,0},{8,12},{12,8},{16,20},{20,16},{24,28},{28,24},{1,5},{5... | collective-permute-start | bytes 2015240 | tf_op jit(solution)/shard_map/ppermute | solution.py:177
  25.8 2.1 %collective-permute-done.4 = bf16[4,656,128]{2,1,0:T(8,128)(2,1)} collective-permute-done((bf16[4,656,128]{2,1,0:T(8,128)(2,1)}, bf16[4,656,128]{2,1,0:T(8,128)(2,1)}, u32[]{:S(2)}, u32[]{:S(2)}) %collective-permute-start.4) | collective-permute-done | bytes 671776 | tf_op jit(solution)/shard_map/ppermute | solution.py:177
  27.9 1.2 %bitcast_add_fusion = f32[4,656,128]{2,1,0:T(8,128)S(1)} fusion(bf16[4,656,128]{2,1,0:T(8,128)(2,1)} %collective-permute-done.4, f32[4,2,656,128]{3,2,1,0:T(8,128)S(1)} %bitcast.225, s32[]{:T(128)S(6)} %select_n.107), kind=kLoop, calls=%fused_computation.1 | loop fusion | flops 671744 | bytes 3358724 | tf_op jit(solution)/shard_map/add | solution.py:184
  29.2 0.6 collective-permute-start.9
  29.8 0.5 copy-done.2
  30.3 0.5 fusion.84
  30.8 0.7 %copy.61 = f32[16,8,256,1]{2,1,0,3:T(8,128)} copy(f32[16,8,256,1]{2,0,1,3:T(8,128)S(1)} %fusion.84) | data formatting | bytes 262144 | tf_op jit(solution)/shard_map/rctn,tmn->rcm/dot_general | solution.py:150
  31.6 4.3 %collective-permute-done.9 = bf16[2,328,128]{2,1,0:T(8,128)(2,1)S(1)} collective-permute-done((bf16[2,328,128]{2,1,0:T(8,128)(2,1)S(1)}, bf16[2,328,128]{2,1,0:T(8,128)(2,1)S(1)}, u32[]{:S(2)}, u32[]{:S(2)}) %collective-permute-start.9) | collective-permute-done | bytes 167968 | tf_op jit(solution)/shard_map/ppermute | solution.py:177
  36.0 2.2 %collective-permute-done.5 = bf16[2,328,128]{2,1,0:T(8,128)(2,1)S(1)} collective-permute-done((bf16[2,328,128]{2,1,0:T(8,128)(2,1)S(1)}, bf16[2,328,128]{2,1,0:T(8,128)(2,1)S(1)}, u32[]{:S(2)}, u32[]{:S(2)}) %collective-permute-start.5) | collective-permute-done | bytes 167968 | tf_op jit(solution)/shard_map/ppermute | solution.py:177
  38.3 0.9 %collective-permute-start.6 = (bf16[328,128]{1,0:T(8,128)(2,1)S(1)}, bf16[328,128]{1,0:T(8,128)(2,1)S(1)}, u32[]{:S(2)}, u32[]{:S(2)}) collective-permute-start(bf16[328,128]{1,0:T(8,128)(2,1)S(1)} %fusion.68), channel_id=1, source_target_pairs={{0,2},{1,3},{2,0},{3,1},{4,6},{5,7},{6,4},{7,5},{8,10},{9,11},{10,... | collective-permute-start | bytes 251912 | tf_op jit(solution)/shard_map/ppermute | solution.py:177
  39.2 1.3 %collective-permute-done.10 = bf16[328,128]{1,0:T(8,128)(2,1)S(1)} collective-permute-done((bf16[328,128]{1,0:T(8,128)(2,1)S(1)}, bf16[328,128]{1,0:T(8,128)(2,1)S(1)}, u32[]{:S(2)}, u32[]{:S(2)}) %collective-permute-start.10) | collective-permute-done | bytes 84000 | tf_op jit(solution)/shard_map/ppermute | solution.py:177
  40.5 2.4 %collective-permute-start.11 = (bf16[328,128]{1,0:T(8,128)(2,1)S(1)}, bf16[328,128]{1,0:T(8,128)(2,1)S(1)}, u32[]{:S(2)}, u32[]{:S(2)}) collective-permute-start(bf16[328,128]{1,0:T(8,128)(2,1)S(1)} %fusion.50), channel_id=1, source_target_pairs={{0,8},{4,12},{8,0},{12,4},{16,24},{20,28},{24,16},{28,20},{1,9},{5... | collective-permute-start | bytes 251912 | tf_op jit(solution)/shard_map/ppermute | solution.py:177
  42.9 3.5 %collective-permute-start.7 = (bf16[328,128]{1,0:T(8,128)(2,1)S(1)}, bf16[328,128]{1,0:T(8,128)(2,1)S(1)}, u32[]{:S(2)}, u32[]{:S(2)}) collective-permute-start(bf16[328,128]{1,0:T(8,128)(2,1)S(1)} %fusion.51), channel_id=1, source_target_pairs={{0,16},{4,20},{8,24},{12,28},{16,0},{20,4},{24,8},{28,12},{1,17},{... | collective-permute-start | bytes 251912 | tf_op jit(solution)/shard_map/ppermute | solution.py:177
  46.4 2.4 %collective-permute-start.12 = (bf16[328,128]{1,0:T(8,128)(2,1)S(1)}, bf16[328,128]{1,0:T(8,128)(2,1)S(1)}, u32[]{:S(2)}, u32[]{:S(2)}) collective-permute-start(bf16[328,128]{1,0:T(8,128)(2,1)S(1)} %add_convert_fusion.3), channel_id=1, source_target_pairs={{0,16},{4,20},{8,24},{12,28},{16,0},{20,4},{24,8},{28,12},{1,17},{... | collective-permute-start | bytes 251912 | tf_op jit(solution)/shard_map/ppermute | solution.py:177
  48.8 2.5 %collective-permute-done.7 = bf16[328,128]{1,0:T(8,128)(2,1)S(1)} collective-permute-done((bf16[328,128]{1,0:T(8,128)(2,1)S(1)}, bf16[328,128]{1,0:T(8,128)(2,1)S(1)}, u32[]{:S(2)}, u32[]{:S(2)}) %collective-permute-start.7) | collective-permute-done | bytes 84000 | tf_op jit(solution)/shard_map/ppermute | solution.py:177
  51.3 0.3 collective-permute-start.8
  51.6 1.1 %collective-permute-done.12 = bf16[328,128]{1,0:T(8,128)(2,1)S(1)} collective-permute-done((bf16[328,128]{1,0:T(8,128)(2,1)S(1)}, bf16[328,128]{1,0:T(8,128)(2,1)S(1)}, u32[]{:S(2)}, u32[]{:S(2)}) %collective-permute-start.12) | collective-permute-done | bytes 84000 | tf_op jit(solution)/shard_map/ppermute | solution.py:177
  52.8 3.1 %collective-permute-done.8 = bf16[328,128]{1,0:T(8,128)(2,1)S(1)} collective-permute-done((bf16[328,128]{1,0:T(8,128)(2,1)S(1)}, bf16[328,128]{1,0:T(8,128)(2,1)S(1)}, u32[]{:S(2)}, u32[]{:S(2)}) %collective-permute-start.8) | collective-permute-done | bytes 84000 | tf_op jit(solution)/shard_map/ppermute | solution.py:177
  56.0 1.1 %convolution_convert_fusion = bf16[32,16,128]{2,1,0:T(8,128)(2,1)} fusion(bf16[32,16,1152]{2,1,0:T(8,128)(2,1)S(1)} %copy-done.4, bf16[1152,128,1]{1,0,2:T(8,128)(2,1)S(1)} %bitcast.222), kind=kOutput, calls=%fused_computation.7 | convolution fusion | flops 151060480 | bytes 1605632 | tf_op jit(solution)/shard_map/rck,kn->rcn/dot_general | solution.py:138
  57.1 0.2 collective-permute-done.13
  57.5 0.8 %slice.411 = f32[1024,128]{1,0:T(8,128)} slice(f32[1312,128]{1,0:T(8,128)S(1)} %convert_multiply_fusion), slice={[0:1024], [0:128]} | slice | bytes 1048576 | tf_op jit(solution)/shard_map/slice | solution.py:170
  58.3 0.7 %slice.412 = f32[288,128]{1,0:T(8,128)} slice(f32[1312,128]{1,0:T(8,128)S(1)} %convert_multiply_fusion), slice={[1024:1312], [0:128]} | slice | bytes 294912 | tf_op jit(solution)/shard_map/slice | solution.py:171
  (109 shorter events, 2.9 us)
Async XLA Ops:
  0.6 19.8 %copy-start = (bf16[3,3,128,128]{3,2,1,0:T(8,128)(2,1)S(1)}, bf16[3,3,128,128]{3,2,1,0:T(8,128)(2,1)}, u32[]{:S(2)}) copy-start(bf16[3,3,128,128]{3,2,1,0:T(8,128)(2,1)} %param.10) | copy-start | bytes 884740
  0.6 2.3 %copy-start.6 = (s32[16,8,256]{2,1,0:T(8,128)S(1)}, s32[16,8,256]{2,1,0:T(8,128)}, u32[]{:S(2)}) copy-start(s32[16,8,256]{2,1,0:T(8,128)} %param.6) | copy-start | bytes 393220
  0.7 6.7 %copy-start.1 = (bf16[4,4,256,128]{3,2,1,0:T(8,128)(2,1)S(1)}, bf16[4,4,256,128]{3,2,1,0:T(8,128)(2,1)}, u32[]{:S(2)}) copy-start(bf16[4,4,256,128]{3,2,1,0:T(8,128)(2,1)} %param.8) | copy-start | bytes 3145732
  3.2 8.8 %copy-start.5 = (bf16[32,16,128]{2,1,0:T(8,128)(2,1)S(1)}, bf16[32,16,128]{2,1,0:T(8,128)(2,1)}, u32[]{:S(2)}) copy-start(bf16[32,16,128]{2,1,0:T(8,128)(2,1)} %param.11) | copy-start | bytes 393220
  3.3 5.5 %collective-permute-start.1 = (bf16[12288]{0:T(1024)(128)(2,1)S(1)}, bf16[12288]{0:T(1024)(128)(2,1)S(1)}, u32[]{:S(2)}, u32[]{:S(2)}) collective-permute-start(bf16[12288]{0:T(1024)(128)(2,1)S(1)} %pad_maximum_fusion.6), channel_id=1, source_target_pairs={{1,0},{2,1},{3,2},{0,3},{5,4},{6,5},{7,6},{4,7},{9,8},{10,9},{11,1... | collective-permute-start | bytes 73736 | tf_op jit(solution)/shard_map/ppermute | solution.py:26
  7.3 4.8 %collective-permute-start = (bf16[12288]{0:T(1024)(128)(2,1)S(1)}, bf16[12288]{0:T(1024)(128)(2,1)S(1)}, u32[]{:S(2)}, u32[]{:S(2)}) collective-permute-start(bf16[12288]{0:T(1024)(128)(2,1)S(1)} %pad_maximum_fusion.5), channel_id=1, source_target_pairs={{0,1},{1,2},{2,3},{3,0},{4,5},{5,6},{6,7},{7,4},{8,9},{9,10},{10,1... | collective-permute-start | bytes 73736 | tf_op jit(solution)/shard_map/ppermute | solution.py:25
  12.2 4.4 %collective-permute-start.2 = (bf16[7680]{0:T(1024)(128)(2,1)S(1)}, bf16[7680]{0:T(1024)(128)(2,1)S(1)}, u32[]{:S(2)}, u32[]{:S(2)}) collective-permute-start(bf16[7680]{0:T(1024)(128)(2,1)S(1)} %pad_maximum_fusion.7), channel_id=1, source_target_pairs={{4,0},{8,4},{12,8},{16,12},{20,16},{24,20},{28,24},{5,1},{9,5},{13... | collective-permute-start | bytes 46088 | tf_op jit(solution)/shard_map/ppermute | solution.py:26
  13.6 3.9 %collective-permute-start.3 = (bf16[7680]{0:T(1024)(128)(2,1)S(1)}, bf16[7680]{0:T(1024)(128)(2,1)S(1)}, u32[]{:S(2)}, u32[]{:S(2)}) collective-permute-start(bf16[7680]{0:T(1024)(128)(2,1)S(1)} %pad_maximum_fusion.8), channel_id=1, source_target_pairs={{0,4},{4,8},{8,12},{12,16},{16,20},{20,24},{24,28},{1,5},{5,9},{9,... | collective-permute-start | bytes 46088 | tf_op jit(solution)/shard_map/ppermute | solution.py:25
  18.8 0.7 %copy-start.7 = (f32[128]{0:T(128)S(1)}, f32[128]{0:T(128)}, u32[]{:S(2)}) copy-start(f32[128]{0:T(128)} %param.9) | copy-start | bytes 1540
  20.1 0.7 %copy-start.8 = (pred[8,3]{0,1:T(4,128)(4,1)S(1)}, pred[8,3]{0,1:T(4,128)(4,1)}, u32[]{:S(2)}) copy-start(pred[8,3]{0,1:T(4,128)(4,1)} %constant.177) | copy-start | bytes 76
  20.1 2.1 %copy-start.3 = (bf16[32,16,1152]{2,1,0:T(8,128)(2,1)}, bf16[32,16,1152]{2,1,0:T(8,128)(2,1)S(1)}, u32[]{:S(2)}) copy-start(bf16[32,16,1152]{2,1,0:T(8,128)(2,1)S(1)} %slice_dynamic-update-slice_fusion) | copy-start | bytes 3538948
  24.5 3.3 %collective-permute-start.4 = (bf16[4,656,128]{2,1,0:T(8,128)(2,1)}, bf16[4,656,128]{2,1,0:T(8,128)(2,1)}, u32[]{:S(2)}, u32[]{:S(2)}) collective-permute-start(bf16[4,656,128]{2,1,0:T(8,128)(2,1)} %fusion.4), channel_id=1, source_target_pairs={{0,4},{4,0},{8,12},{12,8},{16,20},{20,16},{24,28},{28,24},{1,5},{5... | collective-permute-start | bytes 2015240 | tf_op jit(solution)/shard_map/ppermute | solution.py:177
  29.1 1.2 %copy-start.2 = (bf16[4,4,256,128]{3,2,1,0:T(8,128)(2,1)S(1)}, bf16[4,4,256,128]{3,2,1,0:T(8,128)(2,1)}, u32[]{:S(2)}) copy-start(bf16[4,4,256,128]{3,2,1,0:T(8,128)(2,1)} %param.8) | copy-start | bytes 3145732
  29.2 6.7 %collective-permute-start.9 = (bf16[2,328,128]{2,1,0:T(8,128)(2,1)S(1)}, bf16[2,328,128]{2,1,0:T(8,128)(2,1)S(1)}, u32[]{:S(2)}, u32[]{:S(2)}) collective-permute-start(bf16[2,328,128]{2,1,0:T(8,128)(2,1)S(1)} %fusion.49), channel_id=1, source_target_pairs={{0,2},{1,3},{2,0},{3,1},{4,6},{5,7},{6,4},{7,5},{8,10},{9,11},{10,... | collective-permute-start | bytes 503816 | tf_op jit(solution)/shard_map/ppermute | solution.py:177
  31.5 6.7 %collective-permute-start.5 = (bf16[2,328,128]{2,1,0:T(8,128)(2,1)S(1)}, bf16[2,328,128]{2,1,0:T(8,128)(2,1)S(1)}, u32[]{:S(2)}, u32[]{:S(2)}) collective-permute-start(bf16[2,328,128]{2,1,0:T(8,128)(2,1)S(1)} %fusion.48), channel_id=1, source_target_pairs={{0,1},{1,0},{2,3},{3,2},{4,5},{5,4},{6,7},{7,6},{8,9},{9,8},{10,11... | collective-permute-start | bytes 503816 | tf_op jit(solution)/shard_map/ppermute | solution.py:177
  36.0 4.5 %collective-permute-start.10 = (bf16[328,128]{1,0:T(8,128)(2,1)S(1)}, bf16[328,128]{1,0:T(8,128)(2,1)S(1)}, u32[]{:S(2)}, u32[]{:S(2)}) collective-permute-start(bf16[328,128]{1,0:T(8,128)(2,1)S(1)} %fusion.69), channel_id=1, source_target_pairs={{0,1},{1,0},{2,3},{3,2},{4,5},{5,4},{6,7},{7,6},{8,9},{9,8},{10,11... | collective-permute-start | bytes 251912 | tf_op jit(solution)/shard_map/ppermute | solution.py:177
  38.3 17.7 %copy-start.4 = (bf16[32,16,1152]{2,1,0:T(8,128)(2,1)S(1)}, bf16[32,16,1152]{2,1,0:T(8,128)(2,1)}, u32[]{:S(2)}) copy-start(bf16[32,16,1152]{2,1,0:T(8,128)(2,1)} %copy-done.3) | copy-start | bytes 3538948
  38.3 4.6 %collective-permute-start.6 = (bf16[328,128]{1,0:T(8,128)(2,1)S(1)}, bf16[328,128]{1,0:T(8,128)(2,1)S(1)}, u32[]{:S(2)}, u32[]{:S(2)}) collective-permute-start(bf16[328,128]{1,0:T(8,128)(2,1)S(1)} %fusion.68), channel_id=1, source_target_pairs={{0,2},{1,3},{2,0},{3,1},{4,6},{5,7},{6,4},{7,5},{8,10},{9,11},{10,... | collective-permute-start | bytes 251912 | tf_op jit(solution)/shard_map/ppermute | solution.py:177
  40.5 5.9 %collective-permute-start.11 = (bf16[328,128]{1,0:T(8,128)(2,1)S(1)}, bf16[328,128]{1,0:T(8,128)(2,1)S(1)}, u32[]{:S(2)}, u32[]{:S(2)}) collective-permute-start(bf16[328,128]{1,0:T(8,128)(2,1)S(1)} %fusion.50), channel_id=1, source_target_pairs={{0,8},{4,12},{8,0},{12,4},{16,24},{20,28},{24,16},{28,20},{1,9},{5... | collective-permute-start | bytes 251912 | tf_op jit(solution)/shard_map/ppermute | solution.py:177
  42.9 8.4 %collective-permute-start.7 = (bf16[328,128]{1,0:T(8,128)(2,1)S(1)}, bf16[328,128]{1,0:T(8,128)(2,1)S(1)}, u32[]{:S(2)}, u32[]{:S(2)}) collective-permute-start(bf16[328,128]{1,0:T(8,128)(2,1)S(1)} %fusion.51), channel_id=1, source_target_pairs={{0,16},{4,20},{8,24},{12,28},{16,0},{20,4},{24,8},{28,12},{1,17},{... | collective-permute-start | bytes 251912 | tf_op jit(solution)/shard_map/ppermute | solution.py:177
  46.4 6.3 %collective-permute-start.12 = (bf16[328,128]{1,0:T(8,128)(2,1)S(1)}, bf16[328,128]{1,0:T(8,128)(2,1)S(1)}, u32[]{:S(2)}, u32[]{:S(2)}) collective-permute-start(bf16[328,128]{1,0:T(8,128)(2,1)S(1)} %add_convert_fusion.3), channel_id=1, source_target_pairs={{0,16},{4,20},{8,24},{12,28},{16,0},{20,4},{24,8},{28,12},{1,17},{... | collective-permute-start | bytes 251912 | tf_op jit(solution)/shard_map/ppermute | solution.py:177
  51.3 4.5 %collective-permute-start.8 = (bf16[328,128]{1,0:T(8,128)(2,1)S(1)}, bf16[328,128]{1,0:T(8,128)(2,1)S(1)}, u32[]{:S(2)}, u32[]{:S(2)}) collective-permute-start(bf16[328,128]{1,0:T(8,128)(2,1)S(1)} %add_convert_fusion.5), channel_id=1, source_target_pairs={{0,8},{4,12},{8,0},{12,4},{16,24},{20,28},{24,16},{28,20},{1,9},{5... | collective-permute-start | bytes 251912 | tf_op jit(solution)/shard_map/ppermute | solution.py:177
  55.9 1.5 %collective-permute-start.13 = (bf16[656,128]{1,0:T(8,128)(2,1)S(1)}, bf16[656,128]{1,0:T(8,128)(2,1)S(1)}, u32[]{:S(2)}, u32[]{:S(2)}) collective-permute-start(bf16[656,128]{1,0:T(8,128)(2,1)S(1)} %pad_maximum_fusion.3), channel_id=1, source_target_pairs={{0,4},{4,0},{8,12},{12,8},{16,20},{20,16},{24,28},{28,24},{1,5},{5... | collective-permute-start | bytes 503816 | tf_op jit(solution)/shard_map/ppermute | solution.py:177
